TPU v7x, 32 devices: a whole 2x2x4 slice. The times are simulated.
32 devices in a mesh: node: 8 (over y, x, core), hub: 4 (over z).
Axes of the slice: x: 2, y: 2, z: 4, core: 2. Of those that a mesh axis runs over, the one named last changes fastest.
Arguments:
- seed_scores: bfloat16 [32768, 128], P(('node', 'hub')), may hold values from -10 to 10
- seed_mask: int32 [32768], P(('node', 'hub')), may hold values 0 or 1
- band_offsets: int32 [256, 10], P(('node', 'hub')), may hold values from -2 to 2
- band_tiles: bfloat16 [256, 10, 128, 128], P(('node', 'hub')), may hold values from 5e-05 to 1
- hub_blocks: int32 [256, 6], P(('node', 'hub')), may hold values from 0 to 31
- hub_tiles: bfloat16 [256, 6, 128, 128], P(('node', 'hub')), may hold values from 5e-05 to 1
- hub_rows: int32 [4096], P(('node', 'hub')), may hold values from 0 to 1023
Outputs:
- labels: float32 [32768, 128], P(('node', 'hub'))
All inputs are finite; a program needn't handle non-finite values. No bound on the sum of `seed_mask` on one device may be relied on, other than what follows from the above.
Results may differ from a plain program's by a relative error of at most 0.00041.
Values may be sent and summed in bfloat16 or wider, within the bound.
No kernel may reach another device: no remote copies, remote signals or barrier semaphores. Data moves between devices by JAX's collectives and lax.ppermute only.
A program may use at most 64 MiB of HBM per device.

v0:
```python
import jax
import jax.numpy as jnp
from jax import lax
from jax.sharding import PartitionSpec as P

BW = 2
ITERS = 3


spread_weight = 0.8


def extended_2(block, sides, width):
    for axis, dim in sides:
        count = lax.axis_size(axis)
        forward = [(i, i + 1) for i in range(count - 1)]
        backward = [(target, source) for source, target in forward]
        low = lax.ppermute(
            lax.slice_in_dim(block, block.shape[dim] - width, None, axis=dim), axis, forward
        )
        high = lax.ppermute(lax.slice_in_dim(block, 0, width, axis=dim), axis, backward)
        block = jnp.concatenate([low, block, high], axis=dim)
    return block


def band_product(extended, tiles, offsets):
    neighbour = jnp.arange(offsets.shape[0], dtype=jnp.int32)[:, None] + BW + offsets
    return jnp.einsum(
        "bkij,bkjc->bic", tiles, extended[neighbour], preferred_element_type=jnp.float32
    )


def body(seed_scores, seed_mask, band_offsets, band_tiles, hub_blocks, hub_tiles, hub_rows):
    blocks = band_offsets.shape[0]
    block_rows = band_tiles.shape[2]
    classes = seed_scores.shape[1]
    seeds = seed_mask.astype(jnp.float32)[:, None] * seed_scores.astype(jnp.float32)
    degree = jnp.sum(band_tiles, axis=(1, 3), dtype=jnp.float32) + jnp.sum(
        hub_tiles, axis=(1, 3), dtype=jnp.float32
    )
    rim_rows = BW * block_rows
    labels = seeds
    for step in range(ITERS):
        current = labels.astype(jnp.bfloat16)
        owned = current[hub_rows]
        hub_all = lax.all_gather(owned, ("node", "hub"), axis=0, tiled=True)
        hub_labels = hub_all.reshape(-1, block_rows, classes)
        hub_part = jnp.einsum(
            "bhij,bhjc->bic", hub_tiles, hub_labels[hub_blocks], preferred_element_type=jnp.float32
        )
        extended = extended_2(current, ((("node", "hub"), 0),), rim_rows)
        extended = extended.reshape(blocks + 2 * BW, block_rows, classes)
        band_part = band_product(extended, band_tiles, band_offsets)
        gathered = ((band_part + hub_part) / degree[..., None]).reshape(-1, classes)
        labels = spread_weight * gathered + (1.0 - spread_weight) * seeds
    return labels


def solution(mesh):
    placed = (
        P(("node", "hub"), None),
        P(("node", "hub")),
        P(("node", "hub"), None),
        P(("node", "hub"), None, None, None),
        P(("node", "hub"), None),
        P(("node", "hub"), None, None, None),
        P(("node", "hub")),
    )
    return jax.shard_map(
        body, mesh=mesh, in_specs=placed, out_specs=P(("node", "hub"), None), check_vma=False
    )
```

profile of v0, /device:TPU:5, one launch (start us, length us, event | category | flops | bytes accessed | tf_op | source)
XLA Modules:
  0.0 199.3 jit_solution(5771182381775568991)
XLA Ops:
  10.6 3.2 %collective-permute-start = (bf16[256,128]{1,0:T(8,128)(2,1)S(1)}, bf16[256,128]{1,0:T(8,128)(2,1)S(1)}, u32[]{:S(2)}, u32[]{:S(2)}) collective-permute-start(bf16[256,128]{1,0:T(8,128)(2,1)S(1)} %get-tuple-element.9), channel_id=1, source_target_pairs={{0,1},{1,2},{2,3},{3,4},{4,5},{5,6},{6,7},{7,8},{8,9},{9,10},{10,1... | collective-permute-start | bytes 196616 | tf_op jit(solution)/shard_map/ppermute | solution.py:18
  13.8 4.5 %collective-permute-start.1 = (bf16[256,128]{1,0:T(8,128)(2,1)S(1)}, bf16[256,128]{1,0:T(8,128)(2,1)S(1)}, u32[]{:S(2)}, u32[]{:S(2)}) collective-permute-start(bf16[256,128]{1,0:T(8,128)(2,1)S(1)} %get-tuple-element.10), channel_id=1, source_target_pairs={{1,0},{2,1},{3,2},{4,3},{5,4},{6,5},{7,6},{8,7},{9,8},{10,9},{11,1... | collective-permute-start | bytes 196616 | tf_op jit(solution)/shard_map/ppermute | solution.py:21
  20.0 1.7 convert_reduce_fusion.1
  22.7 2.5 %gather_fusion = bf16[80,128,128]{2,1,0:T(8,128)(2,1)} fusion(bf16[12,128,128]{2,1,0:T(8,128)(2,1)S(1)} %bitcast.77, s32[1024]{0:T(1024)S(1)} %pad_clamp_fusion.2), kind=kCustom, calls=%fused_computation | custom fusion | bytes 5243200 | tf_op jit(solution)/shard_map/gather | solution.py:29
  25.3 2.6 %convolution_bitcast_fusion.5 = f32[8,128,128]{1,2,0:T(8,128)S(1)} fusion(bf16[8,10,128,128]{3,2,1,0:T(8,128)(2,1)S(1)} %copy-done, bf16[8,10,128,128]{3,2,1,0:T(8,128)(2,1)} %bitcast.80), kind=kOutput, calls=%fused_computation.16 | convolution fusion | flops 335544320 | bytes 5767168 | tf_op jit(solution)/shard_map/bkij,bkjc->bic/dot_general | solution.py:28
  27.9 38.2 %all-gather.7.cloned.1.call-done = bf16[4096,128]{1,0:T(8,128)(2,1)} async-done(((bf16[128,128]{1,0:T(8,128)(2,1)}), bf16[4096,128]{1,0:T(8,128)(2,1)}) %all-gather.7.cloned.1.call-update) | async-done | bytes 1048592 | tf_op jit(solution)/shard_map/all_gather | solution.py:46
  66.1 3.2 %gather_fusion.2 = bf16[48,128,128]{2,1,0:T(8,128)(2,1)} fusion(bf16[32,128,128]{2,1,0:T(8,128)(2,1)} %bitcast.82, s32[1024]{0:T(1024)S(1)} %pad_clamp_fusion), kind=kCustom, calls=%fused_computation.2 | custom fusion | bytes 3145920 | tf_op jit(solution)/shard_map/gather | solution.py:49
  69.3 2.5 %fusion.2 = f32[8,128,128]{1,2,0:T(8,128)S(1)} fusion(f32[8,128,128]{1,2,0:T(8,128)S(1)} %convolution_bitcast_fusion.5, bf16[8,6,128,128]{3,2,1,0:T(8,128)(2,1)} %param.12, bf16[8,6,128,128]{3,2,1,0:T(8,128)(2,1)} %bitcast.86, f32[8,128]{1,0:T(8,128)S(1)} %copy-done.3), kind=kOutput, calls=%fused_computation.19 | convolution fusion | flops 201719808 | bytes 4198400 | tf_op jit(solution)/shard_map/bhij,bhjc->bic/dot_general | solution.py:48
  73.4 2.3 %collective-permute-start.2 = (bf16[256,128]{1,0:T(8,128)(2,1)S(1)}, bf16[256,128]{1,0:T(8,128)(2,1)S(1)}, u32[]{:S(2)}, u32[]{:S(2)}) collective-permute-start(bf16[256,128]{1,0:T(8,128)(2,1)S(1)} %get-tuple-element.7), channel_id=1, source_target_pairs={{0,1},{1,2},{2,3},{3,4},{4,5},{5,6},{6,7},{7,8},{8,9},{9,10},{10,1... | collective-permute-start | bytes 196616 | tf_op jit(solution)/shard_map/ppermute | solution.py:18
  75.8 5.0 %collective-permute-start.3 = (bf16[256,128]{1,0:T(8,128)(2,1)S(1)}, bf16[256,128]{1,0:T(8,128)(2,1)S(1)}, u32[]{:S(2)}, u32[]{:S(2)}) collective-permute-start(bf16[256,128]{1,0:T(8,128)(2,1)S(1)} %get-tuple-element.8), channel_id=1, source_target_pairs={{1,0},{2,1},{3,2},{4,3},{5,4},{6,5},{7,6},{8,7},{9,8},{10,9},{11,1... | collective-permute-start | bytes 196616 | tf_op jit(solution)/shard_map/ppermute | solution.py:21
  81.3 1.6 collective-permute-done.3
  82.9 2.5 %gather_fusion.3 = bf16[80,128,128]{2,1,0:T(8,128)(2,1)} fusion(bf16[12,128,128]{2,1,0:T(8,128)(2,1)S(1)} %bitcast.78, s32[1024]{0:T(1024)S(1)} %pad_clamp_fusion.2), kind=kCustom, calls=%fused_computation.3 | custom fusion | bytes 5243200 | tf_op jit(solution)/shard_map/gather | solution.py:29
  85.5 2.6 %convolution_bitcast_fusion.3 = f32[8,128,128]{1,2,0:T(8,128)S(1)} fusion(bf16[8,10,128,128]{3,2,1,0:T(8,128)(2,1)S(1)} %copy-done, bf16[8,10,128,128]{3,2,1,0:T(8,128)(2,1)} %bitcast.81), kind=kOutput, calls=%fused_computation.14 | convolution fusion | flops 335544320 | bytes 5767168 | tf_op jit(solution)/shard_map/bkij,bkjc->bic/dot_general | solution.py:28
  88.0 38.3 %all-gather.9.cloned.1.call-done = bf16[4096,128]{1,0:T(8,128)(2,1)} async-done(((bf16[128,128]{1,0:T(8,128)(2,1)}), bf16[4096,128]{1,0:T(8,128)(2,1)}) %all-gather.9.cloned.1.call-update) | async-done | bytes 1048592 | tf_op jit(solution)/shard_map/all_gather | solution.py:46
  126.4 3.2 %gather_fusion.5 = bf16[48,128,128]{2,1,0:T(8,128)(2,1)} fusion(bf16[32,128,128]{2,1,0:T(8,128)(2,1)} %bitcast.83, s32[1024]{0:T(1024)S(1)} %pad_clamp_fusion), kind=kCustom, calls=%fused_computation.5 | custom fusion | bytes 3145920 | tf_op jit(solution)/shard_map/gather | solution.py:49
  129.6 2.5 %fusion.5 = f32[8,128,128]{1,2,0:T(8,128)S(1)} fusion(f32[8,128,128]{1,2,0:T(8,128)S(1)} %convolution_bitcast_fusion.3, bf16[8,6,128,128]{3,2,1,0:T(8,128)(2,1)} %param.12, bf16[8,6,128,128]{3,2,1,0:T(8,128)(2,1)} %bitcast.87, f32[8,128]{1,0:T(8,128)S(1)} %copy-done.4), kind=kOutput, calls=%fused_computation.22 | convolution fusion | flops 201719808 | bytes 4198400 | tf_op jit(solution)/shard_map/bhij,bhjc->bic/dot_general | solution.py:48
  133.6 2.3 %collective-permute-start.4 = (bf16[256,128]{1,0:T(8,128)(2,1)S(1)}, bf16[256,128]{1,0:T(8,128)(2,1)S(1)}, u32[]{:S(2)}, u32[]{:S(2)}) collective-permute-start(bf16[256,128]{1,0:T(8,128)(2,1)S(1)} %get-tuple-element.5), channel_id=1, source_target_pairs={{0,1},{1,2},{2,3},{3,4},{4,5},{5,6},{6,7},{7,8},{8,9},{9,10},{10,1... | collective-permute-start | bytes 196616 | tf_op jit(solution)/shard_map/ppermute | solution.py:18
  135.9 5.0 %collective-permute-start.5 = (bf16[256,128]{1,0:T(8,128)(2,1)S(1)}, bf16[256,128]{1,0:T(8,128)(2,1)S(1)}, u32[]{:S(2)}, u32[]{:S(2)}) collective-permute-start(bf16[256,128]{1,0:T(8,128)(2,1)S(1)} %get-tuple-element.6), channel_id=1, source_target_pairs={{1,0},{2,1},{3,2},{4,3},{5,4},{6,5},{7,6},{8,7},{9,8},{10,9},{11,1... | collective-permute-start | bytes 196616 | tf_op jit(solution)/shard_map/ppermute | solution.py:21
  141.5 1.6 collective-permute-done.5
  143.1 2.5 %gather_fusion.6 = bf16[80,128,128]{2,1,0:T(8,128)(2,1)} fusion(bf16[12,128,128]{2,1,0:T(8,128)(2,1)S(1)} %bitcast.76, s32[1024]{0:T(1024)S(1)} %pad_clamp_fusion.2), kind=kCustom, calls=%fused_computation.6 | custom fusion | bytes 5243200 | tf_op jit(solution)/shard_map/gather | solution.py:29
  145.6 2.6 %convolution_bitcast_fusion.1 = f32[8,128,128]{1,2,0:T(8,128)S(1)} fusion(bf16[8,10,128,128]{3,2,1,0:T(8,128)(2,1)S(1)} %copy-done, bf16[8,10,128,128]{3,2,1,0:T(8,128)(2,1)} %bitcast.79), kind=kOutput, calls=%fused_computation.12 | convolution fusion | flops 335544320 | bytes 5767168 | tf_op jit(solution)/shard_map/bkij,bkjc->bic/dot_general | solution.py:28
  148.2 38.4 %all-gather.11.cloned.1.call-done = bf16[4096,128]{1,0:T(8,128)(2,1)} async-done(((bf16[128,128]{1,0:T(8,128)(2,1)}), bf16[4096,128]{1,0:T(8,128)(2,1)}) %all-gather.11.cloned.1.call-update) | async-done | bytes 1048592 | tf_op jit(solution)/shard_map/all_gather | solution.py:46
  186.6 3.2 %gather_fusion.8 = bf16[48,128,128]{2,1,0:T(8,128)(2,1)} fusion(bf16[32,128,128]{2,1,0:T(8,128)(2,1)} %bitcast.84, s32[1024]{0:T(1024)S(1)} %pad_clamp_fusion), kind=kCustom, calls=%fused_computation.8 | custom fusion | bytes 3145920 | tf_op jit(solution)/shard_map/gather | solution.py:49
  189.8 2.0 fusion.8
  (47 shorter events, 12.0 us)
Async XLA Ops:
  6.5 15.1 %copy-start = (bf16[8,10,128,128]{3,2,1,0:T(8,128)(2,1)S(1)}, bf16[8,10,128,128]{3,2,1,0:T(8,128)(2,1)}, u32[]{:S(2)}) copy-start(bf16[8,10,128,128]{3,2,1,0:T(8,128)(2,1)} %param.10) | copy-start | bytes 7864324
  6.5 59.6 %all-gather.7.cloned.1.call-start = ((), (), s32[]{:S(2)}) async-start(), calls=%async_computation | async-start | bytes 1081344 | tf_op jit(solution)/shard_map/all_gather | solution.py:46
  10.5 115.8 %all-gather.9.cloned.1.call-start = ((), (), s32[]{:S(2)}) async-start(), calls=%async_computation.1 | async-start | bytes 1081344 | tf_op jit(solution)/shard_map/all_gather | solution.py:46
  10.6 12.1 %collective-permute-start = (bf16[256,128]{1,0:T(8,128)(2,1)S(1)}, bf16[256,128]{1,0:T(8,128)(2,1)S(1)}, u32[]{:S(2)}, u32[]{:S(2)}) collective-permute-start(bf16[256,128]{1,0:T(8,128)(2,1)S(1)} %get-tuple-element.9), channel_id=1, source_target_pairs={{0,1},{1,2},{2,3},{3,4},{4,5},{5,6},{6,7},{7,8},{8,9},{9,10},{10,1... | collective-permute-start | bytes 196616 | tf_op jit(solution)/shard_map/ppermute | solution.py:18
  13.8 8.9 %collective-permute-start.1 = (bf16[256,128]{1,0:T(8,128)(2,1)S(1)}, bf16[256,128]{1,0:T(8,128)(2,1)S(1)}, u32[]{:S(2)}, u32[]{:S(2)}) collective-permute-start(bf16[256,128]{1,0:T(8,128)(2,1)S(1)} %get-tuple-element.10), channel_id=1, source_target_pairs={{1,0},{2,1},{3,2},{4,3},{5,4},{6,5},{7,6},{8,7},{9,8},{10,9},{11,1... | collective-permute-start | bytes 196616 | tf_op jit(solution)/shard_map/ppermute | solution.py:21
  27.9 41.4 %copy-start.3 = (f32[8,128]{1,0:T(8,128)S(1)}, f32[8,128]{1,0:T(8,128)}, u32[]{:S(2)}) copy-start(f32[8,128]{1,0:T(8,128)} %add.76) | copy-start | bytes 12292
  69.3 2.5 %copy-start.1 = (bf16[1024,128]{1,0:T(8,128)(2,1)S(1)}, bf16[1024,128]{1,0:T(8,128)(2,1)}, u32[]{:S(2)}) copy-start(bf16[1024,128]{1,0:T(8,128)(2,1)} %param.7) | copy-start | bytes 786436
  73.4 113.2 %all-gather.11.cloned.1.call-start = ((), (), s32[]{:S(2)}) async-start(), calls=%async_computation.2 | async-start | bytes 1081344 | tf_op jit(solution)/shard_map/all_gather | solution.py:46
  73.4 7.9 %collective-permute-start.2 = (bf16[256,128]{1,0:T(8,128)(2,1)S(1)}, bf16[256,128]{1,0:T(8,128)(2,1)S(1)}, u32[]{:S(2)}, u32[]{:S(2)}) collective-permute-start(bf16[256,128]{1,0:T(8,128)(2,1)S(1)} %get-tuple-element.7), channel_id=1, source_target_pairs={{0,1},{1,2},{2,3},{3,4},{4,5},{5,6},{6,7},{7,8},{8,9},{9,10},{10,1... | collective-permute-start | bytes 196616 | tf_op jit(solution)/shard_map/ppermute | solution.py:18
  75.8 7.1 %collective-permute-start.3 = (bf16[256,128]{1,0:T(8,128)(2,1)S(1)}, bf16[256,128]{1,0:T(8,128)(2,1)S(1)}, u32[]{:S(2)}, u32[]{:S(2)}) collective-permute-start(bf16[256,128]{1,0:T(8,128)(2,1)S(1)} %get-tuple-element.8), channel_id=1, source_target_pairs={{1,0},{2,1},{3,2},{4,3},{5,4},{6,5},{7,6},{8,7},{9,8},{10,9},{11,1... | collective-permute-start | bytes 196616 | tf_op jit(solution)/shard_map/ppermute | solution.py:21
  88.0 41.5 %copy-start.4 = (f32[8,128]{1,0:T(8,128)S(1)}, f32[8,128]{1,0:T(8,128)}, u32[]{:S(2)}) copy-start(f32[8,128]{1,0:T(8,128)} %add.76) | copy-start | bytes 12292
  133.6 7.9 %collective-permute-start.4 = (bf16[256,128]{1,0:T(8,128)(2,1)S(1)}, bf16[256,128]{1,0:T(8,128)(2,1)S(1)}, u32[]{:S(2)}, u32[]{:S(2)}) collective-permute-start(bf16[256,128]{1,0:T(8,128)(2,1)S(1)} %get-tuple-element.5), channel_id=1, source_target_pairs={{0,1},{1,2},{2,3},{3,4},{4,5},{5,6},{6,7},{7,8},{8,9},{9,10},{10,1... | collective-permute-start | bytes 196616 | tf_op jit(solution)/shard_map/ppermute | solution.py:18
  135.9 7.1 %collective-permute-start.5 = (bf16[256,128]{1,0:T(8,128)(2,1)S(1)}, bf16[256,128]{1,0:T(8,128)(2,1)S(1)}, u32[]{:S(2)}, u32[]{:S(2)}) collective-permute-start(bf16[256,128]{1,0:T(8,128)(2,1)S(1)} %get-tuple-element.6), channel_id=1, source_target_pairs={{1,0},{2,1},{3,2},{4,3},{5,4},{6,5},{7,6},{8,7},{9,8},{10,9},{11,1... | collective-permute-start | bytes 196616 | tf_op jit(solution)/shard_map/ppermute | solution.py:21
  148.2 41.6 %copy-start.2 = (bf16[8,6,128,128]{3,2,1,0:T(8,128)(2,1)S(1)}, bf16[8,6,128,128]{3,2,1,0:T(8,128)(2,1)}, u32[]{:S(2)}) copy-start(bf16[8,6,128,128]{3,2,1,0:T(8,128)(2,1)} %param.12) | copy-start | bytes 4718596
  148.2 41.6 %copy-start.5 = (f32[8,128]{1,0:T(8,128)S(1)}, f32[8,128]{1,0:T(8,128)}, u32[]{:S(2)}) copy-start(f32[8,128]{1,0:T(8,128)} %add.76) | copy-start | bytes 12292
Sparse Core Ops, SparseCore 0:
  10.7 55.3 all-gather.6
  73.5 52.8 all-gather.8
  133.7 52.8 all-gather.10
where the time goes:
time: 201 us; the launch traced here: 199 us
  waiting for transfers between devices  119 us (59%)
  starting transfers between devices  22.5 us (11%)
  local copies, waits for them, and re-layouts  21.4 us (11%)
  matrix products  14.7 us (7%)
  between operations  13.3 us (7%)
  other arithmetic  8.32 us (4%)
    all_gather x3, waiting for transfers between devices, body(): hub_all = lax.all_gather(owned, ('node', 'hub'), axis=0, tiled=True)  115 us
    ppermute x3, starting transfers between devices, extended_2(): lax.ppermute(lax.slice_in_dim(block, 0, width, axis=dim), axis, backward)  14.5 us
    gather x3, local copies, waits for them, and re-layouts, body(): hub_labels[hub_blocks]  9.58 us
    ppermute x3, starting transfers between devices, extended_2(): lax.ppermute(lax.slice_in_dim(block, block.shape[dim] - width, None, axis...  7.9 us
    dot_general x3, matrix products, band_product(): jnp.einsum('bkij,bkjc->bic', tiles, extended[neighbour], preferred_elemen...  7.71 us
    gather x3, local copies, waits for them, and re-layouts, band_product(): extended[neighbour]  7.61 us
    dot_general x3, matrix products, body(): jnp.einsum('bhij,bhjc->bic', hub_tiles, hub_labels[hub_blocks], preferred...  6.95 us
  transfers between devices with their start and end apart: 9, of which 7 were waited for; matrix products, arithmetic and copies ran while one was open for 10% of the time, Pallas kernels for 0%

commit v1 on v0

--- a/solution.py
+++ b/solution.py
@@ -1,10 +1,13 @@
 import jax
 import jax.numpy as jnp
+import numpy as np
 from jax import lax
 from jax.sharding import PartitionSpec as P
 
 BW = 2
 ITERS = 3
+AXES = ("node", "hub")
+ROUNDS_32 = ((1, 2, 3), (8, 16, 24), (4,))
 
 
 spread_weight = 0.8
@@ -30,6 +33,32 @@
     )
 
 
+def xor_rounds(count):
+    if count == 32:
+        return ROUNDS_32
+    return None
+
+
+def hub_gather(owned, block_rows, hub_blocks):
+    count = lax.axis_size(AXES)
+    rounds = xor_rounds(count)
+    if rounds is None or owned.shape[0] != block_rows:
+        hub_all = lax.all_gather(owned, AXES, axis=0, tiled=True)
+        return hub_all.reshape(-1, block_rows, owned.shape[1]), hub_blocks
+    me = lax.axis_index(AXES)
+    buf = owned[None]
+    offs = [0]
+    for group in rounds:
+        recvs = [lax.ppermute(buf, AXES, [(i, i ^ m) for i in range(count)]) for m in group]
+        buf = jnp.concatenate([buf] + recvs, 0)
+        offs = offs + [o ^ m for m in group for o in offs]
+    assert sorted(offs) == list(range(count))
+    where = np.zeros(count, np.int32)
+    for p, o in enumerate(offs):
+        where[o] = p
+    return buf, jnp.asarray(where)[hub_blocks ^ me]
+
+
 def body(seed_scores, seed_mask, band_offsets, band_tiles, hub_blocks, hub_tiles, hub_rows):
     blocks = band_offsets.shape[0]
     block_rows = band_tiles.shape[2]
@@ -43,12 +72,11 @@
     for step in range(ITERS):
         current = labels.astype(jnp.bfloat16)
         owned = current[hub_rows]
-        hub_all = lax.all_gather(owned, ("node", "hub"), axis=0, tiled=True)
-        hub_labels = hub_all.reshape(-1, block_rows, classes)
+        hub_labels, hub_index = hub_gather(owned, block_rows, hub_blocks)
         hub_part = jnp.einsum(
-            "bhij,bhjc->bic", hub_tiles, hub_labels[hub_blocks], preferred_element_type=jnp.float32
+            "bhij,bhjc->bic", hub_tiles, hub_labels[hub_index], preferred_element_type=jnp.float32
         )
-        extended = extended_2(current, ((("node", "hub"), 0),), rim_rows)
+        extended = extended_2(current, ((AXES, 0),), rim_rows)
         extended = extended.reshape(blocks + 2 * BW, block_rows, classes)
         band_part = band_product(extended, band_tiles, band_offsets)
         gathered = ((band_part + hub_part) / degree[..., None]).reshape(-1, classes)
@@ -58,14 +86,14 @@
 
 def solution(mesh):
     placed = (
-        P(("node", "hub"), None),
-        P(("node", "hub")),
-        P(("node", "hub"), None),
-        P(("node", "hub"), None, None, None),
-        P(("node", "hub"), None),
-        P(("node", "hub"), None, None, None),
-        P(("node", "hub")),
+        P(AXES, None),
+        P(AXES),
+        P(AXES, None),
+        P(AXES, None, None, None),
+        P(AXES, None),
+        P(AXES, None, None, None),
+        P(AXES),
     )
     return jax.shard_map(
-        body, mesh=mesh, in_specs=placed, out_specs=P(("node", "hub"), None), check_vma=False
+        body, mesh=mesh, in_specs=placed, out_specs=P(AXES, None), check_vma=False
     )

time: 201 us -> 122 us (0.61)
  waiting for transfers between devices: 119 us -> 9.62 us
  starting transfers between devices: 22.5 us -> 47.4 us
  local copies, waits for them, and re-layouts: 21.4 us -> 41.2 us
  between operations: 13.3 us -> 0.38 us
    all_gather x3 -> x0, waiting for transfers between devices: 115 us -> none  [body(): hub_all = lax.all_gather(owned, ('node', 'hub'), axis=0, tiled=True)]
    ppermute x0 -> x21, starting transfers between devices: none -> 23.1 us  [hub_gather(): lax.ppermute(buf, AXES, [(i, i ^ m) for i in range(count)])]
    unnamed x12 -> x34, local copies, waits for them, and re-layouts: 0.03 us -> 12.9 us
    ppermute x0 -> x21, waiting for transfers between devices: none -> 9.6 us  [hub_gather(): lax.ppermute(buf, AXES, [(i, i ^ m) for i in range(count)])]
    concatenate x0 -> x6, local copies, waits for them, and re-layouts: none -> 7.95 us  [hub_gather(): buf = jnp.concatenate([buf] + recvs, 0)]
    ppermute x3, starting transfers between devices: 14.5 us -> 18.4 us  [extended_2(): lax.ppermute(lax.slice_in_dim(block, 0, width, axis=dim), axis, backward)]
    ppermute x3, waiting for transfers between devices: 3.14 us -> 0.01 us  [extended_2(): lax.ppermute(lax.slice_in_dim(block, 0, width, axis=dim), axis, backward)]
    gather x3 -> x5, local copies, waits for them, and re-layouts: 9.58 us -> 10.4 us  [the longest x3 9.55 us: body(): hub_labels[hub_index]]
  transfers between devices with their start and end apart: 9 -> 27, of which waited for: 7 -> 6; matrix products, arithmetic and copies ran while one was open for 10% -> 27% of each run, Pallas kernels for 0% -> 0%
where the time goes in v1:
time: 122 us; the launch traced here: 120 us
  starting transfers between devices  47.4 us (39%)
  local copies, waits for them, and re-layouts  41.2 us (34%)
  matrix products  14.7 us (12%)
  waiting for transfers between devices  9.62 us (8%)
  other arithmetic  6.98 us (6%)
    ppermute x21, starting transfers between devices, hub_gather(): lax.ppermute(buf, AXES, [(i, i ^ m) for i in range(count)])  23.1 us
    ppermute x3, starting transfers between devices, extended_2(): lax.ppermute(lax.slice_in_dim(block, 0, width, axis=dim), axis, backward)  18.4 us
    unnamed x34, local copies, waits for them, and re-layouts  12.9 us
    ppermute x21, waiting for transfers between devices, hub_gather(): lax.ppermute(buf, AXES, [(i, i ^ m) for i in range(count)])  9.6 us
    gather x3, local copies, waits for them, and re-layouts, body(): hub_labels[hub_index]  9.55 us
    concatenate x6, local copies, waits for them, and re-layouts, hub_gather(): buf = jnp.concatenate([buf] + recvs, 0)  7.95 us
    dot_general x3, matrix products, band_product(): jnp.einsum('bkij,bkjc->bic', tiles, extended[neighbour], preferred_elemen...  7.71 us
    gather x3, local copies, waits for them, and re-layouts, band_product(): extended[neighbour]  7.57 us
  transfers between devices with their start and end apart: 27, of which 6 were waited for; matrix products, arithmetic and copies ran while one was open for 27% of the time, Pallas kernels for 0%

profile of v1, /device:TPU:5, one launch (start us, length us, event | category | flops | bytes accessed | tf_op | source)
XLA Modules:
  0.0 120.2 jit_solution(2431525053136269424)
XLA Ops:
  5.5 2.3 %collective-permute-start.3 = (bf16[1,128,128]{2,1,0:T(8,128)(2,1)S(1)}, bf16[1,128,128]{2,1,0:T(8,128)(2,1)S(1)}, u32[]{:S(2)}, u32[]{:S(2)}) collective-permute-start(bf16[1,128,128]{2,1,0:T(8,128)(2,1)S(1)} %bitcast.94), channel_id=1, source_target_pairs={{0,2},{1,3},{2,0},{3,1},{4,6},{5,7},{6,4},{7,5},{8,10},{9,11},{10,... | collective-permute-start | bytes 98312 | tf_op jit(solution)/shard_map/ppermute | solution.py:52
  7.9 6.6 %collective-permute-start.1 = (bf16[256,128]{1,0:T(8,128)(2,1)S(1)}, bf16[256,128]{1,0:T(8,128)(2,1)S(1)}, u32[]{:S(2)}, u32[]{:S(2)}) collective-permute-start(bf16[256,128]{1,0:T(8,128)(2,1)S(1)} %get-tuple-element.10), channel_id=1, source_target_pairs={{1,0},{2,1},{3,2},{4,3},{5,4},{6,5},{7,6},{8,7},{9,8},{10,9},{11,1... | collective-permute-start | bytes 196616 | tf_op jit(solution)/shard_map/ppermute | solution.py:24
  27.1 3.0 %collective-permute-done.6 = bf16[4,128,128]{2,1,0:T(8,128)(2,1)S(1)} collective-permute-done((bf16[4,128,128]{2,1,0:T(8,128)(2,1)S(1)}, bf16[4,128,128]{2,1,0:T(8,128)(2,1)S(1)}, u32[]{:S(2)}, u32[]{:S(2)}) %collective-permute-start.6) | collective-permute-done | bytes 131104 | tf_op jit(solution)/shard_map/ppermute | solution.py:52
  32.0 2.5 %gather_fusion = bf16[80,128,128]{2,1,0:T(8,128)(2,1)} fusion(bf16[12,128,128]{2,1,0:T(8,128)(2,1)S(1)} %bitcast.85, s32[1024]{0:T(1024)S(1)} %pad_clamp_fusion.3), kind=kCustom, calls=%fused_computation | custom fusion | bytes 5243200 | tf_op jit(solution)/shard_map/gather | solution.py:32
  34.6 2.6 %convolution_bitcast_fusion.5 = f32[8,128,128]{1,2,0:T(8,128)S(1)} fusion(bf16[8,10,128,128]{3,2,1,0:T(8,128)(2,1)S(1)} %copy-done.1, bf16[8,10,128,128]{3,2,1,0:T(8,128)(2,1)} %bitcast.88), kind=kOutput, calls=%fused_computation.17 | convolution fusion | flops 335544320 | bytes 5767168 | tf_op jit(solution)/shard_map/bkij,bkjc->bic/dot_general | solution.py:31
  39.1 3.2 %gather_fusion.3 = bf16[48,128,128]{2,1,0:T(8,128)(2,1)} fusion(bf16[32,128,128]{2,1,0:T(8,128)(2,1)} %constant_dynamic-update-slice_fusion.7, s32[1024]{0:T(1024)S(1)} %pad_clamp_fusion), kind=kCustom, calls=%fused_computation.3 | custom fusion | bytes 3145920 | tf_op jit(solution)/shard_map/gather | solution.py:77
  42.2 2.5 %fusion.2 = f32[8,128,128]{1,2,0:T(8,128)S(1)} fusion(f32[8,128,128]{1,2,0:T(8,128)S(1)} %convolution_bitcast_fusion.5, bf16[8,6,128,128]{3,2,1,0:T(8,128)(2,1)} %param.15, bf16[8,6,128,128]{3,2,1,0:T(8,128)(2,1)} %bitcast.91, f32[8,128]{1,0:T(8,128)S(1)} %copy-done.5), kind=kOutput, calls=%fused_computation.20 | convolution fusion | flops 201719808 | bytes 4198400 | tf_op jit(solution)/shard_map/bhij,bhjc->bic/dot_general | solution.py:76
  45.8 3.8 %collective-permute-start.12 = (bf16[1,128,128]{2,1,0:T(8,128)(2,1)S(1)}, bf16[1,128,128]{2,1,0:T(8,128)(2,1)S(1)}, u32[]{:S(2)}, u32[]{:S(2)}) collective-permute-start(bf16[1,128,128]{2,1,0:T(8,128)(2,1)S(1)} %bitcast.102), channel_id=1, source_target_pairs={{0,2},{1,3},{2,0},{3,1},{4,6},{5,7},{6,4},{7,5},{8,10},{9,11},{10,... | collective-permute-start | bytes 98312 | tf_op jit(solution)/shard_map/ppermute | solution.py:52
  50.2 5.9 %collective-permute-start.10 = (bf16[256,128]{1,0:T(8,128)(2,1)S(1)}, bf16[256,128]{1,0:T(8,128)(2,1)S(1)}, u32[]{:S(2)}, u32[]{:S(2)}) collective-permute-start(bf16[256,128]{1,0:T(8,128)(2,1)S(1)} %get-tuple-element.8), channel_id=1, source_target_pairs={{1,0},{2,1},{3,2},{4,3},{5,4},{6,5},{7,6},{8,7},{9,8},{10,9},{11,1... | collective-permute-start | bytes 196616 | tf_op jit(solution)/shard_map/ppermute | solution.py:24
  64.4 2.7 %collective-permute-done.16 = bf16[4,128,128]{2,1,0:T(8,128)(2,1)S(1)} collective-permute-done((bf16[4,128,128]{2,1,0:T(8,128)(2,1)S(1)}, bf16[4,128,128]{2,1,0:T(8,128)(2,1)S(1)}, u32[]{:S(2)}, u32[]{:S(2)}) %collective-permute-start.16) | collective-permute-done | bytes 131104 | tf_op jit(solution)/shard_map/ppermute | solution.py:52
  68.8 2.5 %gather_fusion.4 = bf16[80,128,128]{2,1,0:T(8,128)(2,1)} fusion(bf16[12,128,128]{2,1,0:T(8,128)(2,1)S(1)} %bitcast.86, s32[1024]{0:T(1024)S(1)} %pad_clamp_fusion.3), kind=kCustom, calls=%fused_computation.4 | custom fusion | bytes 5243200 | tf_op jit(solution)/shard_map/gather | solution.py:32
  71.4 2.6 %convolution_bitcast_fusion.3 = f32[8,128,128]{1,2,0:T(8,128)S(1)} fusion(bf16[8,10,128,128]{3,2,1,0:T(8,128)(2,1)S(1)} %copy-done.1, bf16[8,10,128,128]{3,2,1,0:T(8,128)(2,1)} %bitcast.89), kind=kOutput, calls=%fused_computation.15 | convolution fusion | flops 335544320 | bytes 5767168 | tf_op jit(solution)/shard_map/bkij,bkjc->bic/dot_general | solution.py:31
  75.9 3.2 %gather_fusion.6 = bf16[48,128,128]{2,1,0:T(8,128)(2,1)} fusion(bf16[32,128,128]{2,1,0:T(8,128)(2,1)} %constant_dynamic-update-slice_fusion.22, s32[1024]{0:T(1024)S(1)} %pad_clamp_fusion), kind=kCustom, calls=%fused_computation.6 | custom fusion | bytes 3145920 | tf_op jit(solution)/shard_map/gather | solution.py:77
  79.0 2.5 %fusion.5 = f32[8,128,128]{1,2,0:T(8,128)S(1)} fusion(f32[8,128,128]{1,2,0:T(8,128)S(1)} %convolution_bitcast_fusion.3, bf16[8,6,128,128]{3,2,1,0:T(8,128)(2,1)} %param.15, bf16[8,6,128,128]{3,2,1,0:T(8,128)(2,1)} %bitcast.92, f32[8,128]{1,0:T(8,128)S(1)} %copy-done.6), kind=kOutput, calls=%fused_computation.23 | convolution fusion | flops 201719808 | bytes 4198400 | tf_op jit(solution)/shard_map/bhij,bhjc->bic/dot_general | solution.py:76
  82.5 3.7 %collective-permute-start.21 = (bf16[1,128,128]{2,1,0:T(8,128)(2,1)S(1)}, bf16[1,128,128]{2,1,0:T(8,128)(2,1)S(1)}, u32[]{:S(2)}, u32[]{:S(2)}) collective-permute-start(bf16[1,128,128]{2,1,0:T(8,128)(2,1)S(1)} %bitcast.98), channel_id=1, source_target_pairs={{0,2},{1,3},{2,0},{3,1},{4,6},{5,7},{6,4},{7,5},{8,10},{9,11},{10,... | collective-permute-start | bytes 98312 | tf_op jit(solution)/shard_map/ppermute | solution.py:52
  86.9 5.9 %collective-permute-start.19 = (bf16[256,128]{1,0:T(8,128)(2,1)S(1)}, bf16[256,128]{1,0:T(8,128)(2,1)S(1)}, u32[]{:S(2)}, u32[]{:S(2)}) collective-permute-start(bf16[256,128]{1,0:T(8,128)(2,1)S(1)} %get-tuple-element.6), channel_id=1, source_target_pairs={{1,0},{2,1},{3,2},{4,3},{5,4},{6,5},{7,6},{8,7},{9,8},{10,9},{11,1... | collective-permute-start | bytes 196616 | tf_op jit(solution)/shard_map/ppermute | solution.py:24
  92.8 2.1 %collective-permute-start.18 = (bf16[256,128]{1,0:T(8,128)(2,1)S(1)}, bf16[256,128]{1,0:T(8,128)(2,1)S(1)}, u32[]{:S(2)}, u32[]{:S(2)}) collective-permute-start(bf16[256,128]{1,0:T(8,128)(2,1)S(1)} %get-tuple-element.5), channel_id=1, source_target_pairs={{0,1},{1,2},{2,3},{3,4},{4,5},{5,6},{6,7},{7,8},{8,9},{9,10},{10,1... | collective-permute-start | bytes 196616 | tf_op jit(solution)/shard_map/ppermute | solution.py:21
  101.7 2.5 %collective-permute-done.25 = bf16[4,128,128]{2,1,0:T(8,128)(2,1)S(1)} collective-permute-done((bf16[4,128,128]{2,1,0:T(8,128)(2,1)S(1)}, bf16[4,128,128]{2,1,0:T(8,128)(2,1)S(1)}, u32[]{:S(2)}, u32[]{:S(2)}) %collective-permute-start.25) | collective-permute-done | bytes 131104 | tf_op jit(solution)/shard_map/ppermute | solution.py:52
  104.9 2.0 %collective-permute-start.26 = (bf16[16,128,128]{2,1,0:T(8,128)(2,1)}, bf16[16,128,128]{2,1,0:T(8,128)(2,1)}, u32[]{:S(2)}, u32[]{:S(2)}) collective-permute-start(bf16[16,128,128]{2,1,0:T(8,128)(2,1)} %get-tuple-element.11), channel_id=1, source_target_pairs={{0,4},{1,5},{2,6},{3,7},{4,0},{5,1},{6,2},{7,3},{8,12},{9,13},{10,... | collective-permute-start | bytes 1572872 | tf_op jit(solution)/shard_map/ppermute | solution.py:52
  106.9 2.5 %gather_fusion.7 = bf16[80,128,128]{2,1,0:T(8,128)(2,1)} fusion(bf16[12,128,128]{2,1,0:T(8,128)(2,1)S(1)} %bitcast.84, s32[1024]{0:T(1024)S(1)} %pad_clamp_fusion.3), kind=kCustom, calls=%fused_computation.7 | custom fusion | bytes 5243200 | tf_op jit(solution)/shard_map/gather | solution.py:32
  109.4 2.6 %convolution_bitcast_fusion.1 = f32[8,128,128]{1,2,0:T(8,128)S(1)} fusion(bf16[8,10,128,128]{3,2,1,0:T(8,128)(2,1)S(1)} %copy-done.1, bf16[8,10,128,128]{3,2,1,0:T(8,128)(2,1)} %bitcast.87), kind=kOutput, calls=%fused_computation.13 | convolution fusion | flops 335544320 | bytes 5767168 | tf_op jit(solution)/shard_map/bkij,bkjc->bic/dot_general | solution.py:31
  112.0 2.0 %constant_dynamic-update-slice_fusion.37 = bf16[32,128,128]{2,1,0:T(8,128)(2,1)} fusion(bf16[32,128,128]{2,1,0:T(8,128)(2,1)} %get-tuple-element.12, bf16[16,128,128]{2,1,0:T(8,128)(2,1)} %collective-permute-done.26), kind=kLoop, calls=%fused_computation.78 | loop fusion | bytes 1048576 | tf_op jit(solution)/shard_map/concatenate | solution.py:53
  114.1 3.2 %gather_fusion.9 = bf16[48,128,128]{2,1,0:T(8,128)(2,1)} fusion(bf16[32,128,128]{2,1,0:T(8,128)(2,1)} %constant_dynamic-update-slice_fusion.37, s32[1024]{0:T(1024)S(1)} %pad_clamp_fusion), kind=kCustom, calls=%fused_computation.9 | custom fusion | bytes 3145920 | tf_op jit(solution)/shard_map/gather | solution.py:77
  117.2 2.0 %fusion.8 = f32[8,128,128]{1,2,0:T(8,128)S(1)} fusion(f32[8,128,128]{1,2,0:T(8,128)S(1)} %convolution_bitcast_fusion.1, bf16[8,6,128,128]{3,2,1,0:T(8,128)(2,1)S(1)} %copy-done.4, bf16[8,6,128,128]{3,2,1,0:T(8,128)(2,1)} %bitcast.90, f32[8,128]{1,0:T(8,128)S(1)} %copy-done.7), kind=kOutput, calls=%fused_computation.26 | convolution fusion | flops 201719808 | bytes 4198400 | tf_op jit(solution)/shard_map/bhij,bhjc->bic/dot_general | solution.py:76
  (115 shorter events, 45.5 us)
Async XLA Ops:
  4.2 16.9 %collective-permute-start.2 = (bf16[1,128,128]{2,1,0:T(8,128)(2,1)S(1)}, bf16[1,128,128]{2,1,0:T(8,128)(2,1)S(1)}, u32[]{:S(2)}, u32[]{:S(2)}) collective-permute-start(bf16[1,128,128]{2,1,0:T(8,128)(2,1)S(1)} %bitcast.93), channel_id=1, source_target_pairs={{0,1},{1,0},{2,3},{3,2},{4,5},{5,4},{6,7},{7,6},{8,9},{9,8},{10,11... | collective-permute-start | bytes 98312 | tf_op jit(solution)/shard_map/ppermute | solution.py:52
  5.5 15.6 %collective-permute-start.3 = (bf16[1,128,128]{2,1,0:T(8,128)(2,1)S(1)}, bf16[1,128,128]{2,1,0:T(8,128)(2,1)S(1)}, u32[]{:S(2)}, u32[]{:S(2)}) collective-permute-start(bf16[1,128,128]{2,1,0:T(8,128)(2,1)S(1)} %bitcast.94), channel_id=1, source_target_pairs={{0,2},{1,3},{2,0},{3,1},{4,6},{5,7},{6,4},{7,5},{8,10},{9,11},{10,... | collective-permute-start | bytes 98312 | tf_op jit(solution)/shard_map/ppermute | solution.py:52
  7.8 13.3 %collective-permute-start.4 = (bf16[1,128,128]{2,1,0:T(8,128)(2,1)S(1)}, bf16[1,128,128]{2,1,0:T(8,128)(2,1)S(1)}, u32[]{:S(2)}, u32[]{:S(2)}) collective-permute-start(bf16[1,128,128]{2,1,0:T(8,128)(2,1)S(1)} %bitcast.95), channel_id=1, source_target_pairs={{0,3},{1,2},{2,1},{3,0},{4,7},{5,6},{6,5},{7,4},{8,11},{9,10},{10,... | collective-permute-start | bytes 98312 | tf_op jit(solution)/shard_map/ppermute | solution.py:52
  7.9 24.2 %collective-permute-start.1 = (bf16[256,128]{1,0:T(8,128)(2,1)S(1)}, bf16[256,128]{1,0:T(8,128)(2,1)S(1)}, u32[]{:S(2)}, u32[]{:S(2)}) collective-permute-start(bf16[256,128]{1,0:T(8,128)(2,1)S(1)} %get-tuple-element.10), channel_id=1, source_target_pairs={{1,0},{2,1},{3,2},{4,3},{5,4},{6,5},{7,6},{8,7},{9,8},{10,9},{11,1... | collective-permute-start | bytes 196616 | tf_op jit(solution)/shard_map/ppermute | solution.py:24
  14.4 17.6 %collective-permute-start = (bf16[256,128]{1,0:T(8,128)(2,1)S(1)}, bf16[256,128]{1,0:T(8,128)(2,1)S(1)}, u32[]{:S(2)}, u32[]{:S(2)}) collective-permute-start(bf16[256,128]{1,0:T(8,128)(2,1)S(1)} %get-tuple-element.9), channel_id=1, source_target_pairs={{0,1},{1,2},{2,3},{3,4},{4,5},{5,6},{6,7},{7,8},{8,9},{9,10},{10,1... | collective-permute-start | bytes 196616 | tf_op jit(solution)/shard_map/ppermute | solution.py:21
  22.4 7.7 %collective-permute-start.6 = (bf16[4,128,128]{2,1,0:T(8,128)(2,1)S(1)}, bf16[4,128,128]{2,1,0:T(8,128)(2,1)S(1)}, u32[]{:S(2)}, u32[]{:S(2)}) collective-permute-start(bf16[4,128,128]{2,1,0:T(8,128)(2,1)S(1)} %pad_maximum_fusion.3), channel_id=1, source_target_pairs={{0,16},{1,17},{2,18},{3,19},{4,20},{5,21},{6,22},{7,23},{8,24},{9,... | collective-permute-start | bytes 393224 | tf_op jit(solution)/shard_map/ppermute | solution.py:52
  22.6 8.2 %collective-permute-start.7 = (bf16[4,128,128]{2,1,0:T(8,128)(2,1)S(1)}, bf16[4,128,128]{2,1,0:T(8,128)(2,1)S(1)}, u32[]{:S(2)}, u32[]{:S(2)}) collective-permute-start(bf16[4,128,128]{2,1,0:T(8,128)(2,1)S(1)} %pad_maximum_fusion.3), channel_id=1, source_target_pairs={{0,24},{1,25},{2,26},{3,27},{4,28},{5,29},{6,30},{7,31},{8,16},{9,... | collective-permute-start | bytes 393224 | tf_op jit(solution)/shard_map/ppermute | solution.py:52
  31.6 5.5 %collective-permute-start.8 = (bf16[16,128,128]{2,1,0:T(8,128)(2,1)}, bf16[16,128,128]{2,1,0:T(8,128)(2,1)}, u32[]{:S(2)}, u32[]{:S(2)}) collective-permute-start(bf16[16,128,128]{2,1,0:T(8,128)(2,1)} %get-tuple-element.23), channel_id=1, source_target_pairs={{0,4},{1,5},{2,6},{3,7},{4,0},{5,1},{6,2},{7,3},{8,12},{9,13},{10,... | collective-permute-start | bytes 1572872 | tf_op jit(solution)/shard_map/ppermute | solution.py:52
  45.7 12.4 %collective-permute-start.11 = (bf16[1,128,128]{2,1,0:T(8,128)(2,1)S(1)}, bf16[1,128,128]{2,1,0:T(8,128)(2,1)S(1)}, u32[]{:S(2)}, u32[]{:S(2)}) collective-permute-start(bf16[1,128,128]{2,1,0:T(8,128)(2,1)S(1)} %bitcast.101), channel_id=1, source_target_pairs={{0,1},{1,0},{2,3},{3,2},{4,5},{5,4},{6,7},{7,6},{8,9},{9,8},{10,11... | collective-permute-start | bytes 98312 | tf_op jit(solution)/shard_map/ppermute | solution.py:52
  45.8 12.3 %collective-permute-start.12 = (bf16[1,128,128]{2,1,0:T(8,128)(2,1)S(1)}, bf16[1,128,128]{2,1,0:T(8,128)(2,1)S(1)}, u32[]{:S(2)}, u32[]{:S(2)}) collective-permute-start(bf16[1,128,128]{2,1,0:T(8,128)(2,1)S(1)} %bitcast.102), channel_id=1, source_target_pairs={{0,2},{1,3},{2,0},{3,1},{4,6},{5,7},{6,4},{7,5},{8,10},{9,11},{10,... | collective-permute-start | bytes 98312 | tf_op jit(solution)/shard_map/ppermute | solution.py:52
  49.6 8.5 %collective-permute-start.13 = (bf16[1,128,128]{2,1,0:T(8,128)(2,1)S(1)}, bf16[1,128,128]{2,1,0:T(8,128)(2,1)S(1)}, u32[]{:S(2)}, u32[]{:S(2)}) collective-permute-start(bf16[1,128,128]{2,1,0:T(8,128)(2,1)S(1)} %bitcast.103), channel_id=1, source_target_pairs={{0,3},{1,2},{2,1},{3,0},{4,7},{5,6},{6,5},{7,4},{8,11},{9,10},{10,... | collective-permute-start | bytes 98312 | tf_op jit(solution)/shard_map/ppermute | solution.py:52
  50.2 18.6 %collective-permute-start.10 = (bf16[256,128]{1,0:T(8,128)(2,1)S(1)}, bf16[256,128]{1,0:T(8,128)(2,1)S(1)}, u32[]{:S(2)}, u32[]{:S(2)}) collective-permute-start(bf16[256,128]{1,0:T(8,128)(2,1)S(1)} %get-tuple-element.8), channel_id=1, source_target_pairs={{1,0},{2,1},{3,2},{4,3},{5,4},{6,5},{7,6},{8,7},{9,8},{10,9},{11,1... | collective-permute-start | bytes 196616 | tf_op jit(solution)/shard_map/ppermute | solution.py:24
  56.2 12.7 %collective-permute-start.9 = (bf16[256,128]{1,0:T(8,128)(2,1)S(1)}, bf16[256,128]{1,0:T(8,128)(2,1)S(1)}, u32[]{:S(2)}, u32[]{:S(2)}) collective-permute-start(bf16[256,128]{1,0:T(8,128)(2,1)S(1)} %get-tuple-element.7), channel_id=1, source_target_pairs={{0,1},{1,2},{2,3},{3,4},{4,5},{5,6},{6,7},{7,8},{8,9},{9,10},{10,1... | collective-permute-start | bytes 196616 | tf_op jit(solution)/shard_map/ppermute | solution.py:21
  58.4 5.3 %collective-permute-start.15 = (bf16[4,128,128]{2,1,0:T(8,128)(2,1)S(1)}, bf16[4,128,128]{2,1,0:T(8,128)(2,1)S(1)}, u32[]{:S(2)}, u32[]{:S(2)}) collective-permute-start(bf16[4,128,128]{2,1,0:T(8,128)(2,1)S(1)} %pad_maximum_fusion.4), channel_id=1, source_target_pairs={{0,16},{1,17},{2,18},{3,19},{4,20},{5,21},{6,22},{7,23},{8,24},{9,... | collective-permute-start | bytes 393224 | tf_op jit(solution)/shard_map/ppermute | solution.py:52
  59.5 7.7 %collective-permute-start.16 = (bf16[4,128,128]{2,1,0:T(8,128)(2,1)S(1)}, bf16[4,128,128]{2,1,0:T(8,128)(2,1)S(1)}, u32[]{:S(2)}, u32[]{:S(2)}) collective-permute-start(bf16[4,128,128]{2,1,0:T(8,128)(2,1)S(1)} %pad_maximum_fusion.4), channel_id=1, source_target_pairs={{0,24},{1,25},{2,26},{3,27},{4,28},{5,29},{6,30},{7,31},{8,16},{9,... | collective-permute-start | bytes 393224 | tf_op jit(solution)/shard_map/ppermute | solution.py:52
  67.8 6.1 %collective-permute-start.17 = (bf16[16,128,128]{2,1,0:T(8,128)(2,1)}, bf16[16,128,128]{2,1,0:T(8,128)(2,1)}, u32[]{:S(2)}, u32[]{:S(2)}) collective-permute-start(bf16[16,128,128]{2,1,0:T(8,128)(2,1)} %get-tuple-element.17), channel_id=1, source_target_pairs={{0,4},{1,5},{2,6},{3,7},{4,0},{5,1},{6,2},{7,3},{8,12},{9,13},{10,... | collective-permute-start | bytes 1572872 | tf_op jit(solution)/shard_map/ppermute | solution.py:52
  82.5 12.4 %collective-permute-start.20 = (bf16[1,128,128]{2,1,0:T(8,128)(2,1)S(1)}, bf16[1,128,128]{2,1,0:T(8,128)(2,1)S(1)}, u32[]{:S(2)}, u32[]{:S(2)}) collective-permute-start(bf16[1,128,128]{2,1,0:T(8,128)(2,1)S(1)} %bitcast.97), channel_id=1, source_target_pairs={{0,1},{1,0},{2,3},{3,2},{4,5},{5,4},{6,7},{7,6},{8,9},{9,8},{10,11... | collective-permute-start | bytes 98312 | tf_op jit(solution)/shard_map/ppermute | solution.py:52
  82.5 12.3 %collective-permute-start.21 = (bf16[1,128,128]{2,1,0:T(8,128)(2,1)S(1)}, bf16[1,128,128]{2,1,0:T(8,128)(2,1)S(1)}, u32[]{:S(2)}, u32[]{:S(2)}) collective-permute-start(bf16[1,128,128]{2,1,0:T(8,128)(2,1)S(1)} %bitcast.98), channel_id=1, source_target_pairs={{0,2},{1,3},{2,0},{3,1},{4,6},{5,7},{6,4},{7,5},{8,10},{9,11},{10,... | collective-permute-start | bytes 98312 | tf_op jit(solution)/shard_map/ppermute | solution.py:52
  86.2 8.7 %collective-permute-start.22 = (bf16[1,128,128]{2,1,0:T(8,128)(2,1)S(1)}, bf16[1,128,128]{2,1,0:T(8,128)(2,1)S(1)}, u32[]{:S(2)}, u32[]{:S(2)}) collective-permute-start(bf16[1,128,128]{2,1,0:T(8,128)(2,1)S(1)} %bitcast.99), channel_id=1, source_target_pairs={{0,3},{1,2},{2,1},{3,0},{4,7},{5,6},{6,5},{7,4},{8,11},{9,10},{10,... | collective-permute-start | bytes 98312 | tf_op jit(solution)/shard_map/ppermute | solution.py:52
  86.9 20.0 %collective-permute-start.19 = (bf16[256,128]{1,0:T(8,128)(2,1)S(1)}, bf16[256,128]{1,0:T(8,128)(2,1)S(1)}, u32[]{:S(2)}, u32[]{:S(2)}) collective-permute-start(bf16[256,128]{1,0:T(8,128)(2,1)S(1)} %get-tuple-element.6), channel_id=1, source_target_pairs={{1,0},{2,1},{3,2},{4,3},{5,4},{6,5},{7,6},{8,7},{9,8},{10,9},{11,1... | collective-permute-start | bytes 196616 | tf_op jit(solution)/shard_map/ppermute | solution.py:24
  92.8 14.1 %collective-permute-start.18 = (bf16[256,128]{1,0:T(8,128)(2,1)S(1)}, bf16[256,128]{1,0:T(8,128)(2,1)S(1)}, u32[]{:S(2)}, u32[]{:S(2)}) collective-permute-start(bf16[256,128]{1,0:T(8,128)(2,1)S(1)} %get-tuple-element.5), channel_id=1, source_target_pairs={{0,1},{1,2},{2,3},{3,4},{4,5},{5,6},{6,7},{7,8},{8,9},{9,10},{10,1... | collective-permute-start | bytes 196616 | tf_op jit(solution)/shard_map/ppermute | solution.py:21
  95.6 5.4 %collective-permute-start.24 = (bf16[4,128,128]{2,1,0:T(8,128)(2,1)S(1)}, bf16[4,128,128]{2,1,0:T(8,128)(2,1)S(1)}, u32[]{:S(2)}, u32[]{:S(2)}) collective-permute-start(bf16[4,128,128]{2,1,0:T(8,128)(2,1)S(1)} %pad_maximum_fusion.5), channel_id=1, source_target_pairs={{0,16},{1,17},{2,18},{3,19},{4,20},{5,21},{6,22},{7,23},{8,24},{9,... | collective-permute-start | bytes 393224 | tf_op jit(solution)/shard_map/ppermute | solution.py:52
  97.5 6.7 %collective-permute-start.25 = (bf16[4,128,128]{2,1,0:T(8,128)(2,1)S(1)}, bf16[4,128,128]{2,1,0:T(8,128)(2,1)S(1)}, u32[]{:S(2)}, u32[]{:S(2)}) collective-permute-start(bf16[4,128,128]{2,1,0:T(8,128)(2,1)S(1)} %pad_maximum_fusion.5), channel_id=1, source_target_pairs={{0,24},{1,25},{2,26},{3,27},{4,28},{5,29},{6,30},{7,31},{8,16},{9,... | collective-permute-start | bytes 393224 | tf_op jit(solution)/shard_map/ppermute | solution.py:52
  104.9 7.2 %collective-permute-start.26 = (bf16[16,128,128]{2,1,0:T(8,128)(2,1)}, bf16[16,128,128]{2,1,0:T(8,128)(2,1)}, u32[]{:S(2)}, u32[]{:S(2)}) collective-permute-start(bf16[16,128,128]{2,1,0:T(8,128)(2,1)} %get-tuple-element.11), channel_id=1, source_target_pairs={{0,4},{1,5},{2,6},{3,7},{4,0},{5,1},{6,2},{7,3},{8,12},{9,13},{10,... | collective-permute-start | bytes 1572872 | tf_op jit(solution)/shard_map/ppermute | solution.py:52
  (11 other events, 74.0 us)

commit v2 on v1

v2 whole, which is shorter than its diff:
```python
import functools

import jax
import jax.numpy as jnp
import numpy as np
from jax import lax
from jax.experimental import pallas as pl
from jax.experimental.pallas import tpu as pltpu
from jax.sharding import PartitionSpec as P

BW = 2
ITERS = 3
AXES = ("node", "hub")
ROUNDS_32 = ((1, 2, 3), (8, 16, 24), (4,))


spread_weight = 0.8


def rims(block, width):
    count = lax.axis_size(AXES)
    forward = [(i, i + 1) for i in range(count - 1)]
    backward = [(target, source) for source, target in forward]
    low = lax.ppermute(lax.slice_in_dim(block, block.shape[0] - width, None, axis=0), AXES, forward)
    high = lax.ppermute(lax.slice_in_dim(block, 0, width, axis=0), AXES, backward)
    return low, high


def xor_rounds(count):
    if count == 32:
        return ROUNDS_32
    return None


def hub_gather(owned, block_rows, hub_blocks):
    count = lax.axis_size(AXES)
    rounds = xor_rounds(count)
    if rounds is None or owned.shape[0] != block_rows:
        hub_all = lax.all_gather(owned, AXES, axis=0, tiled=True)
        return [hub_all.reshape(-1, block_rows, owned.shape[1])], hub_blocks
    me = lax.axis_index(AXES)
    buf = owned[None]
    offs = [0]
    pieces = [buf]
    for r, group in enumerate(rounds):
        recvs = [lax.ppermute(buf, AXES, [(i, i ^ m) for i in range(count)]) for m in group]
        offs = offs + [o ^ m for m in group for o in offs]
        pieces = [buf] + recvs
        if r + 1 < len(rounds):
            buf = jnp.concatenate(pieces, 0)
    assert sorted(offs) == list(range(count))
    where = np.zeros(count, np.int32)
    for p, o in enumerate(offs):
        where[o] = p
    return pieces, jnp.asarray(where)[hub_blocks ^ me]


def spread_kernel(n_hub, off_ref, hidx_ref, cur_hbm, low_hbm, high_hbm, *rest):
    hub_hbm = rest[:n_hub]
    bt_hbm, ht_hbm, deg_ref, seeds_ref, out_ref, cur_out_ref, ext, hub, bt, ht, sem = rest[n_hub:]
    blocks, k_band, rows = bt.shape[0], bt.shape[1], bt.shape[2]
    k_hub = ht.shape[1]
    width = low_hbm.shape[0]
    own = cur_hbm.shape[0]
    copies = [
        pltpu.make_async_copy(low_hbm, ext.at[pl.ds(0, width)], sem.at[0]),
        pltpu.make_async_copy(cur_hbm, ext.at[pl.ds(width, own)], sem.at[1]),
        pltpu.make_async_copy(high_hbm, ext.at[pl.ds(width + own, width)], sem.at[2]),
    ]
    at = 0
    for i, piece in enumerate(hub_hbm):
        n = piece.shape[0]
        copies.append(pltpu.make_async_copy(piece, hub.at[pl.ds(at, n)], sem.at[3 + i]))
        at += n
    first = 3 + n_hub
    band_copies = [
        pltpu.make_async_copy(bt_hbm.at[b], bt.at[b], sem.at[first + b]) for b in range(blocks)
    ]
    hub_copies = [
        pltpu.make_async_copy(ht_hbm.at[b], ht.at[b], sem.at[first + blocks + b])
        for b in range(blocks)
    ]
    for b in range(blocks):
        band_copies[b].start()
        if b == 0:
            for c in copies:
                c.start()
        hub_copies[b].start()
    for c in copies:
        c.wait()
    for b in range(blocks):
        band_copies[b].wait()
        acc = jnp.zeros((rows, cur_out_ref.shape[1]), jnp.float32)
        for k in range(k_band):
            n = b + BW + off_ref[b * k_band + k]
            start = pl.multiple_of(n * rows, rows)
            acc = acc + jnp.dot(bt[b, k], ext[pl.ds(start, rows), :], preferred_element_type=jnp.float32)
        band = acc
        hub_copies[b].wait()
        acc = jnp.zeros_like(band)
        for h in range(k_hub):
            p = hidx_ref[b * k_hub + h]
            acc = acc + jnp.dot(ht[b, h], hub[p], preferred_element_type=jnp.float32)
        gathered = (band + acc) / deg_ref[pl.ds(b * rows, rows), :]
        labels = spread_weight * gathered + (1.0 - spread_weight) * seeds_ref[pl.ds(b * rows, rows), :]
        out_ref[pl.ds(b * rows, rows), :] = labels
        cur_out_ref[pl.ds(b * rows, rows), :] = labels.astype(cur_out_ref.dtype)


def spread(band_offsets, hub_index, current, low, high, hub_pieces, band_tiles, hub_tiles, degree, seeds):
    blocks, k_band, rows, _ = band_tiles.shape
    k_hub = hub_tiles.shape[1]
    classes = current.shape[1]
    n_hub_blocks = sum(p.shape[0] for p in hub_pieces)
    smem = pl.BlockSpec(memory_space=pltpu.SMEM)
    anyspace = pl.BlockSpec(memory_space=pl.ANY)
    vmem = pl.BlockSpec(memory_space=pltpu.VMEM)
    n_hub = len(hub_pieces)
    return pl.pallas_call(
        functools.partial(spread_kernel, n_hub),
        in_specs=[smem, smem] + [anyspace] * (3 + n_hub + 2) + [vmem, vmem],
        out_specs=[vmem, vmem],
        out_shape=[
            jax.ShapeDtypeStruct(seeds.shape, jnp.float32),
            jax.ShapeDtypeStruct(current.shape, current.dtype),
        ],
        scratch_shapes=[
            pltpu.VMEM((low.shape[0] + current.shape[0] + high.shape[0], classes), current.dtype),
            pltpu.VMEM((n_hub_blocks, rows, classes), current.dtype),
            pltpu.VMEM(band_tiles.shape, band_tiles.dtype),
            pltpu.VMEM(hub_tiles.shape, hub_tiles.dtype),
            pltpu.SemaphoreType.DMA((3 + n_hub + 2 * blocks,)),
        ],
    )(
        band_offsets.reshape(-1),
        hub_index.reshape(-1),
        current,
        low,
        high,
        *hub_pieces,
        band_tiles,
        hub_tiles,
        degree,
        seeds,
    )


def body(seed_scores, seed_mask, band_offsets, band_tiles, hub_blocks, hub_tiles, hub_rows):
    block_rows = band_tiles.shape[2]
    seeds = seed_mask.astype(jnp.float32)[:, None] * seed_scores.astype(jnp.float32)
    degree = jnp.sum(band_tiles, axis=(1, 3), dtype=jnp.float32) + jnp.sum(
        hub_tiles, axis=(1, 3), dtype=jnp.float32
    )
    degree = degree.reshape(-1, 1)
    rim_rows = BW * block_rows
    current = seeds.astype(jnp.bfloat16)
    for step in range(ITERS):
        owned = current[hub_rows]
        hub_pieces, hub_index = hub_gather(owned, block_rows, hub_blocks)
        low, high = rims(current, rim_rows)
        labels, current = spread(
            band_offsets, hub_index, current, low, high, hub_pieces, band_tiles, hub_tiles, degree, seeds
        )
    return labels


def solution(mesh):
    placed = (
        P(AXES, None),
        P(AXES),
        P(AXES, None),
        P(AXES, None, None, None),
        P(AXES, None),
        P(AXES, None, None, None),
        P(AXES),
    )
    return jax.shard_map(
        body, mesh=mesh, in_specs=placed, out_specs=P(AXES, None), check_vma=False
    )
```

time: 122 us -> 122 us (level)
  local copies, waits for them, and re-layouts: 41.2 us -> 13.4 us
  waiting for transfers between devices: 9.62 us -> 32.7 us
  Pallas kernels: 0 us -> 21.6 us
  matrix products: 14.7 us -> 0 us
  starting transfers between devices: 47.4 us -> 45 us
    pallas_call x0 -> x3, Pallas kernels: none -> 21.6 us  [spread(): pl.pallas_call(functools.partial(spread_kernel, n_hub), in_specs=[smem, s...]
    gather x8 -> x1, local copies, waits for them, and re-layouts: 18 us -> 1.37 us  [hub_gather(): return (pieces, jnp.asarray(where)[hub_blocks ^ me])]
    dot_general x6 -> x0, matrix products: 14.7 us -> none  [the longest x3 7.71 us: band_product(): jnp.einsum('bkij,bkjc->bic', tiles, extended[neighbour], preferred_elemen...]
    ppermute x21, waiting for transfers between devices: 9.6 us -> 21.5 us  [hub_gather(): lax.ppermute(buf, AXES, [(i, i ^ m) for i in range(count)])]
    ppermute x6, waiting for transfers between devices: 0.02 us -> 11.2 us  [the longest x3 11.2 us: rims(): lax.ppermute(lax.slice_in_dim(block, block.shape[0] - width, None, axis=0...]
    unnamed x34 -> x42, local copies, waits for them, and re-layouts: 12.9 us -> 3.06 us
    concatenate x6 -> x3, local copies, waits for them, and re-layouts: 7.95 us -> 0.06 us  [hub_gather(): buf = jnp.concatenate(pieces, 0)]
    ppermute x6, starting transfers between devices: 24.3 us -> 20.4 us  [the longest x3 14.6 us: rims(): lax.ppermute(lax.slice_in_dim(block, 0, width, axis=0), AXES, backward)]
  transfers between devices with their start and end apart: 27 -> 27, of which waited for: 6 -> 11; matrix products, arithmetic and copies ran while one was open for 27% -> 8% of each run, Pallas kernels for 0% -> 0%
where the time goes in v2:
time: 122 us; the launch traced here: 119 us
  starting transfers between devices  45 us (37%)
  waiting for transfers between devices  32.7 us (27%)
  Pallas kernels  21.6 us (18%)
  local copies, waits for them, and re-layouts  13.4 us (11%)
  other arithmetic  6.31 us (5%)
    ppermute x21, starting transfers between devices, hub_gather(): lax.ppermute(buf, AXES, [(i, i ^ m) for i in range(count)])  24.6 us
    pallas_call x3, Pallas kernels, spread(): pl.pallas_call(functools.partial(spread_kernel, n_hub), in_specs=[smem, s...  21.6 us
    ppermute x21, waiting for transfers between devices, hub_gather(): lax.ppermute(buf, AXES, [(i, i ^ m) for i in range(count)])  21.5 us
    ppermute x3, starting transfers between devices, rims(): lax.ppermute(lax.slice_in_dim(block, 0, width, axis=0), AXES, backward)  14.6 us
    ppermute x3, waiting for transfers between devices, rims(): lax.ppermute(lax.slice_in_dim(block, block.shape[0] - width, None, axis=0...  11.2 us
    ppermute x3, starting transfers between devices, rims(): lax.ppermute(lax.slice_in_dim(block, block.shape[0] - width, None, axis=0...  5.76 us
    gather x3, local copies, waits for them, and re-layouts, body(): owned = current[hub_rows]  3.98 us
    unnamed x42, local copies, waits for them, and re-layouts  3.06 us
  transfers between devices with their start and end apart: 27, of which 11 were waited for; matrix products, arithmetic and copies ran while one was open for 8% of the time, Pallas kernels for 0%

profile of v2, /device:TPU:5, one launch (start us, length us, event | category | flops | bytes accessed | tf_op | source)
XLA Modules:
  0.0 119.3 jit_solution(16402460653002220795)
XLA Ops:
  1.5 1.9 %convert_multiply_fusion = (f32[1024,128]{1,0:T(8,128)}, bf16[1024,128]{1,0:T(8,128)(2,1)S(1)}) fusion(bf16[1024,128]{1,0:T(8,128)(2,1)} %param.10, f32[1024]{0:T(1024)S(1)} %convert_element_type.15), kind=kLoop, calls=%fused_computation.6 | loop fusion | flops 393216 | bytes 1052672 | tf_op jit(solution)/shard_map/mul | solution.py:150
  4.2 3.4 %collective-permute-start.4 = (bf16[1,128,128]{2,1,0:T(8,128)(2,1)S(1)}, bf16[1,128,128]{2,1,0:T(8,128)(2,1)S(1)}, u32[]{:S(2)}, u32[]{:S(2)}) collective-permute-start(bf16[1,128,128]{2,1,0:T(8,128)(2,1)S(1)} %bitcast.7), channel_id=1, source_target_pairs={{0,3},{1,2},{2,1},{3,0},{4,7},{5,6},{6,5},{7,4},{8,11},{9,10},{10,... | collective-permute-start | bytes 98312 | tf_op jit(solution)/shard_map/ppermute | solution.py:46
  8.6 6.5 %collective-permute-start.1 = (bf16[256,128]{1,0:T(8,128)(2,1)}, bf16[256,128]{1,0:T(8,128)(2,1)}, u32[]{:S(2)}, u32[]{:S(2)}) collective-permute-start(bf16[256,128]{1,0:T(8,128)(2,1)} %get-tuple-element.17), channel_id=1, source_target_pairs={{1,0},{2,1},{3,2},{4,3},{5,4},{6,5},{7,6},{8,7},{9,8},{10,9},{11,1... | collective-permute-start | bytes 196616 | tf_op jit(solution)/shard_map/ppermute | solution.py:25
  15.1 1.9 %collective-permute-start = (bf16[256,128]{1,0:T(8,128)(2,1)}, bf16[256,128]{1,0:T(8,128)(2,1)}, u32[]{:S(2)}, u32[]{:S(2)}) collective-permute-start(bf16[256,128]{1,0:T(8,128)(2,1)} %get-tuple-element.18), channel_id=1, source_target_pairs={{0,1},{1,2},{2,3},{3,4},{4,5},{5,6},{6,7},{7,8},{8,9},{9,10},{10,1... | collective-permute-start | bytes 196616 | tf_op jit(solution)/shard_map/ppermute | solution.py:24
  22.0 5.3 %collective-permute-done.5 = bf16[4,128,128]{2,1,0:T(8,128)(2,1)S(1)} collective-permute-done((bf16[4,128,128]{2,1,0:T(8,128)(2,1)S(1)}, bf16[4,128,128]{2,1,0:T(8,128)(2,1)S(1)}, u32[]{:S(2)}, u32[]{:S(2)}) %collective-permute-start.5) | collective-permute-done | bytes 131104 | tf_op jit(solution)/shard_map/ppermute | solution.py:46
  27.3 1.7 %collective-permute-done.6 = bf16[4,128,128]{2,1,0:T(8,128)(2,1)S(1)} collective-permute-done((bf16[4,128,128]{2,1,0:T(8,128)(2,1)S(1)}, bf16[4,128,128]{2,1,0:T(8,128)(2,1)S(1)}, u32[]{:S(2)}, u32[]{:S(2)}) %collective-permute-start.6) | collective-permute-done | bytes 131104 | tf_op jit(solution)/shard_map/ppermute | solution.py:46
  29.6 1.7 %convert_reduce_fusion.1 = f32[8,128]{1,0:T(8,128)S(1)} fusion(bf16[8,6,128,128]{3,2,1,0:T(8,128)(2,1)} %rest_3_.5), kind=kLoop, calls=%fused_computation.5 | loop fusion | flops 1571840 | bytes 1576960 | tf_op jit(solution)/shard_map/reduce_sum | solution.py:151
  34.1 7.2 %shard_map.100 = (f32[1024,128]{1,0:T(8,128)}, bf16[1024,128]{1,0:T(8,128)(2,1)}) custom-call(s32[80]{0:T(128)} %reshape.34.off_ref, s32[48]{0:T(128)} %gather_fusion, bf16[1024,128]{1,0:T(8,128)(2,1)} %copy-done.2, bf16[256,128]{1,0:T(8,128)(2,1)} %collective-permute-done.low_hbm, bf16[256,128]{1,0:T(8,128)(2,1)} %collective-permute-done.1.high_hbm, ...), custom_call_target="tpu_custom_call" | custom-call | tf_op jit(solution)/shard_map/pallas_call | solution.py:119
  41.4 1.6 %gather_fusion.2 = bf16[128,128]{1,0:T(8,128)(2,1)S(1)} fusion(bf16[1024,128]{1,0:T(8,128)(2,1)} %get-tuple-element.8.cur_hbm, s32[1024]{0:T(1024)S(1)} %pad_clamp_fusion), kind=kCustom, calls=%fused_computation.2 | custom fusion | bytes 66048 | tf_op jit(solution)/shard_map/gather | solution.py:158
  43.0 2.6 %collective-permute-start.13 = (bf16[1,128,128]{2,1,0:T(8,128)(2,1)S(1)}, bf16[1,128,128]{2,1,0:T(8,128)(2,1)S(1)}, u32[]{:S(2)}, u32[]{:S(2)}) collective-permute-start(bf16[1,128,128]{2,1,0:T(8,128)(2,1)S(1)} %bitcast.15), channel_id=1, source_target_pairs={{0,3},{1,2},{2,1},{3,0},{4,7},{5,6},{6,5},{7,4},{8,11},{9,10},{10,... | collective-permute-start | bytes 98312 | tf_op jit(solution)/shard_map/ppermute | solution.py:46
  47.6 1.7 %collective-permute-done.12 = bf16[1,128,128]{2,1,0:T(8,128)(2,1)S(1)} collective-permute-done((bf16[1,128,128]{2,1,0:T(8,128)(2,1)S(1)}, bf16[1,128,128]{2,1,0:T(8,128)(2,1)S(1)}, u32[]{:S(2)}, u32[]{:S(2)}) %collective-permute-start.12) | collective-permute-done | bytes 32800 | tf_op jit(solution)/shard_map/ppermute | solution.py:46
  52.1 4.8 %collective-permute-done.14 = bf16[4,128,128]{2,1,0:T(8,128)(2,1)S(1)} collective-permute-done((bf16[4,128,128]{2,1,0:T(8,128)(2,1)S(1)}, bf16[4,128,128]{2,1,0:T(8,128)(2,1)S(1)}, u32[]{:S(2)}, u32[]{:S(2)}) %collective-permute-start.14) | collective-permute-done | bytes 131104 | tf_op jit(solution)/shard_map/ppermute | solution.py:46
  60.1 4.2 %collective-permute-start.10 = (bf16[256,128]{1,0:T(8,128)(2,1)S(1)}, bf16[256,128]{1,0:T(8,128)(2,1)S(1)}, u32[]{:S(2)}, u32[]{:S(2)}) collective-permute-start(bf16[256,128]{1,0:T(8,128)(2,1)S(1)} %get-tuple-element.15), channel_id=1, source_target_pairs={{1,0},{2,1},{3,2},{4,3},{5,4},{6,5},{7,6},{8,7},{9,8},{10,9},{11,1... | collective-permute-start | bytes 196616 | tf_op jit(solution)/shard_map/ppermute | solution.py:25
  64.2 1.9 %collective-permute-start.9 = (bf16[256,128]{1,0:T(8,128)(2,1)S(1)}, bf16[256,128]{1,0:T(8,128)(2,1)S(1)}, u32[]{:S(2)}, u32[]{:S(2)}) collective-permute-start(bf16[256,128]{1,0:T(8,128)(2,1)S(1)} %get-tuple-element.16), channel_id=1, source_target_pairs={{0,1},{1,2},{2,3},{3,4},{4,5},{5,6},{6,7},{7,8},{8,9},{9,10},{10,1... | collective-permute-start | bytes 196616 | tf_op jit(solution)/shard_map/ppermute | solution.py:24
  66.2 5.6 %collective-permute-done.9.low_hbm = bf16[256,128]{1,0:T(8,128)(2,1)S(1)} collective-permute-done((bf16[256,128]{1,0:T(8,128)(2,1)S(1)}, bf16[256,128]{1,0:T(8,128)(2,1)S(1)}, u32[]{:S(2)}, u32[]{:S(2)}) %collective-permute-start.9) | collective-permute-done | bytes 65568 | tf_op jit(solution)/shard_map/ppermute | solution.py:24
  73.2 7.2 %shard_map.101 = (f32[1024,128]{1,0:T(8,128)}, bf16[1024,128]{1,0:T(8,128)(2,1)}) custom-call(s32[80]{0:T(128)} %reshape.34.off_ref, s32[48]{0:T(128)} %gather_fusion, bf16[1024,128]{1,0:T(8,128)(2,1)} %get-tuple-element.8.cur_hbm, bf16[256,128]{1,0:T(8,128)(2,1)} %copy-done.11, bf16[256,128]{1,0:T(8,128)(2,1)} %copy-done.9, ...), custom_call_target="tpu_custom_call" | custom-call | tf_op jit(solution)/shard_map/pallas_call | solution.py:119
  80.4 1.6 %gather_fusion.3 = bf16[128,128]{1,0:T(8,128)(2,1)S(1)} fusion(bf16[1024,128]{1,0:T(8,128)(2,1)} %get-tuple-element.9.cur_hbm, s32[1024]{0:T(1024)S(1)} %pad_clamp_fusion), kind=kCustom, calls=%fused_computation.3 | custom fusion | bytes 66048 | tf_op jit(solution)/shard_map/gather | solution.py:158
  82.2 3.4 %collective-permute-start.20 = (bf16[1,128,128]{2,1,0:T(8,128)(2,1)S(1)}, bf16[1,128,128]{2,1,0:T(8,128)(2,1)S(1)}, u32[]{:S(2)}, u32[]{:S(2)}) collective-permute-start(bf16[1,128,128]{2,1,0:T(8,128)(2,1)S(1)} %bitcast.13), channel_id=1, source_target_pairs={{0,1},{1,0},{2,3},{3,2},{4,5},{5,4},{6,7},{7,6},{8,9},{9,8},{10,11... | collective-permute-start | bytes 98312 | tf_op jit(solution)/shard_map/ppermute | solution.py:46
  89.8 4.8 %collective-permute-done.23 = bf16[4,128,128]{2,1,0:T(8,128)(2,1)S(1)} collective-permute-done((bf16[4,128,128]{2,1,0:T(8,128)(2,1)S(1)}, bf16[4,128,128]{2,1,0:T(8,128)(2,1)S(1)}, u32[]{:S(2)}, u32[]{:S(2)}) %collective-permute-start.23) | collective-permute-done | bytes 131104 | tf_op jit(solution)/shard_map/ppermute | solution.py:46
  94.7 3.5 %collective-permute-start.26 = (bf16[16,128,128]{2,1,0:T(8,128)(2,1)S(1)}, bf16[16,128,128]{2,1,0:T(8,128)(2,1)S(1)}, u32[]{:S(2)}, u32[]{:S(2)}) collective-permute-start(bf16[16,128,128]{2,1,0:T(8,128)(2,1)S(1)} %constant_dynamic-update-slice_fusion.14.rest_0_), channel_id=1, source_target_pairs={{0,4},{1,5},{2,6},{3,7},{4,0},{5,1},{6,2},{7,3},{8,12},{9,13},{10,... | collective-permute-start | bytes 1572872 | tf_op jit(solution)/shard_map/ppermute | solution.py:46
  99.1 4.0 %collective-permute-start.19 = (bf16[256,128]{1,0:T(8,128)(2,1)S(1)}, bf16[256,128]{1,0:T(8,128)(2,1)S(1)}, u32[]{:S(2)}, u32[]{:S(2)}) collective-permute-start(bf16[256,128]{1,0:T(8,128)(2,1)S(1)} %get-tuple-element.13), channel_id=1, source_target_pairs={{1,0},{2,1},{3,2},{4,3},{5,4},{6,5},{7,6},{8,7},{9,8},{10,9},{11,1... | collective-permute-start | bytes 196616 | tf_op jit(solution)/shard_map/ppermute | solution.py:25
  103.1 1.9 %collective-permute-start.18 = (bf16[256,128]{1,0:T(8,128)(2,1)S(1)}, bf16[256,128]{1,0:T(8,128)(2,1)S(1)}, u32[]{:S(2)}, u32[]{:S(2)}) collective-permute-start(bf16[256,128]{1,0:T(8,128)(2,1)S(1)} %get-tuple-element.14), channel_id=1, source_target_pairs={{0,1},{1,2},{2,3},{3,4},{4,5},{5,6},{6,7},{7,8},{8,9},{9,10},{10,1... | collective-permute-start | bytes 196616 | tf_op jit(solution)/shard_map/ppermute | solution.py:24
  105.1 5.6 %collective-permute-done.18.low_hbm = bf16[256,128]{1,0:T(8,128)(2,1)S(1)} collective-permute-done((bf16[256,128]{1,0:T(8,128)(2,1)S(1)}, bf16[256,128]{1,0:T(8,128)(2,1)S(1)}, u32[]{:S(2)}, u32[]{:S(2)}) %collective-permute-start.18) | collective-permute-done | bytes 65568 | tf_op jit(solution)/shard_map/ppermute | solution.py:24
  112.1 7.2 %shard_map.102 = (f32[1024,128]{1,0:T(8,128)}, bf16[1024,128]{1,0:T(8,128)(2,1)}) custom-call(s32[80]{0:T(128)} %reshape.34.off_ref, s32[48]{0:T(128)} %gather_fusion, bf16[1024,128]{1,0:T(8,128)(2,1)} %get-tuple-element.9.cur_hbm, bf16[256,128]{1,0:T(8,128)(2,1)} %copy-done.10, bf16[256,128]{1,0:T(8,128)(2,1)} %copy-done.8, ...), custom_call_target="tpu_custom_call" | custom-call | tf_op jit(solution)/shard_map/pallas_call | solution.py:119
  (100 shorter events, 27.6 us)
Async XLA Ops:
  4.2 15.0 %collective-permute-start.4 = (bf16[1,128,128]{2,1,0:T(8,128)(2,1)S(1)}, bf16[1,128,128]{2,1,0:T(8,128)(2,1)S(1)}, u32[]{:S(2)}, u32[]{:S(2)}) collective-permute-start(bf16[1,128,128]{2,1,0:T(8,128)(2,1)S(1)} %bitcast.7), channel_id=1, source_target_pairs={{0,3},{1,2},{2,1},{3,0},{4,7},{5,6},{6,5},{7,4},{8,11},{9,10},{10,... | collective-permute-start | bytes 98312 | tf_op jit(solution)/shard_map/ppermute | solution.py:46
  7.5 11.6 %collective-permute-start.3 = (bf16[1,128,128]{2,1,0:T(8,128)(2,1)S(1)}, bf16[1,128,128]{2,1,0:T(8,128)(2,1)S(1)}, u32[]{:S(2)}, u32[]{:S(2)}) collective-permute-start(bf16[1,128,128]{2,1,0:T(8,128)(2,1)S(1)} %bitcast.8), channel_id=1, source_target_pairs={{0,2},{1,3},{2,0},{3,1},{4,6},{5,7},{6,4},{7,5},{8,10},{9,11},{10,... | collective-permute-start | bytes 98312 | tf_op jit(solution)/shard_map/ppermute | solution.py:46
  7.6 11.6 %collective-permute-start.2 = (bf16[1,128,128]{2,1,0:T(8,128)(2,1)S(1)}, bf16[1,128,128]{2,1,0:T(8,128)(2,1)S(1)}, u32[]{:S(2)}, u32[]{:S(2)}) collective-permute-start(bf16[1,128,128]{2,1,0:T(8,128)(2,1)S(1)} %bitcast.9), channel_id=1, source_target_pairs={{0,1},{1,0},{2,3},{3,2},{4,5},{5,4},{6,7},{7,6},{8,9},{9,8},{10,11... | collective-permute-start | bytes 98312 | tf_op jit(solution)/shard_map/ppermute | solution.py:46
  8.6 25.5 %collective-permute-start.1 = (bf16[256,128]{1,0:T(8,128)(2,1)}, bf16[256,128]{1,0:T(8,128)(2,1)}, u32[]{:S(2)}, u32[]{:S(2)}) collective-permute-start(bf16[256,128]{1,0:T(8,128)(2,1)} %get-tuple-element.17), channel_id=1, source_target_pairs={{1,0},{2,1},{3,2},{4,3},{5,4},{6,5},{7,6},{8,7},{9,8},{10,9},{11,1... | collective-permute-start | bytes 196616 | tf_op jit(solution)/shard_map/ppermute | solution.py:25
  15.1 19.0 %collective-permute-start = (bf16[256,128]{1,0:T(8,128)(2,1)}, bf16[256,128]{1,0:T(8,128)(2,1)}, u32[]{:S(2)}, u32[]{:S(2)}) collective-permute-start(bf16[256,128]{1,0:T(8,128)(2,1)} %get-tuple-element.18), channel_id=1, source_target_pairs={{0,1},{1,2},{2,3},{3,4},{4,5},{5,6},{6,7},{7,8},{8,9},{9,10},{10,1... | collective-permute-start | bytes 196616 | tf_op jit(solution)/shard_map/ppermute | solution.py:24
  19.2 9.8 %collective-permute-start.7 = (bf16[4,128,128]{2,1,0:T(8,128)(2,1)S(1)}, bf16[4,128,128]{2,1,0:T(8,128)(2,1)S(1)}, u32[]{:S(2)}, u32[]{:S(2)}) collective-permute-start(bf16[4,128,128]{2,1,0:T(8,128)(2,1)S(1)} %pad_maximum_fusion), channel_id=1, source_target_pairs={{0,24},{1,25},{2,26},{3,27},{4,28},{5,29},{6,30},{7,31},{8,16},{9,... | collective-permute-start | bytes 393224 | tf_op jit(solution)/shard_map/ppermute | solution.py:46
  20.4 8.6 %collective-permute-start.6 = (bf16[4,128,128]{2,1,0:T(8,128)(2,1)S(1)}, bf16[4,128,128]{2,1,0:T(8,128)(2,1)S(1)}, u32[]{:S(2)}, u32[]{:S(2)}) collective-permute-start(bf16[4,128,128]{2,1,0:T(8,128)(2,1)S(1)} %pad_maximum_fusion), channel_id=1, source_target_pairs={{0,16},{1,17},{2,18},{3,19},{4,20},{5,21},{6,22},{7,23},{8,24},{9,... | collective-permute-start | bytes 393224 | tf_op jit(solution)/shard_map/ppermute | solution.py:46
  21.7 5.6 %collective-permute-start.5 = (bf16[4,128,128]{2,1,0:T(8,128)(2,1)S(1)}, bf16[4,128,128]{2,1,0:T(8,128)(2,1)S(1)}, u32[]{:S(2)}, u32[]{:S(2)}) collective-permute-start(bf16[4,128,128]{2,1,0:T(8,128)(2,1)S(1)} %pad_maximum_fusion), channel_id=1, source_target_pairs={{0,8},{1,9},{2,10},{3,11},{4,12},{5,13},{6,14},{7,15},{8,0},{9,1},... | collective-permute-start | bytes 393224 | tf_op jit(solution)/shard_map/ppermute | solution.py:46
  29.1 5.0 %collective-permute-start.8 = (bf16[16,128,128]{2,1,0:T(8,128)(2,1)S(1)}, bf16[16,128,128]{2,1,0:T(8,128)(2,1)}, u32[]{:S(2)}, u32[]{:S(2)}) collective-permute-start(bf16[16,128,128]{2,1,0:T(8,128)(2,1)S(1)} %constant_dynamic-update-slice_fusion.rest_0_), channel_id=1, source_target_pairs={{0,4},{1,5},{2,6},{3,7},{4,0},{5,1},{6,2},{7,3},{8,12},{9,13},{10,... | collective-permute-start | bytes 1572872 | tf_op jit(solution)/shard_map/ppermute | solution.py:46
  43.0 4.6 %collective-permute-start.13 = (bf16[1,128,128]{2,1,0:T(8,128)(2,1)S(1)}, bf16[1,128,128]{2,1,0:T(8,128)(2,1)S(1)}, u32[]{:S(2)}, u32[]{:S(2)}) collective-permute-start(bf16[1,128,128]{2,1,0:T(8,128)(2,1)S(1)} %bitcast.15), channel_id=1, source_target_pairs={{0,3},{1,2},{2,1},{3,0},{4,7},{5,6},{6,5},{7,4},{8,11},{9,10},{10,... | collective-permute-start | bytes 98312 | tf_op jit(solution)/shard_map/ppermute | solution.py:46
  49.4 8.3 %collective-permute-start.16 = (bf16[4,128,128]{2,1,0:T(8,128)(2,1)S(1)}, bf16[4,128,128]{2,1,0:T(8,128)(2,1)S(1)}, u32[]{:S(2)}, u32[]{:S(2)}) collective-permute-start(bf16[4,128,128]{2,1,0:T(8,128)(2,1)S(1)} %pad_maximum_fusion.1), channel_id=1, source_target_pairs={{0,24},{1,25},{2,26},{3,27},{4,28},{5,29},{6,30},{7,31},{8,16},{9,... | collective-permute-start | bytes 393224 | tf_op jit(solution)/shard_map/ppermute | solution.py:46
  50.9 6.7 %collective-permute-start.15 = (bf16[4,128,128]{2,1,0:T(8,128)(2,1)S(1)}, bf16[4,128,128]{2,1,0:T(8,128)(2,1)S(1)}, u32[]{:S(2)}, u32[]{:S(2)}) collective-permute-start(bf16[4,128,128]{2,1,0:T(8,128)(2,1)S(1)} %pad_maximum_fusion.1), channel_id=1, source_target_pairs={{0,16},{1,17},{2,18},{3,19},{4,20},{5,21},{6,22},{7,23},{8,24},{9,... | collective-permute-start | bytes 393224 | tf_op jit(solution)/shard_map/ppermute | solution.py:46
  51.9 5.1 %collective-permute-start.14 = (bf16[4,128,128]{2,1,0:T(8,128)(2,1)S(1)}, bf16[4,128,128]{2,1,0:T(8,128)(2,1)S(1)}, u32[]{:S(2)}, u32[]{:S(2)}) collective-permute-start(bf16[4,128,128]{2,1,0:T(8,128)(2,1)S(1)} %pad_maximum_fusion.1), channel_id=1, source_target_pairs={{0,8},{1,9},{2,10},{3,11},{4,12},{5,13},{6,14},{7,15},{8,0},{9,1},... | collective-permute-start | bytes 393224 | tf_op jit(solution)/shard_map/ppermute | solution.py:46
  57.7 14.1 %collective-permute-start.17 = (bf16[16,128,128]{2,1,0:T(8,128)(2,1)S(1)}, bf16[16,128,128]{2,1,0:T(8,128)(2,1)S(1)}, u32[]{:S(2)}, u32[]{:S(2)}) collective-permute-start(bf16[16,128,128]{2,1,0:T(8,128)(2,1)S(1)} %constant_dynamic-update-slice_fusion.7.rest_0_), channel_id=1, source_target_pairs={{0,4},{1,5},{2,6},{3,7},{4,0},{5,1},{6,2},{7,3},{8,12},{9,13},{10,... | collective-permute-start | bytes 1572872 | tf_op jit(solution)/shard_map/ppermute | solution.py:46
  60.1 6.1 %collective-permute-start.10 = (bf16[256,128]{1,0:T(8,128)(2,1)S(1)}, bf16[256,128]{1,0:T(8,128)(2,1)S(1)}, u32[]{:S(2)}, u32[]{:S(2)}) collective-permute-start(bf16[256,128]{1,0:T(8,128)(2,1)S(1)} %get-tuple-element.15), channel_id=1, source_target_pairs={{1,0},{2,1},{3,2},{4,3},{5,4},{6,5},{7,6},{8,7},{9,8},{10,9},{11,1... | collective-permute-start | bytes 196616 | tf_op jit(solution)/shard_map/ppermute | solution.py:25
  64.2 7.6 %collective-permute-start.9 = (bf16[256,128]{1,0:T(8,128)(2,1)S(1)}, bf16[256,128]{1,0:T(8,128)(2,1)S(1)}, u32[]{:S(2)}, u32[]{:S(2)}) collective-permute-start(bf16[256,128]{1,0:T(8,128)(2,1)S(1)} %get-tuple-element.16), channel_id=1, source_target_pairs={{0,1},{1,2},{2,3},{3,4},{4,5},{5,6},{6,7},{7,8},{8,9},{9,10},{10,1... | collective-permute-start | bytes 196616 | tf_op jit(solution)/shard_map/ppermute | solution.py:24
  82.0 4.6 %collective-permute-start.22 = (bf16[1,128,128]{2,1,0:T(8,128)(2,1)S(1)}, bf16[1,128,128]{2,1,0:T(8,128)(2,1)S(1)}, u32[]{:S(2)}, u32[]{:S(2)}) collective-permute-start(bf16[1,128,128]{2,1,0:T(8,128)(2,1)S(1)} %bitcast.11), channel_id=1, source_target_pairs={{0,3},{1,2},{2,1},{3,0},{4,7},{5,6},{6,5},{7,4},{8,11},{9,10},{10,... | collective-permute-start | bytes 98312 | tf_op jit(solution)/shard_map/ppermute | solution.py:46
  82.2 4.8 %collective-permute-start.20 = (bf16[1,128,128]{2,1,0:T(8,128)(2,1)S(1)}, bf16[1,128,128]{2,1,0:T(8,128)(2,1)S(1)}, u32[]{:S(2)}, u32[]{:S(2)}) collective-permute-start(bf16[1,128,128]{2,1,0:T(8,128)(2,1)S(1)} %bitcast.13), channel_id=1, source_target_pairs={{0,1},{1,0},{2,3},{3,2},{4,5},{5,4},{6,7},{7,6},{8,9},{9,8},{10,11... | collective-permute-start | bytes 98312 | tf_op jit(solution)/shard_map/ppermute | solution.py:46
  87.0 7.6 %collective-permute-start.25 = (bf16[4,128,128]{2,1,0:T(8,128)(2,1)S(1)}, bf16[4,128,128]{2,1,0:T(8,128)(2,1)S(1)}, u32[]{:S(2)}, u32[]{:S(2)}) collective-permute-start(bf16[4,128,128]{2,1,0:T(8,128)(2,1)S(1)} %pad_maximum_fusion.2), channel_id=1, source_target_pairs={{0,24},{1,25},{2,26},{3,27},{4,28},{5,29},{6,30},{7,31},{8,16},{9,... | collective-permute-start | bytes 393224 | tf_op jit(solution)/shard_map/ppermute | solution.py:46
  88.2 6.4 %collective-permute-start.24 = (bf16[4,128,128]{2,1,0:T(8,128)(2,1)S(1)}, bf16[4,128,128]{2,1,0:T(8,128)(2,1)S(1)}, u32[]{:S(2)}, u32[]{:S(2)}) collective-permute-start(bf16[4,128,128]{2,1,0:T(8,128)(2,1)S(1)} %pad_maximum_fusion.2), channel_id=1, source_target_pairs={{0,16},{1,17},{2,18},{3,19},{4,20},{5,21},{6,22},{7,23},{8,24},{9,... | collective-permute-start | bytes 393224 | tf_op jit(solution)/shard_map/ppermute | solution.py:46
  88.8 5.8 %collective-permute-start.23 = (bf16[4,128,128]{2,1,0:T(8,128)(2,1)S(1)}, bf16[4,128,128]{2,1,0:T(8,128)(2,1)S(1)}, u32[]{:S(2)}, u32[]{:S(2)}) collective-permute-start(bf16[4,128,128]{2,1,0:T(8,128)(2,1)S(1)} %pad_maximum_fusion.2), channel_id=1, source_target_pairs={{0,8},{1,9},{2,10},{3,11},{4,12},{5,13},{6,14},{7,15},{8,0},{9,1},... | collective-permute-start | bytes 393224 | tf_op jit(solution)/shard_map/ppermute | solution.py:46
  94.7 16.0 %collective-permute-start.26 = (bf16[16,128,128]{2,1,0:T(8,128)(2,1)S(1)}, bf16[16,128,128]{2,1,0:T(8,128)(2,1)S(1)}, u32[]{:S(2)}, u32[]{:S(2)}) collective-permute-start(bf16[16,128,128]{2,1,0:T(8,128)(2,1)S(1)} %constant_dynamic-update-slice_fusion.14.rest_0_), channel_id=1, source_target_pairs={{0,4},{1,5},{2,6},{3,7},{4,0},{5,1},{6,2},{7,3},{8,12},{9,13},{10,... | collective-permute-start | bytes 1572872 | tf_op jit(solution)/shard_map/ppermute | solution.py:46
  99.1 6.0 %collective-permute-start.19 = (bf16[256,128]{1,0:T(8,128)(2,1)S(1)}, bf16[256,128]{1,0:T(8,128)(2,1)S(1)}, u32[]{:S(2)}, u32[]{:S(2)}) collective-permute-start(bf16[256,128]{1,0:T(8,128)(2,1)S(1)} %get-tuple-element.13), channel_id=1, source_target_pairs={{1,0},{2,1},{3,2},{4,3},{5,4},{6,5},{7,6},{8,7},{9,8},{10,9},{11,1... | collective-permute-start | bytes 196616 | tf_op jit(solution)/shard_map/ppermute | solution.py:25
  103.1 7.6 %collective-permute-start.18 = (bf16[256,128]{1,0:T(8,128)(2,1)S(1)}, bf16[256,128]{1,0:T(8,128)(2,1)S(1)}, u32[]{:S(2)}, u32[]{:S(2)}) collective-permute-start(bf16[256,128]{1,0:T(8,128)(2,1)S(1)} %get-tuple-element.14), channel_id=1, source_target_pairs={{0,1},{1,2},{2,3},{3,4},{4,5},{5,6},{6,7},{7,8},{8,9},{9,10},{10,1... | collective-permute-start | bytes 196616 | tf_op jit(solution)/shard_map/ppermute | solution.py:24
  (15 other events, 126.1 us)

commit v3 on v2

--- a/solution.py
+++ b/solution.py
@@ -34,25 +34,50 @@
 
 def hub_gather(owned, block_rows, hub_blocks):
     count = lax.axis_size(AXES)
+    hub_all = lax.all_gather(owned, AXES, axis=0, tiled=True)
+    return [hub_all.reshape(-1, block_rows, owned.shape[1])], hub_blocks
+
+
+def exchange(current, owned, block_rows, hub_blocks, width):
+    count = lax.axis_size(AXES)
     rounds = xor_rounds(count)
-    if rounds is None or owned.shape[0] != block_rows:
-        hub_all = lax.all_gather(owned, AXES, axis=0, tiled=True)
-        return [hub_all.reshape(-1, block_rows, owned.shape[1])], hub_blocks
+    if rounds is None or owned.shape[0] != block_rows or lax.axis_size("hub") != 4:
+        hub_pieces, hub_index = hub_gather(owned, block_rows, hub_blocks)
+        low, high = rims(current, width)
+        return hub_pieces, hub_index, low, high
     me = lax.axis_index(AXES)
-    buf = owned[None]
-    offs = [0]
-    pieces = [buf]
-    for r, group in enumerate(rounds):
+    z = lax.axis_index("hub")
+    top = current[current.shape[0] - width:]
+    bottom = current[:width]
+    rim1 = jnp.where(z % 2 == 0, top, bottom)
+    rim3 = jnp.where(z == 1, top, bottom)
+    rimc = jnp.where(z == 3, top, bottom)
+    pairs = lambda m: [(i, i ^ m) for i in range(count)]
+    r1 = lax.ppermute(jnp.concatenate([owned, rim1], 0), AXES, pairs(1))
+    r2 = lax.ppermute(owned, AXES, pairs(2))
+    r3 = lax.ppermute(jnp.concatenate([owned, rim3], 0), AXES, pairs(3))
+    groups = count // 4
+    cross = [(4 * g + 3, 4 * g + 4) for g in range(groups - 1)]
+    cross += [(4 * g + 4, 4 * g + 3) for g in range(groups - 1)]
+    rc = lax.ppermute(rimc, AXES, cross)
+    rows = owned.shape[0]
+    low = jnp.where(z == 0, rc, jnp.where(z == 2, r3[rows:], r1[rows:]))
+    high = jnp.where(z == 3, rc, jnp.where(z == 1, r3[rows:], r1[rows:]))
+    pieces = [owned[None], r1[None, :rows], r2[None], r3[None, :rows]]
+    offs = [0, 1, 2, 3]
+    assert tuple(rounds[0]) == (1, 2, 3)
+    buf = jnp.concatenate(pieces, 0)
+    for r, group in enumerate(rounds[1:]):
         recvs = [lax.ppermute(buf, AXES, [(i, i ^ m) for i in range(count)]) for m in group]
         offs = offs + [o ^ m for m in group for o in offs]
         pieces = [buf] + recvs
-        if r + 1 < len(rounds):
+        if r + 2 < len(rounds):
             buf = jnp.concatenate(pieces, 0)
     assert sorted(offs) == list(range(count))
     where = np.zeros(count, np.int32)
     for p, o in enumerate(offs):
         where[o] = p
-    return pieces, jnp.asarray(where)[hub_blocks ^ me]
+    return pieces, jnp.asarray(where)[hub_blocks ^ me], low, high
 
 
 def spread_kernel(n_hub, off_ref, hidx_ref, cur_hbm, low_hbm, high_hbm, *rest):
@@ -156,8 +181,7 @@
     current = seeds.astype(jnp.bfloat16)
     for step in range(ITERS):
         owned = current[hub_rows]
-        hub_pieces, hub_index = hub_gather(owned, block_rows, hub_blocks)
-        low, high = rims(current, rim_rows)
+        hub_pieces, hub_index, low, high = exchange(current, owned, block_rows, hub_blocks, rim_rows)
         labels, current = spread(
             band_offsets, hub_index, current, low, high, hub_pieces, band_tiles, hub_tiles, degree, seeds
         )

time: 122 us -> 117 us (0.959)
  starting transfers between devices: 45 us -> 32.1 us
  waiting for transfers between devices: 32.7 us -> 41.9 us
  local copies, waits for them, and re-layouts: 13.4 us -> 9.78 us
  other arithmetic: 6.31 us -> 9.68 us
    ppermute x27 -> x24, starting transfers between devices: 45 us -> 32.1 us  [the longest x12 11.4 us: exchange(): lax.ppermute(buf, AXES, [(i, i ^ m) for i in range(count)])]
    ppermute x27 -> x24, waiting for transfers between devices: 32.7 us -> 41.9 us  [the longest x12 19.2 us: exchange(): lax.ppermute(buf, AXES, [(i, i ^ m) for i in range(count)])]
    select_n x1 -> x7, other arithmetic: 0.69 us -> 3.81 us  [the longest x3 2.01 us: exchange(): high = jnp.where(z == 3, rc, jnp.where(z == 1, r3[rows:], r1[rows:]))]
    slice x3 -> x0, local copies, waits for them, and re-layouts: 2.44 us -> none  [rims(): lax.slice_in_dim(block, 0, width, axis=0)]
    reduce_sum x1, other arithmetic: 0.41 us -> 2.16 us  [body(): jnp.sum(band_tiles, axis=(1, 3), dtype=jnp.float32)]
    reduce_sum x1, other arithmetic: 1.68 us -> 0.28 us  [body(): jnp.sum(hub_tiles, axis=(1, 3), dtype=jnp.float32)]
    unnamed x42 -> x40, local copies, waits for them, and re-layouts: 3.06 us -> 2.63 us
  transfers between devices with their start and end apart: 27 -> 24, of which waited for: 11 -> 14; matrix products, arithmetic and copies ran while one was open for 8% -> 7% of each run, Pallas kernels for 0% -> 0%
where the time goes in v3:
time: 117 us; the launch traced here: 115 us
  waiting for transfers between devices  41.9 us (36%)
  starting transfers between devices  32.1 us (27%)
  Pallas kernels  21.6 us (18%)
  local copies, waits for them, and re-layouts  9.78 us (8%)
  other arithmetic  9.68 us (8%)
    pallas_call x3, Pallas kernels, spread(): pl.pallas_call(functools.partial(spread_kernel, n_hub), in_specs=[smem, s...  21.6 us
    ppermute x12, waiting for transfers between devices, exchange(): lax.ppermute(buf, AXES, [(i, i ^ m) for i in range(count)])  19.2 us
    ppermute x12, starting transfers between devices, exchange(): lax.ppermute(buf, AXES, [(i, i ^ m) for i in range(count)])  11.4 us
    ppermute x3, starting transfers between devices, exchange(): rc = lax.ppermute(rimc, AXES, cross)  9.63 us
    ppermute x3, waiting for transfers between devices, exchange(): rc = lax.ppermute(rimc, AXES, cross)  9.2 us
    ppermute x3, starting transfers between devices, exchange(): r3 = lax.ppermute(jnp.concatenate([owned, rim3], 0), AXES, pairs(3))  6.98 us
    ppermute x3, waiting for transfers between devices, exchange(): r1 = lax.ppermute(jnp.concatenate([owned, rim1], 0), AXES, pairs(1))  6.74 us
    ppermute x3, waiting for transfers between devices, exchange(): r3 = lax.ppermute(jnp.concatenate([owned, rim3], 0), AXES, pairs(3))  6.72 us
  transfers between devices with their start and end apart: 24, of which 14 were waited for; matrix products, arithmetic and copies ran while one was open for 7% of the time, Pallas kernels for 0%

profile of v3, /device:TPU:5, one launch (start us, length us, event | category | flops | bytes accessed | tf_op | source)
XLA Modules:
  0.0 115.3 jit_solution(6770601543851908964)
XLA Ops:
  1.4 1.9 %convert_multiply_fusion = (f32[1024,128]{1,0:T(8,128)}, bf16[1024,128]{1,0:T(8,128)(2,1)S(1)}) fusion(bf16[1024,128]{1,0:T(8,128)(2,1)} %param.10, f32[1024]{0:T(1024)S(1)} %convert_element_type.15), kind=kLoop, calls=%fused_computation.6 | loop fusion | flops 393216 | bytes 1052672 | tf_op jit(solution)/shard_map/mul | solution.py:175
  4.0 2.4 %collective-permute-start.3 = (bf16[128,128]{1,0:T(8,128)(2,1)S(1)}, bf16[128,128]{1,0:T(8,128)(2,1)S(1)}, u32[]{:S(2)}, u32[]{:S(2)}) collective-permute-start(bf16[128,128]{1,0:T(8,128)(2,1)S(1)} %gather_fusion.1), channel_id=1, source_target_pairs={{0,2},{1,3},{2,0},{3,1},{4,6},{5,7},{6,4},{7,5},{8,10},{9,11},{10,... | collective-permute-start | bytes 98312 | tf_op jit(solution)/shard_map/ppermute | solution.py:57
  6.4 3.8 %collective-permute-start = (bf16[256,128]{1,0:T(8,128)(2,1)S(1)}, bf16[256,128]{1,0:T(8,128)(2,1)S(1)}, u32[]{:S(2)}, u32[]{:S(2)}) collective-permute-start(bf16[256,128]{1,0:T(8,128)(2,1)S(1)} %get-tuple-element.27), channel_id=1, source_target_pairs={{3,4},{7,8},{11,12},{15,16},{19,20},{23,24},{27,28},{4,3},{8,7},{1... | collective-permute-start | bytes 196616 | tf_op jit(solution)/shard_map/ppermute | solution.py:62
  10.3 3.2 %collective-permute-start.1 = (bf16[384,128]{1,0:T(8,128)(2,1)S(1)}, bf16[384,128]{1,0:T(8,128)(2,1)S(1)}, u32[]{:S(2)}, u32[]{:S(2)}) collective-permute-start(bf16[384,128]{1,0:T(8,128)(2,1)S(1)} %get-tuple-element.32), channel_id=1, source_target_pairs={{0,3},{1,2},{2,1},{3,0},{4,7},{5,6},{6,5},{7,4},{8,11},{9,10},{10,... | collective-permute-start | bytes 294920 | tf_op jit(solution)/shard_map/ppermute | solution.py:58
  13.5 2.2 %convert_reduce_fusion = f32[8,128]{1,0:T(8,128)S(1)} fusion(bf16[8,10,128,128]{3,2,1,0:T(8,128)(2,1)} %rest_2_.5), kind=kLoop, calls=%fused_computation.4 | loop fusion | flops 2620416 | bytes 2625536 | tf_op jit(solution)/shard_map/reduce_sum | solution.py:176
  16.9 2.5 %collective-permute-done.2 = bf16[384,128]{1,0:T(8,128)(2,1)S(1)} collective-permute-done((bf16[384,128]{1,0:T(8,128)(2,1)S(1)}, bf16[384,128]{1,0:T(8,128)(2,1)S(1)}, u32[]{:S(2)}, u32[]{:S(2)}) %collective-permute-start.2) | collective-permute-done | bytes 98336 | tf_op jit(solution)/shard_map/ppermute | solution.py:56
  22.2 4.1 %collective-permute-done.4 = bf16[4,128,128]{2,1,0:T(8,128)(2,1)S(1)} collective-permute-done((bf16[4,128,128]{2,1,0:T(8,128)(2,1)S(1)}, bf16[4,128,128]{2,1,0:T(8,128)(2,1)S(1)}, u32[]{:S(2)}, u32[]{:S(2)}) %collective-permute-start.4) | collective-permute-done | bytes 131104 | tf_op jit(solution)/shard_map/ppermute | solution.py:71
  26.3 2.3 %collective-permute-done.5 = bf16[4,128,128]{2,1,0:T(8,128)(2,1)S(1)} collective-permute-done((bf16[4,128,128]{2,1,0:T(8,128)(2,1)S(1)}, bf16[4,128,128]{2,1,0:T(8,128)(2,1)S(1)}, u32[]{:S(2)}, u32[]{:S(2)}) %collective-permute-start.5) | collective-permute-done | bytes 131104 | tf_op jit(solution)/shard_map/ppermute | solution.py:71
  33.5 7.2 %shard_map.100 = (f32[1024,128]{1,0:T(8,128)}, bf16[1024,128]{1,0:T(8,128)(2,1)}) custom-call(s32[80]{0:T(128)} %reshape.34.off_ref, s32[48]{0:T(128)} %gather_fusion, bf16[1024,128]{1,0:T(8,128)(2,1)} %copy-done.2, bf16[256,128]{1,0:T(8,128)(2,1)} %get-tuple-element.24.low_hbm, bf16[256,128]{1,0:T(8,128)(2,1)} %get-tuple-element.23.high_hbm, ...), custom_call_target="tpu_custom_call" | custom-call | tf_op jit(solution)/shard_map/pallas_call | solution.py:144
  43.3 1.9 %collective-permute-start.9 = (bf16[384,128]{1,0:T(8,128)(2,1)S(1)}, bf16[384,128]{1,0:T(8,128)(2,1)S(1)}, u32[]{:S(2)}, u32[]{:S(2)}) collective-permute-start(bf16[384,128]{1,0:T(8,128)(2,1)S(1)} %get-tuple-element.30), channel_id=1, source_target_pairs={{0,3},{1,2},{2,1},{3,0},{4,7},{5,6},{6,5},{7,4},{8,11},{9,10},{10,... | collective-permute-start | bytes 294920 | tf_op jit(solution)/shard_map/ppermute | solution.py:58
  46.0 3.5 %collective-permute-done.9 = bf16[384,128]{1,0:T(8,128)(2,1)S(1)} collective-permute-done((bf16[384,128]{1,0:T(8,128)(2,1)S(1)}, bf16[384,128]{1,0:T(8,128)(2,1)S(1)}, u32[]{:S(2)}, u32[]{:S(2)}) %collective-permute-start.9) | collective-permute-done | bytes 98336 | tf_op jit(solution)/shard_map/ppermute | solution.py:58
  49.5 2.6 %collective-permute-done.10 = bf16[384,128]{1,0:T(8,128)(2,1)S(1)} collective-permute-done((bf16[384,128]{1,0:T(8,128)(2,1)S(1)}, bf16[384,128]{1,0:T(8,128)(2,1)S(1)}, u32[]{:S(2)}, u32[]{:S(2)}) %collective-permute-start.10) | collective-permute-done | bytes 98336 | tf_op jit(solution)/shard_map/ppermute | solution.py:56
  54.9 4.7 %collective-permute-done.12 = bf16[4,128,128]{2,1,0:T(8,128)(2,1)S(1)} collective-permute-done((bf16[4,128,128]{2,1,0:T(8,128)(2,1)S(1)}, bf16[4,128,128]{2,1,0:T(8,128)(2,1)S(1)}, u32[]{:S(2)}, u32[]{:S(2)}) %collective-permute-start.12) | collective-permute-done | bytes 131104 | tf_op jit(solution)/shard_map/ppermute | solution.py:71
  59.6 1.8 %collective-permute-done.13 = bf16[4,128,128]{2,1,0:T(8,128)(2,1)S(1)} collective-permute-done((bf16[4,128,128]{2,1,0:T(8,128)(2,1)S(1)}, bf16[4,128,128]{2,1,0:T(8,128)(2,1)S(1)}, u32[]{:S(2)}, u32[]{:S(2)}) %collective-permute-start.13) | collective-permute-done | bytes 131104 | tf_op jit(solution)/shard_map/ppermute | solution.py:71
  61.9 2.8 %collective-permute-start.8 = (bf16[256,128]{1,0:T(8,128)(2,1)S(1)}, bf16[256,128]{1,0:T(8,128)(2,1)S(1)}, u32[]{:S(2)}, u32[]{:S(2)}) collective-permute-start(bf16[256,128]{1,0:T(8,128)(2,1)S(1)} %get-tuple-element.22), channel_id=1, source_target_pairs={{3,4},{7,8},{11,12},{15,16},{19,20},{23,24},{27,28},{4,3},{8,7},{1... | collective-permute-start | bytes 196616 | tf_op jit(solution)/shard_map/ppermute | solution.py:62
  64.8 4.6 %collective-permute-done.8 = bf16[256,128]{1,0:T(8,128)(2,1)S(1)} collective-permute-done((bf16[256,128]{1,0:T(8,128)(2,1)S(1)}, bf16[256,128]{1,0:T(8,128)(2,1)S(1)}, u32[]{:S(2)}, u32[]{:S(2)}) %collective-permute-start.8) | collective-permute-done | bytes 65568 | tf_op jit(solution)/shard_map/ppermute | solution.py:62
  70.8 7.2 %shard_map.101 = (f32[1024,128]{1,0:T(8,128)}, bf16[1024,128]{1,0:T(8,128)(2,1)}) custom-call(s32[80]{0:T(128)} %reshape.34.off_ref, s32[48]{0:T(128)} %gather_fusion, bf16[1024,128]{1,0:T(8,128)(2,1)} %get-tuple-element.8.cur_hbm, bf16[256,128]{1,0:T(8,128)(2,1)} %get-tuple-element.19.low_hbm, bf16[256,128]{1,0:T(8,128)(2,1)} %get-tuple-element.18.high_hbm, ...), custom_call_target="tpu_custom_call" | custom-call | tf_op jit(solution)/shard_map/pallas_call | solution.py:144
  80.7 1.9 %collective-permute-start.17 = (bf16[384,128]{1,0:T(8,128)(2,1)S(1)}, bf16[384,128]{1,0:T(8,128)(2,1)S(1)}, u32[]{:S(2)}, u32[]{:S(2)}) collective-permute-start(bf16[384,128]{1,0:T(8,128)(2,1)S(1)} %get-tuple-element.28), channel_id=1, source_target_pairs={{0,3},{1,2},{2,1},{3,0},{4,7},{5,6},{6,5},{7,4},{8,11},{9,10},{10,... | collective-permute-start | bytes 294920 | tf_op jit(solution)/shard_map/ppermute | solution.py:58
  83.4 2.7 %collective-permute-done.17 = bf16[384,128]{1,0:T(8,128)(2,1)S(1)} collective-permute-done((bf16[384,128]{1,0:T(8,128)(2,1)S(1)}, bf16[384,128]{1,0:T(8,128)(2,1)S(1)}, u32[]{:S(2)}, u32[]{:S(2)}) %collective-permute-start.17) | collective-permute-done | bytes 98336 | tf_op jit(solution)/shard_map/ppermute | solution.py:58
  87.8 3.9 %collective-permute-start.22 = (bf16[4,128,128]{2,1,0:T(8,128)(2,1)S(1)}, bf16[4,128,128]{2,1,0:T(8,128)(2,1)S(1)}, u32[]{:S(2)}, u32[]{:S(2)}) collective-permute-start(bf16[4,128,128]{2,1,0:T(8,128)(2,1)S(1)} %pad_maximum_fusion.2), channel_id=1, source_target_pairs={{0,24},{1,25},{2,26},{3,27},{4,28},{5,29},{6,30},{7,31},{8,16},{9,... | collective-permute-start | bytes 393224 | tf_op jit(solution)/shard_map/ppermute | solution.py:71
  92.0 4.9 %collective-permute-done.20 = bf16[4,128,128]{2,1,0:T(8,128)(2,1)S(1)} collective-permute-done((bf16[4,128,128]{2,1,0:T(8,128)(2,1)S(1)}, bf16[4,128,128]{2,1,0:T(8,128)(2,1)S(1)}, u32[]{:S(2)}, u32[]{:S(2)}) %collective-permute-start.20) | collective-permute-done | bytes 131104 | tf_op jit(solution)/shard_map/ppermute | solution.py:71
  99.1 3.0 %collective-permute-start.16 = (bf16[256,128]{1,0:T(8,128)(2,1)S(1)}, bf16[256,128]{1,0:T(8,128)(2,1)S(1)}, u32[]{:S(2)}, u32[]{:S(2)}) collective-permute-start(bf16[256,128]{1,0:T(8,128)(2,1)S(1)} %get-tuple-element.17), channel_id=1, source_target_pairs={{3,4},{7,8},{11,12},{15,16},{19,20},{23,24},{27,28},{4,3},{8,7},{1... | collective-permute-start | bytes 196616 | tf_op jit(solution)/shard_map/ppermute | solution.py:62
  102.1 4.6 %collective-permute-done.16 = bf16[256,128]{1,0:T(8,128)(2,1)S(1)} collective-permute-done((bf16[256,128]{1,0:T(8,128)(2,1)S(1)}, bf16[256,128]{1,0:T(8,128)(2,1)S(1)}, u32[]{:S(2)}, u32[]{:S(2)}) %collective-permute-start.16) | collective-permute-done | bytes 65568 | tf_op jit(solution)/shard_map/ppermute | solution.py:62
  108.2 7.2 %shard_map.102 = (f32[1024,128]{1,0:T(8,128)}, bf16[1024,128]{1,0:T(8,128)(2,1)}) custom-call(s32[80]{0:T(128)} %reshape.34.off_ref, s32[48]{0:T(128)} %gather_fusion, bf16[1024,128]{1,0:T(8,128)(2,1)} %get-tuple-element.9.cur_hbm, bf16[256,128]{1,0:T(8,128)(2,1)} %get-tuple-element.14.low_hbm, bf16[256,128]{1,0:T(8,128)(2,1)} %get-tuple-element.13.high_hbm, ...), custom_call_target="tpu_custom_call" | custom-call | tf_op jit(solution)/shard_map/pallas_call | solution.py:144
  (104 shorter events, 28.3 us)
Async XLA Ops:
  4.0 15.4 %collective-permute-start.3 = (bf16[128,128]{1,0:T(8,128)(2,1)S(1)}, bf16[128,128]{1,0:T(8,128)(2,1)S(1)}, u32[]{:S(2)}, u32[]{:S(2)}) collective-permute-start(bf16[128,128]{1,0:T(8,128)(2,1)S(1)} %gather_fusion.1), channel_id=1, source_target_pairs={{0,2},{1,3},{2,0},{3,1},{4,6},{5,7},{6,4},{7,5},{8,10},{9,11},{10,... | collective-permute-start | bytes 98312 | tf_op jit(solution)/shard_map/ppermute | solution.py:57
  6.4 25.6 %collective-permute-start = (bf16[256,128]{1,0:T(8,128)(2,1)S(1)}, bf16[256,128]{1,0:T(8,128)(2,1)S(1)}, u32[]{:S(2)}, u32[]{:S(2)}) collective-permute-start(bf16[256,128]{1,0:T(8,128)(2,1)S(1)} %get-tuple-element.27), channel_id=1, source_target_pairs={{3,4},{7,8},{11,12},{15,16},{19,20},{23,24},{27,28},{4,3},{8,7},{1... | collective-permute-start | bytes 196616 | tf_op jit(solution)/shard_map/ppermute | solution.py:62
  10.3 6.7 %collective-permute-start.1 = (bf16[384,128]{1,0:T(8,128)(2,1)S(1)}, bf16[384,128]{1,0:T(8,128)(2,1)S(1)}, u32[]{:S(2)}, u32[]{:S(2)}) collective-permute-start(bf16[384,128]{1,0:T(8,128)(2,1)S(1)} %get-tuple-element.32), channel_id=1, source_target_pairs={{0,3},{1,2},{2,1},{3,0},{4,7},{5,6},{6,5},{7,4},{8,11},{9,10},{10,... | collective-permute-start | bytes 294920 | tf_op jit(solution)/shard_map/ppermute | solution.py:58
  13.5 6.0 %collective-permute-start.2 = (bf16[384,128]{1,0:T(8,128)(2,1)S(1)}, bf16[384,128]{1,0:T(8,128)(2,1)S(1)}, u32[]{:S(2)}, u32[]{:S(2)}) collective-permute-start(bf16[384,128]{1,0:T(8,128)(2,1)S(1)} %get-tuple-element.33), channel_id=1, source_target_pairs={{0,1},{1,0},{2,3},{3,2},{4,5},{5,4},{6,7},{7,6},{8,9},{9,8},{10,11... | collective-permute-start | bytes 294920 | tf_op jit(solution)/shard_map/ppermute | solution.py:56
  19.5 9.2 %collective-permute-start.6 = (bf16[4,128,128]{2,1,0:T(8,128)(2,1)S(1)}, bf16[4,128,128]{2,1,0:T(8,128)(2,1)S(1)}, u32[]{:S(2)}, u32[]{:S(2)}) collective-permute-start(bf16[4,128,128]{2,1,0:T(8,128)(2,1)S(1)} %pad_maximum_fusion), channel_id=1, source_target_pairs={{0,24},{1,25},{2,26},{3,27},{4,28},{5,29},{6,30},{7,31},{8,16},{9,... | collective-permute-start | bytes 393224 | tf_op jit(solution)/shard_map/ppermute | solution.py:71
  20.7 8.0 %collective-permute-start.5 = (bf16[4,128,128]{2,1,0:T(8,128)(2,1)S(1)}, bf16[4,128,128]{2,1,0:T(8,128)(2,1)S(1)}, u32[]{:S(2)}, u32[]{:S(2)}) collective-permute-start(bf16[4,128,128]{2,1,0:T(8,128)(2,1)S(1)} %pad_maximum_fusion), channel_id=1, source_target_pairs={{0,16},{1,17},{2,18},{3,19},{4,20},{5,21},{6,22},{7,23},{8,24},{9,... | collective-permute-start | bytes 393224 | tf_op jit(solution)/shard_map/ppermute | solution.py:71
  20.7 5.6 %collective-permute-start.4 = (bf16[4,128,128]{2,1,0:T(8,128)(2,1)S(1)}, bf16[4,128,128]{2,1,0:T(8,128)(2,1)S(1)}, u32[]{:S(2)}, u32[]{:S(2)}) collective-permute-start(bf16[4,128,128]{2,1,0:T(8,128)(2,1)S(1)} %pad_maximum_fusion), channel_id=1, source_target_pairs={{0,8},{1,9},{2,10},{3,11},{4,12},{5,13},{6,14},{7,15},{8,0},{9,1},... | collective-permute-start | bytes 393224 | tf_op jit(solution)/shard_map/ppermute | solution.py:71
  28.7 3.9 %collective-permute-start.7 = (bf16[16,128,128]{2,1,0:T(8,128)(2,1)S(1)}, bf16[16,128,128]{2,1,0:T(8,128)(2,1)S(1)}, u32[]{:S(2)}, u32[]{:S(2)}) collective-permute-start(bf16[16,128,128]{2,1,0:T(8,128)(2,1)S(1)} %constant_dynamic-update-slice_fusion.rest_0_), channel_id=1, source_target_pairs={{0,4},{1,5},{2,6},{3,7},{4,0},{5,1},{6,2},{7,3},{8,12},{9,13},{10,... | collective-permute-start | bytes 1572872 | tf_op jit(solution)/shard_map/ppermute | solution.py:71
  43.2 8.9 %collective-permute-start.11 = (bf16[128,128]{1,0:T(8,128)(2,1)S(1)}, bf16[128,128]{1,0:T(8,128)(2,1)S(1)}, u32[]{:S(2)}, u32[]{:S(2)}) collective-permute-start(bf16[128,128]{1,0:T(8,128)(2,1)S(1)} %gather_fusion.2), channel_id=1, source_target_pairs={{0,2},{1,3},{2,0},{3,1},{4,6},{5,7},{6,4},{7,5},{8,10},{9,11},{10,... | collective-permute-start | bytes 98312 | tf_op jit(solution)/shard_map/ppermute | solution.py:57
  43.3 6.1 %collective-permute-start.9 = (bf16[384,128]{1,0:T(8,128)(2,1)S(1)}, bf16[384,128]{1,0:T(8,128)(2,1)S(1)}, u32[]{:S(2)}, u32[]{:S(2)}) collective-permute-start(bf16[384,128]{1,0:T(8,128)(2,1)S(1)} %get-tuple-element.30), channel_id=1, source_target_pairs={{0,3},{1,2},{2,1},{3,0},{4,7},{5,6},{6,5},{7,4},{8,11},{9,10},{10,... | collective-permute-start | bytes 294920 | tf_op jit(solution)/shard_map/ppermute | solution.py:58
  45.2 6.9 %collective-permute-start.10 = (bf16[384,128]{1,0:T(8,128)(2,1)S(1)}, bf16[384,128]{1,0:T(8,128)(2,1)S(1)}, u32[]{:S(2)}, u32[]{:S(2)}) collective-permute-start(bf16[384,128]{1,0:T(8,128)(2,1)S(1)} %get-tuple-element.31), channel_id=1, source_target_pairs={{0,1},{1,0},{2,3},{3,2},{4,5},{5,4},{6,7},{7,6},{8,9},{9,8},{10,11... | collective-permute-start | bytes 294920 | tf_op jit(solution)/shard_map/ppermute | solution.py:56
  52.1 9.2 %collective-permute-start.14 = (bf16[4,128,128]{2,1,0:T(8,128)(2,1)S(1)}, bf16[4,128,128]{2,1,0:T(8,128)(2,1)S(1)}, u32[]{:S(2)}, u32[]{:S(2)}) collective-permute-start(bf16[4,128,128]{2,1,0:T(8,128)(2,1)S(1)} %pad_maximum_fusion.1), channel_id=1, source_target_pairs={{0,24},{1,25},{2,26},{3,27},{4,28},{5,29},{6,30},{7,31},{8,16},{9,... | collective-permute-start | bytes 393224 | tf_op jit(solution)/shard_map/ppermute | solution.py:71
  53.3 8.0 %collective-permute-start.13 = (bf16[4,128,128]{2,1,0:T(8,128)(2,1)S(1)}, bf16[4,128,128]{2,1,0:T(8,128)(2,1)S(1)}, u32[]{:S(2)}, u32[]{:S(2)}) collective-permute-start(bf16[4,128,128]{2,1,0:T(8,128)(2,1)S(1)} %pad_maximum_fusion.1), channel_id=1, source_target_pairs={{0,16},{1,17},{2,18},{3,19},{4,20},{5,21},{6,22},{7,23},{8,24},{9,... | collective-permute-start | bytes 393224 | tf_op jit(solution)/shard_map/ppermute | solution.py:71
  53.7 5.9 %collective-permute-start.12 = (bf16[4,128,128]{2,1,0:T(8,128)(2,1)S(1)}, bf16[4,128,128]{2,1,0:T(8,128)(2,1)S(1)}, u32[]{:S(2)}, u32[]{:S(2)}) collective-permute-start(bf16[4,128,128]{2,1,0:T(8,128)(2,1)S(1)} %pad_maximum_fusion.1), channel_id=1, source_target_pairs={{0,8},{1,9},{2,10},{3,11},{4,12},{5,13},{6,14},{7,15},{8,0},{9,1},... | collective-permute-start | bytes 393224 | tf_op jit(solution)/shard_map/ppermute | solution.py:71
  61.4 8.7 %collective-permute-start.15 = (bf16[16,128,128]{2,1,0:T(8,128)(2,1)S(1)}, bf16[16,128,128]{2,1,0:T(8,128)(2,1)S(1)}, u32[]{:S(2)}, u32[]{:S(2)}) collective-permute-start(bf16[16,128,128]{2,1,0:T(8,128)(2,1)S(1)} %constant_dynamic-update-slice_fusion.7.rest_0_), channel_id=1, source_target_pairs={{0,4},{1,5},{2,6},{3,7},{4,0},{5,1},{6,2},{7,3},{8,12},{9,13},{10,... | collective-permute-start | bytes 1572872 | tf_op jit(solution)/shard_map/ppermute | solution.py:71
  61.9 7.4 %collective-permute-start.8 = (bf16[256,128]{1,0:T(8,128)(2,1)S(1)}, bf16[256,128]{1,0:T(8,128)(2,1)S(1)}, u32[]{:S(2)}, u32[]{:S(2)}) collective-permute-start(bf16[256,128]{1,0:T(8,128)(2,1)S(1)} %get-tuple-element.22), channel_id=1, source_target_pairs={{3,4},{7,8},{11,12},{15,16},{19,20},{23,24},{27,28},{4,3},{8,7},{1... | collective-permute-start | bytes 196616 | tf_op jit(solution)/shard_map/ppermute | solution.py:62
  80.6 7.2 %collective-permute-start.19 = (bf16[128,128]{1,0:T(8,128)(2,1)S(1)}, bf16[128,128]{1,0:T(8,128)(2,1)S(1)}, u32[]{:S(2)}, u32[]{:S(2)}) collective-permute-start(bf16[128,128]{1,0:T(8,128)(2,1)S(1)} %gather_fusion.3), channel_id=1, source_target_pairs={{0,2},{1,3},{2,0},{3,1},{4,6},{5,7},{6,4},{7,5},{8,10},{9,11},{10,... | collective-permute-start | bytes 98312 | tf_op jit(solution)/shard_map/ppermute | solution.py:57
  80.7 5.4 %collective-permute-start.17 = (bf16[384,128]{1,0:T(8,128)(2,1)S(1)}, bf16[384,128]{1,0:T(8,128)(2,1)S(1)}, u32[]{:S(2)}, u32[]{:S(2)}) collective-permute-start(bf16[384,128]{1,0:T(8,128)(2,1)S(1)} %get-tuple-element.28), channel_id=1, source_target_pairs={{0,3},{1,2},{2,1},{3,0},{4,7},{5,6},{6,5},{7,4},{8,11},{9,10},{10,... | collective-permute-start | bytes 294920 | tf_op jit(solution)/shard_map/ppermute | solution.py:58
  82.6 5.1 %collective-permute-start.18 = (bf16[384,128]{1,0:T(8,128)(2,1)S(1)}, bf16[384,128]{1,0:T(8,128)(2,1)S(1)}, u32[]{:S(2)}, u32[]{:S(2)}) collective-permute-start(bf16[384,128]{1,0:T(8,128)(2,1)S(1)} %get-tuple-element.29), channel_id=1, source_target_pairs={{0,1},{1,0},{2,3},{3,2},{4,5},{5,4},{6,7},{7,6},{8,9},{9,8},{10,11... | collective-permute-start | bytes 294920 | tf_op jit(solution)/shard_map/ppermute | solution.py:56
  87.8 10.7 %collective-permute-start.22 = (bf16[4,128,128]{2,1,0:T(8,128)(2,1)S(1)}, bf16[4,128,128]{2,1,0:T(8,128)(2,1)S(1)}, u32[]{:S(2)}, u32[]{:S(2)}) collective-permute-start(bf16[4,128,128]{2,1,0:T(8,128)(2,1)S(1)} %pad_maximum_fusion.2), channel_id=1, source_target_pairs={{0,24},{1,25},{2,26},{3,27},{4,28},{5,29},{6,30},{7,31},{8,16},{9,... | collective-permute-start | bytes 393224 | tf_op jit(solution)/shard_map/ppermute | solution.py:71
  91.6 6.8 %collective-permute-start.21 = (bf16[4,128,128]{2,1,0:T(8,128)(2,1)S(1)}, bf16[4,128,128]{2,1,0:T(8,128)(2,1)S(1)}, u32[]{:S(2)}, u32[]{:S(2)}) collective-permute-start(bf16[4,128,128]{2,1,0:T(8,128)(2,1)S(1)} %pad_maximum_fusion.2), channel_id=1, source_target_pairs={{0,16},{1,17},{2,18},{3,19},{4,20},{5,21},{6,22},{7,23},{8,24},{9,... | collective-permute-start | bytes 393224 | tf_op jit(solution)/shard_map/ppermute | solution.py:71
  91.6 5.3 %collective-permute-start.20 = (bf16[4,128,128]{2,1,0:T(8,128)(2,1)S(1)}, bf16[4,128,128]{2,1,0:T(8,128)(2,1)S(1)}, u32[]{:S(2)}, u32[]{:S(2)}) collective-permute-start(bf16[4,128,128]{2,1,0:T(8,128)(2,1)S(1)} %pad_maximum_fusion.2), channel_id=1, source_target_pairs={{0,8},{1,9},{2,10},{3,11},{4,12},{5,13},{6,14},{7,15},{8,0},{9,1},... | collective-permute-start | bytes 393224 | tf_op jit(solution)/shard_map/ppermute | solution.py:71
  98.5 8.8 %collective-permute-start.23 = (bf16[16,128,128]{2,1,0:T(8,128)(2,1)S(1)}, bf16[16,128,128]{2,1,0:T(8,128)(2,1)S(1)}, u32[]{:S(2)}, u32[]{:S(2)}) collective-permute-start(bf16[16,128,128]{2,1,0:T(8,128)(2,1)S(1)} %constant_dynamic-update-slice_fusion.14.rest_0_), channel_id=1, source_target_pairs={{0,4},{1,5},{2,6},{3,7},{4,0},{5,1},{6,2},{7,3},{8,12},{9,13},{10,... | collective-permute-start | bytes 1572872 | tf_op jit(solution)/shard_map/ppermute | solution.py:71
  99.1 7.6 %collective-permute-start.16 = (bf16[256,128]{1,0:T(8,128)(2,1)S(1)}, bf16[256,128]{1,0:T(8,128)(2,1)S(1)}, u32[]{:S(2)}, u32[]{:S(2)}) collective-permute-start(bf16[256,128]{1,0:T(8,128)(2,1)S(1)} %get-tuple-element.17), channel_id=1, source_target_pairs={{3,4},{7,8},{11,12},{15,16},{19,20},{23,24},{27,28},{4,3},{8,7},{1... | collective-permute-start | bytes 196616 | tf_op jit(solution)/shard_map/ppermute | solution.py:62
  (11 other events, 124.0 us)

commit v4 on v1

v4 whole, which is shorter than its diff:
```python
import functools

import jax
import jax.numpy as jnp
import numpy as np
from jax import lax
from jax.experimental import pallas as pl
from jax.experimental.pallas import tpu as pltpu
from jax.sharding import PartitionSpec as P

BW = 2
ITERS = 3
AXES = ("node", "hub")
ROUNDS_32 = ((1, 2, 3), (8, 16, 24), (4,))


spread_weight = 0.8

SMEM = pl.BlockSpec(memory_space=pltpu.SMEM)
ANY = pl.BlockSpec(memory_space=pl.ANY)
VMEM = pl.BlockSpec(memory_space=pltpu.VMEM)


def fast_path(owned, block_rows):
    count = lax.axis_size(AXES)
    return count == 32 and owned.shape[0] == block_rows and lax.axis_size("hub") == 4


def payloads(current, owned, z, width):
    top = current[current.shape[0] - width:]
    bottom = current[:width]
    p1 = jnp.concatenate([owned, jnp.where(z % 2 == 0, top, bottom)], 0)
    p3 = jnp.concatenate([owned, jnp.where(z == 1, top, bottom)], 0)
    pc = jnp.where(z == 3, top, bottom)
    return p1, p3, pc


def exchange(current, owned, p1, p3, pc, hub_blocks, width, block_rows, middle):
    count = lax.axis_size(AXES)
    if not fast_path(owned, block_rows):
        forward = [(i, i + 1) for i in range(count - 1)]
        backward = [(target, source) for source, target in forward]
        low = lax.ppermute(current[current.shape[0] - width:], AXES, forward)
        high = lax.ppermute(current[:width], AXES, backward)
        hub_all = lax.all_gather(owned, AXES, axis=0, tiled=True)
        return middle((low, high)), [hub_all.reshape(-1, block_rows, owned.shape[1])], hub_blocks
    me = lax.axis_index(AXES)
    pairs = lambda m: [(i, i ^ m) for i in range(count)]
    r1 = lax.ppermute(p1, AXES, pairs(1))
    r2 = lax.ppermute(owned, AXES, pairs(2))
    r3 = lax.ppermute(p3, AXES, pairs(3))
    groups = count // 4
    cross = [(4 * g + 3, 4 * g + 4) for g in range(groups - 1)]
    cross += [(4 * g + 4, 4 * g + 3) for g in range(groups - 1)]
    rc = lax.ppermute(pc, AXES, cross)
    rows = block_rows
    buf = jnp.concatenate([owned[None], r1[None, :rows], r2[None], r3[None, :rows]], 0)
    offs = [0, 1, 2, 3]
    rounds = ROUNDS_32
    pieces = [buf]
    done = None
    for r, group in enumerate(rounds[1:]):
        recvs = [lax.ppermute(buf, AXES, pairs(m)) for m in group]
        if done is None:
            done, recvs = lax.optimization_barrier((middle((r1, r3, rc)), recvs))
        offs = offs + [o ^ m for m in group for o in offs]
        pieces = [buf] + recvs
        if r + 2 < len(rounds):
            buf = jnp.concatenate(pieces, 0)
    assert sorted(offs) == list(range(count))
    where = np.zeros(count, np.int32)
    for p, o in enumerate(offs):
        where[o] = p
    return done, pieces, jnp.asarray(where)[hub_blocks ^ me]


def band_kernel(fast, n_own, z_ref, off_ref, cur_hbm, *rest):
    if fast:
        r1_hbm, r3_hbm, rc_hbm, bt_hbm, out_ref, ext, bt, sem = rest
    else:
        low_hbm, high_hbm, bt_hbm, out_ref, ext, bt, sem = rest
    blocks, k_band, rows = bt.shape[0], bt.shape[1], bt.shape[2]
    own = cur_hbm.shape[0]
    width = (ext.shape[0] - own) // 2
    low_dst = ext.at[pl.ds(0, width)]
    high_dst = ext.at[pl.ds(width + own, width)]
    mid = pltpu.make_async_copy(cur_hbm, ext.at[pl.ds(width, own)], sem.at[1])
    band_copies = [pltpu.make_async_copy(bt_hbm.at[b], bt.at[b], sem.at[3 + b]) for b in range(blocks)]
    band_copies[0].start()
    mid.start()
    if fast:
        z = z_ref[0]
        low_r1 = pltpu.make_async_copy(r1_hbm.at[pl.ds(n_own, width)], low_dst, sem.at[0])
        low_r3 = pltpu.make_async_copy(r3_hbm.at[pl.ds(n_own, width)], low_dst, sem.at[0])
        low_rc = pltpu.make_async_copy(rc_hbm, low_dst, sem.at[0])
        high_r1 = pltpu.make_async_copy(r1_hbm.at[pl.ds(n_own, width)], high_dst, sem.at[2])
        high_r3 = pltpu.make_async_copy(r3_hbm.at[pl.ds(n_own, width)], high_dst, sem.at[2])
        high_rc = pltpu.make_async_copy(rc_hbm, high_dst, sem.at[2])

        @pl.when(z == 0)
        def _():
            low_rc.start()
            high_r1.start()

        @pl.when(z == 1)
        def _():
            low_r1.start()
            high_r3.start()

        @pl.when(z == 2)
        def _():
            low_r3.start()
            high_r1.start()

        @pl.when(z == 3)
        def _():
            low_r1.start()
            high_rc.start()

        low_wait, high_wait = low_rc, high_rc
    else:
        low_wait = pltpu.make_async_copy(low_hbm, low_dst, sem.at[0])
        high_wait = pltpu.make_async_copy(high_hbm, high_dst, sem.at[2])
        low_wait.start()
        high_wait.start()
    for b in range(1, blocks):
        band_copies[b].start()
    mid.wait()
    low_wait.wait()
    high_wait.wait()
    for b in range(blocks):
        band_copies[b].wait()
        acc = jnp.zeros((rows, out_ref.shape[1]), jnp.float32)
        for k in range(k_band):
            n = b + BW + off_ref[b * k_band + k]
            start = pl.multiple_of(n * rows, rows)
            acc = acc + jnp.dot(bt[b, k], ext[pl.ds(start, rows), :], preferred_element_type=jnp.float32)
        out_ref[pl.ds(b * rows, rows), :] = acc


def band_call(z, band_offsets, current, rim_sources, band_tiles, fast, n_own, width):
    blocks, k_band, rows, _ = band_tiles.shape
    classes = current.shape[1]
    flops = 2 * blocks * k_band * rows * rows * classes
    bytes_accessed = band_tiles.size * 2 + current.size * 2 * 2 + current.size * 4
    return pl.pallas_call(
        functools.partial(band_kernel, fast, n_own),
        cost_estimate=pl.CostEstimate(flops=flops, transcendentals=0, bytes_accessed=bytes_accessed),
        in_specs=[SMEM, SMEM] + [ANY] * (1 + len(rim_sources) + 1),
        out_specs=VMEM,
        out_shape=jax.ShapeDtypeStruct(current.shape, jnp.float32),
        scratch_shapes=[
            pltpu.VMEM((current.shape[0] + 2 * width, classes), current.dtype),
            pltpu.VMEM(band_tiles.shape, band_tiles.dtype),
            pltpu.SemaphoreType.DMA((3 + blocks,)),
        ],
    )(z, band_offsets.reshape(-1), current, *rim_sources, band_tiles)


def hub_kernel(n_hub, width, z_ref, hidx_ref, rows_ref, *rest):
    hub_hbm = rest[:n_hub]
    (ht_hbm, band_ref, deg_ref, seeds_ref,
     out_ref, cur_ref, owned_ref, p1_ref, p3_ref, pc_ref,
     hub, ht, own32, sem) = rest[n_hub:]
    blocks, k_hub, rows = ht.shape[0], ht.shape[1], ht.shape[2]
    own = cur_ref.shape[0]
    n_own = owned_ref.shape[0]
    hub_copies = [pltpu.make_async_copy(ht_hbm.at[b], ht.at[b], sem.at[n_hub + b]) for b in range(blocks)]
    hub_copies[0].start()
    copies = []
    at = 0
    for i, piece in enumerate(hub_hbm):
        n = piece.shape[0]
        copies.append(pltpu.make_async_copy(piece, hub.at[pl.ds(at, n)], sem.at[i]))
        at += n
    for c in copies:
        c.start()
    for b in range(1, blocks):
        hub_copies[b].start()
    for c in copies:
        c.wait()
    for b in range(blocks):
        hub_copies[b].wait()
        acc = jnp.zeros((rows, out_ref.shape[1]), jnp.float32)
        for h in range(k_hub):
            p = hidx_ref[b * k_hub + h]
            acc = acc + jnp.dot(ht[b, h], hub[p], preferred_element_type=jnp.float32)
        gathered = (band_ref[pl.ds(b * rows, rows), :] + acc) / deg_ref[pl.ds(b * rows, rows), :]
        labels = spread_weight * gathered + (1.0 - spread_weight) * seeds_ref[pl.ds(b * rows, rows), :]
        out_ref[pl.ds(b * rows, rows), :] = labels
        cur_ref[pl.ds(b * rows, rows), :] = labels.astype(cur_ref.dtype)

    def pick(j, carry):
        own32[pl.ds(j, 1), :] = out_ref[pl.ds(rows_ref[j], 1), :]
        return carry

    lax.fori_loop(0, n_own, pick, 0)
    owned = own32[...].astype(owned_ref.dtype)
    owned_ref[...] = owned
    p1_ref[pl.ds(0, n_own), :] = owned
    p3_ref[pl.ds(0, n_own), :] = owned
    z = z_ref[0]
    top = cur_ref[pl.ds(own - width, width), :]
    bottom = cur_ref[pl.ds(0, width), :]
    p1_ref[pl.ds(n_own, width), :] = jnp.where(z % 2 == 0, top, bottom)
    p3_ref[pl.ds(n_own, width), :] = jnp.where(z == 1, top, bottom)
    pc_ref[...] = jnp.where(z == 3, top, bottom)


def hub_call(z, hub_index, hub_rows, hub_pieces, hub_tiles, band, degree, seeds, width):
    blocks, k_hub, rows, _ = hub_tiles.shape
    classes = seeds.shape[1]
    n_hub = len(hub_pieces)
    n_hub_blocks = sum(p.shape[0] for p in hub_pieces)
    n_own = hub_rows.shape[0]
    bf = jnp.bfloat16
    flops = 2 * blocks * k_hub * rows * rows * classes
    bytes_accessed = hub_tiles.size * 2 + n_hub_blocks * rows * classes * 2 + seeds.size * 4 * 4
    return pl.pallas_call(
        functools.partial(hub_kernel, n_hub, width),
        cost_estimate=pl.CostEstimate(flops=flops, transcendentals=0, bytes_accessed=bytes_accessed),
        in_specs=[SMEM, SMEM, SMEM] + [ANY] * (n_hub + 1) + [VMEM, VMEM, VMEM],
        out_specs=[VMEM] * 6,
        out_shape=[
            jax.ShapeDtypeStruct(seeds.shape, jnp.float32),
            jax.ShapeDtypeStruct(seeds.shape, bf),
            jax.ShapeDtypeStruct((n_own, classes), bf),
            jax.ShapeDtypeStruct((n_own + width, classes), bf),
            jax.ShapeDtypeStruct((n_own + width, classes), bf),
            jax.ShapeDtypeStruct((width, classes), bf),
        ],
        scratch_shapes=[
            pltpu.VMEM((n_hub_blocks, rows, classes), bf),
            pltpu.VMEM(hub_tiles.shape, hub_tiles.dtype),
            pltpu.VMEM((n_own, classes), jnp.float32),
            pltpu.SemaphoreType.DMA((n_hub + blocks,)),
        ],
    )(z, hub_index.reshape(-1), hub_rows, *hub_pieces, hub_tiles, band, degree, seeds)


def body(seed_scores, seed_mask, band_offsets, band_tiles, hub_blocks, hub_tiles, hub_rows):
    block_rows = band_tiles.shape[2]
    seeds = seed_mask.astype(jnp.float32)[:, None] * seed_scores.astype(jnp.float32)
    degree = jnp.sum(band_tiles, axis=(1, 3), dtype=jnp.float32) + jnp.sum(
        hub_tiles, axis=(1, 3), dtype=jnp.float32
    )
    degree = degree.reshape(-1, 1)
    width = BW * block_rows
    z = lax.axis_index("hub").astype(jnp.int32).reshape(1)
    current = seeds.astype(jnp.bfloat16)
    owned = current[hub_rows]
    p1, p3, pc = payloads(current, owned, z[0], width)
    fast = fast_path(owned, block_rows)
    for step in range(ITERS):
        middle = functools.partial(
            band_call, z, band_offsets, current, band_tiles=band_tiles, fast=fast, n_own=owned.shape[0], width=width
        )
        band, hub_pieces, hub_index = exchange(
            current, owned, p1, p3, pc, hub_blocks, width, block_rows, lambda rims: middle(rims)
        )
        labels, current, owned, p1, p3, pc = hub_call(
            z, hub_index, hub_rows, hub_pieces, hub_tiles, band, degree, seeds, width
        )
    return labels


def solution(mesh):
    placed = (
        P(AXES, None),
        P(AXES),
        P(AXES, None),
        P(AXES, None, None, None),
        P(AXES, None),
        P(AXES, None, None, None),
        P(AXES),
    )
    return jax.shard_map(
        body, mesh=mesh, in_specs=placed, out_specs=P(AXES, None), check_vma=False
    )
```

time: 122 us -> 115 us (0.943)
  Pallas kernels: 0 us -> 34.8 us
  local copies, waits for them, and re-layouts: 41.2 us -> 14.7 us
  matrix products: 14.7 us -> 0 us
  starting transfers between devices: 47.4 us -> 37.9 us
  waiting for transfers between devices: 9.62 us -> 16.8 us
  other arithmetic: 6.98 us -> 8.4 us
    pallas_call x0 -> x6, Pallas kernels: none -> 34.8 us  [the longest x3 19.5 us: hub_call(): pl.pallas_call(functools.partial(hub_kernel, n_hub, width), cost_estimate...]
    gather x8 -> x1, local copies, waits for them, and re-layouts: 18 us -> 1.35 us  [exchange(): return (done, pieces, jnp.asarray(where)[hub_blocks ^ me])]
    dot_general x6 -> x0, matrix products: 14.7 us -> none  [the longest x3 7.71 us: band_product(): jnp.einsum('bkij,bkjc->bic', tiles, extended[neighbour], preferred_elemen...]
    ppermute x27 -> x24, starting transfers between devices: 47.4 us -> 37.9 us  [the longest x12 13.5 us: exchange(): recvs = [lax.ppermute(buf, AXES, pairs(m)) for m in group]]
    ppermute x27 -> x24, waiting for transfers between devices: 9.62 us -> 16.8 us  [the longest x3 11 us: exchange(): r3 = lax.ppermute(p3, AXES, pairs(3))]
    concatenate x6 -> x3, local copies, waits for them, and re-layouts: 7.95 us -> 0.96 us  [exchange(): buf = jnp.concatenate(pieces, 0)]
    unnamed x34 -> x52, local copies, waits for them, and re-layouts: 12.9 us -> 9.26 us
    concatenate x6 -> x4, other arithmetic: 0.14 us -> 2.3 us  [the longest x3 2.28 us: exchange(): jnp.concatenate([owned[None], r1[None, :rows], r2[None], r3[None, :rows]]...]
  transfers between devices with their start and end apart: 27 -> 24, of which waited for: 6 -> 7; matrix products, arithmetic and copies ran while one was open for 27% -> 11% of each run, Pallas kernels for 0% -> 14%
where the time goes in v4:
time: 115 us; the launch traced here: 113 us
  starting transfers between devices  37.9 us (33%)
  Pallas kernels  34.8 us (30%)
  waiting for transfers between devices  16.8 us (15%)
  local copies, waits for them, and re-layouts  14.7 us (13%)
  other arithmetic  8.4 us (7%)
    pallas_call x3, Pallas kernels, hub_call(): pl.pallas_call(functools.partial(hub_kernel, n_hub, width), cost_estimate...  19.5 us
    pallas_call x3, Pallas kernels, band_call(): pl.pallas_call(functools.partial(band_kernel, fast, n_own), cost_estimate...  15.3 us
    ppermute x12, starting transfers between devices, exchange(): recvs = [lax.ppermute(buf, AXES, pairs(m)) for m in group]  13.5 us
    ppermute x3, starting transfers between devices, exchange(): rc = lax.ppermute(pc, AXES, cross)  13.2 us
    ppermute x3, waiting for transfers between devices, exchange(): r3 = lax.ppermute(p3, AXES, pairs(3))  11 us
    unnamed x52, local copies, waits for them, and re-layouts  9.26 us
    ppermute x3, starting transfers between devices, exchange(): r3 = lax.ppermute(p3, AXES, pairs(3))  5.73 us
    ppermute x12, waiting for transfers between devices, exchange(): recvs = [lax.ppermute(buf, AXES, pairs(m)) for m in group]  3.27 us
  transfers between devices with their start and end apart: 24, of which 7 were waited for; matrix products, arithmetic and copies ran while one was open for 11% of the time, Pallas kernels for 14%

profile of v4, /device:TPU:5, one launch (start us, length us, event | category | flops | bytes accessed | tf_op | source)
XLA Modules:
  0.0 112.9 jit_solution(16968908026535191916)
XLA Ops:
  1.4 1.9 %convert_multiply_fusion = (f32[1024,128]{1,0:T(8,128)}, bf16[1024,128]{1,0:T(8,128)(2,1)S(1)}) fusion(bf16[1024,128]{1,0:T(8,128)(2,1)} %param.10, f32[1024]{0:T(1024)S(1)} %convert_element_type.15), kind=kLoop, calls=%fused_computation.4 | loop fusion | flops 393216 | bytes 1052672 | tf_op jit(solution)/shard_map/mul | solution.py:243
  4.0 2.4 %collective-permute-start.1 = (bf16[128,128]{1,0:T(8,128)(2,1)S(1)}, bf16[128,128]{1,0:T(8,128)(2,1)S(1)}, u32[]{:S(2)}, u32[]{:S(2)}) collective-permute-start(bf16[128,128]{1,0:T(8,128)(2,1)S(1)} %gather_fusion.1), channel_id=1, source_target_pairs={{0,2},{1,3},{2,0},{3,1},{4,6},{5,7},{6,4},{7,5},{8,10},{9,11},{10,... | collective-permute-start | bytes 98312 | tf_op jit(solution)/shard_map/ppermute | solution.py:50
  6.4 3.8 %collective-permute-start.3 = (bf16[256,128]{1,0:T(8,128)(2,1)S(1)}, bf16[256,128]{1,0:T(8,128)(2,1)S(1)}, u32[]{:S(2)}, u32[]{:S(2)}) collective-permute-start(bf16[256,128]{1,0:T(8,128)(2,1)S(1)} %get-tuple-element.53), channel_id=1, source_target_pairs={{3,4},{7,8},{11,12},{15,16},{19,20},{23,24},{27,28},{4,3},{8,7},{1... | collective-permute-start | bytes 196616 | tf_op jit(solution)/shard_map/ppermute | solution.py:55
  10.2 3.2 %collective-permute-start.2 = (bf16[384,128]{1,0:T(8,128)(2,1)S(1)}, bf16[384,128]{1,0:T(8,128)(2,1)S(1)}, u32[]{:S(2)}, u32[]{:S(2)}) collective-permute-start(bf16[384,128]{1,0:T(8,128)(2,1)S(1)} %get-tuple-element.56), channel_id=1, source_target_pairs={{0,3},{1,2},{2,1},{3,0},{4,7},{5,6},{6,5},{7,4},{8,11},{9,10},{10,... | collective-permute-start | bytes 294920 | tf_op jit(solution)/shard_map/ppermute | solution.py:51
  16.9 2.5 %collective-permute-done.rest_0_ = bf16[384,128]{1,0:T(8,128)(2,1)S(1)} collective-permute-done((bf16[384,128]{1,0:T(8,128)(2,1)S(1)}, bf16[384,128]{1,0:T(8,128)(2,1)S(1)}, u32[]{:S(2)}, u32[]{:S(2)}) %collective-permute-start) | collective-permute-done | bytes 98336 | tf_op jit(solution)/shard_map/ppermute | solution.py:49
  23.4 5.2 %shard_map.100.rest_3_ = f32[1024,128]{1,0:T(8,128)} custom-call(s32[1]{0:T(128)} %bitcast.z_ref, s32[80]{0:T(128)} %reshape.41.off_ref, bf16[1024,128]{1,0:T(8,128)(2,1)} %copy-done.2, bf16[384,128]{1,0:T(8,128)(2,1)} %copy-done.9, bf16[384,128]{1,0:T(8,128)(2,1)} %copy-done.8, bf16[256,128]{1,0:T(8,128)(2,1)} %copy-done.14, bf16[8,10,128,128]{3,2,1,0:T(8,128)(2,1)} %rest_3_.5), custom_call_target="tpu_custom_call" | custom-call | flops 335544320 | bytes 3670016 | tf_op jit(solution)/shard_map/pallas_call | solution.py:146
  33.5 1.7 %convert_reduce_fusion.1 = f32[8,128]{1,0:T(8,128)S(1)} fusion(bf16[8,6,128,128]{3,2,1,0:T(8,128)(2,1)} %rest_2_.5), kind=kLoop, calls=%fused_computation.3 | loop fusion | flops 1571840 | bytes 1576960 | tf_op jit(solution)/shard_map/reduce_sum | solution.py:244
  38.0 6.5 %shard_map.101 = (f32[1024,128]{1,0:T(8,128)}, bf16[1024,128]{1,0:T(8,128)(2,1)}, bf16[128,128]{1,0:T(8,128)(2,1)}, bf16[384,128]{1,0:T(8,128)(2,1)}, bf16[384,1...) custom-call(s32[1]{0:T(128)} %bitcast.z_ref, s32[48]{0:T(128)} %gather_fusion, s32[128]{0:T(128)} %rows_ref.5, ...), custom_call_target="tpu_custom_call" | custom-call | flops 201326592 | bytes 4718592 | tf_op jit(solution)/shard_map/pallas_call | solution.py:219
  46.8 4.7 %collective-permute-start.11 = (bf16[256,128]{1,0:T(8,128)(2,1)}, bf16[256,128]{1,0:T(8,128)(2,1)S(1)}, u32[]{:S(2)}, u32[]{:S(2)}) collective-permute-start(bf16[256,128]{1,0:T(8,128)(2,1)} %get-tuple-element.36), channel_id=1, source_target_pairs={{3,4},{7,8},{11,12},{15,16},{19,20},{23,24},{27,28},{4,3},{8,7},{1... | collective-permute-start | bytes 196616 | tf_op jit(solution)/shard_map/ppermute | solution.py:55
  51.5 1.7 %collective-permute-start.10 = (bf16[384,128]{1,0:T(8,128)(2,1)}, bf16[384,128]{1,0:T(8,128)(2,1)S(1)}, u32[]{:S(2)}, u32[]{:S(2)}) collective-permute-start(bf16[384,128]{1,0:T(8,128)(2,1)} %get-tuple-element.34), channel_id=1, source_target_pairs={{0,3},{1,2},{2,1},{3,0},{4,7},{5,6},{6,5},{7,4},{8,11},{9,10},{10,... | collective-permute-start | bytes 294920 | tf_op jit(solution)/shard_map/ppermute | solution.py:51
  53.2 3.8 %collective-permute-done.10.rest_1_ = bf16[384,128]{1,0:T(8,128)(2,1)S(1)} collective-permute-done((bf16[384,128]{1,0:T(8,128)(2,1)}, bf16[384,128]{1,0:T(8,128)(2,1)S(1)}, u32[]{:S(2)}, u32[]{:S(2)}) %collective-permute-start.10) | collective-permute-done | bytes 98336 | tf_op jit(solution)/shard_map/ppermute | solution.py:51
  57.8 2.0 %collective-permute-start.14 = (bf16[4,128,128]{2,1,0:T(8,128)(2,1)S(1)}, bf16[4,128,128]{2,1,0:T(8,128)(2,1)S(1)}, u32[]{:S(2)}, u32[]{:S(2)}) collective-permute-start(bf16[4,128,128]{2,1,0:T(8,128)(2,1)S(1)} %pad_maximum_fusion.1), channel_id=1, source_target_pairs={{0,24},{1,25},{2,26},{3,27},{4,28},{5,29},{6,30},{7,31},{8,16},{9,... | collective-permute-start | bytes 393224 | tf_op jit(solution)/shard_map/ppermute | solution.py:63
  61.2 5.1 %shard_map.102.rest_3_ = f32[1024,128]{1,0:T(8,128)} custom-call(s32[1]{0:T(128)} %bitcast.z_ref, s32[80]{0:T(128)} %reshape.41.off_ref, bf16[1024,128]{1,0:T(8,128)(2,1)} %get-tuple-element.35.cur_hbm, bf16[384,128]{1,0:T(8,128)(2,1)} %copy-done.11, bf16[384,128]{1,0:T(8,128)(2,1)} %copy-done.13, bf16[256,128]{1,0:T(8,128)(2,1)} %copy-done.16, ...), custom_call_target="tpu_custom_call" | custom-call | flops 335544320 | bytes 3670016 | tf_op jit(solution)/shard_map/pallas_call | solution.py:146
  67.1 2.7 %collective-permute-start.15 = (bf16[16,128,128]{2,1,0:T(8,128)(2,1)S(1)}, bf16[16,128,128]{2,1,0:T(8,128)(2,1)S(1)}, u32[]{:S(2)}, u32[]{:S(2)}) collective-permute-start(bf16[16,128,128]{2,1,0:T(8,128)(2,1)S(1)} %constant_dynamic-update-slice_fusion.7.rest_0_), channel_id=1, source_target_pairs={{0,4},{1,5},{2,6},{3,7},{4,0},{5,1},{6,2},{7,3},{8,12},{9,13},{10,... | collective-permute-start | bytes 1572872 | tf_op jit(solution)/shard_map/ppermute | solution.py:63
  69.8 1.5 %collective-permute-done.15.rest_1_ = bf16[16,128,128]{2,1,0:T(8,128)(2,1)S(1)} collective-permute-done((bf16[16,128,128]{2,1,0:T(8,128)(2,1)S(1)}, bf16[16,128,128]{2,1,0:T(8,128)(2,1)S(1)}, u32[]{:S(2)}, u32[]{:S(2)}) %collective-permute-start.15) | collective-permute-done | bytes 524320 | tf_op jit(solution)/shard_map/ppermute | solution.py:63
  72.2 6.5 %shard_map.103 = (f32[1024,128]{1,0:T(8,128)}, bf16[1024,128]{1,0:T(8,128)(2,1)}, bf16[128,128]{1,0:T(8,128)(2,1)}, bf16[384,128]{1,0:T(8,128)(2,1)}, bf16[384,1...) custom-call(s32[1]{0:T(128)} %bitcast.z_ref, s32[48]{0:T(128)} %gather_fusion, s32[128]{0:T(128)} %rows_ref.5, ...), custom_call_target="tpu_custom_call" | custom-call | flops 201326592 | bytes 4718592 | tf_op jit(solution)/shard_map/pallas_call | solution.py:219
  78.8 1.5 %collective-permute-start.16 = (bf16[384,128]{1,0:T(8,128)(2,1)}, bf16[384,128]{1,0:T(8,128)(2,1)S(1)}, u32[]{:S(2)}, u32[]{:S(2)}) collective-permute-start(bf16[384,128]{1,0:T(8,128)(2,1)} %get-tuple-element.42), channel_id=1, source_target_pairs={{0,1},{1,0},{2,3},{3,2},{4,5},{5,4},{6,7},{7,6},{8,9},{9,8},{10,11... | collective-permute-start | bytes 294920 | tf_op jit(solution)/shard_map/ppermute | solution.py:49
  81.1 4.7 %collective-permute-start.19 = (bf16[256,128]{1,0:T(8,128)(2,1)}, bf16[256,128]{1,0:T(8,128)(2,1)S(1)}, u32[]{:S(2)}, u32[]{:S(2)}) collective-permute-start(bf16[256,128]{1,0:T(8,128)(2,1)} %get-tuple-element.45), channel_id=1, source_target_pairs={{3,4},{7,8},{11,12},{15,16},{19,20},{23,24},{27,28},{4,3},{8,7},{1... | collective-permute-start | bytes 196616 | tf_op jit(solution)/shard_map/ppermute | solution.py:55
  86.7 5.8 %collective-permute-done.18.rest_1_ = bf16[384,128]{1,0:T(8,128)(2,1)S(1)} collective-permute-done((bf16[384,128]{1,0:T(8,128)(2,1)}, bf16[384,128]{1,0:T(8,128)(2,1)S(1)}, u32[]{:S(2)}, u32[]{:S(2)}) %collective-permute-start.18) | collective-permute-done | bytes 98336 | tf_op jit(solution)/shard_map/ppermute | solution.py:51
  94.2 1.7 %collective-permute-start.20 = (bf16[4,128,128]{2,1,0:T(8,128)(2,1)S(1)}, bf16[4,128,128]{2,1,0:T(8,128)(2,1)S(1)}, u32[]{:S(2)}, u32[]{:S(2)}) collective-permute-start(bf16[4,128,128]{2,1,0:T(8,128)(2,1)S(1)} %pad_maximum_fusion.2), channel_id=1, source_target_pairs={{0,8},{1,9},{2,10},{3,11},{4,12},{5,13},{6,14},{7,15},{8,0},{9,1},... | collective-permute-start | bytes 393224 | tf_op jit(solution)/shard_map/ppermute | solution.py:63
  96.6 5.0 %shard_map.104.rest_3_ = f32[1024,128]{1,0:T(8,128)} custom-call(s32[1]{0:T(128)} %bitcast.z_ref, s32[80]{0:T(128)} %reshape.41.off_ref, bf16[1024,128]{1,0:T(8,128)(2,1)} %get-tuple-element.44.cur_hbm, bf16[384,128]{1,0:T(8,128)(2,1)} %copy-done.10, bf16[384,128]{1,0:T(8,128)(2,1)} %copy-done.12, bf16[256,128]{1,0:T(8,128)(2,1)} %copy-done.15, ...), custom_call_target="tpu_custom_call" | custom-call | flops 335544320 | bytes 3670016 | tf_op jit(solution)/shard_map/pallas_call | solution.py:146
  102.5 1.6 %collective-permute-start.23 = (bf16[16,128,128]{2,1,0:T(8,128)(2,1)S(1)}, bf16[16,128,128]{2,1,0:T(8,128)(2,1)S(1)}, u32[]{:S(2)}, u32[]{:S(2)}) collective-permute-start(bf16[16,128,128]{2,1,0:T(8,128)(2,1)S(1)} %constant_dynamic-update-slice_fusion.14.rest_0_), channel_id=1, source_target_pairs={{0,4},{1,5},{2,6},{3,7},{4,0},{5,1},{6,2},{7,3},{8,12},{9,13},{10,... | collective-permute-start | bytes 1572872 | tf_op jit(solution)/shard_map/ppermute | solution.py:63
  104.1 1.5 %collective-permute-done.23.rest_1_ = bf16[16,128,128]{2,1,0:T(8,128)(2,1)S(1)} collective-permute-done((bf16[16,128,128]{2,1,0:T(8,128)(2,1)S(1)}, bf16[16,128,128]{2,1,0:T(8,128)(2,1)S(1)}, u32[]{:S(2)}, u32[]{:S(2)}) %collective-permute-start.23) | collective-permute-done | bytes 524320 | tf_op jit(solution)/shard_map/ppermute | solution.py:63
  106.5 6.5 %shard_map.105 = (f32[1024,128]{1,0:T(8,128)}, bf16[1024,128]{1,0:T(8,128)(2,1)}, bf16[128,128]{1,0:T(8,128)(2,1)}, bf16[384,128]{1,0:T(8,128)(2,1)}, bf16[384,1...) custom-call(s32[1]{0:T(128)} %bitcast.z_ref, s32[48]{0:T(128)} %gather_fusion, s32[128]{0:T(128)} %rows_ref.5, ...), custom_call_target="tpu_custom_call" | custom-call | flops 201326592 | bytes 4718592 | tf_op jit(solution)/shard_map/pallas_call | solution.py:219
  (110 shorter events, 28.9 us)
Async XLA Ops:
  4.0 15.4 %collective-permute-start.1 = (bf16[128,128]{1,0:T(8,128)(2,1)S(1)}, bf16[128,128]{1,0:T(8,128)(2,1)S(1)}, u32[]{:S(2)}, u32[]{:S(2)}) collective-permute-start(bf16[128,128]{1,0:T(8,128)(2,1)S(1)} %gather_fusion.1), channel_id=1, source_target_pairs={{0,2},{1,3},{2,0},{3,1},{4,6},{5,7},{6,4},{7,5},{8,10},{9,11},{10,... | collective-permute-start | bytes 98312 | tf_op jit(solution)/shard_map/ppermute | solution.py:50
  6.4 16.4 %collective-permute-start.3 = (bf16[256,128]{1,0:T(8,128)(2,1)S(1)}, bf16[256,128]{1,0:T(8,128)(2,1)S(1)}, u32[]{:S(2)}, u32[]{:S(2)}) collective-permute-start(bf16[256,128]{1,0:T(8,128)(2,1)S(1)} %get-tuple-element.53), channel_id=1, source_target_pairs={{3,4},{7,8},{11,12},{15,16},{19,20},{23,24},{27,28},{4,3},{8,7},{1... | collective-permute-start | bytes 196616 | tf_op jit(solution)/shard_map/ppermute | solution.py:55
  10.2 6.7 %collective-permute-start.2 = (bf16[384,128]{1,0:T(8,128)(2,1)S(1)}, bf16[384,128]{1,0:T(8,128)(2,1)S(1)}, u32[]{:S(2)}, u32[]{:S(2)}) collective-permute-start(bf16[384,128]{1,0:T(8,128)(2,1)S(1)} %get-tuple-element.56), channel_id=1, source_target_pairs={{0,3},{1,2},{2,1},{3,0},{4,7},{5,6},{6,5},{7,4},{8,11},{9,10},{10,... | collective-permute-start | bytes 294920 | tf_op jit(solution)/shard_map/ppermute | solution.py:51
  13.4 6.0 %collective-permute-start = (bf16[384,128]{1,0:T(8,128)(2,1)S(1)}, bf16[384,128]{1,0:T(8,128)(2,1)S(1)}, u32[]{:S(2)}, u32[]{:S(2)}) collective-permute-start(bf16[384,128]{1,0:T(8,128)(2,1)S(1)} %get-tuple-element.57), channel_id=1, source_target_pairs={{0,1},{1,0},{2,3},{3,2},{4,5},{5,4},{6,7},{7,6},{8,9},{9,8},{10,11... | collective-permute-start | bytes 294920 | tf_op jit(solution)/shard_map/ppermute | solution.py:49
  20.1 9.3 %collective-permute-start.6 = (bf16[4,128,128]{2,1,0:T(8,128)(2,1)}, bf16[4,128,128]{2,1,0:T(8,128)(2,1)}, u32[]{:S(2)}, u32[]{:S(2)}) collective-permute-start(bf16[4,128,128]{2,1,0:T(8,128)(2,1)} %pad_maximum_fusion), channel_id=1, source_target_pairs={{0,24},{1,25},{2,26},{3,27},{4,28},{5,29},{6,30},{7,31},{8,16},{9,... | collective-permute-start | bytes 393224 | tf_op jit(solution)/shard_map/ppermute | solution.py:63
  21.3 8.3 %collective-permute-start.5 = (bf16[4,128,128]{2,1,0:T(8,128)(2,1)}, bf16[4,128,128]{2,1,0:T(8,128)(2,1)}, u32[]{:S(2)}, u32[]{:S(2)}) collective-permute-start(bf16[4,128,128]{2,1,0:T(8,128)(2,1)} %pad_maximum_fusion), channel_id=1, source_target_pairs={{0,16},{1,17},{2,18},{3,19},{4,20},{5,21},{6,22},{7,23},{8,24},{9,... | collective-permute-start | bytes 393224 | tf_op jit(solution)/shard_map/ppermute | solution.py:63
  21.3 8.3 %collective-permute-start.4 = (bf16[4,128,128]{2,1,0:T(8,128)(2,1)}, bf16[4,128,128]{2,1,0:T(8,128)(2,1)}, u32[]{:S(2)}, u32[]{:S(2)}) collective-permute-start(bf16[4,128,128]{2,1,0:T(8,128)(2,1)} %pad_maximum_fusion), channel_id=1, source_target_pairs={{0,8},{1,9},{2,10},{3,11},{4,12},{5,13},{6,14},{7,15},{8,0},{9,1},... | collective-permute-start | bytes 393224 | tf_op jit(solution)/shard_map/ppermute | solution.py:63
  32.4 5.7 %collective-permute-start.7 = (bf16[16,128,128]{2,1,0:T(8,128)(2,1)S(1)}, bf16[16,128,128]{2,1,0:T(8,128)(2,1)}, u32[]{:S(2)}, u32[]{:S(2)}) collective-permute-start(bf16[16,128,128]{2,1,0:T(8,128)(2,1)S(1)} %constant_dynamic-update-slice_fusion.rest_0_), channel_id=1, source_target_pairs={{0,4},{1,5},{2,6},{3,7},{4,0},{5,1},{6,2},{7,3},{8,12},{9,13},{10,... | collective-permute-start | bytes 1572872 | tf_op jit(solution)/shard_map/ppermute | solution.py:63
  44.6 12.4 %collective-permute-start.9 = (bf16[128,128]{1,0:T(8,128)(2,1)}, bf16[128,128]{1,0:T(8,128)(2,1)S(1)}, u32[]{:S(2)}, u32[]{:S(2)}) collective-permute-start(bf16[128,128]{1,0:T(8,128)(2,1)} %get-tuple-element.32), channel_id=1, source_target_pairs={{0,2},{1,3},{2,0},{3,1},{4,6},{5,7},{6,4},{7,5},{8,10},{9,11},{10,... | collective-permute-start | bytes 98312 | tf_op jit(solution)/shard_map/ppermute | solution.py:50
  45.0 8.2 %collective-permute-start.8 = (bf16[384,128]{1,0:T(8,128)(2,1)}, bf16[384,128]{1,0:T(8,128)(2,1)S(1)}, u32[]{:S(2)}, u32[]{:S(2)}) collective-permute-start(bf16[384,128]{1,0:T(8,128)(2,1)} %get-tuple-element.33), channel_id=1, source_target_pairs={{0,1},{1,0},{2,3},{3,2},{4,5},{5,4},{6,7},{7,6},{8,9},{9,8},{10,11... | collective-permute-start | bytes 294920 | tf_op jit(solution)/shard_map/ppermute | solution.py:49
  46.8 13.8 %collective-permute-start.11 = (bf16[256,128]{1,0:T(8,128)(2,1)}, bf16[256,128]{1,0:T(8,128)(2,1)S(1)}, u32[]{:S(2)}, u32[]{:S(2)}) collective-permute-start(bf16[256,128]{1,0:T(8,128)(2,1)} %get-tuple-element.36), channel_id=1, source_target_pairs={{3,4},{7,8},{11,12},{15,16},{19,20},{23,24},{27,28},{4,3},{8,7},{1... | collective-permute-start | bytes 196616 | tf_op jit(solution)/shard_map/ppermute | solution.py:55
  51.5 5.5 %collective-permute-start.10 = (bf16[384,128]{1,0:T(8,128)(2,1)}, bf16[384,128]{1,0:T(8,128)(2,1)S(1)}, u32[]{:S(2)}, u32[]{:S(2)}) collective-permute-start(bf16[384,128]{1,0:T(8,128)(2,1)} %get-tuple-element.34), channel_id=1, source_target_pairs={{0,3},{1,2},{2,1},{3,0},{4,7},{5,6},{6,5},{7,4},{8,11},{9,10},{10,... | collective-permute-start | bytes 294920 | tf_op jit(solution)/shard_map/ppermute | solution.py:51
  57.8 9.2 %collective-permute-start.14 = (bf16[4,128,128]{2,1,0:T(8,128)(2,1)S(1)}, bf16[4,128,128]{2,1,0:T(8,128)(2,1)S(1)}, u32[]{:S(2)}, u32[]{:S(2)}) collective-permute-start(bf16[4,128,128]{2,1,0:T(8,128)(2,1)S(1)} %pad_maximum_fusion.1), channel_id=1, source_target_pairs={{0,24},{1,25},{2,26},{3,27},{4,28},{5,29},{6,30},{7,31},{8,16},{9,... | collective-permute-start | bytes 393224 | tf_op jit(solution)/shard_map/ppermute | solution.py:63
  59.8 7.2 %collective-permute-start.13 = (bf16[4,128,128]{2,1,0:T(8,128)(2,1)S(1)}, bf16[4,128,128]{2,1,0:T(8,128)(2,1)S(1)}, u32[]{:S(2)}, u32[]{:S(2)}) collective-permute-start(bf16[4,128,128]{2,1,0:T(8,128)(2,1)S(1)} %pad_maximum_fusion.1), channel_id=1, source_target_pairs={{0,16},{1,17},{2,18},{3,19},{4,20},{5,21},{6,22},{7,23},{8,24},{9,... | collective-permute-start | bytes 393224 | tf_op jit(solution)/shard_map/ppermute | solution.py:63
  59.8 7.2 %collective-permute-start.12 = (bf16[4,128,128]{2,1,0:T(8,128)(2,1)S(1)}, bf16[4,128,128]{2,1,0:T(8,128)(2,1)S(1)}, u32[]{:S(2)}, u32[]{:S(2)}) collective-permute-start(bf16[4,128,128]{2,1,0:T(8,128)(2,1)S(1)} %pad_maximum_fusion.1), channel_id=1, source_target_pairs={{0,8},{1,9},{2,10},{3,11},{4,12},{5,13},{6,14},{7,15},{8,0},{9,1},... | collective-permute-start | bytes 393224 | tf_op jit(solution)/shard_map/ppermute | solution.py:63
  67.1 4.3 %collective-permute-start.15 = (bf16[16,128,128]{2,1,0:T(8,128)(2,1)S(1)}, bf16[16,128,128]{2,1,0:T(8,128)(2,1)S(1)}, u32[]{:S(2)}, u32[]{:S(2)}) collective-permute-start(bf16[16,128,128]{2,1,0:T(8,128)(2,1)S(1)} %constant_dynamic-update-slice_fusion.7.rest_0_), channel_id=1, source_target_pairs={{0,4},{1,5},{2,6},{3,7},{4,0},{5,1},{6,2},{7,3},{8,12},{9,13},{10,... | collective-permute-start | bytes 1572872 | tf_op jit(solution)/shard_map/ppermute | solution.py:63
  78.7 13.7 %collective-permute-start.17 = (bf16[128,128]{1,0:T(8,128)(2,1)}, bf16[128,128]{1,0:T(8,128)(2,1)S(1)}, u32[]{:S(2)}, u32[]{:S(2)}) collective-permute-start(bf16[128,128]{1,0:T(8,128)(2,1)} %get-tuple-element.41), channel_id=1, source_target_pairs={{0,2},{1,3},{2,0},{3,1},{4,6},{5,7},{6,4},{7,5},{8,10},{9,11},{10,... | collective-permute-start | bytes 98312 | tf_op jit(solution)/shard_map/ppermute | solution.py:50
  78.8 7.9 %collective-permute-start.16 = (bf16[384,128]{1,0:T(8,128)(2,1)}, bf16[384,128]{1,0:T(8,128)(2,1)S(1)}, u32[]{:S(2)}, u32[]{:S(2)}) collective-permute-start(bf16[384,128]{1,0:T(8,128)(2,1)} %get-tuple-element.42), channel_id=1, source_target_pairs={{0,1},{1,0},{2,3},{3,2},{4,5},{5,4},{6,7},{7,6},{8,9},{9,8},{10,11... | collective-permute-start | bytes 294920 | tf_op jit(solution)/shard_map/ppermute | solution.py:49
  81.1 14.9 %collective-permute-start.19 = (bf16[256,128]{1,0:T(8,128)(2,1)}, bf16[256,128]{1,0:T(8,128)(2,1)S(1)}, u32[]{:S(2)}, u32[]{:S(2)}) collective-permute-start(bf16[256,128]{1,0:T(8,128)(2,1)} %get-tuple-element.45), channel_id=1, source_target_pairs={{3,4},{7,8},{11,12},{15,16},{19,20},{23,24},{27,28},{4,3},{8,7},{1... | collective-permute-start | bytes 196616 | tf_op jit(solution)/shard_map/ppermute | solution.py:55
  85.8 6.6 %collective-permute-start.18 = (bf16[384,128]{1,0:T(8,128)(2,1)}, bf16[384,128]{1,0:T(8,128)(2,1)S(1)}, u32[]{:S(2)}, u32[]{:S(2)}) collective-permute-start(bf16[384,128]{1,0:T(8,128)(2,1)} %get-tuple-element.43), channel_id=1, source_target_pairs={{0,3},{1,2},{2,1},{3,0},{4,7},{5,6},{6,5},{7,4},{8,11},{9,10},{10,... | collective-permute-start | bytes 294920 | tf_op jit(solution)/shard_map/ppermute | solution.py:51
  93.2 9.2 %collective-permute-start.22 = (bf16[4,128,128]{2,1,0:T(8,128)(2,1)S(1)}, bf16[4,128,128]{2,1,0:T(8,128)(2,1)S(1)}, u32[]{:S(2)}, u32[]{:S(2)}) collective-permute-start(bf16[4,128,128]{2,1,0:T(8,128)(2,1)S(1)} %pad_maximum_fusion.2), channel_id=1, source_target_pairs={{0,24},{1,25},{2,26},{3,27},{4,28},{5,29},{6,30},{7,31},{8,16},{9,... | collective-permute-start | bytes 393224 | tf_op jit(solution)/shard_map/ppermute | solution.py:63
  94.2 8.2 %collective-permute-start.21 = (bf16[4,128,128]{2,1,0:T(8,128)(2,1)S(1)}, bf16[4,128,128]{2,1,0:T(8,128)(2,1)S(1)}, u32[]{:S(2)}, u32[]{:S(2)}) collective-permute-start(bf16[4,128,128]{2,1,0:T(8,128)(2,1)S(1)} %pad_maximum_fusion.2), channel_id=1, source_target_pairs={{0,16},{1,17},{2,18},{3,19},{4,20},{5,21},{6,22},{7,23},{8,24},{9,... | collective-permute-start | bytes 393224 | tf_op jit(solution)/shard_map/ppermute | solution.py:63
  94.2 8.2 %collective-permute-start.20 = (bf16[4,128,128]{2,1,0:T(8,128)(2,1)S(1)}, bf16[4,128,128]{2,1,0:T(8,128)(2,1)S(1)}, u32[]{:S(2)}, u32[]{:S(2)}) collective-permute-start(bf16[4,128,128]{2,1,0:T(8,128)(2,1)S(1)} %pad_maximum_fusion.2), channel_id=1, source_target_pairs={{0,8},{1,9},{2,10},{3,11},{4,12},{5,13},{6,14},{7,15},{8,0},{9,1},... | collective-permute-start | bytes 393224 | tf_op jit(solution)/shard_map/ppermute | solution.py:63
  102.5 3.1 %collective-permute-start.23 = (bf16[16,128,128]{2,1,0:T(8,128)(2,1)S(1)}, bf16[16,128,128]{2,1,0:T(8,128)(2,1)S(1)}, u32[]{:S(2)}, u32[]{:S(2)}) collective-permute-start(bf16[16,128,128]{2,1,0:T(8,128)(2,1)S(1)} %constant_dynamic-update-slice_fusion.14.rest_0_), channel_id=1, source_target_pairs={{0,4},{1,5},{2,6},{3,7},{4,0},{5,1},{6,2},{7,3},{8,12},{9,13},{10,... | collective-permute-start | bytes 1572872 | tf_op jit(solution)/shard_map/ppermute | solution.py:63
  (17 other events, 88.4 us)

commit v5 on v2

v5 whole, which is shorter than its diff:
```python
import functools

import jax
import jax.numpy as jnp
import numpy as np
from jax import lax
from jax.experimental import pallas as pl
from jax.experimental.pallas import tpu as pltpu
from jax.sharding import PartitionSpec as P

BW = 2
ITERS = 3
AXES = ("node", "hub")
ROUNDS_32 = ((1, 2, 3), (8, 16, 24), (4,))


spread_weight = 0.8

SMEM = pl.BlockSpec(memory_space=pltpu.SMEM)
ANY = pl.BlockSpec(memory_space=pl.ANY)
VMEM = pl.BlockSpec(memory_space=pltpu.VMEM)


def rims(current, width):
    count = lax.axis_size(AXES)
    forward = [(i, i + 1) for i in range(count - 1)]
    backward = [(target, source) for source, target in forward]
    low = lax.ppermute(current[current.shape[0] - width:], AXES, forward)
    high = lax.ppermute(current[:width], AXES, backward)
    return low, high


def positions(hub_blocks, owned, block_rows):
    count = lax.axis_size(AXES)
    if count != 32 or owned.shape[0] != block_rows:
        return hub_blocks
    offs = [0]
    for group in ROUNDS_32:
        offs = offs + [o ^ m for m in group for o in offs]
    assert sorted(offs) == list(range(count))
    where = np.zeros(count, np.int32)
    for p, o in enumerate(offs):
        where[o] = p
    return jnp.asarray(where)[hub_blocks ^ lax.axis_index(AXES)]


def hub_exchange(owned, block_rows, middle, after=lambda done: done):
    count = lax.axis_size(AXES)
    classes = owned.shape[1]
    if count != 32 or owned.shape[0] != block_rows:
        done = after(middle())
        hub_all = lax.all_gather(owned, AXES, axis=0, tiled=True)
        return done, [hub_all]
    pairs = lambda m: [(i, i ^ m) for i in range(count)]
    buf = owned[None]
    done = None
    pieces = [buf]
    for r, group in enumerate(ROUNDS_32):
        recvs = [lax.ppermute(buf, AXES, pairs(m)) for m in group]
        if r == 0:
            done, recvs = lax.optimization_barrier((middle(), recvs))
        elif r == 1:
            done, recvs = lax.optimization_barrier((after(done), recvs))
        pieces = [buf] + recvs
        if r + 1 < len(ROUNDS_32):
            buf = jnp.concatenate(pieces, 0)
    return done, [p.reshape(-1, classes) for p in pieces]


def load_ext_hub(cur_hbm, low_hbm, high_hbm, hub_hbm, ext, hub, sem):
    width = low_hbm.shape[0]
    own = cur_hbm.shape[0]
    copies = [
        pltpu.make_async_copy(low_hbm, ext.at[pl.ds(0, width)], sem.at[0]),
        pltpu.make_async_copy(cur_hbm, ext.at[pl.ds(width, own)], sem.at[1]),
        pltpu.make_async_copy(high_hbm, ext.at[pl.ds(width + own, width)], sem.at[2]),
    ]
    at = 0
    for i, piece in enumerate(hub_hbm):
        n = piece.shape[0]
        copies.append(pltpu.make_async_copy(piece, hub.at[pl.ds(at, n)], sem.at[3 + i]))
        at += n
    return copies


def full_kernel(n_hub, off_ref, hidx_ref, cur_hbm, low_hbm, high_hbm, *rest):
    hub_hbm = rest[:n_hub]
    (bt_hbm, ht_hbm, deg_ref, seeds_ref, out_ref, cur_ref, top_ref, bottom_ref,
     ext, hub, bt, ht, sem) = rest[n_hub:]
    blocks, k_band, rows = bt.shape[0], bt.shape[1], bt.shape[2]
    k_hub = ht.shape[1]
    width = top_ref.shape[0]
    own = cur_ref.shape[0]
    copies = load_ext_hub(cur_hbm, low_hbm, high_hbm, hub_hbm, ext, hub, sem)
    first = 3 + n_hub
    band_copies = [pltpu.make_async_copy(bt_hbm.at[b], bt.at[b], sem.at[first + b]) for b in range(blocks)]
    hub_copies = [
        pltpu.make_async_copy(ht_hbm.at[b], ht.at[b], sem.at[first + blocks + b]) for b in range(blocks)
    ]
    band_copies[0].start()
    for c in copies:
        c.start()
    hub_copies[0].start()
    for b in range(1, blocks):
        band_copies[b].start()
        hub_copies[b].start()
    for c in copies:
        c.wait()
    for b in range(blocks):
        band_copies[b].wait()
        band = jnp.zeros((rows, cur_ref.shape[1]), jnp.float32)
        for k in range(k_band):
            n = b + BW + off_ref[b * k_band + k]
            start = pl.multiple_of(n * rows, rows)
            band = band + jnp.dot(bt[b, k], ext[pl.ds(start, rows), :], preferred_element_type=jnp.float32)
        hub_copies[b].wait()
        acc = jnp.zeros_like(band)
        for h in range(k_hub):
            start = pl.multiple_of(hidx_ref[b * k_hub + h] * rows, rows)
            acc = acc + jnp.dot(ht[b, h], hub[pl.ds(start, rows), :], preferred_element_type=jnp.float32)
        gathered = (band + acc) / deg_ref[pl.ds(b * rows, rows), :]
        labels = spread_weight * gathered + (1.0 - spread_weight) * seeds_ref[pl.ds(b * rows, rows), :]
        out_ref[pl.ds(b * rows, rows), :] = labels
        cur_ref[pl.ds(b * rows, rows), :] = labels.astype(cur_ref.dtype)
    top_ref[...] = cur_ref[pl.ds(own - width, width), :]
    bottom_ref[...] = cur_ref[pl.ds(0, width), :]


def full_call(band_offsets, hub_index, current, low, high, hub_pieces, band_tiles, hub_tiles, degree, seeds):
    blocks, k_band, rows, _ = band_tiles.shape
    classes = current.shape[1]
    width = low.shape[0]
    n_hub = len(hub_pieces)
    bf = current.dtype
    return pl.pallas_call(
        functools.partial(full_kernel, n_hub),
        in_specs=[SMEM, SMEM] + [ANY] * (3 + n_hub + 2) + [VMEM, VMEM],
        out_specs=[VMEM] * 4,
        out_shape=[
            jax.ShapeDtypeStruct(seeds.shape, jnp.float32),
            jax.ShapeDtypeStruct(current.shape, bf),
            jax.ShapeDtypeStruct((width, classes), bf),
            jax.ShapeDtypeStruct((width, classes), bf),
        ],
        scratch_shapes=[
            pltpu.VMEM((current.shape[0] + 2 * width, classes), bf),
            pltpu.VMEM((sum(p.shape[0] for p in hub_pieces), classes), bf),
            pltpu.VMEM(band_tiles.shape, band_tiles.dtype),
            pltpu.VMEM(hub_tiles.shape, hub_tiles.dtype),
            pltpu.SemaphoreType.DMA((3 + n_hub + 2 * blocks,)),
        ],
    )(
        band_offsets.reshape(-1), hub_index.reshape(-1), current, low, high, *hub_pieces,
        band_tiles, hub_tiles, degree, seeds,
    )


def early_kernel(n_hub, cur_hbm, low_hbm, high_hbm, *rest):
    hub_hbm = rest[:n_hub]
    rb_hi, rb_lo, rh_hi, rh_lo, deg_ref, seeds_ref, owned_ref, ext, hub, sem = rest[n_hub:]
    copies = load_ext_hub(cur_hbm, low_hbm, high_hbm, hub_hbm, ext, hub, sem)
    for c in copies:
        c.start()
    for c in copies:
        c.wait()
    f32 = jnp.float32
    band = jnp.dot(rb_hi[...], ext[...], preferred_element_type=f32) + jnp.dot(
        rb_lo[...], ext[...], preferred_element_type=f32
    )
    hubs = jnp.dot(rh_hi[...], hub[...], preferred_element_type=f32) + jnp.dot(
        rh_lo[...], hub[...], preferred_element_type=f32
    )
    gathered = (band + hubs) / deg_ref[...]
    labels = spread_weight * gathered + (1.0 - spread_weight) * seeds_ref[...]
    owned_ref[...] = labels.astype(owned_ref.dtype)


def early_call(current, low, high, hub_pieces, weights, deg_rows, seeds_rows):
    classes = current.shape[1]
    width = low.shape[0]
    n_hub = len(hub_pieces)
    bf = current.dtype
    return pl.pallas_call(
        functools.partial(early_kernel, n_hub),
        in_specs=[ANY] * (3 + n_hub) + [VMEM] * 6,
        out_specs=VMEM,
        out_shape=jax.ShapeDtypeStruct(seeds_rows.shape, bf),
        scratch_shapes=[
            pltpu.VMEM((current.shape[0] + 2 * width, classes), bf),
            pltpu.VMEM((sum(p.shape[0] for p in hub_pieces), classes), bf),
            pltpu.SemaphoreType.DMA((3 + n_hub,)),
        ],
    )(current, low, high, *hub_pieces, *weights, deg_rows, seeds_rows)


def split16(x):
    hi = x.astype(jnp.bfloat16)
    lo = (x - hi.astype(jnp.float32)).astype(jnp.bfloat16)
    return hi, lo


def row_weights(hub_rows, band_offsets, band_tiles, hub_tiles, hub_index, n_hub_blocks):
    blocks, k_band, rows, _ = band_tiles.shape
    b = hub_rows // rows
    i = hub_rows % rows
    hi = lax.Precision.HIGHEST
    band_rows = band_tiles[b, :, i, :].astype(jnp.float32)
    near = b[:, None] + BW + band_offsets[b]
    pick = (near[:, :, None] == jnp.arange(blocks + 2 * BW)[None, None, :]).astype(jnp.float32)
    rb = jnp.einsum("jkn,jkc->jnc", pick, band_rows, precision=hi).reshape(hub_rows.shape[0], -1)
    hub_rows_w = hub_tiles[b, :, i, :].astype(jnp.float32)
    where = hub_index[b]
    pick = (where[:, :, None] == jnp.arange(n_hub_blocks)[None, None, :]).astype(jnp.float32)
    rh = jnp.einsum("jhp,jhc->jpc", pick, hub_rows_w, precision=hi).reshape(hub_rows.shape[0], -1)
    return split16(rb) + split16(rh)


def send_rims(done):
    labels, current, top, bottom = done
    count = lax.axis_size(AXES)
    forward = [(i, i + 1) for i in range(count - 1)]
    backward = [(target, source) for source, target in forward]
    return labels, current, lax.ppermute(top, AXES, forward), lax.ppermute(bottom, AXES, backward)


def body(seed_scores, seed_mask, band_offsets, band_tiles, hub_blocks, hub_tiles, hub_rows):
    block_rows = band_tiles.shape[2]
    seeds = seed_mask.astype(jnp.float32)[:, None] * seed_scores.astype(jnp.float32)
    degree = jnp.sum(band_tiles, axis=(1, 3), dtype=jnp.float32) + jnp.sum(
        hub_tiles, axis=(1, 3), dtype=jnp.float32
    )
    degree = degree.reshape(-1, 1)
    width = BW * block_rows
    current = seeds.astype(jnp.bfloat16)
    owned = current[hub_rows]
    hub_index = positions(hub_blocks, owned, block_rows)
    n_hub_blocks = lax.axis_size(AXES) * owned.shape[0] // block_rows
    weights = row_weights(hub_rows, band_offsets, band_tiles, hub_tiles, hub_index, n_hub_blocks)
    deg_rows = degree[hub_rows]
    seeds_rows = seeds[hub_rows]
    low, high = rims(current, width)
    _, hub_pieces = hub_exchange(owned, block_rows, lambda: None)
    for step in range(ITERS - 1):
        owned = early_call(current, low, high, hub_pieces, weights, deg_rows, seeds_rows)
        full = functools.partial(
            full_call, band_offsets, hub_index, current, low, high, hub_pieces, band_tiles, hub_tiles,
            degree, seeds,
        )
        (labels, current, low, high), hub_pieces = hub_exchange(owned, block_rows, full, send_rims)
    labels, _, _, _ = full_call(
        band_offsets, hub_index, current, low, high, hub_pieces, band_tiles, hub_tiles, degree, seeds
    )
    return labels


def solution(mesh):
    placed = (
        P(AXES, None),
        P(AXES),
        P(AXES, None),
        P(AXES, None, None, None),
        P(AXES, None),
        P(AXES, None, None, None),
        P(AXES),
    )
    return jax.shard_map(
        body, mesh=mesh, in_specs=placed, out_specs=P(AXES, None), check_vma=False
    )
```

time: 122 us -> 139 us (1.14)
  waiting for transfers between devices: 32.7 us -> 6.99 us
  local copies, waits for them, and re-layouts: 13.4 us -> 31.2 us
  Pallas kernels: 21.6 us -> 31.1 us
  starting transfers between devices: 45 us -> 53.5 us
  other arithmetic: 6.31 us -> 11.4 us
  matrix products: 0 us -> 2.34 us
    ppermute x27, waiting for transfers between devices: 32.7 us -> 6.99 us  [the longest x21 3.77 us: hub_exchange(): recvs = [lax.ppermute(buf, AXES, pairs(m)) for m in group]]
    unnamed x42 -> x61, local copies, waits for them, and re-layouts: 3.06 us -> 13.6 us
    pallas_call x3 -> x5, Pallas kernels: 21.6 us -> 31.1 us  [the longest x3 21.7 us: full_call(): pl.pallas_call(functools.partial(full_kernel, n_hub), in_specs=[SMEM, SME...]
    ppermute x27, starting transfers between devices: 45 us -> 53.5 us  [the longest x21 29.2 us: hub_exchange(): recvs = [lax.ppermute(buf, AXES, pairs(m)) for m in group]]
    gather x1 -> x9, local copies, waits for them, and re-layouts: 1.37 us -> 9.05 us  [the longest x2 1.89 us: body(): deg_rows = degree[hub_rows]]
    convert_element_type x0 -> x2, other arithmetic: none -> 4.48 us  [split16(): lo = (x - hi.astype(jnp.float32)).astype(jnp.bfloat16)]
    gather x3 -> x1, local copies, waits for them, and re-layouts: 3.98 us -> 0.71 us  [body(): owned = current[hub_rows]]
    dot_general x0 -> x1, local copies, waits for them, and re-layouts: none -> 2.43 us  [row_weights(): jnp.einsum('jkn,jkc->jnc', pick, band_rows, precision=hi)]
  transfers between devices with their start and end apart: 27 -> 27, of which waited for: 11 -> 7; matrix products, arithmetic and copies ran while one was open for 8% -> 27% of each run, Pallas kernels for 0% -> 11%
where the time goes in v5:
time: 139 us; the launch traced here: 137 us
  starting transfers between devices  53.5 us (38%)
  local copies, waits for them, and re-layouts  31.2 us (22%)
  Pallas kernels  31.1 us (22%)
  other arithmetic  11.4 us (8%)
  waiting for transfers between devices  6.99 us (5%)
  matrix products  2.34 us (2%)
    ppermute x21, starting transfers between devices, hub_exchange(): recvs = [lax.ppermute(buf, AXES, pairs(m)) for m in group]  29.2 us
    pallas_call x3, Pallas kernels, full_call(): pl.pallas_call(functools.partial(full_kernel, n_hub), in_specs=[SMEM, SME...  21.7 us
    unnamed x61, local copies, waits for them, and re-layouts  13.6 us
    ppermute x2, starting transfers between devices, send_rims(): lax.ppermute(bottom, AXES, backward)  11.7 us
    pallas_call x2, Pallas kernels, early_call(): pl.pallas_call(functools.partial(early_kernel, n_hub), in_specs=[ANY] * (...  9.39 us
    ppermute x1, starting transfers between devices, rims(): high = lax.ppermute(current[:width], AXES, backward)  6.25 us
    convert_element_type x2, other arithmetic, split16(): lo = (x - hi.astype(jnp.float32)).astype(jnp.bfloat16)  4.48 us
    ppermute x2, starting transfers between devices, send_rims(): lax.ppermute(top, AXES, forward)  4.06 us
  transfers between devices with their start and end apart: 27, of which 7 were waited for; matrix products, arithmetic and copies ran while one was open for 27% of the time, Pallas kernels for 11%

profile of v5, /device:TPU:5, one launch (start us, length us, event | category | flops | bytes accessed | tf_op | source)
XLA Modules:
  0.0 137.1 jit_solution(3130276961667317635)
XLA Ops:
  5.8 2.3 %collective-permute-start.3 = (bf16[1,128,128]{2,1,0:T(8,128)(2,1)S(1)}, bf16[1,128,128]{2,1,0:T(8,128)(2,1)}, u32[]{:S(2)}, u32[]{:S(2)}) collective-permute-start(bf16[1,128,128]{2,1,0:T(8,128)(2,1)S(1)} %bitcast.49), channel_id=1, source_target_pairs={{0,2},{1,3},{2,0},{3,1},{4,6},{5,7},{6,4},{7,5},{8,10},{9,11},{10,... | collective-permute-start | bytes 98312 | tf_op jit(solution)/shard_map/ppermute | solution.py:59
  8.8 2.2 %collective-permute-start = (bf16[256,128]{1,0:T(8,128)(2,1)}, bf16[256,128]{1,0:T(8,128)(2,1)}, u32[]{:S(2)}, u32[]{:S(2)}) collective-permute-start(bf16[256,128]{1,0:T(8,128)(2,1)} %get-tuple-element.86), channel_id=1, source_target_pairs={{0,1},{1,2},{2,3},{3,4},{4,5},{5,6},{6,7},{7,8},{8,9},{9,10},{10,1... | collective-permute-start | bytes 196616 | tf_op jit(solution)/shard_map/ppermute | solution.py:28
  11.0 6.2 %collective-permute-start.1 = (bf16[256,128]{1,0:T(8,128)(2,1)}, bf16[256,128]{1,0:T(8,128)(2,1)}, u32[]{:S(2)}, u32[]{:S(2)}) collective-permute-start(bf16[256,128]{1,0:T(8,128)(2,1)} %get-tuple-element.85), channel_id=1, source_target_pairs={{1,0},{2,1},{3,2},{4,3},{5,4},{6,5},{7,6},{8,7},{9,8},{10,9},{11,1... | collective-permute-start | bytes 196616 | tf_op jit(solution)/shard_map/ppermute | solution.py:29
  23.2 2.1 %fusion.rest_5_ = bf16[128,4096]{1,0:T(8,128)(2,1)} fusion(f32[16,8,32,128]{3,2,1,0:T(8,128)S(1)} %bitcast.27), kind=kLoop, calls=%fused_computation.12 | loop fusion | flops 2097152 | bytes 3145728 | tf_op jit(solution)/shard_map/convert_element_type | solution.py:198
  26.6 1.8 %gather_fusion.3 = bf16[128,10,128]{2,0,1:T(8,128)(2,1)S(1)} fusion(bf16[8,10,128,128]{3,2,1,0:T(8,128)(2,1)S(1)} %copy-done.1, s32[128]{0:T(128)S(1)} %get-tuple-element.88), kind=kCustom, calls=%fused_computation.3 | custom fusion | bytes 656384 | tf_op jit(solution)/shard_map/gather | solution.py:207
  31.4 2.4 %copy.15 = f32[128,12,128]{0,2,1:T(8,128)} copy(f32[128,12,128]{2,1,0:T(8,128)} %fusion.1) | data formatting | bytes 1572864 | tf_op jit(solution)/shard_map/jkn,jkc->jnc/dot_general | solution.py:210
  33.8 2.3 %copy.16 = f32[128,1536]{1,0:T(8,128)} copy(f32[128,1536]{0,1:T(8,128)} %bitcast.31) | data formatting | bytes 1572864 | tf_op jit(solution)/shard_map/reshape | solution.py:210
  45.7 3.4 %collective-permute-start.8 = (bf16[16,128,128]{2,1,0:T(8,128)(2,1)}, bf16[16,128,128]{2,1,0:T(8,128)(2,1)}, u32[]{:S(2)}, u32[]{:S(2)}) collective-permute-start(bf16[16,128,128]{2,1,0:T(8,128)(2,1)} %constant_dynamic-update-slice_fusion), channel_id=1, source_target_pairs={{0,4},{1,5},{2,6},{3,7},{4,0},{5,1},{6,2},{7,3},{8,12},{9,13},{10,... | collective-permute-start | bytes 1572872 | tf_op jit(solution)/shard_map/ppermute | solution.py:59
  49.1 2.4 %subtract_convert_fusion = (bf16[128,1536]{1,0:T(8,128)(2,1)}, bf16[128,1536]{1,0:T(8,128)(2,1)}) fusion(f32[128,1536]{1,0:T(8,128)} %copy.16), kind=kLoop, calls=%fused_computation.15 | loop fusion | flops 786432 | bytes 1572864 | tf_op jit(solution)/shard_map/convert_element_type | solution.py:198
  53.0 2.7 %copy.32 = bf16[16,8,32,128]{3,1,2,0:T(8,128)(2,1)} copy(f32[16,8,32,128]{3,2,1,0:T(8,128)S(1)} %bitcast.28) | data formatting | bytes 3145728
  60.6 4.7 %shard_map.83 = bf16[128,128]{1,0:T(8,128)(2,1)} custom-call(bf16[1024,128]{1,0:T(8,128)(2,1)} %copy-done.8, bf16[256,128]{1,0:T(8,128)(2,1)} %collective-permute-done.low_hbm, bf16[256,128]{1,0:T(8,128)(2,1)} %collective-permute-done.1.high_hbm, bf16[2048,128]{1,0:T(8,128)(2,1)} %bitcast.34, bf16[2048,128]{1,0:T(8,128)(2,1)} %bitcast.2.rest_1_, ...), custom_call_target="tpu_custom_call" | custom-call | tf_op jit(solution)/shard_map/pallas_call | solution.py:183
  66.3 1.7 %collective-permute-start.9 = (bf16[1,128,128]{2,1,0:T(8,128)(2,1)}, bf16[1,128,128]{2,1,0:T(8,128)(2,1)S(1)}, u32[]{:S(2)}, u32[]{:S(2)}) collective-permute-start(bf16[1,128,128]{2,1,0:T(8,128)(2,1)} %bitcast.46), channel_id=1, source_target_pairs={{0,1},{1,0},{2,3},{3,2},{4,5},{5,4},{6,7},{7,6},{8,9},{9,8},{10,11... | collective-permute-start | bytes 98312 | tf_op jit(solution)/shard_map/ppermute | solution.py:59
  68.8 7.2 %shard_map.82 = (f32[1024,128]{1,0:T(8,128)}, bf16[1024,128]{1,0:T(8,128)(2,1)}, bf16[256,128]{1,0:T(8,128)(2,1)}, bf16[256,128]{1,0:T(8,128)(2,1)}) custom-call(s32[80]{0:T(128)} %reshape.74.off_ref, s32[48]{0:T(128)} %copy-done.17, bf16[1024,128]{1,0:T(8,128)(2,1)} %copy-done.8, bf16[256,128]{1,0:T(8,128)(2,1)} %collective-permute-done.low_hbm, ...), custom_call_target="tpu_custom_call" | custom-call | tf_op jit(solution)/shard_map/pallas_call | solution.py:135
  78.9 1.9 %collective-permute-start.12 = (bf16[256,128]{1,0:T(8,128)(2,1)}, bf16[256,128]{1,0:T(8,128)(2,1)S(1)}, u32[]{:S(2)}, u32[]{:S(2)}) collective-permute-start(bf16[256,128]{1,0:T(8,128)(2,1)} %get-tuple-element.52), channel_id=1, source_target_pairs={{0,1},{1,2},{2,3},{3,4},{4,5},{5,6},{6,7},{7,8},{8,9},{9,10},{10,1... | collective-permute-start | bytes 196616 | tf_op jit(solution)/shard_map/ppermute | solution.py:223
  80.8 5.4 %collective-permute-start.13 = (bf16[256,128]{1,0:T(8,128)(2,1)}, bf16[256,128]{1,0:T(8,128)(2,1)S(1)}, u32[]{:S(2)}, u32[]{:S(2)}) collective-permute-start(bf16[256,128]{1,0:T(8,128)(2,1)} %get-tuple-element.53), channel_id=1, source_target_pairs={{1,0},{2,1},{3,2},{4,3},{5,4},{6,5},{7,6},{8,7},{9,8},{10,9},{11,1... | collective-permute-start | bytes 196616 | tf_op jit(solution)/shard_map/ppermute | solution.py:223
  88.0 4.3 %collective-permute-start.17 = (bf16[16,128,128]{2,1,0:T(8,128)(2,1)S(1)}, bf16[16,128,128]{2,1,0:T(8,128)(2,1)S(1)}, u32[]{:S(2)}, u32[]{:S(2)}) collective-permute-start(bf16[16,128,128]{2,1,0:T(8,128)(2,1)S(1)} %constant_dynamic-update-slice_fusion.7), channel_id=1, source_target_pairs={{0,4},{1,5},{2,6},{3,7},{4,0},{5,1},{6,2},{7,3},{8,12},{9,13},{10,... | collective-permute-start | bytes 1572872 | tf_op jit(solution)/shard_map/ppermute | solution.py:59
  94.6 4.7 %shard_map.85 = bf16[128,128]{1,0:T(8,128)(2,1)} custom-call(bf16[1024,128]{1,0:T(8,128)(2,1)} %get-tuple-element.57.cur_hbm, bf16[256,128]{1,0:T(8,128)(2,1)} %copy-done.15, bf16[256,128]{1,0:T(8,128)(2,1)} %copy-done.16, bf16[2048,128]{1,0:T(8,128)(2,1)} %bitcast.32, bf16[2048,128]{1,0:T(8,128)(2,1)} %bitcast.36, ...), custom_call_target="tpu_custom_call" | custom-call | tf_op jit(solution)/shard_map/pallas_call | solution.py:183
  99.4 3.1 %collective-permute-start.19 = (bf16[1,128,128]{2,1,0:T(8,128)(2,1)}, bf16[1,128,128]{2,1,0:T(8,128)(2,1)S(1)}, u32[]{:S(2)}, u32[]{:S(2)}) collective-permute-start(bf16[1,128,128]{2,1,0:T(8,128)(2,1)} %bitcast.41), channel_id=1, source_target_pairs={{0,2},{1,3},{2,0},{3,1},{4,6},{5,7},{6,4},{7,5},{8,10},{9,11},{10,... | collective-permute-start | bytes 98312 | tf_op jit(solution)/shard_map/ppermute | solution.py:59
  103.7 7.3 %shard_map.84 = (f32[1024,128]{1,0:T(8,128)}, bf16[1024,128]{1,0:T(8,128)(2,1)}, bf16[256,128]{1,0:T(8,128)(2,1)}, bf16[256,128]{1,0:T(8,128)(2,1)}) custom-call(s32[80]{0:T(128)} %reshape.74.off_ref, s32[48]{0:T(128)} %copy-done.17, bf16[1024,128]{1,0:T(8,128)(2,1)} %get-tuple-element.57.cur_hbm, bf16[256,128]{1,0:T(8,128)(2,1)} %copy-done.15, ...), custom_call_target="tpu_custom_call" | custom-call | tf_op jit(solution)/shard_map/pallas_call | solution.py:135
  111.1 2.6 %collective-permute-start.24 = (bf16[4,128,128]{2,1,0:T(8,128)(2,1)S(1)}, bf16[4,128,128]{2,1,0:T(8,128)(2,1)S(1)}, u32[]{:S(2)}, u32[]{:S(2)}) collective-permute-start(bf16[4,128,128]{2,1,0:T(8,128)(2,1)S(1)} %pad_maximum_fusion.2), channel_id=1, source_target_pairs={{0,16},{1,17},{2,18},{3,19},{4,20},{5,21},{6,22},{7,23},{8,24},{9,... | collective-permute-start | bytes 393224 | tf_op jit(solution)/shard_map/ppermute | solution.py:59
  113.8 2.1 %collective-permute-start.21 = (bf16[256,128]{1,0:T(8,128)(2,1)}, bf16[256,128]{1,0:T(8,128)(2,1)S(1)}, u32[]{:S(2)}, u32[]{:S(2)}) collective-permute-start(bf16[256,128]{1,0:T(8,128)(2,1)} %get-tuple-element.67), channel_id=1, source_target_pairs={{0,1},{1,2},{2,3},{3,4},{4,5},{5,6},{6,7},{7,8},{8,9},{9,10},{10,1... | collective-permute-start | bytes 196616 | tf_op jit(solution)/shard_map/ppermute | solution.py:223
  115.9 6.3 %collective-permute-start.22 = (bf16[256,128]{1,0:T(8,128)(2,1)}, bf16[256,128]{1,0:T(8,128)(2,1)S(1)}, u32[]{:S(2)}, u32[]{:S(2)}) collective-permute-start(bf16[256,128]{1,0:T(8,128)(2,1)} %get-tuple-element.68), channel_id=1, source_target_pairs={{1,0},{2,1},{3,2},{4,3},{5,4},{6,5},{7,6},{8,7},{9,8},{10,9},{11,1... | collective-permute-start | bytes 196616 | tf_op jit(solution)/shard_map/ppermute | solution.py:223
  124.0 3.4 %collective-permute-start.26 = (bf16[16,128,128]{2,1,0:T(8,128)(2,1)S(1)}, bf16[16,128,128]{2,1,0:T(8,128)(2,1)S(1)}, u32[]{:S(2)}, u32[]{:S(2)}) collective-permute-start(bf16[16,128,128]{2,1,0:T(8,128)(2,1)S(1)} %constant_dynamic-update-slice_fusion.14), channel_id=1, source_target_pairs={{0,4},{1,5},{2,6},{3,7},{4,0},{5,1},{6,2},{7,3},{8,12},{9,13},{10,... | collective-permute-start | bytes 1572872 | tf_op jit(solution)/shard_map/ppermute | solution.py:59
  129.7 7.2 %shard_map.86 = (f32[1024,128]{1,0:T(8,128)}, bf16[1024,128]{1,0:T(8,128)(2,1)}, bf16[256,128]{1,0:T(8,128)(2,1)}, bf16[256,128]{1,0:T(8,128)(2,1)}) custom-call(s32[80]{0:T(128)} %reshape.74.off_ref, s32[48]{0:T(128)} %copy-done.17, bf16[1024,128]{1,0:T(8,128)(2,1)} %get-tuple-element.72.cur_hbm, bf16[256,128]{1,0:T(8,128)(2,1)} %copy-done.18, ...), custom_call_target="tpu_custom_call" | custom-call | tf_op jit(solution)/shard_map/pallas_call | solution.py:135
  (134 shorter events, 46.6 us)
Async XLA Ops:
  4.5 31.7 %collective-permute-start.2 = (bf16[1,128,128]{2,1,0:T(8,128)(2,1)S(1)}, bf16[1,128,128]{2,1,0:T(8,128)(2,1)S(1)}, u32[]{:S(2)}, u32[]{:S(2)}) collective-permute-start(bf16[1,128,128]{2,1,0:T(8,128)(2,1)S(1)} %bitcast.48), channel_id=1, source_target_pairs={{0,1},{1,0},{2,3},{3,2},{4,5},{5,4},{6,7},{7,6},{8,9},{9,8},{10,11... | collective-permute-start | bytes 98312 | tf_op jit(solution)/shard_map/ppermute | solution.py:59
  5.8 30.3 %collective-permute-start.3 = (bf16[1,128,128]{2,1,0:T(8,128)(2,1)S(1)}, bf16[1,128,128]{2,1,0:T(8,128)(2,1)}, u32[]{:S(2)}, u32[]{:S(2)}) collective-permute-start(bf16[1,128,128]{2,1,0:T(8,128)(2,1)S(1)} %bitcast.49), channel_id=1, source_target_pairs={{0,2},{1,3},{2,0},{3,1},{4,6},{5,7},{6,4},{7,5},{8,10},{9,11},{10,... | collective-permute-start | bytes 98312 | tf_op jit(solution)/shard_map/ppermute | solution.py:59
  8.1 28.0 %collective-permute-start.4 = (bf16[1,128,128]{2,1,0:T(8,128)(2,1)S(1)}, bf16[1,128,128]{2,1,0:T(8,128)(2,1)}, u32[]{:S(2)}, u32[]{:S(2)}) collective-permute-start(bf16[1,128,128]{2,1,0:T(8,128)(2,1)S(1)} %bitcast.50), channel_id=1, source_target_pairs={{0,3},{1,2},{2,1},{3,0},{4,7},{5,6},{6,5},{7,4},{8,11},{9,10},{10,... | collective-permute-start | bytes 98312 | tf_op jit(solution)/shard_map/ppermute | solution.py:59
  8.8 51.8 %collective-permute-start = (bf16[256,128]{1,0:T(8,128)(2,1)}, bf16[256,128]{1,0:T(8,128)(2,1)}, u32[]{:S(2)}, u32[]{:S(2)}) collective-permute-start(bf16[256,128]{1,0:T(8,128)(2,1)} %get-tuple-element.86), channel_id=1, source_target_pairs={{0,1},{1,2},{2,3},{3,4},{4,5},{5,6},{6,7},{7,8},{8,9},{9,10},{10,1... | collective-permute-start | bytes 196616 | tf_op jit(solution)/shard_map/ppermute | solution.py:28
  11.0 49.6 %collective-permute-start.1 = (bf16[256,128]{1,0:T(8,128)(2,1)}, bf16[256,128]{1,0:T(8,128)(2,1)}, u32[]{:S(2)}, u32[]{:S(2)}) collective-permute-start(bf16[256,128]{1,0:T(8,128)(2,1)} %get-tuple-element.85), channel_id=1, source_target_pairs={{1,0},{2,1},{3,2},{4,3},{5,4},{6,5},{7,6},{8,7},{9,8},{10,9},{11,1... | collective-permute-start | bytes 196616 | tf_op jit(solution)/shard_map/ppermute | solution.py:29
  37.0 6.1 %collective-permute-start.5 = (bf16[4,128,128]{2,1,0:T(8,128)(2,1)S(1)}, bf16[4,128,128]{2,1,0:T(8,128)(2,1)S(1)}, u32[]{:S(2)}, u32[]{:S(2)}) collective-permute-start(bf16[4,128,128]{2,1,0:T(8,128)(2,1)S(1)} %pad_maximum_fusion), channel_id=1, source_target_pairs={{0,8},{1,9},{2,10},{3,11},{4,12},{5,13},{6,14},{7,15},{8,0},{9,1},... | collective-permute-start | bytes 393224 | tf_op jit(solution)/shard_map/ppermute | solution.py:59
  45.7 14.9 %collective-permute-start.8 = (bf16[16,128,128]{2,1,0:T(8,128)(2,1)}, bf16[16,128,128]{2,1,0:T(8,128)(2,1)}, u32[]{:S(2)}, u32[]{:S(2)}) collective-permute-start(bf16[16,128,128]{2,1,0:T(8,128)(2,1)} %constant_dynamic-update-slice_fusion), channel_id=1, source_target_pairs={{0,4},{1,5},{2,6},{3,7},{4,0},{5,1},{6,2},{7,3},{8,12},{9,13},{10,... | collective-permute-start | bytes 1572872 | tf_op jit(solution)/shard_map/ppermute | solution.py:59
  65.3 10.8 %collective-permute-start.10 = (bf16[1,128,128]{2,1,0:T(8,128)(2,1)}, bf16[1,128,128]{2,1,0:T(8,128)(2,1)S(1)}, u32[]{:S(2)}, u32[]{:S(2)}) collective-permute-start(bf16[1,128,128]{2,1,0:T(8,128)(2,1)} %bitcast.44), channel_id=1, source_target_pairs={{0,2},{1,3},{2,0},{3,1},{4,6},{5,7},{6,4},{7,5},{8,10},{9,11},{10,... | collective-permute-start | bytes 98312 | tf_op jit(solution)/shard_map/ppermute | solution.py:59
  65.4 10.7 %collective-permute-start.11 = (bf16[1,128,128]{2,1,0:T(8,128)(2,1)}, bf16[1,128,128]{2,1,0:T(8,128)(2,1)S(1)}, u32[]{:S(2)}, u32[]{:S(2)}) collective-permute-start(bf16[1,128,128]{2,1,0:T(8,128)(2,1)} %bitcast.45), channel_id=1, source_target_pairs={{0,3},{1,2},{2,1},{3,0},{4,7},{5,6},{6,5},{7,4},{8,11},{9,10},{10,... | collective-permute-start | bytes 98312 | tf_op jit(solution)/shard_map/ppermute | solution.py:59
  66.3 9.8 %collective-permute-start.9 = (bf16[1,128,128]{2,1,0:T(8,128)(2,1)}, bf16[1,128,128]{2,1,0:T(8,128)(2,1)S(1)}, u32[]{:S(2)}, u32[]{:S(2)}) collective-permute-start(bf16[1,128,128]{2,1,0:T(8,128)(2,1)} %bitcast.46), channel_id=1, source_target_pairs={{0,1},{1,0},{2,3},{3,2},{4,5},{5,4},{6,7},{7,6},{8,9},{9,8},{10,11... | collective-permute-start | bytes 98312 | tf_op jit(solution)/shard_map/ppermute | solution.py:59
  76.1 11.7 %collective-permute-start.14 = (bf16[4,128,128]{2,1,0:T(8,128)(2,1)S(1)}, bf16[4,128,128]{2,1,0:T(8,128)(2,1)S(1)}, u32[]{:S(2)}, u32[]{:S(2)}) collective-permute-start(bf16[4,128,128]{2,1,0:T(8,128)(2,1)S(1)} %pad_maximum_fusion.1), channel_id=1, source_target_pairs={{0,8},{1,9},{2,10},{3,11},{4,12},{5,13},{6,14},{7,15},{8,0},{9,1},... | collective-permute-start | bytes 393224 | tf_op jit(solution)/shard_map/ppermute | solution.py:59
  76.8 11.1 %collective-permute-start.15 = (bf16[4,128,128]{2,1,0:T(8,128)(2,1)S(1)}, bf16[4,128,128]{2,1,0:T(8,128)(2,1)S(1)}, u32[]{:S(2)}, u32[]{:S(2)}) collective-permute-start(bf16[4,128,128]{2,1,0:T(8,128)(2,1)S(1)} %pad_maximum_fusion.1), channel_id=1, source_target_pairs={{0,16},{1,17},{2,18},{3,19},{4,20},{5,21},{6,22},{7,23},{8,24},{9,... | collective-permute-start | bytes 393224 | tf_op jit(solution)/shard_map/ppermute | solution.py:59
  77.6 10.3 %collective-permute-start.16 = (bf16[4,128,128]{2,1,0:T(8,128)(2,1)S(1)}, bf16[4,128,128]{2,1,0:T(8,128)(2,1)S(1)}, u32[]{:S(2)}, u32[]{:S(2)}) collective-permute-start(bf16[4,128,128]{2,1,0:T(8,128)(2,1)S(1)} %pad_maximum_fusion.1), channel_id=1, source_target_pairs={{0,24},{1,25},{2,26},{3,27},{4,28},{5,29},{6,30},{7,31},{8,16},{9,... | collective-permute-start | bytes 393224 | tf_op jit(solution)/shard_map/ppermute | solution.py:59
  78.9 7.7 %collective-permute-start.12 = (bf16[256,128]{1,0:T(8,128)(2,1)}, bf16[256,128]{1,0:T(8,128)(2,1)S(1)}, u32[]{:S(2)}, u32[]{:S(2)}) collective-permute-start(bf16[256,128]{1,0:T(8,128)(2,1)} %get-tuple-element.52), channel_id=1, source_target_pairs={{0,1},{1,2},{2,3},{3,4},{4,5},{5,6},{6,7},{7,8},{8,9},{9,10},{10,1... | collective-permute-start | bytes 196616 | tf_op jit(solution)/shard_map/ppermute | solution.py:223
  80.8 7.0 %collective-permute-start.13 = (bf16[256,128]{1,0:T(8,128)(2,1)}, bf16[256,128]{1,0:T(8,128)(2,1)S(1)}, u32[]{:S(2)}, u32[]{:S(2)}) collective-permute-start(bf16[256,128]{1,0:T(8,128)(2,1)} %get-tuple-element.53), channel_id=1, source_target_pairs={{1,0},{2,1},{3,2},{4,3},{5,4},{6,5},{7,6},{8,7},{9,8},{10,9},{11,1... | collective-permute-start | bytes 196616 | tf_op jit(solution)/shard_map/ppermute | solution.py:223
  88.0 5.8 %collective-permute-start.17 = (bf16[16,128,128]{2,1,0:T(8,128)(2,1)S(1)}, bf16[16,128,128]{2,1,0:T(8,128)(2,1)S(1)}, u32[]{:S(2)}, u32[]{:S(2)}) collective-permute-start(bf16[16,128,128]{2,1,0:T(8,128)(2,1)S(1)} %constant_dynamic-update-slice_fusion.7), channel_id=1, source_target_pairs={{0,4},{1,5},{2,6},{3,7},{4,0},{5,1},{6,2},{7,3},{8,12},{9,13},{10,... | collective-permute-start | bytes 1572872 | tf_op jit(solution)/shard_map/ppermute | solution.py:59
  99.3 11.7 %collective-permute-start.18 = (bf16[1,128,128]{2,1,0:T(8,128)(2,1)}, bf16[1,128,128]{2,1,0:T(8,128)(2,1)S(1)}, u32[]{:S(2)}, u32[]{:S(2)}) collective-permute-start(bf16[1,128,128]{2,1,0:T(8,128)(2,1)} %bitcast.40), channel_id=1, source_target_pairs={{0,1},{1,0},{2,3},{3,2},{4,5},{5,4},{6,7},{7,6},{8,9},{9,8},{10,11... | collective-permute-start | bytes 98312 | tf_op jit(solution)/shard_map/ppermute | solution.py:59
  99.4 11.6 %collective-permute-start.19 = (bf16[1,128,128]{2,1,0:T(8,128)(2,1)}, bf16[1,128,128]{2,1,0:T(8,128)(2,1)S(1)}, u32[]{:S(2)}, u32[]{:S(2)}) collective-permute-start(bf16[1,128,128]{2,1,0:T(8,128)(2,1)} %bitcast.41), channel_id=1, source_target_pairs={{0,2},{1,3},{2,0},{3,1},{4,6},{5,7},{6,4},{7,5},{8,10},{9,11},{10,... | collective-permute-start | bytes 98312 | tf_op jit(solution)/shard_map/ppermute | solution.py:59
  102.5 8.5 %collective-permute-start.20 = (bf16[1,128,128]{2,1,0:T(8,128)(2,1)}, bf16[1,128,128]{2,1,0:T(8,128)(2,1)S(1)}, u32[]{:S(2)}, u32[]{:S(2)}) collective-permute-start(bf16[1,128,128]{2,1,0:T(8,128)(2,1)} %bitcast.42), channel_id=1, source_target_pairs={{0,3},{1,2},{2,1},{3,0},{4,7},{5,6},{6,5},{7,4},{8,11},{9,10},{10,... | collective-permute-start | bytes 98312 | tf_op jit(solution)/shard_map/ppermute | solution.py:59
  111.0 12.8 %collective-permute-start.23 = (bf16[4,128,128]{2,1,0:T(8,128)(2,1)S(1)}, bf16[4,128,128]{2,1,0:T(8,128)(2,1)S(1)}, u32[]{:S(2)}, u32[]{:S(2)}) collective-permute-start(bf16[4,128,128]{2,1,0:T(8,128)(2,1)S(1)} %pad_maximum_fusion.2), channel_id=1, source_target_pairs={{0,8},{1,9},{2,10},{3,11},{4,12},{5,13},{6,14},{7,15},{8,0},{9,1},... | collective-permute-start | bytes 393224 | tf_op jit(solution)/shard_map/ppermute | solution.py:59
  111.1 12.8 %collective-permute-start.24 = (bf16[4,128,128]{2,1,0:T(8,128)(2,1)S(1)}, bf16[4,128,128]{2,1,0:T(8,128)(2,1)S(1)}, u32[]{:S(2)}, u32[]{:S(2)}) collective-permute-start(bf16[4,128,128]{2,1,0:T(8,128)(2,1)S(1)} %pad_maximum_fusion.2), channel_id=1, source_target_pairs={{0,16},{1,17},{2,18},{3,19},{4,20},{5,21},{6,22},{7,23},{8,24},{9,... | collective-permute-start | bytes 393224 | tf_op jit(solution)/shard_map/ppermute | solution.py:59
  113.7 10.2 %collective-permute-start.25 = (bf16[4,128,128]{2,1,0:T(8,128)(2,1)S(1)}, bf16[4,128,128]{2,1,0:T(8,128)(2,1)S(1)}, u32[]{:S(2)}, u32[]{:S(2)}) collective-permute-start(bf16[4,128,128]{2,1,0:T(8,128)(2,1)S(1)} %pad_maximum_fusion.2), channel_id=1, source_target_pairs={{0,24},{1,25},{2,26},{3,27},{4,28},{5,29},{6,30},{7,31},{8,16},{9,... | collective-permute-start | bytes 393224 | tf_op jit(solution)/shard_map/ppermute | solution.py:59
  113.8 9.1 %collective-permute-start.21 = (bf16[256,128]{1,0:T(8,128)(2,1)}, bf16[256,128]{1,0:T(8,128)(2,1)S(1)}, u32[]{:S(2)}, u32[]{:S(2)}) collective-permute-start(bf16[256,128]{1,0:T(8,128)(2,1)} %get-tuple-element.67), channel_id=1, source_target_pairs={{0,1},{1,2},{2,3},{3,4},{4,5},{5,6},{6,7},{7,8},{8,9},{9,10},{10,1... | collective-permute-start | bytes 196616 | tf_op jit(solution)/shard_map/ppermute | solution.py:223
  115.9 8.0 %collective-permute-start.22 = (bf16[256,128]{1,0:T(8,128)(2,1)}, bf16[256,128]{1,0:T(8,128)(2,1)S(1)}, u32[]{:S(2)}, u32[]{:S(2)}) collective-permute-start(bf16[256,128]{1,0:T(8,128)(2,1)} %get-tuple-element.68), channel_id=1, source_target_pairs={{1,0},{2,1},{3,2},{4,3},{5,4},{6,5},{7,6},{8,7},{9,8},{10,9},{11,1... | collective-permute-start | bytes 196616 | tf_op jit(solution)/shard_map/ppermute | solution.py:223
  (24 other events, 175.7 us)

commit v6 on v4

--- a/solution.py
+++ b/solution.py
@@ -157,16 +157,25 @@
     )(z, band_offsets.reshape(-1), current, *rim_sources, band_tiles)
 
 
-def hub_kernel(n_hub, width, z_ref, hidx_ref, rows_ref, *rest):
+def hub_kernel(n_hub, width, z_ref, hidx_ref, *rest):
     hub_hbm = rest[:n_hub]
-    (ht_hbm, band_ref, deg_ref, seeds_ref,
+    (ht_hbm, band_hbm, deg_hbm, seeds_hbm, pick_ref,
      out_ref, cur_ref, owned_ref, p1_ref, p3_ref, pc_ref,
-     hub, ht, own32, sem) = rest[n_hub:]
+     hub, ht, band, deg, seeds, sem) = rest[n_hub:]
     blocks, k_hub, rows = ht.shape[0], ht.shape[1], ht.shape[2]
     own = cur_ref.shape[0]
     n_own = owned_ref.shape[0]
-    hub_copies = [pltpu.make_async_copy(ht_hbm.at[b], ht.at[b], sem.at[n_hub + b]) for b in range(blocks)]
-    hub_copies[0].start()
+    per_block = []
+    for b in range(blocks):
+        span = pl.ds(b * rows, rows)
+        per_block.append([
+            pltpu.make_async_copy(ht_hbm.at[b], ht.at[b], sem.at[n_hub + 4 * b]),
+            pltpu.make_async_copy(band_hbm.at[span], band.at[span], sem.at[n_hub + 4 * b + 1]),
+            pltpu.make_async_copy(deg_hbm.at[span], deg.at[span], sem.at[n_hub + 4 * b + 2]),
+            pltpu.make_async_copy(seeds_hbm.at[span], seeds.at[span], sem.at[n_hub + 4 * b + 3]),
+        ])
+    for c in per_block[0]:
+        c.start()
     copies = []
     at = 0
     for i, piece in enumerate(hub_hbm):
@@ -176,26 +185,23 @@
     for c in copies:
         c.start()
     for b in range(1, blocks):
-        hub_copies[b].start()
+        for c in per_block[b]:
+            c.start()
     for c in copies:
         c.wait()
     for b in range(blocks):
-        hub_copies[b].wait()
+        for c in per_block[b]:
+            c.wait()
+        span = pl.ds(b * rows, rows)
         acc = jnp.zeros((rows, out_ref.shape[1]), jnp.float32)
         for h in range(k_hub):
             p = hidx_ref[b * k_hub + h]
             acc = acc + jnp.dot(ht[b, h], hub[p], preferred_element_type=jnp.float32)
-        gathered = (band_ref[pl.ds(b * rows, rows), :] + acc) / deg_ref[pl.ds(b * rows, rows), :]
-        labels = spread_weight * gathered + (1.0 - spread_weight) * seeds_ref[pl.ds(b * rows, rows), :]
-        out_ref[pl.ds(b * rows, rows), :] = labels
-        cur_ref[pl.ds(b * rows, rows), :] = labels.astype(cur_ref.dtype)
-
-    def pick(j, carry):
-        own32[pl.ds(j, 1), :] = out_ref[pl.ds(rows_ref[j], 1), :]
-        return carry
-
-    lax.fori_loop(0, n_own, pick, 0)
-    owned = own32[...].astype(owned_ref.dtype)
+        gathered = (band[span] + acc) / deg[span]
+        labels = spread_weight * gathered + (1.0 - spread_weight) * seeds[span]
+        out_ref[span, :] = labels
+        cur_ref[span, :] = labels.astype(cur_ref.dtype)
+    owned = jnp.dot(pick_ref[...], cur_ref[...], preferred_element_type=jnp.float32).astype(owned_ref.dtype)
     owned_ref[...] = owned
     p1_ref[pl.ds(0, n_own), :] = owned
     p3_ref[pl.ds(0, n_own), :] = owned
@@ -207,19 +213,19 @@
     pc_ref[...] = jnp.where(z == 3, top, bottom)
 
 
-def hub_call(z, hub_index, hub_rows, hub_pieces, hub_tiles, band, degree, seeds, width):
+def hub_call(z, hub_index, pick, hub_pieces, hub_tiles, band, degree, seeds, width):
     blocks, k_hub, rows, _ = hub_tiles.shape
     classes = seeds.shape[1]
     n_hub = len(hub_pieces)
     n_hub_blocks = sum(p.shape[0] for p in hub_pieces)
-    n_own = hub_rows.shape[0]
+    n_own = pick.shape[0]
     bf = jnp.bfloat16
     flops = 2 * blocks * k_hub * rows * rows * classes
     bytes_accessed = hub_tiles.size * 2 + n_hub_blocks * rows * classes * 2 + seeds.size * 4 * 4
     return pl.pallas_call(
         functools.partial(hub_kernel, n_hub, width),
         cost_estimate=pl.CostEstimate(flops=flops, transcendentals=0, bytes_accessed=bytes_accessed),
-        in_specs=[SMEM, SMEM, SMEM] + [ANY] * (n_hub + 1) + [VMEM, VMEM, VMEM],
+        in_specs=[SMEM, SMEM] + [ANY] * (n_hub + 4) + [VMEM],
         out_specs=[VMEM] * 6,
         out_shape=[
             jax.ShapeDtypeStruct(seeds.shape, jnp.float32),
@@ -232,10 +238,12 @@
         scratch_shapes=[
             pltpu.VMEM((n_hub_blocks, rows, classes), bf),
             pltpu.VMEM(hub_tiles.shape, hub_tiles.dtype),
-            pltpu.VMEM((n_own, classes), jnp.float32),
-            pltpu.SemaphoreType.DMA((n_hub + blocks,)),
+            pltpu.VMEM(seeds.shape, jnp.float32),
+            pltpu.VMEM(degree.shape, jnp.float32),
+            pltpu.VMEM(seeds.shape, jnp.float32),
+            pltpu.SemaphoreType.DMA((n_hub + 4 * blocks,)),
         ],
-    )(z, hub_index.reshape(-1), hub_rows, *hub_pieces, hub_tiles, band, degree, seeds)
+    )(z, hub_index.reshape(-1), *hub_pieces, hub_tiles, band, degree, seeds, pick)
 
 
 def body(seed_scores, seed_mask, band_offsets, band_tiles, hub_blocks, hub_tiles, hub_rows):
@@ -251,6 +259,7 @@
     owned = current[hub_rows]
     p1, p3, pc = payloads(current, owned, z[0], width)
     fast = fast_path(owned, block_rows)
+    pick = (hub_rows[:, None] == jnp.arange(current.shape[0], dtype=hub_rows.dtype)[None, :]).astype(jnp.bfloat16)
     for step in range(ITERS):
         middle = functools.partial(
             band_call, z, band_offsets, current, band_tiles=band_tiles, fast=fast, n_own=owned.shape[0], width=width
@@ -259,7 +268,7 @@
             current, owned, p1, p3, pc, hub_blocks, width, block_rows, lambda rims: middle(rims)
         )
         labels, current, owned, p1, p3, pc = hub_call(
-            z, hub_index, hub_rows, hub_pieces, hub_tiles, band, degree, seeds, width
+            z, hub_index, pick, hub_pieces, hub_tiles, band, degree, seeds, width
         )
     return labels
 

time: 115 us -> 108 us (0.939)
  local copies, waits for them, and re-layouts: 14.7 us -> 12.1 us
  Pallas kernels: 34.8 us -> 32.3 us
  waiting for transfers between devices: 16.8 us -> 15.6 us
    pallas_call x3, Pallas kernels: 19.5 us -> 16.9 us  [hub_call(): pl.pallas_call(functools.partial(hub_kernel, n_hub, width), cost_estimate...]
    reduce_sum x1, other arithmetic: 0.41 us -> 2.15 us  [body(): jnp.sum(band_tiles, axis=(1, 3), dtype=jnp.float32)]
    reduce_sum x1, other arithmetic: 1.68 us -> 0.28 us  [body(): jnp.sum(hub_tiles, axis=(1, 3), dtype=jnp.float32)]
    unnamed x52 -> x60, local copies, waits for them, and re-layouts: 9.26 us -> 8.23 us
  transfers between devices with their start and end apart: 24 -> 24, of which waited for: 7 -> 6; matrix products, arithmetic and copies ran while one was open for 11% -> 11% of each run, Pallas kernels for 14% -> 14%
where the time goes in v6:
time: 108 us; the launch traced here: 107 us
  starting transfers between devices  38.2 us (35%)
  Pallas kernels  32.3 us (30%)
  waiting for transfers between devices  15.6 us (14%)
  local copies, waits for them, and re-layouts  12.1 us (11%)
  other arithmetic  8.24 us (8%)
    pallas_call x3, Pallas kernels, hub_call(): pl.pallas_call(functools.partial(hub_kernel, n_hub, width), cost_estimate...  16.9 us
    pallas_call x3, Pallas kernels, band_call(): pl.pallas_call(functools.partial(band_kernel, fast, n_own), cost_estimate...  15.3 us
    ppermute x12, starting transfers between devices, exchange(): recvs = [lax.ppermute(buf, AXES, pairs(m)) for m in group]  13.9 us
    ppermute x3, starting transfers between devices, exchange(): rc = lax.ppermute(pc, AXES, cross)  13 us
    ppermute x3, waiting for transfers between devices, exchange(): r3 = lax.ppermute(p3, AXES, pairs(3))  10 us
    unnamed x60, local copies, waits for them, and re-layouts  8.23 us
    ppermute x3, starting transfers between devices, exchange(): r3 = lax.ppermute(p3, AXES, pairs(3))  5.78 us
    ppermute x12, waiting for transfers between devices, exchange(): recvs = [lax.ppermute(buf, AXES, pairs(m)) for m in group]  3.1 us
  transfers between devices with their start and end apart: 24, of which 6 were waited for; matrix products, arithmetic and copies ran while one was open for 11% of the time, Pallas kernels for 14%

profile of v6, /device:TPU:5, one launch (start us, length us, event | category | flops | bytes accessed | tf_op | source)
XLA Modules:
  0.0 106.9 jit_solution(564811924574361075)
XLA Ops:
  1.4 1.9 %convert_multiply_fusion = (f32[1024,128]{1,0:T(8,128)}, bf16[1024,128]{1,0:T(8,128)(2,1)S(1)}) fusion(bf16[1024,128]{1,0:T(8,128)(2,1)} %param.10, f32[1024]{0:T(1024)S(1)} %convert_element_type.18), kind=kLoop, calls=%fused_computation.5 | loop fusion | flops 393216 | bytes 1052672 | tf_op jit(solution)/shard_map/mul | solution.py:251
  4.0 2.4 %collective-permute-start.1 = (bf16[128,128]{1,0:T(8,128)(2,1)S(1)}, bf16[128,128]{1,0:T(8,128)(2,1)S(1)}, u32[]{:S(2)}, u32[]{:S(2)}) collective-permute-start(bf16[128,128]{1,0:T(8,128)(2,1)S(1)} %gather_fusion.1), channel_id=1, source_target_pairs={{0,2},{1,3},{2,0},{3,1},{4,6},{5,7},{6,4},{7,5},{8,10},{9,11},{10,... | collective-permute-start | bytes 98312 | tf_op jit(solution)/shard_map/ppermute | solution.py:50
  6.4 3.8 %collective-permute-start.3 = (bf16[256,128]{1,0:T(8,128)(2,1)S(1)}, bf16[256,128]{1,0:T(8,128)(2,1)S(1)}, u32[]{:S(2)}, u32[]{:S(2)}) collective-permute-start(bf16[256,128]{1,0:T(8,128)(2,1)S(1)} %get-tuple-element.53), channel_id=1, source_target_pairs={{3,4},{7,8},{11,12},{15,16},{19,20},{23,24},{27,28},{4,3},{8,7},{1... | collective-permute-start | bytes 196616 | tf_op jit(solution)/shard_map/ppermute | solution.py:55
  10.3 3.2 %collective-permute-start.2 = (bf16[384,128]{1,0:T(8,128)(2,1)S(1)}, bf16[384,128]{1,0:T(8,128)(2,1)S(1)}, u32[]{:S(2)}, u32[]{:S(2)}) collective-permute-start(bf16[384,128]{1,0:T(8,128)(2,1)S(1)} %get-tuple-element.56), channel_id=1, source_target_pairs={{0,3},{1,2},{2,1},{3,0},{4,7},{5,6},{6,5},{7,4},{8,11},{9,10},{10,... | collective-permute-start | bytes 294920 | tf_op jit(solution)/shard_map/ppermute | solution.py:51
  13.5 2.2 %convert_reduce_fusion = f32[8,128]{1,0:T(8,128)S(1)} fusion(bf16[8,10,128,128]{3,2,1,0:T(8,128)(2,1)} %rest_3_.5), kind=kLoop, calls=%fused_computation.2 | loop fusion | flops 2620416 | bytes 2625536 | tf_op jit(solution)/shard_map/reduce_sum | solution.py:252
  17.0 2.5 %collective-permute-done.rest_0_ = bf16[384,128]{1,0:T(8,128)(2,1)S(1)} collective-permute-done((bf16[384,128]{1,0:T(8,128)(2,1)S(1)}, bf16[384,128]{1,0:T(8,128)(2,1)S(1)}, u32[]{:S(2)}, u32[]{:S(2)}) %collective-permute-start) | collective-permute-done | bytes 98336 | tf_op jit(solution)/shard_map/ppermute | solution.py:49
  22.9 5.2 %shard_map.100.rest_3_ = f32[1024,128]{1,0:T(8,128)} custom-call(s32[1]{0:T(128)} %bitcast.z_ref, s32[80]{0:T(128)} %reshape.42.off_ref, bf16[1024,128]{1,0:T(8,128)(2,1)} %copy-done.2, bf16[384,128]{1,0:T(8,128)(2,1)} %copy-done.10, bf16[384,128]{1,0:T(8,128)(2,1)} %copy-done.9, bf16[256,128]{1,0:T(8,128)(2,1)} %copy-done.15, bf16[8,10,128,128]{3,2,1,0:T(8,128)(2,1)} %rest_3_.5), custom_call_target="tpu_custom_call" | custom-call | flops 335544320 | bytes 3670016 | tf_op jit(solution)/shard_map/pallas_call | solution.py:146
  34.6 5.6 %shard_map.101 = (f32[1024,128]{1,0:T(8,128)}, bf16[1024,128]{1,0:T(8,128)(2,1)}, bf16[128,128]{1,0:T(8,128)(2,1)}, bf16[384,128]{1,0:T(8,128)(2,1)}, bf16[384,1...) custom-call(s32[1]{0:T(128)} %bitcast.z_ref, s32[48]{0:T(128)} %gather_fusion, bf16[16,128,128]{2,1,0:T(8,128)(2,1)} %copy-done.3, ...), custom_call_target="tpu_custom_call" | custom-call | flops 201326592 | bytes 4718592 | tf_op jit(solution)/shard_map/pallas_call | solution.py:225
  42.4 4.5 %collective-permute-start.11 = (bf16[256,128]{1,0:T(8,128)(2,1)}, bf16[256,128]{1,0:T(8,128)(2,1)S(1)}, u32[]{:S(2)}, u32[]{:S(2)}) collective-permute-start(bf16[256,128]{1,0:T(8,128)(2,1)} %get-tuple-element.36), channel_id=1, source_target_pairs={{3,4},{7,8},{11,12},{15,16},{19,20},{23,24},{27,28},{4,3},{8,7},{1... | collective-permute-start | bytes 196616 | tf_op jit(solution)/shard_map/ppermute | solution.py:55
  47.0 1.7 %collective-permute-start.10 = (bf16[384,128]{1,0:T(8,128)(2,1)}, bf16[384,128]{1,0:T(8,128)(2,1)S(1)}, u32[]{:S(2)}, u32[]{:S(2)}) collective-permute-start(bf16[384,128]{1,0:T(8,128)(2,1)} %get-tuple-element.34), channel_id=1, source_target_pairs={{0,3},{1,2},{2,1},{3,0},{4,7},{5,6},{6,5},{7,4},{8,11},{9,10},{10,... | collective-permute-start | bytes 294920 | tf_op jit(solution)/shard_map/ppermute | solution.py:51
  48.7 3.8 %collective-permute-done.10.rest_1_ = bf16[384,128]{1,0:T(8,128)(2,1)S(1)} collective-permute-done((bf16[384,128]{1,0:T(8,128)(2,1)}, bf16[384,128]{1,0:T(8,128)(2,1)S(1)}, u32[]{:S(2)}, u32[]{:S(2)}) %collective-permute-start.10) | collective-permute-done | bytes 98336 | tf_op jit(solution)/shard_map/ppermute | solution.py:51
  53.3 2.3 %collective-permute-start.14 = (bf16[4,128,128]{2,1,0:T(8,128)(2,1)S(1)}, bf16[4,128,128]{2,1,0:T(8,128)(2,1)S(1)}, u32[]{:S(2)}, u32[]{:S(2)}) collective-permute-start(bf16[4,128,128]{2,1,0:T(8,128)(2,1)S(1)} %pad_maximum_fusion.1), channel_id=1, source_target_pairs={{0,24},{1,25},{2,26},{3,27},{4,28},{5,29},{6,30},{7,31},{8,16},{9,... | collective-permute-start | bytes 393224 | tf_op jit(solution)/shard_map/ppermute | solution.py:63
  56.7 5.1 %shard_map.102.rest_3_ = f32[1024,128]{1,0:T(8,128)} custom-call(s32[1]{0:T(128)} %bitcast.z_ref, s32[80]{0:T(128)} %reshape.42.off_ref, bf16[1024,128]{1,0:T(8,128)(2,1)} %get-tuple-element.35.cur_hbm, bf16[384,128]{1,0:T(8,128)(2,1)} %copy-done.12, bf16[384,128]{1,0:T(8,128)(2,1)} %copy-done.14, bf16[256,128]{1,0:T(8,128)(2,1)} %copy-done.17, ...), custom_call_target="tpu_custom_call" | custom-call | flops 335544320 | bytes 3670016 | tf_op jit(solution)/shard_map/pallas_call | solution.py:146
  62.6 2.9 %collective-permute-start.15 = (bf16[16,128,128]{2,1,0:T(8,128)(2,1)S(1)}, bf16[16,128,128]{2,1,0:T(8,128)(2,1)S(1)}, u32[]{:S(2)}, u32[]{:S(2)}) collective-permute-start(bf16[16,128,128]{2,1,0:T(8,128)(2,1)S(1)} %constant_dynamic-update-slice_fusion.7.rest_0_), channel_id=1, source_target_pairs={{0,4},{1,5},{2,6},{3,7},{4,0},{5,1},{6,2},{7,3},{8,12},{9,13},{10,... | collective-permute-start | bytes 1572872 | tf_op jit(solution)/shard_map/ppermute | solution.py:63
  65.5 1.5 %collective-permute-done.15.rest_1_ = bf16[16,128,128]{2,1,0:T(8,128)(2,1)S(1)} collective-permute-done((bf16[16,128,128]{2,1,0:T(8,128)(2,1)S(1)}, bf16[16,128,128]{2,1,0:T(8,128)(2,1)S(1)}, u32[]{:S(2)}, u32[]{:S(2)}) %collective-permute-start.15) | collective-permute-done | bytes 524320 | tf_op jit(solution)/shard_map/ppermute | solution.py:63
  67.8 5.6 %shard_map.103 = (f32[1024,128]{1,0:T(8,128)}, bf16[1024,128]{1,0:T(8,128)(2,1)}, bf16[128,128]{1,0:T(8,128)(2,1)}, bf16[384,128]{1,0:T(8,128)(2,1)}, bf16[384,1...) custom-call(s32[1]{0:T(128)} %bitcast.z_ref, s32[48]{0:T(128)} %gather_fusion, bf16[16,128,128]{2,1,0:T(8,128)(2,1)} %copy-done.4, ...), custom_call_target="tpu_custom_call" | custom-call | flops 201326592 | bytes 4718592 | tf_op jit(solution)/shard_map/pallas_call | solution.py:225
  73.6 1.7 %collective-permute-start.16 = (bf16[384,128]{1,0:T(8,128)(2,1)}, bf16[384,128]{1,0:T(8,128)(2,1)S(1)}, u32[]{:S(2)}, u32[]{:S(2)}) collective-permute-start(bf16[384,128]{1,0:T(8,128)(2,1)} %get-tuple-element.42), channel_id=1, source_target_pairs={{0,1},{1,0},{2,3},{3,2},{4,5},{5,4},{6,7},{7,6},{8,9},{9,8},{10,11... | collective-permute-start | bytes 294920 | tf_op jit(solution)/shard_map/ppermute | solution.py:49
  76.0 4.6 %collective-permute-start.19 = (bf16[256,128]{1,0:T(8,128)(2,1)}, bf16[256,128]{1,0:T(8,128)(2,1)S(1)}, u32[]{:S(2)}, u32[]{:S(2)}) collective-permute-start(bf16[256,128]{1,0:T(8,128)(2,1)} %get-tuple-element.45), channel_id=1, source_target_pairs={{3,4},{7,8},{11,12},{15,16},{19,20},{23,24},{27,28},{4,3},{8,7},{1... | collective-permute-start | bytes 196616 | tf_op jit(solution)/shard_map/ppermute | solution.py:55
  81.5 5.7 %collective-permute-done.18.rest_1_ = bf16[384,128]{1,0:T(8,128)(2,1)S(1)} collective-permute-done((bf16[384,128]{1,0:T(8,128)(2,1)}, bf16[384,128]{1,0:T(8,128)(2,1)S(1)}, u32[]{:S(2)}, u32[]{:S(2)}) %collective-permute-start.18) | collective-permute-done | bytes 98336 | tf_op jit(solution)/shard_map/ppermute | solution.py:51
  89.0 1.7 %collective-permute-start.20 = (bf16[4,128,128]{2,1,0:T(8,128)(2,1)S(1)}, bf16[4,128,128]{2,1,0:T(8,128)(2,1)S(1)}, u32[]{:S(2)}, u32[]{:S(2)}) collective-permute-start(bf16[4,128,128]{2,1,0:T(8,128)(2,1)S(1)} %pad_maximum_fusion.2), channel_id=1, source_target_pairs={{0,8},{1,9},{2,10},{3,11},{4,12},{5,13},{6,14},{7,15},{8,0},{9,1},... | collective-permute-start | bytes 393224 | tf_op jit(solution)/shard_map/ppermute | solution.py:63
  91.3 5.1 %shard_map.104.rest_3_ = f32[1024,128]{1,0:T(8,128)} custom-call(s32[1]{0:T(128)} %bitcast.z_ref, s32[80]{0:T(128)} %reshape.42.off_ref, bf16[1024,128]{1,0:T(8,128)(2,1)} %get-tuple-element.44.cur_hbm, bf16[384,128]{1,0:T(8,128)(2,1)} %copy-done.11, bf16[384,128]{1,0:T(8,128)(2,1)} %copy-done.13, bf16[256,128]{1,0:T(8,128)(2,1)} %copy-done.16, ...), custom_call_target="tpu_custom_call" | custom-call | flops 335544320 | bytes 3670016 | tf_op jit(solution)/shard_map/pallas_call | solution.py:146
  97.3 1.6 %collective-permute-start.23 = (bf16[16,128,128]{2,1,0:T(8,128)(2,1)S(1)}, bf16[16,128,128]{2,1,0:T(8,128)(2,1)S(1)}, u32[]{:S(2)}, u32[]{:S(2)}) collective-permute-start(bf16[16,128,128]{2,1,0:T(8,128)(2,1)S(1)} %constant_dynamic-update-slice_fusion.14.rest_0_), channel_id=1, source_target_pairs={{0,4},{1,5},{2,6},{3,7},{4,0},{5,1},{6,2},{7,3},{8,12},{9,13},{10,... | collective-permute-start | bytes 1572872 | tf_op jit(solution)/shard_map/ppermute | solution.py:63
  98.9 1.5 %collective-permute-done.23.rest_1_ = bf16[16,128,128]{2,1,0:T(8,128)(2,1)S(1)} collective-permute-done((bf16[16,128,128]{2,1,0:T(8,128)(2,1)S(1)}, bf16[16,128,128]{2,1,0:T(8,128)(2,1)S(1)}, u32[]{:S(2)}, u32[]{:S(2)}) %collective-permute-start.23) | collective-permute-done | bytes 524320 | tf_op jit(solution)/shard_map/ppermute | solution.py:63
  101.3 5.6 %shard_map.105 = (f32[1024,128]{1,0:T(8,128)}, bf16[1024,128]{1,0:T(8,128)(2,1)}, bf16[128,128]{1,0:T(8,128)(2,1)}, bf16[384,128]{1,0:T(8,128)(2,1)}, bf16[384,1...) custom-call(s32[1]{0:T(128)} %bitcast.z_ref, s32[48]{0:T(128)} %gather_fusion, bf16[16,128,128]{2,1,0:T(8,128)(2,1)} %copy-done.5, ...), custom_call_target="tpu_custom_call" | custom-call | flops 201326592 | bytes 4718592 | tf_op jit(solution)/shard_map/pallas_call | solution.py:225
  (119 shorter events, 24.7 us)
Async XLA Ops:
  4.0 15.4 %collective-permute-start.1 = (bf16[128,128]{1,0:T(8,128)(2,1)S(1)}, bf16[128,128]{1,0:T(8,128)(2,1)S(1)}, u32[]{:S(2)}, u32[]{:S(2)}) collective-permute-start(bf16[128,128]{1,0:T(8,128)(2,1)S(1)} %gather_fusion.1), channel_id=1, source_target_pairs={{0,2},{1,3},{2,0},{3,1},{4,6},{5,7},{6,4},{7,5},{8,10},{9,11},{10,... | collective-permute-start | bytes 98312 | tf_op jit(solution)/shard_map/ppermute | solution.py:50
  6.4 15.8 %collective-permute-start.3 = (bf16[256,128]{1,0:T(8,128)(2,1)S(1)}, bf16[256,128]{1,0:T(8,128)(2,1)S(1)}, u32[]{:S(2)}, u32[]{:S(2)}) collective-permute-start(bf16[256,128]{1,0:T(8,128)(2,1)S(1)} %get-tuple-element.53), channel_id=1, source_target_pairs={{3,4},{7,8},{11,12},{15,16},{19,20},{23,24},{27,28},{4,3},{8,7},{1... | collective-permute-start | bytes 196616 | tf_op jit(solution)/shard_map/ppermute | solution.py:55
  10.3 6.7 %collective-permute-start.2 = (bf16[384,128]{1,0:T(8,128)(2,1)S(1)}, bf16[384,128]{1,0:T(8,128)(2,1)S(1)}, u32[]{:S(2)}, u32[]{:S(2)}) collective-permute-start(bf16[384,128]{1,0:T(8,128)(2,1)S(1)} %get-tuple-element.56), channel_id=1, source_target_pairs={{0,3},{1,2},{2,1},{3,0},{4,7},{5,6},{6,5},{7,4},{8,11},{9,10},{10,... | collective-permute-start | bytes 294920 | tf_op jit(solution)/shard_map/ppermute | solution.py:51
  13.5 6.0 %collective-permute-start = (bf16[384,128]{1,0:T(8,128)(2,1)S(1)}, bf16[384,128]{1,0:T(8,128)(2,1)S(1)}, u32[]{:S(2)}, u32[]{:S(2)}) collective-permute-start(bf16[384,128]{1,0:T(8,128)(2,1)S(1)} %get-tuple-element.57), channel_id=1, source_target_pairs={{0,1},{1,0},{2,3},{3,2},{4,5},{5,4},{6,7},{7,6},{8,9},{9,8},{10,11... | collective-permute-start | bytes 294920 | tf_op jit(solution)/shard_map/ppermute | solution.py:49
  19.5 9.3 %collective-permute-start.6 = (bf16[4,128,128]{2,1,0:T(8,128)(2,1)S(1)}, bf16[4,128,128]{2,1,0:T(8,128)(2,1)S(1)}, u32[]{:S(2)}, u32[]{:S(2)}) collective-permute-start(bf16[4,128,128]{2,1,0:T(8,128)(2,1)S(1)} %pad_maximum_fusion), channel_id=1, source_target_pairs={{0,24},{1,25},{2,26},{3,27},{4,28},{5,29},{6,30},{7,31},{8,16},{9,... | collective-permute-start | bytes 393224 | tf_op jit(solution)/shard_map/ppermute | solution.py:63
  20.7 8.1 %collective-permute-start.5 = (bf16[4,128,128]{2,1,0:T(8,128)(2,1)S(1)}, bf16[4,128,128]{2,1,0:T(8,128)(2,1)S(1)}, u32[]{:S(2)}, u32[]{:S(2)}) collective-permute-start(bf16[4,128,128]{2,1,0:T(8,128)(2,1)S(1)} %pad_maximum_fusion), channel_id=1, source_target_pairs={{0,16},{1,17},{2,18},{3,19},{4,20},{5,21},{6,22},{7,23},{8,24},{9,... | collective-permute-start | bytes 393224 | tf_op jit(solution)/shard_map/ppermute | solution.py:63
  20.7 8.1 %collective-permute-start.4 = (bf16[4,128,128]{2,1,0:T(8,128)(2,1)S(1)}, bf16[4,128,128]{2,1,0:T(8,128)(2,1)S(1)}, u32[]{:S(2)}, u32[]{:S(2)}) collective-permute-start(bf16[4,128,128]{2,1,0:T(8,128)(2,1)S(1)} %pad_maximum_fusion), channel_id=1, source_target_pairs={{0,8},{1,9},{2,10},{3,11},{4,12},{5,13},{6,14},{7,15},{8,0},{9,1},... | collective-permute-start | bytes 393224 | tf_op jit(solution)/shard_map/ppermute | solution.py:63
  28.9 4.8 %collective-permute-start.7 = (bf16[16,128,128]{2,1,0:T(8,128)(2,1)S(1)}, bf16[16,128,128]{2,1,0:T(8,128)(2,1)S(1)}, u32[]{:S(2)}, u32[]{:S(2)}) collective-permute-start(bf16[16,128,128]{2,1,0:T(8,128)(2,1)S(1)} %constant_dynamic-update-slice_fusion.rest_0_), channel_id=1, source_target_pairs={{0,4},{1,5},{2,6},{3,7},{4,0},{5,1},{6,2},{7,3},{8,12},{9,13},{10,... | collective-permute-start | bytes 1572872 | tf_op jit(solution)/shard_map/ppermute | solution.py:63
  40.2 12.3 %collective-permute-start.9 = (bf16[128,128]{1,0:T(8,128)(2,1)}, bf16[128,128]{1,0:T(8,128)(2,1)S(1)}, u32[]{:S(2)}, u32[]{:S(2)}) collective-permute-start(bf16[128,128]{1,0:T(8,128)(2,1)} %get-tuple-element.32), channel_id=1, source_target_pairs={{0,2},{1,3},{2,0},{3,1},{4,6},{5,7},{6,4},{7,5},{8,10},{9,11},{10,... | collective-permute-start | bytes 98312 | tf_op jit(solution)/shard_map/ppermute | solution.py:50
  40.6 8.0 %collective-permute-start.8 = (bf16[384,128]{1,0:T(8,128)(2,1)}, bf16[384,128]{1,0:T(8,128)(2,1)S(1)}, u32[]{:S(2)}, u32[]{:S(2)}) collective-permute-start(bf16[384,128]{1,0:T(8,128)(2,1)} %get-tuple-element.33), channel_id=1, source_target_pairs={{0,1},{1,0},{2,3},{3,2},{4,5},{5,4},{6,7},{7,6},{8,9},{9,8},{10,11... | collective-permute-start | bytes 294920 | tf_op jit(solution)/shard_map/ppermute | solution.py:49
  42.4 13.7 %collective-permute-start.11 = (bf16[256,128]{1,0:T(8,128)(2,1)}, bf16[256,128]{1,0:T(8,128)(2,1)S(1)}, u32[]{:S(2)}, u32[]{:S(2)}) collective-permute-start(bf16[256,128]{1,0:T(8,128)(2,1)} %get-tuple-element.36), channel_id=1, source_target_pairs={{3,4},{7,8},{11,12},{15,16},{19,20},{23,24},{27,28},{4,3},{8,7},{1... | collective-permute-start | bytes 196616 | tf_op jit(solution)/shard_map/ppermute | solution.py:55
  47.0 5.5 %collective-permute-start.10 = (bf16[384,128]{1,0:T(8,128)(2,1)}, bf16[384,128]{1,0:T(8,128)(2,1)S(1)}, u32[]{:S(2)}, u32[]{:S(2)}) collective-permute-start(bf16[384,128]{1,0:T(8,128)(2,1)} %get-tuple-element.34), channel_id=1, source_target_pairs={{0,3},{1,2},{2,1},{3,0},{4,7},{5,6},{6,5},{7,4},{8,11},{9,10},{10,... | collective-permute-start | bytes 294920 | tf_op jit(solution)/shard_map/ppermute | solution.py:51
  53.3 9.2 %collective-permute-start.14 = (bf16[4,128,128]{2,1,0:T(8,128)(2,1)S(1)}, bf16[4,128,128]{2,1,0:T(8,128)(2,1)S(1)}, u32[]{:S(2)}, u32[]{:S(2)}) collective-permute-start(bf16[4,128,128]{2,1,0:T(8,128)(2,1)S(1)} %pad_maximum_fusion.1), channel_id=1, source_target_pairs={{0,24},{1,25},{2,26},{3,27},{4,28},{5,29},{6,30},{7,31},{8,16},{9,... | collective-permute-start | bytes 393224 | tf_op jit(solution)/shard_map/ppermute | solution.py:63
  55.6 6.9 %collective-permute-start.13 = (bf16[4,128,128]{2,1,0:T(8,128)(2,1)S(1)}, bf16[4,128,128]{2,1,0:T(8,128)(2,1)S(1)}, u32[]{:S(2)}, u32[]{:S(2)}) collective-permute-start(bf16[4,128,128]{2,1,0:T(8,128)(2,1)S(1)} %pad_maximum_fusion.1), channel_id=1, source_target_pairs={{0,16},{1,17},{2,18},{3,19},{4,20},{5,21},{6,22},{7,23},{8,24},{9,... | collective-permute-start | bytes 393224 | tf_op jit(solution)/shard_map/ppermute | solution.py:63
  55.6 6.9 %collective-permute-start.12 = (bf16[4,128,128]{2,1,0:T(8,128)(2,1)S(1)}, bf16[4,128,128]{2,1,0:T(8,128)(2,1)S(1)}, u32[]{:S(2)}, u32[]{:S(2)}) collective-permute-start(bf16[4,128,128]{2,1,0:T(8,128)(2,1)S(1)} %pad_maximum_fusion.1), channel_id=1, source_target_pairs={{0,8},{1,9},{2,10},{3,11},{4,12},{5,13},{6,14},{7,15},{8,0},{9,1},... | collective-permute-start | bytes 393224 | tf_op jit(solution)/shard_map/ppermute | solution.py:63
  62.6 4.4 %collective-permute-start.15 = (bf16[16,128,128]{2,1,0:T(8,128)(2,1)S(1)}, bf16[16,128,128]{2,1,0:T(8,128)(2,1)S(1)}, u32[]{:S(2)}, u32[]{:S(2)}) collective-permute-start(bf16[16,128,128]{2,1,0:T(8,128)(2,1)S(1)} %constant_dynamic-update-slice_fusion.7.rest_0_), channel_id=1, source_target_pairs={{0,4},{1,5},{2,6},{3,7},{4,0},{5,1},{6,2},{7,3},{8,12},{9,13},{10,... | collective-permute-start | bytes 1572872 | tf_op jit(solution)/shard_map/ppermute | solution.py:63
  73.5 13.7 %collective-permute-start.17 = (bf16[128,128]{1,0:T(8,128)(2,1)}, bf16[128,128]{1,0:T(8,128)(2,1)S(1)}, u32[]{:S(2)}, u32[]{:S(2)}) collective-permute-start(bf16[128,128]{1,0:T(8,128)(2,1)} %get-tuple-element.41), channel_id=1, source_target_pairs={{0,2},{1,3},{2,0},{3,1},{4,6},{5,7},{6,4},{7,5},{8,10},{9,11},{10,... | collective-permute-start | bytes 98312 | tf_op jit(solution)/shard_map/ppermute | solution.py:50
  73.6 7.9 %collective-permute-start.16 = (bf16[384,128]{1,0:T(8,128)(2,1)}, bf16[384,128]{1,0:T(8,128)(2,1)S(1)}, u32[]{:S(2)}, u32[]{:S(2)}) collective-permute-start(bf16[384,128]{1,0:T(8,128)(2,1)} %get-tuple-element.42), channel_id=1, source_target_pairs={{0,1},{1,0},{2,3},{3,2},{4,5},{5,4},{6,7},{7,6},{8,9},{9,8},{10,11... | collective-permute-start | bytes 294920 | tf_op jit(solution)/shard_map/ppermute | solution.py:49
  76.0 14.7 %collective-permute-start.19 = (bf16[256,128]{1,0:T(8,128)(2,1)}, bf16[256,128]{1,0:T(8,128)(2,1)S(1)}, u32[]{:S(2)}, u32[]{:S(2)}) collective-permute-start(bf16[256,128]{1,0:T(8,128)(2,1)} %get-tuple-element.45), channel_id=1, source_target_pairs={{3,4},{7,8},{11,12},{15,16},{19,20},{23,24},{27,28},{4,3},{8,7},{1... | collective-permute-start | bytes 196616 | tf_op jit(solution)/shard_map/ppermute | solution.py:55
  80.6 6.6 %collective-permute-start.18 = (bf16[384,128]{1,0:T(8,128)(2,1)}, bf16[384,128]{1,0:T(8,128)(2,1)S(1)}, u32[]{:S(2)}, u32[]{:S(2)}) collective-permute-start(bf16[384,128]{1,0:T(8,128)(2,1)} %get-tuple-element.43), channel_id=1, source_target_pairs={{0,3},{1,2},{2,1},{3,0},{4,7},{5,6},{6,5},{7,4},{8,11},{9,10},{10,... | collective-permute-start | bytes 294920 | tf_op jit(solution)/shard_map/ppermute | solution.py:51
  88.0 9.2 %collective-permute-start.22 = (bf16[4,128,128]{2,1,0:T(8,128)(2,1)S(1)}, bf16[4,128,128]{2,1,0:T(8,128)(2,1)S(1)}, u32[]{:S(2)}, u32[]{:S(2)}) collective-permute-start(bf16[4,128,128]{2,1,0:T(8,128)(2,1)S(1)} %pad_maximum_fusion.2), channel_id=1, source_target_pairs={{0,24},{1,25},{2,26},{3,27},{4,28},{5,29},{6,30},{7,31},{8,16},{9,... | collective-permute-start | bytes 393224 | tf_op jit(solution)/shard_map/ppermute | solution.py:63
  89.0 8.2 %collective-permute-start.21 = (bf16[4,128,128]{2,1,0:T(8,128)(2,1)S(1)}, bf16[4,128,128]{2,1,0:T(8,128)(2,1)S(1)}, u32[]{:S(2)}, u32[]{:S(2)}) collective-permute-start(bf16[4,128,128]{2,1,0:T(8,128)(2,1)S(1)} %pad_maximum_fusion.2), channel_id=1, source_target_pairs={{0,16},{1,17},{2,18},{3,19},{4,20},{5,21},{6,22},{7,23},{8,24},{9,... | collective-permute-start | bytes 393224 | tf_op jit(solution)/shard_map/ppermute | solution.py:63
  89.0 8.2 %collective-permute-start.20 = (bf16[4,128,128]{2,1,0:T(8,128)(2,1)S(1)}, bf16[4,128,128]{2,1,0:T(8,128)(2,1)S(1)}, u32[]{:S(2)}, u32[]{:S(2)}) collective-permute-start(bf16[4,128,128]{2,1,0:T(8,128)(2,1)S(1)} %pad_maximum_fusion.2), channel_id=1, source_target_pairs={{0,8},{1,9},{2,10},{3,11},{4,12},{5,13},{6,14},{7,15},{8,0},{9,1},... | collective-permute-start | bytes 393224 | tf_op jit(solution)/shard_map/ppermute | solution.py:63
  97.3 3.2 %collective-permute-start.23 = (bf16[16,128,128]{2,1,0:T(8,128)(2,1)S(1)}, bf16[16,128,128]{2,1,0:T(8,128)(2,1)S(1)}, u32[]{:S(2)}, u32[]{:S(2)}) collective-permute-start(bf16[16,128,128]{2,1,0:T(8,128)(2,1)S(1)} %constant_dynamic-update-slice_fusion.14.rest_0_), channel_id=1, source_target_pairs={{0,4},{1,5},{2,6},{3,7},{4,0},{5,1},{6,2},{7,3},{8,12},{9,13},{10,... | collective-permute-start | bytes 1572872 | tf_op jit(solution)/shard_map/ppermute | solution.py:63
  (21 other events, 123.8 us)

commit v7 on v6

--- a/solution.py
+++ b/solution.py
@@ -46,9 +46,9 @@
         return middle((low, high)), [hub_all.reshape(-1, block_rows, owned.shape[1])], hub_blocks
     me = lax.axis_index(AXES)
     pairs = lambda m: [(i, i ^ m) for i in range(count)]
+    r3 = lax.ppermute(p3, AXES, pairs(3))
+    r2 = lax.ppermute(owned, AXES, pairs(2))
     r1 = lax.ppermute(p1, AXES, pairs(1))
-    r2 = lax.ppermute(owned, AXES, pairs(2))
-    r3 = lax.ppermute(p3, AXES, pairs(3))
     groups = count // 4
     cross = [(4 * g + 3, 4 * g + 4) for g in range(groups - 1)]
     cross += [(4 * g + 4, 4 * g + 3) for g in range(groups - 1)]
@@ -60,7 +60,8 @@
     pieces = [buf]
     done = None
     for r, group in enumerate(rounds[1:]):
-        recvs = [lax.ppermute(buf, AXES, pairs(m)) for m in group]
+        sent = {m: lax.ppermute(buf, AXES, pairs(m)) for m in sorted(group, key=lambda m: -m)}
+        recvs = [sent[m] for m in group]
         if done is None:
             done, recvs = lax.optimization_barrier((middle((r1, r3, rc)), recvs))
         offs = offs + [o ^ m for m in group for o in offs]

time: 108 us -> 108 us (level)
  no operation moved by 1% of the time
where the time goes in v7:
time: 108 us; the launch traced here: 107 us
  starting transfers between devices  38.2 us (35%)
  Pallas kernels  32.3 us (30%)
  waiting for transfers between devices  15.6 us (14%)
  local copies, waits for them, and re-layouts  12.1 us (11%)
  other arithmetic  8.24 us (8%)
    pallas_call x3, Pallas kernels, hub_call(): pl.pallas_call(functools.partial(hub_kernel, n_hub, width), cost_estimate...  16.9 us
    pallas_call x3, Pallas kernels, band_call(): pl.pallas_call(functools.partial(band_kernel, fast, n_own), cost_estimate...  15.3 us
    ppermute x12, starting transfers between devices, exchange(): lax.ppermute(buf, AXES, pairs(m))  13.9 us
    ppermute x3, starting transfers between devices, exchange(): rc = lax.ppermute(pc, AXES, cross)  13 us
    ppermute x3, waiting for transfers between devices, exchange(): r3 = lax.ppermute(p3, AXES, pairs(3))  10 us
    unnamed x60, local copies, waits for them, and re-layouts  8.23 us
    ppermute x3, starting transfers between devices, exchange(): r3 = lax.ppermute(p3, AXES, pairs(3))  5.78 us
    ppermute x12, waiting for transfers between devices, exchange(): lax.ppermute(buf, AXES, pairs(m))  3.1 us
  transfers between devices with their start and end apart: 24, of which 6 were waited for; matrix products, arithmetic and copies ran while one was open for 11% of the time, Pallas kernels for 14%

profile of v7, /device:TPU:5, one launch (start us, length us, event | category | flops | bytes accessed | tf_op | source)
XLA Modules:
  0.0 106.9 jit_solution(564811924574361075)
XLA Ops:
  1.4 1.9 %convert_multiply_fusion = (f32[1024,128]{1,0:T(8,128)}, bf16[1024,128]{1,0:T(8,128)(2,1)S(1)}) fusion(bf16[1024,128]{1,0:T(8,128)(2,1)} %param.10, f32[1024]{0:T(1024)S(1)} %convert_element_type.18), kind=kLoop, calls=%fused_computation.5 | loop fusion | flops 393216 | bytes 1052672 | tf_op jit(solution)/shard_map/mul | solution.py:252
  4.0 2.4 %collective-permute-start.1 = (bf16[128,128]{1,0:T(8,128)(2,1)S(1)}, bf16[128,128]{1,0:T(8,128)(2,1)S(1)}, u32[]{:S(2)}, u32[]{:S(2)}) collective-permute-start(bf16[128,128]{1,0:T(8,128)(2,1)S(1)} %gather_fusion.1), channel_id=1, source_target_pairs={{0,2},{1,3},{2,0},{3,1},{4,6},{5,7},{6,4},{7,5},{8,10},{9,11},{10,... | collective-permute-start | bytes 98312 | tf_op jit(solution)/shard_map/ppermute | solution.py:50
  6.4 3.8 %collective-permute-start.3 = (bf16[256,128]{1,0:T(8,128)(2,1)S(1)}, bf16[256,128]{1,0:T(8,128)(2,1)S(1)}, u32[]{:S(2)}, u32[]{:S(2)}) collective-permute-start(bf16[256,128]{1,0:T(8,128)(2,1)S(1)} %get-tuple-element.53), channel_id=1, source_target_pairs={{3,4},{7,8},{11,12},{15,16},{19,20},{23,24},{27,28},{4,3},{8,7},{1... | collective-permute-start | bytes 196616 | tf_op jit(solution)/shard_map/ppermute | solution.py:55
  10.3 3.2 %collective-permute-start.2 = (bf16[384,128]{1,0:T(8,128)(2,1)S(1)}, bf16[384,128]{1,0:T(8,128)(2,1)S(1)}, u32[]{:S(2)}, u32[]{:S(2)}) collective-permute-start(bf16[384,128]{1,0:T(8,128)(2,1)S(1)} %get-tuple-element.56), channel_id=1, source_target_pairs={{0,3},{1,2},{2,1},{3,0},{4,7},{5,6},{6,5},{7,4},{8,11},{9,10},{10,... | collective-permute-start | bytes 294920 | tf_op jit(solution)/shard_map/ppermute | solution.py:49
  13.5 2.2 %convert_reduce_fusion = f32[8,128]{1,0:T(8,128)S(1)} fusion(bf16[8,10,128,128]{3,2,1,0:T(8,128)(2,1)} %rest_3_.5), kind=kLoop, calls=%fused_computation.2 | loop fusion | flops 2620416 | bytes 2625536 | tf_op jit(solution)/shard_map/reduce_sum | solution.py:253
  17.0 2.5 %collective-permute-done.rest_0_ = bf16[384,128]{1,0:T(8,128)(2,1)S(1)} collective-permute-done((bf16[384,128]{1,0:T(8,128)(2,1)S(1)}, bf16[384,128]{1,0:T(8,128)(2,1)S(1)}, u32[]{:S(2)}, u32[]{:S(2)}) %collective-permute-start) | collective-permute-done | bytes 98336 | tf_op jit(solution)/shard_map/ppermute | solution.py:51
  22.9 5.2 %shard_map.100.rest_3_ = f32[1024,128]{1,0:T(8,128)} custom-call(s32[1]{0:T(128)} %bitcast.z_ref, s32[80]{0:T(128)} %reshape.42.off_ref, bf16[1024,128]{1,0:T(8,128)(2,1)} %copy-done.2, bf16[384,128]{1,0:T(8,128)(2,1)} %copy-done.10, bf16[384,128]{1,0:T(8,128)(2,1)} %copy-done.9, bf16[256,128]{1,0:T(8,128)(2,1)} %copy-done.15, bf16[8,10,128,128]{3,2,1,0:T(8,128)(2,1)} %rest_3_.5), custom_call_target="tpu_custom_call" | custom-call | flops 335544320 | bytes 3670016 | tf_op jit(solution)/shard_map/pallas_call | solution.py:147
  34.6 5.6 %shard_map.101 = (f32[1024,128]{1,0:T(8,128)}, bf16[1024,128]{1,0:T(8,128)(2,1)}, bf16[128,128]{1,0:T(8,128)(2,1)}, bf16[384,128]{1,0:T(8,128)(2,1)}, bf16[384,1...) custom-call(s32[1]{0:T(128)} %bitcast.z_ref, s32[48]{0:T(128)} %gather_fusion, bf16[16,128,128]{2,1,0:T(8,128)(2,1)} %copy-done.3, ...), custom_call_target="tpu_custom_call" | custom-call | flops 201326592 | bytes 4718592 | tf_op jit(solution)/shard_map/pallas_call | solution.py:226
  42.4 4.5 %collective-permute-start.11 = (bf16[256,128]{1,0:T(8,128)(2,1)}, bf16[256,128]{1,0:T(8,128)(2,1)S(1)}, u32[]{:S(2)}, u32[]{:S(2)}) collective-permute-start(bf16[256,128]{1,0:T(8,128)(2,1)} %get-tuple-element.36), channel_id=1, source_target_pairs={{3,4},{7,8},{11,12},{15,16},{19,20},{23,24},{27,28},{4,3},{8,7},{1... | collective-permute-start | bytes 196616 | tf_op jit(solution)/shard_map/ppermute | solution.py:55
  47.0 1.7 %collective-permute-start.10 = (bf16[384,128]{1,0:T(8,128)(2,1)}, bf16[384,128]{1,0:T(8,128)(2,1)S(1)}, u32[]{:S(2)}, u32[]{:S(2)}) collective-permute-start(bf16[384,128]{1,0:T(8,128)(2,1)} %get-tuple-element.34), channel_id=1, source_target_pairs={{0,3},{1,2},{2,1},{3,0},{4,7},{5,6},{6,5},{7,4},{8,11},{9,10},{10,... | collective-permute-start | bytes 294920 | tf_op jit(solution)/shard_map/ppermute | solution.py:49
  48.7 3.8 %collective-permute-done.10.rest_1_ = bf16[384,128]{1,0:T(8,128)(2,1)S(1)} collective-permute-done((bf16[384,128]{1,0:T(8,128)(2,1)}, bf16[384,128]{1,0:T(8,128)(2,1)S(1)}, u32[]{:S(2)}, u32[]{:S(2)}) %collective-permute-start.10) | collective-permute-done | bytes 98336 | tf_op jit(solution)/shard_map/ppermute | solution.py:49
  53.3 2.3 %collective-permute-start.14 = (bf16[4,128,128]{2,1,0:T(8,128)(2,1)S(1)}, bf16[4,128,128]{2,1,0:T(8,128)(2,1)S(1)}, u32[]{:S(2)}, u32[]{:S(2)}) collective-permute-start(bf16[4,128,128]{2,1,0:T(8,128)(2,1)S(1)} %pad_maximum_fusion.1), channel_id=1, source_target_pairs={{0,24},{1,25},{2,26},{3,27},{4,28},{5,29},{6,30},{7,31},{8,16},{9,... | collective-permute-start | bytes 393224 | tf_op jit(solution)/shard_map/ppermute | solution.py:63
  56.7 5.1 %shard_map.102.rest_3_ = f32[1024,128]{1,0:T(8,128)} custom-call(s32[1]{0:T(128)} %bitcast.z_ref, s32[80]{0:T(128)} %reshape.42.off_ref, bf16[1024,128]{1,0:T(8,128)(2,1)} %get-tuple-element.35.cur_hbm, bf16[384,128]{1,0:T(8,128)(2,1)} %copy-done.12, bf16[384,128]{1,0:T(8,128)(2,1)} %copy-done.14, bf16[256,128]{1,0:T(8,128)(2,1)} %copy-done.17, ...), custom_call_target="tpu_custom_call" | custom-call | flops 335544320 | bytes 3670016 | tf_op jit(solution)/shard_map/pallas_call | solution.py:147
  62.6 2.9 %collective-permute-start.15 = (bf16[16,128,128]{2,1,0:T(8,128)(2,1)S(1)}, bf16[16,128,128]{2,1,0:T(8,128)(2,1)S(1)}, u32[]{:S(2)}, u32[]{:S(2)}) collective-permute-start(bf16[16,128,128]{2,1,0:T(8,128)(2,1)S(1)} %constant_dynamic-update-slice_fusion.7.rest_0_), channel_id=1, source_target_pairs={{0,4},{1,5},{2,6},{3,7},{4,0},{5,1},{6,2},{7,3},{8,12},{9,13},{10,... | collective-permute-start | bytes 1572872 | tf_op jit(solution)/shard_map/ppermute | solution.py:63
  65.5 1.5 %collective-permute-done.15.rest_1_ = bf16[16,128,128]{2,1,0:T(8,128)(2,1)S(1)} collective-permute-done((bf16[16,128,128]{2,1,0:T(8,128)(2,1)S(1)}, bf16[16,128,128]{2,1,0:T(8,128)(2,1)S(1)}, u32[]{:S(2)}, u32[]{:S(2)}) %collective-permute-start.15) | collective-permute-done | bytes 524320 | tf_op jit(solution)/shard_map/ppermute | solution.py:63
  67.8 5.6 %shard_map.103 = (f32[1024,128]{1,0:T(8,128)}, bf16[1024,128]{1,0:T(8,128)(2,1)}, bf16[128,128]{1,0:T(8,128)(2,1)}, bf16[384,128]{1,0:T(8,128)(2,1)}, bf16[384,1...) custom-call(s32[1]{0:T(128)} %bitcast.z_ref, s32[48]{0:T(128)} %gather_fusion, bf16[16,128,128]{2,1,0:T(8,128)(2,1)} %copy-done.4, ...), custom_call_target="tpu_custom_call" | custom-call | flops 201326592 | bytes 4718592 | tf_op jit(solution)/shard_map/pallas_call | solution.py:226
  73.6 1.7 %collective-permute-start.16 = (bf16[384,128]{1,0:T(8,128)(2,1)}, bf16[384,128]{1,0:T(8,128)(2,1)S(1)}, u32[]{:S(2)}, u32[]{:S(2)}) collective-permute-start(bf16[384,128]{1,0:T(8,128)(2,1)} %get-tuple-element.42), channel_id=1, source_target_pairs={{0,1},{1,0},{2,3},{3,2},{4,5},{5,4},{6,7},{7,6},{8,9},{9,8},{10,11... | collective-permute-start | bytes 294920 | tf_op jit(solution)/shard_map/ppermute | solution.py:51
  76.0 4.6 %collective-permute-start.19 = (bf16[256,128]{1,0:T(8,128)(2,1)}, bf16[256,128]{1,0:T(8,128)(2,1)S(1)}, u32[]{:S(2)}, u32[]{:S(2)}) collective-permute-start(bf16[256,128]{1,0:T(8,128)(2,1)} %get-tuple-element.45), channel_id=1, source_target_pairs={{3,4},{7,8},{11,12},{15,16},{19,20},{23,24},{27,28},{4,3},{8,7},{1... | collective-permute-start | bytes 196616 | tf_op jit(solution)/shard_map/ppermute | solution.py:55
  81.5 5.7 %collective-permute-done.18.rest_1_ = bf16[384,128]{1,0:T(8,128)(2,1)S(1)} collective-permute-done((bf16[384,128]{1,0:T(8,128)(2,1)}, bf16[384,128]{1,0:T(8,128)(2,1)S(1)}, u32[]{:S(2)}, u32[]{:S(2)}) %collective-permute-start.18) | collective-permute-done | bytes 98336 | tf_op jit(solution)/shard_map/ppermute | solution.py:49
  89.0 1.7 %collective-permute-start.20 = (bf16[4,128,128]{2,1,0:T(8,128)(2,1)S(1)}, bf16[4,128,128]{2,1,0:T(8,128)(2,1)S(1)}, u32[]{:S(2)}, u32[]{:S(2)}) collective-permute-start(bf16[4,128,128]{2,1,0:T(8,128)(2,1)S(1)} %pad_maximum_fusion.2), channel_id=1, source_target_pairs={{0,8},{1,9},{2,10},{3,11},{4,12},{5,13},{6,14},{7,15},{8,0},{9,1},... | collective-permute-start | bytes 393224 | tf_op jit(solution)/shard_map/ppermute | solution.py:63
  91.3 5.1 %shard_map.104.rest_3_ = f32[1024,128]{1,0:T(8,128)} custom-call(s32[1]{0:T(128)} %bitcast.z_ref, s32[80]{0:T(128)} %reshape.42.off_ref, bf16[1024,128]{1,0:T(8,128)(2,1)} %get-tuple-element.44.cur_hbm, bf16[384,128]{1,0:T(8,128)(2,1)} %copy-done.11, bf16[384,128]{1,0:T(8,128)(2,1)} %copy-done.13, bf16[256,128]{1,0:T(8,128)(2,1)} %copy-done.16, ...), custom_call_target="tpu_custom_call" | custom-call | flops 335544320 | bytes 3670016 | tf_op jit(solution)/shard_map/pallas_call | solution.py:147
  97.3 1.6 %collective-permute-start.23 = (bf16[16,128,128]{2,1,0:T(8,128)(2,1)S(1)}, bf16[16,128,128]{2,1,0:T(8,128)(2,1)S(1)}, u32[]{:S(2)}, u32[]{:S(2)}) collective-permute-start(bf16[16,128,128]{2,1,0:T(8,128)(2,1)S(1)} %constant_dynamic-update-slice_fusion.14.rest_0_), channel_id=1, source_target_pairs={{0,4},{1,5},{2,6},{3,7},{4,0},{5,1},{6,2},{7,3},{8,12},{9,13},{10,... | collective-permute-start | bytes 1572872 | tf_op jit(solution)/shard_map/ppermute | solution.py:63
  98.9 1.5 %collective-permute-done.23.rest_1_ = bf16[16,128,128]{2,1,0:T(8,128)(2,1)S(1)} collective-permute-done((bf16[16,128,128]{2,1,0:T(8,128)(2,1)S(1)}, bf16[16,128,128]{2,1,0:T(8,128)(2,1)S(1)}, u32[]{:S(2)}, u32[]{:S(2)}) %collective-permute-start.23) | collective-permute-done | bytes 524320 | tf_op jit(solution)/shard_map/ppermute | solution.py:63
  101.3 5.6 %shard_map.105 = (f32[1024,128]{1,0:T(8,128)}, bf16[1024,128]{1,0:T(8,128)(2,1)}, bf16[128,128]{1,0:T(8,128)(2,1)}, bf16[384,128]{1,0:T(8,128)(2,1)}, bf16[384,1...) custom-call(s32[1]{0:T(128)} %bitcast.z_ref, s32[48]{0:T(128)} %gather_fusion, bf16[16,128,128]{2,1,0:T(8,128)(2,1)} %copy-done.5, ...), custom_call_target="tpu_custom_call" | custom-call | flops 201326592 | bytes 4718592 | tf_op jit(solution)/shard_map/pallas_call | solution.py:226
  (119 shorter events, 24.7 us)
Async XLA Ops:
  4.0 15.4 %collective-permute-start.1 = (bf16[128,128]{1,0:T(8,128)(2,1)S(1)}, bf16[128,128]{1,0:T(8,128)(2,1)S(1)}, u32[]{:S(2)}, u32[]{:S(2)}) collective-permute-start(bf16[128,128]{1,0:T(8,128)(2,1)S(1)} %gather_fusion.1), channel_id=1, source_target_pairs={{0,2},{1,3},{2,0},{3,1},{4,6},{5,7},{6,4},{7,5},{8,10},{9,11},{10,... | collective-permute-start | bytes 98312 | tf_op jit(solution)/shard_map/ppermute | solution.py:50
  6.4 15.8 %collective-permute-start.3 = (bf16[256,128]{1,0:T(8,128)(2,1)S(1)}, bf16[256,128]{1,0:T(8,128)(2,1)S(1)}, u32[]{:S(2)}, u32[]{:S(2)}) collective-permute-start(bf16[256,128]{1,0:T(8,128)(2,1)S(1)} %get-tuple-element.53), channel_id=1, source_target_pairs={{3,4},{7,8},{11,12},{15,16},{19,20},{23,24},{27,28},{4,3},{8,7},{1... | collective-permute-start | bytes 196616 | tf_op jit(solution)/shard_map/ppermute | solution.py:55
  10.3 6.7 %collective-permute-start.2 = (bf16[384,128]{1,0:T(8,128)(2,1)S(1)}, bf16[384,128]{1,0:T(8,128)(2,1)S(1)}, u32[]{:S(2)}, u32[]{:S(2)}) collective-permute-start(bf16[384,128]{1,0:T(8,128)(2,1)S(1)} %get-tuple-element.56), channel_id=1, source_target_pairs={{0,3},{1,2},{2,1},{3,0},{4,7},{5,6},{6,5},{7,4},{8,11},{9,10},{10,... | collective-permute-start | bytes 294920 | tf_op jit(solution)/shard_map/ppermute | solution.py:49
  13.5 6.0 %collective-permute-start = (bf16[384,128]{1,0:T(8,128)(2,1)S(1)}, bf16[384,128]{1,0:T(8,128)(2,1)S(1)}, u32[]{:S(2)}, u32[]{:S(2)}) collective-permute-start(bf16[384,128]{1,0:T(8,128)(2,1)S(1)} %get-tuple-element.57), channel_id=1, source_target_pairs={{0,1},{1,0},{2,3},{3,2},{4,5},{5,4},{6,7},{7,6},{8,9},{9,8},{10,11... | collective-permute-start | bytes 294920 | tf_op jit(solution)/shard_map/ppermute | solution.py:51
  19.5 9.3 %collective-permute-start.6 = (bf16[4,128,128]{2,1,0:T(8,128)(2,1)S(1)}, bf16[4,128,128]{2,1,0:T(8,128)(2,1)S(1)}, u32[]{:S(2)}, u32[]{:S(2)}) collective-permute-start(bf16[4,128,128]{2,1,0:T(8,128)(2,1)S(1)} %pad_maximum_fusion), channel_id=1, source_target_pairs={{0,24},{1,25},{2,26},{3,27},{4,28},{5,29},{6,30},{7,31},{8,16},{9,... | collective-permute-start | bytes 393224 | tf_op jit(solution)/shard_map/ppermute | solution.py:63
  20.7 8.1 %collective-permute-start.5 = (bf16[4,128,128]{2,1,0:T(8,128)(2,1)S(1)}, bf16[4,128,128]{2,1,0:T(8,128)(2,1)S(1)}, u32[]{:S(2)}, u32[]{:S(2)}) collective-permute-start(bf16[4,128,128]{2,1,0:T(8,128)(2,1)S(1)} %pad_maximum_fusion), channel_id=1, source_target_pairs={{0,16},{1,17},{2,18},{3,19},{4,20},{5,21},{6,22},{7,23},{8,24},{9,... | collective-permute-start | bytes 393224 | tf_op jit(solution)/shard_map/ppermute | solution.py:63
  20.7 8.1 %collective-permute-start.4 = (bf16[4,128,128]{2,1,0:T(8,128)(2,1)S(1)}, bf16[4,128,128]{2,1,0:T(8,128)(2,1)S(1)}, u32[]{:S(2)}, u32[]{:S(2)}) collective-permute-start(bf16[4,128,128]{2,1,0:T(8,128)(2,1)S(1)} %pad_maximum_fusion), channel_id=1, source_target_pairs={{0,8},{1,9},{2,10},{3,11},{4,12},{5,13},{6,14},{7,15},{8,0},{9,1},... | collective-permute-start | bytes 393224 | tf_op jit(solution)/shard_map/ppermute | solution.py:63
  28.9 4.8 %collective-permute-start.7 = (bf16[16,128,128]{2,1,0:T(8,128)(2,1)S(1)}, bf16[16,128,128]{2,1,0:T(8,128)(2,1)S(1)}, u32[]{:S(2)}, u32[]{:S(2)}) collective-permute-start(bf16[16,128,128]{2,1,0:T(8,128)(2,1)S(1)} %constant_dynamic-update-slice_fusion.rest_0_), channel_id=1, source_target_pairs={{0,4},{1,5},{2,6},{3,7},{4,0},{5,1},{6,2},{7,3},{8,12},{9,13},{10,... | collective-permute-start | bytes 1572872 | tf_op jit(solution)/shard_map/ppermute | solution.py:63
  40.2 12.3 %collective-permute-start.9 = (bf16[128,128]{1,0:T(8,128)(2,1)}, bf16[128,128]{1,0:T(8,128)(2,1)S(1)}, u32[]{:S(2)}, u32[]{:S(2)}) collective-permute-start(bf16[128,128]{1,0:T(8,128)(2,1)} %get-tuple-element.32), channel_id=1, source_target_pairs={{0,2},{1,3},{2,0},{3,1},{4,6},{5,7},{6,4},{7,5},{8,10},{9,11},{10,... | collective-permute-start | bytes 98312 | tf_op jit(solution)/shard_map/ppermute | solution.py:50
  40.6 8.0 %collective-permute-start.8 = (bf16[384,128]{1,0:T(8,128)(2,1)}, bf16[384,128]{1,0:T(8,128)(2,1)S(1)}, u32[]{:S(2)}, u32[]{:S(2)}) collective-permute-start(bf16[384,128]{1,0:T(8,128)(2,1)} %get-tuple-element.33), channel_id=1, source_target_pairs={{0,1},{1,0},{2,3},{3,2},{4,5},{5,4},{6,7},{7,6},{8,9},{9,8},{10,11... | collective-permute-start | bytes 294920 | tf_op jit(solution)/shard_map/ppermute | solution.py:51
  42.4 13.7 %collective-permute-start.11 = (bf16[256,128]{1,0:T(8,128)(2,1)}, bf16[256,128]{1,0:T(8,128)(2,1)S(1)}, u32[]{:S(2)}, u32[]{:S(2)}) collective-permute-start(bf16[256,128]{1,0:T(8,128)(2,1)} %get-tuple-element.36), channel_id=1, source_target_pairs={{3,4},{7,8},{11,12},{15,16},{19,20},{23,24},{27,28},{4,3},{8,7},{1... | collective-permute-start | bytes 196616 | tf_op jit(solution)/shard_map/ppermute | solution.py:55
  47.0 5.5 %collective-permute-start.10 = (bf16[384,128]{1,0:T(8,128)(2,1)}, bf16[384,128]{1,0:T(8,128)(2,1)S(1)}, u32[]{:S(2)}, u32[]{:S(2)}) collective-permute-start(bf16[384,128]{1,0:T(8,128)(2,1)} %get-tuple-element.34), channel_id=1, source_target_pairs={{0,3},{1,2},{2,1},{3,0},{4,7},{5,6},{6,5},{7,4},{8,11},{9,10},{10,... | collective-permute-start | bytes 294920 | tf_op jit(solution)/shard_map/ppermute | solution.py:49
  53.3 9.2 %collective-permute-start.14 = (bf16[4,128,128]{2,1,0:T(8,128)(2,1)S(1)}, bf16[4,128,128]{2,1,0:T(8,128)(2,1)S(1)}, u32[]{:S(2)}, u32[]{:S(2)}) collective-permute-start(bf16[4,128,128]{2,1,0:T(8,128)(2,1)S(1)} %pad_maximum_fusion.1), channel_id=1, source_target_pairs={{0,24},{1,25},{2,26},{3,27},{4,28},{5,29},{6,30},{7,31},{8,16},{9,... | collective-permute-start | bytes 393224 | tf_op jit(solution)/shard_map/ppermute | solution.py:63
  55.6 6.9 %collective-permute-start.13 = (bf16[4,128,128]{2,1,0:T(8,128)(2,1)S(1)}, bf16[4,128,128]{2,1,0:T(8,128)(2,1)S(1)}, u32[]{:S(2)}, u32[]{:S(2)}) collective-permute-start(bf16[4,128,128]{2,1,0:T(8,128)(2,1)S(1)} %pad_maximum_fusion.1), channel_id=1, source_target_pairs={{0,16},{1,17},{2,18},{3,19},{4,20},{5,21},{6,22},{7,23},{8,24},{9,... | collective-permute-start | bytes 393224 | tf_op jit(solution)/shard_map/ppermute | solution.py:63
  55.6 6.9 %collective-permute-start.12 = (bf16[4,128,128]{2,1,0:T(8,128)(2,1)S(1)}, bf16[4,128,128]{2,1,0:T(8,128)(2,1)S(1)}, u32[]{:S(2)}, u32[]{:S(2)}) collective-permute-start(bf16[4,128,128]{2,1,0:T(8,128)(2,1)S(1)} %pad_maximum_fusion.1), channel_id=1, source_target_pairs={{0,8},{1,9},{2,10},{3,11},{4,12},{5,13},{6,14},{7,15},{8,0},{9,1},... | collective-permute-start | bytes 393224 | tf_op jit(solution)/shard_map/ppermute | solution.py:63
  62.6 4.4 %collective-permute-start.15 = (bf16[16,128,128]{2,1,0:T(8,128)(2,1)S(1)}, bf16[16,128,128]{2,1,0:T(8,128)(2,1)S(1)}, u32[]{:S(2)}, u32[]{:S(2)}) collective-permute-start(bf16[16,128,128]{2,1,0:T(8,128)(2,1)S(1)} %constant_dynamic-update-slice_fusion.7.rest_0_), channel_id=1, source_target_pairs={{0,4},{1,5},{2,6},{3,7},{4,0},{5,1},{6,2},{7,3},{8,12},{9,13},{10,... | collective-permute-start | bytes 1572872 | tf_op jit(solution)/shard_map/ppermute | solution.py:63
  73.5 13.7 %collective-permute-start.17 = (bf16[128,128]{1,0:T(8,128)(2,1)}, bf16[128,128]{1,0:T(8,128)(2,1)S(1)}, u32[]{:S(2)}, u32[]{:S(2)}) collective-permute-start(bf16[128,128]{1,0:T(8,128)(2,1)} %get-tuple-element.41), channel_id=1, source_target_pairs={{0,2},{1,3},{2,0},{3,1},{4,6},{5,7},{6,4},{7,5},{8,10},{9,11},{10,... | collective-permute-start | bytes 98312 | tf_op jit(solution)/shard_map/ppermute | solution.py:50
  73.6 7.9 %collective-permute-start.16 = (bf16[384,128]{1,0:T(8,128)(2,1)}, bf16[384,128]{1,0:T(8,128)(2,1)S(1)}, u32[]{:S(2)}, u32[]{:S(2)}) collective-permute-start(bf16[384,128]{1,0:T(8,128)(2,1)} %get-tuple-element.42), channel_id=1, source_target_pairs={{0,1},{1,0},{2,3},{3,2},{4,5},{5,4},{6,7},{7,6},{8,9},{9,8},{10,11... | collective-permute-start | bytes 294920 | tf_op jit(solution)/shard_map/ppermute | solution.py:51
  76.0 14.7 %collective-permute-start.19 = (bf16[256,128]{1,0:T(8,128)(2,1)}, bf16[256,128]{1,0:T(8,128)(2,1)S(1)}, u32[]{:S(2)}, u32[]{:S(2)}) collective-permute-start(bf16[256,128]{1,0:T(8,128)(2,1)} %get-tuple-element.45), channel_id=1, source_target_pairs={{3,4},{7,8},{11,12},{15,16},{19,20},{23,24},{27,28},{4,3},{8,7},{1... | collective-permute-start | bytes 196616 | tf_op jit(solution)/shard_map/ppermute | solution.py:55
  80.6 6.6 %collective-permute-start.18 = (bf16[384,128]{1,0:T(8,128)(2,1)}, bf16[384,128]{1,0:T(8,128)(2,1)S(1)}, u32[]{:S(2)}, u32[]{:S(2)}) collective-permute-start(bf16[384,128]{1,0:T(8,128)(2,1)} %get-tuple-element.43), channel_id=1, source_target_pairs={{0,3},{1,2},{2,1},{3,0},{4,7},{5,6},{6,5},{7,4},{8,11},{9,10},{10,... | collective-permute-start | bytes 294920 | tf_op jit(solution)/shard_map/ppermute | solution.py:49
  88.0 9.2 %collective-permute-start.22 = (bf16[4,128,128]{2,1,0:T(8,128)(2,1)S(1)}, bf16[4,128,128]{2,1,0:T(8,128)(2,1)S(1)}, u32[]{:S(2)}, u32[]{:S(2)}) collective-permute-start(bf16[4,128,128]{2,1,0:T(8,128)(2,1)S(1)} %pad_maximum_fusion.2), channel_id=1, source_target_pairs={{0,24},{1,25},{2,26},{3,27},{4,28},{5,29},{6,30},{7,31},{8,16},{9,... | collective-permute-start | bytes 393224 | tf_op jit(solution)/shard_map/ppermute | solution.py:63
  89.0 8.2 %collective-permute-start.21 = (bf16[4,128,128]{2,1,0:T(8,128)(2,1)S(1)}, bf16[4,128,128]{2,1,0:T(8,128)(2,1)S(1)}, u32[]{:S(2)}, u32[]{:S(2)}) collective-permute-start(bf16[4,128,128]{2,1,0:T(8,128)(2,1)S(1)} %pad_maximum_fusion.2), channel_id=1, source_target_pairs={{0,16},{1,17},{2,18},{3,19},{4,20},{5,21},{6,22},{7,23},{8,24},{9,... | collective-permute-start | bytes 393224 | tf_op jit(solution)/shard_map/ppermute | solution.py:63
  89.0 8.2 %collective-permute-start.20 = (bf16[4,128,128]{2,1,0:T(8,128)(2,1)S(1)}, bf16[4,128,128]{2,1,0:T(8,128)(2,1)S(1)}, u32[]{:S(2)}, u32[]{:S(2)}) collective-permute-start(bf16[4,128,128]{2,1,0:T(8,128)(2,1)S(1)} %pad_maximum_fusion.2), channel_id=1, source_target_pairs={{0,8},{1,9},{2,10},{3,11},{4,12},{5,13},{6,14},{7,15},{8,0},{9,1},... | collective-permute-start | bytes 393224 | tf_op jit(solution)/shard_map/ppermute | solution.py:63
  97.3 3.2 %collective-permute-start.23 = (bf16[16,128,128]{2,1,0:T(8,128)(2,1)S(1)}, bf16[16,128,128]{2,1,0:T(8,128)(2,1)S(1)}, u32[]{:S(2)}, u32[]{:S(2)}) collective-permute-start(bf16[16,128,128]{2,1,0:T(8,128)(2,1)S(1)} %constant_dynamic-update-slice_fusion.14.rest_0_), channel_id=1, source_target_pairs={{0,4},{1,5},{2,6},{3,7},{4,0},{5,1},{6,2},{7,3},{8,12},{9,13},{10,... | collective-permute-start | bytes 1572872 | tf_op jit(solution)/shard_map/ppermute | solution.py:63
  (21 other events, 123.8 us)

commit v8 on v7

--- a/solution.py
+++ b/solution.py
@@ -17,7 +17,7 @@
 spread_weight = 0.8
 
 SMEM = pl.BlockSpec(memory_space=pltpu.SMEM)
-ANY = pl.BlockSpec(memory_space=pl.ANY)
+ANY = pl.BlockSpec(memory_space=pltpu.HBM)
 VMEM = pl.BlockSpec(memory_space=pltpu.VMEM)
 
 
@@ -35,7 +35,7 @@
     return p1, p3, pc
 
 
-def exchange(current, owned, p1, p3, pc, hub_blocks, width, block_rows, middle):
+def exchange(current, owned, p1, p3, pc, hub_blocks, width, block_rows, middle, prep):
     count = lax.axis_size(AXES)
     if not fast_path(owned, block_rows):
         forward = [(i, i + 1) for i in range(count - 1)]
@@ -43,7 +43,7 @@
         low = lax.ppermute(current[current.shape[0] - width:], AXES, forward)
         high = lax.ppermute(current[:width], AXES, backward)
         hub_all = lax.all_gather(owned, AXES, axis=0, tiled=True)
-        return middle((low, high)), [hub_all.reshape(-1, block_rows, owned.shape[1])], hub_blocks
+        return middle((low, high)), [hub_all.reshape(-1, block_rows, owned.shape[1])], hub_blocks, prep
     me = lax.axis_index(AXES)
     pairs = lambda m: [(i, i ^ m) for i in range(count)]
     r3 = lax.ppermute(p3, AXES, pairs(3))
@@ -53,26 +53,26 @@
     cross = [(4 * g + 3, 4 * g + 4) for g in range(groups - 1)]
     cross += [(4 * g + 4, 4 * g + 3) for g in range(groups - 1)]
     rc = lax.ppermute(pc, AXES, cross)
+    if prep is not None:
+        (r1, r2, r3, rc), prep = lax.optimization_barrier(((r1, r2, r3, rc), prep))
     rows = block_rows
     buf = jnp.concatenate([owned[None], r1[None, :rows], r2[None], r3[None, :rows]], 0)
     offs = [0, 1, 2, 3]
-    rounds = ROUNDS_32
-    pieces = [buf]
-    done = None
-    for r, group in enumerate(rounds[1:]):
-        sent = {m: lax.ppermute(buf, AXES, pairs(m)) for m in sorted(group, key=lambda m: -m)}
-        recvs = [sent[m] for m in group]
-        if done is None:
-            done, recvs = lax.optimization_barrier((middle((r1, r3, rc)), recvs))
-        offs = offs + [o ^ m for m in group for o in offs]
-        pieces = [buf] + recvs
-        if r + 2 < len(rounds):
-            buf = jnp.concatenate(pieces, 0)
+    assert ROUNDS_32[0] == (1, 2, 3) and len(ROUNDS_32) == 3 and len(ROUNDS_32[2]) == 1
+    group = ROUNDS_32[1]
+    sent = {m: lax.ppermute(buf, AXES, pairs(m)) for m in sorted(group, key=lambda m: -m)}
+    recvs = [sent[m] for m in group]
+    done, recvs = lax.optimization_barrier((middle((r1, r3, rc)), recvs))
+    offs = offs + [o ^ m for m in group for o in offs]
+    rest = jnp.concatenate(recvs, 0)
+    last = ROUNDS_32[2][0]
+    pieces = [buf, rest, lax.ppermute(buf, AXES, pairs(last)), lax.ppermute(rest, AXES, pairs(last))]
+    offs = offs + [o ^ last for o in offs]
     assert sorted(offs) == list(range(count))
     where = np.zeros(count, np.int32)
     for p, o in enumerate(offs):
         where[o] = p
-    return done, pieces, jnp.asarray(where)[hub_blocks ^ me]
+    return done, pieces, jnp.asarray(where)[hub_blocks ^ me], prep
 
 
 def band_kernel(fast, n_own, z_ref, off_ref, cur_hbm, *rest):
@@ -261,13 +261,20 @@
     p1, p3, pc = payloads(current, owned, z[0], width)
     fast = fast_path(owned, block_rows)
     pick = (hub_rows[:, None] == jnp.arange(current.shape[0], dtype=hub_rows.dtype)[None, :]).astype(jnp.bfloat16)
+    prep = (pick, degree)
+    hub_index = None
     for step in range(ITERS):
         middle = functools.partial(
             band_call, z, band_offsets, current, band_tiles=band_tiles, fast=fast, n_own=owned.shape[0], width=width
         )
-        band, hub_pieces, hub_index = exchange(
-            current, owned, p1, p3, pc, hub_blocks, width, block_rows, lambda rims: middle(rims)
+        band, hub_pieces, index, prep = exchange(
+            current, owned, p1, p3, pc, hub_blocks, width, block_rows, lambda rims: middle(rims), prep
         )
+        if hub_index is None:
+            hub_index = index
+        if prep is not None:
+            pick, degree = prep
+            prep = None
         labels, current, owned, p1, p3, pc = hub_call(
             z, hub_index, pick, hub_pieces, hub_tiles, band, degree, seeds, width
         )

time: 108 us -> 113 us (1.046)
  starting transfers between devices: 38.2 us -> 44.6 us
  local copies, waits for them, and re-layouts: 12.1 us -> 8.81 us
  waiting for transfers between devices: 15.6 us -> 17.7 us
    ppermute x0 -> x6, starting transfers between devices: none -> 6.4 us  [the longest x3 6.16 us: exchange(): lax.ppermute(rest, AXES, pairs(last))]
    ppermute x12 -> x9, starting transfers between devices: 13.9 us -> 8.14 us  [exchange(): lax.ppermute(buf, AXES, pairs(m))]
    ppermute x3, waiting for transfers between devices: 0.01 us -> 4.99 us  [exchange(): rc = lax.ppermute(pc, AXES, cross)]
    ppermute x3, waiting for transfers between devices: 10 us -> 5.05 us  [exchange(): r3 = lax.ppermute(p3, AXES, pairs(3))]
    ppermute x3, starting transfers between devices: 13 us -> 17.3 us  [exchange(): rc = lax.ppermute(pc, AXES, cross)]
    unnamed x60 -> x58, local copies, waits for them, and re-layouts: 8.23 us -> 4.99 us
    ppermute x0 -> x6, waiting for transfers between devices: none -> 2.93 us  [the longest x3 2.92 us: exchange(): lax.ppermute(buf, AXES, pairs(last))]
    ppermute x3, starting transfers between devices: 2.68 us -> 0.14 us  [exchange(): r1 = lax.ppermute(p1, AXES, pairs(1))]
  transfers between devices with their start and end apart: 24 -> 27, of which waited for: 6 -> 10; matrix products, arithmetic and copies ran while one was open for 11% -> 6% of each run, Pallas kernels for 14% -> 13%
where the time goes in v8:
time: 113 us
  starting transfers between devices  44.6 us (39%)
  Pallas kernels  32.2 us (28%)
  waiting for transfers between devices  17.7 us (16%)
  other arithmetic  8.99 us (8%)
  local copies, waits for them, and re-layouts  8.81 us (8%)
    ppermute x3, starting transfers between devices, exchange(): rc = lax.ppermute(pc, AXES, cross)  17.3 us
    pallas_call x3, Pallas kernels, hub_call(): pl.pallas_call(functools.partial(hub_kernel, n_hub, width), cost_estimate...  17 us
    pallas_call x3, Pallas kernels, band_call(): pl.pallas_call(functools.partial(band_kernel, fast, n_own), cost_estimate...  15.2 us
    ppermute x3, starting transfers between devices, exchange(): r3 = lax.ppermute(p3, AXES, pairs(3))  8.26 us
    ppermute x9, starting transfers between devices, exchange(): lax.ppermute(buf, AXES, pairs(m))  8.14 us
    ppermute x3, starting transfers between devices, exchange(): lax.ppermute(rest, AXES, pairs(last))  6.16 us
    ppermute x3, waiting for transfers between devices, exchange(): r3 = lax.ppermute(p3, AXES, pairs(3))  5.05 us
    ppermute x3, waiting for transfers between devices, exchange(): rc = lax.ppermute(pc, AXES, cross)  4.99 us
  transfers between devices with their start and end apart: 27, of which 10 were waited for; matrix products, arithmetic and copies ran while one was open for 6% of the time, Pallas kernels for 13%

profile of v8, /device:TPU:5, one launch (start us, length us, event | category | flops | bytes accessed | tf_op | source)
XLA Modules:
  0.0 112.7 jit_solution(6135794891235212900)
XLA Ops:
  1.5 1.9 %convert_multiply_fusion = (f32[1024,128]{1,0:T(8,128)}, bf16[1024,128]{1,0:T(8,128)(2,1)S(1)}) fusion(bf16[1024,128]{1,0:T(8,128)(2,1)} %param.8, f32[1024]{0:T(1024)S(1)} %convert_element_type.18), kind=kLoop, calls=%fused_computation.5 | loop fusion | flops 393216 | bytes 1052672 | tf_op jit(solution)/shard_map/mul | solution.py:252
  4.1 2.4 %collective-permute-start.1 = (bf16[128,128]{1,0:T(8,128)(2,1)S(1)}, bf16[128,128]{1,0:T(8,128)(2,1)S(1)}, u32[]{:S(2)}, u32[]{:S(2)}) collective-permute-start(bf16[128,128]{1,0:T(8,128)(2,1)S(1)} %gather_fusion.1), channel_id=1, source_target_pairs={{0,2},{1,3},{2,0},{3,1},{4,6},{5,7},{6,4},{7,5},{8,10},{9,11},{10,... | collective-permute-start | bytes 98312 | tf_op jit(solution)/shard_map/ppermute | solution.py:50
  6.5 3.8 %collective-permute-start.3 = (bf16[256,128]{1,0:T(8,128)(2,1)S(1)}, bf16[256,128]{1,0:T(8,128)(2,1)S(1)}, u32[]{:S(2)}, u32[]{:S(2)}) collective-permute-start(bf16[256,128]{1,0:T(8,128)(2,1)S(1)} %get-tuple-element.65), channel_id=1, source_target_pairs={{3,4},{7,8},{11,12},{15,16},{19,20},{23,24},{27,28},{4,3},{8,7},{1... | collective-permute-start | bytes 196616 | tf_op jit(solution)/shard_map/ppermute | solution.py:55
  10.4 3.2 %collective-permute-start.2 = (bf16[384,128]{1,0:T(8,128)(2,1)S(1)}, bf16[384,128]{1,0:T(8,128)(2,1)S(1)}, u32[]{:S(2)}, u32[]{:S(2)}) collective-permute-start(bf16[384,128]{1,0:T(8,128)(2,1)S(1)} %get-tuple-element.68), channel_id=1, source_target_pairs={{0,3},{1,2},{2,1},{3,0},{4,7},{5,6},{6,5},{7,4},{8,11},{9,10},{10,... | collective-permute-start | bytes 294920 | tf_op jit(solution)/shard_map/ppermute | solution.py:49
  15.0 2.2 %convert_reduce_fusion = f32[8,128]{1,0:T(8,128)S(1)} fusion(bf16[8,10,128,128]{3,2,1,0:T(8,128)(2,1)} %rest_3_.5), kind=kLoop, calls=%fused_computation.2 | loop fusion | flops 2620416 | bytes 2625536 | tf_op jit(solution)/shard_map/reduce_sum | solution.py:253
  17.6 2.0 %collective-permute-done.rest_0_ = bf16[384,128]{1,0:T(8,128)(2,1)S(1)} collective-permute-done((bf16[384,128]{1,0:T(8,128)(2,1)S(1)}, bf16[384,128]{1,0:T(8,128)(2,1)S(1)}, u32[]{:S(2)}, u32[]{:S(2)}) %collective-permute-start) | collective-permute-done | bytes 98336 | tf_op jit(solution)/shard_map/ppermute | solution.py:51
  20.8 1.5 %collective-permute-start.4 = (bf16[4,128,128]{2,1,0:T(8,128)(2,1)S(1)}, bf16[4,128,128]{2,1,0:T(8,128)(2,1)S(1)}, u32[]{:S(2)}, u32[]{:S(2)}) collective-permute-start(bf16[4,128,128]{2,1,0:T(8,128)(2,1)S(1)} %pad_maximum_fusion.rest_0_), channel_id=1, source_target_pairs={{0,8},{1,9},{2,10},{3,11},{4,12},{5,13},{6,14},{7,15},{8,0},{9,1},... | collective-permute-start | bytes 393224 | tf_op jit(solution)/shard_map/ppermute | solution.py:63
  23.0 5.1 %shard_map.82.rest_5_ = f32[1024,128]{1,0:T(8,128)} custom-call(s32[1]{0:T(128)} %bitcast.z_ref, s32[80]{0:T(128)} %reshape.36.off_ref, bf16[1024,128]{1,0:T(8,128)(2,1)} %copy-done.2, bf16[384,128]{1,0:T(8,128)(2,1)} %copy-done.17, bf16[384,128]{1,0:T(8,128)(2,1)} %copy-done.16, bf16[256,128]{1,0:T(8,128)(2,1)} %copy-done.21, bf16[8,10,128,128]{3,2,1,0:T(8,128)(2,1)} %rest_3_.5), custom_call_target="tpu_custom_call" | custom-call | flops 335544320 | bytes 3670016 | tf_op jit(solution)/shard_map/pallas_call | solution.py:147
  32.8 5.7 %shard_map.83 = (f32[1024,128]{1,0:T(8,128)}, bf16[1024,128]{1,0:T(8,128)(2,1)}, bf16[128,128]{1,0:T(8,128)(2,1)}, bf16[384,128]{1,0:T(8,128)(2,1)}, bf16[384,128]{1,0:T(8,128)(2,1)}, /*index=5*/bf16[256,128]{1,0:T(8,128)(2,1)}) custom-call(s32[1]{0:T(128)} %bitcast.z_ref, s32[48]{0:T(128)} %gather_fusion, bf16[4,128,128]{2,1,0:T(8,128)(2,1)} %copy-done.6, ...), custom_call_target="tpu_custom_call" | custom-call | flops 201326592 | bytes 4718592 | tf_op jit(solution)/shard_map/pallas_call | solution.py:226
  39.9 2.2 %collective-permute-start.11 = (bf16[384,128]{1,0:T(8,128)(2,1)}, bf16[384,128]{1,0:T(8,128)(2,1)S(1)}, u32[]{:S(2)}, u32[]{:S(2)}) collective-permute-start(bf16[384,128]{1,0:T(8,128)(2,1)} %get-tuple-element.46), channel_id=1, source_target_pairs={{0,3},{1,2},{2,1},{3,0},{4,7},{5,6},{6,5},{7,4},{8,11},{9,10},{10,... | collective-permute-start | bytes 294920 | tf_op jit(solution)/shard_map/ppermute | solution.py:49
  43.0 2.8 %collective-permute-done.11.rest_1_ = bf16[384,128]{1,0:T(8,128)(2,1)S(1)} collective-permute-done((bf16[384,128]{1,0:T(8,128)(2,1)}, bf16[384,128]{1,0:T(8,128)(2,1)S(1)}, u32[]{:S(2)}, u32[]{:S(2)}) %collective-permute-start.11) | collective-permute-done | bytes 98336 | tf_op jit(solution)/shard_map/ppermute | solution.py:49
  49.4 6.5 %collective-permute-start.12 = (bf16[256,128]{1,0:T(8,128)(2,1)}, bf16[256,128]{1,0:T(8,128)(2,1)S(1)}, u32[]{:S(2)}, u32[]{:S(2)}) collective-permute-start(bf16[256,128]{1,0:T(8,128)(2,1)} %get-tuple-element.48), channel_id=1, source_target_pairs={{3,4},{7,8},{11,12},{15,16},{19,20},{23,24},{27,28},{4,3},{8,7},{1... | collective-permute-start | bytes 196616 | tf_op jit(solution)/shard_map/ppermute | solution.py:55
  55.9 2.1 %collective-permute-done.12.rest_2_ = bf16[256,128]{1,0:T(8,128)(2,1)S(1)} collective-permute-done((bf16[256,128]{1,0:T(8,128)(2,1)}, bf16[256,128]{1,0:T(8,128)(2,1)S(1)}, u32[]{:S(2)}, u32[]{:S(2)}) %collective-permute-start.12) | collective-permute-done | bytes 65568 | tf_op jit(solution)/shard_map/ppermute | solution.py:55
  58.7 5.1 %shard_map.84.rest_5_ = f32[1024,128]{1,0:T(8,128)} custom-call(s32[1]{0:T(128)} %bitcast.z_ref, s32[80]{0:T(128)} %reshape.36.off_ref, bf16[1024,128]{1,0:T(8,128)(2,1)} %get-tuple-element.47.cur_hbm, bf16[384,128]{1,0:T(8,128)(2,1)} %copy-done.13, bf16[384,128]{1,0:T(8,128)(2,1)} %copy-done.15, bf16[256,128]{1,0:T(8,128)(2,1)} %copy-done.23, ...), custom_call_target="tpu_custom_call" | custom-call | flops 335544320 | bytes 3670016 | tf_op jit(solution)/shard_map/pallas_call | solution.py:147
  63.8 3.3 %collective-permute-start.17 = (bf16[12,128,128]{2,1,0:T(8,128)(2,1)S(1)}, bf16[12,128,128]{2,1,0:T(8,128)(2,1)S(1)}, u32[]{:S(2)}, u32[]{:S(2)}) collective-permute-start(bf16[12,128,128]{2,1,0:T(8,128)(2,1)S(1)} %constant_dynamic-update-slice_fusion.3.rest_1_), channel_id=1, source_target_pairs={{0,4},{1,5},{2,6},{3,7},{4,0},{5,1},{6,2},{7,3},{8,12},{9,13},{10,... | collective-permute-start | bytes 1179656 | tf_op jit(solution)/shard_map/ppermute | solution.py:69
  70.1 5.7 %shard_map.85 = (f32[1024,128]{1,0:T(8,128)}, bf16[1024,128]{1,0:T(8,128)(2,1)}, bf16[128,128]{1,0:T(8,128)(2,1)}, bf16[384,128]{1,0:T(8,128)(2,1)}, bf16[384,128]{1,0:T(8,128)(2,1)}, /*index=5*/bf16[256,128]{1,0:T(8,128)(2,1)}) custom-call(s32[1]{0:T(128)} %bitcast.z_ref, s32[48]{0:T(128)} %gather_fusion, bf16[4,128,128]{2,1,0:T(8,128)(2,1)} %copy-done.8, ...), custom_call_target="tpu_custom_call" | custom-call | flops 201326592 | bytes 4718592 | tf_op jit(solution)/shard_map/pallas_call | solution.py:226
  76.5 2.9 %collective-permute-start.20 = (bf16[384,128]{1,0:T(8,128)(2,1)}, bf16[384,128]{1,0:T(8,128)(2,1)S(1)}, u32[]{:S(2)}, u32[]{:S(2)}) collective-permute-start(bf16[384,128]{1,0:T(8,128)(2,1)} %get-tuple-element.55), channel_id=1, source_target_pairs={{0,3},{1,2},{2,1},{3,0},{4,7},{5,6},{6,5},{7,4},{8,11},{9,10},{10,... | collective-permute-start | bytes 294920 | tf_op jit(solution)/shard_map/ppermute | solution.py:49
  80.5 2.2 %collective-permute-done.20.rest_1_ = bf16[384,128]{1,0:T(8,128)(2,1)S(1)} collective-permute-done((bf16[384,128]{1,0:T(8,128)(2,1)}, bf16[384,128]{1,0:T(8,128)(2,1)S(1)}, u32[]{:S(2)}, u32[]{:S(2)}) %collective-permute-start.20) | collective-permute-done | bytes 98336 | tf_op jit(solution)/shard_map/ppermute | solution.py:49
  84.7 1.6 %collective-permute-start.22 = (bf16[4,128,128]{2,1,0:T(8,128)(2,1)S(1)}, bf16[4,128,128]{2,1,0:T(8,128)(2,1)S(1)}, u32[]{:S(2)}, u32[]{:S(2)}) collective-permute-start(bf16[4,128,128]{2,1,0:T(8,128)(2,1)S(1)} %pad_maximum_fusion.2.rest_0_), channel_id=1, source_target_pairs={{0,8},{1,9},{2,10},{3,11},{4,12},{5,13},{6,14},{7,15},{8,0},{9,1},... | collective-permute-start | bytes 393224 | tf_op jit(solution)/shard_map/ppermute | solution.py:63
  86.3 7.0 %collective-permute-start.21 = (bf16[256,128]{1,0:T(8,128)(2,1)}, bf16[256,128]{1,0:T(8,128)(2,1)S(1)}, u32[]{:S(2)}, u32[]{:S(2)}) collective-permute-start(bf16[256,128]{1,0:T(8,128)(2,1)} %get-tuple-element.57), channel_id=1, source_target_pairs={{3,4},{7,8},{11,12},{15,16},{19,20},{23,24},{27,28},{4,3},{8,7},{1... | collective-permute-start | bytes 196616 | tf_op jit(solution)/shard_map/ppermute | solution.py:55
  93.2 2.8 %collective-permute-done.21.rest_2_ = bf16[256,128]{1,0:T(8,128)(2,1)S(1)} collective-permute-done((bf16[256,128]{1,0:T(8,128)(2,1)}, bf16[256,128]{1,0:T(8,128)(2,1)S(1)}, u32[]{:S(2)}, u32[]{:S(2)}) %collective-permute-start.21) | collective-permute-done | bytes 65568 | tf_op jit(solution)/shard_map/ppermute | solution.py:55
  96.7 5.1 %shard_map.86.rest_5_ = f32[1024,128]{1,0:T(8,128)} custom-call(s32[1]{0:T(128)} %bitcast.z_ref, s32[80]{0:T(128)} %reshape.36.off_ref, bf16[1024,128]{1,0:T(8,128)(2,1)} %get-tuple-element.56.cur_hbm, bf16[384,128]{1,0:T(8,128)(2,1)} %copy-done.12, bf16[384,128]{1,0:T(8,128)(2,1)} %copy-done.14, bf16[256,128]{1,0:T(8,128)(2,1)} %copy-done.22, ...), custom_call_target="tpu_custom_call" | custom-call | flops 335544320 | bytes 3670016 | tf_op jit(solution)/shard_map/pallas_call | solution.py:147
  101.9 2.2 %collective-permute-start.26 = (bf16[12,128,128]{2,1,0:T(8,128)(2,1)S(1)}, bf16[12,128,128]{2,1,0:T(8,128)(2,1)S(1)}, u32[]{:S(2)}, u32[]{:S(2)}) collective-permute-start(bf16[12,128,128]{2,1,0:T(8,128)(2,1)S(1)} %constant_dynamic-update-slice_fusion.6.rest_1_), channel_id=1, source_target_pairs={{0,4},{1,5},{2,6},{3,7},{4,0},{5,1},{6,2},{7,3},{8,12},{9,13},{10,... | collective-permute-start | bytes 1179656 | tf_op jit(solution)/shard_map/ppermute | solution.py:69
  107.1 5.7 %shard_map.87 = (f32[1024,128]{1,0:T(8,128)}, bf16[1024,128]{1,0:T(8,128)(2,1)}, bf16[128,128]{1,0:T(8,128)(2,1)}, bf16[384,128]{1,0:T(8,128)(2,1)}, bf16[384,128]{1,0:T(8,128)(2,1)}, /*index=5*/bf16[256,128]{1,0:T(8,128)(2,1)}) custom-call(s32[1]{0:T(128)} %bitcast.z_ref, s32[48]{0:T(128)} %gather_fusion, bf16[4,128,128]{2,1,0:T(8,128)(2,1)} %copy-done.7, ...), custom_call_target="tpu_custom_call" | custom-call | flops 201326592 | bytes 4718592 | tf_op jit(solution)/shard_map/pallas_call | solution.py:226
  (122 shorter events, 27.4 us)
Async XLA Ops:
  4.1 13.4 %collective-permute-start.1 = (bf16[128,128]{1,0:T(8,128)(2,1)S(1)}, bf16[128,128]{1,0:T(8,128)(2,1)S(1)}, u32[]{:S(2)}, u32[]{:S(2)}) collective-permute-start(bf16[128,128]{1,0:T(8,128)(2,1)S(1)} %gather_fusion.1), channel_id=1, source_target_pairs={{0,2},{1,3},{2,0},{3,1},{4,6},{5,7},{6,4},{7,5},{8,10},{9,11},{10,... | collective-permute-start | bytes 98312 | tf_op jit(solution)/shard_map/ppermute | solution.py:50
  6.5 11.0 %collective-permute-start.3 = (bf16[256,128]{1,0:T(8,128)(2,1)S(1)}, bf16[256,128]{1,0:T(8,128)(2,1)S(1)}, u32[]{:S(2)}, u32[]{:S(2)}) collective-permute-start(bf16[256,128]{1,0:T(8,128)(2,1)S(1)} %get-tuple-element.65), channel_id=1, source_target_pairs={{3,4},{7,8},{11,12},{15,16},{19,20},{23,24},{27,28},{4,3},{8,7},{1... | collective-permute-start | bytes 196616 | tf_op jit(solution)/shard_map/ppermute | solution.py:55
  10.4 7.2 %collective-permute-start.2 = (bf16[384,128]{1,0:T(8,128)(2,1)S(1)}, bf16[384,128]{1,0:T(8,128)(2,1)S(1)}, u32[]{:S(2)}, u32[]{:S(2)}) collective-permute-start(bf16[384,128]{1,0:T(8,128)(2,1)S(1)} %get-tuple-element.68), channel_id=1, source_target_pairs={{0,3},{1,2},{2,1},{3,0},{4,7},{5,6},{6,5},{7,4},{8,11},{9,10},{10,... | collective-permute-start | bytes 294920 | tf_op jit(solution)/shard_map/ppermute | solution.py:49
  13.6 6.0 %collective-permute-start = (bf16[384,128]{1,0:T(8,128)(2,1)S(1)}, bf16[384,128]{1,0:T(8,128)(2,1)S(1)}, u32[]{:S(2)}, u32[]{:S(2)}) collective-permute-start(bf16[384,128]{1,0:T(8,128)(2,1)S(1)} %get-tuple-element.69), channel_id=1, source_target_pairs={{0,1},{1,0},{2,3},{3,2},{4,5},{5,4},{6,7},{7,6},{8,9},{9,8},{10,11... | collective-permute-start | bytes 294920 | tf_op jit(solution)/shard_map/ppermute | solution.py:51
  19.6 8.5 %collective-permute-start.6 = (bf16[4,128,128]{2,1,0:T(8,128)(2,1)S(1)}, bf16[4,128,128]{2,1,0:T(8,128)(2,1)S(1)}, u32[]{:S(2)}, u32[]{:S(2)}) collective-permute-start(bf16[4,128,128]{2,1,0:T(8,128)(2,1)S(1)} %pad_maximum_fusion.rest_0_), channel_id=1, source_target_pairs={{0,24},{1,25},{2,26},{3,27},{4,28},{5,29},{6,30},{7,31},{8,16},{9,... | collective-permute-start | bytes 393224 | tf_op jit(solution)/shard_map/ppermute | solution.py:63
  20.8 8.0 %collective-permute-start.5 = (bf16[4,128,128]{2,1,0:T(8,128)(2,1)S(1)}, bf16[4,128,128]{2,1,0:T(8,128)(2,1)S(1)}, u32[]{:S(2)}, u32[]{:S(2)}) collective-permute-start(bf16[4,128,128]{2,1,0:T(8,128)(2,1)S(1)} %pad_maximum_fusion.rest_0_), channel_id=1, source_target_pairs={{0,16},{1,17},{2,18},{3,19},{4,20},{5,21},{6,22},{7,23},{8,24},{9,... | collective-permute-start | bytes 393224 | tf_op jit(solution)/shard_map/ppermute | solution.py:63
  20.8 8.0 %collective-permute-start.4 = (bf16[4,128,128]{2,1,0:T(8,128)(2,1)S(1)}, bf16[4,128,128]{2,1,0:T(8,128)(2,1)S(1)}, u32[]{:S(2)}, u32[]{:S(2)}) collective-permute-start(bf16[4,128,128]{2,1,0:T(8,128)(2,1)S(1)} %pad_maximum_fusion.rest_0_), channel_id=1, source_target_pairs={{0,8},{1,9},{2,10},{3,11},{4,12},{5,13},{6,14},{7,15},{8,0},{9,1},... | collective-permute-start | bytes 393224 | tf_op jit(solution)/shard_map/ppermute | solution.py:63
  28.9 3.1 %collective-permute-start.8 = (bf16[12,128,128]{2,1,0:T(8,128)(2,1)S(1)}, bf16[12,128,128]{2,1,0:T(8,128)(2,1)S(1)}, u32[]{:S(2)}, u32[]{:S(2)}) collective-permute-start(bf16[12,128,128]{2,1,0:T(8,128)(2,1)S(1)} %constant_dynamic-update-slice_fusion.rest_1_), channel_id=1, source_target_pairs={{0,4},{1,5},{2,6},{3,7},{4,0},{5,1},{6,2},{7,3},{8,12},{9,13},{10,... | collective-permute-start | bytes 1179656 | tf_op jit(solution)/shard_map/ppermute | solution.py:69
  38.4 4.6 %collective-permute-start.9 = (bf16[384,128]{1,0:T(8,128)(2,1)}, bf16[384,128]{1,0:T(8,128)(2,1)S(1)}, u32[]{:S(2)}, u32[]{:S(2)}) collective-permute-start(bf16[384,128]{1,0:T(8,128)(2,1)} %get-tuple-element.45), channel_id=1, source_target_pairs={{0,1},{1,0},{2,3},{3,2},{4,5},{5,4},{6,7},{7,6},{8,9},{9,8},{10,11... | collective-permute-start | bytes 294920 | tf_op jit(solution)/shard_map/ppermute | solution.py:51
  38.5 7.3 %collective-permute-start.10 = (bf16[128,128]{1,0:T(8,128)(2,1)}, bf16[128,128]{1,0:T(8,128)(2,1)S(1)}, u32[]{:S(2)}, u32[]{:S(2)}) collective-permute-start(bf16[128,128]{1,0:T(8,128)(2,1)} %get-tuple-element.44), channel_id=1, source_target_pairs={{0,2},{1,3},{2,0},{3,1},{4,6},{5,7},{6,4},{7,5},{8,10},{9,11},{10,... | collective-permute-start | bytes 98312 | tf_op jit(solution)/shard_map/ppermute | solution.py:50
  39.9 5.9 %collective-permute-start.11 = (bf16[384,128]{1,0:T(8,128)(2,1)}, bf16[384,128]{1,0:T(8,128)(2,1)S(1)}, u32[]{:S(2)}, u32[]{:S(2)}) collective-permute-start(bf16[384,128]{1,0:T(8,128)(2,1)} %get-tuple-element.46), channel_id=1, source_target_pairs={{0,3},{1,2},{2,1},{3,0},{4,7},{5,6},{6,5},{7,4},{8,11},{9,10},{10,... | collective-permute-start | bytes 294920 | tf_op jit(solution)/shard_map/ppermute | solution.py:49
  46.6 17.1 %collective-permute-start.15 = (bf16[4,128,128]{2,1,0:T(8,128)(2,1)S(1)}, bf16[4,128,128]{2,1,0:T(8,128)(2,1)S(1)}, u32[]{:S(2)}, u32[]{:S(2)}) collective-permute-start(bf16[4,128,128]{2,1,0:T(8,128)(2,1)S(1)} %pad_maximum_fusion.1.rest_0_), channel_id=1, source_target_pairs={{0,24},{1,25},{2,26},{3,27},{4,28},{5,29},{6,30},{7,31},{8,16},{9,... | collective-permute-start | bytes 393224 | tf_op jit(solution)/shard_map/ppermute | solution.py:63
  47.9 15.9 %collective-permute-start.14 = (bf16[4,128,128]{2,1,0:T(8,128)(2,1)S(1)}, bf16[4,128,128]{2,1,0:T(8,128)(2,1)S(1)}, u32[]{:S(2)}, u32[]{:S(2)}) collective-permute-start(bf16[4,128,128]{2,1,0:T(8,128)(2,1)S(1)} %pad_maximum_fusion.1.rest_0_), channel_id=1, source_target_pairs={{0,16},{1,17},{2,18},{3,19},{4,20},{5,21},{6,22},{7,23},{8,24},{9,... | collective-permute-start | bytes 393224 | tf_op jit(solution)/shard_map/ppermute | solution.py:63
  48.3 15.4 %collective-permute-start.13 = (bf16[4,128,128]{2,1,0:T(8,128)(2,1)S(1)}, bf16[4,128,128]{2,1,0:T(8,128)(2,1)S(1)}, u32[]{:S(2)}, u32[]{:S(2)}) collective-permute-start(bf16[4,128,128]{2,1,0:T(8,128)(2,1)S(1)} %pad_maximum_fusion.1.rest_0_), channel_id=1, source_target_pairs={{0,8},{1,9},{2,10},{3,11},{4,12},{5,13},{6,14},{7,15},{8,0},{9,1},... | collective-permute-start | bytes 393224 | tf_op jit(solution)/shard_map/ppermute | solution.py:63
  49.4 8.7 %collective-permute-start.12 = (bf16[256,128]{1,0:T(8,128)(2,1)}, bf16[256,128]{1,0:T(8,128)(2,1)S(1)}, u32[]{:S(2)}, u32[]{:S(2)}) collective-permute-start(bf16[256,128]{1,0:T(8,128)(2,1)} %get-tuple-element.48), channel_id=1, source_target_pairs={{3,4},{7,8},{11,12},{15,16},{19,20},{23,24},{27,28},{4,3},{8,7},{1... | collective-permute-start | bytes 196616 | tf_op jit(solution)/shard_map/ppermute | solution.py:55
  63.8 4.9 %collective-permute-start.17 = (bf16[12,128,128]{2,1,0:T(8,128)(2,1)S(1)}, bf16[12,128,128]{2,1,0:T(8,128)(2,1)S(1)}, u32[]{:S(2)}, u32[]{:S(2)}) collective-permute-start(bf16[12,128,128]{2,1,0:T(8,128)(2,1)S(1)} %constant_dynamic-update-slice_fusion.3.rest_1_), channel_id=1, source_target_pairs={{0,4},{1,5},{2,6},{3,7},{4,0},{5,1},{6,2},{7,3},{8,12},{9,13},{10,... | collective-permute-start | bytes 1179656 | tf_op jit(solution)/shard_map/ppermute | solution.py:69
  75.8 4.6 %collective-permute-start.18 = (bf16[384,128]{1,0:T(8,128)(2,1)}, bf16[384,128]{1,0:T(8,128)(2,1)S(1)}, u32[]{:S(2)}, u32[]{:S(2)}) collective-permute-start(bf16[384,128]{1,0:T(8,128)(2,1)} %get-tuple-element.54), channel_id=1, source_target_pairs={{0,1},{1,0},{2,3},{3,2},{4,5},{5,4},{6,7},{7,6},{8,9},{9,8},{10,11... | collective-permute-start | bytes 294920 | tf_op jit(solution)/shard_map/ppermute | solution.py:51
  75.9 6.8 %collective-permute-start.19 = (bf16[128,128]{1,0:T(8,128)(2,1)}, bf16[128,128]{1,0:T(8,128)(2,1)S(1)}, u32[]{:S(2)}, u32[]{:S(2)}) collective-permute-start(bf16[128,128]{1,0:T(8,128)(2,1)} %get-tuple-element.53), channel_id=1, source_target_pairs={{0,2},{1,3},{2,0},{3,1},{4,6},{5,7},{6,4},{7,5},{8,10},{9,11},{10,... | collective-permute-start | bytes 98312 | tf_op jit(solution)/shard_map/ppermute | solution.py:50
  76.5 6.2 %collective-permute-start.20 = (bf16[384,128]{1,0:T(8,128)(2,1)}, bf16[384,128]{1,0:T(8,128)(2,1)S(1)}, u32[]{:S(2)}, u32[]{:S(2)}) collective-permute-start(bf16[384,128]{1,0:T(8,128)(2,1)} %get-tuple-element.55), channel_id=1, source_target_pairs={{0,3},{1,2},{2,1},{3,0},{4,7},{5,6},{6,5},{7,4},{8,11},{9,10},{10,... | collective-permute-start | bytes 294920 | tf_op jit(solution)/shard_map/ppermute | solution.py:49
  83.5 18.2 %collective-permute-start.24 = (bf16[4,128,128]{2,1,0:T(8,128)(2,1)S(1)}, bf16[4,128,128]{2,1,0:T(8,128)(2,1)S(1)}, u32[]{:S(2)}, u32[]{:S(2)}) collective-permute-start(bf16[4,128,128]{2,1,0:T(8,128)(2,1)S(1)} %pad_maximum_fusion.2.rest_0_), channel_id=1, source_target_pairs={{0,24},{1,25},{2,26},{3,27},{4,28},{5,29},{6,30},{7,31},{8,16},{9,... | collective-permute-start | bytes 393224 | tf_op jit(solution)/shard_map/ppermute | solution.py:63
  84.4 17.4 %collective-permute-start.23 = (bf16[4,128,128]{2,1,0:T(8,128)(2,1)S(1)}, bf16[4,128,128]{2,1,0:T(8,128)(2,1)S(1)}, u32[]{:S(2)}, u32[]{:S(2)}) collective-permute-start(bf16[4,128,128]{2,1,0:T(8,128)(2,1)S(1)} %pad_maximum_fusion.2.rest_0_), channel_id=1, source_target_pairs={{0,16},{1,17},{2,18},{3,19},{4,20},{5,21},{6,22},{7,23},{8,24},{9,... | collective-permute-start | bytes 393224 | tf_op jit(solution)/shard_map/ppermute | solution.py:63
  84.7 17.1 %collective-permute-start.22 = (bf16[4,128,128]{2,1,0:T(8,128)(2,1)S(1)}, bf16[4,128,128]{2,1,0:T(8,128)(2,1)S(1)}, u32[]{:S(2)}, u32[]{:S(2)}) collective-permute-start(bf16[4,128,128]{2,1,0:T(8,128)(2,1)S(1)} %pad_maximum_fusion.2.rest_0_), channel_id=1, source_target_pairs={{0,8},{1,9},{2,10},{3,11},{4,12},{5,13},{6,14},{7,15},{8,0},{9,1},... | collective-permute-start | bytes 393224 | tf_op jit(solution)/shard_map/ppermute | solution.py:63
  86.3 9.8 %collective-permute-start.21 = (bf16[256,128]{1,0:T(8,128)(2,1)}, bf16[256,128]{1,0:T(8,128)(2,1)S(1)}, u32[]{:S(2)}, u32[]{:S(2)}) collective-permute-start(bf16[256,128]{1,0:T(8,128)(2,1)} %get-tuple-element.57), channel_id=1, source_target_pairs={{3,4},{7,8},{11,12},{15,16},{19,20},{23,24},{27,28},{4,3},{8,7},{1... | collective-permute-start | bytes 196616 | tf_op jit(solution)/shard_map/ppermute | solution.py:55
  101.9 3.8 %collective-permute-start.26 = (bf16[12,128,128]{2,1,0:T(8,128)(2,1)S(1)}, bf16[12,128,128]{2,1,0:T(8,128)(2,1)S(1)}, u32[]{:S(2)}, u32[]{:S(2)}) collective-permute-start(bf16[12,128,128]{2,1,0:T(8,128)(2,1)S(1)} %constant_dynamic-update-slice_fusion.6.rest_1_), channel_id=1, source_target_pairs={{0,4},{1,5},{2,6},{3,7},{4,0},{5,1},{6,2},{7,3},{8,12},{9,13},{10,... | collective-permute-start | bytes 1179656 | tf_op jit(solution)/shard_map/ppermute | solution.py:69
  (29 other events, 216.4 us)

commit v9 on v7

--- a/solution.py
+++ b/solution.py
@@ -35,7 +35,7 @@
     return p1, p3, pc
 
 
-def exchange(current, owned, p1, p3, pc, hub_blocks, width, block_rows, middle):
+def exchange(current, owned, p1, p3, pc, hub_blocks, width, block_rows, middle, late):
     count = lax.axis_size(AXES)
     if not fast_path(owned, block_rows):
         forward = [(i, i + 1) for i in range(count - 1)]
@@ -43,7 +43,7 @@
         low = lax.ppermute(current[current.shape[0] - width:], AXES, forward)
         high = lax.ppermute(current[:width], AXES, backward)
         hub_all = lax.all_gather(owned, AXES, axis=0, tiled=True)
-        return middle((low, high)), [hub_all.reshape(-1, block_rows, owned.shape[1])], hub_blocks
+        return middle((low, high)), [hub_all.reshape(-1, block_rows, owned.shape[1])], hub_blocks, 0
     me = lax.axis_index(AXES)
     pairs = lambda m: [(i, i ^ m) for i in range(count)]
     r3 = lax.ppermute(p3, AXES, pairs(3))
@@ -64,6 +64,8 @@
         recvs = [sent[m] for m in group]
         if done is None:
             done, recvs = lax.optimization_barrier((middle((r1, r3, rc)), recvs))
+        elif r + 2 == len(rounds):
+            done, recvs = lax.optimization_barrier((late(done, buf), recvs))
         offs = offs + [o ^ m for m in group for o in offs]
         pieces = [buf] + recvs
         if r + 2 < len(rounds):
@@ -72,7 +74,8 @@
     where = np.zeros(count, np.int32)
     for p, o in enumerate(offs):
         where[o] = p
-    return done, pieces, jnp.asarray(where)[hub_blocks ^ me]
+    assert len(rounds[-1]) == 1
+    return done, pieces[1:], jnp.asarray(where)[hub_blocks ^ me], pieces[0].shape[0]
 
 
 def band_kernel(fast, n_own, z_ref, off_ref, cur_hbm, *rest):
@@ -158,7 +161,44 @@
     )(z, band_offsets.reshape(-1), current, *rim_sources, band_tiles)
 
 
-def hub_kernel(n_hub, width, z_ref, hidx_ref, *rest):
+def early_kernel(hidx_ref, band_ref, hub_hbm, ht_hbm, out_ref, hub, ht, sem):
+    blocks, k_hub, rows = ht.shape[0], ht.shape[1], ht.shape[2]
+    n_early = hub.shape[0]
+    tiles = [pltpu.make_async_copy(ht_hbm.at[b], ht.at[b], sem.at[1 + b]) for b in range(blocks)]
+    mine = pltpu.make_async_copy(hub_hbm, hub, sem.at[0])
+    tiles[0].start()
+    mine.start()
+    for b in range(1, blocks):
+        tiles[b].start()
+    mine.wait()
+    for b in range(blocks):
+        tiles[b].wait()
+        span = pl.ds(b * rows, rows)
+        out_ref[span, :] = band_ref[span, :]
+        for h in range(k_hub):
+            p = hidx_ref[b * k_hub + h]
+
+            @pl.when(p < n_early)
+            def _():
+                out_ref[span, :] += jnp.dot(ht[b, h], hub[p], preferred_element_type=jnp.float32)
+
+
+def early_call(hub_index, band, mine, hub_tiles):
+    blocks = hub_tiles.shape[0]
+    return pl.pallas_call(
+        early_kernel,
+        in_specs=[SMEM, VMEM, ANY, ANY],
+        out_specs=VMEM,
+        out_shape=jax.ShapeDtypeStruct(band.shape, jnp.float32),
+        scratch_shapes=[
+            pltpu.VMEM(mine.shape, mine.dtype),
+            pltpu.VMEM(hub_tiles.shape, hub_tiles.dtype),
+            pltpu.SemaphoreType.DMA((1 + blocks,)),
+        ],
+    )(hub_index.reshape(-1), band, mine, hub_tiles)
+
+
+def hub_kernel(n_hub, width, lo, z_ref, hidx_ref, *rest):
     hub_hbm = rest[:n_hub]
     (ht_hbm, band_hbm, deg_hbm, seeds_hbm, pick_ref,
      out_ref, cur_ref, owned_ref, p1_ref, p3_ref, pc_ref,
@@ -194,11 +234,15 @@
         for c in per_block[b]:
             c.wait()
         span = pl.ds(b * rows, rows)
-        acc = jnp.zeros((rows, out_ref.shape[1]), jnp.float32)
+        out_ref[span, :] = band[span]
         for h in range(k_hub):
-            p = hidx_ref[b * k_hub + h]
-            acc = acc + jnp.dot(ht[b, h], hub[p], preferred_element_type=jnp.float32)
-        gathered = (band[span] + acc) / deg[span]
+            p = hidx_ref[b * k_hub + h] - lo
+
+            @pl.when(p >= 0)
+            def _():
+                out_ref[span, :] += jnp.dot(ht[b, h], hub[p], preferred_element_type=jnp.float32)
+
+        gathered = out_ref[span, :] / deg[span]
         labels = spread_weight * gathered + (1.0 - spread_weight) * seeds[span]
         out_ref[span, :] = labels
         cur_ref[span, :] = labels.astype(cur_ref.dtype)
@@ -214,7 +258,7 @@
     pc_ref[...] = jnp.where(z == 3, top, bottom)
 
 
-def hub_call(z, hub_index, pick, hub_pieces, hub_tiles, band, degree, seeds, width):
+def hub_call(z, hub_index, pick, hub_pieces, hub_tiles, band, degree, seeds, width, lo):
     blocks, k_hub, rows, _ = hub_tiles.shape
     classes = seeds.shape[1]
     n_hub = len(hub_pieces)
@@ -224,7 +268,7 @@
     flops = 2 * blocks * k_hub * rows * rows * classes
     bytes_accessed = hub_tiles.size * 2 + n_hub_blocks * rows * classes * 2 + seeds.size * 4 * 4
     return pl.pallas_call(
-        functools.partial(hub_kernel, n_hub, width),
+        functools.partial(hub_kernel, n_hub, width, lo),
         cost_estimate=pl.CostEstimate(flops=flops, transcendentals=0, bytes_accessed=bytes_accessed),
         in_specs=[SMEM, SMEM] + [ANY] * (n_hub + 4) + [VMEM],
         out_specs=[VMEM] * 6,
@@ -247,6 +291,19 @@
     )(z, hub_index.reshape(-1), *hub_pieces, hub_tiles, band, degree, seeds, pick)
 
 
+def positions_of(hub_blocks, owned, block_rows):
+    count = lax.axis_size(AXES)
+    if not fast_path(owned, block_rows):
+        return hub_blocks
+    offs = [0]
+    for group in ROUNDS_32:
+        offs = offs + [o ^ m for m in group for o in offs]
+    where = np.zeros(count, np.int32)
+    for p, o in enumerate(offs):
+        where[o] = p
+    return jnp.asarray(where)[hub_blocks ^ lax.axis_index(AXES)]
+
+
 def body(seed_scores, seed_mask, band_offsets, band_tiles, hub_blocks, hub_tiles, hub_rows):
     block_rows = band_tiles.shape[2]
     seeds = seed_mask.astype(jnp.float32)[:, None] * seed_scores.astype(jnp.float32)
@@ -265,11 +322,13 @@
         middle = functools.partial(
             band_call, z, band_offsets, current, band_tiles=band_tiles, fast=fast, n_own=owned.shape[0], width=width
         )
-        band, hub_pieces, hub_index = exchange(
-            current, owned, p1, p3, pc, hub_blocks, width, block_rows, lambda rims: middle(rims)
+        index = positions_of(hub_blocks, owned, block_rows)
+        band, hub_pieces, hub_index, lo = exchange(
+            current, owned, p1, p3, pc, hub_blocks, width, block_rows, lambda rims: middle(rims),
+            lambda band, mine: early_call(index, band, mine, hub_tiles),
         )
         labels, current, owned, p1, p3, pc = hub_call(
-            z, hub_index, pick, hub_pieces, hub_tiles, band, degree, seeds, width
+            z, hub_index, pick, hub_pieces, hub_tiles, band, degree, seeds, width, lo
         )
     return labels
 

time: 108 us -> 121 us (1.12)
  Pallas kernels: 32.3 us -> 58 us
  waiting for transfers between devices: 15.6 us -> 2.94 us
    pallas_call x3 -> x6, Pallas kernels: 16.9 us -> 42.7 us  [the longest x3 26 us: hub_call(): pl.pallas_call(functools.partial(hub_kernel, n_hub, width, lo), cost_esti...]
    ppermute x3, waiting for transfers between devices: 10 us -> 0.01 us  [exchange(): r3 = lax.ppermute(p3, AXES, pairs(3))]
    ppermute x3, starting transfers between devices: 2.68 us -> 7.65 us  [exchange(): r1 = lax.ppermute(p1, AXES, pairs(1))]
    ppermute x3, starting transfers between devices: 5.78 us -> 0.93 us  [exchange(): r3 = lax.ppermute(p3, AXES, pairs(3))]
    ppermute x12, waiting for transfers between devices: 3.1 us -> 0.03 us  [exchange(): lax.ppermute(buf, AXES, pairs(m))]
  transfers between devices with their start and end apart: 24 -> 24, of which waited for: 6 -> 2; matrix products, arithmetic and copies ran while one was open for 11% -> 10% of each run, Pallas kernels for 14% -> 27%
where the time goes in v9:
time: 121 us; the launch traced here: 120 us
  Pallas kernels  58 us (48%)
  starting transfers between devices  38 us (31%)
  local copies, waits for them, and re-layouts  12.2 us (10%)
  other arithmetic  8.25 us (7%)
  waiting for transfers between devices  2.94 us (2%)
    pallas_call x3, Pallas kernels, hub_call(): pl.pallas_call(functools.partial(hub_kernel, n_hub, width, lo), cost_esti...  26 us
    pallas_call x3, Pallas kernels, early_call(): pl.pallas_call(early_kernel, in_specs=[SMEM, VMEM, ANY, ANY], out_specs=V...  16.7 us
    pallas_call x3, Pallas kernels, band_call(): pl.pallas_call(functools.partial(band_kernel, fast, n_own), cost_estimate...  15.3 us
    ppermute x3, starting transfers between devices, exchange(): rc = lax.ppermute(pc, AXES, cross)  13.7 us
    ppermute x12, starting transfers between devices, exchange(): lax.ppermute(buf, AXES, pairs(m))  13.3 us
    unnamed x60, local copies, waits for them, and re-layouts  8.2 us
    ppermute x3, starting transfers between devices, exchange(): r1 = lax.ppermute(p1, AXES, pairs(1))  7.65 us
    ppermute x3, waiting for transfers between devices, exchange(): r1 = lax.ppermute(p1, AXES, pairs(1))  2.88 us
  transfers between devices with their start and end apart: 24, of which 2 were waited for; matrix products, arithmetic and copies ran while one was open for 10% of the time, Pallas kernels for 27%

profile of v9, /device:TPU:5, one launch (start us, length us, event | category | flops | bytes accessed | tf_op | source)
XLA Modules:
  0.0 120.1 jit_solution(9304784406322454170)
XLA Ops:
  1.4 1.9 %convert_multiply_fusion = (f32[1024,128]{1,0:T(8,128)}, bf16[1024,128]{1,0:T(8,128)(2,1)S(1)}) fusion(bf16[1024,128]{1,0:T(8,128)(2,1)} %param.13, f32[1024]{0:T(1024)S(1)} %convert_element_type.18), kind=kLoop, calls=%fused_computation.5 | loop fusion | flops 393216 | bytes 1052672 | tf_op jit(solution)/shard_map/mul | solution.py:309
  4.0 2.4 %collective-permute-start.3 = (bf16[128,128]{1,0:T(8,128)(2,1)S(1)}, bf16[128,128]{1,0:T(8,128)(2,1)S(1)}, u32[]{:S(2)}, u32[]{:S(2)}) collective-permute-start(bf16[128,128]{1,0:T(8,128)(2,1)S(1)} %gather_fusion.1), channel_id=1, source_target_pairs={{0,2},{1,3},{2,0},{3,1},{4,6},{5,7},{6,4},{7,5},{8,10},{9,11},{10,... | collective-permute-start | bytes 98312 | tf_op jit(solution)/shard_map/ppermute | solution.py:50
  6.5 1.4 %collective-permute-start = (bf16[384,128]{1,0:T(8,128)(2,1)S(1)}, bf16[384,128]{1,0:T(8,128)(2,1)S(1)}, u32[]{:S(2)}, u32[]{:S(2)}) collective-permute-start(bf16[384,128]{1,0:T(8,128)(2,1)S(1)} %get-tuple-element.69), channel_id=1, source_target_pairs={{0,1},{1,0},{2,3},{3,2},{4,5},{5,4},{6,7},{7,6},{8,9},{9,8},{10,11... | collective-permute-start | bytes 294920 | tf_op jit(solution)/shard_map/ppermute | solution.py:51
  7.8 6.6 %collective-permute-start.2 = (bf16[256,128]{1,0:T(8,128)(2,1)S(1)}, bf16[256,128]{1,0:T(8,128)(2,1)S(1)}, u32[]{:S(2)}, u32[]{:S(2)}) collective-permute-start(bf16[256,128]{1,0:T(8,128)(2,1)S(1)} %get-tuple-element.65), channel_id=1, source_target_pairs={{3,4},{7,8},{11,12},{15,16},{19,20},{23,24},{27,28},{4,3},{8,7},{1... | collective-permute-start | bytes 196616 | tf_op jit(solution)/shard_map/ppermute | solution.py:55
  14.4 2.2 %convert_reduce_fusion = f32[8,128]{1,0:T(8,128)S(1)} fusion(bf16[8,10,128,128]{3,2,1,0:T(8,128)(2,1)} %rest_3_.5), kind=kLoop, calls=%fused_computation.2 | loop fusion | flops 2620416 | bytes 2625536 | tf_op jit(solution)/shard_map/reduce_sum | solution.py:310
  20.8 5.2 %shard_map.127.band_ref = f32[1024,128]{1,0:T(8,128)} custom-call(s32[1]{0:T(128)} %bitcast.z_ref, s32[80]{0:T(128)} %reshape.50.off_ref, bf16[1024,128]{1,0:T(8,128)(2,1)} %copy-done.2, bf16[384,128]{1,0:T(8,128)(2,1)} %copy-done.9, bf16[384,128]{1,0:T(8,128)(2,1)} %copy-done.10, bf16[256,128]{1,0:T(8,128)(2,1)} %copy-done.15, bf16[8,10,128,128]{3,2,1,0:T(8,128)(2,1)} %rest_3_.5), custom_call_target="tpu_custom_call" | custom-call | flops 335544320 | bytes 3670016 | tf_op jit(solution)/shard_map/pallas_call | solution.py:150
  29.0 1.4 %gather_fusion = s32[48]{0:T(128)} fusion(s32[32]{0:T(128)S(1)} %copy-done, s32[1024]{0:T(1024)S(1)} %pad_clamp_fusion.1), kind=kCustom, calls=%fused_computation | custom fusion | bytes 576 | tf_op jit(solution)/shard_map/gather | solution.py:78
  31.2 5.6 %shard_map.128.rest_2_ = f32[1024,128]{1,0:T(8,128)} custom-call(s32[48]{0:T(128)} %gather_fusion, f32[1024,128]{1,0:T(8,128)} %shard_map.127.band_ref, bf16[16,128,128]{2,1,0:T(8,128)(2,1)} %copy-done.3, bf16[8,6,128,128]{3,2,1,0:T(8,128)(2,1)} %rest_1_.5), custom_call_target="tpu_custom_call" | custom-call | tf_op jit(solution)/shard_map/pallas_call | solution.py:188
  37.6 8.7 %shard_map.129 = (f32[1024,128]{1,0:T(8,128)}, bf16[1024,128]{1,0:T(8,128)(2,1)}, bf16[128,128]{1,0:T(8,128)(2,1)}, bf16[384,128]{1,0:T(8,128)(2,1)}, bf16[384,1...) custom-call(s32[1]{0:T(128)} %bitcast.z_ref, s32[48]{0:T(128)} %gather_fusion, bf16[16,128,128]{2,1,0:T(8,128)(2,1)} %copy-done.6, ...), custom_call_target="tpu_custom_call" | custom-call | flops 201326592 | bytes 4194304 | tf_op jit(solution)/shard_map/pallas_call | solution.py:270
  47.4 3.3 %collective-permute-start.8 = (bf16[384,128]{1,0:T(8,128)(2,1)}, bf16[384,128]{1,0:T(8,128)(2,1)S(1)}, u32[]{:S(2)}, u32[]{:S(2)}) collective-permute-start(bf16[384,128]{1,0:T(8,128)(2,1)} %get-tuple-element.41), channel_id=1, source_target_pairs={{0,1},{1,0},{2,3},{3,2},{4,5},{5,4},{6,7},{7,6},{8,9},{9,8},{10,11... | collective-permute-start | bytes 294920 | tf_op jit(solution)/shard_map/ppermute | solution.py:51
  50.7 3.3 %collective-permute-start.10 = (bf16[256,128]{1,0:T(8,128)(2,1)}, bf16[256,128]{1,0:T(8,128)(2,1)S(1)}, u32[]{:S(2)}, u32[]{:S(2)}) collective-permute-start(bf16[256,128]{1,0:T(8,128)(2,1)} %get-tuple-element.43), channel_id=1, source_target_pairs={{3,4},{7,8},{11,12},{15,16},{19,20},{23,24},{27,28},{4,3},{8,7},{1... | collective-permute-start | bytes 196616 | tf_op jit(solution)/shard_map/ppermute | solution.py:55
  54.0 1.9 %collective-permute-done.8.rest_0_ = bf16[384,128]{1,0:T(8,128)(2,1)S(1)} collective-permute-done((bf16[384,128]{1,0:T(8,128)(2,1)}, bf16[384,128]{1,0:T(8,128)(2,1)S(1)}, u32[]{:S(2)}, u32[]{:S(2)}) %collective-permute-start.8) | collective-permute-done | bytes 98336 | tf_op jit(solution)/shard_map/ppermute | solution.py:51
  57.2 2.3 %collective-permute-start.14 = (bf16[4,128,128]{2,1,0:T(8,128)(2,1)S(1)}, bf16[4,128,128]{2,1,0:T(8,128)(2,1)S(1)}, u32[]{:S(2)}, u32[]{:S(2)}) collective-permute-start(bf16[4,128,128]{2,1,0:T(8,128)(2,1)S(1)} %pad_maximum_fusion.1), channel_id=1, source_target_pairs={{0,24},{1,25},{2,26},{3,27},{4,28},{5,29},{6,30},{7,31},{8,16},{9,... | collective-permute-start | bytes 393224 | tf_op jit(solution)/shard_map/ppermute | solution.py:63
  60.1 5.1 %shard_map.130.band_ref = f32[1024,128]{1,0:T(8,128)} custom-call(s32[1]{0:T(128)} %bitcast.z_ref, s32[80]{0:T(128)} %reshape.50.off_ref, bf16[1024,128]{1,0:T(8,128)(2,1)} %get-tuple-element.40.cur_hbm, bf16[384,128]{1,0:T(8,128)(2,1)} %copy-done.14, bf16[384,128]{1,0:T(8,128)(2,1)} %copy-done.12, bf16[256,128]{1,0:T(8,128)(2,1)} %copy-done.17, ...), custom_call_target="tpu_custom_call" | custom-call | flops 335544320 | bytes 3670016 | tf_op jit(solution)/shard_map/pallas_call | solution.py:150
  66.1 1.6 %collective-permute-start.15 = (bf16[16,128,128]{2,1,0:T(8,128)(2,1)S(1)}, bf16[16,128,128]{2,1,0:T(8,128)(2,1)S(1)}, u32[]{:S(2)}, u32[]{:S(2)}) collective-permute-start(bf16[16,128,128]{2,1,0:T(8,128)(2,1)S(1)} %constant_dynamic-update-slice_fusion.7.hub_hbm), channel_id=1, source_target_pairs={{0,4},{1,5},{2,6},{3,7},{4,0},{5,1},{6,2},{7,3},{8,12},{9,13},{10,... | collective-permute-start | bytes 1572872 | tf_op jit(solution)/shard_map/ppermute | solution.py:63
  67.7 5.6 %shard_map.131.rest_2_ = f32[1024,128]{1,0:T(8,128)} custom-call(s32[48]{0:T(128)} %gather_fusion, f32[1024,128]{1,0:T(8,128)} %shard_map.130.band_ref, bf16[16,128,128]{2,1,0:T(8,128)(2,1)} %copy-done.4, bf16[8,6,128,128]{3,2,1,0:T(8,128)(2,1)} %rest_1_.5), custom_call_target="tpu_custom_call" | custom-call | tf_op jit(solution)/shard_map/pallas_call | solution.py:188
  74.1 8.7 %shard_map.132 = (f32[1024,128]{1,0:T(8,128)}, bf16[1024,128]{1,0:T(8,128)(2,1)}, bf16[128,128]{1,0:T(8,128)(2,1)}, bf16[384,128]{1,0:T(8,128)(2,1)}, bf16[384,1...) custom-call(s32[1]{0:T(128)} %bitcast.z_ref, s32[48]{0:T(128)} %gather_fusion, bf16[16,128,128]{2,1,0:T(8,128)(2,1)} %copy-done.8, ...), custom_call_target="tpu_custom_call" | custom-call | flops 201326592 | bytes 4194304 | tf_op jit(solution)/shard_map/pallas_call | solution.py:270
  84.1 3.0 %collective-permute-start.16 = (bf16[384,128]{1,0:T(8,128)(2,1)}, bf16[384,128]{1,0:T(8,128)(2,1)S(1)}, u32[]{:S(2)}, u32[]{:S(2)}) collective-permute-start(bf16[384,128]{1,0:T(8,128)(2,1)} %get-tuple-element.52), channel_id=1, source_target_pairs={{0,1},{1,0},{2,3},{3,2},{4,5},{5,4},{6,7},{7,6},{8,9},{9,8},{10,11... | collective-permute-start | bytes 294920 | tf_op jit(solution)/shard_map/ppermute | solution.py:51
  87.1 3.9 %collective-permute-start.18 = (bf16[256,128]{1,0:T(8,128)(2,1)}, bf16[256,128]{1,0:T(8,128)(2,1)S(1)}, u32[]{:S(2)}, u32[]{:S(2)}) collective-permute-start(bf16[256,128]{1,0:T(8,128)(2,1)} %get-tuple-element.54), channel_id=1, source_target_pairs={{3,4},{7,8},{11,12},{15,16},{19,20},{23,24},{27,28},{4,3},{8,7},{1... | collective-permute-start | bytes 196616 | tf_op jit(solution)/shard_map/ppermute | solution.py:55
  93.4 2.1 %collective-permute-start.22 = (bf16[4,128,128]{2,1,0:T(8,128)(2,1)S(1)}, bf16[4,128,128]{2,1,0:T(8,128)(2,1)S(1)}, u32[]{:S(2)}, u32[]{:S(2)}) collective-permute-start(bf16[4,128,128]{2,1,0:T(8,128)(2,1)S(1)} %pad_maximum_fusion.2), channel_id=1, source_target_pairs={{0,24},{1,25},{2,26},{3,27},{4,28},{5,29},{6,30},{7,31},{8,16},{9,... | collective-permute-start | bytes 393224 | tf_op jit(solution)/shard_map/ppermute | solution.py:63
  96.2 5.1 %shard_map.133.band_ref = f32[1024,128]{1,0:T(8,128)} custom-call(s32[1]{0:T(128)} %bitcast.z_ref, s32[80]{0:T(128)} %reshape.50.off_ref, bf16[1024,128]{1,0:T(8,128)(2,1)} %get-tuple-element.51.cur_hbm, bf16[384,128]{1,0:T(8,128)(2,1)} %copy-done.13, bf16[384,128]{1,0:T(8,128)(2,1)} %copy-done.11, bf16[256,128]{1,0:T(8,128)(2,1)} %copy-done.16, ...), custom_call_target="tpu_custom_call" | custom-call | flops 335544320 | bytes 3670016 | tf_op jit(solution)/shard_map/pallas_call | solution.py:150
  102.1 2.7 %collective-permute-start.23 = (bf16[16,128,128]{2,1,0:T(8,128)(2,1)S(1)}, bf16[16,128,128]{2,1,0:T(8,128)(2,1)S(1)}, u32[]{:S(2)}, u32[]{:S(2)}) collective-permute-start(bf16[16,128,128]{2,1,0:T(8,128)(2,1)S(1)} %constant_dynamic-update-slice_fusion.14.hub_hbm), channel_id=1, source_target_pairs={{0,4},{1,5},{2,6},{3,7},{4,0},{5,1},{6,2},{7,3},{8,12},{9,13},{10,... | collective-permute-start | bytes 1572872 | tf_op jit(solution)/shard_map/ppermute | solution.py:63
  104.9 5.6 %shard_map.134.rest_2_ = f32[1024,128]{1,0:T(8,128)} custom-call(s32[48]{0:T(128)} %gather_fusion, f32[1024,128]{1,0:T(8,128)} %shard_map.133.band_ref, bf16[16,128,128]{2,1,0:T(8,128)(2,1)} %copy-done.5, bf16[8,6,128,128]{3,2,1,0:T(8,128)(2,1)} %rest_1_.5), custom_call_target="tpu_custom_call" | custom-call | tf_op jit(solution)/shard_map/pallas_call | solution.py:188
  111.3 8.6 %shard_map.135 = (f32[1024,128]{1,0:T(8,128)}, bf16[1024,128]{1,0:T(8,128)(2,1)}, bf16[128,128]{1,0:T(8,128)(2,1)}, bf16[384,128]{1,0:T(8,128)(2,1)}, bf16[384,1...) custom-call(s32[1]{0:T(128)} %bitcast.z_ref, s32[48]{0:T(128)} %gather_fusion, bf16[16,128,128]{2,1,0:T(8,128)(2,1)} %copy-done.7, ...), custom_call_target="tpu_custom_call" | custom-call | flops 201326592 | bytes 4194304 | tf_op jit(solution)/shard_map/pallas_call | solution.py:270
  (122 shorter events, 21.4 us)
Async XLA Ops:
  4.0 13.4 %collective-permute-start.3 = (bf16[128,128]{1,0:T(8,128)(2,1)S(1)}, bf16[128,128]{1,0:T(8,128)(2,1)S(1)}, u32[]{:S(2)}, u32[]{:S(2)}) collective-permute-start(bf16[128,128]{1,0:T(8,128)(2,1)S(1)} %gather_fusion.1), channel_id=1, source_target_pairs={{0,2},{1,3},{2,0},{3,1},{4,6},{5,7},{6,4},{7,5},{8,10},{9,11},{10,... | collective-permute-start | bytes 98312 | tf_op jit(solution)/shard_map/ppermute | solution.py:50
  6.5 10.9 %collective-permute-start = (bf16[384,128]{1,0:T(8,128)(2,1)S(1)}, bf16[384,128]{1,0:T(8,128)(2,1)S(1)}, u32[]{:S(2)}, u32[]{:S(2)}) collective-permute-start(bf16[384,128]{1,0:T(8,128)(2,1)S(1)} %get-tuple-element.69), channel_id=1, source_target_pairs={{0,1},{1,0},{2,3},{3,2},{4,5},{5,4},{6,7},{7,6},{8,9},{9,8},{10,11... | collective-permute-start | bytes 294920 | tf_op jit(solution)/shard_map/ppermute | solution.py:51
  7.8 9.5 %collective-permute-start.1 = (bf16[384,128]{1,0:T(8,128)(2,1)S(1)}, bf16[384,128]{1,0:T(8,128)(2,1)S(1)}, u32[]{:S(2)}, u32[]{:S(2)}) collective-permute-start(bf16[384,128]{1,0:T(8,128)(2,1)S(1)} %get-tuple-element.68), channel_id=1, source_target_pairs={{0,3},{1,2},{2,1},{3,0},{4,7},{5,6},{6,5},{7,4},{8,11},{9,10},{10,... | collective-permute-start | bytes 294920 | tf_op jit(solution)/shard_map/ppermute | solution.py:49
  7.8 12.4 %collective-permute-start.2 = (bf16[256,128]{1,0:T(8,128)(2,1)S(1)}, bf16[256,128]{1,0:T(8,128)(2,1)S(1)}, u32[]{:S(2)}, u32[]{:S(2)}) collective-permute-start(bf16[256,128]{1,0:T(8,128)(2,1)S(1)} %get-tuple-element.65), channel_id=1, source_target_pairs={{3,4},{7,8},{11,12},{15,16},{19,20},{23,24},{27,28},{4,3},{8,7},{1... | collective-permute-start | bytes 196616 | tf_op jit(solution)/shard_map/ppermute | solution.py:55
  17.4 9.3 %collective-permute-start.4 = (bf16[4,128,128]{2,1,0:T(8,128)(2,1)S(1)}, bf16[4,128,128]{2,1,0:T(8,128)(2,1)S(1)}, u32[]{:S(2)}, u32[]{:S(2)}) collective-permute-start(bf16[4,128,128]{2,1,0:T(8,128)(2,1)S(1)} %pad_maximum_fusion), channel_id=1, source_target_pairs={{0,8},{1,9},{2,10},{3,11},{4,12},{5,13},{6,14},{7,15},{8,0},{9,1},... | collective-permute-start | bytes 393224 | tf_op jit(solution)/shard_map/ppermute | solution.py:63
  18.7 8.1 %collective-permute-start.5 = (bf16[4,128,128]{2,1,0:T(8,128)(2,1)S(1)}, bf16[4,128,128]{2,1,0:T(8,128)(2,1)S(1)}, u32[]{:S(2)}, u32[]{:S(2)}) collective-permute-start(bf16[4,128,128]{2,1,0:T(8,128)(2,1)S(1)} %pad_maximum_fusion), channel_id=1, source_target_pairs={{0,16},{1,17},{2,18},{3,19},{4,20},{5,21},{6,22},{7,23},{8,24},{9,... | collective-permute-start | bytes 393224 | tf_op jit(solution)/shard_map/ppermute | solution.py:63
  18.9 7.8 %collective-permute-start.6 = (bf16[4,128,128]{2,1,0:T(8,128)(2,1)S(1)}, bf16[4,128,128]{2,1,0:T(8,128)(2,1)S(1)}, u32[]{:S(2)}, u32[]{:S(2)}) collective-permute-start(bf16[4,128,128]{2,1,0:T(8,128)(2,1)S(1)} %pad_maximum_fusion), channel_id=1, source_target_pairs={{0,24},{1,25},{2,26},{3,27},{4,28},{5,29},{6,30},{7,31},{8,16},{9,... | collective-permute-start | bytes 393224 | tf_op jit(solution)/shard_map/ppermute | solution.py:63
  26.9 9.9 %collective-permute-start.7 = (bf16[16,128,128]{2,1,0:T(8,128)(2,1)S(1)}, bf16[16,128,128]{2,1,0:T(8,128)(2,1)S(1)}, u32[]{:S(2)}, u32[]{:S(2)}) collective-permute-start(bf16[16,128,128]{2,1,0:T(8,128)(2,1)S(1)} %constant_dynamic-update-slice_fusion.hub_hbm), channel_id=1, source_target_pairs={{0,4},{1,5},{2,6},{3,7},{4,0},{5,1},{6,2},{7,3},{8,12},{9,13},{10,... | collective-permute-start | bytes 1572872 | tf_op jit(solution)/shard_map/ppermute | solution.py:63
  46.3 7.7 %collective-permute-start.9 = (bf16[384,128]{1,0:T(8,128)(2,1)}, bf16[384,128]{1,0:T(8,128)(2,1)S(1)}, u32[]{:S(2)}, u32[]{:S(2)}) collective-permute-start(bf16[384,128]{1,0:T(8,128)(2,1)} %get-tuple-element.42), channel_id=1, source_target_pairs={{0,3},{1,2},{2,1},{3,0},{4,7},{5,6},{6,5},{7,4},{8,11},{9,10},{10,... | collective-permute-start | bytes 294920 | tf_op jit(solution)/shard_map/ppermute | solution.py:49
  47.4 8.5 %collective-permute-start.11 = (bf16[128,128]{1,0:T(8,128)(2,1)}, bf16[128,128]{1,0:T(8,128)(2,1)S(1)}, u32[]{:S(2)}, u32[]{:S(2)}) collective-permute-start(bf16[128,128]{1,0:T(8,128)(2,1)} %get-tuple-element.44), channel_id=1, source_target_pairs={{0,2},{1,3},{2,0},{3,1},{4,6},{5,7},{6,4},{7,5},{8,10},{9,11},{10,... | collective-permute-start | bytes 98312 | tf_op jit(solution)/shard_map/ppermute | solution.py:50
  47.4 8.5 %collective-permute-start.8 = (bf16[384,128]{1,0:T(8,128)(2,1)}, bf16[384,128]{1,0:T(8,128)(2,1)S(1)}, u32[]{:S(2)}, u32[]{:S(2)}) collective-permute-start(bf16[384,128]{1,0:T(8,128)(2,1)} %get-tuple-element.41), channel_id=1, source_target_pairs={{0,1},{1,0},{2,3},{3,2},{4,5},{5,4},{6,7},{7,6},{8,9},{9,8},{10,11... | collective-permute-start | bytes 294920 | tf_op jit(solution)/shard_map/ppermute | solution.py:51
  50.7 8.8 %collective-permute-start.10 = (bf16[256,128]{1,0:T(8,128)(2,1)}, bf16[256,128]{1,0:T(8,128)(2,1)S(1)}, u32[]{:S(2)}, u32[]{:S(2)}) collective-permute-start(bf16[256,128]{1,0:T(8,128)(2,1)} %get-tuple-element.43), channel_id=1, source_target_pairs={{3,4},{7,8},{11,12},{15,16},{19,20},{23,24},{27,28},{4,3},{8,7},{1... | collective-permute-start | bytes 196616 | tf_op jit(solution)/shard_map/ppermute | solution.py:55
  56.8 9.2 %collective-permute-start.12 = (bf16[4,128,128]{2,1,0:T(8,128)(2,1)S(1)}, bf16[4,128,128]{2,1,0:T(8,128)(2,1)S(1)}, u32[]{:S(2)}, u32[]{:S(2)}) collective-permute-start(bf16[4,128,128]{2,1,0:T(8,128)(2,1)S(1)} %pad_maximum_fusion.1), channel_id=1, source_target_pairs={{0,8},{1,9},{2,10},{3,11},{4,12},{5,13},{6,14},{7,15},{8,0},{9,1},... | collective-permute-start | bytes 393224 | tf_op jit(solution)/shard_map/ppermute | solution.py:63
  56.9 9.0 %collective-permute-start.13 = (bf16[4,128,128]{2,1,0:T(8,128)(2,1)S(1)}, bf16[4,128,128]{2,1,0:T(8,128)(2,1)S(1)}, u32[]{:S(2)}, u32[]{:S(2)}) collective-permute-start(bf16[4,128,128]{2,1,0:T(8,128)(2,1)S(1)} %pad_maximum_fusion.1), channel_id=1, source_target_pairs={{0,16},{1,17},{2,18},{3,19},{4,20},{5,21},{6,22},{7,23},{8,24},{9,... | collective-permute-start | bytes 393224 | tf_op jit(solution)/shard_map/ppermute | solution.py:63
  57.2 8.8 %collective-permute-start.14 = (bf16[4,128,128]{2,1,0:T(8,128)(2,1)S(1)}, bf16[4,128,128]{2,1,0:T(8,128)(2,1)S(1)}, u32[]{:S(2)}, u32[]{:S(2)}) collective-permute-start(bf16[4,128,128]{2,1,0:T(8,128)(2,1)S(1)} %pad_maximum_fusion.1), channel_id=1, source_target_pairs={{0,24},{1,25},{2,26},{3,27},{4,28},{5,29},{6,30},{7,31},{8,16},{9,... | collective-permute-start | bytes 393224 | tf_op jit(solution)/shard_map/ppermute | solution.py:63
  66.1 7.2 %collective-permute-start.15 = (bf16[16,128,128]{2,1,0:T(8,128)(2,1)S(1)}, bf16[16,128,128]{2,1,0:T(8,128)(2,1)S(1)}, u32[]{:S(2)}, u32[]{:S(2)}) collective-permute-start(bf16[16,128,128]{2,1,0:T(8,128)(2,1)S(1)} %constant_dynamic-update-slice_fusion.7.hub_hbm), channel_id=1, source_target_pairs={{0,4},{1,5},{2,6},{3,7},{4,0},{5,1},{6,2},{7,3},{8,12},{9,13},{10,... | collective-permute-start | bytes 1572872 | tf_op jit(solution)/shard_map/ppermute | solution.py:63
  82.8 8.2 %collective-permute-start.17 = (bf16[384,128]{1,0:T(8,128)(2,1)}, bf16[384,128]{1,0:T(8,128)(2,1)S(1)}, u32[]{:S(2)}, u32[]{:S(2)}) collective-permute-start(bf16[384,128]{1,0:T(8,128)(2,1)} %get-tuple-element.53), channel_id=1, source_target_pairs={{0,3},{1,2},{2,1},{3,0},{4,7},{5,6},{6,5},{7,4},{8,11},{9,10},{10,... | collective-permute-start | bytes 294920 | tf_op jit(solution)/shard_map/ppermute | solution.py:49
  84.1 7.9 %collective-permute-start.19 = (bf16[128,128]{1,0:T(8,128)(2,1)}, bf16[128,128]{1,0:T(8,128)(2,1)S(1)}, u32[]{:S(2)}, u32[]{:S(2)}) collective-permute-start(bf16[128,128]{1,0:T(8,128)(2,1)} %get-tuple-element.55), channel_id=1, source_target_pairs={{0,2},{1,3},{2,0},{3,1},{4,6},{5,7},{6,4},{7,5},{8,10},{9,11},{10,... | collective-permute-start | bytes 98312 | tf_op jit(solution)/shard_map/ppermute | solution.py:50
  84.1 7.9 %collective-permute-start.16 = (bf16[384,128]{1,0:T(8,128)(2,1)}, bf16[384,128]{1,0:T(8,128)(2,1)S(1)}, u32[]{:S(2)}, u32[]{:S(2)}) collective-permute-start(bf16[384,128]{1,0:T(8,128)(2,1)} %get-tuple-element.52), channel_id=1, source_target_pairs={{0,1},{1,0},{2,3},{3,2},{4,5},{5,4},{6,7},{7,6},{8,9},{9,8},{10,11... | collective-permute-start | bytes 294920 | tf_op jit(solution)/shard_map/ppermute | solution.py:51
  87.1 8.4 %collective-permute-start.18 = (bf16[256,128]{1,0:T(8,128)(2,1)}, bf16[256,128]{1,0:T(8,128)(2,1)S(1)}, u32[]{:S(2)}, u32[]{:S(2)}) collective-permute-start(bf16[256,128]{1,0:T(8,128)(2,1)} %get-tuple-element.54), channel_id=1, source_target_pairs={{3,4},{7,8},{11,12},{15,16},{19,20},{23,24},{27,28},{4,3},{8,7},{1... | collective-permute-start | bytes 196616 | tf_op jit(solution)/shard_map/ppermute | solution.py:55
  92.8 9.2 %collective-permute-start.20 = (bf16[4,128,128]{2,1,0:T(8,128)(2,1)S(1)}, bf16[4,128,128]{2,1,0:T(8,128)(2,1)S(1)}, u32[]{:S(2)}, u32[]{:S(2)}) collective-permute-start(bf16[4,128,128]{2,1,0:T(8,128)(2,1)S(1)} %pad_maximum_fusion.2), channel_id=1, source_target_pairs={{0,8},{1,9},{2,10},{3,11},{4,12},{5,13},{6,14},{7,15},{8,0},{9,1},... | collective-permute-start | bytes 393224 | tf_op jit(solution)/shard_map/ppermute | solution.py:63
  93.0 9.0 %collective-permute-start.21 = (bf16[4,128,128]{2,1,0:T(8,128)(2,1)S(1)}, bf16[4,128,128]{2,1,0:T(8,128)(2,1)S(1)}, u32[]{:S(2)}, u32[]{:S(2)}) collective-permute-start(bf16[4,128,128]{2,1,0:T(8,128)(2,1)S(1)} %pad_maximum_fusion.2), channel_id=1, source_target_pairs={{0,16},{1,17},{2,18},{3,19},{4,20},{5,21},{6,22},{7,23},{8,24},{9,... | collective-permute-start | bytes 393224 | tf_op jit(solution)/shard_map/ppermute | solution.py:63
  93.4 8.6 %collective-permute-start.22 = (bf16[4,128,128]{2,1,0:T(8,128)(2,1)S(1)}, bf16[4,128,128]{2,1,0:T(8,128)(2,1)S(1)}, u32[]{:S(2)}, u32[]{:S(2)}) collective-permute-start(bf16[4,128,128]{2,1,0:T(8,128)(2,1)S(1)} %pad_maximum_fusion.2), channel_id=1, source_target_pairs={{0,24},{1,25},{2,26},{3,27},{4,28},{5,29},{6,30},{7,31},{8,16},{9,... | collective-permute-start | bytes 393224 | tf_op jit(solution)/shard_map/ppermute | solution.py:63
  102.1 8.3 %collective-permute-start.23 = (bf16[16,128,128]{2,1,0:T(8,128)(2,1)S(1)}, bf16[16,128,128]{2,1,0:T(8,128)(2,1)S(1)}, u32[]{:S(2)}, u32[]{:S(2)}) collective-permute-start(bf16[16,128,128]{2,1,0:T(8,128)(2,1)S(1)} %constant_dynamic-update-slice_fusion.14.hub_hbm), channel_id=1, source_target_pairs={{0,4},{1,5},{2,6},{3,7},{4,0},{5,1},{6,2},{7,3},{8,12},{9,13},{10,... | collective-permute-start | bytes 1572872 | tf_op jit(solution)/shard_map/ppermute | solution.py:63
  (21 other events, 106.9 us)

commit v10 on v7

--- a/solution.py
+++ b/solution.py
@@ -35,7 +35,7 @@
     return p1, p3, pc
 
 
-def exchange(current, owned, p1, p3, pc, hub_blocks, width, block_rows, middle):
+def exchange(current, owned, p1, p3, pc, hub_blocks, width, block_rows, middle, prep):
     count = lax.axis_size(AXES)
     if not fast_path(owned, block_rows):
         forward = [(i, i + 1) for i in range(count - 1)]
@@ -43,7 +43,7 @@
         low = lax.ppermute(current[current.shape[0] - width:], AXES, forward)
         high = lax.ppermute(current[:width], AXES, backward)
         hub_all = lax.all_gather(owned, AXES, axis=0, tiled=True)
-        return middle((low, high)), [hub_all.reshape(-1, block_rows, owned.shape[1])], hub_blocks
+        return middle((low, high)), [hub_all.reshape(-1, block_rows, owned.shape[1])], prep
     me = lax.axis_index(AXES)
     pairs = lambda m: [(i, i ^ m) for i in range(count)]
     r3 = lax.ppermute(p3, AXES, pairs(3))
@@ -53,6 +53,8 @@
     cross = [(4 * g + 3, 4 * g + 4) for g in range(groups - 1)]
     cross += [(4 * g + 4, 4 * g + 3) for g in range(groups - 1)]
     rc = lax.ppermute(pc, AXES, cross)
+    if prep is not None:
+        (r1, r2, r3, rc), prep = lax.optimization_barrier(((r1, r2, r3, rc), prep))
     rows = block_rows
     buf = jnp.concatenate([owned[None], r1[None, :rows], r2[None], r3[None, :rows]], 0)
     offs = [0, 1, 2, 3]
@@ -72,7 +74,7 @@
     where = np.zeros(count, np.int32)
     for p, o in enumerate(offs):
         where[o] = p
-    return done, pieces, jnp.asarray(where)[hub_blocks ^ me]
+    return done, pieces, prep
 
 
 def band_kernel(fast, n_own, z_ref, off_ref, cur_hbm, *rest):
@@ -158,14 +160,15 @@
     )(z, band_offsets.reshape(-1), current, *rim_sources, band_tiles)
 
 
-def hub_kernel(n_hub, width, z_ref, hidx_ref, *rest):
+def hub_kernel(n_hub, width, final, z_ref, hidx_ref, *rest):
     hub_hbm = rest[:n_hub]
-    (ht_hbm, band_hbm, deg_hbm, seeds_hbm, pick_ref,
-     out_ref, cur_ref, owned_ref, p1_ref, p3_ref, pc_ref,
-     hub, ht, band, deg, seeds, sem) = rest[n_hub:]
+    if final:
+        (ht_hbm, band_hbm, deg_hbm, seeds_hbm, out_ref, hub, ht, band, deg, seeds, sem) = rest[n_hub:]
+    else:
+        (ht_hbm, band_hbm, deg_hbm, seeds_hbm, pick_ref,
+         cur_ref, owned_ref, p1_ref, p3_ref, pc_ref,
+         hub, ht, band, deg, seeds, sem) = rest[n_hub:]
     blocks, k_hub, rows = ht.shape[0], ht.shape[1], ht.shape[2]
-    own = cur_ref.shape[0]
-    n_own = owned_ref.shape[0]
     per_block = []
     for b in range(blocks):
         span = pl.ds(b * rows, rows)
@@ -194,14 +197,20 @@
         for c in per_block[b]:
             c.wait()
         span = pl.ds(b * rows, rows)
-        acc = jnp.zeros((rows, out_ref.shape[1]), jnp.float32)
+        acc = jnp.zeros((rows, hub.shape[2]), jnp.float32)
         for h in range(k_hub):
             p = hidx_ref[b * k_hub + h]
             acc = acc + jnp.dot(ht[b, h], hub[p], preferred_element_type=jnp.float32)
         gathered = (band[span] + acc) / deg[span]
-        labels = spread_weight * gathered + (1.0 - spread_weight) * seeds[span]
-        out_ref[span, :] = labels
-        cur_ref[span, :] = labels.astype(cur_ref.dtype)
+        labels = spread_weight * gathered + (1.0 - spread_weight) * seeds[span].astype(jnp.float32)
+        if final:
+            out_ref[span, :] = labels
+        else:
+            cur_ref[span, :] = labels.astype(cur_ref.dtype)
+    if final:
+        return
+    own = cur_ref.shape[0]
+    n_own = owned_ref.shape[0]
     owned = jnp.dot(pick_ref[...], cur_ref[...], preferred_element_type=jnp.float32).astype(owned_ref.dtype)
     owned_ref[...] = owned
     p1_ref[pl.ds(0, n_own), :] = owned
@@ -214,7 +223,7 @@
     pc_ref[...] = jnp.where(z == 3, top, bottom)
 
 
-def hub_call(z, hub_index, pick, hub_pieces, hub_tiles, band, degree, seeds, width):
+def hub_call(z, hub_index, pick, hub_pieces, hub_tiles, band, degree, seeds, width, final):
     blocks, k_hub, rows, _ = hub_tiles.shape
     classes = seeds.shape[1]
     n_hub = len(hub_pieces)
@@ -223,28 +232,44 @@
     bf = jnp.bfloat16
     flops = 2 * blocks * k_hub * rows * rows * classes
     bytes_accessed = hub_tiles.size * 2 + n_hub_blocks * rows * classes * 2 + seeds.size * 4 * 4
-    return pl.pallas_call(
-        functools.partial(hub_kernel, n_hub, width),
-        cost_estimate=pl.CostEstimate(flops=flops, transcendentals=0, bytes_accessed=bytes_accessed),
-        in_specs=[SMEM, SMEM] + [ANY] * (n_hub + 4) + [VMEM],
-        out_specs=[VMEM] * 6,
-        out_shape=[
-            jax.ShapeDtypeStruct(seeds.shape, jnp.float32),
+    if final:
+        outs = [jax.ShapeDtypeStruct(seeds.shape, jnp.float32)]
+    else:
+        outs = [
             jax.ShapeDtypeStruct(seeds.shape, bf),
             jax.ShapeDtypeStruct((n_own, classes), bf),
             jax.ShapeDtypeStruct((n_own + width, classes), bf),
             jax.ShapeDtypeStruct((n_own + width, classes), bf),
             jax.ShapeDtypeStruct((width, classes), bf),
-        ],
+        ]
+    return pl.pallas_call(
+        functools.partial(hub_kernel, n_hub, width, final),
+        cost_estimate=pl.CostEstimate(flops=flops, transcendentals=0, bytes_accessed=bytes_accessed),
+        in_specs=[SMEM, SMEM] + [ANY] * (n_hub + 4) + ([] if final else [VMEM]),
+        out_specs=[VMEM] * len(outs),
+        out_shape=outs,
         scratch_shapes=[
             pltpu.VMEM((n_hub_blocks, rows, classes), bf),
             pltpu.VMEM(hub_tiles.shape, hub_tiles.dtype),
             pltpu.VMEM(seeds.shape, jnp.float32),
             pltpu.VMEM(degree.shape, jnp.float32),
-            pltpu.VMEM(seeds.shape, jnp.float32),
+            pltpu.VMEM(seeds.shape, seeds.dtype),
             pltpu.SemaphoreType.DMA((n_hub + 4 * blocks,)),
         ],
-    )(z, hub_index.reshape(-1), *hub_pieces, hub_tiles, band, degree, seeds, pick)
+    )(z, hub_index.reshape(-1), *hub_pieces, hub_tiles, band, degree, seeds, *([] if final else [pick]))
+
+
+def positions_of(hub_blocks, owned, block_rows):
+    count = lax.axis_size(AXES)
+    if not fast_path(owned, block_rows):
+        return hub_blocks
+    offs = [0]
+    for group in ROUNDS_32:
+        offs = offs + [o ^ m for m in group for o in offs]
+    where = np.zeros(count, np.int32)
+    for p, o in enumerate(offs):
+        where[o] = p
+    return jnp.asarray(where)[hub_blocks ^ lax.axis_index(AXES)]
 
 
 def body(seed_scores, seed_mask, band_offsets, band_tiles, hub_blocks, hub_tiles, hub_rows):
@@ -257,20 +282,28 @@
     width = BW * block_rows
     z = lax.axis_index("hub").astype(jnp.int32).reshape(1)
     current = seeds.astype(jnp.bfloat16)
+    seeds16 = current
     owned = current[hub_rows]
     p1, p3, pc = payloads(current, owned, z[0], width)
     fast = fast_path(owned, block_rows)
     pick = (hub_rows[:, None] == jnp.arange(current.shape[0], dtype=hub_rows.dtype)[None, :]).astype(jnp.bfloat16)
+    prep = (pick, degree, positions_of(hub_blocks, owned, block_rows))
     for step in range(ITERS):
         middle = functools.partial(
             band_call, z, band_offsets, current, band_tiles=band_tiles, fast=fast, n_own=owned.shape[0], width=width
         )
-        band, hub_pieces, hub_index = exchange(
-            current, owned, p1, p3, pc, hub_blocks, width, block_rows, lambda rims: middle(rims)
+        band, hub_pieces, prep_out = exchange(
+            current, owned, p1, p3, pc, hub_blocks, width, block_rows, lambda rims: middle(rims), prep
         )
-        labels, current, owned, p1, p3, pc = hub_call(
-            z, hub_index, pick, hub_pieces, hub_tiles, band, degree, seeds, width
-        )
+        if prep is not None:
+            pick, degree, hub_index = prep_out
+            prep = None
+        final = step + 1 == ITERS
+        outs = hub_call(z, hub_index, pick, hub_pieces, hub_tiles, band, degree, seeds16, width, final)
+        if final:
+            labels = outs[0]
+        else:
+            current, owned, p1, p3, pc = outs
     return labels
 
 

time: 108 us -> 97.7 us (0.905)
  waiting for transfers between devices: 15.6 us -> 6.41 us
    ppermute x3, waiting for transfers between devices: 10 us -> 0.01 us  [exchange(): r3 = lax.ppermute(p3, AXES, pairs(3))]
    ppermute x3, starting transfers between devices: 5.78 us -> 1.22 us  [exchange(): r3 = lax.ppermute(p3, AXES, pairs(3))]
    ppermute x3, starting transfers between devices: 2.68 us -> 7.07 us  [exchange(): r1 = lax.ppermute(p1, AXES, pairs(1))]
    mul x1 -> x0, other arithmetic: 1.94 us -> none  [body(): seed_mask.astype(jnp.float32)[:, None] * seed_scores.astype(jnp.float32)]
    convert_element_type x0 -> x1, other arithmetic: none -> 1.15 us  [body(): current = seeds.astype(jnp.bfloat16)]
    unnamed x60 -> x56, local copies, waits for them, and re-layouts: 8.23 us -> 7.65 us
  transfers between devices with their start and end apart: 24 -> 24, of which waited for: 6 -> 5; matrix products, arithmetic and copies ran while one was open for 11% -> 13% of each run, Pallas kernels for 14% -> 16%
where the time goes in v10:
time: 97.7 us; the launch traced here: 96.5 us
  starting transfers between devices  37.6 us (38%)
  Pallas kernels  31.5 us (32%)
  local copies, waits for them, and re-layouts  11.7 us (12%)
  other arithmetic  8.87 us (9%)
  waiting for transfers between devices  6.41 us (7%)
    pallas_call x3, Pallas kernels, hub_call(): pl.pallas_call(functools.partial(hub_kernel, n_hub, width, final), cost_e...  16.2 us
    pallas_call x3, Pallas kernels, band_call(): pl.pallas_call(functools.partial(band_kernel, fast, n_own), cost_estimate...  15.3 us
    ppermute x3, starting transfers between devices, exchange(): rc = lax.ppermute(pc, AXES, cross)  13.5 us
    ppermute x12, starting transfers between devices, exchange(): lax.ppermute(buf, AXES, pairs(m))  13.1 us
    unnamed x56, local copies, waits for them, and re-layouts  7.65 us
    ppermute x3, starting transfers between devices, exchange(): r1 = lax.ppermute(p1, AXES, pairs(1))  7.07 us
    ppermute x12, waiting for transfers between devices, exchange(): lax.ppermute(buf, AXES, pairs(m))  3.47 us
    ppermute x3, waiting for transfers between devices, exchange(): r1 = lax.ppermute(p1, AXES, pairs(1))  2.92 us
  transfers between devices with their start and end apart: 24, of which 5 were waited for; matrix products, arithmetic and copies ran while one was open for 13% of the time, Pallas kernels for 16%

profile of v10, /device:TPU:5, one launch (start us, length us, event | category | flops | bytes accessed | tf_op | source)
XLA Modules:
  0.0 96.5 jit_solution(9418826356338970640)
XLA Ops:
  4.1 2.4 %collective-permute-start.1 = (bf16[128,128]{1,0:T(8,128)(2,1)S(1)}, bf16[128,128]{1,0:T(8,128)(2,1)S(1)}, u32[]{:S(2)}, u32[]{:S(2)}) collective-permute-start(bf16[128,128]{1,0:T(8,128)(2,1)S(1)} %gather_fusion), channel_id=1, source_target_pairs={{0,2},{1,3},{2,0},{3,1},{4,6},{5,7},{6,4},{7,5},{8,10},{9,11},{10,... | collective-permute-start | bytes 98312 | tf_op jit(solution)/shard_map/ppermute | solution.py:50
  6.5 1.4 %collective-permute-start = (bf16[384,128]{1,0:T(8,128)(2,1)S(1)}, bf16[384,128]{1,0:T(8,128)(2,1)S(1)}, u32[]{:S(2)}, u32[]{:S(2)}) collective-permute-start(bf16[384,128]{1,0:T(8,128)(2,1)S(1)} %get-tuple-element.67), channel_id=1, source_target_pairs={{0,1},{1,0},{2,3},{3,2},{4,5},{5,4},{6,7},{7,6},{8,9},{9,8},{10,11... | collective-permute-start | bytes 294920 | tf_op jit(solution)/shard_map/ppermute | solution.py:51
  7.9 6.6 %collective-permute-start.3 = (bf16[256,128]{1,0:T(8,128)(2,1)S(1)}, bf16[256,128]{1,0:T(8,128)(2,1)S(1)}, u32[]{:S(2)}, u32[]{:S(2)}) collective-permute-start(bf16[256,128]{1,0:T(8,128)(2,1)S(1)} %get-tuple-element.63), channel_id=1, source_target_pairs={{3,4},{7,8},{11,12},{15,16},{19,20},{23,24},{27,28},{4,3},{8,7},{1... | collective-permute-start | bytes 196616 | tf_op jit(solution)/shard_map/ppermute | solution.py:55
  14.5 1.5 %fusion.rest_6_ = bf16[128,1024]{1,0:T(8,128)(2,1)} fusion(s32[128]{0:T(128)} %param.14), kind=kLoop, calls=%fused_computation.6 | loop fusion | flops 262144 | bytes 262656 | tf_op jit(solution)/shard_map/convert_element_type | solution.py:289
  15.9 2.2 %convert_reduce_fusion = f32[8,128]{1,0:T(8,128)S(1)} fusion(bf16[8,10,128,128]{3,2,1,0:T(8,128)(2,1)} %rest_3_.5), kind=kLoop, calls=%fused_computation.2 | loop fusion | flops 2620416 | bytes 2625536 | tf_op jit(solution)/shard_map/reduce_sum | solution.py:278
  20.1 1.3 %collective-permute-start.4 = (bf16[4,128,128]{2,1,0:T(8,128)(2,1)S(1)}, bf16[4,128,128]{2,1,0:T(8,128)(2,1)S(1)}, u32[]{:S(2)}, u32[]{:S(2)}) collective-permute-start(bf16[4,128,128]{2,1,0:T(8,128)(2,1)S(1)} %pad_maximum_fusion), channel_id=1, source_target_pairs={{0,8},{1,9},{2,10},{3,11},{4,12},{5,13},{6,14},{7,15},{8,0},{9,1},... | collective-permute-start | bytes 393224 | tf_op jit(solution)/shard_map/ppermute | solution.py:65
  22.8 5.1 %shard_map.82.rest_3_ = f32[1024,128]{1,0:T(8,128)} custom-call(s32[1]{0:T(128)} %bitcast.z_ref, s32[80]{0:T(128)} %reshape.36.off_ref, bf16[1024,128]{1,0:T(8,128)(2,1)} %copy-done.2, bf16[384,128]{1,0:T(8,128)(2,1)} %copy-done.9, bf16[384,128]{1,0:T(8,128)(2,1)} %copy-done.10, bf16[256,128]{1,0:T(8,128)(2,1)} %copy-done.15, bf16[8,10,128,128]{3,2,1,0:T(8,128)(2,1)} %rest_3_.5), custom_call_target="tpu_custom_call" | custom-call | flops 335544320 | bytes 3670016 | tf_op jit(solution)/shard_map/pallas_call | solution.py:149
  32.1 5.5 %shard_map.83 = (bf16[1024,128]{1,0:T(8,128)(2,1)}, bf16[128,128]{1,0:T(8,128)(2,1)}, bf16[384,128]{1,0:T(8,128)(2,1)}, bf16[384,128]{1,0:T(8,128)(2,1)}, bf16[256,128]{1,0:T(8,128)(2,1)}) custom-call(s32[1]{0:T(128)} %bitcast.z_ref, s32[48]{0:T(128)} %reshape.35.hidx_ref, bf16[16,128,128]{2,1,0:T(8,128)(2,1)} %copy-done.3, bf16[16,128,128]{2,1,0:T(8,128)(2,1)} %copy-done.6, ...), custom_call_target="tpu_custom_call" | custom-call | flops 201326592 | bytes 4718592 | tf_op jit(solution)/shard_map/pallas_call | solution.py:245
  39.3 2.7 %collective-permute-start.8 = (bf16[384,128]{1,0:T(8,128)(2,1)}, bf16[384,128]{1,0:T(8,128)(2,1)S(1)}, u32[]{:S(2)}, u32[]{:S(2)}) collective-permute-start(bf16[384,128]{1,0:T(8,128)(2,1)} %get-tuple-element.46), channel_id=1, source_target_pairs={{0,1},{1,0},{2,3},{3,2},{4,5},{5,4},{6,7},{7,6},{8,9},{9,8},{10,11... | collective-permute-start | bytes 294920 | tf_op jit(solution)/shard_map/ppermute | solution.py:51
  42.0 3.7 %collective-permute-start.11 = (bf16[256,128]{1,0:T(8,128)(2,1)}, bf16[256,128]{1,0:T(8,128)(2,1)S(1)}, u32[]{:S(2)}, u32[]{:S(2)}) collective-permute-start(bf16[256,128]{1,0:T(8,128)(2,1)} %get-tuple-element.49), channel_id=1, source_target_pairs={{3,4},{7,8},{11,12},{15,16},{19,20},{23,24},{27,28},{4,3},{8,7},{1... | collective-permute-start | bytes 196616 | tf_op jit(solution)/shard_map/ppermute | solution.py:55
  45.8 1.2 %collective-permute-done.8.rest_0_ = bf16[384,128]{1,0:T(8,128)(2,1)S(1)} collective-permute-done((bf16[384,128]{1,0:T(8,128)(2,1)}, bf16[384,128]{1,0:T(8,128)(2,1)S(1)}, u32[]{:S(2)}, u32[]{:S(2)}) %collective-permute-start.8) | collective-permute-done | bytes 98336 | tf_op jit(solution)/shard_map/ppermute | solution.py:51
  49.1 1.4 %collective-permute-start.14 = (bf16[4,128,128]{2,1,0:T(8,128)(2,1)S(1)}, bf16[4,128,128]{2,1,0:T(8,128)(2,1)S(1)}, u32[]{:S(2)}, u32[]{:S(2)}) collective-permute-start(bf16[4,128,128]{2,1,0:T(8,128)(2,1)S(1)} %pad_maximum_fusion.1), channel_id=1, source_target_pairs={{0,24},{1,25},{2,26},{3,27},{4,28},{5,29},{6,30},{7,31},{8,16},{9,... | collective-permute-start | bytes 393224 | tf_op jit(solution)/shard_map/ppermute | solution.py:65
  51.2 5.1 %shard_map.84.rest_3_ = f32[1024,128]{1,0:T(8,128)} custom-call(s32[1]{0:T(128)} %bitcast.z_ref, s32[80]{0:T(128)} %reshape.36.off_ref, bf16[1024,128]{1,0:T(8,128)(2,1)} %get-tuple-element.48.cur_hbm, bf16[384,128]{1,0:T(8,128)(2,1)} %copy-done.14, bf16[384,128]{1,0:T(8,128)(2,1)} %copy-done.12, bf16[256,128]{1,0:T(8,128)(2,1)} %copy-done.17, ...), custom_call_target="tpu_custom_call" | custom-call | flops 335544320 | bytes 3670016 | tf_op jit(solution)/shard_map/pallas_call | solution.py:149
  57.2 2.2 %collective-permute-start.15 = (bf16[16,128,128]{2,1,0:T(8,128)(2,1)S(1)}, bf16[16,128,128]{2,1,0:T(8,128)(2,1)S(1)}, u32[]{:S(2)}, u32[]{:S(2)}) collective-permute-start(bf16[16,128,128]{2,1,0:T(8,128)(2,1)S(1)} %constant_dynamic-update-slice_fusion.7.rest_0_), channel_id=1, source_target_pairs={{0,4},{1,5},{2,6},{3,7},{4,0},{5,1},{6,2},{7,3},{8,12},{9,13},{10,... | collective-permute-start | bytes 1572872 | tf_op jit(solution)/shard_map/ppermute | solution.py:65
  59.4 1.5 %collective-permute-done.15.rest_1_ = bf16[16,128,128]{2,1,0:T(8,128)(2,1)S(1)} collective-permute-done((bf16[16,128,128]{2,1,0:T(8,128)(2,1)S(1)}, bf16[16,128,128]{2,1,0:T(8,128)(2,1)S(1)}, u32[]{:S(2)}, u32[]{:S(2)}) %collective-permute-start.15) | collective-permute-done | bytes 524320 | tf_op jit(solution)/shard_map/ppermute | solution.py:65
  61.7 5.5 %shard_map.85 = (bf16[1024,128]{1,0:T(8,128)(2,1)}, bf16[128,128]{1,0:T(8,128)(2,1)}, bf16[384,128]{1,0:T(8,128)(2,1)}, bf16[384,128]{1,0:T(8,128)(2,1)}, bf16[256,128]{1,0:T(8,128)(2,1)}) custom-call(s32[1]{0:T(128)} %bitcast.z_ref, s32[48]{0:T(128)} %reshape.35.hidx_ref, bf16[16,128,128]{2,1,0:T(8,128)(2,1)} %copy-done.4, bf16[16,128,128]{2,1,0:T(8,128)(2,1)} %copy-done.7, ...), custom_call_target="tpu_custom_call" | custom-call | flops 201326592 | bytes 4718592 | tf_op jit(solution)/shard_map/pallas_call | solution.py:245
  68.6 3.0 %collective-permute-start.16 = (bf16[384,128]{1,0:T(8,128)(2,1)}, bf16[384,128]{1,0:T(8,128)(2,1)S(1)}, u32[]{:S(2)}, u32[]{:S(2)}) collective-permute-start(bf16[384,128]{1,0:T(8,128)(2,1)} %get-tuple-element.55), channel_id=1, source_target_pairs={{0,1},{1,0},{2,3},{3,2},{4,5},{5,4},{6,7},{7,6},{8,9},{9,8},{10,11... | collective-permute-start | bytes 294920 | tf_op jit(solution)/shard_map/ppermute | solution.py:51
  71.6 3.2 %collective-permute-start.19 = (bf16[256,128]{1,0:T(8,128)(2,1)}, bf16[256,128]{1,0:T(8,128)(2,1)S(1)}, u32[]{:S(2)}, u32[]{:S(2)}) collective-permute-start(bf16[256,128]{1,0:T(8,128)(2,1)} %get-tuple-element.58), channel_id=1, source_target_pairs={{3,4},{7,8},{11,12},{15,16},{19,20},{23,24},{27,28},{4,3},{8,7},{1... | collective-permute-start | bytes 196616 | tf_op jit(solution)/shard_map/ppermute | solution.py:55
  74.9 1.7 %collective-permute-done.16.rest_0_ = bf16[384,128]{1,0:T(8,128)(2,1)S(1)} collective-permute-done((bf16[384,128]{1,0:T(8,128)(2,1)}, bf16[384,128]{1,0:T(8,128)(2,1)S(1)}, u32[]{:S(2)}, u32[]{:S(2)}) %collective-permute-start.16) | collective-permute-done | bytes 98336 | tf_op jit(solution)/shard_map/ppermute | solution.py:51
  78.1 2.0 %collective-permute-start.22 = (bf16[4,128,128]{2,1,0:T(8,128)(2,1)S(1)}, bf16[4,128,128]{2,1,0:T(8,128)(2,1)S(1)}, u32[]{:S(2)}, u32[]{:S(2)}) collective-permute-start(bf16[4,128,128]{2,1,0:T(8,128)(2,1)S(1)} %pad_maximum_fusion.2), channel_id=1, source_target_pairs={{0,24},{1,25},{2,26},{3,27},{4,28},{5,29},{6,30},{7,31},{8,16},{9,... | collective-permute-start | bytes 393224 | tf_op jit(solution)/shard_map/ppermute | solution.py:65
  80.8 5.1 %shard_map.86.rest_3_ = f32[1024,128]{1,0:T(8,128)} custom-call(s32[1]{0:T(128)} %bitcast.z_ref, s32[80]{0:T(128)} %reshape.36.off_ref, bf16[1024,128]{1,0:T(8,128)(2,1)} %get-tuple-element.57.cur_hbm, bf16[384,128]{1,0:T(8,128)(2,1)} %copy-done.13, bf16[384,128]{1,0:T(8,128)(2,1)} %copy-done.11, bf16[256,128]{1,0:T(8,128)(2,1)} %copy-done.16, ...), custom_call_target="tpu_custom_call" | custom-call | flops 335544320 | bytes 3670016 | tf_op jit(solution)/shard_map/pallas_call | solution.py:149
  86.8 2.3 %collective-permute-start.23 = (bf16[16,128,128]{2,1,0:T(8,128)(2,1)S(1)}, bf16[16,128,128]{2,1,0:T(8,128)(2,1)S(1)}, u32[]{:S(2)}, u32[]{:S(2)}) collective-permute-start(bf16[16,128,128]{2,1,0:T(8,128)(2,1)S(1)} %constant_dynamic-update-slice_fusion.14.rest_0_), channel_id=1, source_target_pairs={{0,4},{1,5},{2,6},{3,7},{4,0},{5,1},{6,2},{7,3},{8,12},{9,13},{10,... | collective-permute-start | bytes 1572872 | tf_op jit(solution)/shard_map/ppermute | solution.py:65
  89.1 1.5 %collective-permute-done.23.rest_1_ = bf16[16,128,128]{2,1,0:T(8,128)(2,1)S(1)} collective-permute-done((bf16[16,128,128]{2,1,0:T(8,128)(2,1)S(1)}, bf16[16,128,128]{2,1,0:T(8,128)(2,1)S(1)}, u32[]{:S(2)}, u32[]{:S(2)}) %collective-permute-start.23) | collective-permute-done | bytes 524320 | tf_op jit(solution)/shard_map/ppermute | solution.py:65
  91.4 5.1 %shard_map.87 = f32[1024,128]{1,0:T(8,128)} custom-call(s32[1]{0:T(128)} %bitcast.z_ref, s32[48]{0:T(128)} %reshape.35.hidx_ref, bf16[16,128,128]{2,1,0:T(8,128)(2,1)} %copy-done.5, bf16[16,128,128]{2,1,0:T(8,128)(2,1)} %copy-done.8, bf16[8,6,128,128]{3,2,1,0:T(8,128)(2,1)} %rest_2_.5, f32[1024,128]{1,0:T(8,128)} %shard_map.86.rest_3_, ...), custom_call_target="tpu_custom_call" | custom-call | flops 201326592 | bytes 4718592 | tf_op jit(solution)/shard_map/pallas_call | solution.py:245
  (116 shorter events, 22.7 us)
Async XLA Ops:
  4.1 15.8 %collective-permute-start.1 = (bf16[128,128]{1,0:T(8,128)(2,1)S(1)}, bf16[128,128]{1,0:T(8,128)(2,1)S(1)}, u32[]{:S(2)}, u32[]{:S(2)}) collective-permute-start(bf16[128,128]{1,0:T(8,128)(2,1)S(1)} %gather_fusion), channel_id=1, source_target_pairs={{0,2},{1,3},{2,0},{3,1},{4,6},{5,7},{6,4},{7,5},{8,10},{9,11},{10,... | collective-permute-start | bytes 98312 | tf_op jit(solution)/shard_map/ppermute | solution.py:50
  6.5 13.4 %collective-permute-start = (bf16[384,128]{1,0:T(8,128)(2,1)S(1)}, bf16[384,128]{1,0:T(8,128)(2,1)S(1)}, u32[]{:S(2)}, u32[]{:S(2)}) collective-permute-start(bf16[384,128]{1,0:T(8,128)(2,1)S(1)} %get-tuple-element.67), channel_id=1, source_target_pairs={{0,1},{1,0},{2,3},{3,2},{4,5},{5,4},{6,7},{7,6},{8,9},{9,8},{10,11... | collective-permute-start | bytes 294920 | tf_op jit(solution)/shard_map/ppermute | solution.py:51
  7.9 12.1 %collective-permute-start.2 = (bf16[384,128]{1,0:T(8,128)(2,1)S(1)}, bf16[384,128]{1,0:T(8,128)(2,1)S(1)}, u32[]{:S(2)}, u32[]{:S(2)}) collective-permute-start(bf16[384,128]{1,0:T(8,128)(2,1)S(1)} %get-tuple-element.66), channel_id=1, source_target_pairs={{0,3},{1,2},{2,1},{3,0},{4,7},{5,6},{6,5},{7,4},{8,11},{9,10},{10,... | collective-permute-start | bytes 294920 | tf_op jit(solution)/shard_map/ppermute | solution.py:49
  7.9 12.0 %collective-permute-start.3 = (bf16[256,128]{1,0:T(8,128)(2,1)S(1)}, bf16[256,128]{1,0:T(8,128)(2,1)S(1)}, u32[]{:S(2)}, u32[]{:S(2)}) collective-permute-start(bf16[256,128]{1,0:T(8,128)(2,1)S(1)} %get-tuple-element.63), channel_id=1, source_target_pairs={{3,4},{7,8},{11,12},{15,16},{19,20},{23,24},{27,28},{4,3},{8,7},{1... | collective-permute-start | bytes 196616 | tf_op jit(solution)/shard_map/ppermute | solution.py:55
  20.1 8.6 %collective-permute-start.4 = (bf16[4,128,128]{2,1,0:T(8,128)(2,1)S(1)}, bf16[4,128,128]{2,1,0:T(8,128)(2,1)S(1)}, u32[]{:S(2)}, u32[]{:S(2)}) collective-permute-start(bf16[4,128,128]{2,1,0:T(8,128)(2,1)S(1)} %pad_maximum_fusion), channel_id=1, source_target_pairs={{0,8},{1,9},{2,10},{3,11},{4,12},{5,13},{6,14},{7,15},{8,0},{9,1},... | collective-permute-start | bytes 393224 | tf_op jit(solution)/shard_map/ppermute | solution.py:65
  21.3 7.7 %collective-permute-start.5 = (bf16[4,128,128]{2,1,0:T(8,128)(2,1)S(1)}, bf16[4,128,128]{2,1,0:T(8,128)(2,1)S(1)}, u32[]{:S(2)}, u32[]{:S(2)}) collective-permute-start(bf16[4,128,128]{2,1,0:T(8,128)(2,1)S(1)} %pad_maximum_fusion), channel_id=1, source_target_pairs={{0,16},{1,17},{2,18},{3,19},{4,20},{5,21},{6,22},{7,23},{8,24},{9,... | collective-permute-start | bytes 393224 | tf_op jit(solution)/shard_map/ppermute | solution.py:65
  21.6 7.5 %collective-permute-start.6 = (bf16[4,128,128]{2,1,0:T(8,128)(2,1)S(1)}, bf16[4,128,128]{2,1,0:T(8,128)(2,1)S(1)}, u32[]{:S(2)}, u32[]{:S(2)}) collective-permute-start(bf16[4,128,128]{2,1,0:T(8,128)(2,1)S(1)} %pad_maximum_fusion), channel_id=1, source_target_pairs={{0,24},{1,25},{2,26},{3,27},{4,28},{5,29},{6,30},{7,31},{8,16},{9,... | collective-permute-start | bytes 393224 | tf_op jit(solution)/shard_map/ppermute | solution.py:65
  29.2 2.1 %collective-permute-start.7 = (bf16[16,128,128]{2,1,0:T(8,128)(2,1)S(1)}, bf16[16,128,128]{2,1,0:T(8,128)(2,1)S(1)}, u32[]{:S(2)}, u32[]{:S(2)}) collective-permute-start(bf16[16,128,128]{2,1,0:T(8,128)(2,1)S(1)} %constant_dynamic-update-slice_fusion.rest_0_), channel_id=1, source_target_pairs={{0,4},{1,5},{2,6},{3,7},{4,0},{5,1},{6,2},{7,3},{8,12},{9,13},{10,... | collective-permute-start | bytes 1572872 | tf_op jit(solution)/shard_map/ppermute | solution.py:65
  37.6 8.1 %collective-permute-start.10 = (bf16[384,128]{1,0:T(8,128)(2,1)}, bf16[384,128]{1,0:T(8,128)(2,1)S(1)}, u32[]{:S(2)}, u32[]{:S(2)}) collective-permute-start(bf16[384,128]{1,0:T(8,128)(2,1)} %get-tuple-element.47), channel_id=1, source_target_pairs={{0,3},{1,2},{2,1},{3,0},{4,7},{5,6},{6,5},{7,4},{8,11},{9,10},{10,... | collective-permute-start | bytes 294920 | tf_op jit(solution)/shard_map/ppermute | solution.py:49
  39.3 7.7 %collective-permute-start.9 = (bf16[128,128]{1,0:T(8,128)(2,1)}, bf16[128,128]{1,0:T(8,128)(2,1)S(1)}, u32[]{:S(2)}, u32[]{:S(2)}) collective-permute-start(bf16[128,128]{1,0:T(8,128)(2,1)} %get-tuple-element.45), channel_id=1, source_target_pairs={{0,2},{1,3},{2,0},{3,1},{4,6},{5,7},{6,4},{7,5},{8,10},{9,11},{10,... | collective-permute-start | bytes 98312 | tf_op jit(solution)/shard_map/ppermute | solution.py:50
  39.3 7.7 %collective-permute-start.8 = (bf16[384,128]{1,0:T(8,128)(2,1)}, bf16[384,128]{1,0:T(8,128)(2,1)S(1)}, u32[]{:S(2)}, u32[]{:S(2)}) collective-permute-start(bf16[384,128]{1,0:T(8,128)(2,1)} %get-tuple-element.46), channel_id=1, source_target_pairs={{0,1},{1,0},{2,3},{3,2},{4,5},{5,4},{6,7},{7,6},{8,9},{9,8},{10,11... | collective-permute-start | bytes 294920 | tf_op jit(solution)/shard_map/ppermute | solution.py:51
  42.0 8.6 %collective-permute-start.11 = (bf16[256,128]{1,0:T(8,128)(2,1)}, bf16[256,128]{1,0:T(8,128)(2,1)S(1)}, u32[]{:S(2)}, u32[]{:S(2)}) collective-permute-start(bf16[256,128]{1,0:T(8,128)(2,1)} %get-tuple-element.49), channel_id=1, source_target_pairs={{3,4},{7,8},{11,12},{15,16},{19,20},{23,24},{27,28},{4,3},{8,7},{1... | collective-permute-start | bytes 196616 | tf_op jit(solution)/shard_map/ppermute | solution.py:55
  47.8 9.2 %collective-permute-start.12 = (bf16[4,128,128]{2,1,0:T(8,128)(2,1)S(1)}, bf16[4,128,128]{2,1,0:T(8,128)(2,1)S(1)}, u32[]{:S(2)}, u32[]{:S(2)}) collective-permute-start(bf16[4,128,128]{2,1,0:T(8,128)(2,1)S(1)} %pad_maximum_fusion.1), channel_id=1, source_target_pairs={{0,8},{1,9},{2,10},{3,11},{4,12},{5,13},{6,14},{7,15},{8,0},{9,1},... | collective-permute-start | bytes 393224 | tf_op jit(solution)/shard_map/ppermute | solution.py:65
  48.7 8.3 %collective-permute-start.13 = (bf16[4,128,128]{2,1,0:T(8,128)(2,1)S(1)}, bf16[4,128,128]{2,1,0:T(8,128)(2,1)S(1)}, u32[]{:S(2)}, u32[]{:S(2)}) collective-permute-start(bf16[4,128,128]{2,1,0:T(8,128)(2,1)S(1)} %pad_maximum_fusion.1), channel_id=1, source_target_pairs={{0,16},{1,17},{2,18},{3,19},{4,20},{5,21},{6,22},{7,23},{8,24},{9,... | collective-permute-start | bytes 393224 | tf_op jit(solution)/shard_map/ppermute | solution.py:65
  49.1 8.0 %collective-permute-start.14 = (bf16[4,128,128]{2,1,0:T(8,128)(2,1)S(1)}, bf16[4,128,128]{2,1,0:T(8,128)(2,1)S(1)}, u32[]{:S(2)}, u32[]{:S(2)}) collective-permute-start(bf16[4,128,128]{2,1,0:T(8,128)(2,1)S(1)} %pad_maximum_fusion.1), channel_id=1, source_target_pairs={{0,24},{1,25},{2,26},{3,27},{4,28},{5,29},{6,30},{7,31},{8,16},{9,... | collective-permute-start | bytes 393224 | tf_op jit(solution)/shard_map/ppermute | solution.py:65
  57.2 3.7 %collective-permute-start.15 = (bf16[16,128,128]{2,1,0:T(8,128)(2,1)S(1)}, bf16[16,128,128]{2,1,0:T(8,128)(2,1)S(1)}, u32[]{:S(2)}, u32[]{:S(2)}) collective-permute-start(bf16[16,128,128]{2,1,0:T(8,128)(2,1)S(1)} %constant_dynamic-update-slice_fusion.7.rest_0_), channel_id=1, source_target_pairs={{0,4},{1,5},{2,6},{3,7},{4,0},{5,1},{6,2},{7,3},{8,12},{9,13},{10,... | collective-permute-start | bytes 1572872 | tf_op jit(solution)/shard_map/ppermute | solution.py:65
  67.3 7.6 %collective-permute-start.18 = (bf16[384,128]{1,0:T(8,128)(2,1)}, bf16[384,128]{1,0:T(8,128)(2,1)S(1)}, u32[]{:S(2)}, u32[]{:S(2)}) collective-permute-start(bf16[384,128]{1,0:T(8,128)(2,1)} %get-tuple-element.56), channel_id=1, source_target_pairs={{0,3},{1,2},{2,1},{3,0},{4,7},{5,6},{6,5},{7,4},{8,11},{9,10},{10,... | collective-permute-start | bytes 294920 | tf_op jit(solution)/shard_map/ppermute | solution.py:49
  68.3 8.3 %collective-permute-start.17 = (bf16[128,128]{1,0:T(8,128)(2,1)}, bf16[128,128]{1,0:T(8,128)(2,1)S(1)}, u32[]{:S(2)}, u32[]{:S(2)}) collective-permute-start(bf16[128,128]{1,0:T(8,128)(2,1)} %get-tuple-element.54), channel_id=1, source_target_pairs={{0,2},{1,3},{2,0},{3,1},{4,6},{5,7},{6,4},{7,5},{8,10},{9,11},{10,... | collective-permute-start | bytes 98312 | tf_op jit(solution)/shard_map/ppermute | solution.py:50
  68.6 8.0 %collective-permute-start.16 = (bf16[384,128]{1,0:T(8,128)(2,1)}, bf16[384,128]{1,0:T(8,128)(2,1)S(1)}, u32[]{:S(2)}, u32[]{:S(2)}) collective-permute-start(bf16[384,128]{1,0:T(8,128)(2,1)} %get-tuple-element.55), channel_id=1, source_target_pairs={{0,1},{1,0},{2,3},{3,2},{4,5},{5,4},{6,7},{7,6},{8,9},{9,8},{10,11... | collective-permute-start | bytes 294920 | tf_op jit(solution)/shard_map/ppermute | solution.py:51
  71.6 8.5 %collective-permute-start.19 = (bf16[256,128]{1,0:T(8,128)(2,1)}, bf16[256,128]{1,0:T(8,128)(2,1)S(1)}, u32[]{:S(2)}, u32[]{:S(2)}) collective-permute-start(bf16[256,128]{1,0:T(8,128)(2,1)} %get-tuple-element.58), channel_id=1, source_target_pairs={{3,4},{7,8},{11,12},{15,16},{19,20},{23,24},{27,28},{4,3},{8,7},{1... | collective-permute-start | bytes 196616 | tf_op jit(solution)/shard_map/ppermute | solution.py:55
  77.4 9.2 %collective-permute-start.20 = (bf16[4,128,128]{2,1,0:T(8,128)(2,1)S(1)}, bf16[4,128,128]{2,1,0:T(8,128)(2,1)S(1)}, u32[]{:S(2)}, u32[]{:S(2)}) collective-permute-start(bf16[4,128,128]{2,1,0:T(8,128)(2,1)S(1)} %pad_maximum_fusion.2), channel_id=1, source_target_pairs={{0,8},{1,9},{2,10},{3,11},{4,12},{5,13},{6,14},{7,15},{8,0},{9,1},... | collective-permute-start | bytes 393224 | tf_op jit(solution)/shard_map/ppermute | solution.py:65
  77.7 8.9 %collective-permute-start.21 = (bf16[4,128,128]{2,1,0:T(8,128)(2,1)S(1)}, bf16[4,128,128]{2,1,0:T(8,128)(2,1)S(1)}, u32[]{:S(2)}, u32[]{:S(2)}) collective-permute-start(bf16[4,128,128]{2,1,0:T(8,128)(2,1)S(1)} %pad_maximum_fusion.2), channel_id=1, source_target_pairs={{0,16},{1,17},{2,18},{3,19},{4,20},{5,21},{6,22},{7,23},{8,24},{9,... | collective-permute-start | bytes 393224 | tf_op jit(solution)/shard_map/ppermute | solution.py:65
  78.1 8.6 %collective-permute-start.22 = (bf16[4,128,128]{2,1,0:T(8,128)(2,1)S(1)}, bf16[4,128,128]{2,1,0:T(8,128)(2,1)S(1)}, u32[]{:S(2)}, u32[]{:S(2)}) collective-permute-start(bf16[4,128,128]{2,1,0:T(8,128)(2,1)S(1)} %pad_maximum_fusion.2), channel_id=1, source_target_pairs={{0,24},{1,25},{2,26},{3,27},{4,28},{5,29},{6,30},{7,31},{8,16},{9,... | collective-permute-start | bytes 393224 | tf_op jit(solution)/shard_map/ppermute | solution.py:65
  86.8 3.8 %collective-permute-start.23 = (bf16[16,128,128]{2,1,0:T(8,128)(2,1)S(1)}, bf16[16,128,128]{2,1,0:T(8,128)(2,1)S(1)}, u32[]{:S(2)}, u32[]{:S(2)}) collective-permute-start(bf16[16,128,128]{2,1,0:T(8,128)(2,1)S(1)} %constant_dynamic-update-slice_fusion.14.rest_0_), channel_id=1, source_target_pairs={{0,4},{1,5},{2,6},{3,7},{4,0},{5,1},{6,2},{7,3},{8,12},{9,13},{10,... | collective-permute-start | bytes 1572872 | tf_op jit(solution)/shard_map/ppermute | solution.py:65
  (19 other events, 85.3 us)

commit v11 on v10

--- a/solution.py
+++ b/solution.py
@@ -43,7 +43,8 @@
         low = lax.ppermute(current[current.shape[0] - width:], AXES, forward)
         high = lax.ppermute(current[:width], AXES, backward)
         hub_all = lax.all_gather(owned, AXES, axis=0, tiled=True)
-        return middle((low, high)), [hub_all.reshape(-1, block_rows, owned.shape[1])], prep
+        done = (middle((low, high), 0), middle((low, high), 1))
+        return done, [hub_all.reshape(-1, block_rows, owned.shape[1])], prep
     me = lax.axis_index(AXES)
     pairs = lambda m: [(i, i ^ m) for i in range(count)]
     r3 = lax.ppermute(p3, AXES, pairs(3))
@@ -65,19 +66,18 @@
         sent = {m: lax.ppermute(buf, AXES, pairs(m)) for m in sorted(group, key=lambda m: -m)}
         recvs = [sent[m] for m in group]
         if done is None:
-            done, recvs = lax.optimization_barrier((middle((r1, r3, rc)), recvs))
+            done, recvs = lax.optimization_barrier((middle((r1, r3, rc), 0), recvs))
+        else:
+            done, recvs = lax.optimization_barrier(((done, middle((r1, r3, rc), 1)), recvs))
         offs = offs + [o ^ m for m in group for o in offs]
         pieces = [buf] + recvs
         if r + 2 < len(rounds):
             buf = jnp.concatenate(pieces, 0)
-    assert sorted(offs) == list(range(count))
-    where = np.zeros(count, np.int32)
-    for p, o in enumerate(offs):
-        where[o] = p
+    assert sorted(offs) == list(range(count)) and len(rounds) == 3
     return done, pieces, prep
 
 
-def band_kernel(fast, n_own, z_ref, off_ref, cur_hbm, *rest):
+def band_kernel(fast, n_own, b0, z_ref, off_ref, cur_hbm, *rest):
     if fast:
         r1_hbm, r3_hbm, rc_hbm, bt_hbm, out_ref, ext, bt, sem = rest
     else:
@@ -88,7 +88,7 @@
     low_dst = ext.at[pl.ds(0, width)]
     high_dst = ext.at[pl.ds(width + own, width)]
     mid = pltpu.make_async_copy(cur_hbm, ext.at[pl.ds(width, own)], sem.at[1])
-    band_copies = [pltpu.make_async_copy(bt_hbm.at[b], bt.at[b], sem.at[3 + b]) for b in range(blocks)]
+    band_copies = [pltpu.make_async_copy(bt_hbm.at[b0 + b], bt.at[b], sem.at[3 + b]) for b in range(blocks)]
     band_copies[0].start()
     mid.start()
     if fast:
@@ -135,26 +135,28 @@
         band_copies[b].wait()
         acc = jnp.zeros((rows, out_ref.shape[1]), jnp.float32)
         for k in range(k_band):
-            n = b + BW + off_ref[b * k_band + k]
+            n = b0 + b + BW + off_ref[(b0 + b) * k_band + k]
             start = pl.multiple_of(n * rows, rows)
             acc = acc + jnp.dot(bt[b, k], ext[pl.ds(start, rows), :], preferred_element_type=jnp.float32)
         out_ref[pl.ds(b * rows, rows), :] = acc
 
 
-def band_call(z, band_offsets, current, rim_sources, band_tiles, fast, n_own, width):
-    blocks, k_band, rows, _ = band_tiles.shape
+def band_call(z, band_offsets, current, rim_sources, half, band_tiles, fast, n_own, width):
+    all_blocks, k_band, rows, _ = band_tiles.shape
+    first = (all_blocks + 1) // 2
+    b0, blocks = (0, first) if half == 0 else (first, all_blocks - first)
     classes = current.shape[1]
     flops = 2 * blocks * k_band * rows * rows * classes
     bytes_accessed = band_tiles.size * 2 + current.size * 2 * 2 + current.size * 4
     return pl.pallas_call(
-        functools.partial(band_kernel, fast, n_own),
+        functools.partial(band_kernel, fast, n_own, b0),
         cost_estimate=pl.CostEstimate(flops=flops, transcendentals=0, bytes_accessed=bytes_accessed),
         in_specs=[SMEM, SMEM] + [ANY] * (1 + len(rim_sources) + 1),
         out_specs=VMEM,
-        out_shape=jax.ShapeDtypeStruct(current.shape, jnp.float32),
+        out_shape=jax.ShapeDtypeStruct((blocks * rows, classes), jnp.float32),
         scratch_shapes=[
             pltpu.VMEM((current.shape[0] + 2 * width, classes), current.dtype),
-            pltpu.VMEM(band_tiles.shape, band_tiles.dtype),
+            pltpu.VMEM((blocks,) + band_tiles.shape[1:], band_tiles.dtype),
             pltpu.SemaphoreType.DMA((3 + blocks,)),
         ],
     )(z, band_offsets.reshape(-1), current, *rim_sources, band_tiles)
@@ -163,18 +165,23 @@
 def hub_kernel(n_hub, width, final, z_ref, hidx_ref, *rest):
     hub_hbm = rest[:n_hub]
     if final:
-        (ht_hbm, band_hbm, deg_hbm, seeds_hbm, out_ref, hub, ht, band, deg, seeds, sem) = rest[n_hub:]
+        (ht_hbm, band_a, band_b, deg_hbm, seeds_hbm, out_ref, hub, ht, band, deg, seeds, sem) = rest[n_hub:]
     else:
-        (ht_hbm, band_hbm, deg_hbm, seeds_hbm, pick_ref,
+        (ht_hbm, band_a, band_b, deg_hbm, seeds_hbm, pick_ref,
          cur_ref, owned_ref, p1_ref, p3_ref, pc_ref,
          hub, ht, band, deg, seeds, sem) = rest[n_hub:]
     blocks, k_hub, rows = ht.shape[0], ht.shape[1], ht.shape[2]
+    split = band_a.shape[0] // rows
     per_block = []
     for b in range(blocks):
         span = pl.ds(b * rows, rows)
         per_block.append([
             pltpu.make_async_copy(ht_hbm.at[b], ht.at[b], sem.at[n_hub + 4 * b]),
-            pltpu.make_async_copy(band_hbm.at[span], band.at[span], sem.at[n_hub + 4 * b + 1]),
+            pltpu.make_async_copy(
+                band_a.at[span] if b < split else band_b.at[pl.ds((b - split) * rows, rows)],
+                band.at[span],
+                sem.at[n_hub + 4 * b + 1],
+            ),
             pltpu.make_async_copy(deg_hbm.at[span], deg.at[span], sem.at[n_hub + 4 * b + 2]),
             pltpu.make_async_copy(seeds_hbm.at[span], seeds.at[span], sem.at[n_hub + 4 * b + 3]),
         ])
@@ -245,18 +252,18 @@
     return pl.pallas_call(
         functools.partial(hub_kernel, n_hub, width, final),
         cost_estimate=pl.CostEstimate(flops=flops, transcendentals=0, bytes_accessed=bytes_accessed),
-        in_specs=[SMEM, SMEM] + [ANY] * (n_hub + 4) + ([] if final else [VMEM]),
+        in_specs=[SMEM, SMEM] + [ANY] * (n_hub + 5) + ([] if final else [VMEM]),
         out_specs=[VMEM] * len(outs),
         out_shape=outs,
         scratch_shapes=[
             pltpu.VMEM((n_hub_blocks, rows, classes), bf),
             pltpu.VMEM(hub_tiles.shape, hub_tiles.dtype),
-            pltpu.VMEM(seeds.shape, jnp.float32),
+            pltpu.VMEM((seeds.shape[0], classes), jnp.float32),
             pltpu.VMEM(degree.shape, jnp.float32),
             pltpu.VMEM(seeds.shape, seeds.dtype),
             pltpu.SemaphoreType.DMA((n_hub + 4 * blocks,)),
         ],
-    )(z, hub_index.reshape(-1), *hub_pieces, hub_tiles, band, degree, seeds, *([] if final else [pick]))
+    )(z, hub_index.reshape(-1), *hub_pieces, hub_tiles, *band, degree, seeds, *([] if final else [pick]))
 
 
 def positions_of(hub_blocks, owned, block_rows):
@@ -293,7 +300,7 @@
             band_call, z, band_offsets, current, band_tiles=band_tiles, fast=fast, n_own=owned.shape[0], width=width
         )
         band, hub_pieces, prep_out = exchange(
-            current, owned, p1, p3, pc, hub_blocks, width, block_rows, lambda rims: middle(rims), prep
+            current, owned, p1, p3, pc, hub_blocks, width, block_rows, lambda rims, half: middle(rims, half), prep
         )
         if prep is not None:
             pick, degree, hub_index = prep_out

time: 97.7 us -> 110 us (1.13)
  Pallas kernels: 31.5 us -> 38.4 us
  waiting for transfers between devices: 6.41 us -> 10.9 us
    ppermute x3, waiting for transfers between devices: 0.01 us -> 8.43 us  [exchange(): r3 = lax.ppermute(p3, AXES, pairs(3))]
    pallas_call x3 -> x6, Pallas kernels: 15.3 us -> 22.2 us  [band_call(): pl.pallas_call(functools.partial(band_kernel, fast, n_own, b0), cost_esti...]
    ppermute x3, starting transfers between devices: 7.07 us -> 2.31 us  [exchange(): r1 = lax.ppermute(p1, AXES, pairs(1))]
    ppermute x3, starting transfers between devices: 1.22 us -> 5.81 us  [exchange(): r3 = lax.ppermute(p3, AXES, pairs(3))]
    ppermute x3, waiting for transfers between devices: 2.92 us -> 0.49 us  [exchange(): r1 = lax.ppermute(p1, AXES, pairs(1))]
    ppermute x12, waiting for transfers between devices: 3.47 us -> 2 us  [exchange(): lax.ppermute(buf, AXES, pairs(m))]
  transfers between devices with their start and end apart: 24 -> 24, of which waited for: 5 -> 4; matrix products, arithmetic and copies ran while one was open for 13% -> 12% of each run, Pallas kernels for 16% -> 20%
where the time goes in v11:
time: 110 us; the launch traced here: 109 us
  Pallas kernels  38.4 us (35%)
  starting transfers between devices  38.1 us (35%)
  local copies, waits for them, and re-layouts  11.7 us (11%)
  waiting for transfers between devices  10.9 us (10%)
  other arithmetic  8.88 us (8%)
    pallas_call x6, Pallas kernels, band_call(): pl.pallas_call(functools.partial(band_kernel, fast, n_own, b0), cost_esti...  22.2 us
    pallas_call x3, Pallas kernels, hub_call(): pl.pallas_call(functools.partial(hub_kernel, n_hub, width, final), cost_e...  16.2 us
    ppermute x12, starting transfers between devices, exchange(): lax.ppermute(buf, AXES, pairs(m))  14.2 us
    ppermute x3, starting transfers between devices, exchange(): rc = lax.ppermute(pc, AXES, cross)  13.3 us
    ppermute x3, waiting for transfers between devices, exchange(): r3 = lax.ppermute(p3, AXES, pairs(3))  8.43 us
    unnamed x56, local copies, waits for them, and re-layouts  7.69 us
    ppermute x3, starting transfers between devices, exchange(): r3 = lax.ppermute(p3, AXES, pairs(3))  5.81 us
    ppermute x3, starting transfers between devices, exchange(): r2 = lax.ppermute(owned, AXES, pairs(2))  2.51 us
  transfers between devices with their start and end apart: 24, of which 4 were waited for; matrix products, arithmetic and copies ran while one was open for 12% of the time, Pallas kernels for 20%

profile of v11, /device:TPU:5, one launch (start us, length us, event | category | flops | bytes accessed | tf_op | source)
XLA Modules:
  0.0 108.5 jit_solution(6574964604493186965)
XLA Ops:
  4.1 2.4 %collective-permute-start.1 = (bf16[128,128]{1,0:T(8,128)(2,1)S(1)}, bf16[128,128]{1,0:T(8,128)(2,1)S(1)}, u32[]{:S(2)}, u32[]{:S(2)}) collective-permute-start(bf16[128,128]{1,0:T(8,128)(2,1)S(1)} %gather_fusion), channel_id=1, source_target_pairs={{0,2},{1,3},{2,0},{3,1},{4,6},{5,7},{6,4},{7,5},{8,10},{9,11},{10,... | collective-permute-start | bytes 98312 | tf_op jit(solution)/shard_map/ppermute | solution.py:51
  6.5 3.8 %collective-permute-start.3 = (bf16[256,128]{1,0:T(8,128)(2,1)S(1)}, bf16[256,128]{1,0:T(8,128)(2,1)S(1)}, u32[]{:S(2)}, u32[]{:S(2)}) collective-permute-start(bf16[256,128]{1,0:T(8,128)(2,1)S(1)} %get-tuple-element.81), channel_id=1, source_target_pairs={{3,4},{7,8},{11,12},{15,16},{19,20},{23,24},{27,28},{4,3},{8,7},{1... | collective-permute-start | bytes 196616 | tf_op jit(solution)/shard_map/ppermute | solution.py:56
  10.4 3.2 %collective-permute-start.2 = (bf16[384,128]{1,0:T(8,128)(2,1)S(1)}, bf16[384,128]{1,0:T(8,128)(2,1)S(1)}, u32[]{:S(2)}, u32[]{:S(2)}) collective-permute-start(bf16[384,128]{1,0:T(8,128)(2,1)S(1)} %get-tuple-element.84), channel_id=1, source_target_pairs={{0,3},{1,2},{2,1},{3,0},{4,7},{5,6},{6,5},{7,4},{8,11},{9,10},{10,... | collective-permute-start | bytes 294920 | tf_op jit(solution)/shard_map/ppermute | solution.py:50
  15.0 2.2 %convert_reduce_fusion = f32[8,128]{1,0:T(8,128)S(1)} fusion(bf16[8,10,128,128]{3,2,1,0:T(8,128)(2,1)} %rest_3_.11), kind=kLoop, calls=%fused_computation.2 | loop fusion | flops 2620416 | bytes 2625536 | tf_op jit(solution)/shard_map/reduce_sum | solution.py:285
  22.3 3.7 %shard_map.82.rest_3_ = f32[512,128]{1,0:T(8,128)} custom-call(s32[1]{0:T(128)} %bitcast.z_ref, s32[80]{0:T(128)} %reshape.39.off_ref, bf16[1024,128]{1,0:T(8,128)(2,1)} %copy-done.2, bf16[384,128]{1,0:T(8,128)(2,1)} %copy-done.8, bf16[384,128]{1,0:T(8,128)(2,1)} %copy-done.7, bf16[256,128]{1,0:T(8,128)(2,1)} %copy-done.15, bf16[8,10,128,128]{3,2,1,0:T(8,128)(2,1)} %rest_3_.11), custom_call_target="tpu_custom_call" | custom-call | flops 167772160 | bytes 3670016 | tf_op jit(solution)/shard_map/pallas_call | solution.py:151
  26.8 1.9 %collective-permute-done.5 = bf16[4,128,128]{2,1,0:T(8,128)(2,1)S(1)} collective-permute-done((bf16[4,128,128]{2,1,0:T(8,128)(2,1)S(1)}, bf16[4,128,128]{2,1,0:T(8,128)(2,1)S(1)}, u32[]{:S(2)}, u32[]{:S(2)}) %collective-permute-start.5) | collective-permute-done | bytes 131104 | tf_op jit(solution)/shard_map/ppermute | solution.py:66
  31.0 3.7 %shard_map.83.rest_4_ = f32[512,128]{1,0:T(8,128)} custom-call(s32[1]{0:T(128)} %bitcast.z_ref, s32[80]{0:T(128)} %reshape.39.off_ref, bf16[1024,128]{1,0:T(8,128)(2,1)} %copy-done.2, bf16[384,128]{1,0:T(8,128)(2,1)} %copy-done.8, bf16[384,128]{1,0:T(8,128)(2,1)} %copy-done.7, bf16[256,128]{1,0:T(8,128)(2,1)} %copy-done.15, bf16[8,10,128,128]{3,2,1,0:T(8,128)(2,1)} %rest_3_.11), custom_call_target="tpu_custom_call" | custom-call | flops 167772160 | bytes 3670016 | tf_op jit(solution)/shard_map/pallas_call | solution.py:151
  35.6 5.5 %shard_map.84 = (bf16[1024,128]{1,0:T(8,128)(2,1)}, bf16[128,128]{1,0:T(8,128)(2,1)}, bf16[384,128]{1,0:T(8,128)(2,1)}, bf16[384,128]{1,0:T(8,128)(2,1)}, bf16[256,128]{1,0:T(8,128)(2,1)}) custom-call(s32[1]{0:T(128)} %bitcast.z_ref, s32[48]{0:T(128)} %reshape.38.hidx_ref, bf16[16,128,128]{2,1,0:T(8,128)(2,1)} %copy-done.9, ...), custom_call_target="tpu_custom_call" | custom-call | flops 201326592 | bytes 4718592 | tf_op jit(solution)/shard_map/pallas_call | solution.py:252
  42.7 5.2 %collective-permute-start.11 = (bf16[256,128]{1,0:T(8,128)(2,1)}, bf16[256,128]{1,0:T(8,128)(2,1)S(1)}, u32[]{:S(2)}, u32[]{:S(2)}) collective-permute-start(bf16[256,128]{1,0:T(8,128)(2,1)} %get-tuple-element.61), channel_id=1, source_target_pairs={{3,4},{7,8},{11,12},{15,16},{19,20},{23,24},{27,28},{4,3},{8,7},{1... | collective-permute-start | bytes 196616 | tf_op jit(solution)/shard_map/ppermute | solution.py:56
  48.8 4.6 %collective-permute-done.10.rest_1_ = bf16[384,128]{1,0:T(8,128)(2,1)S(1)} collective-permute-done((bf16[384,128]{1,0:T(8,128)(2,1)}, bf16[384,128]{1,0:T(8,128)(2,1)S(1)}, u32[]{:S(2)}, u32[]{:S(2)}) %collective-permute-start.10) | collective-permute-done | bytes 98336 | tf_op jit(solution)/shard_map/ppermute | solution.py:50
  54.3 2.2 %collective-permute-start.14 = (bf16[4,128,128]{2,1,0:T(8,128)(2,1)S(1)}, bf16[4,128,128]{2,1,0:T(8,128)(2,1)S(1)}, u32[]{:S(2)}, u32[]{:S(2)}) collective-permute-start(bf16[4,128,128]{2,1,0:T(8,128)(2,1)S(1)} %pad_maximum_fusion.1), channel_id=1, source_target_pairs={{0,24},{1,25},{2,26},{3,27},{4,28},{5,29},{6,30},{7,31},{8,16},{9,... | collective-permute-start | bytes 393224 | tf_op jit(solution)/shard_map/ppermute | solution.py:66
  57.6 3.7 %shard_map.85.rest_3_ = f32[512,128]{1,0:T(8,128)} custom-call(s32[1]{0:T(128)} %bitcast.z_ref, s32[80]{0:T(128)} %reshape.39.off_ref, bf16[1024,128]{1,0:T(8,128)(2,1)} %get-tuple-element.60.cur_hbm, bf16[384,128]{1,0:T(8,128)(2,1)} %copy-done.4, bf16[384,128]{1,0:T(8,128)(2,1)} %copy-done.6, bf16[256,128]{1,0:T(8,128)(2,1)} %copy-done.17, ...), custom_call_target="tpu_custom_call" | custom-call | flops 167772160 | bytes 3670016 | tf_op jit(solution)/shard_map/pallas_call | solution.py:151
  62.2 2.9 %collective-permute-start.15 = (bf16[16,128,128]{2,1,0:T(8,128)(2,1)S(1)}, bf16[16,128,128]{2,1,0:T(8,128)(2,1)S(1)}, u32[]{:S(2)}, u32[]{:S(2)}) collective-permute-start(bf16[16,128,128]{2,1,0:T(8,128)(2,1)S(1)} %constant_dynamic-update-slice_fusion.7.rest_0_), channel_id=1, source_target_pairs={{0,4},{1,5},{2,6},{3,7},{4,0},{5,1},{6,2},{7,3},{8,12},{9,13},{10,... | collective-permute-start | bytes 1572872 | tf_op jit(solution)/shard_map/ppermute | solution.py:66
  65.1 3.7 %shard_map.86.rest_4_ = f32[512,128]{1,0:T(8,128)} custom-call(s32[1]{0:T(128)} %bitcast.z_ref, s32[80]{0:T(128)} %reshape.39.off_ref, bf16[1024,128]{1,0:T(8,128)(2,1)} %get-tuple-element.60.cur_hbm, bf16[384,128]{1,0:T(8,128)(2,1)} %copy-done.4, bf16[384,128]{1,0:T(8,128)(2,1)} %copy-done.6, bf16[256,128]{1,0:T(8,128)(2,1)} %copy-done.17, ...), custom_call_target="tpu_custom_call" | custom-call | flops 167772160 | bytes 3670016 | tf_op jit(solution)/shard_map/pallas_call | solution.py:151
  69.7 5.5 %shard_map.87 = (bf16[1024,128]{1,0:T(8,128)(2,1)}, bf16[128,128]{1,0:T(8,128)(2,1)}, bf16[384,128]{1,0:T(8,128)(2,1)}, bf16[384,128]{1,0:T(8,128)(2,1)}, bf16[256,128]{1,0:T(8,128)(2,1)}) custom-call(s32[1]{0:T(128)} %bitcast.z_ref, s32[48]{0:T(128)} %reshape.38.hidx_ref, bf16[16,128,128]{2,1,0:T(8,128)(2,1)} %copy-done.10, ...), custom_call_target="tpu_custom_call" | custom-call | flops 201326592 | bytes 4718592 | tf_op jit(solution)/shard_map/pallas_call | solution.py:252
  75.3 1.6 %collective-permute-start.16 = (bf16[384,128]{1,0:T(8,128)(2,1)}, bf16[384,128]{1,0:T(8,128)(2,1)S(1)}, u32[]{:S(2)}, u32[]{:S(2)}) collective-permute-start(bf16[384,128]{1,0:T(8,128)(2,1)} %get-tuple-element.70), channel_id=1, source_target_pairs={{0,1},{1,0},{2,3},{3,2},{4,5},{5,4},{6,7},{7,6},{8,9},{9,8},{10,11... | collective-permute-start | bytes 294920 | tf_op jit(solution)/shard_map/ppermute | solution.py:52
  77.6 4.3 %collective-permute-start.19 = (bf16[256,128]{1,0:T(8,128)(2,1)}, bf16[256,128]{1,0:T(8,128)(2,1)S(1)}, u32[]{:S(2)}, u32[]{:S(2)}) collective-permute-start(bf16[256,128]{1,0:T(8,128)(2,1)} %get-tuple-element.73), channel_id=1, source_target_pairs={{3,4},{7,8},{11,12},{15,16},{19,20},{23,24},{27,28},{4,3},{8,7},{1... | collective-permute-start | bytes 196616 | tf_op jit(solution)/shard_map/ppermute | solution.py:56
  81.9 1.7 %collective-permute-start.18 = (bf16[384,128]{1,0:T(8,128)(2,1)}, bf16[384,128]{1,0:T(8,128)(2,1)S(1)}, u32[]{:S(2)}, u32[]{:S(2)}) collective-permute-start(bf16[384,128]{1,0:T(8,128)(2,1)} %get-tuple-element.71), channel_id=1, source_target_pairs={{0,3},{1,2},{2,1},{3,0},{4,7},{5,6},{6,5},{7,4},{8,11},{9,10},{10,... | collective-permute-start | bytes 294920 | tf_op jit(solution)/shard_map/ppermute | solution.py:50
  83.7 3.8 %collective-permute-done.18.rest_1_ = bf16[384,128]{1,0:T(8,128)(2,1)S(1)} collective-permute-done((bf16[384,128]{1,0:T(8,128)(2,1)}, bf16[384,128]{1,0:T(8,128)(2,1)S(1)}, u32[]{:S(2)}, u32[]{:S(2)}) %collective-permute-start.18) | collective-permute-done | bytes 98336 | tf_op jit(solution)/shard_map/ppermute | solution.py:50
  88.3 1.7 %collective-permute-start.22 = (bf16[4,128,128]{2,1,0:T(8,128)(2,1)S(1)}, bf16[4,128,128]{2,1,0:T(8,128)(2,1)S(1)}, u32[]{:S(2)}, u32[]{:S(2)}) collective-permute-start(bf16[4,128,128]{2,1,0:T(8,128)(2,1)S(1)} %pad_maximum_fusion.2), channel_id=1, source_target_pairs={{0,24},{1,25},{2,26},{3,27},{4,28},{5,29},{6,30},{7,31},{8,16},{9,... | collective-permute-start | bytes 393224 | tf_op jit(solution)/shard_map/ppermute | solution.py:66
  91.6 3.7 %shard_map.88.rest_3_ = f32[512,128]{1,0:T(8,128)} custom-call(s32[1]{0:T(128)} %bitcast.z_ref, s32[80]{0:T(128)} %reshape.39.off_ref, bf16[1024,128]{1,0:T(8,128)(2,1)} %get-tuple-element.72.cur_hbm, bf16[384,128]{1,0:T(8,128)(2,1)} %copy-done.3, bf16[384,128]{1,0:T(8,128)(2,1)} %copy-done.5, bf16[256,128]{1,0:T(8,128)(2,1)} %copy-done.16, ...), custom_call_target="tpu_custom_call" | custom-call | flops 167772160 | bytes 3670016 | tf_op jit(solution)/shard_map/pallas_call | solution.py:151
  96.3 2.6 %collective-permute-start.23 = (bf16[16,128,128]{2,1,0:T(8,128)(2,1)S(1)}, bf16[16,128,128]{2,1,0:T(8,128)(2,1)S(1)}, u32[]{:S(2)}, u32[]{:S(2)}) collective-permute-start(bf16[16,128,128]{2,1,0:T(8,128)(2,1)S(1)} %constant_dynamic-update-slice_fusion.14.rest_0_), channel_id=1, source_target_pairs={{0,4},{1,5},{2,6},{3,7},{4,0},{5,1},{6,2},{7,3},{8,12},{9,13},{10,... | collective-permute-start | bytes 1572872 | tf_op jit(solution)/shard_map/ppermute | solution.py:66
  98.9 3.7 %shard_map.89.rest_4_ = f32[512,128]{1,0:T(8,128)} custom-call(s32[1]{0:T(128)} %bitcast.z_ref, s32[80]{0:T(128)} %reshape.39.off_ref, bf16[1024,128]{1,0:T(8,128)(2,1)} %get-tuple-element.72.cur_hbm, bf16[384,128]{1,0:T(8,128)(2,1)} %copy-done.3, bf16[384,128]{1,0:T(8,128)(2,1)} %copy-done.5, bf16[256,128]{1,0:T(8,128)(2,1)} %copy-done.16, ...), custom_call_target="tpu_custom_call" | custom-call | flops 167772160 | bytes 3670016 | tf_op jit(solution)/shard_map/pallas_call | solution.py:151
  103.4 5.1 %shard_map.90 = f32[1024,128]{1,0:T(8,128)} custom-call(s32[1]{0:T(128)} %bitcast.z_ref, s32[48]{0:T(128)} %reshape.38.hidx_ref, bf16[16,128,128]{2,1,0:T(8,128)(2,1)} %copy-done.11, bf16[16,128,128]{2,1,0:T(8,128)(2,1)} %copy-done.14, bf16[8,6,128,128]{3,2,1,0:T(8,128)(2,1)} %rest_2_.5, f32[512,128]{1,0:T(8,128)} %shard_map.88.rest_3_, ...), custom_call_target="tpu_custom_call" | custom-call | flops 201326592 | bytes 4718592 | tf_op jit(solution)/shard_map/pallas_call | solution.py:252
  (119 shorter events, 25.5 us)
Async XLA Ops:
  4.1 14.9 %collective-permute-start.1 = (bf16[128,128]{1,0:T(8,128)(2,1)S(1)}, bf16[128,128]{1,0:T(8,128)(2,1)S(1)}, u32[]{:S(2)}, u32[]{:S(2)}) collective-permute-start(bf16[128,128]{1,0:T(8,128)(2,1)S(1)} %gather_fusion), channel_id=1, source_target_pairs={{0,2},{1,3},{2,0},{3,1},{4,6},{5,7},{6,4},{7,5},{8,10},{9,11},{10,... | collective-permute-start | bytes 98312 | tf_op jit(solution)/shard_map/ppermute | solution.py:51
  6.5 12.5 %collective-permute-start.3 = (bf16[256,128]{1,0:T(8,128)(2,1)S(1)}, bf16[256,128]{1,0:T(8,128)(2,1)S(1)}, u32[]{:S(2)}, u32[]{:S(2)}) collective-permute-start(bf16[256,128]{1,0:T(8,128)(2,1)S(1)} %get-tuple-element.81), channel_id=1, source_target_pairs={{3,4},{7,8},{11,12},{15,16},{19,20},{23,24},{27,28},{4,3},{8,7},{1... | collective-permute-start | bytes 196616 | tf_op jit(solution)/shard_map/ppermute | solution.py:56
  10.4 8.7 %collective-permute-start.2 = (bf16[384,128]{1,0:T(8,128)(2,1)S(1)}, bf16[384,128]{1,0:T(8,128)(2,1)S(1)}, u32[]{:S(2)}, u32[]{:S(2)}) collective-permute-start(bf16[384,128]{1,0:T(8,128)(2,1)S(1)} %get-tuple-element.84), channel_id=1, source_target_pairs={{0,3},{1,2},{2,1},{3,0},{4,7},{5,6},{6,5},{7,4},{8,11},{9,10},{10,... | collective-permute-start | bytes 294920 | tf_op jit(solution)/shard_map/ppermute | solution.py:50
  13.6 6.0 %collective-permute-start = (bf16[384,128]{1,0:T(8,128)(2,1)S(1)}, bf16[384,128]{1,0:T(8,128)(2,1)S(1)}, u32[]{:S(2)}, u32[]{:S(2)}) collective-permute-start(bf16[384,128]{1,0:T(8,128)(2,1)S(1)} %get-tuple-element.85), channel_id=1, source_target_pairs={{0,1},{1,0},{2,3},{3,2},{4,5},{5,4},{6,7},{7,6},{8,9},{9,8},{10,11... | collective-permute-start | bytes 294920 | tf_op jit(solution)/shard_map/ppermute | solution.py:52
  19.6 7.3 %collective-permute-start.6 = (bf16[4,128,128]{2,1,0:T(8,128)(2,1)S(1)}, bf16[4,128,128]{2,1,0:T(8,128)(2,1)S(1)}, u32[]{:S(2)}, u32[]{:S(2)}) collective-permute-start(bf16[4,128,128]{2,1,0:T(8,128)(2,1)S(1)} %pad_maximum_fusion), channel_id=1, source_target_pairs={{0,24},{1,25},{2,26},{3,27},{4,28},{5,29},{6,30},{7,31},{8,16},{9,... | collective-permute-start | bytes 393224 | tf_op jit(solution)/shard_map/ppermute | solution.py:66
  20.8 8.0 %collective-permute-start.5 = (bf16[4,128,128]{2,1,0:T(8,128)(2,1)S(1)}, bf16[4,128,128]{2,1,0:T(8,128)(2,1)S(1)}, u32[]{:S(2)}, u32[]{:S(2)}) collective-permute-start(bf16[4,128,128]{2,1,0:T(8,128)(2,1)S(1)} %pad_maximum_fusion), channel_id=1, source_target_pairs={{0,16},{1,17},{2,18},{3,19},{4,20},{5,21},{6,22},{7,23},{8,24},{9,... | collective-permute-start | bytes 393224 | tf_op jit(solution)/shard_map/ppermute | solution.py:66
  20.8 8.0 %collective-permute-start.4 = (bf16[4,128,128]{2,1,0:T(8,128)(2,1)S(1)}, bf16[4,128,128]{2,1,0:T(8,128)(2,1)S(1)}, u32[]{:S(2)}, u32[]{:S(2)}) collective-permute-start(bf16[4,128,128]{2,1,0:T(8,128)(2,1)S(1)} %pad_maximum_fusion), channel_id=1, source_target_pairs={{0,8},{1,9},{2,10},{3,11},{4,12},{5,13},{6,14},{7,15},{8,0},{9,1},... | collective-permute-start | bytes 393224 | tf_op jit(solution)/shard_map/ppermute | solution.py:66
  28.9 5.9 %collective-permute-start.7 = (bf16[16,128,128]{2,1,0:T(8,128)(2,1)S(1)}, bf16[16,128,128]{2,1,0:T(8,128)(2,1)S(1)}, u32[]{:S(2)}, u32[]{:S(2)}) collective-permute-start(bf16[16,128,128]{2,1,0:T(8,128)(2,1)S(1)} %constant_dynamic-update-slice_fusion.rest_0_), channel_id=1, source_target_pairs={{0,4},{1,5},{2,6},{3,7},{4,0},{5,1},{6,2},{7,3},{8,12},{9,13},{10,... | collective-permute-start | bytes 1572872 | tf_op jit(solution)/shard_map/ppermute | solution.py:66
  41.2 12.3 %collective-permute-start.9 = (bf16[128,128]{1,0:T(8,128)(2,1)}, bf16[128,128]{1,0:T(8,128)(2,1)S(1)}, u32[]{:S(2)}, u32[]{:S(2)}) collective-permute-start(bf16[128,128]{1,0:T(8,128)(2,1)} %get-tuple-element.57), channel_id=1, source_target_pairs={{0,2},{1,3},{2,0},{3,1},{4,6},{5,7},{6,4},{7,5},{8,10},{9,11},{10,... | collective-permute-start | bytes 98312 | tf_op jit(solution)/shard_map/ppermute | solution.py:51
  41.2 7.6 %collective-permute-start.8 = (bf16[384,128]{1,0:T(8,128)(2,1)}, bf16[384,128]{1,0:T(8,128)(2,1)S(1)}, u32[]{:S(2)}, u32[]{:S(2)}) collective-permute-start(bf16[384,128]{1,0:T(8,128)(2,1)} %get-tuple-element.58), channel_id=1, source_target_pairs={{0,1},{1,0},{2,3},{3,2},{4,5},{5,4},{6,7},{7,6},{8,9},{9,8},{10,11... | collective-permute-start | bytes 294920 | tf_op jit(solution)/shard_map/ppermute | solution.py:52
  42.7 14.3 %collective-permute-start.11 = (bf16[256,128]{1,0:T(8,128)(2,1)}, bf16[256,128]{1,0:T(8,128)(2,1)S(1)}, u32[]{:S(2)}, u32[]{:S(2)}) collective-permute-start(bf16[256,128]{1,0:T(8,128)(2,1)} %get-tuple-element.61), channel_id=1, source_target_pairs={{3,4},{7,8},{11,12},{15,16},{19,20},{23,24},{27,28},{4,3},{8,7},{1... | collective-permute-start | bytes 196616 | tf_op jit(solution)/shard_map/ppermute | solution.py:56
  47.9 5.5 %collective-permute-start.10 = (bf16[384,128]{1,0:T(8,128)(2,1)}, bf16[384,128]{1,0:T(8,128)(2,1)S(1)}, u32[]{:S(2)}, u32[]{:S(2)}) collective-permute-start(bf16[384,128]{1,0:T(8,128)(2,1)} %get-tuple-element.59), channel_id=1, source_target_pairs={{0,3},{1,2},{2,1},{3,0},{4,7},{5,6},{6,5},{7,4},{8,11},{9,10},{10,... | collective-permute-start | bytes 294920 | tf_op jit(solution)/shard_map/ppermute | solution.py:50
  54.3 7.8 %collective-permute-start.14 = (bf16[4,128,128]{2,1,0:T(8,128)(2,1)S(1)}, bf16[4,128,128]{2,1,0:T(8,128)(2,1)S(1)}, u32[]{:S(2)}, u32[]{:S(2)}) collective-permute-start(bf16[4,128,128]{2,1,0:T(8,128)(2,1)S(1)} %pad_maximum_fusion.1), channel_id=1, source_target_pairs={{0,24},{1,25},{2,26},{3,27},{4,28},{5,29},{6,30},{7,31},{8,16},{9,... | collective-permute-start | bytes 393224 | tf_op jit(solution)/shard_map/ppermute | solution.py:66
  56.5 5.6 %collective-permute-start.13 = (bf16[4,128,128]{2,1,0:T(8,128)(2,1)S(1)}, bf16[4,128,128]{2,1,0:T(8,128)(2,1)S(1)}, u32[]{:S(2)}, u32[]{:S(2)}) collective-permute-start(bf16[4,128,128]{2,1,0:T(8,128)(2,1)S(1)} %pad_maximum_fusion.1), channel_id=1, source_target_pairs={{0,16},{1,17},{2,18},{3,19},{4,20},{5,21},{6,22},{7,23},{8,24},{9,... | collective-permute-start | bytes 393224 | tf_op jit(solution)/shard_map/ppermute | solution.py:66
  56.5 5.6 %collective-permute-start.12 = (bf16[4,128,128]{2,1,0:T(8,128)(2,1)S(1)}, bf16[4,128,128]{2,1,0:T(8,128)(2,1)S(1)}, u32[]{:S(2)}, u32[]{:S(2)}) collective-permute-start(bf16[4,128,128]{2,1,0:T(8,128)(2,1)S(1)} %pad_maximum_fusion.1), channel_id=1, source_target_pairs={{0,8},{1,9},{2,10},{3,11},{4,12},{5,13},{6,14},{7,15},{8,0},{9,1},... | collective-permute-start | bytes 393224 | tf_op jit(solution)/shard_map/ppermute | solution.py:66
  62.2 6.6 %collective-permute-start.15 = (bf16[16,128,128]{2,1,0:T(8,128)(2,1)S(1)}, bf16[16,128,128]{2,1,0:T(8,128)(2,1)S(1)}, u32[]{:S(2)}, u32[]{:S(2)}) collective-permute-start(bf16[16,128,128]{2,1,0:T(8,128)(2,1)S(1)} %constant_dynamic-update-slice_fusion.7.rest_0_), channel_id=1, source_target_pairs={{0,4},{1,5},{2,6},{3,7},{4,0},{5,1},{6,2},{7,3},{8,12},{9,13},{10,... | collective-permute-start | bytes 1572872 | tf_op jit(solution)/shard_map/ppermute | solution.py:66
  75.2 12.3 %collective-permute-start.17 = (bf16[128,128]{1,0:T(8,128)(2,1)}, bf16[128,128]{1,0:T(8,128)(2,1)S(1)}, u32[]{:S(2)}, u32[]{:S(2)}) collective-permute-start(bf16[128,128]{1,0:T(8,128)(2,1)} %get-tuple-element.69), channel_id=1, source_target_pairs={{0,2},{1,3},{2,0},{3,1},{4,6},{5,7},{6,4},{7,5},{8,10},{9,11},{10,... | collective-permute-start | bytes 98312 | tf_op jit(solution)/shard_map/ppermute | solution.py:51
  75.3 8.4 %collective-permute-start.16 = (bf16[384,128]{1,0:T(8,128)(2,1)}, bf16[384,128]{1,0:T(8,128)(2,1)S(1)}, u32[]{:S(2)}, u32[]{:S(2)}) collective-permute-start(bf16[384,128]{1,0:T(8,128)(2,1)} %get-tuple-element.70), channel_id=1, source_target_pairs={{0,1},{1,0},{2,3},{3,2},{4,5},{5,4},{6,7},{7,6},{8,9},{9,8},{10,11... | collective-permute-start | bytes 294920 | tf_op jit(solution)/shard_map/ppermute | solution.py:52
  77.6 13.4 %collective-permute-start.19 = (bf16[256,128]{1,0:T(8,128)(2,1)}, bf16[256,128]{1,0:T(8,128)(2,1)S(1)}, u32[]{:S(2)}, u32[]{:S(2)}) collective-permute-start(bf16[256,128]{1,0:T(8,128)(2,1)} %get-tuple-element.73), channel_id=1, source_target_pairs={{3,4},{7,8},{11,12},{15,16},{19,20},{23,24},{27,28},{4,3},{8,7},{1... | collective-permute-start | bytes 196616 | tf_op jit(solution)/shard_map/ppermute | solution.py:56
  81.9 5.5 %collective-permute-start.18 = (bf16[384,128]{1,0:T(8,128)(2,1)}, bf16[384,128]{1,0:T(8,128)(2,1)S(1)}, u32[]{:S(2)}, u32[]{:S(2)}) collective-permute-start(bf16[384,128]{1,0:T(8,128)(2,1)} %get-tuple-element.71), channel_id=1, source_target_pairs={{0,3},{1,2},{2,1},{3,0},{4,7},{5,6},{6,5},{7,4},{8,11},{9,10},{10,... | collective-permute-start | bytes 294920 | tf_op jit(solution)/shard_map/ppermute | solution.py:50
  88.3 7.8 %collective-permute-start.22 = (bf16[4,128,128]{2,1,0:T(8,128)(2,1)S(1)}, bf16[4,128,128]{2,1,0:T(8,128)(2,1)S(1)}, u32[]{:S(2)}, u32[]{:S(2)}) collective-permute-start(bf16[4,128,128]{2,1,0:T(8,128)(2,1)S(1)} %pad_maximum_fusion.2), channel_id=1, source_target_pairs={{0,24},{1,25},{2,26},{3,27},{4,28},{5,29},{6,30},{7,31},{8,16},{9,... | collective-permute-start | bytes 393224 | tf_op jit(solution)/shard_map/ppermute | solution.py:66
  90.0 6.1 %collective-permute-start.21 = (bf16[4,128,128]{2,1,0:T(8,128)(2,1)S(1)}, bf16[4,128,128]{2,1,0:T(8,128)(2,1)S(1)}, u32[]{:S(2)}, u32[]{:S(2)}) collective-permute-start(bf16[4,128,128]{2,1,0:T(8,128)(2,1)S(1)} %pad_maximum_fusion.2), channel_id=1, source_target_pairs={{0,16},{1,17},{2,18},{3,19},{4,20},{5,21},{6,22},{7,23},{8,24},{9,... | collective-permute-start | bytes 393224 | tf_op jit(solution)/shard_map/ppermute | solution.py:66
  90.0 6.2 %collective-permute-start.20 = (bf16[4,128,128]{2,1,0:T(8,128)(2,1)S(1)}, bf16[4,128,128]{2,1,0:T(8,128)(2,1)S(1)}, u32[]{:S(2)}, u32[]{:S(2)}) collective-permute-start(bf16[4,128,128]{2,1,0:T(8,128)(2,1)S(1)} %pad_maximum_fusion.2), channel_id=1, source_target_pairs={{0,8},{1,9},{2,10},{3,11},{4,12},{5,13},{6,14},{7,15},{8,0},{9,1},... | collective-permute-start | bytes 393224 | tf_op jit(solution)/shard_map/ppermute | solution.py:66
  96.3 6.3 %collective-permute-start.23 = (bf16[16,128,128]{2,1,0:T(8,128)(2,1)S(1)}, bf16[16,128,128]{2,1,0:T(8,128)(2,1)S(1)}, u32[]{:S(2)}, u32[]{:S(2)}) collective-permute-start(bf16[16,128,128]{2,1,0:T(8,128)(2,1)S(1)} %constant_dynamic-update-slice_fusion.14.rest_0_), channel_id=1, source_target_pairs={{0,4},{1,5},{2,6},{3,7},{4,0},{5,1},{6,2},{7,3},{8,12},{9,13},{10,... | collective-permute-start | bytes 1572872 | tf_op jit(solution)/shard_map/ppermute | solution.py:66
  (19 other events, 108.6 us)

commit v12 on v10

--- a/solution.py
+++ b/solution.py
@@ -256,7 +256,7 @@
             pltpu.VMEM(seeds.shape, seeds.dtype),
             pltpu.SemaphoreType.DMA((n_hub + 4 * blocks,)),
         ],
-    )(z, hub_index.reshape(-1), *hub_pieces, hub_tiles, band, degree, seeds, *([] if final else [pick]))
+    )(z, hub_index, *hub_pieces, hub_tiles, band, degree, seeds, *([] if final else [pick]))
 
 
 def positions_of(hub_blocks, owned, block_rows):
@@ -278,7 +278,7 @@
     degree = jnp.sum(band_tiles, axis=(1, 3), dtype=jnp.float32) + jnp.sum(
         hub_tiles, axis=(1, 3), dtype=jnp.float32
     )
-    degree = degree.reshape(-1, 1)
+    degree = jnp.broadcast_to(degree.reshape(-1, 1), seeds.shape)
     width = BW * block_rows
     z = lax.axis_index("hub").astype(jnp.int32).reshape(1)
     current = seeds.astype(jnp.bfloat16)
@@ -287,7 +287,7 @@
     p1, p3, pc = payloads(current, owned, z[0], width)
     fast = fast_path(owned, block_rows)
     pick = (hub_rows[:, None] == jnp.arange(current.shape[0], dtype=hub_rows.dtype)[None, :]).astype(jnp.bfloat16)
-    prep = (pick, degree, positions_of(hub_blocks, owned, block_rows))
+    prep = (pick, degree, positions_of(hub_blocks, owned, block_rows).reshape(-1))
     for step in range(ITERS):
         middle = functools.partial(
             band_call, z, band_offsets, current, band_tiles=band_tiles, fast=fast, n_own=owned.shape[0], width=width

time: 97.7 us -> 98.3 us (level)
  waiting for transfers between devices: 6.41 us -> 8.51 us
    ppermute x12, waiting for transfers between devices: 3.47 us -> 5.02 us  [exchange(): lax.ppermute(buf, AXES, pairs(m))]
    optimization_barrier x1 -> x0, local copies, waits for them, and re-layouts: 1.01 us -> none  [exchange(): (r1, r2, r3, rc), prep = lax.optimization_barrier(((r1, r2, r3, rc), prep))]
    broadcast_in_dim x0 -> x1, local copies, waits for them, and re-layouts: none -> 0.98 us  [body(): degree = jnp.broadcast_to(degree.reshape(-1, 1), seeds.shape)]
    unnamed x56 -> x58, local copies, waits for them, and re-layouts: 7.65 us -> 7.62 us
  transfers between devices with their start and end apart: 24 -> 24, of which waited for: 5 -> 6; matrix products, arithmetic and copies ran while one was open for 13% -> 12% of each run, Pallas kernels for 16% -> 16%
where the time goes in v12:
time: 98.3 us; the launch traced here: 97.1 us
  starting transfers between devices  37.1 us (38%)
  Pallas kernels  31.5 us (32%)
  local copies, waits for them, and re-layouts  11.4 us (12%)
  waiting for transfers between devices  8.51 us (9%)
  other arithmetic  8.19 us (8%)
    pallas_call x3, Pallas kernels, hub_call(): pl.pallas_call(functools.partial(hub_kernel, n_hub, width, final), cost_e...  16.2 us
    pallas_call x3, Pallas kernels, band_call(): pl.pallas_call(functools.partial(band_kernel, fast, n_own), cost_estimate...  15.3 us
    ppermute x12, starting transfers between devices, exchange(): lax.ppermute(buf, AXES, pairs(m))  13.3 us
    ppermute x3, starting transfers between devices, exchange(): rc = lax.ppermute(pc, AXES, cross)  12.9 us
    unnamed x58, local copies, waits for them, and re-layouts  7.62 us
    ppermute x3, starting transfers between devices, exchange(): r1 = lax.ppermute(p1, AXES, pairs(1))  7.39 us
    ppermute x12, waiting for transfers between devices, exchange(): lax.ppermute(buf, AXES, pairs(m))  5.02 us
    ppermute x3, waiting for transfers between devices, exchange(): r1 = lax.ppermute(p1, AXES, pairs(1))  3.47 us
  transfers between devices with their start and end apart: 24, of which 6 were waited for; matrix products, arithmetic and copies ran while one was open for 12% of the time, Pallas kernels for 16%

profile of v12, /device:TPU:5, one launch (start us, length us, event | category | flops | bytes accessed | tf_op | source)
XLA Modules:
  0.0 97.1 jit_solution(8146582929454917062)
XLA Ops:
  3.4 2.4 %collective-permute-start.1 = (bf16[128,128]{1,0:T(8,128)(2,1)S(1)}, bf16[128,128]{1,0:T(8,128)(2,1)S(1)}, u32[]{:S(2)}, u32[]{:S(2)}) collective-permute-start(bf16[128,128]{1,0:T(8,128)(2,1)S(1)} %gather_fusion), channel_id=1, source_target_pairs={{0,2},{1,3},{2,0},{3,1},{4,6},{5,7},{6,4},{7,5},{8,10},{9,11},{10,... | collective-permute-start | bytes 98312 | tf_op jit(solution)/shard_map/ppermute | solution.py:50
  5.8 1.4 %collective-permute-start = (bf16[384,128]{1,0:T(8,128)(2,1)S(1)}, bf16[384,128]{1,0:T(8,128)(2,1)S(1)}, u32[]{:S(2)}, u32[]{:S(2)}) collective-permute-start(bf16[384,128]{1,0:T(8,128)(2,1)S(1)} %get-tuple-element.67), channel_id=1, source_target_pairs={{0,1},{1,0},{2,3},{3,2},{4,5},{5,4},{6,7},{7,6},{8,9},{9,8},{10,11... | collective-permute-start | bytes 294920 | tf_op jit(solution)/shard_map/ppermute | solution.py:51
  7.1 6.6 %collective-permute-start.3 = (bf16[256,128]{1,0:T(8,128)(2,1)S(1)}, bf16[256,128]{1,0:T(8,128)(2,1)S(1)}, u32[]{:S(2)}, u32[]{:S(2)}) collective-permute-start(bf16[256,128]{1,0:T(8,128)(2,1)S(1)} %get-tuple-element.63), channel_id=1, source_target_pairs={{3,4},{7,8},{11,12},{15,16},{19,20},{23,24},{27,28},{4,3},{8,7},{1... | collective-permute-start | bytes 196616 | tf_op jit(solution)/shard_map/ppermute | solution.py:55
  13.7 1.5 %fusion.rest_6_ = bf16[128,1024]{1,0:T(8,128)(2,1)} fusion(s32[128]{0:T(128)} %param.14), kind=kLoop, calls=%fused_computation.6 | loop fusion | flops 262144 | bytes 262656 | tf_op jit(solution)/shard_map/convert_element_type | solution.py:289
  15.2 2.2 %convert_reduce_fusion = f32[8,128]{1,0:T(8,128)S(1)} fusion(bf16[8,10,128,128]{3,2,1,0:T(8,128)(2,1)} %rest_3_.5), kind=kLoop, calls=%fused_computation.2 | loop fusion | flops 2620416 | bytes 2625536 | tf_op jit(solution)/shard_map/reduce_sum | solution.py:278
  23.5 5.1 %shard_map.82.rest_3_ = f32[1024,128]{1,0:T(8,128)} custom-call(s32[1]{0:T(128)} %bitcast.z_ref, s32[80]{0:T(128)} %reshape.26.off_ref, bf16[1024,128]{1,0:T(8,128)(2,1)} %copy-done.2, bf16[384,128]{1,0:T(8,128)(2,1)} %copy-done.13, bf16[384,128]{1,0:T(8,128)(2,1)} %copy-done.14, bf16[256,128]{1,0:T(8,128)(2,1)} %copy-done.15, bf16[8,10,128,128]{3,2,1,0:T(8,128)(2,1)} %rest_3_.5), custom_call_target="tpu_custom_call" | custom-call | flops 335544320 | bytes 3670016 | tf_op jit(solution)/shard_map/pallas_call | solution.py:149
  30.3 1.5 %collective-permute-done.7.rest_1_ = bf16[16,128,128]{2,1,0:T(8,128)(2,1)S(1)} collective-permute-done((bf16[16,128,128]{2,1,0:T(8,128)(2,1)S(1)}, bf16[16,128,128]{2,1,0:T(8,128)(2,1)S(1)}, u32[]{:S(2)}, u32[]{:S(2)}) %collective-permute-start.7) | collective-permute-done | bytes 524320 | tf_op jit(solution)/shard_map/ppermute | solution.py:65
  32.7 5.5 %shard_map.83 = (bf16[1024,128]{1,0:T(8,128)(2,1)}, bf16[128,128]{1,0:T(8,128)(2,1)}, bf16[384,128]{1,0:T(8,128)(2,1)}, bf16[384,128]{1,0:T(8,128)(2,1)}, bf16[256,128]{1,0:T(8,128)(2,1)}) custom-call(s32[1]{0:T(128)} %bitcast.z_ref, s32[48]{0:T(128)} %gather_fusion.1, bf16[16,128,128]{2,1,0:T(8,128)(2,1)} %copy-done.3, bf16[16,128,128]{2,1,0:T(8,128)(2,1)} %copy-done.7, ...), custom_call_target="tpu_custom_call" | custom-call | flops 201326592 | bytes 4718592 | tf_op jit(solution)/shard_map/pallas_call | solution.py:245
  39.5 3.1 %collective-permute-start.8 = (bf16[384,128]{1,0:T(8,128)(2,1)}, bf16[384,128]{1,0:T(8,128)(2,1)S(1)}, u32[]{:S(2)}, u32[]{:S(2)}) collective-permute-start(bf16[384,128]{1,0:T(8,128)(2,1)} %get-tuple-element.46), channel_id=1, source_target_pairs={{0,1},{1,0},{2,3},{3,2},{4,5},{5,4},{6,7},{7,6},{8,9},{9,8},{10,11... | collective-permute-start | bytes 294920 | tf_op jit(solution)/shard_map/ppermute | solution.py:51
  42.6 3.3 %collective-permute-start.11 = (bf16[256,128]{1,0:T(8,128)(2,1)}, bf16[256,128]{1,0:T(8,128)(2,1)S(1)}, u32[]{:S(2)}, u32[]{:S(2)}) collective-permute-start(bf16[256,128]{1,0:T(8,128)(2,1)} %get-tuple-element.49), channel_id=1, source_target_pairs={{3,4},{7,8},{11,12},{15,16},{19,20},{23,24},{27,28},{4,3},{8,7},{1... | collective-permute-start | bytes 196616 | tf_op jit(solution)/shard_map/ppermute | solution.py:55
  46.0 1.6 %collective-permute-done.8.rest_0_ = bf16[384,128]{1,0:T(8,128)(2,1)S(1)} collective-permute-done((bf16[384,128]{1,0:T(8,128)(2,1)}, bf16[384,128]{1,0:T(8,128)(2,1)S(1)}, u32[]{:S(2)}, u32[]{:S(2)}) %collective-permute-start.8) | collective-permute-done | bytes 98336 | tf_op jit(solution)/shard_map/ppermute | solution.py:51
  49.6 1.5 %collective-permute-start.14 = (bf16[4,128,128]{2,1,0:T(8,128)(2,1)S(1)}, bf16[4,128,128]{2,1,0:T(8,128)(2,1)S(1)}, u32[]{:S(2)}, u32[]{:S(2)}) collective-permute-start(bf16[4,128,128]{2,1,0:T(8,128)(2,1)S(1)} %pad_maximum_fusion.1), channel_id=1, source_target_pairs={{0,24},{1,25},{2,26},{3,27},{4,28},{5,29},{6,30},{7,31},{8,16},{9,... | collective-permute-start | bytes 393224 | tf_op jit(solution)/shard_map/ppermute | solution.py:65
  51.7 5.1 %shard_map.84.rest_3_ = f32[1024,128]{1,0:T(8,128)} custom-call(s32[1]{0:T(128)} %bitcast.z_ref, s32[80]{0:T(128)} %reshape.26.off_ref, bf16[1024,128]{1,0:T(8,128)(2,1)} %get-tuple-element.48.cur_hbm, bf16[384,128]{1,0:T(8,128)(2,1)} %copy-done.12, bf16[384,128]{1,0:T(8,128)(2,1)} %copy-done.10, bf16[256,128]{1,0:T(8,128)(2,1)} %copy-done.17, ...), custom_call_target="tpu_custom_call" | custom-call | flops 335544320 | bytes 3670016 | tf_op jit(solution)/shard_map/pallas_call | solution.py:149
  57.7 2.3 %collective-permute-start.15 = (bf16[16,128,128]{2,1,0:T(8,128)(2,1)S(1)}, bf16[16,128,128]{2,1,0:T(8,128)(2,1)S(1)}, u32[]{:S(2)}, u32[]{:S(2)}) collective-permute-start(bf16[16,128,128]{2,1,0:T(8,128)(2,1)S(1)} %constant_dynamic-update-slice_fusion.7.rest_0_), channel_id=1, source_target_pairs={{0,4},{1,5},{2,6},{3,7},{4,0},{5,1},{6,2},{7,3},{8,12},{9,13},{10,... | collective-permute-start | bytes 1572872 | tf_op jit(solution)/shard_map/ppermute | solution.py:65
  60.0 1.5 %collective-permute-done.15.rest_1_ = bf16[16,128,128]{2,1,0:T(8,128)(2,1)S(1)} collective-permute-done((bf16[16,128,128]{2,1,0:T(8,128)(2,1)S(1)}, bf16[16,128,128]{2,1,0:T(8,128)(2,1)S(1)}, u32[]{:S(2)}, u32[]{:S(2)}) %collective-permute-start.15) | collective-permute-done | bytes 524320 | tf_op jit(solution)/shard_map/ppermute | solution.py:65
  62.3 5.5 %shard_map.85 = (bf16[1024,128]{1,0:T(8,128)(2,1)}, bf16[128,128]{1,0:T(8,128)(2,1)}, bf16[384,128]{1,0:T(8,128)(2,1)}, bf16[384,128]{1,0:T(8,128)(2,1)}, bf16[256,128]{1,0:T(8,128)(2,1)}) custom-call(s32[1]{0:T(128)} %bitcast.z_ref, s32[48]{0:T(128)} %gather_fusion.1, bf16[16,128,128]{2,1,0:T(8,128)(2,1)} %copy-done.4, bf16[16,128,128]{2,1,0:T(8,128)(2,1)} %copy-done.6, ...), custom_call_target="tpu_custom_call" | custom-call | flops 201326592 | bytes 4718592 | tf_op jit(solution)/shard_map/pallas_call | solution.py:245
  69.3 3.0 %collective-permute-start.16 = (bf16[384,128]{1,0:T(8,128)(2,1)}, bf16[384,128]{1,0:T(8,128)(2,1)S(1)}, u32[]{:S(2)}, u32[]{:S(2)}) collective-permute-start(bf16[384,128]{1,0:T(8,128)(2,1)} %get-tuple-element.55), channel_id=1, source_target_pairs={{0,1},{1,0},{2,3},{3,2},{4,5},{5,4},{6,7},{7,6},{8,9},{9,8},{10,11... | collective-permute-start | bytes 294920 | tf_op jit(solution)/shard_map/ppermute | solution.py:51
  72.3 3.0 %collective-permute-start.19 = (bf16[256,128]{1,0:T(8,128)(2,1)}, bf16[256,128]{1,0:T(8,128)(2,1)S(1)}, u32[]{:S(2)}, u32[]{:S(2)}) collective-permute-start(bf16[256,128]{1,0:T(8,128)(2,1)} %get-tuple-element.58), channel_id=1, source_target_pairs={{3,4},{7,8},{11,12},{15,16},{19,20},{23,24},{27,28},{4,3},{8,7},{1... | collective-permute-start | bytes 196616 | tf_op jit(solution)/shard_map/ppermute | solution.py:55
  75.3 1.9 %collective-permute-done.16.rest_0_ = bf16[384,128]{1,0:T(8,128)(2,1)S(1)} collective-permute-done((bf16[384,128]{1,0:T(8,128)(2,1)}, bf16[384,128]{1,0:T(8,128)(2,1)S(1)}, u32[]{:S(2)}, u32[]{:S(2)}) %collective-permute-start.16) | collective-permute-done | bytes 98336 | tf_op jit(solution)/shard_map/ppermute | solution.py:51
  78.7 2.0 %collective-permute-start.22 = (bf16[4,128,128]{2,1,0:T(8,128)(2,1)S(1)}, bf16[4,128,128]{2,1,0:T(8,128)(2,1)S(1)}, u32[]{:S(2)}, u32[]{:S(2)}) collective-permute-start(bf16[4,128,128]{2,1,0:T(8,128)(2,1)S(1)} %pad_maximum_fusion.2), channel_id=1, source_target_pairs={{0,24},{1,25},{2,26},{3,27},{4,28},{5,29},{6,30},{7,31},{8,16},{9,... | collective-permute-start | bytes 393224 | tf_op jit(solution)/shard_map/ppermute | solution.py:65
  81.3 5.1 %shard_map.86.rest_3_ = f32[1024,128]{1,0:T(8,128)} custom-call(s32[1]{0:T(128)} %bitcast.z_ref, s32[80]{0:T(128)} %reshape.26.off_ref, bf16[1024,128]{1,0:T(8,128)(2,1)} %get-tuple-element.57.cur_hbm, bf16[384,128]{1,0:T(8,128)(2,1)} %copy-done.11, bf16[384,128]{1,0:T(8,128)(2,1)} %copy-done.9, bf16[256,128]{1,0:T(8,128)(2,1)} %copy-done.16, ...), custom_call_target="tpu_custom_call" | custom-call | flops 335544320 | bytes 3670016 | tf_op jit(solution)/shard_map/pallas_call | solution.py:149
  87.3 2.4 %collective-permute-start.23 = (bf16[16,128,128]{2,1,0:T(8,128)(2,1)S(1)}, bf16[16,128,128]{2,1,0:T(8,128)(2,1)S(1)}, u32[]{:S(2)}, u32[]{:S(2)}) collective-permute-start(bf16[16,128,128]{2,1,0:T(8,128)(2,1)S(1)} %constant_dynamic-update-slice_fusion.14.rest_0_), channel_id=1, source_target_pairs={{0,4},{1,5},{2,6},{3,7},{4,0},{5,1},{6,2},{7,3},{8,12},{9,13},{10,... | collective-permute-start | bytes 1572872 | tf_op jit(solution)/shard_map/ppermute | solution.py:65
  89.7 1.5 %collective-permute-done.23.rest_1_ = bf16[16,128,128]{2,1,0:T(8,128)(2,1)S(1)} collective-permute-done((bf16[16,128,128]{2,1,0:T(8,128)(2,1)S(1)}, bf16[16,128,128]{2,1,0:T(8,128)(2,1)S(1)}, u32[]{:S(2)}, u32[]{:S(2)}) %collective-permute-start.23) | collective-permute-done | bytes 524320 | tf_op jit(solution)/shard_map/ppermute | solution.py:65
  92.0 5.1 %shard_map.87 = f32[1024,128]{1,0:T(8,128)} custom-call(s32[1]{0:T(128)} %bitcast.z_ref, s32[48]{0:T(128)} %gather_fusion.1, bf16[16,128,128]{2,1,0:T(8,128)(2,1)} %copy-done.5, bf16[16,128,128]{2,1,0:T(8,128)(2,1)} %copy-done.8, bf16[8,6,128,128]{3,2,1,0:T(8,128)(2,1)} %rest_2_.5, f32[1024,128]{1,0:T(8,128)} %shard_map.86.rest_3_, ...), custom_call_target="tpu_custom_call" | custom-call | flops 201326592 | bytes 4718592 | tf_op jit(solution)/shard_map/pallas_call | solution.py:245
  (116 shorter events, 22.8 us)
Async XLA Ops:
  3.4 16.3 %collective-permute-start.1 = (bf16[128,128]{1,0:T(8,128)(2,1)S(1)}, bf16[128,128]{1,0:T(8,128)(2,1)S(1)}, u32[]{:S(2)}, u32[]{:S(2)}) collective-permute-start(bf16[128,128]{1,0:T(8,128)(2,1)S(1)} %gather_fusion), channel_id=1, source_target_pairs={{0,2},{1,3},{2,0},{3,1},{4,6},{5,7},{6,4},{7,5},{8,10},{9,11},{10,... | collective-permute-start | bytes 98312 | tf_op jit(solution)/shard_map/ppermute | solution.py:50
  5.8 13.9 %collective-permute-start = (bf16[384,128]{1,0:T(8,128)(2,1)S(1)}, bf16[384,128]{1,0:T(8,128)(2,1)S(1)}, u32[]{:S(2)}, u32[]{:S(2)}) collective-permute-start(bf16[384,128]{1,0:T(8,128)(2,1)S(1)} %get-tuple-element.67), channel_id=1, source_target_pairs={{0,1},{1,0},{2,3},{3,2},{4,5},{5,4},{6,7},{7,6},{8,9},{9,8},{10,11... | collective-permute-start | bytes 294920 | tf_op jit(solution)/shard_map/ppermute | solution.py:51
  7.1 12.6 %collective-permute-start.2 = (bf16[384,128]{1,0:T(8,128)(2,1)S(1)}, bf16[384,128]{1,0:T(8,128)(2,1)S(1)}, u32[]{:S(2)}, u32[]{:S(2)}) collective-permute-start(bf16[384,128]{1,0:T(8,128)(2,1)S(1)} %get-tuple-element.66), channel_id=1, source_target_pairs={{0,3},{1,2},{2,1},{3,0},{4,7},{5,6},{6,5},{7,4},{8,11},{9,10},{10,... | collective-permute-start | bytes 294920 | tf_op jit(solution)/shard_map/ppermute | solution.py:49
  7.1 12.6 %collective-permute-start.3 = (bf16[256,128]{1,0:T(8,128)(2,1)S(1)}, bf16[256,128]{1,0:T(8,128)(2,1)S(1)}, u32[]{:S(2)}, u32[]{:S(2)}) collective-permute-start(bf16[256,128]{1,0:T(8,128)(2,1)S(1)} %get-tuple-element.63), channel_id=1, source_target_pairs={{3,4},{7,8},{11,12},{15,16},{19,20},{23,24},{27,28},{4,3},{8,7},{1... | collective-permute-start | bytes 196616 | tf_op jit(solution)/shard_map/ppermute | solution.py:55
  20.8 8.6 %collective-permute-start.4 = (bf16[4,128,128]{2,1,0:T(8,128)(2,1)S(1)}, bf16[4,128,128]{2,1,0:T(8,128)(2,1)S(1)}, u32[]{:S(2)}, u32[]{:S(2)}) collective-permute-start(bf16[4,128,128]{2,1,0:T(8,128)(2,1)S(1)} %pad_maximum_fusion), channel_id=1, source_target_pairs={{0,8},{1,9},{2,10},{3,11},{4,12},{5,13},{6,14},{7,15},{8,0},{9,1},... | collective-permute-start | bytes 393224 | tf_op jit(solution)/shard_map/ppermute | solution.py:65
  22.0 7.7 %collective-permute-start.5 = (bf16[4,128,128]{2,1,0:T(8,128)(2,1)S(1)}, bf16[4,128,128]{2,1,0:T(8,128)(2,1)S(1)}, u32[]{:S(2)}, u32[]{:S(2)}) collective-permute-start(bf16[4,128,128]{2,1,0:T(8,128)(2,1)S(1)} %pad_maximum_fusion), channel_id=1, source_target_pairs={{0,16},{1,17},{2,18},{3,19},{4,20},{5,21},{6,22},{7,23},{8,24},{9,... | collective-permute-start | bytes 393224 | tf_op jit(solution)/shard_map/ppermute | solution.py:65
  22.3 7.5 %collective-permute-start.6 = (bf16[4,128,128]{2,1,0:T(8,128)(2,1)S(1)}, bf16[4,128,128]{2,1,0:T(8,128)(2,1)S(1)}, u32[]{:S(2)}, u32[]{:S(2)}) collective-permute-start(bf16[4,128,128]{2,1,0:T(8,128)(2,1)S(1)} %pad_maximum_fusion), channel_id=1, source_target_pairs={{0,24},{1,25},{2,26},{3,27},{4,28},{5,29},{6,30},{7,31},{8,16},{9,... | collective-permute-start | bytes 393224 | tf_op jit(solution)/shard_map/ppermute | solution.py:65
  29.9 2.0 %collective-permute-start.7 = (bf16[16,128,128]{2,1,0:T(8,128)(2,1)S(1)}, bf16[16,128,128]{2,1,0:T(8,128)(2,1)S(1)}, u32[]{:S(2)}, u32[]{:S(2)}) collective-permute-start(bf16[16,128,128]{2,1,0:T(8,128)(2,1)S(1)} %constant_dynamic-update-slice_fusion.rest_0_), channel_id=1, source_target_pairs={{0,4},{1,5},{2,6},{3,7},{4,0},{5,1},{6,2},{7,3},{8,12},{9,13},{10,... | collective-permute-start | bytes 1572872 | tf_op jit(solution)/shard_map/ppermute | solution.py:65
  38.2 7.7 %collective-permute-start.10 = (bf16[384,128]{1,0:T(8,128)(2,1)}, bf16[384,128]{1,0:T(8,128)(2,1)S(1)}, u32[]{:S(2)}, u32[]{:S(2)}) collective-permute-start(bf16[384,128]{1,0:T(8,128)(2,1)} %get-tuple-element.47), channel_id=1, source_target_pairs={{0,3},{1,2},{2,1},{3,0},{4,7},{5,6},{6,5},{7,4},{8,11},{9,10},{10,... | collective-permute-start | bytes 294920 | tf_op jit(solution)/shard_map/ppermute | solution.py:49
  39.5 8.0 %collective-permute-start.9 = (bf16[128,128]{1,0:T(8,128)(2,1)}, bf16[128,128]{1,0:T(8,128)(2,1)S(1)}, u32[]{:S(2)}, u32[]{:S(2)}) collective-permute-start(bf16[128,128]{1,0:T(8,128)(2,1)} %get-tuple-element.45), channel_id=1, source_target_pairs={{0,2},{1,3},{2,0},{3,1},{4,6},{5,7},{6,4},{7,5},{8,10},{9,11},{10,... | collective-permute-start | bytes 98312 | tf_op jit(solution)/shard_map/ppermute | solution.py:50
  39.5 8.0 %collective-permute-start.8 = (bf16[384,128]{1,0:T(8,128)(2,1)}, bf16[384,128]{1,0:T(8,128)(2,1)S(1)}, u32[]{:S(2)}, u32[]{:S(2)}) collective-permute-start(bf16[384,128]{1,0:T(8,128)(2,1)} %get-tuple-element.46), channel_id=1, source_target_pairs={{0,1},{1,0},{2,3},{3,2},{4,5},{5,4},{6,7},{7,6},{8,9},{9,8},{10,11... | collective-permute-start | bytes 294920 | tf_op jit(solution)/shard_map/ppermute | solution.py:51
  42.6 8.5 %collective-permute-start.11 = (bf16[256,128]{1,0:T(8,128)(2,1)}, bf16[256,128]{1,0:T(8,128)(2,1)S(1)}, u32[]{:S(2)}, u32[]{:S(2)}) collective-permute-start(bf16[256,128]{1,0:T(8,128)(2,1)} %get-tuple-element.49), channel_id=1, source_target_pairs={{3,4},{7,8},{11,12},{15,16},{19,20},{23,24},{27,28},{4,3},{8,7},{1... | collective-permute-start | bytes 196616 | tf_op jit(solution)/shard_map/ppermute | solution.py:55
  48.4 9.2 %collective-permute-start.12 = (bf16[4,128,128]{2,1,0:T(8,128)(2,1)S(1)}, bf16[4,128,128]{2,1,0:T(8,128)(2,1)S(1)}, u32[]{:S(2)}, u32[]{:S(2)}) collective-permute-start(bf16[4,128,128]{2,1,0:T(8,128)(2,1)S(1)} %pad_maximum_fusion.1), channel_id=1, source_target_pairs={{0,8},{1,9},{2,10},{3,11},{4,12},{5,13},{6,14},{7,15},{8,0},{9,1},... | collective-permute-start | bytes 393224 | tf_op jit(solution)/shard_map/ppermute | solution.py:65
  49.3 8.3 %collective-permute-start.13 = (bf16[4,128,128]{2,1,0:T(8,128)(2,1)S(1)}, bf16[4,128,128]{2,1,0:T(8,128)(2,1)S(1)}, u32[]{:S(2)}, u32[]{:S(2)}) collective-permute-start(bf16[4,128,128]{2,1,0:T(8,128)(2,1)S(1)} %pad_maximum_fusion.1), channel_id=1, source_target_pairs={{0,16},{1,17},{2,18},{3,19},{4,20},{5,21},{6,22},{7,23},{8,24},{9,... | collective-permute-start | bytes 393224 | tf_op jit(solution)/shard_map/ppermute | solution.py:65
  49.6 8.0 %collective-permute-start.14 = (bf16[4,128,128]{2,1,0:T(8,128)(2,1)S(1)}, bf16[4,128,128]{2,1,0:T(8,128)(2,1)S(1)}, u32[]{:S(2)}, u32[]{:S(2)}) collective-permute-start(bf16[4,128,128]{2,1,0:T(8,128)(2,1)S(1)} %pad_maximum_fusion.1), channel_id=1, source_target_pairs={{0,24},{1,25},{2,26},{3,27},{4,28},{5,29},{6,30},{7,31},{8,16},{9,... | collective-permute-start | bytes 393224 | tf_op jit(solution)/shard_map/ppermute | solution.py:65
  57.7 3.8 %collective-permute-start.15 = (bf16[16,128,128]{2,1,0:T(8,128)(2,1)S(1)}, bf16[16,128,128]{2,1,0:T(8,128)(2,1)S(1)}, u32[]{:S(2)}, u32[]{:S(2)}) collective-permute-start(bf16[16,128,128]{2,1,0:T(8,128)(2,1)S(1)} %constant_dynamic-update-slice_fusion.7.rest_0_), channel_id=1, source_target_pairs={{0,4},{1,5},{2,6},{3,7},{4,0},{5,1},{6,2},{7,3},{8,12},{9,13},{10,... | collective-permute-start | bytes 1572872 | tf_op jit(solution)/shard_map/ppermute | solution.py:65
  67.9 7.4 %collective-permute-start.18 = (bf16[384,128]{1,0:T(8,128)(2,1)}, bf16[384,128]{1,0:T(8,128)(2,1)S(1)}, u32[]{:S(2)}, u32[]{:S(2)}) collective-permute-start(bf16[384,128]{1,0:T(8,128)(2,1)} %get-tuple-element.56), channel_id=1, source_target_pairs={{0,3},{1,2},{2,1},{3,0},{4,7},{5,6},{6,5},{7,4},{8,11},{9,10},{10,... | collective-permute-start | bytes 294920 | tf_op jit(solution)/shard_map/ppermute | solution.py:49
  68.8 8.4 %collective-permute-start.17 = (bf16[128,128]{1,0:T(8,128)(2,1)}, bf16[128,128]{1,0:T(8,128)(2,1)S(1)}, u32[]{:S(2)}, u32[]{:S(2)}) collective-permute-start(bf16[128,128]{1,0:T(8,128)(2,1)} %get-tuple-element.54), channel_id=1, source_target_pairs={{0,2},{1,3},{2,0},{3,1},{4,6},{5,7},{6,4},{7,5},{8,10},{9,11},{10,... | collective-permute-start | bytes 98312 | tf_op jit(solution)/shard_map/ppermute | solution.py:50
  69.3 7.8 %collective-permute-start.16 = (bf16[384,128]{1,0:T(8,128)(2,1)}, bf16[384,128]{1,0:T(8,128)(2,1)S(1)}, u32[]{:S(2)}, u32[]{:S(2)}) collective-permute-start(bf16[384,128]{1,0:T(8,128)(2,1)} %get-tuple-element.55), channel_id=1, source_target_pairs={{0,1},{1,0},{2,3},{3,2},{4,5},{5,4},{6,7},{7,6},{8,9},{9,8},{10,11... | collective-permute-start | bytes 294920 | tf_op jit(solution)/shard_map/ppermute | solution.py:51
  72.3 8.4 %collective-permute-start.19 = (bf16[256,128]{1,0:T(8,128)(2,1)}, bf16[256,128]{1,0:T(8,128)(2,1)S(1)}, u32[]{:S(2)}, u32[]{:S(2)}) collective-permute-start(bf16[256,128]{1,0:T(8,128)(2,1)} %get-tuple-element.58), channel_id=1, source_target_pairs={{3,4},{7,8},{11,12},{15,16},{19,20},{23,24},{27,28},{4,3},{8,7},{1... | collective-permute-start | bytes 196616 | tf_op jit(solution)/shard_map/ppermute | solution.py:55
  78.0 9.2 %collective-permute-start.20 = (bf16[4,128,128]{2,1,0:T(8,128)(2,1)S(1)}, bf16[4,128,128]{2,1,0:T(8,128)(2,1)S(1)}, u32[]{:S(2)}, u32[]{:S(2)}) collective-permute-start(bf16[4,128,128]{2,1,0:T(8,128)(2,1)S(1)} %pad_maximum_fusion.2), channel_id=1, source_target_pairs={{0,8},{1,9},{2,10},{3,11},{4,12},{5,13},{6,14},{7,15},{8,0},{9,1},... | collective-permute-start | bytes 393224 | tf_op jit(solution)/shard_map/ppermute | solution.py:65
  78.4 8.8 %collective-permute-start.21 = (bf16[4,128,128]{2,1,0:T(8,128)(2,1)S(1)}, bf16[4,128,128]{2,1,0:T(8,128)(2,1)S(1)}, u32[]{:S(2)}, u32[]{:S(2)}) collective-permute-start(bf16[4,128,128]{2,1,0:T(8,128)(2,1)S(1)} %pad_maximum_fusion.2), channel_id=1, source_target_pairs={{0,16},{1,17},{2,18},{3,19},{4,20},{5,21},{6,22},{7,23},{8,24},{9,... | collective-permute-start | bytes 393224 | tf_op jit(solution)/shard_map/ppermute | solution.py:65
  78.7 8.5 %collective-permute-start.22 = (bf16[4,128,128]{2,1,0:T(8,128)(2,1)S(1)}, bf16[4,128,128]{2,1,0:T(8,128)(2,1)S(1)}, u32[]{:S(2)}, u32[]{:S(2)}) collective-permute-start(bf16[4,128,128]{2,1,0:T(8,128)(2,1)S(1)} %pad_maximum_fusion.2), channel_id=1, source_target_pairs={{0,24},{1,25},{2,26},{3,27},{4,28},{5,29},{6,30},{7,31},{8,16},{9,... | collective-permute-start | bytes 393224 | tf_op jit(solution)/shard_map/ppermute | solution.py:65
  87.3 3.9 %collective-permute-start.23 = (bf16[16,128,128]{2,1,0:T(8,128)(2,1)S(1)}, bf16[16,128,128]{2,1,0:T(8,128)(2,1)S(1)}, u32[]{:S(2)}, u32[]{:S(2)}) collective-permute-start(bf16[16,128,128]{2,1,0:T(8,128)(2,1)S(1)} %constant_dynamic-update-slice_fusion.14.rest_0_), channel_id=1, source_target_pairs={{0,4},{1,5},{2,6},{3,7},{4,0},{5,1},{6,2},{7,3},{8,12},{9,13},{10,... | collective-permute-start | bytes 1572872 | tf_op jit(solution)/shard_map/ppermute | solution.py:65
  (20 other events, 111.4 us)

commit v13 on v12

--- a/solution.py
+++ b/solution.py
@@ -134,10 +134,17 @@
     for b in range(blocks):
         band_copies[b].wait()
         acc = jnp.zeros((rows, out_ref.shape[1]), jnp.float32)
-        for k in range(k_band):
+
+        def near(k):
             n = b + BW + off_ref[b * k_band + k]
-            start = pl.multiple_of(n * rows, rows)
-            acc = acc + jnp.dot(bt[b, k], ext[pl.ds(start, rows), :], preferred_element_type=jnp.float32)
+            return ext[pl.ds(pl.multiple_of(n * rows, rows), rows), :]
+
+        for k in range(0, k_band - 1, 2):
+            lhs = jnp.concatenate([bt[b, k], bt[b, k + 1]], axis=1)
+            rhs = jnp.concatenate([near(k), near(k + 1)], axis=0)
+            acc = acc + jnp.dot(lhs, rhs, preferred_element_type=jnp.float32)
+        if k_band % 2:
+            acc = acc + jnp.dot(bt[b, k_band - 1], near(k_band - 1), preferred_element_type=jnp.float32)
         out_ref[pl.ds(b * rows, rows), :] = acc
 
 
@@ -198,9 +205,13 @@
             c.wait()
         span = pl.ds(b * rows, rows)
         acc = jnp.zeros((rows, hub.shape[2]), jnp.float32)
-        for h in range(k_hub):
-            p = hidx_ref[b * k_hub + h]
-            acc = acc + jnp.dot(ht[b, h], hub[p], preferred_element_type=jnp.float32)
+        blk = lambda h: hub[hidx_ref[b * k_hub + h]]
+        for h in range(0, k_hub - 1, 2):
+            lhs = jnp.concatenate([ht[b, h], ht[b, h + 1]], axis=1)
+            rhs = jnp.concatenate([blk(h), blk(h + 1)], axis=0)
+            acc = acc + jnp.dot(lhs, rhs, preferred_element_type=jnp.float32)
+        if k_hub % 2:
+            acc = acc + jnp.dot(ht[b, k_hub - 1], blk(k_hub - 1), preferred_element_type=jnp.float32)
         gathered = (band[span] + acc) / deg[span]
         labels = spread_weight * gathered + (1.0 - spread_weight) * seeds[span].astype(jnp.float32)
         if final:

time: 98.3 us -> 97.2 us (0.989)
  Pallas kernels: 31.5 us -> 29.9 us
    pallas_call x3, Pallas kernels: 15.3 us -> 14.1 us  [band_call(): pl.pallas_call(functools.partial(band_kernel, fast, n_own), cost_estimate...]
  transfers between devices with their start and end apart: 24 -> 24, of which waited for: 6 -> 6; matrix products, arithmetic and copies ran while one was open for 12% -> 12% of each run, Pallas kernels for 16% -> 15%
where the time goes in v13:
time: 97.2 us; the launch traced here: 96.1 us
  starting transfers between devices  37.3 us (38%)
  Pallas kernels  29.9 us (31%)
  local copies, waits for them, and re-layouts  11.4 us (12%)
  waiting for transfers between devices  8.7 us (9%)
  other arithmetic  8.19 us (8%)
    pallas_call x3, Pallas kernels, hub_call(): pl.pallas_call(functools.partial(hub_kernel, n_hub, width, final), cost_e...  15.8 us
    pallas_call x3, Pallas kernels, band_call(): pl.pallas_call(functools.partial(band_kernel, fast, n_own), cost_estimate...  14.1 us
    ppermute x12, starting transfers between devices, exchange(): lax.ppermute(buf, AXES, pairs(m))  13.3 us
    ppermute x3, starting transfers between devices, exchange(): rc = lax.ppermute(pc, AXES, cross)  13 us
    unnamed x58, local copies, waits for them, and re-layouts  7.62 us
    ppermute x3, starting transfers between devices, exchange(): r1 = lax.ppermute(p1, AXES, pairs(1))  7.54 us
    ppermute x12, waiting for transfers between devices, exchange(): lax.ppermute(buf, AXES, pairs(m))  5.41 us
    ppermute x3, waiting for transfers between devices, exchange(): r1 = lax.ppermute(p1, AXES, pairs(1))  3.27 us
  transfers between devices with their start and end apart: 24, of which 6 were waited for; matrix products, arithmetic and copies ran while one was open for 12% of the time, Pallas kernels for 15%

profile of v13, /device:TPU:5, one launch (start us, length us, event | category | flops | bytes accessed | tf_op | source)
XLA Modules:
  0.0 96.1 jit_solution(15478597919962933705)
XLA Ops:
  3.4 2.4 %collective-permute-start.1 = (bf16[128,128]{1,0:T(8,128)(2,1)S(1)}, bf16[128,128]{1,0:T(8,128)(2,1)S(1)}, u32[]{:S(2)}, u32[]{:S(2)}) collective-permute-start(bf16[128,128]{1,0:T(8,128)(2,1)S(1)} %gather_fusion), channel_id=1, source_target_pairs={{0,2},{1,3},{2,0},{3,1},{4,6},{5,7},{6,4},{7,5},{8,10},{9,11},{10,... | collective-permute-start | bytes 98312 | tf_op jit(solution)/shard_map/ppermute | solution.py:50
  5.8 1.4 %collective-permute-start = (bf16[384,128]{1,0:T(8,128)(2,1)S(1)}, bf16[384,128]{1,0:T(8,128)(2,1)S(1)}, u32[]{:S(2)}, u32[]{:S(2)}) collective-permute-start(bf16[384,128]{1,0:T(8,128)(2,1)S(1)} %get-tuple-element.67), channel_id=1, source_target_pairs={{0,1},{1,0},{2,3},{3,2},{4,5},{5,4},{6,7},{7,6},{8,9},{9,8},{10,11... | collective-permute-start | bytes 294920 | tf_op jit(solution)/shard_map/ppermute | solution.py:51
  7.1 6.6 %collective-permute-start.3 = (bf16[256,128]{1,0:T(8,128)(2,1)S(1)}, bf16[256,128]{1,0:T(8,128)(2,1)S(1)}, u32[]{:S(2)}, u32[]{:S(2)}) collective-permute-start(bf16[256,128]{1,0:T(8,128)(2,1)S(1)} %get-tuple-element.63), channel_id=1, source_target_pairs={{3,4},{7,8},{11,12},{15,16},{19,20},{23,24},{27,28},{4,3},{8,7},{1... | collective-permute-start | bytes 196616 | tf_op jit(solution)/shard_map/ppermute | solution.py:55
  13.7 1.5 %fusion.rest_6_ = bf16[128,1024]{1,0:T(8,128)(2,1)} fusion(s32[128]{0:T(128)} %param.14), kind=kLoop, calls=%fused_computation.6 | loop fusion | flops 262144 | bytes 262656 | tf_op jit(solution)/shard_map/convert_element_type | solution.py:300
  15.2 2.2 %convert_reduce_fusion = f32[8,128]{1,0:T(8,128)S(1)} fusion(bf16[8,10,128,128]{3,2,1,0:T(8,128)(2,1)} %rest_3_.5), kind=kLoop, calls=%fused_computation.2 | loop fusion | flops 2620416 | bytes 2625536 | tf_op jit(solution)/shard_map/reduce_sum | solution.py:289
  23.5 4.7 %shard_map.82.rest_3_ = f32[1024,128]{1,0:T(8,128)} custom-call(s32[1]{0:T(128)} %bitcast.z_ref, s32[80]{0:T(128)} %reshape.26.off_ref, bf16[1024,128]{1,0:T(8,128)(2,1)} %copy-done.2, bf16[384,128]{1,0:T(8,128)(2,1)} %copy-done.13, bf16[384,128]{1,0:T(8,128)(2,1)} %copy-done.14, bf16[256,128]{1,0:T(8,128)(2,1)} %copy-done.15, bf16[8,10,128,128]{3,2,1,0:T(8,128)(2,1)} %rest_3_.5), custom_call_target="tpu_custom_call" | custom-call | flops 335544320 | bytes 3670016 | tf_op jit(solution)/shard_map/pallas_call | solution.py:156
  30.3 1.5 %collective-permute-done.7.rest_1_ = bf16[16,128,128]{2,1,0:T(8,128)(2,1)S(1)} collective-permute-done((bf16[16,128,128]{2,1,0:T(8,128)(2,1)S(1)}, bf16[16,128,128]{2,1,0:T(8,128)(2,1)S(1)}, u32[]{:S(2)}, u32[]{:S(2)}) %collective-permute-start.7) | collective-permute-done | bytes 524320 | tf_op jit(solution)/shard_map/ppermute | solution.py:65
  32.7 5.4 %shard_map.83 = (bf16[1024,128]{1,0:T(8,128)(2,1)}, bf16[128,128]{1,0:T(8,128)(2,1)}, bf16[384,128]{1,0:T(8,128)(2,1)}, bf16[384,128]{1,0:T(8,128)(2,1)}, bf16[256,128]{1,0:T(8,128)(2,1)}) custom-call(s32[1]{0:T(128)} %bitcast.z_ref, s32[48]{0:T(128)} %gather_fusion.1, bf16[16,128,128]{2,1,0:T(8,128)(2,1)} %copy-done.3, bf16[16,128,128]{2,1,0:T(8,128)(2,1)} %copy-done.7, ...), custom_call_target="tpu_custom_call" | custom-call | flops 201326592 | bytes 4718592 | tf_op jit(solution)/shard_map/pallas_call | solution.py:256
  39.2 3.2 %collective-permute-start.8 = (bf16[384,128]{1,0:T(8,128)(2,1)}, bf16[384,128]{1,0:T(8,128)(2,1)S(1)}, u32[]{:S(2)}, u32[]{:S(2)}) collective-permute-start(bf16[384,128]{1,0:T(8,128)(2,1)} %get-tuple-element.46), channel_id=1, source_target_pairs={{0,1},{1,0},{2,3},{3,2},{4,5},{5,4},{6,7},{7,6},{8,9},{9,8},{10,11... | collective-permute-start | bytes 294920 | tf_op jit(solution)/shard_map/ppermute | solution.py:51
  42.4 3.3 %collective-permute-start.11 = (bf16[256,128]{1,0:T(8,128)(2,1)}, bf16[256,128]{1,0:T(8,128)(2,1)S(1)}, u32[]{:S(2)}, u32[]{:S(2)}) collective-permute-start(bf16[256,128]{1,0:T(8,128)(2,1)} %get-tuple-element.49), channel_id=1, source_target_pairs={{3,4},{7,8},{11,12},{15,16},{19,20},{23,24},{27,28},{4,3},{8,7},{1... | collective-permute-start | bytes 196616 | tf_op jit(solution)/shard_map/ppermute | solution.py:55
  45.8 1.6 %collective-permute-done.8.rest_0_ = bf16[384,128]{1,0:T(8,128)(2,1)S(1)} collective-permute-done((bf16[384,128]{1,0:T(8,128)(2,1)}, bf16[384,128]{1,0:T(8,128)(2,1)S(1)}, u32[]{:S(2)}, u32[]{:S(2)}) %collective-permute-start.8) | collective-permute-done | bytes 98336 | tf_op jit(solution)/shard_map/ppermute | solution.py:51
  49.5 1.5 %collective-permute-start.14 = (bf16[4,128,128]{2,1,0:T(8,128)(2,1)S(1)}, bf16[4,128,128]{2,1,0:T(8,128)(2,1)S(1)}, u32[]{:S(2)}, u32[]{:S(2)}) collective-permute-start(bf16[4,128,128]{2,1,0:T(8,128)(2,1)S(1)} %pad_maximum_fusion.1), channel_id=1, source_target_pairs={{0,24},{1,25},{2,26},{3,27},{4,28},{5,29},{6,30},{7,31},{8,16},{9,... | collective-permute-start | bytes 393224 | tf_op jit(solution)/shard_map/ppermute | solution.py:65
  51.6 4.7 %shard_map.84.rest_3_ = f32[1024,128]{1,0:T(8,128)} custom-call(s32[1]{0:T(128)} %bitcast.z_ref, s32[80]{0:T(128)} %reshape.26.off_ref, bf16[1024,128]{1,0:T(8,128)(2,1)} %get-tuple-element.48.cur_hbm, bf16[384,128]{1,0:T(8,128)(2,1)} %copy-done.12, bf16[384,128]{1,0:T(8,128)(2,1)} %copy-done.10, bf16[256,128]{1,0:T(8,128)(2,1)} %copy-done.17, ...), custom_call_target="tpu_custom_call" | custom-call | flops 335544320 | bytes 3670016 | tf_op jit(solution)/shard_map/pallas_call | solution.py:156
  57.2 2.3 %collective-permute-start.15 = (bf16[16,128,128]{2,1,0:T(8,128)(2,1)S(1)}, bf16[16,128,128]{2,1,0:T(8,128)(2,1)S(1)}, u32[]{:S(2)}, u32[]{:S(2)}) collective-permute-start(bf16[16,128,128]{2,1,0:T(8,128)(2,1)S(1)} %constant_dynamic-update-slice_fusion.7.rest_0_), channel_id=1, source_target_pairs={{0,4},{1,5},{2,6},{3,7},{4,0},{5,1},{6,2},{7,3},{8,12},{9,13},{10,... | collective-permute-start | bytes 1572872 | tf_op jit(solution)/shard_map/ppermute | solution.py:65
  59.5 1.5 %collective-permute-done.15.rest_1_ = bf16[16,128,128]{2,1,0:T(8,128)(2,1)S(1)} collective-permute-done((bf16[16,128,128]{2,1,0:T(8,128)(2,1)S(1)}, bf16[16,128,128]{2,1,0:T(8,128)(2,1)S(1)}, u32[]{:S(2)}, u32[]{:S(2)}) %collective-permute-start.15) | collective-permute-done | bytes 524320 | tf_op jit(solution)/shard_map/ppermute | solution.py:65
  61.8 5.4 %shard_map.85 = (bf16[1024,128]{1,0:T(8,128)(2,1)}, bf16[128,128]{1,0:T(8,128)(2,1)}, bf16[384,128]{1,0:T(8,128)(2,1)}, bf16[384,128]{1,0:T(8,128)(2,1)}, bf16[256,128]{1,0:T(8,128)(2,1)}) custom-call(s32[1]{0:T(128)} %bitcast.z_ref, s32[48]{0:T(128)} %gather_fusion.1, bf16[16,128,128]{2,1,0:T(8,128)(2,1)} %copy-done.4, bf16[16,128,128]{2,1,0:T(8,128)(2,1)} %copy-done.6, ...), custom_call_target="tpu_custom_call" | custom-call | flops 201326592 | bytes 4718592 | tf_op jit(solution)/shard_map/pallas_call | solution.py:256
  68.6 3.0 %collective-permute-start.16 = (bf16[384,128]{1,0:T(8,128)(2,1)}, bf16[384,128]{1,0:T(8,128)(2,1)S(1)}, u32[]{:S(2)}, u32[]{:S(2)}) collective-permute-start(bf16[384,128]{1,0:T(8,128)(2,1)} %get-tuple-element.55), channel_id=1, source_target_pairs={{0,1},{1,0},{2,3},{3,2},{4,5},{5,4},{6,7},{7,6},{8,9},{9,8},{10,11... | collective-permute-start | bytes 294920 | tf_op jit(solution)/shard_map/ppermute | solution.py:51
  71.6 3.2 %collective-permute-start.19 = (bf16[256,128]{1,0:T(8,128)(2,1)}, bf16[256,128]{1,0:T(8,128)(2,1)S(1)}, u32[]{:S(2)}, u32[]{:S(2)}) collective-permute-start(bf16[256,128]{1,0:T(8,128)(2,1)} %get-tuple-element.58), channel_id=1, source_target_pairs={{3,4},{7,8},{11,12},{15,16},{19,20},{23,24},{27,28},{4,3},{8,7},{1... | collective-permute-start | bytes 196616 | tf_op jit(solution)/shard_map/ppermute | solution.py:55
  74.8 1.7 %collective-permute-done.16.rest_0_ = bf16[384,128]{1,0:T(8,128)(2,1)S(1)} collective-permute-done((bf16[384,128]{1,0:T(8,128)(2,1)}, bf16[384,128]{1,0:T(8,128)(2,1)S(1)}, u32[]{:S(2)}, u32[]{:S(2)}) %collective-permute-start.16) | collective-permute-done | bytes 98336 | tf_op jit(solution)/shard_map/ppermute | solution.py:51
  78.0 1.9 %collective-permute-start.22 = (bf16[4,128,128]{2,1,0:T(8,128)(2,1)S(1)}, bf16[4,128,128]{2,1,0:T(8,128)(2,1)S(1)}, u32[]{:S(2)}, u32[]{:S(2)}) collective-permute-start(bf16[4,128,128]{2,1,0:T(8,128)(2,1)S(1)} %pad_maximum_fusion.2), channel_id=1, source_target_pairs={{0,24},{1,25},{2,26},{3,27},{4,28},{5,29},{6,30},{7,31},{8,16},{9,... | collective-permute-start | bytes 393224 | tf_op jit(solution)/shard_map/ppermute | solution.py:65
  80.6 4.7 %shard_map.86.rest_3_ = f32[1024,128]{1,0:T(8,128)} custom-call(s32[1]{0:T(128)} %bitcast.z_ref, s32[80]{0:T(128)} %reshape.26.off_ref, bf16[1024,128]{1,0:T(8,128)(2,1)} %get-tuple-element.57.cur_hbm, bf16[384,128]{1,0:T(8,128)(2,1)} %copy-done.11, bf16[384,128]{1,0:T(8,128)(2,1)} %copy-done.9, bf16[256,128]{1,0:T(8,128)(2,1)} %copy-done.16, ...), custom_call_target="tpu_custom_call" | custom-call | flops 335544320 | bytes 3670016 | tf_op jit(solution)/shard_map/pallas_call | solution.py:156
  86.2 2.4 %collective-permute-start.23 = (bf16[16,128,128]{2,1,0:T(8,128)(2,1)S(1)}, bf16[16,128,128]{2,1,0:T(8,128)(2,1)S(1)}, u32[]{:S(2)}, u32[]{:S(2)}) collective-permute-start(bf16[16,128,128]{2,1,0:T(8,128)(2,1)S(1)} %constant_dynamic-update-slice_fusion.14.rest_0_), channel_id=1, source_target_pairs={{0,4},{1,5},{2,6},{3,7},{4,0},{5,1},{6,2},{7,3},{8,12},{9,13},{10,... | collective-permute-start | bytes 1572872 | tf_op jit(solution)/shard_map/ppermute | solution.py:65
  88.6 1.5 %collective-permute-done.23.rest_1_ = bf16[16,128,128]{2,1,0:T(8,128)(2,1)S(1)} collective-permute-done((bf16[16,128,128]{2,1,0:T(8,128)(2,1)S(1)}, bf16[16,128,128]{2,1,0:T(8,128)(2,1)S(1)}, u32[]{:S(2)}, u32[]{:S(2)}) %collective-permute-start.23) | collective-permute-done | bytes 524320 | tf_op jit(solution)/shard_map/ppermute | solution.py:65
  90.9 5.0 %shard_map.87 = f32[1024,128]{1,0:T(8,128)} custom-call(s32[1]{0:T(128)} %bitcast.z_ref, s32[48]{0:T(128)} %gather_fusion.1, bf16[16,128,128]{2,1,0:T(8,128)(2,1)} %copy-done.5, bf16[16,128,128]{2,1,0:T(8,128)(2,1)} %copy-done.8, bf16[8,6,128,128]{3,2,1,0:T(8,128)(2,1)} %rest_2_.5, f32[1024,128]{1,0:T(8,128)} %shard_map.86.rest_3_, ...), custom_call_target="tpu_custom_call" | custom-call | flops 201326592 | bytes 4718592 | tf_op jit(solution)/shard_map/pallas_call | solution.py:256
  (116 shorter events, 23.0 us)
Async XLA Ops:
  3.4 16.3 %collective-permute-start.1 = (bf16[128,128]{1,0:T(8,128)(2,1)S(1)}, bf16[128,128]{1,0:T(8,128)(2,1)S(1)}, u32[]{:S(2)}, u32[]{:S(2)}) collective-permute-start(bf16[128,128]{1,0:T(8,128)(2,1)S(1)} %gather_fusion), channel_id=1, source_target_pairs={{0,2},{1,3},{2,0},{3,1},{4,6},{5,7},{6,4},{7,5},{8,10},{9,11},{10,... | collective-permute-start | bytes 98312 | tf_op jit(solution)/shard_map/ppermute | solution.py:50
  5.8 13.9 %collective-permute-start = (bf16[384,128]{1,0:T(8,128)(2,1)S(1)}, bf16[384,128]{1,0:T(8,128)(2,1)S(1)}, u32[]{:S(2)}, u32[]{:S(2)}) collective-permute-start(bf16[384,128]{1,0:T(8,128)(2,1)S(1)} %get-tuple-element.67), channel_id=1, source_target_pairs={{0,1},{1,0},{2,3},{3,2},{4,5},{5,4},{6,7},{7,6},{8,9},{9,8},{10,11... | collective-permute-start | bytes 294920 | tf_op jit(solution)/shard_map/ppermute | solution.py:51
  7.1 12.6 %collective-permute-start.2 = (bf16[384,128]{1,0:T(8,128)(2,1)S(1)}, bf16[384,128]{1,0:T(8,128)(2,1)S(1)}, u32[]{:S(2)}, u32[]{:S(2)}) collective-permute-start(bf16[384,128]{1,0:T(8,128)(2,1)S(1)} %get-tuple-element.66), channel_id=1, source_target_pairs={{0,3},{1,2},{2,1},{3,0},{4,7},{5,6},{6,5},{7,4},{8,11},{9,10},{10,... | collective-permute-start | bytes 294920 | tf_op jit(solution)/shard_map/ppermute | solution.py:49
  7.1 12.6 %collective-permute-start.3 = (bf16[256,128]{1,0:T(8,128)(2,1)S(1)}, bf16[256,128]{1,0:T(8,128)(2,1)S(1)}, u32[]{:S(2)}, u32[]{:S(2)}) collective-permute-start(bf16[256,128]{1,0:T(8,128)(2,1)S(1)} %get-tuple-element.63), channel_id=1, source_target_pairs={{3,4},{7,8},{11,12},{15,16},{19,20},{23,24},{27,28},{4,3},{8,7},{1... | collective-permute-start | bytes 196616 | tf_op jit(solution)/shard_map/ppermute | solution.py:55
  20.8 8.2 %collective-permute-start.4 = (bf16[4,128,128]{2,1,0:T(8,128)(2,1)S(1)}, bf16[4,128,128]{2,1,0:T(8,128)(2,1)S(1)}, u32[]{:S(2)}, u32[]{:S(2)}) collective-permute-start(bf16[4,128,128]{2,1,0:T(8,128)(2,1)S(1)} %pad_maximum_fusion), channel_id=1, source_target_pairs={{0,8},{1,9},{2,10},{3,11},{4,12},{5,13},{6,14},{7,15},{8,0},{9,1},... | collective-permute-start | bytes 393224 | tf_op jit(solution)/shard_map/ppermute | solution.py:65
  22.0 7.7 %collective-permute-start.5 = (bf16[4,128,128]{2,1,0:T(8,128)(2,1)S(1)}, bf16[4,128,128]{2,1,0:T(8,128)(2,1)S(1)}, u32[]{:S(2)}, u32[]{:S(2)}) collective-permute-start(bf16[4,128,128]{2,1,0:T(8,128)(2,1)S(1)} %pad_maximum_fusion), channel_id=1, source_target_pairs={{0,16},{1,17},{2,18},{3,19},{4,20},{5,21},{6,22},{7,23},{8,24},{9,... | collective-permute-start | bytes 393224 | tf_op jit(solution)/shard_map/ppermute | solution.py:65
  22.3 7.5 %collective-permute-start.6 = (bf16[4,128,128]{2,1,0:T(8,128)(2,1)S(1)}, bf16[4,128,128]{2,1,0:T(8,128)(2,1)S(1)}, u32[]{:S(2)}, u32[]{:S(2)}) collective-permute-start(bf16[4,128,128]{2,1,0:T(8,128)(2,1)S(1)} %pad_maximum_fusion), channel_id=1, source_target_pairs={{0,24},{1,25},{2,26},{3,27},{4,28},{5,29},{6,30},{7,31},{8,16},{9,... | collective-permute-start | bytes 393224 | tf_op jit(solution)/shard_map/ppermute | solution.py:65
  29.9 2.0 %collective-permute-start.7 = (bf16[16,128,128]{2,1,0:T(8,128)(2,1)S(1)}, bf16[16,128,128]{2,1,0:T(8,128)(2,1)S(1)}, u32[]{:S(2)}, u32[]{:S(2)}) collective-permute-start(bf16[16,128,128]{2,1,0:T(8,128)(2,1)S(1)} %constant_dynamic-update-slice_fusion.rest_0_), channel_id=1, source_target_pairs={{0,4},{1,5},{2,6},{3,7},{4,0},{5,1},{6,2},{7,3},{8,12},{9,13},{10,... | collective-permute-start | bytes 1572872 | tf_op jit(solution)/shard_map/ppermute | solution.py:65
  38.1 7.7 %collective-permute-start.10 = (bf16[384,128]{1,0:T(8,128)(2,1)}, bf16[384,128]{1,0:T(8,128)(2,1)S(1)}, u32[]{:S(2)}, u32[]{:S(2)}) collective-permute-start(bf16[384,128]{1,0:T(8,128)(2,1)} %get-tuple-element.47), channel_id=1, source_target_pairs={{0,3},{1,2},{2,1},{3,0},{4,7},{5,6},{6,5},{7,4},{8,11},{9,10},{10,... | collective-permute-start | bytes 294920 | tf_op jit(solution)/shard_map/ppermute | solution.py:49
  39.2 8.2 %collective-permute-start.9 = (bf16[128,128]{1,0:T(8,128)(2,1)}, bf16[128,128]{1,0:T(8,128)(2,1)S(1)}, u32[]{:S(2)}, u32[]{:S(2)}) collective-permute-start(bf16[128,128]{1,0:T(8,128)(2,1)} %get-tuple-element.45), channel_id=1, source_target_pairs={{0,2},{1,3},{2,0},{3,1},{4,6},{5,7},{6,4},{7,5},{8,10},{9,11},{10,... | collective-permute-start | bytes 98312 | tf_op jit(solution)/shard_map/ppermute | solution.py:50
  39.2 8.2 %collective-permute-start.8 = (bf16[384,128]{1,0:T(8,128)(2,1)}, bf16[384,128]{1,0:T(8,128)(2,1)S(1)}, u32[]{:S(2)}, u32[]{:S(2)}) collective-permute-start(bf16[384,128]{1,0:T(8,128)(2,1)} %get-tuple-element.46), channel_id=1, source_target_pairs={{0,1},{1,0},{2,3},{3,2},{4,5},{5,4},{6,7},{7,6},{8,9},{9,8},{10,11... | collective-permute-start | bytes 294920 | tf_op jit(solution)/shard_map/ppermute | solution.py:51
  42.4 8.5 %collective-permute-start.11 = (bf16[256,128]{1,0:T(8,128)(2,1)}, bf16[256,128]{1,0:T(8,128)(2,1)S(1)}, u32[]{:S(2)}, u32[]{:S(2)}) collective-permute-start(bf16[256,128]{1,0:T(8,128)(2,1)} %get-tuple-element.49), channel_id=1, source_target_pairs={{3,4},{7,8},{11,12},{15,16},{19,20},{23,24},{27,28},{4,3},{8,7},{1... | collective-permute-start | bytes 196616 | tf_op jit(solution)/shard_map/ppermute | solution.py:55
  48.2 8.8 %collective-permute-start.12 = (bf16[4,128,128]{2,1,0:T(8,128)(2,1)S(1)}, bf16[4,128,128]{2,1,0:T(8,128)(2,1)S(1)}, u32[]{:S(2)}, u32[]{:S(2)}) collective-permute-start(bf16[4,128,128]{2,1,0:T(8,128)(2,1)S(1)} %pad_maximum_fusion.1), channel_id=1, source_target_pairs={{0,8},{1,9},{2,10},{3,11},{4,12},{5,13},{6,14},{7,15},{8,0},{9,1},... | collective-permute-start | bytes 393224 | tf_op jit(solution)/shard_map/ppermute | solution.py:65
  49.1 7.9 %collective-permute-start.13 = (bf16[4,128,128]{2,1,0:T(8,128)(2,1)S(1)}, bf16[4,128,128]{2,1,0:T(8,128)(2,1)S(1)}, u32[]{:S(2)}, u32[]{:S(2)}) collective-permute-start(bf16[4,128,128]{2,1,0:T(8,128)(2,1)S(1)} %pad_maximum_fusion.1), channel_id=1, source_target_pairs={{0,16},{1,17},{2,18},{3,19},{4,20},{5,21},{6,22},{7,23},{8,24},{9,... | collective-permute-start | bytes 393224 | tf_op jit(solution)/shard_map/ppermute | solution.py:65
  49.5 7.6 %collective-permute-start.14 = (bf16[4,128,128]{2,1,0:T(8,128)(2,1)S(1)}, bf16[4,128,128]{2,1,0:T(8,128)(2,1)S(1)}, u32[]{:S(2)}, u32[]{:S(2)}) collective-permute-start(bf16[4,128,128]{2,1,0:T(8,128)(2,1)S(1)} %pad_maximum_fusion.1), channel_id=1, source_target_pairs={{0,24},{1,25},{2,26},{3,27},{4,28},{5,29},{6,30},{7,31},{8,16},{9,... | collective-permute-start | bytes 393224 | tf_op jit(solution)/shard_map/ppermute | solution.py:65
  57.2 3.8 %collective-permute-start.15 = (bf16[16,128,128]{2,1,0:T(8,128)(2,1)S(1)}, bf16[16,128,128]{2,1,0:T(8,128)(2,1)S(1)}, u32[]{:S(2)}, u32[]{:S(2)}) collective-permute-start(bf16[16,128,128]{2,1,0:T(8,128)(2,1)S(1)} %constant_dynamic-update-slice_fusion.7.rest_0_), channel_id=1, source_target_pairs={{0,4},{1,5},{2,6},{3,7},{4,0},{5,1},{6,2},{7,3},{8,12},{9,13},{10,... | collective-permute-start | bytes 1572872 | tf_op jit(solution)/shard_map/ppermute | solution.py:65
  67.2 7.6 %collective-permute-start.18 = (bf16[384,128]{1,0:T(8,128)(2,1)}, bf16[384,128]{1,0:T(8,128)(2,1)S(1)}, u32[]{:S(2)}, u32[]{:S(2)}) collective-permute-start(bf16[384,128]{1,0:T(8,128)(2,1)} %get-tuple-element.56), channel_id=1, source_target_pairs={{0,3},{1,2},{2,1},{3,0},{4,7},{5,6},{6,5},{7,4},{8,11},{9,10},{10,... | collective-permute-start | bytes 294920 | tf_op jit(solution)/shard_map/ppermute | solution.py:49
  68.1 8.4 %collective-permute-start.17 = (bf16[128,128]{1,0:T(8,128)(2,1)}, bf16[128,128]{1,0:T(8,128)(2,1)S(1)}, u32[]{:S(2)}, u32[]{:S(2)}) collective-permute-start(bf16[128,128]{1,0:T(8,128)(2,1)} %get-tuple-element.54), channel_id=1, source_target_pairs={{0,2},{1,3},{2,0},{3,1},{4,6},{5,7},{6,4},{7,5},{8,10},{9,11},{10,... | collective-permute-start | bytes 98312 | tf_op jit(solution)/shard_map/ppermute | solution.py:50
  68.6 7.8 %collective-permute-start.16 = (bf16[384,128]{1,0:T(8,128)(2,1)}, bf16[384,128]{1,0:T(8,128)(2,1)S(1)}, u32[]{:S(2)}, u32[]{:S(2)}) collective-permute-start(bf16[384,128]{1,0:T(8,128)(2,1)} %get-tuple-element.55), channel_id=1, source_target_pairs={{0,1},{1,0},{2,3},{3,2},{4,5},{5,4},{6,7},{7,6},{8,9},{9,8},{10,11... | collective-permute-start | bytes 294920 | tf_op jit(solution)/shard_map/ppermute | solution.py:51
  71.6 8.4 %collective-permute-start.19 = (bf16[256,128]{1,0:T(8,128)(2,1)}, bf16[256,128]{1,0:T(8,128)(2,1)S(1)}, u32[]{:S(2)}, u32[]{:S(2)}) collective-permute-start(bf16[256,128]{1,0:T(8,128)(2,1)} %get-tuple-element.58), channel_id=1, source_target_pairs={{3,4},{7,8},{11,12},{15,16},{19,20},{23,24},{27,28},{4,3},{8,7},{1... | collective-permute-start | bytes 196616 | tf_op jit(solution)/shard_map/ppermute | solution.py:55
  77.3 8.8 %collective-permute-start.20 = (bf16[4,128,128]{2,1,0:T(8,128)(2,1)S(1)}, bf16[4,128,128]{2,1,0:T(8,128)(2,1)S(1)}, u32[]{:S(2)}, u32[]{:S(2)}) collective-permute-start(bf16[4,128,128]{2,1,0:T(8,128)(2,1)S(1)} %pad_maximum_fusion.2), channel_id=1, source_target_pairs={{0,8},{1,9},{2,10},{3,11},{4,12},{5,13},{6,14},{7,15},{8,0},{9,1},... | collective-permute-start | bytes 393224 | tf_op jit(solution)/shard_map/ppermute | solution.py:65
  77.7 8.4 %collective-permute-start.21 = (bf16[4,128,128]{2,1,0:T(8,128)(2,1)S(1)}, bf16[4,128,128]{2,1,0:T(8,128)(2,1)S(1)}, u32[]{:S(2)}, u32[]{:S(2)}) collective-permute-start(bf16[4,128,128]{2,1,0:T(8,128)(2,1)S(1)} %pad_maximum_fusion.2), channel_id=1, source_target_pairs={{0,16},{1,17},{2,18},{3,19},{4,20},{5,21},{6,22},{7,23},{8,24},{9,... | collective-permute-start | bytes 393224 | tf_op jit(solution)/shard_map/ppermute | solution.py:65
  78.0 8.1 %collective-permute-start.22 = (bf16[4,128,128]{2,1,0:T(8,128)(2,1)S(1)}, bf16[4,128,128]{2,1,0:T(8,128)(2,1)S(1)}, u32[]{:S(2)}, u32[]{:S(2)}) collective-permute-start(bf16[4,128,128]{2,1,0:T(8,128)(2,1)S(1)} %pad_maximum_fusion.2), channel_id=1, source_target_pairs={{0,24},{1,25},{2,26},{3,27},{4,28},{5,29},{6,30},{7,31},{8,16},{9,... | collective-permute-start | bytes 393224 | tf_op jit(solution)/shard_map/ppermute | solution.py:65
  86.2 3.9 %collective-permute-start.23 = (bf16[16,128,128]{2,1,0:T(8,128)(2,1)S(1)}, bf16[16,128,128]{2,1,0:T(8,128)(2,1)S(1)}, u32[]{:S(2)}, u32[]{:S(2)}) collective-permute-start(bf16[16,128,128]{2,1,0:T(8,128)(2,1)S(1)} %constant_dynamic-update-slice_fusion.14.rest_0_), channel_id=1, source_target_pairs={{0,4},{1,5},{2,6},{3,7},{4,0},{5,1},{6,2},{7,3},{8,12},{9,13},{10,... | collective-permute-start | bytes 1572872 | tf_op jit(solution)/shard_map/ppermute | solution.py:65
  (20 other events, 111.3 us)

commit v14 on v13

--- a/solution.py
+++ b/solution.py
@@ -185,8 +185,6 @@
             pltpu.make_async_copy(deg_hbm.at[span], deg.at[span], sem.at[n_hub + 4 * b + 2]),
             pltpu.make_async_copy(seeds_hbm.at[span], seeds.at[span], sem.at[n_hub + 4 * b + 3]),
         ])
-    for c in per_block[0]:
-        c.start()
     copies = []
     at = 0
     for i, piece in enumerate(hub_hbm):
@@ -194,6 +192,8 @@
         copies.append(pltpu.make_async_copy(piece, hub.at[pl.ds(at, n)], sem.at[i]))
         at += n
     for c in copies:
+        c.start()
+    for c in per_block[0]:
         c.start()
     for b in range(1, blocks):
         for c in per_block[b]:

time: 97.2 us -> 96.8 us (level)
  no operation moved by 1% of the time
where the time goes in v14:
time: 96.8 us; the launch traced here: 95.6 us
  starting transfers between devices  37.3 us (39%)
  Pallas kernels  29.4 us (30%)
  local copies, waits for them, and re-layouts  11.4 us (12%)
  waiting for transfers between devices  8.71 us (9%)
  other arithmetic  8.19 us (8%)
    pallas_call x3, Pallas kernels, hub_call(): pl.pallas_call(functools.partial(hub_kernel, n_hub, width, final), cost_e...  15.3 us
    pallas_call x3, Pallas kernels, band_call(): pl.pallas_call(functools.partial(band_kernel, fast, n_own), cost_estimate...  14.1 us
    ppermute x12, starting transfers between devices, exchange(): lax.ppermute(buf, AXES, pairs(m))  13.3 us
    ppermute x3, starting transfers between devices, exchange(): rc = lax.ppermute(pc, AXES, cross)  13 us
    unnamed x58, local copies, waits for them, and re-layouts  7.62 us
    ppermute x3, starting transfers between devices, exchange(): r1 = lax.ppermute(p1, AXES, pairs(1))  7.53 us
    ppermute x12, waiting for transfers between devices, exchange(): lax.ppermute(buf, AXES, pairs(m))  5.41 us
    ppermute x3, waiting for transfers between devices, exchange(): r1 = lax.ppermute(p1, AXES, pairs(1))  3.27 us
  transfers between devices with their start and end apart: 24, of which 6 were waited for; matrix products, arithmetic and copies ran while one was open for 12% of the time, Pallas kernels for 15%

profile of v14, /device:TPU:5, one launch (start us, length us, event | category | flops | bytes accessed | tf_op | source)
XLA Modules:
  0.0 95.6 jit_solution(14765920637366859606)
XLA Ops:
  3.4 2.4 %collective-permute-start.1 = (bf16[128,128]{1,0:T(8,128)(2,1)S(1)}, bf16[128,128]{1,0:T(8,128)(2,1)S(1)}, u32[]{:S(2)}, u32[]{:S(2)}) collective-permute-start(bf16[128,128]{1,0:T(8,128)(2,1)S(1)} %gather_fusion), channel_id=1, source_target_pairs={{0,2},{1,3},{2,0},{3,1},{4,6},{5,7},{6,4},{7,5},{8,10},{9,11},{10,... | collective-permute-start | bytes 98312 | tf_op jit(solution)/shard_map/ppermute | solution.py:50
  5.8 1.4 %collective-permute-start = (bf16[384,128]{1,0:T(8,128)(2,1)S(1)}, bf16[384,128]{1,0:T(8,128)(2,1)S(1)}, u32[]{:S(2)}, u32[]{:S(2)}) collective-permute-start(bf16[384,128]{1,0:T(8,128)(2,1)S(1)} %get-tuple-element.67), channel_id=1, source_target_pairs={{0,1},{1,0},{2,3},{3,2},{4,5},{5,4},{6,7},{7,6},{8,9},{9,8},{10,11... | collective-permute-start | bytes 294920 | tf_op jit(solution)/shard_map/ppermute | solution.py:51
  7.1 6.6 %collective-permute-start.3 = (bf16[256,128]{1,0:T(8,128)(2,1)S(1)}, bf16[256,128]{1,0:T(8,128)(2,1)S(1)}, u32[]{:S(2)}, u32[]{:S(2)}) collective-permute-start(bf16[256,128]{1,0:T(8,128)(2,1)S(1)} %get-tuple-element.63), channel_id=1, source_target_pairs={{3,4},{7,8},{11,12},{15,16},{19,20},{23,24},{27,28},{4,3},{8,7},{1... | collective-permute-start | bytes 196616 | tf_op jit(solution)/shard_map/ppermute | solution.py:55
  13.7 1.5 %fusion.rest_6_ = bf16[128,1024]{1,0:T(8,128)(2,1)} fusion(s32[128]{0:T(128)} %param.14), kind=kLoop, calls=%fused_computation.6 | loop fusion | flops 262144 | bytes 262656 | tf_op jit(solution)/shard_map/convert_element_type | solution.py:300
  15.2 2.2 %convert_reduce_fusion = f32[8,128]{1,0:T(8,128)S(1)} fusion(bf16[8,10,128,128]{3,2,1,0:T(8,128)(2,1)} %rest_3_.5), kind=kLoop, calls=%fused_computation.2 | loop fusion | flops 2620416 | bytes 2625536 | tf_op jit(solution)/shard_map/reduce_sum | solution.py:289
  23.5 4.7 %shard_map.82.rest_3_ = f32[1024,128]{1,0:T(8,128)} custom-call(s32[1]{0:T(128)} %bitcast.z_ref, s32[80]{0:T(128)} %reshape.26.off_ref, bf16[1024,128]{1,0:T(8,128)(2,1)} %copy-done.2, bf16[384,128]{1,0:T(8,128)(2,1)} %copy-done.13, bf16[384,128]{1,0:T(8,128)(2,1)} %copy-done.14, bf16[256,128]{1,0:T(8,128)(2,1)} %copy-done.15, bf16[8,10,128,128]{3,2,1,0:T(8,128)(2,1)} %rest_3_.5), custom_call_target="tpu_custom_call" | custom-call | flops 335544320 | bytes 3670016 | tf_op jit(solution)/shard_map/pallas_call | solution.py:156
  30.3 1.5 %collective-permute-done.7.rest_1_ = bf16[16,128,128]{2,1,0:T(8,128)(2,1)S(1)} collective-permute-done((bf16[16,128,128]{2,1,0:T(8,128)(2,1)S(1)}, bf16[16,128,128]{2,1,0:T(8,128)(2,1)S(1)}, u32[]{:S(2)}, u32[]{:S(2)}) %collective-permute-start.7) | collective-permute-done | bytes 524320 | tf_op jit(solution)/shard_map/ppermute | solution.py:65
  32.7 5.3 %shard_map.83 = (bf16[1024,128]{1,0:T(8,128)(2,1)}, bf16[128,128]{1,0:T(8,128)(2,1)}, bf16[384,128]{1,0:T(8,128)(2,1)}, bf16[384,128]{1,0:T(8,128)(2,1)}, bf16[256,128]{1,0:T(8,128)(2,1)}) custom-call(s32[1]{0:T(128)} %bitcast.z_ref, s32[48]{0:T(128)} %gather_fusion.1, bf16[16,128,128]{2,1,0:T(8,128)(2,1)} %copy-done.3, bf16[16,128,128]{2,1,0:T(8,128)(2,1)} %copy-done.7, ...), custom_call_target="tpu_custom_call" | custom-call | flops 201326592 | bytes 4718592 | tf_op jit(solution)/shard_map/pallas_call | solution.py:256
  39.1 3.2 %collective-permute-start.8 = (bf16[384,128]{1,0:T(8,128)(2,1)}, bf16[384,128]{1,0:T(8,128)(2,1)S(1)}, u32[]{:S(2)}, u32[]{:S(2)}) collective-permute-start(bf16[384,128]{1,0:T(8,128)(2,1)} %get-tuple-element.46), channel_id=1, source_target_pairs={{0,1},{1,0},{2,3},{3,2},{4,5},{5,4},{6,7},{7,6},{8,9},{9,8},{10,11... | collective-permute-start | bytes 294920 | tf_op jit(solution)/shard_map/ppermute | solution.py:51
  42.3 3.3 %collective-permute-start.11 = (bf16[256,128]{1,0:T(8,128)(2,1)}, bf16[256,128]{1,0:T(8,128)(2,1)S(1)}, u32[]{:S(2)}, u32[]{:S(2)}) collective-permute-start(bf16[256,128]{1,0:T(8,128)(2,1)} %get-tuple-element.49), channel_id=1, source_target_pairs={{3,4},{7,8},{11,12},{15,16},{19,20},{23,24},{27,28},{4,3},{8,7},{1... | collective-permute-start | bytes 196616 | tf_op jit(solution)/shard_map/ppermute | solution.py:55
  45.7 1.6 %collective-permute-done.8.rest_0_ = bf16[384,128]{1,0:T(8,128)(2,1)S(1)} collective-permute-done((bf16[384,128]{1,0:T(8,128)(2,1)}, bf16[384,128]{1,0:T(8,128)(2,1)S(1)}, u32[]{:S(2)}, u32[]{:S(2)}) %collective-permute-start.8) | collective-permute-done | bytes 98336 | tf_op jit(solution)/shard_map/ppermute | solution.py:51
  49.3 1.5 %collective-permute-start.14 = (bf16[4,128,128]{2,1,0:T(8,128)(2,1)S(1)}, bf16[4,128,128]{2,1,0:T(8,128)(2,1)S(1)}, u32[]{:S(2)}, u32[]{:S(2)}) collective-permute-start(bf16[4,128,128]{2,1,0:T(8,128)(2,1)S(1)} %pad_maximum_fusion.1), channel_id=1, source_target_pairs={{0,24},{1,25},{2,26},{3,27},{4,28},{5,29},{6,30},{7,31},{8,16},{9,... | collective-permute-start | bytes 393224 | tf_op jit(solution)/shard_map/ppermute | solution.py:65
  51.4 4.7 %shard_map.84.rest_3_ = f32[1024,128]{1,0:T(8,128)} custom-call(s32[1]{0:T(128)} %bitcast.z_ref, s32[80]{0:T(128)} %reshape.26.off_ref, bf16[1024,128]{1,0:T(8,128)(2,1)} %get-tuple-element.48.cur_hbm, bf16[384,128]{1,0:T(8,128)(2,1)} %copy-done.12, bf16[384,128]{1,0:T(8,128)(2,1)} %copy-done.10, bf16[256,128]{1,0:T(8,128)(2,1)} %copy-done.17, ...), custom_call_target="tpu_custom_call" | custom-call | flops 335544320 | bytes 3670016 | tf_op jit(solution)/shard_map/pallas_call | solution.py:156
  57.0 2.3 %collective-permute-start.15 = (bf16[16,128,128]{2,1,0:T(8,128)(2,1)S(1)}, bf16[16,128,128]{2,1,0:T(8,128)(2,1)S(1)}, u32[]{:S(2)}, u32[]{:S(2)}) collective-permute-start(bf16[16,128,128]{2,1,0:T(8,128)(2,1)S(1)} %constant_dynamic-update-slice_fusion.7.rest_0_), channel_id=1, source_target_pairs={{0,4},{1,5},{2,6},{3,7},{4,0},{5,1},{6,2},{7,3},{8,12},{9,13},{10,... | collective-permute-start | bytes 1572872 | tf_op jit(solution)/shard_map/ppermute | solution.py:65
  59.3 1.5 %collective-permute-done.15.rest_1_ = bf16[16,128,128]{2,1,0:T(8,128)(2,1)S(1)} collective-permute-done((bf16[16,128,128]{2,1,0:T(8,128)(2,1)S(1)}, bf16[16,128,128]{2,1,0:T(8,128)(2,1)S(1)}, u32[]{:S(2)}, u32[]{:S(2)}) %collective-permute-start.15) | collective-permute-done | bytes 524320 | tf_op jit(solution)/shard_map/ppermute | solution.py:65
  61.7 5.3 %shard_map.85 = (bf16[1024,128]{1,0:T(8,128)(2,1)}, bf16[128,128]{1,0:T(8,128)(2,1)}, bf16[384,128]{1,0:T(8,128)(2,1)}, bf16[384,128]{1,0:T(8,128)(2,1)}, bf16[256,128]{1,0:T(8,128)(2,1)}) custom-call(s32[1]{0:T(128)} %bitcast.z_ref, s32[48]{0:T(128)} %gather_fusion.1, bf16[16,128,128]{2,1,0:T(8,128)(2,1)} %copy-done.4, bf16[16,128,128]{2,1,0:T(8,128)(2,1)} %copy-done.6, ...), custom_call_target="tpu_custom_call" | custom-call | flops 201326592 | bytes 4718592 | tf_op jit(solution)/shard_map/pallas_call | solution.py:256
  68.3 3.0 %collective-permute-start.16 = (bf16[384,128]{1,0:T(8,128)(2,1)}, bf16[384,128]{1,0:T(8,128)(2,1)S(1)}, u32[]{:S(2)}, u32[]{:S(2)}) collective-permute-start(bf16[384,128]{1,0:T(8,128)(2,1)} %get-tuple-element.55), channel_id=1, source_target_pairs={{0,1},{1,0},{2,3},{3,2},{4,5},{5,4},{6,7},{7,6},{8,9},{9,8},{10,11... | collective-permute-start | bytes 294920 | tf_op jit(solution)/shard_map/ppermute | solution.py:51
  71.3 3.2 %collective-permute-start.19 = (bf16[256,128]{1,0:T(8,128)(2,1)}, bf16[256,128]{1,0:T(8,128)(2,1)S(1)}, u32[]{:S(2)}, u32[]{:S(2)}) collective-permute-start(bf16[256,128]{1,0:T(8,128)(2,1)} %get-tuple-element.58), channel_id=1, source_target_pairs={{3,4},{7,8},{11,12},{15,16},{19,20},{23,24},{27,28},{4,3},{8,7},{1... | collective-permute-start | bytes 196616 | tf_op jit(solution)/shard_map/ppermute | solution.py:55
  74.5 1.7 %collective-permute-done.16.rest_0_ = bf16[384,128]{1,0:T(8,128)(2,1)S(1)} collective-permute-done((bf16[384,128]{1,0:T(8,128)(2,1)}, bf16[384,128]{1,0:T(8,128)(2,1)S(1)}, u32[]{:S(2)}, u32[]{:S(2)}) %collective-permute-start.16) | collective-permute-done | bytes 98336 | tf_op jit(solution)/shard_map/ppermute | solution.py:51
  77.8 2.0 %collective-permute-start.22 = (bf16[4,128,128]{2,1,0:T(8,128)(2,1)S(1)}, bf16[4,128,128]{2,1,0:T(8,128)(2,1)S(1)}, u32[]{:S(2)}, u32[]{:S(2)}) collective-permute-start(bf16[4,128,128]{2,1,0:T(8,128)(2,1)S(1)} %pad_maximum_fusion.2), channel_id=1, source_target_pairs={{0,24},{1,25},{2,26},{3,27},{4,28},{5,29},{6,30},{7,31},{8,16},{9,... | collective-permute-start | bytes 393224 | tf_op jit(solution)/shard_map/ppermute | solution.py:65
  80.3 4.7 %shard_map.86.rest_3_ = f32[1024,128]{1,0:T(8,128)} custom-call(s32[1]{0:T(128)} %bitcast.z_ref, s32[80]{0:T(128)} %reshape.26.off_ref, bf16[1024,128]{1,0:T(8,128)(2,1)} %get-tuple-element.57.cur_hbm, bf16[384,128]{1,0:T(8,128)(2,1)} %copy-done.11, bf16[384,128]{1,0:T(8,128)(2,1)} %copy-done.9, bf16[256,128]{1,0:T(8,128)(2,1)} %copy-done.16, ...), custom_call_target="tpu_custom_call" | custom-call | flops 335544320 | bytes 3670016 | tf_op jit(solution)/shard_map/pallas_call | solution.py:156
  85.9 2.4 %collective-permute-start.23 = (bf16[16,128,128]{2,1,0:T(8,128)(2,1)S(1)}, bf16[16,128,128]{2,1,0:T(8,128)(2,1)S(1)}, u32[]{:S(2)}, u32[]{:S(2)}) collective-permute-start(bf16[16,128,128]{2,1,0:T(8,128)(2,1)S(1)} %constant_dynamic-update-slice_fusion.14.rest_0_), channel_id=1, source_target_pairs={{0,4},{1,5},{2,6},{3,7},{4,0},{5,1},{6,2},{7,3},{8,12},{9,13},{10,... | collective-permute-start | bytes 1572872 | tf_op jit(solution)/shard_map/ppermute | solution.py:65
  88.3 1.5 %collective-permute-done.23.rest_1_ = bf16[16,128,128]{2,1,0:T(8,128)(2,1)S(1)} collective-permute-done((bf16[16,128,128]{2,1,0:T(8,128)(2,1)S(1)}, bf16[16,128,128]{2,1,0:T(8,128)(2,1)S(1)}, u32[]{:S(2)}, u32[]{:S(2)}) %collective-permute-start.23) | collective-permute-done | bytes 524320 | tf_op jit(solution)/shard_map/ppermute | solution.py:65
  90.6 4.8 %shard_map.87 = f32[1024,128]{1,0:T(8,128)} custom-call(s32[1]{0:T(128)} %bitcast.z_ref, s32[48]{0:T(128)} %gather_fusion.1, bf16[16,128,128]{2,1,0:T(8,128)(2,1)} %copy-done.5, bf16[16,128,128]{2,1,0:T(8,128)(2,1)} %copy-done.8, bf16[8,6,128,128]{3,2,1,0:T(8,128)(2,1)} %rest_2_.5, f32[1024,128]{1,0:T(8,128)} %shard_map.86.rest_3_, ...), custom_call_target="tpu_custom_call" | custom-call | flops 201326592 | bytes 4718592 | tf_op jit(solution)/shard_map/pallas_call | solution.py:256
  (116 shorter events, 23.0 us)
Async XLA Ops:
  3.4 16.3 %collective-permute-start.1 = (bf16[128,128]{1,0:T(8,128)(2,1)S(1)}, bf16[128,128]{1,0:T(8,128)(2,1)S(1)}, u32[]{:S(2)}, u32[]{:S(2)}) collective-permute-start(bf16[128,128]{1,0:T(8,128)(2,1)S(1)} %gather_fusion), channel_id=1, source_target_pairs={{0,2},{1,3},{2,0},{3,1},{4,6},{5,7},{6,4},{7,5},{8,10},{9,11},{10,... | collective-permute-start | bytes 98312 | tf_op jit(solution)/shard_map/ppermute | solution.py:50
  5.8 13.9 %collective-permute-start = (bf16[384,128]{1,0:T(8,128)(2,1)S(1)}, bf16[384,128]{1,0:T(8,128)(2,1)S(1)}, u32[]{:S(2)}, u32[]{:S(2)}) collective-permute-start(bf16[384,128]{1,0:T(8,128)(2,1)S(1)} %get-tuple-element.67), channel_id=1, source_target_pairs={{0,1},{1,0},{2,3},{3,2},{4,5},{5,4},{6,7},{7,6},{8,9},{9,8},{10,11... | collective-permute-start | bytes 294920 | tf_op jit(solution)/shard_map/ppermute | solution.py:51
  7.1 12.6 %collective-permute-start.2 = (bf16[384,128]{1,0:T(8,128)(2,1)S(1)}, bf16[384,128]{1,0:T(8,128)(2,1)S(1)}, u32[]{:S(2)}, u32[]{:S(2)}) collective-permute-start(bf16[384,128]{1,0:T(8,128)(2,1)S(1)} %get-tuple-element.66), channel_id=1, source_target_pairs={{0,3},{1,2},{2,1},{3,0},{4,7},{5,6},{6,5},{7,4},{8,11},{9,10},{10,... | collective-permute-start | bytes 294920 | tf_op jit(solution)/shard_map/ppermute | solution.py:49
  7.1 12.6 %collective-permute-start.3 = (bf16[256,128]{1,0:T(8,128)(2,1)S(1)}, bf16[256,128]{1,0:T(8,128)(2,1)S(1)}, u32[]{:S(2)}, u32[]{:S(2)}) collective-permute-start(bf16[256,128]{1,0:T(8,128)(2,1)S(1)} %get-tuple-element.63), channel_id=1, source_target_pairs={{3,4},{7,8},{11,12},{15,16},{19,20},{23,24},{27,28},{4,3},{8,7},{1... | collective-permute-start | bytes 196616 | tf_op jit(solution)/shard_map/ppermute | solution.py:55
  20.8 8.2 %collective-permute-start.4 = (bf16[4,128,128]{2,1,0:T(8,128)(2,1)S(1)}, bf16[4,128,128]{2,1,0:T(8,128)(2,1)S(1)}, u32[]{:S(2)}, u32[]{:S(2)}) collective-permute-start(bf16[4,128,128]{2,1,0:T(8,128)(2,1)S(1)} %pad_maximum_fusion), channel_id=1, source_target_pairs={{0,8},{1,9},{2,10},{3,11},{4,12},{5,13},{6,14},{7,15},{8,0},{9,1},... | collective-permute-start | bytes 393224 | tf_op jit(solution)/shard_map/ppermute | solution.py:65
  22.0 7.7 %collective-permute-start.5 = (bf16[4,128,128]{2,1,0:T(8,128)(2,1)S(1)}, bf16[4,128,128]{2,1,0:T(8,128)(2,1)S(1)}, u32[]{:S(2)}, u32[]{:S(2)}) collective-permute-start(bf16[4,128,128]{2,1,0:T(8,128)(2,1)S(1)} %pad_maximum_fusion), channel_id=1, source_target_pairs={{0,16},{1,17},{2,18},{3,19},{4,20},{5,21},{6,22},{7,23},{8,24},{9,... | collective-permute-start | bytes 393224 | tf_op jit(solution)/shard_map/ppermute | solution.py:65
  22.3 7.5 %collective-permute-start.6 = (bf16[4,128,128]{2,1,0:T(8,128)(2,1)S(1)}, bf16[4,128,128]{2,1,0:T(8,128)(2,1)S(1)}, u32[]{:S(2)}, u32[]{:S(2)}) collective-permute-start(bf16[4,128,128]{2,1,0:T(8,128)(2,1)S(1)} %pad_maximum_fusion), channel_id=1, source_target_pairs={{0,24},{1,25},{2,26},{3,27},{4,28},{5,29},{6,30},{7,31},{8,16},{9,... | collective-permute-start | bytes 393224 | tf_op jit(solution)/shard_map/ppermute | solution.py:65
  29.9 2.0 %collective-permute-start.7 = (bf16[16,128,128]{2,1,0:T(8,128)(2,1)S(1)}, bf16[16,128,128]{2,1,0:T(8,128)(2,1)S(1)}, u32[]{:S(2)}, u32[]{:S(2)}) collective-permute-start(bf16[16,128,128]{2,1,0:T(8,128)(2,1)S(1)} %constant_dynamic-update-slice_fusion.rest_0_), channel_id=1, source_target_pairs={{0,4},{1,5},{2,6},{3,7},{4,0},{5,1},{6,2},{7,3},{8,12},{9,13},{10,... | collective-permute-start | bytes 1572872 | tf_op jit(solution)/shard_map/ppermute | solution.py:65
  37.9 7.7 %collective-permute-start.10 = (bf16[384,128]{1,0:T(8,128)(2,1)}, bf16[384,128]{1,0:T(8,128)(2,1)S(1)}, u32[]{:S(2)}, u32[]{:S(2)}) collective-permute-start(bf16[384,128]{1,0:T(8,128)(2,1)} %get-tuple-element.47), channel_id=1, source_target_pairs={{0,3},{1,2},{2,1},{3,0},{4,7},{5,6},{6,5},{7,4},{8,11},{9,10},{10,... | collective-permute-start | bytes 294920 | tf_op jit(solution)/shard_map/ppermute | solution.py:49
  39.1 8.2 %collective-permute-start.9 = (bf16[128,128]{1,0:T(8,128)(2,1)}, bf16[128,128]{1,0:T(8,128)(2,1)S(1)}, u32[]{:S(2)}, u32[]{:S(2)}) collective-permute-start(bf16[128,128]{1,0:T(8,128)(2,1)} %get-tuple-element.45), channel_id=1, source_target_pairs={{0,2},{1,3},{2,0},{3,1},{4,6},{5,7},{6,4},{7,5},{8,10},{9,11},{10,... | collective-permute-start | bytes 98312 | tf_op jit(solution)/shard_map/ppermute | solution.py:50
  39.1 8.2 %collective-permute-start.8 = (bf16[384,128]{1,0:T(8,128)(2,1)}, bf16[384,128]{1,0:T(8,128)(2,1)S(1)}, u32[]{:S(2)}, u32[]{:S(2)}) collective-permute-start(bf16[384,128]{1,0:T(8,128)(2,1)} %get-tuple-element.46), channel_id=1, source_target_pairs={{0,1},{1,0},{2,3},{3,2},{4,5},{5,4},{6,7},{7,6},{8,9},{9,8},{10,11... | collective-permute-start | bytes 294920 | tf_op jit(solution)/shard_map/ppermute | solution.py:51
  42.3 8.5 %collective-permute-start.11 = (bf16[256,128]{1,0:T(8,128)(2,1)}, bf16[256,128]{1,0:T(8,128)(2,1)S(1)}, u32[]{:S(2)}, u32[]{:S(2)}) collective-permute-start(bf16[256,128]{1,0:T(8,128)(2,1)} %get-tuple-element.49), channel_id=1, source_target_pairs={{3,4},{7,8},{11,12},{15,16},{19,20},{23,24},{27,28},{4,3},{8,7},{1... | collective-permute-start | bytes 196616 | tf_op jit(solution)/shard_map/ppermute | solution.py:55
  48.1 8.8 %collective-permute-start.12 = (bf16[4,128,128]{2,1,0:T(8,128)(2,1)S(1)}, bf16[4,128,128]{2,1,0:T(8,128)(2,1)S(1)}, u32[]{:S(2)}, u32[]{:S(2)}) collective-permute-start(bf16[4,128,128]{2,1,0:T(8,128)(2,1)S(1)} %pad_maximum_fusion.1), channel_id=1, source_target_pairs={{0,8},{1,9},{2,10},{3,11},{4,12},{5,13},{6,14},{7,15},{8,0},{9,1},... | collective-permute-start | bytes 393224 | tf_op jit(solution)/shard_map/ppermute | solution.py:65
  49.0 7.9 %collective-permute-start.13 = (bf16[4,128,128]{2,1,0:T(8,128)(2,1)S(1)}, bf16[4,128,128]{2,1,0:T(8,128)(2,1)S(1)}, u32[]{:S(2)}, u32[]{:S(2)}) collective-permute-start(bf16[4,128,128]{2,1,0:T(8,128)(2,1)S(1)} %pad_maximum_fusion.1), channel_id=1, source_target_pairs={{0,16},{1,17},{2,18},{3,19},{4,20},{5,21},{6,22},{7,23},{8,24},{9,... | collective-permute-start | bytes 393224 | tf_op jit(solution)/shard_map/ppermute | solution.py:65
  49.3 7.6 %collective-permute-start.14 = (bf16[4,128,128]{2,1,0:T(8,128)(2,1)S(1)}, bf16[4,128,128]{2,1,0:T(8,128)(2,1)S(1)}, u32[]{:S(2)}, u32[]{:S(2)}) collective-permute-start(bf16[4,128,128]{2,1,0:T(8,128)(2,1)S(1)} %pad_maximum_fusion.1), channel_id=1, source_target_pairs={{0,24},{1,25},{2,26},{3,27},{4,28},{5,29},{6,30},{7,31},{8,16},{9,... | collective-permute-start | bytes 393224 | tf_op jit(solution)/shard_map/ppermute | solution.py:65
  57.0 3.8 %collective-permute-start.15 = (bf16[16,128,128]{2,1,0:T(8,128)(2,1)S(1)}, bf16[16,128,128]{2,1,0:T(8,128)(2,1)S(1)}, u32[]{:S(2)}, u32[]{:S(2)}) collective-permute-start(bf16[16,128,128]{2,1,0:T(8,128)(2,1)S(1)} %constant_dynamic-update-slice_fusion.7.rest_0_), channel_id=1, source_target_pairs={{0,4},{1,5},{2,6},{3,7},{4,0},{5,1},{6,2},{7,3},{8,12},{9,13},{10,... | collective-permute-start | bytes 1572872 | tf_op jit(solution)/shard_map/ppermute | solution.py:65
  66.9 7.6 %collective-permute-start.18 = (bf16[384,128]{1,0:T(8,128)(2,1)}, bf16[384,128]{1,0:T(8,128)(2,1)S(1)}, u32[]{:S(2)}, u32[]{:S(2)}) collective-permute-start(bf16[384,128]{1,0:T(8,128)(2,1)} %get-tuple-element.56), channel_id=1, source_target_pairs={{0,3},{1,2},{2,1},{3,0},{4,7},{5,6},{6,5},{7,4},{8,11},{9,10},{10,... | collective-permute-start | bytes 294920 | tf_op jit(solution)/shard_map/ppermute | solution.py:49
  67.8 8.4 %collective-permute-start.17 = (bf16[128,128]{1,0:T(8,128)(2,1)}, bf16[128,128]{1,0:T(8,128)(2,1)S(1)}, u32[]{:S(2)}, u32[]{:S(2)}) collective-permute-start(bf16[128,128]{1,0:T(8,128)(2,1)} %get-tuple-element.54), channel_id=1, source_target_pairs={{0,2},{1,3},{2,0},{3,1},{4,6},{5,7},{6,4},{7,5},{8,10},{9,11},{10,... | collective-permute-start | bytes 98312 | tf_op jit(solution)/shard_map/ppermute | solution.py:50
  68.3 7.8 %collective-permute-start.16 = (bf16[384,128]{1,0:T(8,128)(2,1)}, bf16[384,128]{1,0:T(8,128)(2,1)S(1)}, u32[]{:S(2)}, u32[]{:S(2)}) collective-permute-start(bf16[384,128]{1,0:T(8,128)(2,1)} %get-tuple-element.55), channel_id=1, source_target_pairs={{0,1},{1,0},{2,3},{3,2},{4,5},{5,4},{6,7},{7,6},{8,9},{9,8},{10,11... | collective-permute-start | bytes 294920 | tf_op jit(solution)/shard_map/ppermute | solution.py:51
  71.3 8.4 %collective-permute-start.19 = (bf16[256,128]{1,0:T(8,128)(2,1)}, bf16[256,128]{1,0:T(8,128)(2,1)S(1)}, u32[]{:S(2)}, u32[]{:S(2)}) collective-permute-start(bf16[256,128]{1,0:T(8,128)(2,1)} %get-tuple-element.58), channel_id=1, source_target_pairs={{3,4},{7,8},{11,12},{15,16},{19,20},{23,24},{27,28},{4,3},{8,7},{1... | collective-permute-start | bytes 196616 | tf_op jit(solution)/shard_map/ppermute | solution.py:55
  77.0 8.8 %collective-permute-start.20 = (bf16[4,128,128]{2,1,0:T(8,128)(2,1)S(1)}, bf16[4,128,128]{2,1,0:T(8,128)(2,1)S(1)}, u32[]{:S(2)}, u32[]{:S(2)}) collective-permute-start(bf16[4,128,128]{2,1,0:T(8,128)(2,1)S(1)} %pad_maximum_fusion.2), channel_id=1, source_target_pairs={{0,8},{1,9},{2,10},{3,11},{4,12},{5,13},{6,14},{7,15},{8,0},{9,1},... | collective-permute-start | bytes 393224 | tf_op jit(solution)/shard_map/ppermute | solution.py:65
  77.4 8.4 %collective-permute-start.21 = (bf16[4,128,128]{2,1,0:T(8,128)(2,1)S(1)}, bf16[4,128,128]{2,1,0:T(8,128)(2,1)S(1)}, u32[]{:S(2)}, u32[]{:S(2)}) collective-permute-start(bf16[4,128,128]{2,1,0:T(8,128)(2,1)S(1)} %pad_maximum_fusion.2), channel_id=1, source_target_pairs={{0,16},{1,17},{2,18},{3,19},{4,20},{5,21},{6,22},{7,23},{8,24},{9,... | collective-permute-start | bytes 393224 | tf_op jit(solution)/shard_map/ppermute | solution.py:65
  77.8 8.1 %collective-permute-start.22 = (bf16[4,128,128]{2,1,0:T(8,128)(2,1)S(1)}, bf16[4,128,128]{2,1,0:T(8,128)(2,1)S(1)}, u32[]{:S(2)}, u32[]{:S(2)}) collective-permute-start(bf16[4,128,128]{2,1,0:T(8,128)(2,1)S(1)} %pad_maximum_fusion.2), channel_id=1, source_target_pairs={{0,24},{1,25},{2,26},{3,27},{4,28},{5,29},{6,30},{7,31},{8,16},{9,... | collective-permute-start | bytes 393224 | tf_op jit(solution)/shard_map/ppermute | solution.py:65
  85.9 3.9 %collective-permute-start.23 = (bf16[16,128,128]{2,1,0:T(8,128)(2,1)S(1)}, bf16[16,128,128]{2,1,0:T(8,128)(2,1)S(1)}, u32[]{:S(2)}, u32[]{:S(2)}) collective-permute-start(bf16[16,128,128]{2,1,0:T(8,128)(2,1)S(1)} %constant_dynamic-update-slice_fusion.14.rest_0_), channel_id=1, source_target_pairs={{0,4},{1,5},{2,6},{3,7},{4,0},{5,1},{6,2},{7,3},{8,12},{9,13},{10,... | collective-permute-start | bytes 1572872 | tf_op jit(solution)/shard_map/ppermute | solution.py:65
  (20 other events, 111.3 us)

commit v15 on v14

--- a/solution.py
+++ b/solution.py
@@ -285,16 +285,15 @@
 
 def body(seed_scores, seed_mask, band_offsets, band_tiles, hub_blocks, hub_tiles, hub_rows):
     block_rows = band_tiles.shape[2]
-    seeds = seed_mask.astype(jnp.float32)[:, None] * seed_scores.astype(jnp.float32)
+    seeds16 = seed_mask.astype(seed_scores.dtype)[:, None] * seed_scores
     degree = jnp.sum(band_tiles, axis=(1, 3), dtype=jnp.float32) + jnp.sum(
         hub_tiles, axis=(1, 3), dtype=jnp.float32
     )
-    degree = jnp.broadcast_to(degree.reshape(-1, 1), seeds.shape)
+    degree = jnp.broadcast_to(degree.reshape(-1, 1), seeds16.shape)
     width = BW * block_rows
     z = lax.axis_index("hub").astype(jnp.int32).reshape(1)
-    current = seeds.astype(jnp.bfloat16)
-    seeds16 = current
-    owned = current[hub_rows]
+    current = seeds16
+    owned = current.at[hub_rows].get(mode="promise_in_bounds")
     p1, p3, pc = payloads(current, owned, z[0], width)
     fast = fast_path(owned, block_rows)
     pick = (hub_rows[:, None] == jnp.arange(current.shape[0], dtype=hub_rows.dtype)[None, :]).astype(jnp.bfloat16)

time: 96.8 us -> 96.8 us (level)
    convert_element_type x2 -> x1, other arithmetic: 1.96 us -> 0.81 us  [body(): seeds16 = seed_mask.astype(seed_scores.dtype)[:, None] * seed_scores]
    mul x0 -> x1, other arithmetic: none -> 1.15 us  [body(): seeds16 = seed_mask.astype(seed_scores.dtype)[:, None] * seed_scores]
where the time goes in v15:
time: 96.8 us; the launch traced here: 95.6 us
  starting transfers between devices  37.3 us (39%)
  Pallas kernels  29.4 us (30%)
  local copies, waits for them, and re-layouts  11.4 us (12%)
  waiting for transfers between devices  8.7 us (9%)
  other arithmetic  8.18 us (8%)
    pallas_call x3, Pallas kernels, hub_call(): pl.pallas_call(functools.partial(hub_kernel, n_hub, width, final), cost_e...  15.3 us
    pallas_call x3, Pallas kernels, band_call(): pl.pallas_call(functools.partial(band_kernel, fast, n_own), cost_estimate...  14.1 us
    ppermute x12, starting transfers between devices, exchange(): lax.ppermute(buf, AXES, pairs(m))  13.3 us
    ppermute x3, starting transfers between devices, exchange(): rc = lax.ppermute(pc, AXES, cross)  13.1 us
    unnamed x58, local copies, waits for them, and re-layouts  7.62 us
    ppermute x3, starting transfers between devices, exchange(): r1 = lax.ppermute(p1, AXES, pairs(1))  7.53 us
    ppermute x12, waiting for transfers between devices, exchange(): lax.ppermute(buf, AXES, pairs(m))  5.4 us
    ppermute x3, waiting for transfers between devices, exchange(): r1 = lax.ppermute(p1, AXES, pairs(1))  3.27 us
  transfers between devices with their start and end apart: 24, of which 6 were waited for; matrix products, arithmetic and copies ran while one was open for 12% of the time, Pallas kernels for 15%

profile of v15, /device:TPU:5, one launch (start us, length us, event | category | flops | bytes accessed | tf_op | source)
XLA Modules:
  0.0 95.6 jit_solution(8659756023419486445)
XLA Ops:
  3.4 2.4 %collective-permute-start.1 = (bf16[128,128]{1,0:T(8,128)(2,1)S(1)}, bf16[128,128]{1,0:T(8,128)(2,1)S(1)}, u32[]{:S(2)}, u32[]{:S(2)}) collective-permute-start(bf16[128,128]{1,0:T(8,128)(2,1)S(1)} %gather_fusion), channel_id=1, source_target_pairs={{0,2},{1,3},{2,0},{3,1},{4,6},{5,7},{6,4},{7,5},{8,10},{9,11},{10,... | collective-permute-start | bytes 98312 | tf_op jit(solution)/shard_map/ppermute | solution.py:50
  5.8 1.4 %collective-permute-start = (bf16[384,128]{1,0:T(8,128)(2,1)S(1)}, bf16[384,128]{1,0:T(8,128)(2,1)S(1)}, u32[]{:S(2)}, u32[]{:S(2)}) collective-permute-start(bf16[384,128]{1,0:T(8,128)(2,1)S(1)} %get-tuple-element.67), channel_id=1, source_target_pairs={{0,1},{1,0},{2,3},{3,2},{4,5},{5,4},{6,7},{7,6},{8,9},{9,8},{10,11... | collective-permute-start | bytes 294920 | tf_op jit(solution)/shard_map/ppermute | solution.py:51
  7.1 6.6 %collective-permute-start.3 = (bf16[256,128]{1,0:T(8,128)(2,1)S(1)}, bf16[256,128]{1,0:T(8,128)(2,1)S(1)}, u32[]{:S(2)}, u32[]{:S(2)}) collective-permute-start(bf16[256,128]{1,0:T(8,128)(2,1)S(1)} %get-tuple-element.63), channel_id=1, source_target_pairs={{3,4},{7,8},{11,12},{15,16},{19,20},{23,24},{27,28},{4,3},{8,7},{1... | collective-permute-start | bytes 196616 | tf_op jit(solution)/shard_map/ppermute | solution.py:55
  13.7 1.5 %fusion.rest_6_ = bf16[128,1024]{1,0:T(8,128)(2,1)} fusion(s32[128]{0:T(128)} %param.14), kind=kLoop, calls=%fused_computation.5 | loop fusion | flops 262144 | bytes 262656 | tf_op jit(solution)/shard_map/convert_element_type | solution.py:299
  15.2 2.2 %convert_reduce_fusion = f32[8,128]{1,0:T(8,128)S(1)} fusion(bf16[8,10,128,128]{3,2,1,0:T(8,128)(2,1)} %rest_3_.5), kind=kLoop, calls=%fused_computation.2 | loop fusion | flops 2620416 | bytes 2625536 | tf_op jit(solution)/shard_map/reduce_sum | solution.py:289
  23.5 4.7 %shard_map.82.rest_3_ = f32[1024,128]{1,0:T(8,128)} custom-call(s32[1]{0:T(128)} %bitcast.z_ref, s32[80]{0:T(128)} %reshape.26.off_ref, bf16[1024,128]{1,0:T(8,128)(2,1)} %copy-done.2, bf16[384,128]{1,0:T(8,128)(2,1)} %copy-done.13, bf16[384,128]{1,0:T(8,128)(2,1)} %copy-done.14, bf16[256,128]{1,0:T(8,128)(2,1)} %copy-done.15, bf16[8,10,128,128]{3,2,1,0:T(8,128)(2,1)} %rest_3_.5), custom_call_target="tpu_custom_call" | custom-call | flops 335544320 | bytes 3670016 | tf_op jit(solution)/shard_map/pallas_call | solution.py:156
  30.3 1.5 %collective-permute-done.7.rest_1_ = bf16[16,128,128]{2,1,0:T(8,128)(2,1)S(1)} collective-permute-done((bf16[16,128,128]{2,1,0:T(8,128)(2,1)S(1)}, bf16[16,128,128]{2,1,0:T(8,128)(2,1)S(1)}, u32[]{:S(2)}, u32[]{:S(2)}) %collective-permute-start.7) | collective-permute-done | bytes 524320 | tf_op jit(solution)/shard_map/ppermute | solution.py:65
  32.7 5.3 %shard_map.83 = (bf16[1024,128]{1,0:T(8,128)(2,1)}, bf16[128,128]{1,0:T(8,128)(2,1)}, bf16[384,128]{1,0:T(8,128)(2,1)}, bf16[384,128]{1,0:T(8,128)(2,1)}, bf16[256,128]{1,0:T(8,128)(2,1)}) custom-call(s32[1]{0:T(128)} %bitcast.z_ref, s32[48]{0:T(128)} %gather_fusion.1, bf16[16,128,128]{2,1,0:T(8,128)(2,1)} %copy-done.3, bf16[16,128,128]{2,1,0:T(8,128)(2,1)} %copy-done.7, ...), custom_call_target="tpu_custom_call" | custom-call | flops 201326592 | bytes 4718592 | tf_op jit(solution)/shard_map/pallas_call | solution.py:256
  39.1 3.2 %collective-permute-start.8 = (bf16[384,128]{1,0:T(8,128)(2,1)}, bf16[384,128]{1,0:T(8,128)(2,1)S(1)}, u32[]{:S(2)}, u32[]{:S(2)}) collective-permute-start(bf16[384,128]{1,0:T(8,128)(2,1)} %get-tuple-element.46), channel_id=1, source_target_pairs={{0,1},{1,0},{2,3},{3,2},{4,5},{5,4},{6,7},{7,6},{8,9},{9,8},{10,11... | collective-permute-start | bytes 294920 | tf_op jit(solution)/shard_map/ppermute | solution.py:51
  42.3 3.3 %collective-permute-start.11 = (bf16[256,128]{1,0:T(8,128)(2,1)}, bf16[256,128]{1,0:T(8,128)(2,1)S(1)}, u32[]{:S(2)}, u32[]{:S(2)}) collective-permute-start(bf16[256,128]{1,0:T(8,128)(2,1)} %get-tuple-element.49), channel_id=1, source_target_pairs={{3,4},{7,8},{11,12},{15,16},{19,20},{23,24},{27,28},{4,3},{8,7},{1... | collective-permute-start | bytes 196616 | tf_op jit(solution)/shard_map/ppermute | solution.py:55
  45.7 1.6 %collective-permute-done.8.rest_0_ = bf16[384,128]{1,0:T(8,128)(2,1)S(1)} collective-permute-done((bf16[384,128]{1,0:T(8,128)(2,1)}, bf16[384,128]{1,0:T(8,128)(2,1)S(1)}, u32[]{:S(2)}, u32[]{:S(2)}) %collective-permute-start.8) | collective-permute-done | bytes 98336 | tf_op jit(solution)/shard_map/ppermute | solution.py:51
  49.3 1.5 %collective-permute-start.14 = (bf16[4,128,128]{2,1,0:T(8,128)(2,1)S(1)}, bf16[4,128,128]{2,1,0:T(8,128)(2,1)S(1)}, u32[]{:S(2)}, u32[]{:S(2)}) collective-permute-start(bf16[4,128,128]{2,1,0:T(8,128)(2,1)S(1)} %pad_maximum_fusion.1), channel_id=1, source_target_pairs={{0,24},{1,25},{2,26},{3,27},{4,28},{5,29},{6,30},{7,31},{8,16},{9,... | collective-permute-start | bytes 393224 | tf_op jit(solution)/shard_map/ppermute | solution.py:65
  51.4 4.7 %shard_map.84.rest_3_ = f32[1024,128]{1,0:T(8,128)} custom-call(s32[1]{0:T(128)} %bitcast.z_ref, s32[80]{0:T(128)} %reshape.26.off_ref, bf16[1024,128]{1,0:T(8,128)(2,1)} %get-tuple-element.48.cur_hbm, bf16[384,128]{1,0:T(8,128)(2,1)} %copy-done.12, bf16[384,128]{1,0:T(8,128)(2,1)} %copy-done.10, bf16[256,128]{1,0:T(8,128)(2,1)} %copy-done.17, ...), custom_call_target="tpu_custom_call" | custom-call | flops 335544320 | bytes 3670016 | tf_op jit(solution)/shard_map/pallas_call | solution.py:156
  57.0 2.3 %collective-permute-start.15 = (bf16[16,128,128]{2,1,0:T(8,128)(2,1)S(1)}, bf16[16,128,128]{2,1,0:T(8,128)(2,1)S(1)}, u32[]{:S(2)}, u32[]{:S(2)}) collective-permute-start(bf16[16,128,128]{2,1,0:T(8,128)(2,1)S(1)} %constant_dynamic-update-slice_fusion.7.rest_0_), channel_id=1, source_target_pairs={{0,4},{1,5},{2,6},{3,7},{4,0},{5,1},{6,2},{7,3},{8,12},{9,13},{10,... | collective-permute-start | bytes 1572872 | tf_op jit(solution)/shard_map/ppermute | solution.py:65
  59.3 1.5 %collective-permute-done.15.rest_1_ = bf16[16,128,128]{2,1,0:T(8,128)(2,1)S(1)} collective-permute-done((bf16[16,128,128]{2,1,0:T(8,128)(2,1)S(1)}, bf16[16,128,128]{2,1,0:T(8,128)(2,1)S(1)}, u32[]{:S(2)}, u32[]{:S(2)}) %collective-permute-start.15) | collective-permute-done | bytes 524320 | tf_op jit(solution)/shard_map/ppermute | solution.py:65
  61.7 5.3 %shard_map.85 = (bf16[1024,128]{1,0:T(8,128)(2,1)}, bf16[128,128]{1,0:T(8,128)(2,1)}, bf16[384,128]{1,0:T(8,128)(2,1)}, bf16[384,128]{1,0:T(8,128)(2,1)}, bf16[256,128]{1,0:T(8,128)(2,1)}) custom-call(s32[1]{0:T(128)} %bitcast.z_ref, s32[48]{0:T(128)} %gather_fusion.1, bf16[16,128,128]{2,1,0:T(8,128)(2,1)} %copy-done.4, bf16[16,128,128]{2,1,0:T(8,128)(2,1)} %copy-done.6, ...), custom_call_target="tpu_custom_call" | custom-call | flops 201326592 | bytes 4718592 | tf_op jit(solution)/shard_map/pallas_call | solution.py:256
  68.3 3.0 %collective-permute-start.16 = (bf16[384,128]{1,0:T(8,128)(2,1)}, bf16[384,128]{1,0:T(8,128)(2,1)S(1)}, u32[]{:S(2)}, u32[]{:S(2)}) collective-permute-start(bf16[384,128]{1,0:T(8,128)(2,1)} %get-tuple-element.55), channel_id=1, source_target_pairs={{0,1},{1,0},{2,3},{3,2},{4,5},{5,4},{6,7},{7,6},{8,9},{9,8},{10,11... | collective-permute-start | bytes 294920 | tf_op jit(solution)/shard_map/ppermute | solution.py:51
  71.3 3.2 %collective-permute-start.19 = (bf16[256,128]{1,0:T(8,128)(2,1)}, bf16[256,128]{1,0:T(8,128)(2,1)S(1)}, u32[]{:S(2)}, u32[]{:S(2)}) collective-permute-start(bf16[256,128]{1,0:T(8,128)(2,1)} %get-tuple-element.58), channel_id=1, source_target_pairs={{3,4},{7,8},{11,12},{15,16},{19,20},{23,24},{27,28},{4,3},{8,7},{1... | collective-permute-start | bytes 196616 | tf_op jit(solution)/shard_map/ppermute | solution.py:55
  74.5 1.7 %collective-permute-done.16.rest_0_ = bf16[384,128]{1,0:T(8,128)(2,1)S(1)} collective-permute-done((bf16[384,128]{1,0:T(8,128)(2,1)}, bf16[384,128]{1,0:T(8,128)(2,1)S(1)}, u32[]{:S(2)}, u32[]{:S(2)}) %collective-permute-start.16) | collective-permute-done | bytes 98336 | tf_op jit(solution)/shard_map/ppermute | solution.py:51
  77.8 2.0 %collective-permute-start.22 = (bf16[4,128,128]{2,1,0:T(8,128)(2,1)S(1)}, bf16[4,128,128]{2,1,0:T(8,128)(2,1)S(1)}, u32[]{:S(2)}, u32[]{:S(2)}) collective-permute-start(bf16[4,128,128]{2,1,0:T(8,128)(2,1)S(1)} %pad_maximum_fusion.2), channel_id=1, source_target_pairs={{0,24},{1,25},{2,26},{3,27},{4,28},{5,29},{6,30},{7,31},{8,16},{9,... | collective-permute-start | bytes 393224 | tf_op jit(solution)/shard_map/ppermute | solution.py:65
  80.3 4.7 %shard_map.86.rest_3_ = f32[1024,128]{1,0:T(8,128)} custom-call(s32[1]{0:T(128)} %bitcast.z_ref, s32[80]{0:T(128)} %reshape.26.off_ref, bf16[1024,128]{1,0:T(8,128)(2,1)} %get-tuple-element.57.cur_hbm, bf16[384,128]{1,0:T(8,128)(2,1)} %copy-done.11, bf16[384,128]{1,0:T(8,128)(2,1)} %copy-done.9, bf16[256,128]{1,0:T(8,128)(2,1)} %copy-done.16, ...), custom_call_target="tpu_custom_call" | custom-call | flops 335544320 | bytes 3670016 | tf_op jit(solution)/shard_map/pallas_call | solution.py:156
  85.9 2.4 %collective-permute-start.23 = (bf16[16,128,128]{2,1,0:T(8,128)(2,1)S(1)}, bf16[16,128,128]{2,1,0:T(8,128)(2,1)S(1)}, u32[]{:S(2)}, u32[]{:S(2)}) collective-permute-start(bf16[16,128,128]{2,1,0:T(8,128)(2,1)S(1)} %constant_dynamic-update-slice_fusion.14.rest_0_), channel_id=1, source_target_pairs={{0,4},{1,5},{2,6},{3,7},{4,0},{5,1},{6,2},{7,3},{8,12},{9,13},{10,... | collective-permute-start | bytes 1572872 | tf_op jit(solution)/shard_map/ppermute | solution.py:65
  88.3 1.5 %collective-permute-done.23.rest_1_ = bf16[16,128,128]{2,1,0:T(8,128)(2,1)S(1)} collective-permute-done((bf16[16,128,128]{2,1,0:T(8,128)(2,1)S(1)}, bf16[16,128,128]{2,1,0:T(8,128)(2,1)S(1)}, u32[]{:S(2)}, u32[]{:S(2)}) %collective-permute-start.23) | collective-permute-done | bytes 524320 | tf_op jit(solution)/shard_map/ppermute | solution.py:65
  90.6 4.8 %shard_map.87 = f32[1024,128]{1,0:T(8,128)} custom-call(s32[1]{0:T(128)} %bitcast.z_ref, s32[48]{0:T(128)} %gather_fusion.1, bf16[16,128,128]{2,1,0:T(8,128)(2,1)} %copy-done.5, bf16[16,128,128]{2,1,0:T(8,128)(2,1)} %copy-done.8, bf16[8,6,128,128]{3,2,1,0:T(8,128)(2,1)} %rest_2_.5, f32[1024,128]{1,0:T(8,128)} %shard_map.86.rest_3_, ...), custom_call_target="tpu_custom_call" | custom-call | flops 201326592 | bytes 4718592 | tf_op jit(solution)/shard_map/pallas_call | solution.py:256
  (116 shorter events, 23.0 us)
Async XLA Ops:
  3.4 16.3 %collective-permute-start.1 = (bf16[128,128]{1,0:T(8,128)(2,1)S(1)}, bf16[128,128]{1,0:T(8,128)(2,1)S(1)}, u32[]{:S(2)}, u32[]{:S(2)}) collective-permute-start(bf16[128,128]{1,0:T(8,128)(2,1)S(1)} %gather_fusion), channel_id=1, source_target_pairs={{0,2},{1,3},{2,0},{3,1},{4,6},{5,7},{6,4},{7,5},{8,10},{9,11},{10,... | collective-permute-start | bytes 98312 | tf_op jit(solution)/shard_map/ppermute | solution.py:50
  5.8 13.9 %collective-permute-start = (bf16[384,128]{1,0:T(8,128)(2,1)S(1)}, bf16[384,128]{1,0:T(8,128)(2,1)S(1)}, u32[]{:S(2)}, u32[]{:S(2)}) collective-permute-start(bf16[384,128]{1,0:T(8,128)(2,1)S(1)} %get-tuple-element.67), channel_id=1, source_target_pairs={{0,1},{1,0},{2,3},{3,2},{4,5},{5,4},{6,7},{7,6},{8,9},{9,8},{10,11... | collective-permute-start | bytes 294920 | tf_op jit(solution)/shard_map/ppermute | solution.py:51
  7.1 12.6 %collective-permute-start.2 = (bf16[384,128]{1,0:T(8,128)(2,1)S(1)}, bf16[384,128]{1,0:T(8,128)(2,1)S(1)}, u32[]{:S(2)}, u32[]{:S(2)}) collective-permute-start(bf16[384,128]{1,0:T(8,128)(2,1)S(1)} %get-tuple-element.66), channel_id=1, source_target_pairs={{0,3},{1,2},{2,1},{3,0},{4,7},{5,6},{6,5},{7,4},{8,11},{9,10},{10,... | collective-permute-start | bytes 294920 | tf_op jit(solution)/shard_map/ppermute | solution.py:49
  7.1 12.6 %collective-permute-start.3 = (bf16[256,128]{1,0:T(8,128)(2,1)S(1)}, bf16[256,128]{1,0:T(8,128)(2,1)S(1)}, u32[]{:S(2)}, u32[]{:S(2)}) collective-permute-start(bf16[256,128]{1,0:T(8,128)(2,1)S(1)} %get-tuple-element.63), channel_id=1, source_target_pairs={{3,4},{7,8},{11,12},{15,16},{19,20},{23,24},{27,28},{4,3},{8,7},{1... | collective-permute-start | bytes 196616 | tf_op jit(solution)/shard_map/ppermute | solution.py:55
  20.8 8.2 %collective-permute-start.4 = (bf16[4,128,128]{2,1,0:T(8,128)(2,1)S(1)}, bf16[4,128,128]{2,1,0:T(8,128)(2,1)S(1)}, u32[]{:S(2)}, u32[]{:S(2)}) collective-permute-start(bf16[4,128,128]{2,1,0:T(8,128)(2,1)S(1)} %pad_maximum_fusion), channel_id=1, source_target_pairs={{0,8},{1,9},{2,10},{3,11},{4,12},{5,13},{6,14},{7,15},{8,0},{9,1},... | collective-permute-start | bytes 393224 | tf_op jit(solution)/shard_map/ppermute | solution.py:65
  22.0 7.7 %collective-permute-start.5 = (bf16[4,128,128]{2,1,0:T(8,128)(2,1)S(1)}, bf16[4,128,128]{2,1,0:T(8,128)(2,1)S(1)}, u32[]{:S(2)}, u32[]{:S(2)}) collective-permute-start(bf16[4,128,128]{2,1,0:T(8,128)(2,1)S(1)} %pad_maximum_fusion), channel_id=1, source_target_pairs={{0,16},{1,17},{2,18},{3,19},{4,20},{5,21},{6,22},{7,23},{8,24},{9,... | collective-permute-start | bytes 393224 | tf_op jit(solution)/shard_map/ppermute | solution.py:65
  22.3 7.5 %collective-permute-start.6 = (bf16[4,128,128]{2,1,0:T(8,128)(2,1)S(1)}, bf16[4,128,128]{2,1,0:T(8,128)(2,1)S(1)}, u32[]{:S(2)}, u32[]{:S(2)}) collective-permute-start(bf16[4,128,128]{2,1,0:T(8,128)(2,1)S(1)} %pad_maximum_fusion), channel_id=1, source_target_pairs={{0,24},{1,25},{2,26},{3,27},{4,28},{5,29},{6,30},{7,31},{8,16},{9,... | collective-permute-start | bytes 393224 | tf_op jit(solution)/shard_map/ppermute | solution.py:65
  29.9 2.0 %collective-permute-start.7 = (bf16[16,128,128]{2,1,0:T(8,128)(2,1)S(1)}, bf16[16,128,128]{2,1,0:T(8,128)(2,1)S(1)}, u32[]{:S(2)}, u32[]{:S(2)}) collective-permute-start(bf16[16,128,128]{2,1,0:T(8,128)(2,1)S(1)} %constant_dynamic-update-slice_fusion.rest_0_), channel_id=1, source_target_pairs={{0,4},{1,5},{2,6},{3,7},{4,0},{5,1},{6,2},{7,3},{8,12},{9,13},{10,... | collective-permute-start | bytes 1572872 | tf_op jit(solution)/shard_map/ppermute | solution.py:65
  37.9 7.7 %collective-permute-start.10 = (bf16[384,128]{1,0:T(8,128)(2,1)}, bf16[384,128]{1,0:T(8,128)(2,1)S(1)}, u32[]{:S(2)}, u32[]{:S(2)}) collective-permute-start(bf16[384,128]{1,0:T(8,128)(2,1)} %get-tuple-element.47), channel_id=1, source_target_pairs={{0,3},{1,2},{2,1},{3,0},{4,7},{5,6},{6,5},{7,4},{8,11},{9,10},{10,... | collective-permute-start | bytes 294920 | tf_op jit(solution)/shard_map/ppermute | solution.py:49
  39.1 8.2 %collective-permute-start.9 = (bf16[128,128]{1,0:T(8,128)(2,1)}, bf16[128,128]{1,0:T(8,128)(2,1)S(1)}, u32[]{:S(2)}, u32[]{:S(2)}) collective-permute-start(bf16[128,128]{1,0:T(8,128)(2,1)} %get-tuple-element.45), channel_id=1, source_target_pairs={{0,2},{1,3},{2,0},{3,1},{4,6},{5,7},{6,4},{7,5},{8,10},{9,11},{10,... | collective-permute-start | bytes 98312 | tf_op jit(solution)/shard_map/ppermute | solution.py:50
  39.1 8.2 %collective-permute-start.8 = (bf16[384,128]{1,0:T(8,128)(2,1)}, bf16[384,128]{1,0:T(8,128)(2,1)S(1)}, u32[]{:S(2)}, u32[]{:S(2)}) collective-permute-start(bf16[384,128]{1,0:T(8,128)(2,1)} %get-tuple-element.46), channel_id=1, source_target_pairs={{0,1},{1,0},{2,3},{3,2},{4,5},{5,4},{6,7},{7,6},{8,9},{9,8},{10,11... | collective-permute-start | bytes 294920 | tf_op jit(solution)/shard_map/ppermute | solution.py:51
  42.3 8.5 %collective-permute-start.11 = (bf16[256,128]{1,0:T(8,128)(2,1)}, bf16[256,128]{1,0:T(8,128)(2,1)S(1)}, u32[]{:S(2)}, u32[]{:S(2)}) collective-permute-start(bf16[256,128]{1,0:T(8,128)(2,1)} %get-tuple-element.49), channel_id=1, source_target_pairs={{3,4},{7,8},{11,12},{15,16},{19,20},{23,24},{27,28},{4,3},{8,7},{1... | collective-permute-start | bytes 196616 | tf_op jit(solution)/shard_map/ppermute | solution.py:55
  48.1 8.8 %collective-permute-start.12 = (bf16[4,128,128]{2,1,0:T(8,128)(2,1)S(1)}, bf16[4,128,128]{2,1,0:T(8,128)(2,1)S(1)}, u32[]{:S(2)}, u32[]{:S(2)}) collective-permute-start(bf16[4,128,128]{2,1,0:T(8,128)(2,1)S(1)} %pad_maximum_fusion.1), channel_id=1, source_target_pairs={{0,8},{1,9},{2,10},{3,11},{4,12},{5,13},{6,14},{7,15},{8,0},{9,1},... | collective-permute-start | bytes 393224 | tf_op jit(solution)/shard_map/ppermute | solution.py:65
  49.0 7.9 %collective-permute-start.13 = (bf16[4,128,128]{2,1,0:T(8,128)(2,1)S(1)}, bf16[4,128,128]{2,1,0:T(8,128)(2,1)S(1)}, u32[]{:S(2)}, u32[]{:S(2)}) collective-permute-start(bf16[4,128,128]{2,1,0:T(8,128)(2,1)S(1)} %pad_maximum_fusion.1), channel_id=1, source_target_pairs={{0,16},{1,17},{2,18},{3,19},{4,20},{5,21},{6,22},{7,23},{8,24},{9,... | collective-permute-start | bytes 393224 | tf_op jit(solution)/shard_map/ppermute | solution.py:65
  49.3 7.6 %collective-permute-start.14 = (bf16[4,128,128]{2,1,0:T(8,128)(2,1)S(1)}, bf16[4,128,128]{2,1,0:T(8,128)(2,1)S(1)}, u32[]{:S(2)}, u32[]{:S(2)}) collective-permute-start(bf16[4,128,128]{2,1,0:T(8,128)(2,1)S(1)} %pad_maximum_fusion.1), channel_id=1, source_target_pairs={{0,24},{1,25},{2,26},{3,27},{4,28},{5,29},{6,30},{7,31},{8,16},{9,... | collective-permute-start | bytes 393224 | tf_op jit(solution)/shard_map/ppermute | solution.py:65
  57.0 3.8 %collective-permute-start.15 = (bf16[16,128,128]{2,1,0:T(8,128)(2,1)S(1)}, bf16[16,128,128]{2,1,0:T(8,128)(2,1)S(1)}, u32[]{:S(2)}, u32[]{:S(2)}) collective-permute-start(bf16[16,128,128]{2,1,0:T(8,128)(2,1)S(1)} %constant_dynamic-update-slice_fusion.7.rest_0_), channel_id=1, source_target_pairs={{0,4},{1,5},{2,6},{3,7},{4,0},{5,1},{6,2},{7,3},{8,12},{9,13},{10,... | collective-permute-start | bytes 1572872 | tf_op jit(solution)/shard_map/ppermute | solution.py:65
  66.9 7.6 %collective-permute-start.18 = (bf16[384,128]{1,0:T(8,128)(2,1)}, bf16[384,128]{1,0:T(8,128)(2,1)S(1)}, u32[]{:S(2)}, u32[]{:S(2)}) collective-permute-start(bf16[384,128]{1,0:T(8,128)(2,1)} %get-tuple-element.56), channel_id=1, source_target_pairs={{0,3},{1,2},{2,1},{3,0},{4,7},{5,6},{6,5},{7,4},{8,11},{9,10},{10,... | collective-permute-start | bytes 294920 | tf_op jit(solution)/shard_map/ppermute | solution.py:49
  67.8 8.4 %collective-permute-start.17 = (bf16[128,128]{1,0:T(8,128)(2,1)}, bf16[128,128]{1,0:T(8,128)(2,1)S(1)}, u32[]{:S(2)}, u32[]{:S(2)}) collective-permute-start(bf16[128,128]{1,0:T(8,128)(2,1)} %get-tuple-element.54), channel_id=1, source_target_pairs={{0,2},{1,3},{2,0},{3,1},{4,6},{5,7},{6,4},{7,5},{8,10},{9,11},{10,... | collective-permute-start | bytes 98312 | tf_op jit(solution)/shard_map/ppermute | solution.py:50
  68.3 7.8 %collective-permute-start.16 = (bf16[384,128]{1,0:T(8,128)(2,1)}, bf16[384,128]{1,0:T(8,128)(2,1)S(1)}, u32[]{:S(2)}, u32[]{:S(2)}) collective-permute-start(bf16[384,128]{1,0:T(8,128)(2,1)} %get-tuple-element.55), channel_id=1, source_target_pairs={{0,1},{1,0},{2,3},{3,2},{4,5},{5,4},{6,7},{7,6},{8,9},{9,8},{10,11... | collective-permute-start | bytes 294920 | tf_op jit(solution)/shard_map/ppermute | solution.py:51
  71.3 8.4 %collective-permute-start.19 = (bf16[256,128]{1,0:T(8,128)(2,1)}, bf16[256,128]{1,0:T(8,128)(2,1)S(1)}, u32[]{:S(2)}, u32[]{:S(2)}) collective-permute-start(bf16[256,128]{1,0:T(8,128)(2,1)} %get-tuple-element.58), channel_id=1, source_target_pairs={{3,4},{7,8},{11,12},{15,16},{19,20},{23,24},{27,28},{4,3},{8,7},{1... | collective-permute-start | bytes 196616 | tf_op jit(solution)/shard_map/ppermute | solution.py:55
  77.0 8.8 %collective-permute-start.20 = (bf16[4,128,128]{2,1,0:T(8,128)(2,1)S(1)}, bf16[4,128,128]{2,1,0:T(8,128)(2,1)S(1)}, u32[]{:S(2)}, u32[]{:S(2)}) collective-permute-start(bf16[4,128,128]{2,1,0:T(8,128)(2,1)S(1)} %pad_maximum_fusion.2), channel_id=1, source_target_pairs={{0,8},{1,9},{2,10},{3,11},{4,12},{5,13},{6,14},{7,15},{8,0},{9,1},... | collective-permute-start | bytes 393224 | tf_op jit(solution)/shard_map/ppermute | solution.py:65
  77.4 8.4 %collective-permute-start.21 = (bf16[4,128,128]{2,1,0:T(8,128)(2,1)S(1)}, bf16[4,128,128]{2,1,0:T(8,128)(2,1)S(1)}, u32[]{:S(2)}, u32[]{:S(2)}) collective-permute-start(bf16[4,128,128]{2,1,0:T(8,128)(2,1)S(1)} %pad_maximum_fusion.2), channel_id=1, source_target_pairs={{0,16},{1,17},{2,18},{3,19},{4,20},{5,21},{6,22},{7,23},{8,24},{9,... | collective-permute-start | bytes 393224 | tf_op jit(solution)/shard_map/ppermute | solution.py:65
  77.8 8.1 %collective-permute-start.22 = (bf16[4,128,128]{2,1,0:T(8,128)(2,1)S(1)}, bf16[4,128,128]{2,1,0:T(8,128)(2,1)S(1)}, u32[]{:S(2)}, u32[]{:S(2)}) collective-permute-start(bf16[4,128,128]{2,1,0:T(8,128)(2,1)S(1)} %pad_maximum_fusion.2), channel_id=1, source_target_pairs={{0,24},{1,25},{2,26},{3,27},{4,28},{5,29},{6,30},{7,31},{8,16},{9,... | collective-permute-start | bytes 393224 | tf_op jit(solution)/shard_map/ppermute | solution.py:65
  85.9 3.9 %collective-permute-start.23 = (bf16[16,128,128]{2,1,0:T(8,128)(2,1)S(1)}, bf16[16,128,128]{2,1,0:T(8,128)(2,1)S(1)}, u32[]{:S(2)}, u32[]{:S(2)}) collective-permute-start(bf16[16,128,128]{2,1,0:T(8,128)(2,1)S(1)} %constant_dynamic-update-slice_fusion.14.rest_0_), channel_id=1, source_target_pairs={{0,4},{1,5},{2,6},{3,7},{4,0},{5,1},{6,2},{7,3},{8,12},{9,13},{10,... | collective-permute-start | bytes 1572872 | tf_op jit(solution)/shard_map/ppermute | solution.py:65
  (20 other events, 111.3 us)

commit v16 on v15

--- a/solution.py
+++ b/solution.py
@@ -35,7 +35,7 @@
     return p1, p3, pc
 
 
-def exchange(current, owned, p1, p3, pc, hub_blocks, width, block_rows, middle, prep):
+def exchange(current, owned, p1, p3, pc, hub_blocks, width, block_rows, first, middle, prep):
     count = lax.axis_size(AXES)
     if not fast_path(owned, block_rows):
         forward = [(i, i + 1) for i in range(count - 1)]
@@ -43,7 +43,8 @@
         low = lax.ppermute(current[current.shape[0] - width:], AXES, forward)
         high = lax.ppermute(current[:width], AXES, backward)
         hub_all = lax.all_gather(owned, AXES, axis=0, tiled=True)
-        return middle((low, high)), [hub_all.reshape(-1, block_rows, owned.shape[1])], prep
+        done = (first(), middle((low, high)))
+        return done, [hub_all.reshape(-1, block_rows, owned.shape[1])], prep
     me = lax.axis_index(AXES)
     pairs = lambda m: [(i, i ^ m) for i in range(count)]
     r3 = lax.ppermute(p3, AXES, pairs(3))
@@ -53,8 +54,7 @@
     cross = [(4 * g + 3, 4 * g + 4) for g in range(groups - 1)]
     cross += [(4 * g + 4, 4 * g + 3) for g in range(groups - 1)]
     rc = lax.ppermute(pc, AXES, cross)
-    if prep is not None:
-        (r1, r2, r3, rc), prep = lax.optimization_barrier(((r1, r2, r3, rc), prep))
+    (r1, r2, r3, rc), (inner, prep) = lax.optimization_barrier(((r1, r2, r3, rc), (first(), prep)))
     rows = block_rows
     buf = jnp.concatenate([owned[None], r1[None, :rows], r2[None], r3[None, :rows]], 0)
     offs = [0, 1, 2, 3]
@@ -71,68 +71,81 @@
         if r + 2 < len(rounds):
             buf = jnp.concatenate(pieces, 0)
     assert sorted(offs) == list(range(count))
-    where = np.zeros(count, np.int32)
-    for p, o in enumerate(offs):
-        where[o] = p
-    return done, pieces, prep
-
-
-def band_kernel(fast, n_own, z_ref, off_ref, cur_hbm, *rest):
-    if fast:
+    return (inner, done), pieces, prep
+
+
+def rim_blocks(blocks):
+    return sorted(set(range(min(BW, blocks))) | set(range(max(blocks - BW, 0), blocks)))
+
+
+def band_kernel(fast, n_own, rims_part, z_ref, off_ref, cur_hbm, *rest):
+    if not rims_part:
+        bt_hbm, out_ref, ext, bt, sem = rest
+    elif fast:
         r1_hbm, r3_hbm, rc_hbm, bt_hbm, out_ref, ext, bt, sem = rest
     else:
         low_hbm, high_hbm, bt_hbm, out_ref, ext, bt, sem = rest
-    blocks, k_band, rows = bt.shape[0], bt.shape[1], bt.shape[2]
+    k_band, rows = bt.shape[1], bt.shape[2]
     own = cur_hbm.shape[0]
     width = (ext.shape[0] - own) // 2
-    low_dst = ext.at[pl.ds(0, width)]
-    high_dst = ext.at[pl.ds(width + own, width)]
-    mid = pltpu.make_async_copy(cur_hbm, ext.at[pl.ds(width, own)], sem.at[1])
-    band_copies = [pltpu.make_async_copy(bt_hbm.at[b], bt.at[b], sem.at[3 + b]) for b in range(blocks)]
+    blocks = own // rows
+    chosen = rim_blocks(blocks) if rims_part else list(range(blocks))
+    band_copies = [pltpu.make_async_copy(bt_hbm.at[g], bt.at[i], sem.at[3 + i]) for i, g in enumerate(chosen)]
     band_copies[0].start()
-    mid.start()
-    if fast:
-        z = z_ref[0]
-        low_r1 = pltpu.make_async_copy(r1_hbm.at[pl.ds(n_own, width)], low_dst, sem.at[0])
-        low_r3 = pltpu.make_async_copy(r3_hbm.at[pl.ds(n_own, width)], low_dst, sem.at[0])
-        low_rc = pltpu.make_async_copy(rc_hbm, low_dst, sem.at[0])
-        high_r1 = pltpu.make_async_copy(r1_hbm.at[pl.ds(n_own, width)], high_dst, sem.at[2])
-        high_r3 = pltpu.make_async_copy(r3_hbm.at[pl.ds(n_own, width)], high_dst, sem.at[2])
-        high_rc = pltpu.make_async_copy(rc_hbm, high_dst, sem.at[2])
-
-        @pl.when(z == 0)
-        def _():
-            low_rc.start()
-            high_r1.start()
-
-        @pl.when(z == 1)
-        def _():
-            low_r1.start()
-            high_r3.start()
-
-        @pl.when(z == 2)
-        def _():
-            low_r3.start()
-            high_r1.start()
-
-        @pl.when(z == 3)
-        def _():
-            low_r1.start()
-            high_rc.start()
-
-        low_wait, high_wait = low_rc, high_rc
+    if not rims_part:
+        mid = pltpu.make_async_copy(cur_hbm, ext.at[pl.ds(width, own)], sem.at[1])
+        mid.start()
+        for i in range(1, len(chosen)):
+            band_copies[i].start()
+        zeros = jnp.zeros((width, ext.shape[1]), ext.dtype)
+        ext[pl.ds(0, width), :] = zeros
+        ext[pl.ds(width + own, width), :] = zeros
+        mid.wait()
     else:
-        low_wait = pltpu.make_async_copy(low_hbm, low_dst, sem.at[0])
-        high_wait = pltpu.make_async_copy(high_hbm, high_dst, sem.at[2])
-        low_wait.start()
-        high_wait.start()
-    for b in range(1, blocks):
-        band_copies[b].start()
-    mid.wait()
-    low_wait.wait()
-    high_wait.wait()
-    for b in range(blocks):
-        band_copies[b].wait()
+        low_dst = ext.at[pl.ds(0, width)]
+        high_dst = ext.at[pl.ds(width + own, width)]
+        if fast:
+            z = z_ref[0]
+            low_r1 = pltpu.make_async_copy(r1_hbm.at[pl.ds(n_own, width)], low_dst, sem.at[0])
+            low_r3 = pltpu.make_async_copy(r3_hbm.at[pl.ds(n_own, width)], low_dst, sem.at[0])
+            low_rc = pltpu.make_async_copy(rc_hbm, low_dst, sem.at[0])
+            high_r1 = pltpu.make_async_copy(r1_hbm.at[pl.ds(n_own, width)], high_dst, sem.at[2])
+            high_r3 = pltpu.make_async_copy(r3_hbm.at[pl.ds(n_own, width)], high_dst, sem.at[2])
+            high_rc = pltpu.make_async_copy(rc_hbm, high_dst, sem.at[2])
+
+            @pl.when(z == 0)
+            def _():
+                low_rc.start()
+                high_r1.start()
+
+            @pl.when(z == 1)
+            def _():
+                low_r1.start()
+                high_r3.start()
+
+            @pl.when(z == 2)
+            def _():
+                low_r3.start()
+                high_r1.start()
+
+            @pl.when(z == 3)
+            def _():
+                low_r1.start()
+                high_rc.start()
+
+            low_wait, high_wait = low_rc, high_rc
+        else:
+            low_wait = pltpu.make_async_copy(low_hbm, low_dst, sem.at[0])
+            high_wait = pltpu.make_async_copy(high_hbm, high_dst, sem.at[2])
+            low_wait.start()
+            high_wait.start()
+        for i in range(1, len(chosen)):
+            band_copies[i].start()
+        ext[pl.ds(width, own), :] = jnp.zeros((own, ext.shape[1]), ext.dtype)
+        low_wait.wait()
+        high_wait.wait()
+    for i, b in enumerate(chosen):
+        band_copies[i].wait()
         acc = jnp.zeros((rows, out_ref.shape[1]), jnp.float32)
 
         def near(k):
@@ -140,29 +153,30 @@
             return ext[pl.ds(pl.multiple_of(n * rows, rows), rows), :]
 
         for k in range(0, k_band - 1, 2):
-            lhs = jnp.concatenate([bt[b, k], bt[b, k + 1]], axis=1)
+            lhs = jnp.concatenate([bt[i, k], bt[i, k + 1]], axis=1)
             rhs = jnp.concatenate([near(k), near(k + 1)], axis=0)
             acc = acc + jnp.dot(lhs, rhs, preferred_element_type=jnp.float32)
         if k_band % 2:
-            acc = acc + jnp.dot(bt[b, k_band - 1], near(k_band - 1), preferred_element_type=jnp.float32)
-        out_ref[pl.ds(b * rows, rows), :] = acc
-
-
-def band_call(z, band_offsets, current, rim_sources, band_tiles, fast, n_own, width):
+            acc = acc + jnp.dot(bt[i, k_band - 1], near(k_band - 1), preferred_element_type=jnp.float32)
+        out_ref[pl.ds(i * rows, rows), :] = acc
+
+
+def band_call(z, band_offsets, current, rim_sources, band_tiles, fast, n_own, width, rims_part):
     blocks, k_band, rows, _ = band_tiles.shape
     classes = current.shape[1]
-    flops = 2 * blocks * k_band * rows * rows * classes
-    bytes_accessed = band_tiles.size * 2 + current.size * 2 * 2 + current.size * 4
+    chosen = len(rim_blocks(blocks)) if rims_part else blocks
+    flops = 2 * chosen * k_band * rows * rows * classes
+    bytes_accessed = chosen * k_band * rows * rows * 2 + current.size * 2 + chosen * rows * classes * 4
     return pl.pallas_call(
-        functools.partial(band_kernel, fast, n_own),
+        functools.partial(band_kernel, fast, n_own, rims_part),
         cost_estimate=pl.CostEstimate(flops=flops, transcendentals=0, bytes_accessed=bytes_accessed),
         in_specs=[SMEM, SMEM] + [ANY] * (1 + len(rim_sources) + 1),
         out_specs=VMEM,
-        out_shape=jax.ShapeDtypeStruct(current.shape, jnp.float32),
+        out_shape=jax.ShapeDtypeStruct((chosen * rows, classes), jnp.float32),
         scratch_shapes=[
             pltpu.VMEM((current.shape[0] + 2 * width, classes), current.dtype),
-            pltpu.VMEM(band_tiles.shape, band_tiles.dtype),
-            pltpu.SemaphoreType.DMA((3 + blocks,)),
+            pltpu.VMEM((chosen,) + band_tiles.shape[1:], band_tiles.dtype),
+            pltpu.SemaphoreType.DMA((3 + chosen,)),
         ],
     )(z, band_offsets.reshape(-1), current, *rim_sources, band_tiles)
 
@@ -170,12 +184,15 @@
 def hub_kernel(n_hub, width, final, z_ref, hidx_ref, *rest):
     hub_hbm = rest[:n_hub]
     if final:
-        (ht_hbm, band_hbm, deg_hbm, seeds_hbm, out_ref, hub, ht, band, deg, seeds, sem) = rest[n_hub:]
+        (ht_hbm, band_hbm, rim_hbm, deg_hbm, seeds_hbm, out_ref, hub, ht, band, rim, deg, seeds, sem) = rest[n_hub:]
     else:
-        (ht_hbm, band_hbm, deg_hbm, seeds_hbm, pick_ref,
+        (ht_hbm, band_hbm, rim_hbm, deg_hbm, seeds_hbm, pick_ref,
          cur_ref, owned_ref, p1_ref, p3_ref, pc_ref,
-         hub, ht, band, deg, seeds, sem) = rest[n_hub:]
+         hub, ht, band, rim, deg, seeds, sem) = rest[n_hub:]
     blocks, k_hub, rows = ht.shape[0], ht.shape[1], ht.shape[2]
+    chosen = rim_blocks(blocks)
+    rim_copy = pltpu.make_async_copy(rim_hbm, rim, sem.at[n_hub + 4 * blocks])
+    rim_copy.start()
     per_block = []
     for b in range(blocks):
         span = pl.ds(b * rows, rows)
@@ -200,6 +217,7 @@
             c.start()
     for c in copies:
         c.wait()
+    rim_copy.wait()
     for b in range(blocks):
         for c in per_block[b]:
             c.wait()
@@ -212,7 +230,10 @@
             acc = acc + jnp.dot(lhs, rhs, preferred_element_type=jnp.float32)
         if k_hub % 2:
             acc = acc + jnp.dot(ht[b, k_hub - 1], blk(k_hub - 1), preferred_element_type=jnp.float32)
-        gathered = (band[span] + acc) / deg[span]
+        near = band[span]
+        if b in chosen:
+            near = near + rim[pl.ds(chosen.index(b) * rows, rows), :]
+        gathered = (near + acc) / deg[span]
         labels = spread_weight * gathered + (1.0 - spread_weight) * seeds[span].astype(jnp.float32)
         if final:
             out_ref[span, :] = labels
@@ -256,18 +277,19 @@
     return pl.pallas_call(
         functools.partial(hub_kernel, n_hub, width, final),
         cost_estimate=pl.CostEstimate(flops=flops, transcendentals=0, bytes_accessed=bytes_accessed),
-        in_specs=[SMEM, SMEM] + [ANY] * (n_hub + 4) + ([] if final else [VMEM]),
+        in_specs=[SMEM, SMEM] + [ANY] * (n_hub + 5) + ([] if final else [VMEM]),
         out_specs=[VMEM] * len(outs),
         out_shape=outs,
         scratch_shapes=[
             pltpu.VMEM((n_hub_blocks, rows, classes), bf),
             pltpu.VMEM(hub_tiles.shape, hub_tiles.dtype),
             pltpu.VMEM(seeds.shape, jnp.float32),
+            pltpu.VMEM(band[1].shape, jnp.float32),
             pltpu.VMEM(degree.shape, jnp.float32),
             pltpu.VMEM(seeds.shape, seeds.dtype),
-            pltpu.SemaphoreType.DMA((n_hub + 4 * blocks,)),
+            pltpu.SemaphoreType.DMA((n_hub + 4 * blocks + 1,)),
         ],
-    )(z, hub_index, *hub_pieces, hub_tiles, band, degree, seeds, *([] if final else [pick]))
+    )(z, hub_index, *hub_pieces, hub_tiles, *band, degree, seeds, *([] if final else [pick]))
 
 
 def positions_of(hub_blocks, owned, block_rows):
@@ -299,11 +321,12 @@
     pick = (hub_rows[:, None] == jnp.arange(current.shape[0], dtype=hub_rows.dtype)[None, :]).astype(jnp.bfloat16)
     prep = (pick, degree, positions_of(hub_blocks, owned, block_rows).reshape(-1))
     for step in range(ITERS):
-        middle = functools.partial(
+        part = functools.partial(
             band_call, z, band_offsets, current, band_tiles=band_tiles, fast=fast, n_own=owned.shape[0], width=width
         )
         band, hub_pieces, prep_out = exchange(
-            current, owned, p1, p3, pc, hub_blocks, width, block_rows, lambda rims: middle(rims), prep
+            current, owned, p1, p3, pc, hub_blocks, width, block_rows,
+            lambda: part((), rims_part=False), lambda rims: part(rims, rims_part=True), prep,
         )
         if prep is not None:
             pick, degree, hub_index = prep_out

time: 96.8 us -> 107 us (1.11)
  the two profiles are of different devices: /device:TPU:5 before, /device:TPU:0 now
where the time goes in v16:
time: 107 us
  Pallas kernels  40 us (37%)
  starting transfers between devices  36.4 us (34%)
  waiting for transfers between devices  12.4 us (12%)
  local copies, waits for them, and re-layouts  10.4 us (10%)
  other arithmetic  6.62 us (6%)
    pallas_call x6, Pallas kernels, band_call(): pl.pallas_call(functools.partial(band_kernel, fast, n_own, rims_part), co...  24.5 us
    ppermute x12, starting transfers between devices, exchange(): lax.ppermute(buf, AXES, pairs(m))  19.6 us
    pallas_call x3, Pallas kernels, hub_call(): pl.pallas_call(functools.partial(hub_kernel, n_hub, width, final), cost_e...  15.5 us
    ppermute x12, waiting for transfers between devices, exchange(): lax.ppermute(buf, AXES, pairs(m))  12.4 us
    ppermute x3, starting transfers between devices, exchange(): r2 = lax.ppermute(owned, AXES, pairs(2))  8.71 us
    unnamed x62, local copies, waits for them, and re-layouts  6.49 us
    ppermute x3, starting transfers between devices, exchange(): r3 = lax.ppermute(p3, AXES, pairs(3))  4.14 us
    reduce_sum x1, other arithmetic, body(): jnp.sum(band_tiles, axis=(1, 3), dtype=jnp.float32)  2.15 us
  transfers between devices with their start and end apart: 24, of which 9 were waited for; matrix products, arithmetic and copies ran while one was open for 9% of the time, Pallas kernels for 23%

profile of v16, /device:TPU:0, one launch (start us, length us, event | category | flops | bytes accessed | tf_op | source)
XLA Modules:
  0.0 106.7 jit_solution(16781302841598687151)
XLA Ops:
  3.4 4.1 %collective-permute-start.1 = (bf16[128,128]{1,0:T(8,128)(2,1)S(1)}, bf16[128,128]{1,0:T(8,128)(2,1)S(1)}, u32[]{:S(2)}, u32[]{:S(2)}) collective-permute-start(bf16[128,128]{1,0:T(8,128)(2,1)S(1)} %gather_fusion), channel_id=1, source_target_pairs={{0,2},{1,3},{2,0},{3,1},{4,6},{5,7},{6,4},{7,5},{8,10},{9,11},{10,... | collective-permute-start | bytes 98312 | tf_op jit(solution)/shard_map/ppermute | solution.py:51
  7.5 1.6 %collective-permute-start = (bf16[384,128]{1,0:T(8,128)(2,1)S(1)}, bf16[384,128]{1,0:T(8,128)(2,1)S(1)}, u32[]{:S(2)}, u32[]{:S(2)}) collective-permute-start(bf16[384,128]{1,0:T(8,128)(2,1)S(1)} %get-tuple-element.89), channel_id=1, source_target_pairs={{0,1},{1,0},{2,3},{3,2},{4,5},{5,4},{6,7},{7,6},{8,9},{9,8},{10,11... | collective-permute-start | bytes 294920 | tf_op jit(solution)/shard_map/ppermute | solution.py:52
  11.3 2.2 %convert_reduce_fusion = f32[8,128]{1,0:T(8,128)S(1)} fusion(bf16[8,10,128,128]{3,2,1,0:T(8,128)(2,1)} %rest_3_.5), kind=kLoop, calls=%fused_computation.2 | loop fusion | flops 2620416 | bytes 2625536 | tf_op jit(solution)/shard_map/reduce_sum | solution.py:311
  15.9 4.7 %shard_map.82.rest_3_ = f32[1024,128]{1,0:T(8,128)} custom-call(s32[1]{0:T(128)} %bitcast.z_ref, s32[80]{0:T(128)} %reshape.28.off_ref, bf16[1024,128]{1,0:T(8,128)(2,1)} %copy-done.2, bf16[8,10,128,128]{3,2,1,0:T(8,128)(2,1)} %rest_3_.5), custom_call_target="tpu_custom_call" | custom-call | flops 335544320 | bytes 3407872 | tf_op jit(solution)/shard_map/pallas_call | solution.py:170
  21.7 5.2 %collective-permute-start.4 = (bf16[4,128,128]{2,1,0:T(8,128)(2,1)S(1)}, bf16[4,128,128]{2,1,0:T(8,128)(2,1)S(1)}, u32[]{:S(2)}, u32[]{:S(2)}) collective-permute-start(bf16[4,128,128]{2,1,0:T(8,128)(2,1)S(1)} %pad_maximum_fusion), channel_id=1, source_target_pairs={{0,8},{1,9},{2,10},{3,11},{4,12},{5,13},{6,14},{7,15},{8,0},{9,1},... | collective-permute-start | bytes 393224 | tf_op jit(solution)/shard_map/ppermute | solution.py:65
  29.3 3.5 %shard_map.83.rest_4_ = f32[512,128]{1,0:T(8,128)} custom-call(s32[1]{0:T(128)} %bitcast.z_ref, s32[80]{0:T(128)} %reshape.28.off_ref, bf16[1024,128]{1,0:T(8,128)(2,1)} %copy-done.2, bf16[384,128]{1,0:T(8,128)(2,1)} %copy-done.13, bf16[384,128]{1,0:T(8,128)(2,1)} %copy-done.14, bf16[256,128]{1,0:T(8,128)(2,1)} %copy-done.17, bf16[8,10,128,128]{3,2,1,0:T(8,128)(2,1)} %rest_3_.5), custom_call_target="tpu_custom_call" | custom-call | flops 167772160 | bytes 1835008 | tf_op jit(solution)/shard_map/pallas_call | solution.py:170
  36.3 1.9 %collective-permute-done.7.rest_1_ = bf16[16,128,128]{2,1,0:T(8,128)(2,1)S(1)} collective-permute-done((bf16[16,128,128]{2,1,0:T(8,128)(2,1)S(1)}, bf16[16,128,128]{2,1,0:T(8,128)(2,1)S(1)}, u32[]{:S(2)}, u32[]{:S(2)}) %collective-permute-start.7) | collective-permute-done | bytes 524320 | tf_op jit(solution)/shard_map/ppermute | solution.py:65
  39.0 5.3 %shard_map.84 = (bf16[1024,128]{1,0:T(8,128)(2,1)}, bf16[128,128]{1,0:T(8,128)(2,1)}, bf16[384,128]{1,0:T(8,128)(2,1)}, bf16[384,128]{1,0:T(8,128)(2,1)}, bf16[256,128]{1,0:T(8,128)(2,1)}) custom-call(s32[1]{0:T(128)} %bitcast.z_ref, s32[48]{0:T(128)} %gather_fusion.1, bf16[16,128,128]{2,1,0:T(8,128)(2,1)} %copy-done.3, bf16[16,128,128]{2,1,0:T(8,128)(2,1)} %copy-done.7, ...), custom_call_target="tpu_custom_call" | custom-call | flops 201326592 | bytes 4718592 | tf_op jit(solution)/shard_map/pallas_call | solution.py:277
  44.4 2.0 %collective-permute-start.9 = (bf16[128,128]{1,0:T(8,128)(2,1)}, bf16[128,128]{1,0:T(8,128)(2,1)S(1)}, u32[]{:S(2)}, u32[]{:S(2)}) collective-permute-start(bf16[128,128]{1,0:T(8,128)(2,1)} %get-tuple-element.57), channel_id=1, source_target_pairs={{0,2},{1,3},{2,0},{3,1},{4,6},{5,7},{6,4},{7,5},{8,10},{9,11},{10,... | collective-permute-start | bytes 98312 | tf_op jit(solution)/shard_map/ppermute | solution.py:51
  46.3 2.4 %collective-permute-start.10 = (bf16[384,128]{1,0:T(8,128)(2,1)}, bf16[384,128]{1,0:T(8,128)(2,1)S(1)}, u32[]{:S(2)}, u32[]{:S(2)}) collective-permute-start(bf16[384,128]{1,0:T(8,128)(2,1)} %get-tuple-element.59), channel_id=1, source_target_pairs={{0,3},{1,2},{2,1},{3,0},{4,7},{5,6},{6,5},{7,4},{8,11},{9,10},{10,... | collective-permute-start | bytes 294920 | tf_op jit(solution)/shard_map/ppermute | solution.py:50
  50.2 4.7 %shard_map.85.rest_3_ = f32[1024,128]{1,0:T(8,128)} custom-call(s32[1]{0:T(128)} %bitcast.z_ref, s32[80]{0:T(128)} %reshape.28.off_ref, bf16[1024,128]{1,0:T(8,128)(2,1)} %get-tuple-element.61.cur_hbm, bf16[8,10,128,128]{3,2,1,0:T(8,128)(2,1)} %rest_3_.5), custom_call_target="tpu_custom_call" | custom-call | flops 335544320 | bytes 3407872 | tf_op jit(solution)/shard_map/pallas_call | solution.py:170
  55.0 3.3 %collective-permute-start.12 = (bf16[4,128,128]{2,1,0:T(8,128)(2,1)S(1)}, bf16[4,128,128]{2,1,0:T(8,128)(2,1)S(1)}, u32[]{:S(2)}, u32[]{:S(2)}) collective-permute-start(bf16[4,128,128]{2,1,0:T(8,128)(2,1)S(1)} %pad_maximum_fusion.1), channel_id=1, source_target_pairs={{0,8},{1,9},{2,10},{3,11},{4,12},{5,13},{6,14},{7,15},{8,0},{9,1},... | collective-permute-start | bytes 393224 | tf_op jit(solution)/shard_map/ppermute | solution.py:65
  61.0 3.5 %shard_map.86.rest_4_ = f32[512,128]{1,0:T(8,128)} custom-call(s32[1]{0:T(128)} %bitcast.z_ref, s32[80]{0:T(128)} %reshape.28.off_ref, bf16[1024,128]{1,0:T(8,128)(2,1)} %get-tuple-element.61.cur_hbm, bf16[384,128]{1,0:T(8,128)(2,1)} %copy-done.10, bf16[384,128]{1,0:T(8,128)(2,1)} %copy-done.12, bf16[256,128]{1,0:T(8,128)(2,1)} %copy-done.19, ...), custom_call_target="tpu_custom_call" | custom-call | flops 167772160 | bytes 1835008 | tf_op jit(solution)/shard_map/pallas_call | solution.py:170
  66.9 1.9 %collective-permute-done.15.rest_1_ = bf16[16,128,128]{2,1,0:T(8,128)(2,1)S(1)} collective-permute-done((bf16[16,128,128]{2,1,0:T(8,128)(2,1)S(1)}, bf16[16,128,128]{2,1,0:T(8,128)(2,1)S(1)}, u32[]{:S(2)}, u32[]{:S(2)}) %collective-permute-start.15) | collective-permute-done | bytes 524320 | tf_op jit(solution)/shard_map/ppermute | solution.py:65
  69.6 5.3 %shard_map.87 = (bf16[1024,128]{1,0:T(8,128)(2,1)}, bf16[128,128]{1,0:T(8,128)(2,1)}, bf16[384,128]{1,0:T(8,128)(2,1)}, bf16[384,128]{1,0:T(8,128)(2,1)}, bf16[256,128]{1,0:T(8,128)(2,1)}) custom-call(s32[1]{0:T(128)} %bitcast.z_ref, s32[48]{0:T(128)} %gather_fusion.1, bf16[16,128,128]{2,1,0:T(8,128)(2,1)} %copy-done.4, bf16[16,128,128]{2,1,0:T(8,128)(2,1)} %copy-done.6, ...), custom_call_target="tpu_custom_call" | custom-call | flops 201326592 | bytes 4718592 | tf_op jit(solution)/shard_map/pallas_call | solution.py:277
  75.0 2.7 %collective-permute-start.17 = (bf16[128,128]{1,0:T(8,128)(2,1)}, bf16[128,128]{1,0:T(8,128)(2,1)S(1)}, u32[]{:S(2)}, u32[]{:S(2)}) collective-permute-start(bf16[128,128]{1,0:T(8,128)(2,1)} %get-tuple-element.71), channel_id=1, source_target_pairs={{0,2},{1,3},{2,0},{3,1},{4,6},{5,7},{6,4},{7,5},{8,10},{9,11},{10,... | collective-permute-start | bytes 98312 | tf_op jit(solution)/shard_map/ppermute | solution.py:51
  77.7 1.7 %collective-permute-start.18 = (bf16[384,128]{1,0:T(8,128)(2,1)}, bf16[384,128]{1,0:T(8,128)(2,1)S(1)}, u32[]{:S(2)}, u32[]{:S(2)}) collective-permute-start(bf16[384,128]{1,0:T(8,128)(2,1)} %get-tuple-element.73), channel_id=1, source_target_pairs={{0,3},{1,2},{2,1},{3,0},{4,7},{5,6},{6,5},{7,4},{8,11},{9,10},{10,... | collective-permute-start | bytes 294920 | tf_op jit(solution)/shard_map/ppermute | solution.py:50
  81.0 4.7 %shard_map.88.rest_3_ = f32[1024,128]{1,0:T(8,128)} custom-call(s32[1]{0:T(128)} %bitcast.z_ref, s32[80]{0:T(128)} %reshape.28.off_ref, bf16[1024,128]{1,0:T(8,128)(2,1)} %get-tuple-element.75.cur_hbm, bf16[8,10,128,128]{3,2,1,0:T(8,128)(2,1)} %rest_3_.5), custom_call_target="tpu_custom_call" | custom-call | flops 335544320 | bytes 3407872 | tf_op jit(solution)/shard_map/pallas_call | solution.py:170
  85.8 3.8 %collective-permute-start.20 = (bf16[4,128,128]{2,1,0:T(8,128)(2,1)S(1)}, bf16[4,128,128]{2,1,0:T(8,128)(2,1)S(1)}, u32[]{:S(2)}, u32[]{:S(2)}) collective-permute-start(bf16[4,128,128]{2,1,0:T(8,128)(2,1)S(1)} %pad_maximum_fusion.2), channel_id=1, source_target_pairs={{0,8},{1,9},{2,10},{3,11},{4,12},{5,13},{6,14},{7,15},{8,0},{9,1},... | collective-permute-start | bytes 393224 | tf_op jit(solution)/shard_map/ppermute | solution.py:65
  89.6 1.7 %collective-permute-start.21 = (bf16[4,128,128]{2,1,0:T(8,128)(2,1)S(1)}, bf16[4,128,128]{2,1,0:T(8,128)(2,1)S(1)}, u32[]{:S(2)}, u32[]{:S(2)}) collective-permute-start(bf16[4,128,128]{2,1,0:T(8,128)(2,1)S(1)} %pad_maximum_fusion.2), channel_id=1, source_target_pairs={{0,16},{1,17},{2,18},{3,19},{4,20},{5,21},{6,22},{7,23},{8,24},{9,... | collective-permute-start | bytes 393224 | tf_op jit(solution)/shard_map/ppermute | solution.py:65
  91.8 3.5 %shard_map.89.rest_4_ = f32[512,128]{1,0:T(8,128)} custom-call(s32[1]{0:T(128)} %bitcast.z_ref, s32[80]{0:T(128)} %reshape.28.off_ref, bf16[1024,128]{1,0:T(8,128)(2,1)} %get-tuple-element.75.cur_hbm, bf16[384,128]{1,0:T(8,128)(2,1)} %copy-done.9, bf16[384,128]{1,0:T(8,128)(2,1)} %copy-done.11, bf16[256,128]{1,0:T(8,128)(2,1)} %copy-done.18, ...), custom_call_target="tpu_custom_call" | custom-call | flops 167772160 | bytes 1835008 | tf_op jit(solution)/shard_map/pallas_call | solution.py:170
  97.0 1.7 %collective-permute-done.22 = bf16[4,128,128]{2,1,0:T(8,128)(2,1)S(1)} collective-permute-done((bf16[4,128,128]{2,1,0:T(8,128)(2,1)S(1)}, bf16[4,128,128]{2,1,0:T(8,128)(2,1)S(1)}, u32[]{:S(2)}, u32[]{:S(2)}) %collective-permute-start.22) | collective-permute-done | bytes 131104 | tf_op jit(solution)/shard_map/ppermute | solution.py:65
  98.9 1.9 %collective-permute-done.23.rest_1_ = bf16[16,128,128]{2,1,0:T(8,128)(2,1)S(1)} collective-permute-done((bf16[16,128,128]{2,1,0:T(8,128)(2,1)S(1)}, bf16[16,128,128]{2,1,0:T(8,128)(2,1)S(1)}, u32[]{:S(2)}, u32[]{:S(2)}) %collective-permute-start.23) | collective-permute-done | bytes 524320 | tf_op jit(solution)/shard_map/ppermute | solution.py:65
  101.6 4.9 %shard_map.90 = f32[1024,128]{1,0:T(8,128)} custom-call(s32[1]{0:T(128)} %bitcast.z_ref, s32[48]{0:T(128)} %gather_fusion.1, bf16[16,128,128]{2,1,0:T(8,128)(2,1)} %copy-done.5, bf16[16,128,128]{2,1,0:T(8,128)(2,1)} %copy-done.8, bf16[8,6,128,128]{3,2,1,0:T(8,128)(2,1)} %rest_2_.5, f32[1024,128]{1,0:T(8,128)} %shard_map.88.rest_3_, ...), custom_call_target="tpu_custom_call" | custom-call | flops 201326592 | bytes 4718592 | tf_op jit(solution)/shard_map/pallas_call | solution.py:277
  (123 shorter events, 27.8 us)
Async XLA Ops:
  3.4 17.3 %collective-permute-start.1 = (bf16[128,128]{1,0:T(8,128)(2,1)S(1)}, bf16[128,128]{1,0:T(8,128)(2,1)S(1)}, u32[]{:S(2)}, u32[]{:S(2)}) collective-permute-start(bf16[128,128]{1,0:T(8,128)(2,1)S(1)} %gather_fusion), channel_id=1, source_target_pairs={{0,2},{1,3},{2,0},{3,1},{4,6},{5,7},{6,4},{7,5},{8,10},{9,11},{10,... | collective-permute-start | bytes 98312 | tf_op jit(solution)/shard_map/ppermute | solution.py:51
  7.5 13.1 %collective-permute-start = (bf16[384,128]{1,0:T(8,128)(2,1)S(1)}, bf16[384,128]{1,0:T(8,128)(2,1)S(1)}, u32[]{:S(2)}, u32[]{:S(2)}) collective-permute-start(bf16[384,128]{1,0:T(8,128)(2,1)S(1)} %get-tuple-element.89), channel_id=1, source_target_pairs={{0,1},{1,0},{2,3},{3,2},{4,5},{5,4},{6,7},{7,6},{8,9},{9,8},{10,11... | collective-permute-start | bytes 294920 | tf_op jit(solution)/shard_map/ppermute | solution.py:52
  9.1 11.5 %collective-permute-start.2 = (bf16[384,128]{1,0:T(8,128)(2,1)S(1)}, bf16[384,128]{1,0:T(8,128)(2,1)S(1)}, u32[]{:S(2)}, u32[]{:S(2)}) collective-permute-start(bf16[384,128]{1,0:T(8,128)(2,1)S(1)} %get-tuple-element.88), channel_id=1, source_target_pairs={{0,3},{1,2},{2,1},{3,0},{4,7},{5,6},{6,5},{7,4},{8,11},{9,10},{10,... | collective-permute-start | bytes 294920 | tf_op jit(solution)/shard_map/ppermute | solution.py:50
  9.1 11.5 %collective-permute-start.3 = (bf16[256,128]{1,0:T(8,128)(2,1)S(1)}, bf16[256,128]{1,0:T(8,128)(2,1)S(1)}, u32[]{:S(2)}, u32[]{:S(2)}) collective-permute-start(bf16[256,128]{1,0:T(8,128)(2,1)S(1)} %get-tuple-element.85), channel_id=1, source_target_pairs={{3,4},{7,8},{11,12},{15,16},{19,20},{23,24},{27,28},{4,3},{8,7},{1... | collective-permute-start | bytes 196616 | tf_op jit(solution)/shard_map/ppermute | solution.py:56
  21.7 11.9 %collective-permute-start.4 = (bf16[4,128,128]{2,1,0:T(8,128)(2,1)S(1)}, bf16[4,128,128]{2,1,0:T(8,128)(2,1)S(1)}, u32[]{:S(2)}, u32[]{:S(2)}) collective-permute-start(bf16[4,128,128]{2,1,0:T(8,128)(2,1)S(1)} %pad_maximum_fusion), channel_id=1, source_target_pairs={{0,8},{1,9},{2,10},{3,11},{4,12},{5,13},{6,14},{7,15},{8,0},{9,1},... | collective-permute-start | bytes 393224 | tf_op jit(solution)/shard_map/ppermute | solution.py:65
  26.9 7.9 %collective-permute-start.5 = (bf16[4,128,128]{2,1,0:T(8,128)(2,1)S(1)}, bf16[4,128,128]{2,1,0:T(8,128)(2,1)S(1)}, u32[]{:S(2)}, u32[]{:S(2)}) collective-permute-start(bf16[4,128,128]{2,1,0:T(8,128)(2,1)S(1)} %pad_maximum_fusion), channel_id=1, source_target_pairs={{0,16},{1,17},{2,18},{3,19},{4,20},{5,21},{6,22},{7,23},{8,24},{9,... | collective-permute-start | bytes 393224 | tf_op jit(solution)/shard_map/ppermute | solution.py:65
  28.4 7.7 %collective-permute-start.6 = (bf16[4,128,128]{2,1,0:T(8,128)(2,1)S(1)}, bf16[4,128,128]{2,1,0:T(8,128)(2,1)S(1)}, u32[]{:S(2)}, u32[]{:S(2)}) collective-permute-start(bf16[4,128,128]{2,1,0:T(8,128)(2,1)S(1)} %pad_maximum_fusion), channel_id=1, source_target_pairs={{0,24},{1,25},{2,26},{3,27},{4,28},{5,29},{6,30},{7,31},{8,16},{9,... | collective-permute-start | bytes 393224 | tf_op jit(solution)/shard_map/ppermute | solution.py:65
  36.2 2.0 %collective-permute-start.7 = (bf16[16,128,128]{2,1,0:T(8,128)(2,1)S(1)}, bf16[16,128,128]{2,1,0:T(8,128)(2,1)S(1)}, u32[]{:S(2)}, u32[]{:S(2)}) collective-permute-start(bf16[16,128,128]{2,1,0:T(8,128)(2,1)S(1)} %constant_dynamic-update-slice_fusion.rest_0_), channel_id=1, source_target_pairs={{0,4},{1,5},{2,6},{3,7},{4,0},{5,1},{6,2},{7,3},{8,12},{9,13},{10,... | collective-permute-start | bytes 1572872 | tf_op jit(solution)/shard_map/ppermute | solution.py:65
  44.3 10.6 %collective-permute-start.8 = (bf16[384,128]{1,0:T(8,128)(2,1)}, bf16[384,128]{1,0:T(8,128)(2,1)S(1)}, u32[]{:S(2)}, u32[]{:S(2)}) collective-permute-start(bf16[384,128]{1,0:T(8,128)(2,1)} %get-tuple-element.58), channel_id=1, source_target_pairs={{0,1},{1,0},{2,3},{3,2},{4,5},{5,4},{6,7},{7,6},{8,9},{9,8},{10,11... | collective-permute-start | bytes 294920 | tf_op jit(solution)/shard_map/ppermute | solution.py:52
  44.4 10.5 %collective-permute-start.9 = (bf16[128,128]{1,0:T(8,128)(2,1)}, bf16[128,128]{1,0:T(8,128)(2,1)S(1)}, u32[]{:S(2)}, u32[]{:S(2)}) collective-permute-start(bf16[128,128]{1,0:T(8,128)(2,1)} %get-tuple-element.57), channel_id=1, source_target_pairs={{0,2},{1,3},{2,0},{3,1},{4,6},{5,7},{6,4},{7,5},{8,10},{9,11},{10,... | collective-permute-start | bytes 98312 | tf_op jit(solution)/shard_map/ppermute | solution.py:51
  46.3 8.6 %collective-permute-start.10 = (bf16[384,128]{1,0:T(8,128)(2,1)}, bf16[384,128]{1,0:T(8,128)(2,1)S(1)}, u32[]{:S(2)}, u32[]{:S(2)}) collective-permute-start(bf16[384,128]{1,0:T(8,128)(2,1)} %get-tuple-element.59), channel_id=1, source_target_pairs={{0,3},{1,2},{2,1},{3,0},{4,7},{5,6},{6,5},{7,4},{8,11},{9,10},{10,... | collective-permute-start | bytes 294920 | tf_op jit(solution)/shard_map/ppermute | solution.py:50
  48.8 6.2 %collective-permute-start.11 = (bf16[256,128]{1,0:T(8,128)(2,1)}, bf16[256,128]{1,0:T(8,128)(2,1)S(1)}, u32[]{:S(2)}, u32[]{:S(2)}) collective-permute-start(bf16[256,128]{1,0:T(8,128)(2,1)} %get-tuple-element.60), channel_id=1, source_target_pairs={{3,4},{7,8},{11,12},{15,16},{19,20},{23,24},{27,28},{4,3},{8,7},{1... | collective-permute-start | bytes 196616 | tf_op jit(solution)/shard_map/ppermute | solution.py:56
  55.0 10.2 %collective-permute-start.12 = (bf16[4,128,128]{2,1,0:T(8,128)(2,1)S(1)}, bf16[4,128,128]{2,1,0:T(8,128)(2,1)S(1)}, u32[]{:S(2)}, u32[]{:S(2)}) collective-permute-start(bf16[4,128,128]{2,1,0:T(8,128)(2,1)S(1)} %pad_maximum_fusion.1), channel_id=1, source_target_pairs={{0,8},{1,9},{2,10},{3,11},{4,12},{5,13},{6,14},{7,15},{8,0},{9,1},... | collective-permute-start | bytes 393224 | tf_op jit(solution)/shard_map/ppermute | solution.py:65
  58.3 7.0 %collective-permute-start.13 = (bf16[4,128,128]{2,1,0:T(8,128)(2,1)S(1)}, bf16[4,128,128]{2,1,0:T(8,128)(2,1)S(1)}, u32[]{:S(2)}, u32[]{:S(2)}) collective-permute-start(bf16[4,128,128]{2,1,0:T(8,128)(2,1)S(1)} %pad_maximum_fusion.1), channel_id=1, source_target_pairs={{0,16},{1,17},{2,18},{3,19},{4,20},{5,21},{6,22},{7,23},{8,24},{9,... | collective-permute-start | bytes 393224 | tf_op jit(solution)/shard_map/ppermute | solution.py:65
  59.7 7.0 %collective-permute-start.14 = (bf16[4,128,128]{2,1,0:T(8,128)(2,1)S(1)}, bf16[4,128,128]{2,1,0:T(8,128)(2,1)S(1)}, u32[]{:S(2)}, u32[]{:S(2)}) collective-permute-start(bf16[4,128,128]{2,1,0:T(8,128)(2,1)S(1)} %pad_maximum_fusion.1), channel_id=1, source_target_pairs={{0,24},{1,25},{2,26},{3,27},{4,28},{5,29},{6,30},{7,31},{8,16},{9,... | collective-permute-start | bytes 393224 | tf_op jit(solution)/shard_map/ppermute | solution.py:65
  66.8 2.0 %collective-permute-start.15 = (bf16[16,128,128]{2,1,0:T(8,128)(2,1)S(1)}, bf16[16,128,128]{2,1,0:T(8,128)(2,1)S(1)}, u32[]{:S(2)}, u32[]{:S(2)}) collective-permute-start(bf16[16,128,128]{2,1,0:T(8,128)(2,1)S(1)} %constant_dynamic-update-slice_fusion.7.rest_0_), channel_id=1, source_target_pairs={{0,4},{1,5},{2,6},{3,7},{4,0},{5,1},{6,2},{7,3},{8,12},{9,13},{10,... | collective-permute-start | bytes 1572872 | tf_op jit(solution)/shard_map/ppermute | solution.py:65
  74.9 10.8 %collective-permute-start.16 = (bf16[384,128]{1,0:T(8,128)(2,1)}, bf16[384,128]{1,0:T(8,128)(2,1)S(1)}, u32[]{:S(2)}, u32[]{:S(2)}) collective-permute-start(bf16[384,128]{1,0:T(8,128)(2,1)} %get-tuple-element.72), channel_id=1, source_target_pairs={{0,1},{1,0},{2,3},{3,2},{4,5},{5,4},{6,7},{7,6},{8,9},{9,8},{10,11... | collective-permute-start | bytes 294920 | tf_op jit(solution)/shard_map/ppermute | solution.py:52
  75.0 10.7 %collective-permute-start.17 = (bf16[128,128]{1,0:T(8,128)(2,1)}, bf16[128,128]{1,0:T(8,128)(2,1)S(1)}, u32[]{:S(2)}, u32[]{:S(2)}) collective-permute-start(bf16[128,128]{1,0:T(8,128)(2,1)} %get-tuple-element.71), channel_id=1, source_target_pairs={{0,2},{1,3},{2,0},{3,1},{4,6},{5,7},{6,4},{7,5},{8,10},{9,11},{10,... | collective-permute-start | bytes 98312 | tf_op jit(solution)/shard_map/ppermute | solution.py:51
  77.7 8.1 %collective-permute-start.18 = (bf16[384,128]{1,0:T(8,128)(2,1)}, bf16[384,128]{1,0:T(8,128)(2,1)S(1)}, u32[]{:S(2)}, u32[]{:S(2)}) collective-permute-start(bf16[384,128]{1,0:T(8,128)(2,1)} %get-tuple-element.73), channel_id=1, source_target_pairs={{0,3},{1,2},{2,1},{3,0},{4,7},{5,6},{6,5},{7,4},{8,11},{9,10},{10,... | collective-permute-start | bytes 294920 | tf_op jit(solution)/shard_map/ppermute | solution.py:50
  79.4 6.3 %collective-permute-start.19 = (bf16[256,128]{1,0:T(8,128)(2,1)}, bf16[256,128]{1,0:T(8,128)(2,1)S(1)}, u32[]{:S(2)}, u32[]{:S(2)}) collective-permute-start(bf16[256,128]{1,0:T(8,128)(2,1)} %get-tuple-element.74), channel_id=1, source_target_pairs={{3,4},{7,8},{11,12},{15,16},{19,20},{23,24},{27,28},{4,3},{8,7},{1... | collective-permute-start | bytes 196616 | tf_op jit(solution)/shard_map/ppermute | solution.py:56
  85.8 10.2 %collective-permute-start.20 = (bf16[4,128,128]{2,1,0:T(8,128)(2,1)S(1)}, bf16[4,128,128]{2,1,0:T(8,128)(2,1)S(1)}, u32[]{:S(2)}, u32[]{:S(2)}) collective-permute-start(bf16[4,128,128]{2,1,0:T(8,128)(2,1)S(1)} %pad_maximum_fusion.2), channel_id=1, source_target_pairs={{0,8},{1,9},{2,10},{3,11},{4,12},{5,13},{6,14},{7,15},{8,0},{9,1},... | collective-permute-start | bytes 393224 | tf_op jit(solution)/shard_map/ppermute | solution.py:65
  89.6 7.4 %collective-permute-start.21 = (bf16[4,128,128]{2,1,0:T(8,128)(2,1)S(1)}, bf16[4,128,128]{2,1,0:T(8,128)(2,1)S(1)}, u32[]{:S(2)}, u32[]{:S(2)}) collective-permute-start(bf16[4,128,128]{2,1,0:T(8,128)(2,1)S(1)} %pad_maximum_fusion.2), channel_id=1, source_target_pairs={{0,16},{1,17},{2,18},{3,19},{4,20},{5,21},{6,22},{7,23},{8,24},{9,... | collective-permute-start | bytes 393224 | tf_op jit(solution)/shard_map/ppermute | solution.py:65
  91.3 7.4 %collective-permute-start.22 = (bf16[4,128,128]{2,1,0:T(8,128)(2,1)S(1)}, bf16[4,128,128]{2,1,0:T(8,128)(2,1)S(1)}, u32[]{:S(2)}, u32[]{:S(2)}) collective-permute-start(bf16[4,128,128]{2,1,0:T(8,128)(2,1)S(1)} %pad_maximum_fusion.2), channel_id=1, source_target_pairs={{0,24},{1,25},{2,26},{3,27},{4,28},{5,29},{6,30},{7,31},{8,16},{9,... | collective-permute-start | bytes 393224 | tf_op jit(solution)/shard_map/ppermute | solution.py:65
  98.8 2.0 %collective-permute-start.23 = (bf16[16,128,128]{2,1,0:T(8,128)(2,1)S(1)}, bf16[16,128,128]{2,1,0:T(8,128)(2,1)S(1)}, u32[]{:S(2)}, u32[]{:S(2)}) collective-permute-start(bf16[16,128,128]{2,1,0:T(8,128)(2,1)S(1)} %constant_dynamic-update-slice_fusion.14.rest_0_), channel_id=1, source_target_pairs={{0,4},{1,5},{2,6},{3,7},{4,0},{5,1},{6,2},{7,3},{8,12},{9,13},{10,... | collective-permute-start | bytes 1572872 | tf_op jit(solution)/shard_map/ppermute | solution.py:65
  (22 other events, 136.6 us)

commit v17 on v14

--- a/solution.py
+++ b/solution.py
@@ -170,11 +170,11 @@
 def hub_kernel(n_hub, width, final, z_ref, hidx_ref, *rest):
     hub_hbm = rest[:n_hub]
     if final:
-        (ht_hbm, band_hbm, deg_hbm, seeds_hbm, out_ref, hub, ht, band, deg, seeds, sem) = rest[n_hub:]
+        (ht_hbm, band_hbm, deg_hbm, seeds_hbm, out_ref, ht, band, deg, seeds, sem) = rest[n_hub:]
     else:
         (ht_hbm, band_hbm, deg_hbm, seeds_hbm, pick_ref,
          cur_ref, owned_ref, p1_ref, p3_ref, pc_ref,
-         hub, ht, band, deg, seeds, sem) = rest[n_hub:]
+         ht, band, deg, seeds, sem) = rest[n_hub:]
     blocks, k_hub, rows = ht.shape[0], ht.shape[1], ht.shape[2]
     per_block = []
     for b in range(blocks):
@@ -186,13 +186,6 @@
             pltpu.make_async_copy(seeds_hbm.at[span], seeds.at[span], sem.at[n_hub + 4 * b + 3]),
         ])
     copies = []
-    at = 0
-    for i, piece in enumerate(hub_hbm):
-        n = piece.shape[0]
-        copies.append(pltpu.make_async_copy(piece, hub.at[pl.ds(at, n)], sem.at[i]))
-        at += n
-    for c in copies:
-        c.start()
     for c in per_block[0]:
         c.start()
     for b in range(1, blocks):
@@ -204,8 +197,17 @@
         for c in per_block[b]:
             c.wait()
         span = pl.ds(b * rows, rows)
-        acc = jnp.zeros((rows, hub.shape[2]), jnp.float32)
-        blk = lambda h: hub[hidx_ref[b * k_hub + h]]
+        acc = jnp.zeros((rows, rows), jnp.float32)
+
+        def blk(h):
+            p = hidx_ref[b * k_hub + h]
+            first = hub_hbm[0].shape[0]
+            if n_hub == 1:
+                return hub_hbm[0][p]
+            mine = hub_hbm[0][jnp.minimum(p, first - 1)]
+            theirs = hub_hbm[1][jnp.maximum(p - first, 0)]
+            return jnp.where(p < first, mine, theirs)
+
         for h in range(0, k_hub - 1, 2):
             lhs = jnp.concatenate([ht[b, h], ht[b, h + 1]], axis=1)
             rhs = jnp.concatenate([blk(h), blk(h + 1)], axis=0)
@@ -256,11 +258,10 @@
     return pl.pallas_call(
         functools.partial(hub_kernel, n_hub, width, final),
         cost_estimate=pl.CostEstimate(flops=flops, transcendentals=0, bytes_accessed=bytes_accessed),
-        in_specs=[SMEM, SMEM] + [ANY] * (n_hub + 4) + ([] if final else [VMEM]),
+        in_specs=[SMEM, SMEM] + [VMEM] * n_hub + [ANY] * 4 + ([] if final else [VMEM]),
         out_specs=[VMEM] * len(outs),
         out_shape=outs,
         scratch_shapes=[
-            pltpu.VMEM((n_hub_blocks, rows, classes), bf),
             pltpu.VMEM(hub_tiles.shape, hub_tiles.dtype),
             pltpu.VMEM(seeds.shape, jnp.float32),
             pltpu.VMEM(degree.shape, jnp.float32),

time: 96.8 us -> 97.5 us (level)
  no operation moved by 1% of the time
where the time goes in v17:
time: 97.5 us; the launch traced here: 96.2 us
  starting transfers between devices  37.3 us (38%)
  Pallas kernels  30 us (31%)
  local copies, waits for them, and re-layouts  11.4 us (12%)
  waiting for transfers between devices  8.71 us (9%)
  other arithmetic  8.19 us (8%)
    pallas_call x3, Pallas kernels, hub_call(): pl.pallas_call(functools.partial(hub_kernel, n_hub, width, final), cost_e...  15.9 us
    pallas_call x3, Pallas kernels, band_call(): pl.pallas_call(functools.partial(band_kernel, fast, n_own), cost_estimate...  14.1 us
    ppermute x12, starting transfers between devices, exchange(): lax.ppermute(buf, AXES, pairs(m))  13.3 us
    ppermute x3, starting transfers between devices, exchange(): rc = lax.ppermute(pc, AXES, cross)  13 us
    unnamed x58, local copies, waits for them, and re-layouts  7.62 us
    ppermute x3, starting transfers between devices, exchange(): r1 = lax.ppermute(p1, AXES, pairs(1))  7.54 us
    ppermute x12, waiting for transfers between devices, exchange(): lax.ppermute(buf, AXES, pairs(m))  5.41 us
    ppermute x3, waiting for transfers between devices, exchange(): r1 = lax.ppermute(p1, AXES, pairs(1))  3.27 us
  transfers between devices with their start and end apart: 24, of which 6 were waited for; matrix products, arithmetic and copies ran while one was open for 12% of the time, Pallas kernels for 15%

profile of v17, /device:TPU:5, one launch (start us, length us, event | category | flops | bytes accessed | tf_op | source)
XLA Modules:
  0.0 96.2 jit_solution(1257601773633657884)
XLA Ops:
  3.4 2.4 %collective-permute-start.1 = (bf16[128,128]{1,0:T(8,128)(2,1)S(1)}, bf16[128,128]{1,0:T(8,128)(2,1)S(1)}, u32[]{:S(2)}, u32[]{:S(2)}) collective-permute-start(bf16[128,128]{1,0:T(8,128)(2,1)S(1)} %gather_fusion), channel_id=1, source_target_pairs={{0,2},{1,3},{2,0},{3,1},{4,6},{5,7},{6,4},{7,5},{8,10},{9,11},{10,... | collective-permute-start | bytes 98312 | tf_op jit(solution)/shard_map/ppermute | solution.py:50
  5.8 1.4 %collective-permute-start = (bf16[384,128]{1,0:T(8,128)(2,1)S(1)}, bf16[384,128]{1,0:T(8,128)(2,1)S(1)}, u32[]{:S(2)}, u32[]{:S(2)}) collective-permute-start(bf16[384,128]{1,0:T(8,128)(2,1)S(1)} %get-tuple-element.67), channel_id=1, source_target_pairs={{0,1},{1,0},{2,3},{3,2},{4,5},{5,4},{6,7},{7,6},{8,9},{9,8},{10,11... | collective-permute-start | bytes 294920 | tf_op jit(solution)/shard_map/ppermute | solution.py:51
  7.1 6.6 %collective-permute-start.3 = (bf16[256,128]{1,0:T(8,128)(2,1)S(1)}, bf16[256,128]{1,0:T(8,128)(2,1)S(1)}, u32[]{:S(2)}, u32[]{:S(2)}) collective-permute-start(bf16[256,128]{1,0:T(8,128)(2,1)S(1)} %get-tuple-element.63), channel_id=1, source_target_pairs={{3,4},{7,8},{11,12},{15,16},{19,20},{23,24},{27,28},{4,3},{8,7},{1... | collective-permute-start | bytes 196616 | tf_op jit(solution)/shard_map/ppermute | solution.py:55
  13.7 1.5 %fusion.rest_6_ = bf16[128,1024]{1,0:T(8,128)(2,1)} fusion(s32[128]{0:T(128)} %param.14), kind=kLoop, calls=%fused_computation.6 | loop fusion | flops 262144 | bytes 262656 | tf_op jit(solution)/shard_map/convert_element_type | solution.py:301
  15.2 2.2 %convert_reduce_fusion = f32[8,128]{1,0:T(8,128)S(1)} fusion(bf16[8,10,128,128]{3,2,1,0:T(8,128)(2,1)} %rest_3_.5), kind=kLoop, calls=%fused_computation.2 | loop fusion | flops 2620416 | bytes 2625536 | tf_op jit(solution)/shard_map/reduce_sum | solution.py:290
  23.5 4.7 %shard_map.82.rest_3_ = f32[1024,128]{1,0:T(8,128)} custom-call(s32[1]{0:T(128)} %bitcast.z_ref, s32[80]{0:T(128)} %reshape.26.off_ref, bf16[1024,128]{1,0:T(8,128)(2,1)} %copy-done.2, bf16[384,128]{1,0:T(8,128)(2,1)} %copy-done.13, bf16[384,128]{1,0:T(8,128)(2,1)} %copy-done.14, bf16[256,128]{1,0:T(8,128)(2,1)} %copy-done.15, bf16[8,10,128,128]{3,2,1,0:T(8,128)(2,1)} %rest_3_.5), custom_call_target="tpu_custom_call" | custom-call | flops 335544320 | bytes 3670016 | tf_op jit(solution)/shard_map/pallas_call | solution.py:156
  30.3 1.5 %collective-permute-done.7.rest_1_ = bf16[16,128,128]{2,1,0:T(8,128)(2,1)S(1)} collective-permute-done((bf16[16,128,128]{2,1,0:T(8,128)(2,1)S(1)}, bf16[16,128,128]{2,1,0:T(8,128)(2,1)S(1)}, u32[]{:S(2)}, u32[]{:S(2)}) %collective-permute-start.7) | collective-permute-done | bytes 524320 | tf_op jit(solution)/shard_map/ppermute | solution.py:65
  32.7 5.4 %shard_map.83 = (bf16[1024,128]{1,0:T(8,128)(2,1)}, bf16[128,128]{1,0:T(8,128)(2,1)}, bf16[384,128]{1,0:T(8,128)(2,1)}, bf16[384,128]{1,0:T(8,128)(2,1)}, bf16[256,128]{1,0:T(8,128)(2,1)}) custom-call(s32[1]{0:T(128)} %bitcast.z_ref, s32[48]{0:T(128)} %gather_fusion.1, bf16[16,128,128]{2,1,0:T(8,128)(2,1)} %copy-done.3, bf16[16,128,128]{2,1,0:T(8,128)(2,1)} %copy-done.7, ...), custom_call_target="tpu_custom_call" | custom-call | flops 201326592 | bytes 4718592 | tf_op jit(solution)/shard_map/pallas_call | solution.py:258
  39.2 3.2 %collective-permute-start.8 = (bf16[384,128]{1,0:T(8,128)(2,1)}, bf16[384,128]{1,0:T(8,128)(2,1)S(1)}, u32[]{:S(2)}, u32[]{:S(2)}) collective-permute-start(bf16[384,128]{1,0:T(8,128)(2,1)} %get-tuple-element.46), channel_id=1, source_target_pairs={{0,1},{1,0},{2,3},{3,2},{4,5},{5,4},{6,7},{7,6},{8,9},{9,8},{10,11... | collective-permute-start | bytes 294920 | tf_op jit(solution)/shard_map/ppermute | solution.py:51
  42.4 3.3 %collective-permute-start.11 = (bf16[256,128]{1,0:T(8,128)(2,1)}, bf16[256,128]{1,0:T(8,128)(2,1)S(1)}, u32[]{:S(2)}, u32[]{:S(2)}) collective-permute-start(bf16[256,128]{1,0:T(8,128)(2,1)} %get-tuple-element.49), channel_id=1, source_target_pairs={{3,4},{7,8},{11,12},{15,16},{19,20},{23,24},{27,28},{4,3},{8,7},{1... | collective-permute-start | bytes 196616 | tf_op jit(solution)/shard_map/ppermute | solution.py:55
  45.8 1.6 %collective-permute-done.8.rest_0_ = bf16[384,128]{1,0:T(8,128)(2,1)S(1)} collective-permute-done((bf16[384,128]{1,0:T(8,128)(2,1)}, bf16[384,128]{1,0:T(8,128)(2,1)S(1)}, u32[]{:S(2)}, u32[]{:S(2)}) %collective-permute-start.8) | collective-permute-done | bytes 98336 | tf_op jit(solution)/shard_map/ppermute | solution.py:51
  49.4 1.5 %collective-permute-start.14 = (bf16[4,128,128]{2,1,0:T(8,128)(2,1)S(1)}, bf16[4,128,128]{2,1,0:T(8,128)(2,1)S(1)}, u32[]{:S(2)}, u32[]{:S(2)}) collective-permute-start(bf16[4,128,128]{2,1,0:T(8,128)(2,1)S(1)} %pad_maximum_fusion.1), channel_id=1, source_target_pairs={{0,24},{1,25},{2,26},{3,27},{4,28},{5,29},{6,30},{7,31},{8,16},{9,... | collective-permute-start | bytes 393224 | tf_op jit(solution)/shard_map/ppermute | solution.py:65
  51.5 4.7 %shard_map.84.rest_3_ = f32[1024,128]{1,0:T(8,128)} custom-call(s32[1]{0:T(128)} %bitcast.z_ref, s32[80]{0:T(128)} %reshape.26.off_ref, bf16[1024,128]{1,0:T(8,128)(2,1)} %get-tuple-element.48.cur_hbm, bf16[384,128]{1,0:T(8,128)(2,1)} %copy-done.12, bf16[384,128]{1,0:T(8,128)(2,1)} %copy-done.10, bf16[256,128]{1,0:T(8,128)(2,1)} %copy-done.17, ...), custom_call_target="tpu_custom_call" | custom-call | flops 335544320 | bytes 3670016 | tf_op jit(solution)/shard_map/pallas_call | solution.py:156
  57.1 2.3 %collective-permute-start.15 = (bf16[16,128,128]{2,1,0:T(8,128)(2,1)S(1)}, bf16[16,128,128]{2,1,0:T(8,128)(2,1)S(1)}, u32[]{:S(2)}, u32[]{:S(2)}) collective-permute-start(bf16[16,128,128]{2,1,0:T(8,128)(2,1)S(1)} %constant_dynamic-update-slice_fusion.7.rest_0_), channel_id=1, source_target_pairs={{0,4},{1,5},{2,6},{3,7},{4,0},{5,1},{6,2},{7,3},{8,12},{9,13},{10,... | collective-permute-start | bytes 1572872 | tf_op jit(solution)/shard_map/ppermute | solution.py:65
  59.4 1.5 %collective-permute-done.15.rest_1_ = bf16[16,128,128]{2,1,0:T(8,128)(2,1)S(1)} collective-permute-done((bf16[16,128,128]{2,1,0:T(8,128)(2,1)S(1)}, bf16[16,128,128]{2,1,0:T(8,128)(2,1)S(1)}, u32[]{:S(2)}, u32[]{:S(2)}) %collective-permute-start.15) | collective-permute-done | bytes 524320 | tf_op jit(solution)/shard_map/ppermute | solution.py:65
  61.8 5.4 %shard_map.85 = (bf16[1024,128]{1,0:T(8,128)(2,1)}, bf16[128,128]{1,0:T(8,128)(2,1)}, bf16[384,128]{1,0:T(8,128)(2,1)}, bf16[384,128]{1,0:T(8,128)(2,1)}, bf16[256,128]{1,0:T(8,128)(2,1)}) custom-call(s32[1]{0:T(128)} %bitcast.z_ref, s32[48]{0:T(128)} %gather_fusion.1, bf16[16,128,128]{2,1,0:T(8,128)(2,1)} %copy-done.4, bf16[16,128,128]{2,1,0:T(8,128)(2,1)} %copy-done.6, ...), custom_call_target="tpu_custom_call" | custom-call | flops 201326592 | bytes 4718592 | tf_op jit(solution)/shard_map/pallas_call | solution.py:258
  68.6 3.0 %collective-permute-start.16 = (bf16[384,128]{1,0:T(8,128)(2,1)}, bf16[384,128]{1,0:T(8,128)(2,1)S(1)}, u32[]{:S(2)}, u32[]{:S(2)}) collective-permute-start(bf16[384,128]{1,0:T(8,128)(2,1)} %get-tuple-element.55), channel_id=1, source_target_pairs={{0,1},{1,0},{2,3},{3,2},{4,5},{5,4},{6,7},{7,6},{8,9},{9,8},{10,11... | collective-permute-start | bytes 294920 | tf_op jit(solution)/shard_map/ppermute | solution.py:51
  71.5 3.2 %collective-permute-start.19 = (bf16[256,128]{1,0:T(8,128)(2,1)}, bf16[256,128]{1,0:T(8,128)(2,1)S(1)}, u32[]{:S(2)}, u32[]{:S(2)}) collective-permute-start(bf16[256,128]{1,0:T(8,128)(2,1)} %get-tuple-element.58), channel_id=1, source_target_pairs={{3,4},{7,8},{11,12},{15,16},{19,20},{23,24},{27,28},{4,3},{8,7},{1... | collective-permute-start | bytes 196616 | tf_op jit(solution)/shard_map/ppermute | solution.py:55
  74.7 1.7 %collective-permute-done.16.rest_0_ = bf16[384,128]{1,0:T(8,128)(2,1)S(1)} collective-permute-done((bf16[384,128]{1,0:T(8,128)(2,1)}, bf16[384,128]{1,0:T(8,128)(2,1)S(1)}, u32[]{:S(2)}, u32[]{:S(2)}) %collective-permute-start.16) | collective-permute-done | bytes 98336 | tf_op jit(solution)/shard_map/ppermute | solution.py:51
  78.0 2.0 %collective-permute-start.22 = (bf16[4,128,128]{2,1,0:T(8,128)(2,1)S(1)}, bf16[4,128,128]{2,1,0:T(8,128)(2,1)S(1)}, u32[]{:S(2)}, u32[]{:S(2)}) collective-permute-start(bf16[4,128,128]{2,1,0:T(8,128)(2,1)S(1)} %pad_maximum_fusion.2), channel_id=1, source_target_pairs={{0,24},{1,25},{2,26},{3,27},{4,28},{5,29},{6,30},{7,31},{8,16},{9,... | collective-permute-start | bytes 393224 | tf_op jit(solution)/shard_map/ppermute | solution.py:65
  80.6 4.7 %shard_map.86.rest_3_ = f32[1024,128]{1,0:T(8,128)} custom-call(s32[1]{0:T(128)} %bitcast.z_ref, s32[80]{0:T(128)} %reshape.26.off_ref, bf16[1024,128]{1,0:T(8,128)(2,1)} %get-tuple-element.57.cur_hbm, bf16[384,128]{1,0:T(8,128)(2,1)} %copy-done.11, bf16[384,128]{1,0:T(8,128)(2,1)} %copy-done.9, bf16[256,128]{1,0:T(8,128)(2,1)} %copy-done.16, ...), custom_call_target="tpu_custom_call" | custom-call | flops 335544320 | bytes 3670016 | tf_op jit(solution)/shard_map/pallas_call | solution.py:156
  86.2 2.4 %collective-permute-start.23 = (bf16[16,128,128]{2,1,0:T(8,128)(2,1)S(1)}, bf16[16,128,128]{2,1,0:T(8,128)(2,1)S(1)}, u32[]{:S(2)}, u32[]{:S(2)}) collective-permute-start(bf16[16,128,128]{2,1,0:T(8,128)(2,1)S(1)} %constant_dynamic-update-slice_fusion.14.rest_0_), channel_id=1, source_target_pairs={{0,4},{1,5},{2,6},{3,7},{4,0},{5,1},{6,2},{7,3},{8,12},{9,13},{10,... | collective-permute-start | bytes 1572872 | tf_op jit(solution)/shard_map/ppermute | solution.py:65
  88.5 1.5 %collective-permute-done.23.rest_1_ = bf16[16,128,128]{2,1,0:T(8,128)(2,1)S(1)} collective-permute-done((bf16[16,128,128]{2,1,0:T(8,128)(2,1)S(1)}, bf16[16,128,128]{2,1,0:T(8,128)(2,1)S(1)}, u32[]{:S(2)}, u32[]{:S(2)}) %collective-permute-start.23) | collective-permute-done | bytes 524320 | tf_op jit(solution)/shard_map/ppermute | solution.py:65
  90.9 5.2 %shard_map.87 = f32[1024,128]{1,0:T(8,128)} custom-call(s32[1]{0:T(128)} %bitcast.z_ref, s32[48]{0:T(128)} %gather_fusion.1, bf16[16,128,128]{2,1,0:T(8,128)(2,1)} %copy-done.5, bf16[16,128,128]{2,1,0:T(8,128)(2,1)} %copy-done.8, bf16[8,6,128,128]{3,2,1,0:T(8,128)(2,1)} %rest_2_.5, f32[1024,128]{1,0:T(8,128)} %shard_map.86.rest_3_, ...), custom_call_target="tpu_custom_call" | custom-call | flops 201326592 | bytes 4718592 | tf_op jit(solution)/shard_map/pallas_call | solution.py:258
  (116 shorter events, 23.0 us)
Async XLA Ops:
  3.4 16.3 %collective-permute-start.1 = (bf16[128,128]{1,0:T(8,128)(2,1)S(1)}, bf16[128,128]{1,0:T(8,128)(2,1)S(1)}, u32[]{:S(2)}, u32[]{:S(2)}) collective-permute-start(bf16[128,128]{1,0:T(8,128)(2,1)S(1)} %gather_fusion), channel_id=1, source_target_pairs={{0,2},{1,3},{2,0},{3,1},{4,6},{5,7},{6,4},{7,5},{8,10},{9,11},{10,... | collective-permute-start | bytes 98312 | tf_op jit(solution)/shard_map/ppermute | solution.py:50
  5.8 13.9 %collective-permute-start = (bf16[384,128]{1,0:T(8,128)(2,1)S(1)}, bf16[384,128]{1,0:T(8,128)(2,1)S(1)}, u32[]{:S(2)}, u32[]{:S(2)}) collective-permute-start(bf16[384,128]{1,0:T(8,128)(2,1)S(1)} %get-tuple-element.67), channel_id=1, source_target_pairs={{0,1},{1,0},{2,3},{3,2},{4,5},{5,4},{6,7},{7,6},{8,9},{9,8},{10,11... | collective-permute-start | bytes 294920 | tf_op jit(solution)/shard_map/ppermute | solution.py:51
  7.1 12.6 %collective-permute-start.2 = (bf16[384,128]{1,0:T(8,128)(2,1)S(1)}, bf16[384,128]{1,0:T(8,128)(2,1)S(1)}, u32[]{:S(2)}, u32[]{:S(2)}) collective-permute-start(bf16[384,128]{1,0:T(8,128)(2,1)S(1)} %get-tuple-element.66), channel_id=1, source_target_pairs={{0,3},{1,2},{2,1},{3,0},{4,7},{5,6},{6,5},{7,4},{8,11},{9,10},{10,... | collective-permute-start | bytes 294920 | tf_op jit(solution)/shard_map/ppermute | solution.py:49
  7.1 12.6 %collective-permute-start.3 = (bf16[256,128]{1,0:T(8,128)(2,1)S(1)}, bf16[256,128]{1,0:T(8,128)(2,1)S(1)}, u32[]{:S(2)}, u32[]{:S(2)}) collective-permute-start(bf16[256,128]{1,0:T(8,128)(2,1)S(1)} %get-tuple-element.63), channel_id=1, source_target_pairs={{3,4},{7,8},{11,12},{15,16},{19,20},{23,24},{27,28},{4,3},{8,7},{1... | collective-permute-start | bytes 196616 | tf_op jit(solution)/shard_map/ppermute | solution.py:55
  20.8 8.2 %collective-permute-start.4 = (bf16[4,128,128]{2,1,0:T(8,128)(2,1)S(1)}, bf16[4,128,128]{2,1,0:T(8,128)(2,1)S(1)}, u32[]{:S(2)}, u32[]{:S(2)}) collective-permute-start(bf16[4,128,128]{2,1,0:T(8,128)(2,1)S(1)} %pad_maximum_fusion), channel_id=1, source_target_pairs={{0,8},{1,9},{2,10},{3,11},{4,12},{5,13},{6,14},{7,15},{8,0},{9,1},... | collective-permute-start | bytes 393224 | tf_op jit(solution)/shard_map/ppermute | solution.py:65
  22.0 7.7 %collective-permute-start.5 = (bf16[4,128,128]{2,1,0:T(8,128)(2,1)S(1)}, bf16[4,128,128]{2,1,0:T(8,128)(2,1)S(1)}, u32[]{:S(2)}, u32[]{:S(2)}) collective-permute-start(bf16[4,128,128]{2,1,0:T(8,128)(2,1)S(1)} %pad_maximum_fusion), channel_id=1, source_target_pairs={{0,16},{1,17},{2,18},{3,19},{4,20},{5,21},{6,22},{7,23},{8,24},{9,... | collective-permute-start | bytes 393224 | tf_op jit(solution)/shard_map/ppermute | solution.py:65
  22.3 7.5 %collective-permute-start.6 = (bf16[4,128,128]{2,1,0:T(8,128)(2,1)S(1)}, bf16[4,128,128]{2,1,0:T(8,128)(2,1)S(1)}, u32[]{:S(2)}, u32[]{:S(2)}) collective-permute-start(bf16[4,128,128]{2,1,0:T(8,128)(2,1)S(1)} %pad_maximum_fusion), channel_id=1, source_target_pairs={{0,24},{1,25},{2,26},{3,27},{4,28},{5,29},{6,30},{7,31},{8,16},{9,... | collective-permute-start | bytes 393224 | tf_op jit(solution)/shard_map/ppermute | solution.py:65
  29.9 2.0 %collective-permute-start.7 = (bf16[16,128,128]{2,1,0:T(8,128)(2,1)S(1)}, bf16[16,128,128]{2,1,0:T(8,128)(2,1)S(1)}, u32[]{:S(2)}, u32[]{:S(2)}) collective-permute-start(bf16[16,128,128]{2,1,0:T(8,128)(2,1)S(1)} %constant_dynamic-update-slice_fusion.rest_0_), channel_id=1, source_target_pairs={{0,4},{1,5},{2,6},{3,7},{4,0},{5,1},{6,2},{7,3},{8,12},{9,13},{10,... | collective-permute-start | bytes 1572872 | tf_op jit(solution)/shard_map/ppermute | solution.py:65
  38.0 7.7 %collective-permute-start.10 = (bf16[384,128]{1,0:T(8,128)(2,1)}, bf16[384,128]{1,0:T(8,128)(2,1)S(1)}, u32[]{:S(2)}, u32[]{:S(2)}) collective-permute-start(bf16[384,128]{1,0:T(8,128)(2,1)} %get-tuple-element.47), channel_id=1, source_target_pairs={{0,3},{1,2},{2,1},{3,0},{4,7},{5,6},{6,5},{7,4},{8,11},{9,10},{10,... | collective-permute-start | bytes 294920 | tf_op jit(solution)/shard_map/ppermute | solution.py:49
  39.2 8.2 %collective-permute-start.9 = (bf16[128,128]{1,0:T(8,128)(2,1)}, bf16[128,128]{1,0:T(8,128)(2,1)S(1)}, u32[]{:S(2)}, u32[]{:S(2)}) collective-permute-start(bf16[128,128]{1,0:T(8,128)(2,1)} %get-tuple-element.45), channel_id=1, source_target_pairs={{0,2},{1,3},{2,0},{3,1},{4,6},{5,7},{6,4},{7,5},{8,10},{9,11},{10,... | collective-permute-start | bytes 98312 | tf_op jit(solution)/shard_map/ppermute | solution.py:50
  39.2 8.2 %collective-permute-start.8 = (bf16[384,128]{1,0:T(8,128)(2,1)}, bf16[384,128]{1,0:T(8,128)(2,1)S(1)}, u32[]{:S(2)}, u32[]{:S(2)}) collective-permute-start(bf16[384,128]{1,0:T(8,128)(2,1)} %get-tuple-element.46), channel_id=1, source_target_pairs={{0,1},{1,0},{2,3},{3,2},{4,5},{5,4},{6,7},{7,6},{8,9},{9,8},{10,11... | collective-permute-start | bytes 294920 | tf_op jit(solution)/shard_map/ppermute | solution.py:51
  42.4 8.5 %collective-permute-start.11 = (bf16[256,128]{1,0:T(8,128)(2,1)}, bf16[256,128]{1,0:T(8,128)(2,1)S(1)}, u32[]{:S(2)}, u32[]{:S(2)}) collective-permute-start(bf16[256,128]{1,0:T(8,128)(2,1)} %get-tuple-element.49), channel_id=1, source_target_pairs={{3,4},{7,8},{11,12},{15,16},{19,20},{23,24},{27,28},{4,3},{8,7},{1... | collective-permute-start | bytes 196616 | tf_op jit(solution)/shard_map/ppermute | solution.py:55
  48.2 8.8 %collective-permute-start.12 = (bf16[4,128,128]{2,1,0:T(8,128)(2,1)S(1)}, bf16[4,128,128]{2,1,0:T(8,128)(2,1)S(1)}, u32[]{:S(2)}, u32[]{:S(2)}) collective-permute-start(bf16[4,128,128]{2,1,0:T(8,128)(2,1)S(1)} %pad_maximum_fusion.1), channel_id=1, source_target_pairs={{0,8},{1,9},{2,10},{3,11},{4,12},{5,13},{6,14},{7,15},{8,0},{9,1},... | collective-permute-start | bytes 393224 | tf_op jit(solution)/shard_map/ppermute | solution.py:65
  49.1 7.9 %collective-permute-start.13 = (bf16[4,128,128]{2,1,0:T(8,128)(2,1)S(1)}, bf16[4,128,128]{2,1,0:T(8,128)(2,1)S(1)}, u32[]{:S(2)}, u32[]{:S(2)}) collective-permute-start(bf16[4,128,128]{2,1,0:T(8,128)(2,1)S(1)} %pad_maximum_fusion.1), channel_id=1, source_target_pairs={{0,16},{1,17},{2,18},{3,19},{4,20},{5,21},{6,22},{7,23},{8,24},{9,... | collective-permute-start | bytes 393224 | tf_op jit(solution)/shard_map/ppermute | solution.py:65
  49.4 7.6 %collective-permute-start.14 = (bf16[4,128,128]{2,1,0:T(8,128)(2,1)S(1)}, bf16[4,128,128]{2,1,0:T(8,128)(2,1)S(1)}, u32[]{:S(2)}, u32[]{:S(2)}) collective-permute-start(bf16[4,128,128]{2,1,0:T(8,128)(2,1)S(1)} %pad_maximum_fusion.1), channel_id=1, source_target_pairs={{0,24},{1,25},{2,26},{3,27},{4,28},{5,29},{6,30},{7,31},{8,16},{9,... | collective-permute-start | bytes 393224 | tf_op jit(solution)/shard_map/ppermute | solution.py:65
  57.1 3.8 %collective-permute-start.15 = (bf16[16,128,128]{2,1,0:T(8,128)(2,1)S(1)}, bf16[16,128,128]{2,1,0:T(8,128)(2,1)S(1)}, u32[]{:S(2)}, u32[]{:S(2)}) collective-permute-start(bf16[16,128,128]{2,1,0:T(8,128)(2,1)S(1)} %constant_dynamic-update-slice_fusion.7.rest_0_), channel_id=1, source_target_pairs={{0,4},{1,5},{2,6},{3,7},{4,0},{5,1},{6,2},{7,3},{8,12},{9,13},{10,... | collective-permute-start | bytes 1572872 | tf_op jit(solution)/shard_map/ppermute | solution.py:65
  67.1 7.5 %collective-permute-start.18 = (bf16[384,128]{1,0:T(8,128)(2,1)}, bf16[384,128]{1,0:T(8,128)(2,1)S(1)}, u32[]{:S(2)}, u32[]{:S(2)}) collective-permute-start(bf16[384,128]{1,0:T(8,128)(2,1)} %get-tuple-element.56), channel_id=1, source_target_pairs={{0,3},{1,2},{2,1},{3,0},{4,7},{5,6},{6,5},{7,4},{8,11},{9,10},{10,... | collective-permute-start | bytes 294920 | tf_op jit(solution)/shard_map/ppermute | solution.py:49
  68.0 8.4 %collective-permute-start.17 = (bf16[128,128]{1,0:T(8,128)(2,1)}, bf16[128,128]{1,0:T(8,128)(2,1)S(1)}, u32[]{:S(2)}, u32[]{:S(2)}) collective-permute-start(bf16[128,128]{1,0:T(8,128)(2,1)} %get-tuple-element.54), channel_id=1, source_target_pairs={{0,2},{1,3},{2,0},{3,1},{4,6},{5,7},{6,4},{7,5},{8,10},{9,11},{10,... | collective-permute-start | bytes 98312 | tf_op jit(solution)/shard_map/ppermute | solution.py:50
  68.6 7.8 %collective-permute-start.16 = (bf16[384,128]{1,0:T(8,128)(2,1)}, bf16[384,128]{1,0:T(8,128)(2,1)S(1)}, u32[]{:S(2)}, u32[]{:S(2)}) collective-permute-start(bf16[384,128]{1,0:T(8,128)(2,1)} %get-tuple-element.55), channel_id=1, source_target_pairs={{0,1},{1,0},{2,3},{3,2},{4,5},{5,4},{6,7},{7,6},{8,9},{9,8},{10,11... | collective-permute-start | bytes 294920 | tf_op jit(solution)/shard_map/ppermute | solution.py:51
  71.5 8.4 %collective-permute-start.19 = (bf16[256,128]{1,0:T(8,128)(2,1)}, bf16[256,128]{1,0:T(8,128)(2,1)S(1)}, u32[]{:S(2)}, u32[]{:S(2)}) collective-permute-start(bf16[256,128]{1,0:T(8,128)(2,1)} %get-tuple-element.58), channel_id=1, source_target_pairs={{3,4},{7,8},{11,12},{15,16},{19,20},{23,24},{27,28},{4,3},{8,7},{1... | collective-permute-start | bytes 196616 | tf_op jit(solution)/shard_map/ppermute | solution.py:55
  77.2 8.8 %collective-permute-start.20 = (bf16[4,128,128]{2,1,0:T(8,128)(2,1)S(1)}, bf16[4,128,128]{2,1,0:T(8,128)(2,1)S(1)}, u32[]{:S(2)}, u32[]{:S(2)}) collective-permute-start(bf16[4,128,128]{2,1,0:T(8,128)(2,1)S(1)} %pad_maximum_fusion.2), channel_id=1, source_target_pairs={{0,8},{1,9},{2,10},{3,11},{4,12},{5,13},{6,14},{7,15},{8,0},{9,1},... | collective-permute-start | bytes 393224 | tf_op jit(solution)/shard_map/ppermute | solution.py:65
  77.6 8.4 %collective-permute-start.21 = (bf16[4,128,128]{2,1,0:T(8,128)(2,1)S(1)}, bf16[4,128,128]{2,1,0:T(8,128)(2,1)S(1)}, u32[]{:S(2)}, u32[]{:S(2)}) collective-permute-start(bf16[4,128,128]{2,1,0:T(8,128)(2,1)S(1)} %pad_maximum_fusion.2), channel_id=1, source_target_pairs={{0,16},{1,17},{2,18},{3,19},{4,20},{5,21},{6,22},{7,23},{8,24},{9,... | collective-permute-start | bytes 393224 | tf_op jit(solution)/shard_map/ppermute | solution.py:65
  78.0 8.1 %collective-permute-start.22 = (bf16[4,128,128]{2,1,0:T(8,128)(2,1)S(1)}, bf16[4,128,128]{2,1,0:T(8,128)(2,1)S(1)}, u32[]{:S(2)}, u32[]{:S(2)}) collective-permute-start(bf16[4,128,128]{2,1,0:T(8,128)(2,1)S(1)} %pad_maximum_fusion.2), channel_id=1, source_target_pairs={{0,24},{1,25},{2,26},{3,27},{4,28},{5,29},{6,30},{7,31},{8,16},{9,... | collective-permute-start | bytes 393224 | tf_op jit(solution)/shard_map/ppermute | solution.py:65
  86.2 3.9 %collective-permute-start.23 = (bf16[16,128,128]{2,1,0:T(8,128)(2,1)S(1)}, bf16[16,128,128]{2,1,0:T(8,128)(2,1)S(1)}, u32[]{:S(2)}, u32[]{:S(2)}) collective-permute-start(bf16[16,128,128]{2,1,0:T(8,128)(2,1)S(1)} %constant_dynamic-update-slice_fusion.14.rest_0_), channel_id=1, source_target_pairs={{0,4},{1,5},{2,6},{3,7},{4,0},{5,1},{6,2},{7,3},{8,12},{9,13},{10,... | collective-permute-start | bytes 1572872 | tf_op jit(solution)/shard_map/ppermute | solution.py:65
  (20 other events, 111.3 us)

commit v18 on v14

--- a/solution.py
+++ b/solution.py
@@ -59,21 +59,18 @@
     buf = jnp.concatenate([owned[None], r1[None, :rows], r2[None], r3[None, :rows]], 0)
     offs = [0, 1, 2, 3]
     rounds = ROUNDS_32
-    pieces = [buf]
-    done = None
-    for r, group in enumerate(rounds[1:]):
-        sent = {m: lax.ppermute(buf, AXES, pairs(m)) for m in sorted(group, key=lambda m: -m)}
-        recvs = [sent[m] for m in group]
-        if done is None:
-            done, recvs = lax.optimization_barrier((middle((r1, r3, rc)), recvs))
-        offs = offs + [o ^ m for m in group for o in offs]
-        pieces = [buf] + recvs
-        if r + 2 < len(rounds):
-            buf = jnp.concatenate(pieces, 0)
+    assert len(rounds) == 3 and len(rounds[2]) == 1
+    last = rounds[2][0]
+    early = lax.ppermute(buf, AXES, pairs(last))
+    group = rounds[1]
+    sent = {m: lax.ppermute(buf, AXES, pairs(m)) for m in sorted(group, key=lambda m: -m)}
+    recvs = [sent[m] for m in group]
+    done, recvs = lax.optimization_barrier((middle((r1, r3, rc)), recvs))
+    more = [o ^ m for m in group for o in offs]
+    rest = jnp.concatenate(recvs, 0)
+    pieces = [buf, rest, early, lax.ppermute(rest, AXES, pairs(last))]
+    offs = offs + more + [o ^ last for o in offs] + [o ^ last for o in more]
     assert sorted(offs) == list(range(count))
-    where = np.zeros(count, np.int32)
-    for p, o in enumerate(offs):
-        where[o] = p
     return done, pieces, prep
 
 

time: 96.8 us -> 111 us (1.15)
  waiting for transfers between devices: 8.71 us -> 17.2 us
  starting transfers between devices: 37.3 us -> 45.4 us
  local copies, waits for them, and re-layouts: 11.4 us -> 9.3 us
    ppermute x3, starting transfers between devices: 0.53 us -> 8.82 us  [exchange(): r3 = lax.ppermute(p3, AXES, pairs(3))]
    ppermute x0 -> x6, starting transfers between devices: none -> 6.84 us  [the longest x3 6.61 us: exchange(): pieces = [buf, rest, early, lax.ppermute(rest, AXES, pairs(last))]]
    ppermute x3, starting transfers between devices: 7.53 us -> 1.24 us  [exchange(): r1 = lax.ppermute(p1, AXES, pairs(1))]
    ppermute x3, waiting for transfers between devices: 0.01 us -> 5.25 us  [exchange(): r3 = lax.ppermute(p3, AXES, pairs(3))]
    ppermute x12 -> x9, starting transfers between devices: 13.3 us -> 8.14 us  [exchange(): lax.ppermute(buf, AXES, pairs(m))]
    ppermute x3, waiting for transfers between devices: 0.01 us -> 4.62 us  [exchange(): rc = lax.ppermute(pc, AXES, cross)]
    ppermute x3, starting transfers between devices: 13 us -> 17.6 us  [exchange(): rc = lax.ppermute(pc, AXES, cross)]
    ppermute x0 -> x6, waiting for transfers between devices: none -> 4.38 us  [the longest x3 4.37 us: exchange(): early = lax.ppermute(buf, AXES, pairs(last))]
  transfers between devices with their start and end apart: 24 -> 27, of which waited for: 6 -> 10; matrix products, arithmetic and copies ran while one was open for 12% -> 6% of each run, Pallas kernels for 15% -> 13%
where the time goes in v18:
time: 111 us
  starting transfers between devices  45.4 us (41%)
  Pallas kernels  29.5 us (27%)
  waiting for transfers between devices  17.2 us (15%)
  local copies, waits for them, and re-layouts  9.3 us (8%)
  other arithmetic  8.9 us (8%)
    ppermute x3, starting transfers between devices, exchange(): rc = lax.ppermute(pc, AXES, cross)  17.6 us
    pallas_call x3, Pallas kernels, hub_call(): pl.pallas_call(functools.partial(hub_kernel, n_hub, width, final), cost_e...  15.4 us
    pallas_call x3, Pallas kernels, band_call(): pl.pallas_call(functools.partial(band_kernel, fast, n_own), cost_estimate...  14 us
    ppermute x3, starting transfers between devices, exchange(): r3 = lax.ppermute(p3, AXES, pairs(3))  8.82 us
    ppermute x9, starting transfers between devices, exchange(): lax.ppermute(buf, AXES, pairs(m))  8.14 us
    ppermute x3, starting transfers between devices, exchange(): pieces = [buf, rest, early, lax.ppermute(rest, AXES, pairs(last))]  6.61 us
    unnamed x56, local copies, waits for them, and re-layouts  5.55 us
    ppermute x3, waiting for transfers between devices, exchange(): r3 = lax.ppermute(p3, AXES, pairs(3))  5.25 us
  transfers between devices with their start and end apart: 27, of which 10 were waited for; matrix products, arithmetic and copies ran while one was open for 6% of the time, Pallas kernels for 13%

profile of v18, /device:TPU:5, one launch (start us, length us, event | category | flops | bytes accessed | tf_op | source)
XLA Modules:
  0.0 110.8 jit_solution(9578412764032061764)
XLA Ops:
  3.4 2.4 %collective-permute-start.1 = (bf16[128,128]{1,0:T(8,128)(2,1)S(1)}, bf16[128,128]{1,0:T(8,128)(2,1)S(1)}, u32[]{:S(2)}, u32[]{:S(2)}) collective-permute-start(bf16[128,128]{1,0:T(8,128)(2,1)S(1)} %gather_fusion), channel_id=1, source_target_pairs={{0,2},{1,3},{2,0},{3,1},{4,6},{5,7},{6,4},{7,5},{8,10},{9,11},{10,... | collective-permute-start | bytes 98312 | tf_op jit(solution)/shard_map/ppermute | solution.py:50
  5.8 3.8 %collective-permute-start.3 = (bf16[256,128]{1,0:T(8,128)(2,1)S(1)}, bf16[256,128]{1,0:T(8,128)(2,1)S(1)}, u32[]{:S(2)}, u32[]{:S(2)}) collective-permute-start(bf16[256,128]{1,0:T(8,128)(2,1)S(1)} %get-tuple-element.63), channel_id=1, source_target_pairs={{3,4},{7,8},{11,12},{15,16},{19,20},{23,24},{27,28},{4,3},{8,7},{1... | collective-permute-start | bytes 196616 | tf_op jit(solution)/shard_map/ppermute | solution.py:55
  9.6 3.2 %collective-permute-start.2 = (bf16[384,128]{1,0:T(8,128)(2,1)S(1)}, bf16[384,128]{1,0:T(8,128)(2,1)S(1)}, u32[]{:S(2)}, u32[]{:S(2)}) collective-permute-start(bf16[384,128]{1,0:T(8,128)(2,1)S(1)} %get-tuple-element.66), channel_id=1, source_target_pairs={{0,3},{1,2},{2,1},{3,0},{4,7},{5,6},{6,5},{7,4},{8,11},{9,10},{10,... | collective-permute-start | bytes 294920 | tf_op jit(solution)/shard_map/ppermute | solution.py:49
  12.8 1.5 %fusion.rest_8_ = bf16[128,1024]{1,0:T(8,128)(2,1)} fusion(s32[128]{0:T(128)} %param.14), kind=kLoop, calls=%fused_computation.6 | loop fusion | flops 262144 | bytes 262656 | tf_op jit(solution)/shard_map/convert_element_type | solution.py:297
  15.1 2.2 %convert_reduce_fusion = f32[8,128]{1,0:T(8,128)S(1)} fusion(bf16[8,10,128,128]{3,2,1,0:T(8,128)(2,1)} %rest_3_.5), kind=kLoop, calls=%fused_computation.2 | loop fusion | flops 2620416 | bytes 2625536 | tf_op jit(solution)/shard_map/reduce_sum | solution.py:286
  21.2 1.5 %collective-permute-start.4 = (bf16[4,128,128]{2,1,0:T(8,128)(2,1)S(1)}, bf16[4,128,128]{2,1,0:T(8,128)(2,1)S(1)}, u32[]{:S(2)}, u32[]{:S(2)}) collective-permute-start(bf16[4,128,128]{2,1,0:T(8,128)(2,1)S(1)} %pad_maximum_fusion.rest_0_), channel_id=1, source_target_pairs={{0,8},{1,9},{2,10},{3,11},{4,12},{5,13},{6,14},{7,15},{8,0},{9,1},... | collective-permute-start | bytes 393224 | tf_op jit(solution)/shard_map/ppermute | solution.py:66
  23.3 4.7 %shard_map.82.rest_5_ = f32[1024,128]{1,0:T(8,128)} custom-call(s32[1]{0:T(128)} %bitcast.z_ref, s32[80]{0:T(128)} %reshape.26.off_ref, bf16[1024,128]{1,0:T(8,128)(2,1)} %copy-done.2, bf16[384,128]{1,0:T(8,128)(2,1)} %copy-done.17, bf16[384,128]{1,0:T(8,128)(2,1)} %copy-done.16, bf16[256,128]{1,0:T(8,128)(2,1)} %copy-done.21, bf16[8,10,128,128]{3,2,1,0:T(8,128)(2,1)} %rest_3_.5), custom_call_target="tpu_custom_call" | custom-call | flops 335544320 | bytes 3670016 | tf_op jit(solution)/shard_map/pallas_call | solution.py:153
  32.7 5.3 %shard_map.83 = (bf16[1024,128]{1,0:T(8,128)(2,1)}, bf16[128,128]{1,0:T(8,128)(2,1)}, bf16[384,128]{1,0:T(8,128)(2,1)}, bf16[384,128]{1,0:T(8,128)(2,1)}, bf16[256,128]{1,0:T(8,128)(2,1)}) custom-call(s32[1]{0:T(128)} %bitcast.z_ref, s32[48]{0:T(128)} %gather_fusion.1, bf16[4,128,128]{2,1,0:T(8,128)(2,1)} %copy-done.8, bf16[12,128,128]{2,1,0:T(8,128)(2,1)} %copy-done.3, ...), custom_call_target="tpu_custom_call" | custom-call | flops 201326592 | bytes 4718592 | tf_op jit(solution)/shard_map/pallas_call | solution.py:253
  39.2 2.4 %collective-permute-start.11 = (bf16[384,128]{1,0:T(8,128)(2,1)}, bf16[384,128]{1,0:T(8,128)(2,1)S(1)}, u32[]{:S(2)}, u32[]{:S(2)}) collective-permute-start(bf16[384,128]{1,0:T(8,128)(2,1)} %get-tuple-element.47), channel_id=1, source_target_pairs={{0,3},{1,2},{2,1},{3,0},{4,7},{5,6},{6,5},{7,4},{8,11},{9,10},{10,... | collective-permute-start | bytes 294920 | tf_op jit(solution)/shard_map/ppermute | solution.py:49
  42.3 3.3 %collective-permute-done.11.rest_1_ = bf16[384,128]{1,0:T(8,128)(2,1)S(1)} collective-permute-done((bf16[384,128]{1,0:T(8,128)(2,1)}, bf16[384,128]{1,0:T(8,128)(2,1)S(1)}, u32[]{:S(2)}, u32[]{:S(2)}) %collective-permute-start.11) | collective-permute-done | bytes 98336 | tf_op jit(solution)/shard_map/ppermute | solution.py:49
  47.6 1.5 %collective-permute-start.13 = (bf16[4,128,128]{2,1,0:T(8,128)(2,1)S(1)}, bf16[4,128,128]{2,1,0:T(8,128)(2,1)S(1)}, u32[]{:S(2)}, u32[]{:S(2)}) collective-permute-start(bf16[4,128,128]{2,1,0:T(8,128)(2,1)S(1)} %pad_maximum_fusion.1.rest_0_), channel_id=1, source_target_pairs={{0,8},{1,9},{2,10},{3,11},{4,12},{5,13},{6,14},{7,15},{8,0},{9,1},... | collective-permute-start | bytes 393224 | tf_op jit(solution)/shard_map/ppermute | solution.py:66
  49.1 6.3 %collective-permute-start.12 = (bf16[256,128]{1,0:T(8,128)(2,1)}, bf16[256,128]{1,0:T(8,128)(2,1)S(1)}, u32[]{:S(2)}, u32[]{:S(2)}) collective-permute-start(bf16[256,128]{1,0:T(8,128)(2,1)} %get-tuple-element.49), channel_id=1, source_target_pairs={{3,4},{7,8},{11,12},{15,16},{19,20},{23,24},{27,28},{4,3},{8,7},{1... | collective-permute-start | bytes 196616 | tf_op jit(solution)/shard_map/ppermute | solution.py:55
  55.5 2.1 %collective-permute-done.12.rest_2_ = bf16[256,128]{1,0:T(8,128)(2,1)S(1)} collective-permute-done((bf16[256,128]{1,0:T(8,128)(2,1)}, bf16[256,128]{1,0:T(8,128)(2,1)S(1)}, u32[]{:S(2)}, u32[]{:S(2)}) %collective-permute-start.12) | collective-permute-done | bytes 65568 | tf_op jit(solution)/shard_map/ppermute | solution.py:55
  58.2 4.7 %shard_map.84.rest_5_ = f32[1024,128]{1,0:T(8,128)} custom-call(s32[1]{0:T(128)} %bitcast.z_ref, s32[80]{0:T(128)} %reshape.26.off_ref, bf16[1024,128]{1,0:T(8,128)(2,1)} %get-tuple-element.48.cur_hbm, bf16[384,128]{1,0:T(8,128)(2,1)} %copy-done.13, bf16[384,128]{1,0:T(8,128)(2,1)} %copy-done.15, bf16[256,128]{1,0:T(8,128)(2,1)} %copy-done.23, ...), custom_call_target="tpu_custom_call" | custom-call | flops 335544320 | bytes 3670016 | tf_op jit(solution)/shard_map/pallas_call | solution.py:153
  63.0 3.6 %collective-permute-start.17 = (bf16[12,128,128]{2,1,0:T(8,128)(2,1)S(1)}, bf16[12,128,128]{2,1,0:T(8,128)(2,1)S(1)}, u32[]{:S(2)}, u32[]{:S(2)}) collective-permute-start(bf16[12,128,128]{2,1,0:T(8,128)(2,1)S(1)} %constant_dynamic-update-slice_fusion.3.rest_1_), channel_id=1, source_target_pairs={{0,4},{1,5},{2,6},{3,7},{4,0},{5,1},{6,2},{7,3},{8,12},{9,13},{10,... | collective-permute-start | bytes 1179656 | tf_op jit(solution)/shard_map/ppermute | solution.py:71
  69.6 5.3 %shard_map.85 = (bf16[1024,128]{1,0:T(8,128)(2,1)}, bf16[128,128]{1,0:T(8,128)(2,1)}, bf16[384,128]{1,0:T(8,128)(2,1)}, bf16[384,128]{1,0:T(8,128)(2,1)}, bf16[256,128]{1,0:T(8,128)(2,1)}) custom-call(s32[1]{0:T(128)} %bitcast.z_ref, s32[48]{0:T(128)} %gather_fusion.1, bf16[4,128,128]{2,1,0:T(8,128)(2,1)} %copy-done.6, bf16[12,128,128]{2,1,0:T(8,128)(2,1)} %copy-done.4, ...), custom_call_target="tpu_custom_call" | custom-call | flops 201326592 | bytes 4718592 | tf_op jit(solution)/shard_map/pallas_call | solution.py:253
  75.3 3.2 %collective-permute-start.20 = (bf16[384,128]{1,0:T(8,128)(2,1)}, bf16[384,128]{1,0:T(8,128)(2,1)S(1)}, u32[]{:S(2)}, u32[]{:S(2)}) collective-permute-start(bf16[384,128]{1,0:T(8,128)(2,1)} %get-tuple-element.56), channel_id=1, source_target_pairs={{0,3},{1,2},{2,1},{3,0},{4,7},{5,6},{6,5},{7,4},{8,11},{9,10},{10,... | collective-permute-start | bytes 294920 | tf_op jit(solution)/shard_map/ppermute | solution.py:49
  79.5 2.0 %collective-permute-done.20.rest_1_ = bf16[384,128]{1,0:T(8,128)(2,1)S(1)} collective-permute-done((bf16[384,128]{1,0:T(8,128)(2,1)}, bf16[384,128]{1,0:T(8,128)(2,1)S(1)}, u32[]{:S(2)}, u32[]{:S(2)}) %collective-permute-start.20) | collective-permute-done | bytes 98336 | tf_op jit(solution)/shard_map/ppermute | solution.py:49
  83.6 1.5 %collective-permute-start.22 = (bf16[4,128,128]{2,1,0:T(8,128)(2,1)S(1)}, bf16[4,128,128]{2,1,0:T(8,128)(2,1)S(1)}, u32[]{:S(2)}, u32[]{:S(2)}) collective-permute-start(bf16[4,128,128]{2,1,0:T(8,128)(2,1)S(1)} %pad_maximum_fusion.2.rest_0_), channel_id=1, source_target_pairs={{0,8},{1,9},{2,10},{3,11},{4,12},{5,13},{6,14},{7,15},{8,0},{9,1},... | collective-permute-start | bytes 393224 | tf_op jit(solution)/shard_map/ppermute | solution.py:66
  85.0 7.4 %collective-permute-start.21 = (bf16[256,128]{1,0:T(8,128)(2,1)}, bf16[256,128]{1,0:T(8,128)(2,1)S(1)}, u32[]{:S(2)}, u32[]{:S(2)}) collective-permute-start(bf16[256,128]{1,0:T(8,128)(2,1)} %get-tuple-element.58), channel_id=1, source_target_pairs={{3,4},{7,8},{11,12},{15,16},{19,20},{23,24},{27,28},{4,3},{8,7},{1... | collective-permute-start | bytes 196616 | tf_op jit(solution)/shard_map/ppermute | solution.py:55
  92.5 2.5 %collective-permute-done.21.rest_2_ = bf16[256,128]{1,0:T(8,128)(2,1)S(1)} collective-permute-done((bf16[256,128]{1,0:T(8,128)(2,1)}, bf16[256,128]{1,0:T(8,128)(2,1)S(1)}, u32[]{:S(2)}, u32[]{:S(2)}) %collective-permute-start.21) | collective-permute-done | bytes 65568 | tf_op jit(solution)/shard_map/ppermute | solution.py:55
  95.6 4.7 %shard_map.86.rest_5_ = f32[1024,128]{1,0:T(8,128)} custom-call(s32[1]{0:T(128)} %bitcast.z_ref, s32[80]{0:T(128)} %reshape.26.off_ref, bf16[1024,128]{1,0:T(8,128)(2,1)} %get-tuple-element.57.cur_hbm, bf16[384,128]{1,0:T(8,128)(2,1)} %copy-done.12, bf16[384,128]{1,0:T(8,128)(2,1)} %copy-done.14, bf16[256,128]{1,0:T(8,128)(2,1)} %copy-done.22, ...), custom_call_target="tpu_custom_call" | custom-call | flops 335544320 | bytes 3670016 | tf_op jit(solution)/shard_map/pallas_call | solution.py:153
  100.4 2.4 %collective-permute-start.26 = (bf16[12,128,128]{2,1,0:T(8,128)(2,1)S(1)}, bf16[12,128,128]{2,1,0:T(8,128)(2,1)S(1)}, u32[]{:S(2)}, u32[]{:S(2)}) collective-permute-start(bf16[12,128,128]{2,1,0:T(8,128)(2,1)S(1)} %constant_dynamic-update-slice_fusion.6.rest_1_), channel_id=1, source_target_pairs={{0,4},{1,5},{2,6},{3,7},{4,0},{5,1},{6,2},{7,3},{8,12},{9,13},{10,... | collective-permute-start | bytes 1179656 | tf_op jit(solution)/shard_map/ppermute | solution.py:71
  105.7 4.9 %shard_map.87 = f32[1024,128]{1,0:T(8,128)} custom-call(s32[1]{0:T(128)} %bitcast.z_ref, s32[48]{0:T(128)} %gather_fusion.1, bf16[4,128,128]{2,1,0:T(8,128)(2,1)} %copy-done.7, bf16[12,128,128]{2,1,0:T(8,128)(2,1)} %copy-done.5, bf16[4,128,128]{2,1,0:T(8,128)(2,1)} %copy-done.20, bf16[12,128,128]{2,1,0:T(8,128)(2,1)} %copy-done.11, ...), custom_call_target="tpu_custom_call" | custom-call | flops 201326592 | bytes 4718592 | tf_op jit(solution)/shard_map/pallas_call | solution.py:253
  (120 shorter events, 27.9 us)
Async XLA Ops:
  3.4 15.5 %collective-permute-start.1 = (bf16[128,128]{1,0:T(8,128)(2,1)S(1)}, bf16[128,128]{1,0:T(8,128)(2,1)S(1)}, u32[]{:S(2)}, u32[]{:S(2)}) collective-permute-start(bf16[128,128]{1,0:T(8,128)(2,1)S(1)} %gather_fusion), channel_id=1, source_target_pairs={{0,2},{1,3},{2,0},{3,1},{4,6},{5,7},{6,4},{7,5},{8,10},{9,11},{10,... | collective-permute-start | bytes 98312 | tf_op jit(solution)/shard_map/ppermute | solution.py:50
  5.8 13.1 %collective-permute-start.3 = (bf16[256,128]{1,0:T(8,128)(2,1)S(1)}, bf16[256,128]{1,0:T(8,128)(2,1)S(1)}, u32[]{:S(2)}, u32[]{:S(2)}) collective-permute-start(bf16[256,128]{1,0:T(8,128)(2,1)S(1)} %get-tuple-element.63), channel_id=1, source_target_pairs={{3,4},{7,8},{11,12},{15,16},{19,20},{23,24},{27,28},{4,3},{8,7},{1... | collective-permute-start | bytes 196616 | tf_op jit(solution)/shard_map/ppermute | solution.py:55
  9.6 9.3 %collective-permute-start.2 = (bf16[384,128]{1,0:T(8,128)(2,1)S(1)}, bf16[384,128]{1,0:T(8,128)(2,1)S(1)}, u32[]{:S(2)}, u32[]{:S(2)}) collective-permute-start(bf16[384,128]{1,0:T(8,128)(2,1)S(1)} %get-tuple-element.66), channel_id=1, source_target_pairs={{0,3},{1,2},{2,1},{3,0},{4,7},{5,6},{6,5},{7,4},{8,11},{9,10},{10,... | collective-permute-start | bytes 294920 | tf_op jit(solution)/shard_map/ppermute | solution.py:49
  12.8 6.1 %collective-permute-start = (bf16[384,128]{1,0:T(8,128)(2,1)S(1)}, bf16[384,128]{1,0:T(8,128)(2,1)S(1)}, u32[]{:S(2)}, u32[]{:S(2)}) collective-permute-start(bf16[384,128]{1,0:T(8,128)(2,1)S(1)} %get-tuple-element.67), channel_id=1, source_target_pairs={{0,1},{1,0},{2,3},{3,2},{4,5},{5,4},{6,7},{7,6},{8,9},{9,8},{10,11... | collective-permute-start | bytes 294920 | tf_op jit(solution)/shard_map/ppermute | solution.py:51
  19.9 8.0 %collective-permute-start.6 = (bf16[4,128,128]{2,1,0:T(8,128)(2,1)S(1)}, bf16[4,128,128]{2,1,0:T(8,128)(2,1)S(1)}, u32[]{:S(2)}, u32[]{:S(2)}) collective-permute-start(bf16[4,128,128]{2,1,0:T(8,128)(2,1)S(1)} %pad_maximum_fusion.rest_0_), channel_id=1, source_target_pairs={{0,24},{1,25},{2,26},{3,27},{4,28},{5,29},{6,30},{7,31},{8,16},{9,... | collective-permute-start | bytes 393224 | tf_op jit(solution)/shard_map/ppermute | solution.py:66
  21.2 8.0 %collective-permute-start.5 = (bf16[4,128,128]{2,1,0:T(8,128)(2,1)S(1)}, bf16[4,128,128]{2,1,0:T(8,128)(2,1)S(1)}, u32[]{:S(2)}, u32[]{:S(2)}) collective-permute-start(bf16[4,128,128]{2,1,0:T(8,128)(2,1)S(1)} %pad_maximum_fusion.rest_0_), channel_id=1, source_target_pairs={{0,16},{1,17},{2,18},{3,19},{4,20},{5,21},{6,22},{7,23},{8,24},{9,... | collective-permute-start | bytes 393224 | tf_op jit(solution)/shard_map/ppermute | solution.py:66
  21.2 8.0 %collective-permute-start.4 = (bf16[4,128,128]{2,1,0:T(8,128)(2,1)S(1)}, bf16[4,128,128]{2,1,0:T(8,128)(2,1)S(1)}, u32[]{:S(2)}, u32[]{:S(2)}) collective-permute-start(bf16[4,128,128]{2,1,0:T(8,128)(2,1)S(1)} %pad_maximum_fusion.rest_0_), channel_id=1, source_target_pairs={{0,8},{1,9},{2,10},{3,11},{4,12},{5,13},{6,14},{7,15},{8,0},{9,1},... | collective-permute-start | bytes 393224 | tf_op jit(solution)/shard_map/ppermute | solution.py:66
  29.2 2.1 %collective-permute-start.8 = (bf16[12,128,128]{2,1,0:T(8,128)(2,1)S(1)}, bf16[12,128,128]{2,1,0:T(8,128)(2,1)S(1)}, u32[]{:S(2)}, u32[]{:S(2)}) collective-permute-start(bf16[12,128,128]{2,1,0:T(8,128)(2,1)S(1)} %constant_dynamic-update-slice_fusion.rest_1_), channel_id=1, source_target_pairs={{0,4},{1,5},{2,6},{3,7},{4,0},{5,1},{6,2},{7,3},{8,12},{9,13},{10,... | collective-permute-start | bytes 1179656 | tf_op jit(solution)/shard_map/ppermute | solution.py:71
  38.0 4.3 %collective-permute-start.9 = (bf16[384,128]{1,0:T(8,128)(2,1)}, bf16[384,128]{1,0:T(8,128)(2,1)S(1)}, u32[]{:S(2)}, u32[]{:S(2)}) collective-permute-start(bf16[384,128]{1,0:T(8,128)(2,1)} %get-tuple-element.46), channel_id=1, source_target_pairs={{0,1},{1,0},{2,3},{3,2},{4,5},{5,4},{6,7},{7,6},{8,9},{9,8},{10,11... | collective-permute-start | bytes 294920 | tf_op jit(solution)/shard_map/ppermute | solution.py:51
  39.2 6.4 %collective-permute-start.10 = (bf16[128,128]{1,0:T(8,128)(2,1)}, bf16[128,128]{1,0:T(8,128)(2,1)S(1)}, u32[]{:S(2)}, u32[]{:S(2)}) collective-permute-start(bf16[128,128]{1,0:T(8,128)(2,1)} %get-tuple-element.45), channel_id=1, source_target_pairs={{0,2},{1,3},{2,0},{3,1},{4,6},{5,7},{6,4},{7,5},{8,10},{9,11},{10,... | collective-permute-start | bytes 98312 | tf_op jit(solution)/shard_map/ppermute | solution.py:50
  39.2 6.4 %collective-permute-start.11 = (bf16[384,128]{1,0:T(8,128)(2,1)}, bf16[384,128]{1,0:T(8,128)(2,1)S(1)}, u32[]{:S(2)}, u32[]{:S(2)}) collective-permute-start(bf16[384,128]{1,0:T(8,128)(2,1)} %get-tuple-element.47), channel_id=1, source_target_pairs={{0,3},{1,2},{2,1},{3,0},{4,7},{5,6},{6,5},{7,4},{8,11},{9,10},{10,... | collective-permute-start | bytes 294920 | tf_op jit(solution)/shard_map/ppermute | solution.py:49
  46.4 16.5 %collective-permute-start.15 = (bf16[4,128,128]{2,1,0:T(8,128)(2,1)S(1)}, bf16[4,128,128]{2,1,0:T(8,128)(2,1)S(1)}, u32[]{:S(2)}, u32[]{:S(2)}) collective-permute-start(bf16[4,128,128]{2,1,0:T(8,128)(2,1)S(1)} %pad_maximum_fusion.1.rest_0_), channel_id=1, source_target_pairs={{0,24},{1,25},{2,26},{3,27},{4,28},{5,29},{6,30},{7,31},{8,16},{9,... | collective-permute-start | bytes 393224 | tf_op jit(solution)/shard_map/ppermute | solution.py:66
  47.5 15.4 %collective-permute-start.14 = (bf16[4,128,128]{2,1,0:T(8,128)(2,1)S(1)}, bf16[4,128,128]{2,1,0:T(8,128)(2,1)S(1)}, u32[]{:S(2)}, u32[]{:S(2)}) collective-permute-start(bf16[4,128,128]{2,1,0:T(8,128)(2,1)S(1)} %pad_maximum_fusion.1.rest_0_), channel_id=1, source_target_pairs={{0,16},{1,17},{2,18},{3,19},{4,20},{5,21},{6,22},{7,23},{8,24},{9,... | collective-permute-start | bytes 393224 | tf_op jit(solution)/shard_map/ppermute | solution.py:66
  47.6 15.3 %collective-permute-start.13 = (bf16[4,128,128]{2,1,0:T(8,128)(2,1)S(1)}, bf16[4,128,128]{2,1,0:T(8,128)(2,1)S(1)}, u32[]{:S(2)}, u32[]{:S(2)}) collective-permute-start(bf16[4,128,128]{2,1,0:T(8,128)(2,1)S(1)} %pad_maximum_fusion.1.rest_0_), channel_id=1, source_target_pairs={{0,8},{1,9},{2,10},{3,11},{4,12},{5,13},{6,14},{7,15},{8,0},{9,1},... | collective-permute-start | bytes 393224 | tf_op jit(solution)/shard_map/ppermute | solution.py:66
  49.1 8.5 %collective-permute-start.12 = (bf16[256,128]{1,0:T(8,128)(2,1)}, bf16[256,128]{1,0:T(8,128)(2,1)S(1)}, u32[]{:S(2)}, u32[]{:S(2)}) collective-permute-start(bf16[256,128]{1,0:T(8,128)(2,1)} %get-tuple-element.49), channel_id=1, source_target_pairs={{3,4},{7,8},{11,12},{15,16},{19,20},{23,24},{27,28},{4,3},{8,7},{1... | collective-permute-start | bytes 196616 | tf_op jit(solution)/shard_map/ppermute | solution.py:55
  63.0 5.2 %collective-permute-start.17 = (bf16[12,128,128]{2,1,0:T(8,128)(2,1)S(1)}, bf16[12,128,128]{2,1,0:T(8,128)(2,1)S(1)}, u32[]{:S(2)}, u32[]{:S(2)}) collective-permute-start(bf16[12,128,128]{2,1,0:T(8,128)(2,1)S(1)} %constant_dynamic-update-slice_fusion.3.rest_1_), channel_id=1, source_target_pairs={{0,4},{1,5},{2,6},{3,7},{4,0},{5,1},{6,2},{7,3},{8,12},{9,13},{10,... | collective-permute-start | bytes 1179656 | tf_op jit(solution)/shard_map/ppermute | solution.py:71
  74.9 4.6 %collective-permute-start.18 = (bf16[384,128]{1,0:T(8,128)(2,1)}, bf16[384,128]{1,0:T(8,128)(2,1)S(1)}, u32[]{:S(2)}, u32[]{:S(2)}) collective-permute-start(bf16[384,128]{1,0:T(8,128)(2,1)} %get-tuple-element.55), channel_id=1, source_target_pairs={{0,1},{1,0},{2,3},{3,2},{4,5},{5,4},{6,7},{7,6},{8,9},{9,8},{10,11... | collective-permute-start | bytes 294920 | tf_op jit(solution)/shard_map/ppermute | solution.py:51
  75.0 6.5 %collective-permute-start.19 = (bf16[128,128]{1,0:T(8,128)(2,1)}, bf16[128,128]{1,0:T(8,128)(2,1)S(1)}, u32[]{:S(2)}, u32[]{:S(2)}) collective-permute-start(bf16[128,128]{1,0:T(8,128)(2,1)} %get-tuple-element.54), channel_id=1, source_target_pairs={{0,2},{1,3},{2,0},{3,1},{4,6},{5,7},{6,4},{7,5},{8,10},{9,11},{10,... | collective-permute-start | bytes 98312 | tf_op jit(solution)/shard_map/ppermute | solution.py:50
  75.3 6.2 %collective-permute-start.20 = (bf16[384,128]{1,0:T(8,128)(2,1)}, bf16[384,128]{1,0:T(8,128)(2,1)S(1)}, u32[]{:S(2)}, u32[]{:S(2)}) collective-permute-start(bf16[384,128]{1,0:T(8,128)(2,1)} %get-tuple-element.56), channel_id=1, source_target_pairs={{0,3},{1,2},{2,1},{3,0},{4,7},{5,6},{6,5},{7,4},{8,11},{9,10},{10,... | collective-permute-start | bytes 294920 | tf_op jit(solution)/shard_map/ppermute | solution.py:49
  82.3 17.9 %collective-permute-start.24 = (bf16[4,128,128]{2,1,0:T(8,128)(2,1)S(1)}, bf16[4,128,128]{2,1,0:T(8,128)(2,1)S(1)}, u32[]{:S(2)}, u32[]{:S(2)}) collective-permute-start(bf16[4,128,128]{2,1,0:T(8,128)(2,1)S(1)} %pad_maximum_fusion.2.rest_0_), channel_id=1, source_target_pairs={{0,24},{1,25},{2,26},{3,27},{4,28},{5,29},{6,30},{7,31},{8,16},{9,... | collective-permute-start | bytes 393224 | tf_op jit(solution)/shard_map/ppermute | solution.py:66
  83.3 17.0 %collective-permute-start.23 = (bf16[4,128,128]{2,1,0:T(8,128)(2,1)S(1)}, bf16[4,128,128]{2,1,0:T(8,128)(2,1)S(1)}, u32[]{:S(2)}, u32[]{:S(2)}) collective-permute-start(bf16[4,128,128]{2,1,0:T(8,128)(2,1)S(1)} %pad_maximum_fusion.2.rest_0_), channel_id=1, source_target_pairs={{0,16},{1,17},{2,18},{3,19},{4,20},{5,21},{6,22},{7,23},{8,24},{9,... | collective-permute-start | bytes 393224 | tf_op jit(solution)/shard_map/ppermute | solution.py:66
  83.6 16.7 %collective-permute-start.22 = (bf16[4,128,128]{2,1,0:T(8,128)(2,1)S(1)}, bf16[4,128,128]{2,1,0:T(8,128)(2,1)S(1)}, u32[]{:S(2)}, u32[]{:S(2)}) collective-permute-start(bf16[4,128,128]{2,1,0:T(8,128)(2,1)S(1)} %pad_maximum_fusion.2.rest_0_), channel_id=1, source_target_pairs={{0,8},{1,9},{2,10},{3,11},{4,12},{5,13},{6,14},{7,15},{8,0},{9,1},... | collective-permute-start | bytes 393224 | tf_op jit(solution)/shard_map/ppermute | solution.py:66
  85.0 9.9 %collective-permute-start.21 = (bf16[256,128]{1,0:T(8,128)(2,1)}, bf16[256,128]{1,0:T(8,128)(2,1)S(1)}, u32[]{:S(2)}, u32[]{:S(2)}) collective-permute-start(bf16[256,128]{1,0:T(8,128)(2,1)} %get-tuple-element.58), channel_id=1, source_target_pairs={{3,4},{7,8},{11,12},{15,16},{19,20},{23,24},{27,28},{4,3},{8,7},{1... | collective-permute-start | bytes 196616 | tf_op jit(solution)/shard_map/ppermute | solution.py:55
  100.4 4.0 %collective-permute-start.26 = (bf16[12,128,128]{2,1,0:T(8,128)(2,1)S(1)}, bf16[12,128,128]{2,1,0:T(8,128)(2,1)S(1)}, u32[]{:S(2)}, u32[]{:S(2)}) collective-permute-start(bf16[12,128,128]{2,1,0:T(8,128)(2,1)S(1)} %constant_dynamic-update-slice_fusion.6.rest_1_), channel_id=1, source_target_pairs={{0,4},{1,5},{2,6},{3,7},{4,0},{5,1},{6,2},{7,3},{8,12},{9,13},{10,... | collective-permute-start | bytes 1179656 | tf_op jit(solution)/shard_map/ppermute | solution.py:71
  (28 other events, 197.4 us)

commit v19 on v14

--- a/solution.py
+++ b/solution.py
@@ -170,11 +170,11 @@
 def hub_kernel(n_hub, width, final, z_ref, hidx_ref, *rest):
     hub_hbm = rest[:n_hub]
     if final:
-        (ht_hbm, band_hbm, deg_hbm, seeds_hbm, out_ref, hub, ht, band, deg, seeds, sem) = rest[n_hub:]
+        (ht_hbm, band_hbm, deg_ref, seeds_hbm, out_ref, hub, ht, band, seeds, sem) = rest[n_hub:]
     else:
-        (ht_hbm, band_hbm, deg_hbm, seeds_hbm, pick_ref,
+        (ht_hbm, band_hbm, deg_ref, seeds_hbm, pick_ref,
          cur_ref, owned_ref, p1_ref, p3_ref, pc_ref,
-         hub, ht, band, deg, seeds, sem) = rest[n_hub:]
+         hub, ht, band, seeds, sem) = rest[n_hub:]
     blocks, k_hub, rows = ht.shape[0], ht.shape[1], ht.shape[2]
     per_block = []
     for b in range(blocks):
@@ -182,7 +182,6 @@
         per_block.append([
             pltpu.make_async_copy(ht_hbm.at[b], ht.at[b], sem.at[n_hub + 4 * b]),
             pltpu.make_async_copy(band_hbm.at[span], band.at[span], sem.at[n_hub + 4 * b + 1]),
-            pltpu.make_async_copy(deg_hbm.at[span], deg.at[span], sem.at[n_hub + 4 * b + 2]),
             pltpu.make_async_copy(seeds_hbm.at[span], seeds.at[span], sem.at[n_hub + 4 * b + 3]),
         ])
     copies = []
@@ -198,6 +197,7 @@
     for b in range(1, blocks):
         for c in per_block[b]:
             c.start()
+    by_row = jnp.transpose(deg_ref[...])
     for c in copies:
         c.wait()
     for b in range(blocks):
@@ -212,7 +212,7 @@
             acc = acc + jnp.dot(lhs, rhs, preferred_element_type=jnp.float32)
         if k_hub % 2:
             acc = acc + jnp.dot(ht[b, k_hub - 1], blk(k_hub - 1), preferred_element_type=jnp.float32)
-        gathered = (band[span] + acc) / deg[span]
+        gathered = (band[span] + acc) / by_row[:, b:b + 1]
         labels = spread_weight * gathered + (1.0 - spread_weight) * seeds[span].astype(jnp.float32)
         if final:
             out_ref[span, :] = labels
@@ -256,14 +256,13 @@
     return pl.pallas_call(
         functools.partial(hub_kernel, n_hub, width, final),
         cost_estimate=pl.CostEstimate(flops=flops, transcendentals=0, bytes_accessed=bytes_accessed),
-        in_specs=[SMEM, SMEM] + [ANY] * (n_hub + 4) + ([] if final else [VMEM]),
+        in_specs=[SMEM, SMEM] + [ANY] * (n_hub + 2) + [VMEM, ANY] + ([] if final else [VMEM]),
         out_specs=[VMEM] * len(outs),
         out_shape=outs,
         scratch_shapes=[
             pltpu.VMEM((n_hub_blocks, rows, classes), bf),
             pltpu.VMEM(hub_tiles.shape, hub_tiles.dtype),
             pltpu.VMEM(seeds.shape, jnp.float32),
-            pltpu.VMEM(degree.shape, jnp.float32),
             pltpu.VMEM(seeds.shape, seeds.dtype),
             pltpu.SemaphoreType.DMA((n_hub + 4 * blocks,)),
         ],
@@ -289,7 +288,8 @@
     degree = jnp.sum(band_tiles, axis=(1, 3), dtype=jnp.float32) + jnp.sum(
         hub_tiles, axis=(1, 3), dtype=jnp.float32
     )
-    degree = jnp.broadcast_to(degree.reshape(-1, 1), seeds.shape)
+    lanes = degree.shape[1]
+    degree = jnp.zeros((lanes, lanes), jnp.float32).at[: degree.shape[0]].set(degree)
     width = BW * block_rows
     z = lax.axis_index("hub").astype(jnp.int32).reshape(1)
     current = seeds.astype(jnp.bfloat16)

time: 96.8 us -> 96.5 us (level)
    broadcast_in_dim x1 -> x0, local copies, waits for them, and re-layouts: 0.98 us -> none  [body(): degree = jnp.broadcast_to(degree.reshape(-1, 1), seeds.shape)]
  transfers between devices with their start and end apart: 24 -> 24, of which waited for: 6 -> 6; matrix products, arithmetic and copies ran while one was open for 12% -> 13% of each run, Pallas kernels for 15% -> 15%
where the time goes in v19:
time: 96.5 us; the launch traced here: 95.2 us
  starting transfers between devices  37.1 us (38%)
  Pallas kernels  29.5 us (31%)
  local copies, waits for them, and re-layouts  11.1 us (12%)
  waiting for transfers between devices  8.91 us (9%)
  other arithmetic  8.19 us (8%)
    pallas_call x3, Pallas kernels, hub_call(): pl.pallas_call(functools.partial(hub_kernel, n_hub, width, final), cost_e...  15.5 us
    pallas_call x3, Pallas kernels, band_call(): pl.pallas_call(functools.partial(band_kernel, fast, n_own), cost_estimate...  14 us
    ppermute x12, starting transfers between devices, exchange(): lax.ppermute(buf, AXES, pairs(m))  13.3 us
    ppermute x3, starting transfers between devices, exchange(): rc = lax.ppermute(pc, AXES, cross)  12.9 us
    unnamed x58, local copies, waits for them, and re-layouts  7.68 us
    ppermute x3, starting transfers between devices, exchange(): r1 = lax.ppermute(p1, AXES, pairs(1))  7.54 us
    ppermute x12, waiting for transfers between devices, exchange(): lax.ppermute(buf, AXES, pairs(m))  5.44 us
    ppermute x3, waiting for transfers between devices, exchange(): r1 = lax.ppermute(p1, AXES, pairs(1))  3.44 us
  transfers between devices with their start and end apart: 24, of which 6 were waited for; matrix products, arithmetic and copies ran while one was open for 13% of the time, Pallas kernels for 15%

profile of v19, /device:TPU:5, one launch (start us, length us, event | category | flops | bytes accessed | tf_op | source)
XLA Modules:
  0.0 95.2 jit_solution(14460080371049318032)
XLA Ops:
  3.4 2.4 %collective-permute-start.1 = (bf16[128,128]{1,0:T(8,128)(2,1)S(1)}, bf16[128,128]{1,0:T(8,128)(2,1)S(1)}, u32[]{:S(2)}, u32[]{:S(2)}) collective-permute-start(bf16[128,128]{1,0:T(8,128)(2,1)S(1)} %gather_fusion), channel_id=1, source_target_pairs={{0,2},{1,3},{2,0},{3,1},{4,6},{5,7},{6,4},{7,5},{8,10},{9,11},{10,... | collective-permute-start | bytes 98312 | tf_op jit(solution)/shard_map/ppermute | solution.py:50
  5.8 1.4 %collective-permute-start = (bf16[384,128]{1,0:T(8,128)(2,1)S(1)}, bf16[384,128]{1,0:T(8,128)(2,1)S(1)}, u32[]{:S(2)}, u32[]{:S(2)}) collective-permute-start(bf16[384,128]{1,0:T(8,128)(2,1)S(1)} %get-tuple-element.79), channel_id=1, source_target_pairs={{0,1},{1,0},{2,3},{3,2},{4,5},{5,4},{6,7},{7,6},{8,9},{9,8},{10,11... | collective-permute-start | bytes 294920 | tf_op jit(solution)/shard_map/ppermute | solution.py:51
  7.1 6.6 %collective-permute-start.3 = (bf16[256,128]{1,0:T(8,128)(2,1)S(1)}, bf16[256,128]{1,0:T(8,128)(2,1)S(1)}, u32[]{:S(2)}, u32[]{:S(2)}) collective-permute-start(bf16[256,128]{1,0:T(8,128)(2,1)S(1)} %get-tuple-element.75), channel_id=1, source_target_pairs={{3,4},{7,8},{11,12},{15,16},{19,20},{23,24},{27,28},{4,3},{8,7},{1... | collective-permute-start | bytes 196616 | tf_op jit(solution)/shard_map/ppermute | solution.py:55
  13.7 1.5 %fusion.rest_6_ = bf16[128,1024]{1,0:T(8,128)(2,1)} fusion(s32[128]{0:T(128)} %param.16), kind=kLoop, calls=%fused_computation.6 | loop fusion | flops 262144 | bytes 262656 | tf_op jit(solution)/shard_map/convert_element_type | solution.py:300
  15.2 2.2 %convert_reduce_fusion = f32[8,128]{1,0:T(8,128)S(1)} fusion(bf16[8,10,128,128]{3,2,1,0:T(8,128)(2,1)} %rest_3_.5), kind=kLoop, calls=%fused_computation.2 | loop fusion | flops 2620416 | bytes 2625536 | tf_op jit(solution)/shard_map/reduce_sum | solution.py:288
  23.1 4.7 %shard_map.82.rest_3_ = f32[1024,128]{1,0:T(8,128)} custom-call(s32[1]{0:T(128)} %bitcast.z_ref, s32[80]{0:T(128)} %reshape.41.off_ref, bf16[1024,128]{1,0:T(8,128)(2,1)} %copy-done.2, bf16[384,128]{1,0:T(8,128)(2,1)} %copy-done.13, bf16[384,128]{1,0:T(8,128)(2,1)} %copy-done.14, bf16[256,128]{1,0:T(8,128)(2,1)} %copy-done.15, bf16[8,10,128,128]{3,2,1,0:T(8,128)(2,1)} %rest_3_.5), custom_call_target="tpu_custom_call" | custom-call | flops 335544320 | bytes 3670016 | tf_op jit(solution)/shard_map/pallas_call | solution.py:156
  29.9 1.5 %collective-permute-done.7.rest_1_ = bf16[16,128,128]{2,1,0:T(8,128)(2,1)S(1)} collective-permute-done((bf16[16,128,128]{2,1,0:T(8,128)(2,1)S(1)}, bf16[16,128,128]{2,1,0:T(8,128)(2,1)S(1)}, u32[]{:S(2)}, u32[]{:S(2)}) %collective-permute-start.7) | collective-permute-done | bytes 524320 | tf_op jit(solution)/shard_map/ppermute | solution.py:65
  32.3 5.2 %shard_map.83 = (bf16[1024,128]{1,0:T(8,128)(2,1)}, bf16[128,128]{1,0:T(8,128)(2,1)}, bf16[384,128]{1,0:T(8,128)(2,1)}, bf16[384,128]{1,0:T(8,128)(2,1)}, bf16[256,128]{1,0:T(8,128)(2,1)}) custom-call(s32[1]{0:T(128)} %bitcast.z_ref, s32[48]{0:T(128)} %gather_fusion.1, bf16[16,128,128]{2,1,0:T(8,128)(2,1)} %copy-done.4, bf16[16,128,128]{2,1,0:T(8,128)(2,1)} %copy-done.8, ...), custom_call_target="tpu_custom_call" | custom-call | flops 201326592 | bytes 4718592 | tf_op jit(solution)/shard_map/pallas_call | solution.py:256
  38.7 3.2 %collective-permute-start.8 = (bf16[384,128]{1,0:T(8,128)(2,1)}, bf16[384,128]{1,0:T(8,128)(2,1)S(1)}, u32[]{:S(2)}, u32[]{:S(2)}) collective-permute-start(bf16[384,128]{1,0:T(8,128)(2,1)} %get-tuple-element.58), channel_id=1, source_target_pairs={{0,1},{1,0},{2,3},{3,2},{4,5},{5,4},{6,7},{7,6},{8,9},{9,8},{10,11... | collective-permute-start | bytes 294920 | tf_op jit(solution)/shard_map/ppermute | solution.py:51
  41.9 3.3 %collective-permute-start.11 = (bf16[256,128]{1,0:T(8,128)(2,1)}, bf16[256,128]{1,0:T(8,128)(2,1)S(1)}, u32[]{:S(2)}, u32[]{:S(2)}) collective-permute-start(bf16[256,128]{1,0:T(8,128)(2,1)} %get-tuple-element.61), channel_id=1, source_target_pairs={{3,4},{7,8},{11,12},{15,16},{19,20},{23,24},{27,28},{4,3},{8,7},{1... | collective-permute-start | bytes 196616 | tf_op jit(solution)/shard_map/ppermute | solution.py:55
  45.3 1.6 %collective-permute-done.8.rest_0_ = bf16[384,128]{1,0:T(8,128)(2,1)S(1)} collective-permute-done((bf16[384,128]{1,0:T(8,128)(2,1)}, bf16[384,128]{1,0:T(8,128)(2,1)S(1)}, u32[]{:S(2)}, u32[]{:S(2)}) %collective-permute-start.8) | collective-permute-done | bytes 98336 | tf_op jit(solution)/shard_map/ppermute | solution.py:51
  49.0 1.5 %collective-permute-start.14 = (bf16[4,128,128]{2,1,0:T(8,128)(2,1)S(1)}, bf16[4,128,128]{2,1,0:T(8,128)(2,1)S(1)}, u32[]{:S(2)}, u32[]{:S(2)}) collective-permute-start(bf16[4,128,128]{2,1,0:T(8,128)(2,1)S(1)} %pad_maximum_fusion.1), channel_id=1, source_target_pairs={{0,24},{1,25},{2,26},{3,27},{4,28},{5,29},{6,30},{7,31},{8,16},{9,... | collective-permute-start | bytes 393224 | tf_op jit(solution)/shard_map/ppermute | solution.py:65
  51.1 4.7 %shard_map.84.rest_3_ = f32[1024,128]{1,0:T(8,128)} custom-call(s32[1]{0:T(128)} %bitcast.z_ref, s32[80]{0:T(128)} %reshape.41.off_ref, bf16[1024,128]{1,0:T(8,128)(2,1)} %get-tuple-element.60.cur_hbm, bf16[384,128]{1,0:T(8,128)(2,1)} %copy-done.12, bf16[384,128]{1,0:T(8,128)(2,1)} %copy-done.10, bf16[256,128]{1,0:T(8,128)(2,1)} %copy-done.17, ...), custom_call_target="tpu_custom_call" | custom-call | flops 335544320 | bytes 3670016 | tf_op jit(solution)/shard_map/pallas_call | solution.py:156
  56.6 2.3 %collective-permute-start.15 = (bf16[16,128,128]{2,1,0:T(8,128)(2,1)S(1)}, bf16[16,128,128]{2,1,0:T(8,128)(2,1)S(1)}, u32[]{:S(2)}, u32[]{:S(2)}) collective-permute-start(bf16[16,128,128]{2,1,0:T(8,128)(2,1)S(1)} %constant_dynamic-update-slice_fusion.7.rest_0_), channel_id=1, source_target_pairs={{0,4},{1,5},{2,6},{3,7},{4,0},{5,1},{6,2},{7,3},{8,12},{9,13},{10,... | collective-permute-start | bytes 1572872 | tf_op jit(solution)/shard_map/ppermute | solution.py:65
  58.9 1.5 %collective-permute-done.15.rest_1_ = bf16[16,128,128]{2,1,0:T(8,128)(2,1)S(1)} collective-permute-done((bf16[16,128,128]{2,1,0:T(8,128)(2,1)S(1)}, bf16[16,128,128]{2,1,0:T(8,128)(2,1)S(1)}, u32[]{:S(2)}, u32[]{:S(2)}) %collective-permute-start.15) | collective-permute-done | bytes 524320 | tf_op jit(solution)/shard_map/ppermute | solution.py:65
  61.3 5.3 %shard_map.85 = (bf16[1024,128]{1,0:T(8,128)(2,1)}, bf16[128,128]{1,0:T(8,128)(2,1)}, bf16[384,128]{1,0:T(8,128)(2,1)}, bf16[384,128]{1,0:T(8,128)(2,1)}, bf16[256,128]{1,0:T(8,128)(2,1)}) custom-call(s32[1]{0:T(128)} %bitcast.z_ref, s32[48]{0:T(128)} %gather_fusion.1, bf16[16,128,128]{2,1,0:T(8,128)(2,1)} %copy-done.5, bf16[16,128,128]{2,1,0:T(8,128)(2,1)} %copy-done.7, ...), custom_call_target="tpu_custom_call" | custom-call | flops 201326592 | bytes 4718592 | tf_op jit(solution)/shard_map/pallas_call | solution.py:256
  67.9 3.0 %collective-permute-start.16 = (bf16[384,128]{1,0:T(8,128)(2,1)}, bf16[384,128]{1,0:T(8,128)(2,1)S(1)}, u32[]{:S(2)}, u32[]{:S(2)}) collective-permute-start(bf16[384,128]{1,0:T(8,128)(2,1)} %get-tuple-element.67), channel_id=1, source_target_pairs={{0,1},{1,0},{2,3},{3,2},{4,5},{5,4},{6,7},{7,6},{8,9},{9,8},{10,11... | collective-permute-start | bytes 294920 | tf_op jit(solution)/shard_map/ppermute | solution.py:51
  70.9 3.0 %collective-permute-start.19 = (bf16[256,128]{1,0:T(8,128)(2,1)}, bf16[256,128]{1,0:T(8,128)(2,1)S(1)}, u32[]{:S(2)}, u32[]{:S(2)}) collective-permute-start(bf16[256,128]{1,0:T(8,128)(2,1)} %get-tuple-element.70), channel_id=1, source_target_pairs={{3,4},{7,8},{11,12},{15,16},{19,20},{23,24},{27,28},{4,3},{8,7},{1... | collective-permute-start | bytes 196616 | tf_op jit(solution)/shard_map/ppermute | solution.py:55
  73.9 1.8 %collective-permute-done.16.rest_0_ = bf16[384,128]{1,0:T(8,128)(2,1)S(1)} collective-permute-done((bf16[384,128]{1,0:T(8,128)(2,1)}, bf16[384,128]{1,0:T(8,128)(2,1)S(1)}, u32[]{:S(2)}, u32[]{:S(2)}) %collective-permute-start.16) | collective-permute-done | bytes 98336 | tf_op jit(solution)/shard_map/ppermute | solution.py:51
  77.4 1.9 %collective-permute-start.22 = (bf16[4,128,128]{2,1,0:T(8,128)(2,1)S(1)}, bf16[4,128,128]{2,1,0:T(8,128)(2,1)S(1)}, u32[]{:S(2)}, u32[]{:S(2)}) collective-permute-start(bf16[4,128,128]{2,1,0:T(8,128)(2,1)S(1)} %pad_maximum_fusion.2), channel_id=1, source_target_pairs={{0,24},{1,25},{2,26},{3,27},{4,28},{5,29},{6,30},{7,31},{8,16},{9,... | collective-permute-start | bytes 393224 | tf_op jit(solution)/shard_map/ppermute | solution.py:65
  80.0 4.7 %shard_map.86.rest_3_ = f32[1024,128]{1,0:T(8,128)} custom-call(s32[1]{0:T(128)} %bitcast.z_ref, s32[80]{0:T(128)} %reshape.41.off_ref, bf16[1024,128]{1,0:T(8,128)(2,1)} %get-tuple-element.69.cur_hbm, bf16[384,128]{1,0:T(8,128)(2,1)} %copy-done.11, bf16[384,128]{1,0:T(8,128)(2,1)} %copy-done.9, bf16[256,128]{1,0:T(8,128)(2,1)} %copy-done.16, ...), custom_call_target="tpu_custom_call" | custom-call | flops 335544320 | bytes 3670016 | tf_op jit(solution)/shard_map/pallas_call | solution.py:156
  85.5 2.4 %collective-permute-start.23 = (bf16[16,128,128]{2,1,0:T(8,128)(2,1)S(1)}, bf16[16,128,128]{2,1,0:T(8,128)(2,1)S(1)}, u32[]{:S(2)}, u32[]{:S(2)}) collective-permute-start(bf16[16,128,128]{2,1,0:T(8,128)(2,1)S(1)} %constant_dynamic-update-slice_fusion.14.rest_0_), channel_id=1, source_target_pairs={{0,4},{1,5},{2,6},{3,7},{4,0},{5,1},{6,2},{7,3},{8,12},{9,13},{10,... | collective-permute-start | bytes 1572872 | tf_op jit(solution)/shard_map/ppermute | solution.py:65
  87.9 1.5 %collective-permute-done.23.rest_1_ = bf16[16,128,128]{2,1,0:T(8,128)(2,1)S(1)} collective-permute-done((bf16[16,128,128]{2,1,0:T(8,128)(2,1)S(1)}, bf16[16,128,128]{2,1,0:T(8,128)(2,1)S(1)}, u32[]{:S(2)}, u32[]{:S(2)}) %collective-permute-start.23) | collective-permute-done | bytes 524320 | tf_op jit(solution)/shard_map/ppermute | solution.py:65
  90.2 5.0 %shard_map.87 = f32[1024,128]{1,0:T(8,128)} custom-call(s32[1]{0:T(128)} %bitcast.z_ref, s32[48]{0:T(128)} %gather_fusion.1, bf16[16,128,128]{2,1,0:T(8,128)(2,1)} %copy-done.3, bf16[16,128,128]{2,1,0:T(8,128)(2,1)} %copy-done.6, bf16[8,6,128,128]{3,2,1,0:T(8,128)(2,1)} %rest_2_.5, f32[1024,128]{1,0:T(8,128)} %shard_map.86.rest_3_, ...), custom_call_target="tpu_custom_call" | custom-call | flops 201326592 | bytes 4718592 | tf_op jit(solution)/shard_map/pallas_call | solution.py:256
  (116 shorter events, 22.7 us)
Async XLA Ops:
  3.4 16.9 %collective-permute-start.1 = (bf16[128,128]{1,0:T(8,128)(2,1)S(1)}, bf16[128,128]{1,0:T(8,128)(2,1)S(1)}, u32[]{:S(2)}, u32[]{:S(2)}) collective-permute-start(bf16[128,128]{1,0:T(8,128)(2,1)S(1)} %gather_fusion), channel_id=1, source_target_pairs={{0,2},{1,3},{2,0},{3,1},{4,6},{5,7},{6,4},{7,5},{8,10},{9,11},{10,... | collective-permute-start | bytes 98312 | tf_op jit(solution)/shard_map/ppermute | solution.py:50
  5.8 14.5 %collective-permute-start = (bf16[384,128]{1,0:T(8,128)(2,1)S(1)}, bf16[384,128]{1,0:T(8,128)(2,1)S(1)}, u32[]{:S(2)}, u32[]{:S(2)}) collective-permute-start(bf16[384,128]{1,0:T(8,128)(2,1)S(1)} %get-tuple-element.79), channel_id=1, source_target_pairs={{0,1},{1,0},{2,3},{3,2},{4,5},{5,4},{6,7},{7,6},{8,9},{9,8},{10,11... | collective-permute-start | bytes 294920 | tf_op jit(solution)/shard_map/ppermute | solution.py:51
  7.1 13.2 %collective-permute-start.2 = (bf16[384,128]{1,0:T(8,128)(2,1)S(1)}, bf16[384,128]{1,0:T(8,128)(2,1)S(1)}, u32[]{:S(2)}, u32[]{:S(2)}) collective-permute-start(bf16[384,128]{1,0:T(8,128)(2,1)S(1)} %get-tuple-element.78), channel_id=1, source_target_pairs={{0,3},{1,2},{2,1},{3,0},{4,7},{5,6},{6,5},{7,4},{8,11},{9,10},{10,... | collective-permute-start | bytes 294920 | tf_op jit(solution)/shard_map/ppermute | solution.py:49
  7.1 13.1 %collective-permute-start.3 = (bf16[256,128]{1,0:T(8,128)(2,1)S(1)}, bf16[256,128]{1,0:T(8,128)(2,1)S(1)}, u32[]{:S(2)}, u32[]{:S(2)}) collective-permute-start(bf16[256,128]{1,0:T(8,128)(2,1)S(1)} %get-tuple-element.75), channel_id=1, source_target_pairs={{3,4},{7,8},{11,12},{15,16},{19,20},{23,24},{27,28},{4,3},{8,7},{1... | collective-permute-start | bytes 196616 | tf_op jit(solution)/shard_map/ppermute | solution.py:55
  20.4 8.2 %collective-permute-start.4 = (bf16[4,128,128]{2,1,0:T(8,128)(2,1)S(1)}, bf16[4,128,128]{2,1,0:T(8,128)(2,1)S(1)}, u32[]{:S(2)}, u32[]{:S(2)}) collective-permute-start(bf16[4,128,128]{2,1,0:T(8,128)(2,1)S(1)} %pad_maximum_fusion), channel_id=1, source_target_pairs={{0,8},{1,9},{2,10},{3,11},{4,12},{5,13},{6,14},{7,15},{8,0},{9,1},... | collective-permute-start | bytes 393224 | tf_op jit(solution)/shard_map/ppermute | solution.py:65
  21.6 7.7 %collective-permute-start.5 = (bf16[4,128,128]{2,1,0:T(8,128)(2,1)S(1)}, bf16[4,128,128]{2,1,0:T(8,128)(2,1)S(1)}, u32[]{:S(2)}, u32[]{:S(2)}) collective-permute-start(bf16[4,128,128]{2,1,0:T(8,128)(2,1)S(1)} %pad_maximum_fusion), channel_id=1, source_target_pairs={{0,16},{1,17},{2,18},{3,19},{4,20},{5,21},{6,22},{7,23},{8,24},{9,... | collective-permute-start | bytes 393224 | tf_op jit(solution)/shard_map/ppermute | solution.py:65
  21.9 7.5 %collective-permute-start.6 = (bf16[4,128,128]{2,1,0:T(8,128)(2,1)S(1)}, bf16[4,128,128]{2,1,0:T(8,128)(2,1)S(1)}, u32[]{:S(2)}, u32[]{:S(2)}) collective-permute-start(bf16[4,128,128]{2,1,0:T(8,128)(2,1)S(1)} %pad_maximum_fusion), channel_id=1, source_target_pairs={{0,24},{1,25},{2,26},{3,27},{4,28},{5,29},{6,30},{7,31},{8,16},{9,... | collective-permute-start | bytes 393224 | tf_op jit(solution)/shard_map/ppermute | solution.py:65
  29.5 2.0 %collective-permute-start.7 = (bf16[16,128,128]{2,1,0:T(8,128)(2,1)S(1)}, bf16[16,128,128]{2,1,0:T(8,128)(2,1)S(1)}, u32[]{:S(2)}, u32[]{:S(2)}) collective-permute-start(bf16[16,128,128]{2,1,0:T(8,128)(2,1)S(1)} %constant_dynamic-update-slice_fusion.rest_0_), channel_id=1, source_target_pairs={{0,4},{1,5},{2,6},{3,7},{4,0},{5,1},{6,2},{7,3},{8,12},{9,13},{10,... | collective-permute-start | bytes 1572872 | tf_op jit(solution)/shard_map/ppermute | solution.py:65
  37.5 7.7 %collective-permute-start.10 = (bf16[384,128]{1,0:T(8,128)(2,1)}, bf16[384,128]{1,0:T(8,128)(2,1)S(1)}, u32[]{:S(2)}, u32[]{:S(2)}) collective-permute-start(bf16[384,128]{1,0:T(8,128)(2,1)} %get-tuple-element.59), channel_id=1, source_target_pairs={{0,3},{1,2},{2,1},{3,0},{4,7},{5,6},{6,5},{7,4},{8,11},{9,10},{10,... | collective-permute-start | bytes 294920 | tf_op jit(solution)/shard_map/ppermute | solution.py:49
  38.7 8.2 %collective-permute-start.9 = (bf16[128,128]{1,0:T(8,128)(2,1)}, bf16[128,128]{1,0:T(8,128)(2,1)S(1)}, u32[]{:S(2)}, u32[]{:S(2)}) collective-permute-start(bf16[128,128]{1,0:T(8,128)(2,1)} %get-tuple-element.57), channel_id=1, source_target_pairs={{0,2},{1,3},{2,0},{3,1},{4,6},{5,7},{6,4},{7,5},{8,10},{9,11},{10,... | collective-permute-start | bytes 98312 | tf_op jit(solution)/shard_map/ppermute | solution.py:50
  38.7 8.2 %collective-permute-start.8 = (bf16[384,128]{1,0:T(8,128)(2,1)}, bf16[384,128]{1,0:T(8,128)(2,1)S(1)}, u32[]{:S(2)}, u32[]{:S(2)}) collective-permute-start(bf16[384,128]{1,0:T(8,128)(2,1)} %get-tuple-element.58), channel_id=1, source_target_pairs={{0,1},{1,0},{2,3},{3,2},{4,5},{5,4},{6,7},{7,6},{8,9},{9,8},{10,11... | collective-permute-start | bytes 294920 | tf_op jit(solution)/shard_map/ppermute | solution.py:51
  41.9 8.5 %collective-permute-start.11 = (bf16[256,128]{1,0:T(8,128)(2,1)}, bf16[256,128]{1,0:T(8,128)(2,1)S(1)}, u32[]{:S(2)}, u32[]{:S(2)}) collective-permute-start(bf16[256,128]{1,0:T(8,128)(2,1)} %get-tuple-element.61), channel_id=1, source_target_pairs={{3,4},{7,8},{11,12},{15,16},{19,20},{23,24},{27,28},{4,3},{8,7},{1... | collective-permute-start | bytes 196616 | tf_op jit(solution)/shard_map/ppermute | solution.py:55
  47.7 8.8 %collective-permute-start.12 = (bf16[4,128,128]{2,1,0:T(8,128)(2,1)S(1)}, bf16[4,128,128]{2,1,0:T(8,128)(2,1)S(1)}, u32[]{:S(2)}, u32[]{:S(2)}) collective-permute-start(bf16[4,128,128]{2,1,0:T(8,128)(2,1)S(1)} %pad_maximum_fusion.1), channel_id=1, source_target_pairs={{0,8},{1,9},{2,10},{3,11},{4,12},{5,13},{6,14},{7,15},{8,0},{9,1},... | collective-permute-start | bytes 393224 | tf_op jit(solution)/shard_map/ppermute | solution.py:65
  48.6 7.9 %collective-permute-start.13 = (bf16[4,128,128]{2,1,0:T(8,128)(2,1)S(1)}, bf16[4,128,128]{2,1,0:T(8,128)(2,1)S(1)}, u32[]{:S(2)}, u32[]{:S(2)}) collective-permute-start(bf16[4,128,128]{2,1,0:T(8,128)(2,1)S(1)} %pad_maximum_fusion.1), channel_id=1, source_target_pairs={{0,16},{1,17},{2,18},{3,19},{4,20},{5,21},{6,22},{7,23},{8,24},{9,... | collective-permute-start | bytes 393224 | tf_op jit(solution)/shard_map/ppermute | solution.py:65
  49.0 7.6 %collective-permute-start.14 = (bf16[4,128,128]{2,1,0:T(8,128)(2,1)S(1)}, bf16[4,128,128]{2,1,0:T(8,128)(2,1)S(1)}, u32[]{:S(2)}, u32[]{:S(2)}) collective-permute-start(bf16[4,128,128]{2,1,0:T(8,128)(2,1)S(1)} %pad_maximum_fusion.1), channel_id=1, source_target_pairs={{0,24},{1,25},{2,26},{3,27},{4,28},{5,29},{6,30},{7,31},{8,16},{9,... | collective-permute-start | bytes 393224 | tf_op jit(solution)/shard_map/ppermute | solution.py:65
  56.6 3.8 %collective-permute-start.15 = (bf16[16,128,128]{2,1,0:T(8,128)(2,1)S(1)}, bf16[16,128,128]{2,1,0:T(8,128)(2,1)S(1)}, u32[]{:S(2)}, u32[]{:S(2)}) collective-permute-start(bf16[16,128,128]{2,1,0:T(8,128)(2,1)S(1)} %constant_dynamic-update-slice_fusion.7.rest_0_), channel_id=1, source_target_pairs={{0,4},{1,5},{2,6},{3,7},{4,0},{5,1},{6,2},{7,3},{8,12},{9,13},{10,... | collective-permute-start | bytes 1572872 | tf_op jit(solution)/shard_map/ppermute | solution.py:65
  66.5 7.4 %collective-permute-start.18 = (bf16[384,128]{1,0:T(8,128)(2,1)}, bf16[384,128]{1,0:T(8,128)(2,1)S(1)}, u32[]{:S(2)}, u32[]{:S(2)}) collective-permute-start(bf16[384,128]{1,0:T(8,128)(2,1)} %get-tuple-element.68), channel_id=1, source_target_pairs={{0,3},{1,2},{2,1},{3,0},{4,7},{5,6},{6,5},{7,4},{8,11},{9,10},{10,... | collective-permute-start | bytes 294920 | tf_op jit(solution)/shard_map/ppermute | solution.py:49
  67.4 8.4 %collective-permute-start.17 = (bf16[128,128]{1,0:T(8,128)(2,1)}, bf16[128,128]{1,0:T(8,128)(2,1)S(1)}, u32[]{:S(2)}, u32[]{:S(2)}) collective-permute-start(bf16[128,128]{1,0:T(8,128)(2,1)} %get-tuple-element.66), channel_id=1, source_target_pairs={{0,2},{1,3},{2,0},{3,1},{4,6},{5,7},{6,4},{7,5},{8,10},{9,11},{10,... | collective-permute-start | bytes 98312 | tf_op jit(solution)/shard_map/ppermute | solution.py:50
  67.9 7.8 %collective-permute-start.16 = (bf16[384,128]{1,0:T(8,128)(2,1)}, bf16[384,128]{1,0:T(8,128)(2,1)S(1)}, u32[]{:S(2)}, u32[]{:S(2)}) collective-permute-start(bf16[384,128]{1,0:T(8,128)(2,1)} %get-tuple-element.67), channel_id=1, source_target_pairs={{0,1},{1,0},{2,3},{3,2},{4,5},{5,4},{6,7},{7,6},{8,9},{9,8},{10,11... | collective-permute-start | bytes 294920 | tf_op jit(solution)/shard_map/ppermute | solution.py:51
  70.9 8.4 %collective-permute-start.19 = (bf16[256,128]{1,0:T(8,128)(2,1)}, bf16[256,128]{1,0:T(8,128)(2,1)S(1)}, u32[]{:S(2)}, u32[]{:S(2)}) collective-permute-start(bf16[256,128]{1,0:T(8,128)(2,1)} %get-tuple-element.70), channel_id=1, source_target_pairs={{3,4},{7,8},{11,12},{15,16},{19,20},{23,24},{27,28},{4,3},{8,7},{1... | collective-permute-start | bytes 196616 | tf_op jit(solution)/shard_map/ppermute | solution.py:55
  76.6 8.8 %collective-permute-start.20 = (bf16[4,128,128]{2,1,0:T(8,128)(2,1)S(1)}, bf16[4,128,128]{2,1,0:T(8,128)(2,1)S(1)}, u32[]{:S(2)}, u32[]{:S(2)}) collective-permute-start(bf16[4,128,128]{2,1,0:T(8,128)(2,1)S(1)} %pad_maximum_fusion.2), channel_id=1, source_target_pairs={{0,8},{1,9},{2,10},{3,11},{4,12},{5,13},{6,14},{7,15},{8,0},{9,1},... | collective-permute-start | bytes 393224 | tf_op jit(solution)/shard_map/ppermute | solution.py:65
  77.0 8.4 %collective-permute-start.21 = (bf16[4,128,128]{2,1,0:T(8,128)(2,1)S(1)}, bf16[4,128,128]{2,1,0:T(8,128)(2,1)S(1)}, u32[]{:S(2)}, u32[]{:S(2)}) collective-permute-start(bf16[4,128,128]{2,1,0:T(8,128)(2,1)S(1)} %pad_maximum_fusion.2), channel_id=1, source_target_pairs={{0,16},{1,17},{2,18},{3,19},{4,20},{5,21},{6,22},{7,23},{8,24},{9,... | collective-permute-start | bytes 393224 | tf_op jit(solution)/shard_map/ppermute | solution.py:65
  77.4 8.0 %collective-permute-start.22 = (bf16[4,128,128]{2,1,0:T(8,128)(2,1)S(1)}, bf16[4,128,128]{2,1,0:T(8,128)(2,1)S(1)}, u32[]{:S(2)}, u32[]{:S(2)}) collective-permute-start(bf16[4,128,128]{2,1,0:T(8,128)(2,1)S(1)} %pad_maximum_fusion.2), channel_id=1, source_target_pairs={{0,24},{1,25},{2,26},{3,27},{4,28},{5,29},{6,30},{7,31},{8,16},{9,... | collective-permute-start | bytes 393224 | tf_op jit(solution)/shard_map/ppermute | solution.py:65
  85.5 3.9 %collective-permute-start.23 = (bf16[16,128,128]{2,1,0:T(8,128)(2,1)S(1)}, bf16[16,128,128]{2,1,0:T(8,128)(2,1)S(1)}, u32[]{:S(2)}, u32[]{:S(2)}) collective-permute-start(bf16[16,128,128]{2,1,0:T(8,128)(2,1)S(1)} %constant_dynamic-update-slice_fusion.14.rest_0_), channel_id=1, source_target_pairs={{0,4},{1,5},{2,6},{3,7},{4,0},{5,1},{6,2},{7,3},{8,12},{9,13},{10,... | collective-permute-start | bytes 1572872 | tf_op jit(solution)/shard_map/ppermute | solution.py:65
  (20 other events, 109.2 us)

commit v20 on v19

--- a/solution.py
+++ b/solution.py
@@ -79,9 +79,9 @@
 
 def band_kernel(fast, n_own, z_ref, off_ref, cur_hbm, *rest):
     if fast:
-        r1_hbm, r3_hbm, rc_hbm, bt_hbm, out_ref, ext, bt, sem = rest
+        r1_hbm, r3_hbm, rc_hbm, bt_hbm, out_hbm, ext, bt, stage, sem = rest
     else:
-        low_hbm, high_hbm, bt_hbm, out_ref, ext, bt, sem = rest
+        low_hbm, high_hbm, bt_hbm, out_hbm, ext, bt, stage, sem = rest
     blocks, k_band, rows = bt.shape[0], bt.shape[1], bt.shape[2]
     own = cur_hbm.shape[0]
     width = (ext.shape[0] - own) // 2
@@ -131,9 +131,10 @@
     mid.wait()
     low_wait.wait()
     high_wait.wait()
+    outs = []
     for b in range(blocks):
         band_copies[b].wait()
-        acc = jnp.zeros((rows, out_ref.shape[1]), jnp.float32)
+        acc = jnp.zeros((rows, stage.shape[1]), jnp.float32)
 
         def near(k):
             n = b + BW + off_ref[b * k_band + k]
@@ -145,7 +146,12 @@
             acc = acc + jnp.dot(lhs, rhs, preferred_element_type=jnp.float32)
         if k_band % 2:
             acc = acc + jnp.dot(bt[b, k_band - 1], near(k_band - 1), preferred_element_type=jnp.float32)
-        out_ref[pl.ds(b * rows, rows), :] = acc
+        span = pl.ds(b * rows, rows)
+        stage[span, :] = acc
+        outs.append(pltpu.make_async_copy(stage.at[span], out_hbm.at[span], sem.at[3 + blocks + b]))
+        outs[-1].start()
+    for c in outs:
+        c.wait()
 
 
 def band_call(z, band_offsets, current, rim_sources, band_tiles, fast, n_own, width):
@@ -157,12 +163,13 @@
         functools.partial(band_kernel, fast, n_own),
         cost_estimate=pl.CostEstimate(flops=flops, transcendentals=0, bytes_accessed=bytes_accessed),
         in_specs=[SMEM, SMEM] + [ANY] * (1 + len(rim_sources) + 1),
-        out_specs=VMEM,
+        out_specs=ANY,
         out_shape=jax.ShapeDtypeStruct(current.shape, jnp.float32),
         scratch_shapes=[
             pltpu.VMEM((current.shape[0] + 2 * width, classes), current.dtype),
             pltpu.VMEM(band_tiles.shape, band_tiles.dtype),
-            pltpu.SemaphoreType.DMA((3 + blocks,)),
+            pltpu.VMEM(current.shape, jnp.float32),
+            pltpu.SemaphoreType.DMA((3 + 2 * blocks,)),
         ],
     )(z, band_offsets.reshape(-1), current, *rim_sources, band_tiles)
 
@@ -170,7 +177,7 @@
 def hub_kernel(n_hub, width, final, z_ref, hidx_ref, *rest):
     hub_hbm = rest[:n_hub]
     if final:
-        (ht_hbm, band_hbm, deg_ref, seeds_hbm, out_ref, hub, ht, band, seeds, sem) = rest[n_hub:]
+        (ht_hbm, band_hbm, deg_ref, seeds_hbm, out_hbm, hub, ht, band, seeds, stage, sem) = rest[n_hub:]
     else:
         (ht_hbm, band_hbm, deg_ref, seeds_hbm, pick_ref,
          cur_ref, owned_ref, p1_ref, p3_ref, pc_ref,
@@ -198,6 +205,7 @@
         for c in per_block[b]:
             c.start()
     by_row = jnp.transpose(deg_ref[...])
+    outs = []
     for c in copies:
         c.wait()
     for b in range(blocks):
@@ -215,10 +223,14 @@
         gathered = (band[span] + acc) / by_row[:, b:b + 1]
         labels = spread_weight * gathered + (1.0 - spread_weight) * seeds[span].astype(jnp.float32)
         if final:
-            out_ref[span, :] = labels
+            stage[span, :] = labels
+            outs.append(pltpu.make_async_copy(stage.at[span], out_hbm.at[span], sem.at[n_hub + 4 * blocks + b]))
+            outs[-1].start()
         else:
             cur_ref[span, :] = labels.astype(cur_ref.dtype)
     if final:
+        for c in outs:
+            c.wait()
         return
     own = cur_ref.shape[0]
     n_own = owned_ref.shape[0]
@@ -257,14 +269,15 @@
         functools.partial(hub_kernel, n_hub, width, final),
         cost_estimate=pl.CostEstimate(flops=flops, transcendentals=0, bytes_accessed=bytes_accessed),
         in_specs=[SMEM, SMEM] + [ANY] * (n_hub + 2) + [VMEM, ANY] + ([] if final else [VMEM]),
-        out_specs=[VMEM] * len(outs),
+        out_specs=[ANY] if final else [VMEM] * len(outs),
         out_shape=outs,
         scratch_shapes=[
             pltpu.VMEM((n_hub_blocks, rows, classes), bf),
             pltpu.VMEM(hub_tiles.shape, hub_tiles.dtype),
             pltpu.VMEM(seeds.shape, jnp.float32),
             pltpu.VMEM(seeds.shape, seeds.dtype),
-            pltpu.SemaphoreType.DMA((n_hub + 4 * blocks,)),
+            *([pltpu.VMEM(seeds.shape, jnp.float32)] if final else []),
+            pltpu.SemaphoreType.DMA((n_hub + 5 * blocks,)),
         ],
     )(z, hub_index, *hub_pieces, hub_tiles, band, degree, seeds, *([] if final else [pick]))
 

time: 96.5 us -> 96.5 us (level)
  transfers between devices with their start and end apart: 24 -> 24, of which waited for: 6 -> 6; matrix products, arithmetic and copies ran while one was open for 13% -> 13% of each run, Pallas kernels for 15% -> 14%
where the time goes in v20:
time: 96.5 us; the launch traced here: 95.3 us
  starting transfers between devices  37.4 us (39%)
  Pallas kernels  29.3 us (30%)
  local copies, waits for them, and re-layouts  11.1 us (12%)
  waiting for transfers between devices  8.73 us (9%)
  other arithmetic  8.19 us (8%)
    pallas_call x3, Pallas kernels, hub_call(): pl.pallas_call(functools.partial(hub_kernel, n_hub, width, final), cost_e...  15.5 us
    pallas_call x3, Pallas kernels, band_call(): pl.pallas_call(functools.partial(band_kernel, fast, n_own), cost_estimate...  13.7 us
    ppermute x12, starting transfers between devices, exchange(): lax.ppermute(buf, AXES, pairs(m))  13.3 us
    ppermute x3, starting transfers between devices, exchange(): rc = lax.ppermute(pc, AXES, cross)  13.2 us
    unnamed x58, local copies, waits for them, and re-layouts  7.68 us
    ppermute x3, starting transfers between devices, exchange(): r1 = lax.ppermute(p1, AXES, pairs(1))  7.54 us
    ppermute x12, waiting for transfers between devices, exchange(): lax.ppermute(buf, AXES, pairs(m))  5.53 us
    ppermute x3, waiting for transfers between devices, exchange(): r1 = lax.ppermute(p1, AXES, pairs(1))  3.18 us
  transfers between devices with their start and end apart: 24, of which 6 were waited for; matrix products, arithmetic and copies ran while one was open for 13% of the time, Pallas kernels for 14%

profile of v20, /device:TPU:5, one launch (start us, length us, event | category | flops | bytes accessed | tf_op | source)
XLA Modules:
  0.0 95.3 jit_solution(6700413452688146294)
XLA Ops:
  3.4 2.4 %collective-permute-start.1 = (bf16[128,128]{1,0:T(8,128)(2,1)S(1)}, bf16[128,128]{1,0:T(8,128)(2,1)S(1)}, u32[]{:S(2)}, u32[]{:S(2)}) collective-permute-start(bf16[128,128]{1,0:T(8,128)(2,1)S(1)} %gather_fusion), channel_id=1, source_target_pairs={{0,2},{1,3},{2,0},{3,1},{4,6},{5,7},{6,4},{7,5},{8,10},{9,11},{10,... | collective-permute-start | bytes 98312 | tf_op jit(solution)/shard_map/ppermute | solution.py:50
  5.8 1.4 %collective-permute-start = (bf16[384,128]{1,0:T(8,128)(2,1)S(1)}, bf16[384,128]{1,0:T(8,128)(2,1)S(1)}, u32[]{:S(2)}, u32[]{:S(2)}) collective-permute-start(bf16[384,128]{1,0:T(8,128)(2,1)S(1)} %get-tuple-element.79), channel_id=1, source_target_pairs={{0,1},{1,0},{2,3},{3,2},{4,5},{5,4},{6,7},{7,6},{8,9},{9,8},{10,11... | collective-permute-start | bytes 294920 | tf_op jit(solution)/shard_map/ppermute | solution.py:51
  7.1 6.6 %collective-permute-start.3 = (bf16[256,128]{1,0:T(8,128)(2,1)S(1)}, bf16[256,128]{1,0:T(8,128)(2,1)S(1)}, u32[]{:S(2)}, u32[]{:S(2)}) collective-permute-start(bf16[256,128]{1,0:T(8,128)(2,1)S(1)} %get-tuple-element.75), channel_id=1, source_target_pairs={{3,4},{7,8},{11,12},{15,16},{19,20},{23,24},{27,28},{4,3},{8,7},{1... | collective-permute-start | bytes 196616 | tf_op jit(solution)/shard_map/ppermute | solution.py:55
  13.7 1.5 %fusion.rest_6_ = bf16[128,1024]{1,0:T(8,128)(2,1)} fusion(s32[128]{0:T(128)} %param.16), kind=kLoop, calls=%fused_computation.6 | loop fusion | flops 262144 | bytes 262656 | tf_op jit(solution)/shard_map/convert_element_type | solution.py:313
  15.2 2.2 %convert_reduce_fusion = f32[8,128]{1,0:T(8,128)S(1)} fusion(bf16[8,10,128,128]{3,2,1,0:T(8,128)(2,1)} %rest_3_.5), kind=kLoop, calls=%fused_computation.2 | loop fusion | flops 2620416 | bytes 2625536 | tf_op jit(solution)/shard_map/reduce_sum | solution.py:301
  23.1 4.6 %shard_map.82.rest_3_ = f32[1024,128]{1,0:T(8,128)} custom-call(s32[1]{0:T(128)} %bitcast.z_ref, s32[80]{0:T(128)} %reshape.41.off_ref, bf16[1024,128]{1,0:T(8,128)(2,1)} %copy-done.2, bf16[384,128]{1,0:T(8,128)(2,1)} %copy-done.13, bf16[384,128]{1,0:T(8,128)(2,1)} %copy-done.14, bf16[256,128]{1,0:T(8,128)(2,1)} %copy-done.15, bf16[8,10,128,128]{3,2,1,0:T(8,128)(2,1)} %rest_3_.5), custom_call_target="tpu_custom_call" | custom-call | flops 335544320 | bytes 3670016 | tf_op jit(solution)/shard_map/pallas_call | solution.py:162
  29.9 1.5 %collective-permute-done.7.rest_1_ = bf16[16,128,128]{2,1,0:T(8,128)(2,1)S(1)} collective-permute-done((bf16[16,128,128]{2,1,0:T(8,128)(2,1)S(1)}, bf16[16,128,128]{2,1,0:T(8,128)(2,1)S(1)}, u32[]{:S(2)}, u32[]{:S(2)}) %collective-permute-start.7) | collective-permute-done | bytes 524320 | tf_op jit(solution)/shard_map/ppermute | solution.py:65
  32.3 5.3 %shard_map.83 = (bf16[1024,128]{1,0:T(8,128)(2,1)}, bf16[128,128]{1,0:T(8,128)(2,1)}, bf16[384,128]{1,0:T(8,128)(2,1)}, bf16[384,128]{1,0:T(8,128)(2,1)}, bf16[256,128]{1,0:T(8,128)(2,1)}) custom-call(s32[1]{0:T(128)} %bitcast.z_ref, s32[48]{0:T(128)} %gather_fusion.1, bf16[16,128,128]{2,1,0:T(8,128)(2,1)} %copy-done.4, bf16[16,128,128]{2,1,0:T(8,128)(2,1)} %copy-done.8, ...), custom_call_target="tpu_custom_call" | custom-call | flops 201326592 | bytes 4718592 | tf_op jit(solution)/shard_map/pallas_call | solution.py:268
  38.8 3.2 %collective-permute-start.8 = (bf16[384,128]{1,0:T(8,128)(2,1)}, bf16[384,128]{1,0:T(8,128)(2,1)S(1)}, u32[]{:S(2)}, u32[]{:S(2)}) collective-permute-start(bf16[384,128]{1,0:T(8,128)(2,1)} %get-tuple-element.58), channel_id=1, source_target_pairs={{0,1},{1,0},{2,3},{3,2},{4,5},{5,4},{6,7},{7,6},{8,9},{9,8},{10,11... | collective-permute-start | bytes 294920 | tf_op jit(solution)/shard_map/ppermute | solution.py:51
  42.0 3.3 %collective-permute-start.11 = (bf16[256,128]{1,0:T(8,128)(2,1)}, bf16[256,128]{1,0:T(8,128)(2,1)S(1)}, u32[]{:S(2)}, u32[]{:S(2)}) collective-permute-start(bf16[256,128]{1,0:T(8,128)(2,1)} %get-tuple-element.61), channel_id=1, source_target_pairs={{3,4},{7,8},{11,12},{15,16},{19,20},{23,24},{27,28},{4,3},{8,7},{1... | collective-permute-start | bytes 196616 | tf_op jit(solution)/shard_map/ppermute | solution.py:55
  45.4 1.6 %collective-permute-done.8.rest_0_ = bf16[384,128]{1,0:T(8,128)(2,1)S(1)} collective-permute-done((bf16[384,128]{1,0:T(8,128)(2,1)}, bf16[384,128]{1,0:T(8,128)(2,1)S(1)}, u32[]{:S(2)}, u32[]{:S(2)}) %collective-permute-start.8) | collective-permute-done | bytes 98336 | tf_op jit(solution)/shard_map/ppermute | solution.py:51
  49.0 1.4 %collective-permute-start.14 = (bf16[4,128,128]{2,1,0:T(8,128)(2,1)S(1)}, bf16[4,128,128]{2,1,0:T(8,128)(2,1)S(1)}, u32[]{:S(2)}, u32[]{:S(2)}) collective-permute-start(bf16[4,128,128]{2,1,0:T(8,128)(2,1)S(1)} %pad_maximum_fusion.1), channel_id=1, source_target_pairs={{0,24},{1,25},{2,26},{3,27},{4,28},{5,29},{6,30},{7,31},{8,16},{9,... | collective-permute-start | bytes 393224 | tf_op jit(solution)/shard_map/ppermute | solution.py:65
  51.1 4.6 %shard_map.84.rest_3_ = f32[1024,128]{1,0:T(8,128)} custom-call(s32[1]{0:T(128)} %bitcast.z_ref, s32[80]{0:T(128)} %reshape.41.off_ref, bf16[1024,128]{1,0:T(8,128)(2,1)} %get-tuple-element.60.cur_hbm, bf16[384,128]{1,0:T(8,128)(2,1)} %copy-done.12, bf16[384,128]{1,0:T(8,128)(2,1)} %copy-done.10, bf16[256,128]{1,0:T(8,128)(2,1)} %copy-done.17, ...), custom_call_target="tpu_custom_call" | custom-call | flops 335544320 | bytes 3670016 | tf_op jit(solution)/shard_map/pallas_call | solution.py:162
  56.6 2.3 %collective-permute-start.15 = (bf16[16,128,128]{2,1,0:T(8,128)(2,1)S(1)}, bf16[16,128,128]{2,1,0:T(8,128)(2,1)S(1)}, u32[]{:S(2)}, u32[]{:S(2)}) collective-permute-start(bf16[16,128,128]{2,1,0:T(8,128)(2,1)S(1)} %constant_dynamic-update-slice_fusion.7.rest_0_), channel_id=1, source_target_pairs={{0,4},{1,5},{2,6},{3,7},{4,0},{5,1},{6,2},{7,3},{8,12},{9,13},{10,... | collective-permute-start | bytes 1572872 | tf_op jit(solution)/shard_map/ppermute | solution.py:65
  58.9 1.5 %collective-permute-done.15.rest_1_ = bf16[16,128,128]{2,1,0:T(8,128)(2,1)S(1)} collective-permute-done((bf16[16,128,128]{2,1,0:T(8,128)(2,1)S(1)}, bf16[16,128,128]{2,1,0:T(8,128)(2,1)S(1)}, u32[]{:S(2)}, u32[]{:S(2)}) %collective-permute-start.15) | collective-permute-done | bytes 524320 | tf_op jit(solution)/shard_map/ppermute | solution.py:65
  61.3 5.3 %shard_map.85 = (bf16[1024,128]{1,0:T(8,128)(2,1)}, bf16[128,128]{1,0:T(8,128)(2,1)}, bf16[384,128]{1,0:T(8,128)(2,1)}, bf16[384,128]{1,0:T(8,128)(2,1)}, bf16[256,128]{1,0:T(8,128)(2,1)}) custom-call(s32[1]{0:T(128)} %bitcast.z_ref, s32[48]{0:T(128)} %gather_fusion.1, bf16[16,128,128]{2,1,0:T(8,128)(2,1)} %copy-done.5, bf16[16,128,128]{2,1,0:T(8,128)(2,1)} %copy-done.7, ...), custom_call_target="tpu_custom_call" | custom-call | flops 201326592 | bytes 4718592 | tf_op jit(solution)/shard_map/pallas_call | solution.py:268
  68.0 3.0 %collective-permute-start.16 = (bf16[384,128]{1,0:T(8,128)(2,1)}, bf16[384,128]{1,0:T(8,128)(2,1)S(1)}, u32[]{:S(2)}, u32[]{:S(2)}) collective-permute-start(bf16[384,128]{1,0:T(8,128)(2,1)} %get-tuple-element.67), channel_id=1, source_target_pairs={{0,1},{1,0},{2,3},{3,2},{4,5},{5,4},{6,7},{7,6},{8,9},{9,8},{10,11... | collective-permute-start | bytes 294920 | tf_op jit(solution)/shard_map/ppermute | solution.py:51
  71.0 3.3 %collective-permute-start.19 = (bf16[256,128]{1,0:T(8,128)(2,1)}, bf16[256,128]{1,0:T(8,128)(2,1)S(1)}, u32[]{:S(2)}, u32[]{:S(2)}) collective-permute-start(bf16[256,128]{1,0:T(8,128)(2,1)} %get-tuple-element.70), channel_id=1, source_target_pairs={{3,4},{7,8},{11,12},{15,16},{19,20},{23,24},{27,28},{4,3},{8,7},{1... | collective-permute-start | bytes 196616 | tf_op jit(solution)/shard_map/ppermute | solution.py:55
  74.3 1.6 %collective-permute-done.16.rest_0_ = bf16[384,128]{1,0:T(8,128)(2,1)S(1)} collective-permute-done((bf16[384,128]{1,0:T(8,128)(2,1)}, bf16[384,128]{1,0:T(8,128)(2,1)S(1)}, u32[]{:S(2)}, u32[]{:S(2)}) %collective-permute-start.16) | collective-permute-done | bytes 98336 | tf_op jit(solution)/shard_map/ppermute | solution.py:51
  77.4 2.0 %collective-permute-start.22 = (bf16[4,128,128]{2,1,0:T(8,128)(2,1)S(1)}, bf16[4,128,128]{2,1,0:T(8,128)(2,1)S(1)}, u32[]{:S(2)}, u32[]{:S(2)}) collective-permute-start(bf16[4,128,128]{2,1,0:T(8,128)(2,1)S(1)} %pad_maximum_fusion.2), channel_id=1, source_target_pairs={{0,24},{1,25},{2,26},{3,27},{4,28},{5,29},{6,30},{7,31},{8,16},{9,... | collective-permute-start | bytes 393224 | tf_op jit(solution)/shard_map/ppermute | solution.py:65
  80.0 4.6 %shard_map.86.rest_3_ = f32[1024,128]{1,0:T(8,128)} custom-call(s32[1]{0:T(128)} %bitcast.z_ref, s32[80]{0:T(128)} %reshape.41.off_ref, bf16[1024,128]{1,0:T(8,128)(2,1)} %get-tuple-element.69.cur_hbm, bf16[384,128]{1,0:T(8,128)(2,1)} %copy-done.11, bf16[384,128]{1,0:T(8,128)(2,1)} %copy-done.9, bf16[256,128]{1,0:T(8,128)(2,1)} %copy-done.16, ...), custom_call_target="tpu_custom_call" | custom-call | flops 335544320 | bytes 3670016 | tf_op jit(solution)/shard_map/pallas_call | solution.py:162
  85.5 2.3 %collective-permute-start.23 = (bf16[16,128,128]{2,1,0:T(8,128)(2,1)S(1)}, bf16[16,128,128]{2,1,0:T(8,128)(2,1)S(1)}, u32[]{:S(2)}, u32[]{:S(2)}) collective-permute-start(bf16[16,128,128]{2,1,0:T(8,128)(2,1)S(1)} %constant_dynamic-update-slice_fusion.14.rest_0_), channel_id=1, source_target_pairs={{0,4},{1,5},{2,6},{3,7},{4,0},{5,1},{6,2},{7,3},{8,12},{9,13},{10,... | collective-permute-start | bytes 1572872 | tf_op jit(solution)/shard_map/ppermute | solution.py:65
  87.9 1.5 %collective-permute-done.23.rest_1_ = bf16[16,128,128]{2,1,0:T(8,128)(2,1)S(1)} collective-permute-done((bf16[16,128,128]{2,1,0:T(8,128)(2,1)S(1)}, bf16[16,128,128]{2,1,0:T(8,128)(2,1)S(1)}, u32[]{:S(2)}, u32[]{:S(2)}) %collective-permute-start.23) | collective-permute-done | bytes 524320 | tf_op jit(solution)/shard_map/ppermute | solution.py:65
  90.2 4.9 %shard_map.87 = f32[1024,128]{1,0:T(8,128)} custom-call(s32[1]{0:T(128)} %bitcast.z_ref, s32[48]{0:T(128)} %gather_fusion.1, bf16[16,128,128]{2,1,0:T(8,128)(2,1)} %copy-done.3, bf16[16,128,128]{2,1,0:T(8,128)(2,1)} %copy-done.6, bf16[8,6,128,128]{3,2,1,0:T(8,128)(2,1)} %rest_2_.5, f32[1024,128]{1,0:T(8,128)} %shard_map.86.rest_3_, ...), custom_call_target="tpu_custom_call" | custom-call | flops 201326592 | bytes 4718592 | tf_op jit(solution)/shard_map/pallas_call | solution.py:268
  (116 shorter events, 22.8 us)
Async XLA Ops:
  3.4 16.9 %collective-permute-start.1 = (bf16[128,128]{1,0:T(8,128)(2,1)S(1)}, bf16[128,128]{1,0:T(8,128)(2,1)S(1)}, u32[]{:S(2)}, u32[]{:S(2)}) collective-permute-start(bf16[128,128]{1,0:T(8,128)(2,1)S(1)} %gather_fusion), channel_id=1, source_target_pairs={{0,2},{1,3},{2,0},{3,1},{4,6},{5,7},{6,4},{7,5},{8,10},{9,11},{10,... | collective-permute-start | bytes 98312 | tf_op jit(solution)/shard_map/ppermute | solution.py:50
  5.8 14.5 %collective-permute-start = (bf16[384,128]{1,0:T(8,128)(2,1)S(1)}, bf16[384,128]{1,0:T(8,128)(2,1)S(1)}, u32[]{:S(2)}, u32[]{:S(2)}) collective-permute-start(bf16[384,128]{1,0:T(8,128)(2,1)S(1)} %get-tuple-element.79), channel_id=1, source_target_pairs={{0,1},{1,0},{2,3},{3,2},{4,5},{5,4},{6,7},{7,6},{8,9},{9,8},{10,11... | collective-permute-start | bytes 294920 | tf_op jit(solution)/shard_map/ppermute | solution.py:51
  7.1 13.2 %collective-permute-start.2 = (bf16[384,128]{1,0:T(8,128)(2,1)S(1)}, bf16[384,128]{1,0:T(8,128)(2,1)S(1)}, u32[]{:S(2)}, u32[]{:S(2)}) collective-permute-start(bf16[384,128]{1,0:T(8,128)(2,1)S(1)} %get-tuple-element.78), channel_id=1, source_target_pairs={{0,3},{1,2},{2,1},{3,0},{4,7},{5,6},{6,5},{7,4},{8,11},{9,10},{10,... | collective-permute-start | bytes 294920 | tf_op jit(solution)/shard_map/ppermute | solution.py:49
  7.1 13.1 %collective-permute-start.3 = (bf16[256,128]{1,0:T(8,128)(2,1)S(1)}, bf16[256,128]{1,0:T(8,128)(2,1)S(1)}, u32[]{:S(2)}, u32[]{:S(2)}) collective-permute-start(bf16[256,128]{1,0:T(8,128)(2,1)S(1)} %get-tuple-element.75), channel_id=1, source_target_pairs={{3,4},{7,8},{11,12},{15,16},{19,20},{23,24},{27,28},{4,3},{8,7},{1... | collective-permute-start | bytes 196616 | tf_op jit(solution)/shard_map/ppermute | solution.py:55
  20.4 8.1 %collective-permute-start.4 = (bf16[4,128,128]{2,1,0:T(8,128)(2,1)S(1)}, bf16[4,128,128]{2,1,0:T(8,128)(2,1)S(1)}, u32[]{:S(2)}, u32[]{:S(2)}) collective-permute-start(bf16[4,128,128]{2,1,0:T(8,128)(2,1)S(1)} %pad_maximum_fusion), channel_id=1, source_target_pairs={{0,8},{1,9},{2,10},{3,11},{4,12},{5,13},{6,14},{7,15},{8,0},{9,1},... | collective-permute-start | bytes 393224 | tf_op jit(solution)/shard_map/ppermute | solution.py:65
  21.6 7.7 %collective-permute-start.5 = (bf16[4,128,128]{2,1,0:T(8,128)(2,1)S(1)}, bf16[4,128,128]{2,1,0:T(8,128)(2,1)S(1)}, u32[]{:S(2)}, u32[]{:S(2)}) collective-permute-start(bf16[4,128,128]{2,1,0:T(8,128)(2,1)S(1)} %pad_maximum_fusion), channel_id=1, source_target_pairs={{0,16},{1,17},{2,18},{3,19},{4,20},{5,21},{6,22},{7,23},{8,24},{9,... | collective-permute-start | bytes 393224 | tf_op jit(solution)/shard_map/ppermute | solution.py:65
  21.9 7.5 %collective-permute-start.6 = (bf16[4,128,128]{2,1,0:T(8,128)(2,1)S(1)}, bf16[4,128,128]{2,1,0:T(8,128)(2,1)S(1)}, u32[]{:S(2)}, u32[]{:S(2)}) collective-permute-start(bf16[4,128,128]{2,1,0:T(8,128)(2,1)S(1)} %pad_maximum_fusion), channel_id=1, source_target_pairs={{0,24},{1,25},{2,26},{3,27},{4,28},{5,29},{6,30},{7,31},{8,16},{9,... | collective-permute-start | bytes 393224 | tf_op jit(solution)/shard_map/ppermute | solution.py:65
  29.5 2.0 %collective-permute-start.7 = (bf16[16,128,128]{2,1,0:T(8,128)(2,1)S(1)}, bf16[16,128,128]{2,1,0:T(8,128)(2,1)S(1)}, u32[]{:S(2)}, u32[]{:S(2)}) collective-permute-start(bf16[16,128,128]{2,1,0:T(8,128)(2,1)S(1)} %constant_dynamic-update-slice_fusion.rest_0_), channel_id=1, source_target_pairs={{0,4},{1,5},{2,6},{3,7},{4,0},{5,1},{6,2},{7,3},{8,12},{9,13},{10,... | collective-permute-start | bytes 1572872 | tf_op jit(solution)/shard_map/ppermute | solution.py:65
  37.6 7.7 %collective-permute-start.10 = (bf16[384,128]{1,0:T(8,128)(2,1)}, bf16[384,128]{1,0:T(8,128)(2,1)S(1)}, u32[]{:S(2)}, u32[]{:S(2)}) collective-permute-start(bf16[384,128]{1,0:T(8,128)(2,1)} %get-tuple-element.59), channel_id=1, source_target_pairs={{0,3},{1,2},{2,1},{3,0},{4,7},{5,6},{6,5},{7,4},{8,11},{9,10},{10,... | collective-permute-start | bytes 294920 | tf_op jit(solution)/shard_map/ppermute | solution.py:49
  38.8 8.2 %collective-permute-start.9 = (bf16[128,128]{1,0:T(8,128)(2,1)}, bf16[128,128]{1,0:T(8,128)(2,1)S(1)}, u32[]{:S(2)}, u32[]{:S(2)}) collective-permute-start(bf16[128,128]{1,0:T(8,128)(2,1)} %get-tuple-element.57), channel_id=1, source_target_pairs={{0,2},{1,3},{2,0},{3,1},{4,6},{5,7},{6,4},{7,5},{8,10},{9,11},{10,... | collective-permute-start | bytes 98312 | tf_op jit(solution)/shard_map/ppermute | solution.py:50
  38.8 8.2 %collective-permute-start.8 = (bf16[384,128]{1,0:T(8,128)(2,1)}, bf16[384,128]{1,0:T(8,128)(2,1)S(1)}, u32[]{:S(2)}, u32[]{:S(2)}) collective-permute-start(bf16[384,128]{1,0:T(8,128)(2,1)} %get-tuple-element.58), channel_id=1, source_target_pairs={{0,1},{1,0},{2,3},{3,2},{4,5},{5,4},{6,7},{7,6},{8,9},{9,8},{10,11... | collective-permute-start | bytes 294920 | tf_op jit(solution)/shard_map/ppermute | solution.py:51
  42.0 8.5 %collective-permute-start.11 = (bf16[256,128]{1,0:T(8,128)(2,1)}, bf16[256,128]{1,0:T(8,128)(2,1)S(1)}, u32[]{:S(2)}, u32[]{:S(2)}) collective-permute-start(bf16[256,128]{1,0:T(8,128)(2,1)} %get-tuple-element.61), channel_id=1, source_target_pairs={{3,4},{7,8},{11,12},{15,16},{19,20},{23,24},{27,28},{4,3},{8,7},{1... | collective-permute-start | bytes 196616 | tf_op jit(solution)/shard_map/ppermute | solution.py:55
  47.8 8.7 %collective-permute-start.12 = (bf16[4,128,128]{2,1,0:T(8,128)(2,1)S(1)}, bf16[4,128,128]{2,1,0:T(8,128)(2,1)S(1)}, u32[]{:S(2)}, u32[]{:S(2)}) collective-permute-start(bf16[4,128,128]{2,1,0:T(8,128)(2,1)S(1)} %pad_maximum_fusion.1), channel_id=1, source_target_pairs={{0,8},{1,9},{2,10},{3,11},{4,12},{5,13},{6,14},{7,15},{8,0},{9,1},... | collective-permute-start | bytes 393224 | tf_op jit(solution)/shard_map/ppermute | solution.py:65
  48.7 7.8 %collective-permute-start.13 = (bf16[4,128,128]{2,1,0:T(8,128)(2,1)S(1)}, bf16[4,128,128]{2,1,0:T(8,128)(2,1)S(1)}, u32[]{:S(2)}, u32[]{:S(2)}) collective-permute-start(bf16[4,128,128]{2,1,0:T(8,128)(2,1)S(1)} %pad_maximum_fusion.1), channel_id=1, source_target_pairs={{0,16},{1,17},{2,18},{3,19},{4,20},{5,21},{6,22},{7,23},{8,24},{9,... | collective-permute-start | bytes 393224 | tf_op jit(solution)/shard_map/ppermute | solution.py:65
  49.0 7.4 %collective-permute-start.14 = (bf16[4,128,128]{2,1,0:T(8,128)(2,1)S(1)}, bf16[4,128,128]{2,1,0:T(8,128)(2,1)S(1)}, u32[]{:S(2)}, u32[]{:S(2)}) collective-permute-start(bf16[4,128,128]{2,1,0:T(8,128)(2,1)S(1)} %pad_maximum_fusion.1), channel_id=1, source_target_pairs={{0,24},{1,25},{2,26},{3,27},{4,28},{5,29},{6,30},{7,31},{8,16},{9,... | collective-permute-start | bytes 393224 | tf_op jit(solution)/shard_map/ppermute | solution.py:65
  56.6 3.8 %collective-permute-start.15 = (bf16[16,128,128]{2,1,0:T(8,128)(2,1)S(1)}, bf16[16,128,128]{2,1,0:T(8,128)(2,1)S(1)}, u32[]{:S(2)}, u32[]{:S(2)}) collective-permute-start(bf16[16,128,128]{2,1,0:T(8,128)(2,1)S(1)} %constant_dynamic-update-slice_fusion.7.rest_0_), channel_id=1, source_target_pairs={{0,4},{1,5},{2,6},{3,7},{4,0},{5,1},{6,2},{7,3},{8,12},{9,13},{10,... | collective-permute-start | bytes 1572872 | tf_op jit(solution)/shard_map/ppermute | solution.py:65
  66.6 7.7 %collective-permute-start.18 = (bf16[384,128]{1,0:T(8,128)(2,1)}, bf16[384,128]{1,0:T(8,128)(2,1)S(1)}, u32[]{:S(2)}, u32[]{:S(2)}) collective-permute-start(bf16[384,128]{1,0:T(8,128)(2,1)} %get-tuple-element.68), channel_id=1, source_target_pairs={{0,3},{1,2},{2,1},{3,0},{4,7},{5,6},{6,5},{7,4},{8,11},{9,10},{10,... | collective-permute-start | bytes 294920 | tf_op jit(solution)/shard_map/ppermute | solution.py:49
  67.5 8.4 %collective-permute-start.17 = (bf16[128,128]{1,0:T(8,128)(2,1)}, bf16[128,128]{1,0:T(8,128)(2,1)S(1)}, u32[]{:S(2)}, u32[]{:S(2)}) collective-permute-start(bf16[128,128]{1,0:T(8,128)(2,1)} %get-tuple-element.66), channel_id=1, source_target_pairs={{0,2},{1,3},{2,0},{3,1},{4,6},{5,7},{6,4},{7,5},{8,10},{9,11},{10,... | collective-permute-start | bytes 98312 | tf_op jit(solution)/shard_map/ppermute | solution.py:50
  68.0 7.9 %collective-permute-start.16 = (bf16[384,128]{1,0:T(8,128)(2,1)}, bf16[384,128]{1,0:T(8,128)(2,1)S(1)}, u32[]{:S(2)}, u32[]{:S(2)}) collective-permute-start(bf16[384,128]{1,0:T(8,128)(2,1)} %get-tuple-element.67), channel_id=1, source_target_pairs={{0,1},{1,0},{2,3},{3,2},{4,5},{5,4},{6,7},{7,6},{8,9},{9,8},{10,11... | collective-permute-start | bytes 294920 | tf_op jit(solution)/shard_map/ppermute | solution.py:51
  71.0 8.5 %collective-permute-start.19 = (bf16[256,128]{1,0:T(8,128)(2,1)}, bf16[256,128]{1,0:T(8,128)(2,1)S(1)}, u32[]{:S(2)}, u32[]{:S(2)}) collective-permute-start(bf16[256,128]{1,0:T(8,128)(2,1)} %get-tuple-element.70), channel_id=1, source_target_pairs={{3,4},{7,8},{11,12},{15,16},{19,20},{23,24},{27,28},{4,3},{8,7},{1... | collective-permute-start | bytes 196616 | tf_op jit(solution)/shard_map/ppermute | solution.py:55
  76.7 8.7 %collective-permute-start.20 = (bf16[4,128,128]{2,1,0:T(8,128)(2,1)S(1)}, bf16[4,128,128]{2,1,0:T(8,128)(2,1)S(1)}, u32[]{:S(2)}, u32[]{:S(2)}) collective-permute-start(bf16[4,128,128]{2,1,0:T(8,128)(2,1)S(1)} %pad_maximum_fusion.2), channel_id=1, source_target_pairs={{0,8},{1,9},{2,10},{3,11},{4,12},{5,13},{6,14},{7,15},{8,0},{9,1},... | collective-permute-start | bytes 393224 | tf_op jit(solution)/shard_map/ppermute | solution.py:65
  77.1 8.3 %collective-permute-start.21 = (bf16[4,128,128]{2,1,0:T(8,128)(2,1)S(1)}, bf16[4,128,128]{2,1,0:T(8,128)(2,1)S(1)}, u32[]{:S(2)}, u32[]{:S(2)}) collective-permute-start(bf16[4,128,128]{2,1,0:T(8,128)(2,1)S(1)} %pad_maximum_fusion.2), channel_id=1, source_target_pairs={{0,16},{1,17},{2,18},{3,19},{4,20},{5,21},{6,22},{7,23},{8,24},{9,... | collective-permute-start | bytes 393224 | tf_op jit(solution)/shard_map/ppermute | solution.py:65
  77.4 8.0 %collective-permute-start.22 = (bf16[4,128,128]{2,1,0:T(8,128)(2,1)S(1)}, bf16[4,128,128]{2,1,0:T(8,128)(2,1)S(1)}, u32[]{:S(2)}, u32[]{:S(2)}) collective-permute-start(bf16[4,128,128]{2,1,0:T(8,128)(2,1)S(1)} %pad_maximum_fusion.2), channel_id=1, source_target_pairs={{0,24},{1,25},{2,26},{3,27},{4,28},{5,29},{6,30},{7,31},{8,16},{9,... | collective-permute-start | bytes 393224 | tf_op jit(solution)/shard_map/ppermute | solution.py:65
  85.5 3.9 %collective-permute-start.23 = (bf16[16,128,128]{2,1,0:T(8,128)(2,1)S(1)}, bf16[16,128,128]{2,1,0:T(8,128)(2,1)S(1)}, u32[]{:S(2)}, u32[]{:S(2)}) collective-permute-start(bf16[16,128,128]{2,1,0:T(8,128)(2,1)S(1)} %constant_dynamic-update-slice_fusion.14.rest_0_), channel_id=1, source_target_pairs={{0,4},{1,5},{2,6},{3,7},{4,0},{5,1},{6,2},{7,3},{8,12},{9,13},{10,... | collective-permute-start | bytes 1572872 | tf_op jit(solution)/shard_map/ppermute | solution.py:65
  (20 other events, 108.9 us)

commit v21 on v20

--- a/solution.py
+++ b/solution.py
@@ -35,7 +35,7 @@
     return p1, p3, pc
 
 
-def exchange(current, owned, p1, p3, pc, hub_blocks, width, block_rows, middle, prep):
+def exchange(current, owned, p1, p3, pc, hub_blocks, width, block_rows, first, middle, prep):
     count = lax.axis_size(AXES)
     if not fast_path(owned, block_rows):
         forward = [(i, i + 1) for i in range(count - 1)]
@@ -43,7 +43,8 @@
         low = lax.ppermute(current[current.shape[0] - width:], AXES, forward)
         high = lax.ppermute(current[:width], AXES, backward)
         hub_all = lax.all_gather(owned, AXES, axis=0, tiled=True)
-        return middle((low, high)), [hub_all.reshape(-1, block_rows, owned.shape[1])], prep
+        done = (first(), middle((low, high)))
+        return done, [hub_all.reshape(-1, block_rows, owned.shape[1])], prep
     me = lax.axis_index(AXES)
     pairs = lambda m: [(i, i ^ m) for i in range(count)]
     r3 = lax.ppermute(p3, AXES, pairs(3))
@@ -53,8 +54,7 @@
     cross = [(4 * g + 3, 4 * g + 4) for g in range(groups - 1)]
     cross += [(4 * g + 4, 4 * g + 3) for g in range(groups - 1)]
     rc = lax.ppermute(pc, AXES, cross)
-    if prep is not None:
-        (r1, r2, r3, rc), prep = lax.optimization_barrier(((r1, r2, r3, rc), prep))
+    (r1, r2, r3, rc), (inner, prep) = lax.optimization_barrier(((r1, r2, r3, rc), (first(), prep)))
     rows = block_rows
     buf = jnp.concatenate([owned[None], r1[None, :rows], r2[None], r3[None, :rows]], 0)
     offs = [0, 1, 2, 3]
@@ -74,24 +74,33 @@
     where = np.zeros(count, np.int32)
     for p, o in enumerate(offs):
         where[o] = p
-    return done, pieces, prep
-
-
-def band_kernel(fast, n_own, z_ref, off_ref, cur_hbm, *rest):
-    if fast:
+    return (inner, done), pieces, prep
+
+
+def inner_blocks(blocks):
+    return [b for b in range(blocks) if b - BW >= 0 and b + BW < blocks]
+
+
+def band_kernel(fast, n_own, chosen, z_ref, off_ref, cur_hbm, *rest):
+    if not chosen[1]:
+        bt_hbm, out_hbm, ext, bt, stage, sem = rest
+    elif fast:
         r1_hbm, r3_hbm, rc_hbm, bt_hbm, out_hbm, ext, bt, stage, sem = rest
     else:
         low_hbm, high_hbm, bt_hbm, out_hbm, ext, bt, stage, sem = rest
+    chosen, with_rims = chosen
     blocks, k_band, rows = bt.shape[0], bt.shape[1], bt.shape[2]
     own = cur_hbm.shape[0]
     width = (ext.shape[0] - own) // 2
     low_dst = ext.at[pl.ds(0, width)]
     high_dst = ext.at[pl.ds(width + own, width)]
     mid = pltpu.make_async_copy(cur_hbm, ext.at[pl.ds(width, own)], sem.at[1])
-    band_copies = [pltpu.make_async_copy(bt_hbm.at[b], bt.at[b], sem.at[3 + b]) for b in range(blocks)]
+    band_copies = [pltpu.make_async_copy(bt_hbm.at[g], bt.at[b], sem.at[3 + b]) for b, g in enumerate(chosen)]
     band_copies[0].start()
     mid.start()
-    if fast:
+    if not with_rims:
+        low_wait = high_wait = None
+    elif fast:
         z = z_ref[0]
         low_r1 = pltpu.make_async_copy(r1_hbm.at[pl.ds(n_own, width)], low_dst, sem.at[0])
         low_r3 = pltpu.make_async_copy(r3_hbm.at[pl.ds(n_own, width)], low_dst, sem.at[0])
@@ -129,15 +138,17 @@
     for b in range(1, blocks):
         band_copies[b].start()
     mid.wait()
-    low_wait.wait()
-    high_wait.wait()
+    if with_rims:
+        low_wait.wait()
+        high_wait.wait()
     outs = []
-    for b in range(blocks):
+    for i, g in enumerate(chosen):
+        b = i
         band_copies[b].wait()
         acc = jnp.zeros((rows, stage.shape[1]), jnp.float32)
 
         def near(k):
-            n = b + BW + off_ref[b * k_band + k]
+            n = g + BW + off_ref[g * k_band + k]
             return ext[pl.ds(pl.multiple_of(n * rows, rows), rows), :]
 
         for k in range(0, k_band - 1, 2):
@@ -154,41 +165,51 @@
         c.wait()
 
 
-def band_call(z, band_offsets, current, rim_sources, band_tiles, fast, n_own, width):
-    blocks, k_band, rows, _ = band_tiles.shape
+def band_call(z, band_offsets, current, rim_sources, band_tiles, fast, n_own, width, inner):
+    all_blocks, k_band, rows, _ = band_tiles.shape
+    middle = inner_blocks(all_blocks)
+    chosen = middle if inner else [b for b in range(all_blocks) if b not in middle]
+    blocks = len(chosen)
     classes = current.shape[1]
     flops = 2 * blocks * k_band * rows * rows * classes
     bytes_accessed = band_tiles.size * 2 + current.size * 2 * 2 + current.size * 4
     return pl.pallas_call(
-        functools.partial(band_kernel, fast, n_own),
+        functools.partial(band_kernel, fast, n_own, (tuple(chosen), not inner)),
         cost_estimate=pl.CostEstimate(flops=flops, transcendentals=0, bytes_accessed=bytes_accessed),
         in_specs=[SMEM, SMEM] + [ANY] * (1 + len(rim_sources) + 1),
         out_specs=ANY,
-        out_shape=jax.ShapeDtypeStruct(current.shape, jnp.float32),
+        out_shape=jax.ShapeDtypeStruct((blocks * rows, classes), jnp.float32),
         scratch_shapes=[
             pltpu.VMEM((current.shape[0] + 2 * width, classes), current.dtype),
-            pltpu.VMEM(band_tiles.shape, band_tiles.dtype),
-            pltpu.VMEM(current.shape, jnp.float32),
+            pltpu.VMEM((blocks,) + band_tiles.shape[1:], band_tiles.dtype),
+            pltpu.VMEM((blocks * rows, classes), jnp.float32),
             pltpu.SemaphoreType.DMA((3 + 2 * blocks,)),
         ],
-    )(z, band_offsets.reshape(-1), current, *rim_sources, band_tiles)
+    )(z, band_offsets.reshape(-1), current, *(() if inner else rim_sources), band_tiles)
 
 
 def hub_kernel(n_hub, width, final, z_ref, hidx_ref, *rest):
     hub_hbm = rest[:n_hub]
     if final:
-        (ht_hbm, band_hbm, deg_ref, seeds_hbm, out_hbm, hub, ht, band, seeds, stage, sem) = rest[n_hub:]
+        (ht_hbm, band_in, band_edge, deg_ref, seeds_hbm, out_hbm, hub, ht, band, seeds, stage, sem) = rest[n_hub:]
     else:
-        (ht_hbm, band_hbm, deg_ref, seeds_hbm, pick_ref,
+        (ht_hbm, band_in, band_edge, deg_ref, seeds_hbm, pick_ref,
          cur_ref, owned_ref, p1_ref, p3_ref, pc_ref,
          hub, ht, band, seeds, sem) = rest[n_hub:]
     blocks, k_hub, rows = ht.shape[0], ht.shape[1], ht.shape[2]
+    middle = inner_blocks(blocks)
+    edge = [b for b in range(blocks) if b not in middle]
     per_block = []
     for b in range(blocks):
         span = pl.ds(b * rows, rows)
         per_block.append([
             pltpu.make_async_copy(ht_hbm.at[b], ht.at[b], sem.at[n_hub + 4 * b]),
-            pltpu.make_async_copy(band_hbm.at[span], band.at[span], sem.at[n_hub + 4 * b + 1]),
+            pltpu.make_async_copy(
+                band_in.at[pl.ds(middle.index(b) * rows, rows)] if b in middle
+                else band_edge.at[pl.ds(edge.index(b) * rows, rows)],
+                band.at[span],
+                sem.at[n_hub + 4 * b + 1],
+            ),
             pltpu.make_async_copy(seeds_hbm.at[span], seeds.at[span], sem.at[n_hub + 4 * b + 3]),
         ])
     copies = []
@@ -268,7 +289,7 @@
     return pl.pallas_call(
         functools.partial(hub_kernel, n_hub, width, final),
         cost_estimate=pl.CostEstimate(flops=flops, transcendentals=0, bytes_accessed=bytes_accessed),
-        in_specs=[SMEM, SMEM] + [ANY] * (n_hub + 2) + [VMEM, ANY] + ([] if final else [VMEM]),
+        in_specs=[SMEM, SMEM] + [ANY] * (n_hub + 3) + [VMEM, ANY] + ([] if final else [VMEM]),
         out_specs=[ANY] if final else [VMEM] * len(outs),
         out_shape=outs,
         scratch_shapes=[
@@ -279,7 +300,7 @@
             *([pltpu.VMEM(seeds.shape, jnp.float32)] if final else []),
             pltpu.SemaphoreType.DMA((n_hub + 5 * blocks,)),
         ],
-    )(z, hub_index, *hub_pieces, hub_tiles, band, degree, seeds, *([] if final else [pick]))
+    )(z, hub_index, *hub_pieces, hub_tiles, *band, degree, seeds, *([] if final else [pick]))
 
 
 def positions_of(hub_blocks, owned, block_rows):
@@ -317,7 +338,8 @@
             band_call, z, band_offsets, current, band_tiles=band_tiles, fast=fast, n_own=owned.shape[0], width=width
         )
         band, hub_pieces, prep_out = exchange(
-            current, owned, p1, p3, pc, hub_blocks, width, block_rows, lambda rims: middle(rims), prep
+            current, owned, p1, p3, pc, hub_blocks, width, block_rows,
+            lambda: middle((), inner=True), lambda rims: middle(rims, inner=False), prep,
         )
         if prep is not None:
             pick, degree, hub_index = prep_out

time: 96.5 us -> 103 us (1.067)
  the two profiles are of different devices: /device:TPU:5 before, /device:TPU:0 now
where the time goes in v21:
time: 103 us; the launch traced here: 102 us
  starting transfers between devices  39 us (38%)
  Pallas kernels  36.4 us (35%)
  local copies, waits for them, and re-layouts  9.87 us (10%)
  waiting for transfers between devices  9.77 us (9%)
  other arithmetic  6.63 us (6%)
    ppermute x12, starting transfers between devices, exchange(): lax.ppermute(buf, AXES, pairs(m))  22.2 us
    pallas_call x6, Pallas kernels, band_call(): pl.pallas_call(functools.partial(band_kernel, fast, n_own, (tuple(chosen)...  20.8 us
    pallas_call x3, Pallas kernels, hub_call(): pl.pallas_call(functools.partial(hub_kernel, n_hub, width, final), cost_e...  15.6 us
    ppermute x12, waiting for transfers between devices, exchange(): lax.ppermute(buf, AXES, pairs(m))  9.74 us
    ppermute x3, starting transfers between devices, exchange(): r2 = lax.ppermute(owned, AXES, pairs(2))  8.35 us
    unnamed x62, local copies, waits for them, and re-layouts  6.45 us
    ppermute x3, starting transfers between devices, exchange(): r3 = lax.ppermute(p3, AXES, pairs(3))  4.49 us
    reduce_sum x1, other arithmetic, body(): jnp.sum(band_tiles, axis=(1, 3), dtype=jnp.float32)  2.15 us
  transfers between devices with their start and end apart: 24, of which 7 were waited for; matrix products, arithmetic and copies ran while one was open for 10% of the time, Pallas kernels for 20%

profile of v21, /device:TPU:0, one launch (start us, length us, event | category | flops | bytes accessed | tf_op | source)
XLA Modules:
  0.0 102.5 jit_solution(194998520985555870)
XLA Ops:
  3.4 4.1 %collective-permute-start.1 = (bf16[128,128]{1,0:T(8,128)(2,1)S(1)}, bf16[128,128]{1,0:T(8,128)(2,1)S(1)}, u32[]{:S(2)}, u32[]{:S(2)}) collective-permute-start(bf16[128,128]{1,0:T(8,128)(2,1)S(1)} %gather_fusion), channel_id=1, source_target_pairs={{0,2},{1,3},{2,0},{3,1},{4,6},{5,7},{6,4},{7,5},{8,10},{9,11},{10,... | collective-permute-start | bytes 98312 | tf_op jit(solution)/shard_map/ppermute | solution.py:51
  7.5 1.6 %collective-permute-start = (bf16[384,128]{1,0:T(8,128)(2,1)S(1)}, bf16[384,128]{1,0:T(8,128)(2,1)S(1)}, u32[]{:S(2)}, u32[]{:S(2)}) collective-permute-start(bf16[384,128]{1,0:T(8,128)(2,1)S(1)} %get-tuple-element.101), channel_id=1, source_target_pairs={{0,1},{1,0},{2,3},{3,2},{4,5},{5,4},{6,7},{7,6},{8,9},{9,8},{10,11... | collective-permute-start | bytes 294920 | tf_op jit(solution)/shard_map/ppermute | solution.py:52
  9.8 1.5 %fusion.rest_7_ = bf16[128,1024]{1,0:T(8,128)(2,1)} fusion(s32[128]{0:T(128)} %param.16), kind=kLoop, calls=%fused_computation.6 | loop fusion | flops 262144 | bytes 262656 | tf_op jit(solution)/shard_map/convert_element_type | solution.py:334
  11.3 2.2 %convert_reduce_fusion = f32[8,128]{1,0:T(8,128)S(1)} fusion(bf16[8,10,128,128]{3,2,1,0:T(8,128)(2,1)} %rest_3_.5), kind=kLoop, calls=%fused_computation.2 | loop fusion | flops 2620416 | bytes 2625536 | tf_op jit(solution)/shard_map/reduce_sum | solution.py:322
  16.4 3.5 %shard_map.82.rest_3_ = f32[512,128]{1,0:T(8,128)} custom-call(s32[1]{0:T(128)} %bitcast.z_ref, s32[80]{0:T(128)} %reshape.43.off_ref, bf16[1024,128]{1,0:T(8,128)(2,1)} %copy-done.2, bf16[8,10,128,128]{3,2,1,0:T(8,128)(2,1)} %rest_3_.5), custom_call_target="tpu_custom_call" | custom-call | flops 167772160 | bytes 3670016 | tf_op jit(solution)/shard_map/pallas_call | solution.py:176
  20.0 5.2 %collective-permute-start.4 = (bf16[4,128,128]{2,1,0:T(8,128)(2,1)S(1)}, bf16[4,128,128]{2,1,0:T(8,128)(2,1)S(1)}, u32[]{:S(2)}, u32[]{:S(2)}) collective-permute-start(bf16[4,128,128]{2,1,0:T(8,128)(2,1)S(1)} %pad_maximum_fusion), channel_id=1, source_target_pairs={{0,8},{1,9},{2,10},{3,11},{4,12},{5,13},{6,14},{7,15},{8,0},{9,1},... | collective-permute-start | bytes 393224 | tf_op jit(solution)/shard_map/ppermute | solution.py:65
  25.2 1.5 %collective-permute-start.5 = (bf16[4,128,128]{2,1,0:T(8,128)(2,1)S(1)}, bf16[4,128,128]{2,1,0:T(8,128)(2,1)S(1)}, u32[]{:S(2)}, u32[]{:S(2)}) collective-permute-start(bf16[4,128,128]{2,1,0:T(8,128)(2,1)S(1)} %pad_maximum_fusion), channel_id=1, source_target_pairs={{0,16},{1,17},{2,18},{3,19},{4,20},{5,21},{6,22},{7,23},{8,24},{9,... | collective-permute-start | bytes 393224 | tf_op jit(solution)/shard_map/ppermute | solution.py:65
  27.6 3.5 %shard_map.83.rest_4_ = f32[512,128]{1,0:T(8,128)} custom-call(s32[1]{0:T(128)} %bitcast.z_ref, s32[80]{0:T(128)} %reshape.43.off_ref, bf16[1024,128]{1,0:T(8,128)(2,1)} %copy-done.2, bf16[384,128]{1,0:T(8,128)(2,1)} %copy-done.13, bf16[384,128]{1,0:T(8,128)(2,1)} %copy-done.14, bf16[256,128]{1,0:T(8,128)(2,1)} %copy-done.17, bf16[8,10,128,128]{3,2,1,0:T(8,128)(2,1)} %rest_3_.5), custom_call_target="tpu_custom_call" | custom-call | flops 167772160 | bytes 3670016 | tf_op jit(solution)/shard_map/pallas_call | solution.py:176
  34.6 1.9 %collective-permute-done.7.rest_1_ = bf16[16,128,128]{2,1,0:T(8,128)(2,1)S(1)} collective-permute-done((bf16[16,128,128]{2,1,0:T(8,128)(2,1)S(1)}, bf16[16,128,128]{2,1,0:T(8,128)(2,1)S(1)}, u32[]{:S(2)}, u32[]{:S(2)}) %collective-permute-start.7) | collective-permute-done | bytes 524320 | tf_op jit(solution)/shard_map/ppermute | solution.py:65
  37.3 5.3 %shard_map.84 = (bf16[1024,128]{1,0:T(8,128)(2,1)}, bf16[128,128]{1,0:T(8,128)(2,1)}, bf16[384,128]{1,0:T(8,128)(2,1)}, bf16[384,128]{1,0:T(8,128)(2,1)}, bf16[256,128]{1,0:T(8,128)(2,1)}) custom-call(s32[1]{0:T(128)} %bitcast.z_ref, s32[48]{0:T(128)} %gather_fusion.1, bf16[16,128,128]{2,1,0:T(8,128)(2,1)} %copy-done.4, bf16[16,128,128]{2,1,0:T(8,128)(2,1)} %copy-done.8, ...), custom_call_target="tpu_custom_call" | custom-call | flops 201326592 | bytes 4718592 | tf_op jit(solution)/shard_map/pallas_call | solution.py:289
  42.7 2.0 %collective-permute-start.9 = (bf16[128,128]{1,0:T(8,128)(2,1)}, bf16[128,128]{1,0:T(8,128)(2,1)S(1)}, u32[]{:S(2)}, u32[]{:S(2)}) collective-permute-start(bf16[128,128]{1,0:T(8,128)(2,1)} %get-tuple-element.69), channel_id=1, source_target_pairs={{0,2},{1,3},{2,0},{3,1},{4,6},{5,7},{6,4},{7,5},{8,10},{9,11},{10,... | collective-permute-start | bytes 98312 | tf_op jit(solution)/shard_map/ppermute | solution.py:51
  44.7 2.4 %collective-permute-start.10 = (bf16[384,128]{1,0:T(8,128)(2,1)}, bf16[384,128]{1,0:T(8,128)(2,1)S(1)}, u32[]{:S(2)}, u32[]{:S(2)}) collective-permute-start(bf16[384,128]{1,0:T(8,128)(2,1)} %get-tuple-element.71), channel_id=1, source_target_pairs={{0,3},{1,2},{2,1},{3,0},{4,7},{5,6},{6,5},{7,4},{8,11},{9,10},{10,... | collective-permute-start | bytes 294920 | tf_op jit(solution)/shard_map/ppermute | solution.py:50
  48.5 3.5 %shard_map.85.rest_3_ = f32[512,128]{1,0:T(8,128)} custom-call(s32[1]{0:T(128)} %bitcast.z_ref, s32[80]{0:T(128)} %reshape.43.off_ref, bf16[1024,128]{1,0:T(8,128)(2,1)} %get-tuple-element.73.cur_hbm, bf16[8,10,128,128]{3,2,1,0:T(8,128)(2,1)} %rest_3_.5), custom_call_target="tpu_custom_call" | custom-call | flops 167772160 | bytes 3670016 | tf_op jit(solution)/shard_map/pallas_call | solution.py:176
  52.1 4.5 %collective-permute-start.12 = (bf16[4,128,128]{2,1,0:T(8,128)(2,1)S(1)}, bf16[4,128,128]{2,1,0:T(8,128)(2,1)S(1)}, u32[]{:S(2)}, u32[]{:S(2)}) collective-permute-start(bf16[4,128,128]{2,1,0:T(8,128)(2,1)S(1)} %pad_maximum_fusion.1), channel_id=1, source_target_pairs={{0,8},{1,9},{2,10},{3,11},{4,12},{5,13},{6,14},{7,15},{8,0},{9,1},... | collective-permute-start | bytes 393224 | tf_op jit(solution)/shard_map/ppermute | solution.py:65
  59.3 3.5 %shard_map.86.rest_4_ = f32[512,128]{1,0:T(8,128)} custom-call(s32[1]{0:T(128)} %bitcast.z_ref, s32[80]{0:T(128)} %reshape.43.off_ref, bf16[1024,128]{1,0:T(8,128)(2,1)} %get-tuple-element.73.cur_hbm, bf16[384,128]{1,0:T(8,128)(2,1)} %copy-done.10, bf16[384,128]{1,0:T(8,128)(2,1)} %copy-done.12, bf16[256,128]{1,0:T(8,128)(2,1)} %copy-done.19, ...), custom_call_target="tpu_custom_call" | custom-call | flops 167772160 | bytes 3670016 | tf_op jit(solution)/shard_map/pallas_call | solution.py:176
  64.3 1.9 %collective-permute-done.15.rest_1_ = bf16[16,128,128]{2,1,0:T(8,128)(2,1)S(1)} collective-permute-done((bf16[16,128,128]{2,1,0:T(8,128)(2,1)S(1)}, bf16[16,128,128]{2,1,0:T(8,128)(2,1)S(1)}, u32[]{:S(2)}, u32[]{:S(2)}) %collective-permute-start.15) | collective-permute-done | bytes 524320 | tf_op jit(solution)/shard_map/ppermute | solution.py:65
  67.0 5.3 %shard_map.87 = (bf16[1024,128]{1,0:T(8,128)(2,1)}, bf16[128,128]{1,0:T(8,128)(2,1)}, bf16[384,128]{1,0:T(8,128)(2,1)}, bf16[384,128]{1,0:T(8,128)(2,1)}, bf16[256,128]{1,0:T(8,128)(2,1)}) custom-call(s32[1]{0:T(128)} %bitcast.z_ref, s32[48]{0:T(128)} %gather_fusion.1, bf16[16,128,128]{2,1,0:T(8,128)(2,1)} %copy-done.5, bf16[16,128,128]{2,1,0:T(8,128)(2,1)} %copy-done.7, ...), custom_call_target="tpu_custom_call" | custom-call | flops 201326592 | bytes 4718592 | tf_op jit(solution)/shard_map/pallas_call | solution.py:289
  72.4 2.3 %collective-permute-start.17 = (bf16[128,128]{1,0:T(8,128)(2,1)}, bf16[128,128]{1,0:T(8,128)(2,1)S(1)}, u32[]{:S(2)}, u32[]{:S(2)}) collective-permute-start(bf16[128,128]{1,0:T(8,128)(2,1)} %get-tuple-element.83), channel_id=1, source_target_pairs={{0,2},{1,3},{2,0},{3,1},{4,6},{5,7},{6,4},{7,5},{8,10},{9,11},{10,... | collective-permute-start | bytes 98312 | tf_op jit(solution)/shard_map/ppermute | solution.py:51
  74.7 2.1 %collective-permute-start.18 = (bf16[384,128]{1,0:T(8,128)(2,1)}, bf16[384,128]{1,0:T(8,128)(2,1)S(1)}, u32[]{:S(2)}, u32[]{:S(2)}) collective-permute-start(bf16[384,128]{1,0:T(8,128)(2,1)} %get-tuple-element.85), channel_id=1, source_target_pairs={{0,3},{1,2},{2,1},{3,0},{4,7},{5,6},{6,5},{7,4},{8,11},{9,10},{10,... | collective-permute-start | bytes 294920 | tf_op jit(solution)/shard_map/ppermute | solution.py:50
  78.4 3.5 %shard_map.88.rest_3_ = f32[512,128]{1,0:T(8,128)} custom-call(s32[1]{0:T(128)} %bitcast.z_ref, s32[80]{0:T(128)} %reshape.43.off_ref, bf16[1024,128]{1,0:T(8,128)(2,1)} %get-tuple-element.87.cur_hbm, bf16[8,10,128,128]{3,2,1,0:T(8,128)(2,1)} %rest_3_.5), custom_call_target="tpu_custom_call" | custom-call | flops 167772160 | bytes 3670016 | tf_op jit(solution)/shard_map/pallas_call | solution.py:176
  82.0 5.0 %collective-permute-start.20 = (bf16[4,128,128]{2,1,0:T(8,128)(2,1)S(1)}, bf16[4,128,128]{2,1,0:T(8,128)(2,1)S(1)}, u32[]{:S(2)}, u32[]{:S(2)}) collective-permute-start(bf16[4,128,128]{2,1,0:T(8,128)(2,1)S(1)} %pad_maximum_fusion.2), channel_id=1, source_target_pairs={{0,8},{1,9},{2,10},{3,11},{4,12},{5,13},{6,14},{7,15},{8,0},{9,1},... | collective-permute-start | bytes 393224 | tf_op jit(solution)/shard_map/ppermute | solution.py:65
  89.3 3.5 %shard_map.89.rest_4_ = f32[512,128]{1,0:T(8,128)} custom-call(s32[1]{0:T(128)} %bitcast.z_ref, s32[80]{0:T(128)} %reshape.43.off_ref, bf16[1024,128]{1,0:T(8,128)(2,1)} %get-tuple-element.87.cur_hbm, bf16[384,128]{1,0:T(8,128)(2,1)} %copy-done.9, bf16[384,128]{1,0:T(8,128)(2,1)} %copy-done.11, bf16[256,128]{1,0:T(8,128)(2,1)} %copy-done.18, ...), custom_call_target="tpu_custom_call" | custom-call | flops 167772160 | bytes 3670016 | tf_op jit(solution)/shard_map/pallas_call | solution.py:176
  94.7 1.9 %collective-permute-done.23.rest_1_ = bf16[16,128,128]{2,1,0:T(8,128)(2,1)S(1)} collective-permute-done((bf16[16,128,128]{2,1,0:T(8,128)(2,1)S(1)}, bf16[16,128,128]{2,1,0:T(8,128)(2,1)S(1)}, u32[]{:S(2)}, u32[]{:S(2)}) %collective-permute-start.23) | collective-permute-done | bytes 524320 | tf_op jit(solution)/shard_map/ppermute | solution.py:65
  97.4 4.9 %shard_map.90 = f32[1024,128]{1,0:T(8,128)} custom-call(s32[1]{0:T(128)} %bitcast.z_ref, s32[48]{0:T(128)} %gather_fusion.1, bf16[16,128,128]{2,1,0:T(8,128)(2,1)} %copy-done.3, bf16[16,128,128]{2,1,0:T(8,128)(2,1)} %copy-done.6, bf16[8,6,128,128]{3,2,1,0:T(8,128)(2,1)} %rest_2_.5, f32[512,128]{1,0:T(8,128)} %shard_map.88.rest_3_, ...), custom_call_target="tpu_custom_call" | custom-call | flops 201326592 | bytes 4718592 | tf_op jit(solution)/shard_map/pallas_call | solution.py:289
  (123 shorter events, 25.3 us)
Async XLA Ops:
  3.4 16.5 %collective-permute-start.1 = (bf16[128,128]{1,0:T(8,128)(2,1)S(1)}, bf16[128,128]{1,0:T(8,128)(2,1)S(1)}, u32[]{:S(2)}, u32[]{:S(2)}) collective-permute-start(bf16[128,128]{1,0:T(8,128)(2,1)S(1)} %gather_fusion), channel_id=1, source_target_pairs={{0,2},{1,3},{2,0},{3,1},{4,6},{5,7},{6,4},{7,5},{8,10},{9,11},{10,... | collective-permute-start | bytes 98312 | tf_op jit(solution)/shard_map/ppermute | solution.py:51
  7.5 12.4 %collective-permute-start = (bf16[384,128]{1,0:T(8,128)(2,1)S(1)}, bf16[384,128]{1,0:T(8,128)(2,1)S(1)}, u32[]{:S(2)}, u32[]{:S(2)}) collective-permute-start(bf16[384,128]{1,0:T(8,128)(2,1)S(1)} %get-tuple-element.101), channel_id=1, source_target_pairs={{0,1},{1,0},{2,3},{3,2},{4,5},{5,4},{6,7},{7,6},{8,9},{9,8},{10,11... | collective-permute-start | bytes 294920 | tf_op jit(solution)/shard_map/ppermute | solution.py:52
  9.1 10.8 %collective-permute-start.2 = (bf16[384,128]{1,0:T(8,128)(2,1)S(1)}, bf16[384,128]{1,0:T(8,128)(2,1)S(1)}, u32[]{:S(2)}, u32[]{:S(2)}) collective-permute-start(bf16[384,128]{1,0:T(8,128)(2,1)S(1)} %get-tuple-element.100), channel_id=1, source_target_pairs={{0,3},{1,2},{2,1},{3,0},{4,7},{5,6},{6,5},{7,4},{8,11},{9,10},{10,... | collective-permute-start | bytes 294920 | tf_op jit(solution)/shard_map/ppermute | solution.py:50
  9.1 10.8 %collective-permute-start.3 = (bf16[256,128]{1,0:T(8,128)(2,1)S(1)}, bf16[256,128]{1,0:T(8,128)(2,1)S(1)}, u32[]{:S(2)}, u32[]{:S(2)}) collective-permute-start(bf16[256,128]{1,0:T(8,128)(2,1)S(1)} %get-tuple-element.97), channel_id=1, source_target_pairs={{3,4},{7,8},{11,12},{15,16},{19,20},{23,24},{27,28},{4,3},{8,7},{1... | collective-permute-start | bytes 196616 | tf_op jit(solution)/shard_map/ppermute | solution.py:56
  20.0 11.9 %collective-permute-start.4 = (bf16[4,128,128]{2,1,0:T(8,128)(2,1)S(1)}, bf16[4,128,128]{2,1,0:T(8,128)(2,1)S(1)}, u32[]{:S(2)}, u32[]{:S(2)}) collective-permute-start(bf16[4,128,128]{2,1,0:T(8,128)(2,1)S(1)} %pad_maximum_fusion), channel_id=1, source_target_pairs={{0,8},{1,9},{2,10},{3,11},{4,12},{5,13},{6,14},{7,15},{8,0},{9,1},... | collective-permute-start | bytes 393224 | tf_op jit(solution)/shard_map/ppermute | solution.py:65
  25.2 7.9 %collective-permute-start.5 = (bf16[4,128,128]{2,1,0:T(8,128)(2,1)S(1)}, bf16[4,128,128]{2,1,0:T(8,128)(2,1)S(1)}, u32[]{:S(2)}, u32[]{:S(2)}) collective-permute-start(bf16[4,128,128]{2,1,0:T(8,128)(2,1)S(1)} %pad_maximum_fusion), channel_id=1, source_target_pairs={{0,16},{1,17},{2,18},{3,19},{4,20},{5,21},{6,22},{7,23},{8,24},{9,... | collective-permute-start | bytes 393224 | tf_op jit(solution)/shard_map/ppermute | solution.py:65
  26.7 7.7 %collective-permute-start.6 = (bf16[4,128,128]{2,1,0:T(8,128)(2,1)S(1)}, bf16[4,128,128]{2,1,0:T(8,128)(2,1)S(1)}, u32[]{:S(2)}, u32[]{:S(2)}) collective-permute-start(bf16[4,128,128]{2,1,0:T(8,128)(2,1)S(1)} %pad_maximum_fusion), channel_id=1, source_target_pairs={{0,24},{1,25},{2,26},{3,27},{4,28},{5,29},{6,30},{7,31},{8,16},{9,... | collective-permute-start | bytes 393224 | tf_op jit(solution)/shard_map/ppermute | solution.py:65
  34.5 2.0 %collective-permute-start.7 = (bf16[16,128,128]{2,1,0:T(8,128)(2,1)S(1)}, bf16[16,128,128]{2,1,0:T(8,128)(2,1)S(1)}, u32[]{:S(2)}, u32[]{:S(2)}) collective-permute-start(bf16[16,128,128]{2,1,0:T(8,128)(2,1)S(1)} %constant_dynamic-update-slice_fusion.rest_0_), channel_id=1, source_target_pairs={{0,4},{1,5},{2,6},{3,7},{4,0},{5,1},{6,2},{7,3},{8,12},{9,13},{10,... | collective-permute-start | bytes 1572872 | tf_op jit(solution)/shard_map/ppermute | solution.py:65
  42.6 9.4 %collective-permute-start.8 = (bf16[384,128]{1,0:T(8,128)(2,1)}, bf16[384,128]{1,0:T(8,128)(2,1)S(1)}, u32[]{:S(2)}, u32[]{:S(2)}) collective-permute-start(bf16[384,128]{1,0:T(8,128)(2,1)} %get-tuple-element.70), channel_id=1, source_target_pairs={{0,1},{1,0},{2,3},{3,2},{4,5},{5,4},{6,7},{7,6},{8,9},{9,8},{10,11... | collective-permute-start | bytes 294920 | tf_op jit(solution)/shard_map/ppermute | solution.py:52
  42.7 9.3 %collective-permute-start.9 = (bf16[128,128]{1,0:T(8,128)(2,1)}, bf16[128,128]{1,0:T(8,128)(2,1)S(1)}, u32[]{:S(2)}, u32[]{:S(2)}) collective-permute-start(bf16[128,128]{1,0:T(8,128)(2,1)} %get-tuple-element.69), channel_id=1, source_target_pairs={{0,2},{1,3},{2,0},{3,1},{4,6},{5,7},{6,4},{7,5},{8,10},{9,11},{10,... | collective-permute-start | bytes 98312 | tf_op jit(solution)/shard_map/ppermute | solution.py:51
  44.7 7.4 %collective-permute-start.10 = (bf16[384,128]{1,0:T(8,128)(2,1)}, bf16[384,128]{1,0:T(8,128)(2,1)S(1)}, u32[]{:S(2)}, u32[]{:S(2)}) collective-permute-start(bf16[384,128]{1,0:T(8,128)(2,1)} %get-tuple-element.71), channel_id=1, source_target_pairs={{0,3},{1,2},{2,1},{3,0},{4,7},{5,6},{6,5},{7,4},{8,11},{9,10},{10,... | collective-permute-start | bytes 294920 | tf_op jit(solution)/shard_map/ppermute | solution.py:50
  47.1 4.9 %collective-permute-start.11 = (bf16[256,128]{1,0:T(8,128)(2,1)}, bf16[256,128]{1,0:T(8,128)(2,1)S(1)}, u32[]{:S(2)}, u32[]{:S(2)}) collective-permute-start(bf16[256,128]{1,0:T(8,128)(2,1)} %get-tuple-element.72), channel_id=1, source_target_pairs={{3,4},{7,8},{11,12},{15,16},{19,20},{23,24},{27,28},{4,3},{8,7},{1... | collective-permute-start | bytes 196616 | tf_op jit(solution)/shard_map/ppermute | solution.py:56
  52.1 11.5 %collective-permute-start.12 = (bf16[4,128,128]{2,1,0:T(8,128)(2,1)S(1)}, bf16[4,128,128]{2,1,0:T(8,128)(2,1)S(1)}, u32[]{:S(2)}, u32[]{:S(2)}) collective-permute-start(bf16[4,128,128]{2,1,0:T(8,128)(2,1)S(1)} %pad_maximum_fusion.1), channel_id=1, source_target_pairs={{0,8},{1,9},{2,10},{3,11},{4,12},{5,13},{6,14},{7,15},{8,0},{9,1},... | collective-permute-start | bytes 393224 | tf_op jit(solution)/shard_map/ppermute | solution.py:65
  56.6 7.0 %collective-permute-start.13 = (bf16[4,128,128]{2,1,0:T(8,128)(2,1)S(1)}, bf16[4,128,128]{2,1,0:T(8,128)(2,1)S(1)}, u32[]{:S(2)}, u32[]{:S(2)}) collective-permute-start(bf16[4,128,128]{2,1,0:T(8,128)(2,1)S(1)} %pad_maximum_fusion.1), channel_id=1, source_target_pairs={{0,16},{1,17},{2,18},{3,19},{4,20},{5,21},{6,22},{7,23},{8,24},{9,... | collective-permute-start | bytes 393224 | tf_op jit(solution)/shard_map/ppermute | solution.py:65
  58.0 6.1 %collective-permute-start.14 = (bf16[4,128,128]{2,1,0:T(8,128)(2,1)S(1)}, bf16[4,128,128]{2,1,0:T(8,128)(2,1)S(1)}, u32[]{:S(2)}, u32[]{:S(2)}) collective-permute-start(bf16[4,128,128]{2,1,0:T(8,128)(2,1)S(1)} %pad_maximum_fusion.1), channel_id=1, source_target_pairs={{0,24},{1,25},{2,26},{3,27},{4,28},{5,29},{6,30},{7,31},{8,16},{9,... | collective-permute-start | bytes 393224 | tf_op jit(solution)/shard_map/ppermute | solution.py:65
  64.2 2.0 %collective-permute-start.15 = (bf16[16,128,128]{2,1,0:T(8,128)(2,1)S(1)}, bf16[16,128,128]{2,1,0:T(8,128)(2,1)S(1)}, u32[]{:S(2)}, u32[]{:S(2)}) collective-permute-start(bf16[16,128,128]{2,1,0:T(8,128)(2,1)S(1)} %constant_dynamic-update-slice_fusion.7.rest_0_), channel_id=1, source_target_pairs={{0,4},{1,5},{2,6},{3,7},{4,0},{5,1},{6,2},{7,3},{8,12},{9,13},{10,... | collective-permute-start | bytes 1572872 | tf_op jit(solution)/shard_map/ppermute | solution.py:65
  72.3 9.6 %collective-permute-start.16 = (bf16[384,128]{1,0:T(8,128)(2,1)}, bf16[384,128]{1,0:T(8,128)(2,1)S(1)}, u32[]{:S(2)}, u32[]{:S(2)}) collective-permute-start(bf16[384,128]{1,0:T(8,128)(2,1)} %get-tuple-element.84), channel_id=1, source_target_pairs={{0,1},{1,0},{2,3},{3,2},{4,5},{5,4},{6,7},{7,6},{8,9},{9,8},{10,11... | collective-permute-start | bytes 294920 | tf_op jit(solution)/shard_map/ppermute | solution.py:52
  72.4 9.5 %collective-permute-start.17 = (bf16[128,128]{1,0:T(8,128)(2,1)}, bf16[128,128]{1,0:T(8,128)(2,1)S(1)}, u32[]{:S(2)}, u32[]{:S(2)}) collective-permute-start(bf16[128,128]{1,0:T(8,128)(2,1)} %get-tuple-element.83), channel_id=1, source_target_pairs={{0,2},{1,3},{2,0},{3,1},{4,6},{5,7},{6,4},{7,5},{8,10},{9,11},{10,... | collective-permute-start | bytes 98312 | tf_op jit(solution)/shard_map/ppermute | solution.py:51
  74.7 7.2 %collective-permute-start.18 = (bf16[384,128]{1,0:T(8,128)(2,1)}, bf16[384,128]{1,0:T(8,128)(2,1)S(1)}, u32[]{:S(2)}, u32[]{:S(2)}) collective-permute-start(bf16[384,128]{1,0:T(8,128)(2,1)} %get-tuple-element.85), channel_id=1, source_target_pairs={{0,3},{1,2},{2,1},{3,0},{4,7},{5,6},{6,5},{7,4},{8,11},{9,10},{10,... | collective-permute-start | bytes 294920 | tf_op jit(solution)/shard_map/ppermute | solution.py:50
  76.8 5.1 %collective-permute-start.19 = (bf16[256,128]{1,0:T(8,128)(2,1)}, bf16[256,128]{1,0:T(8,128)(2,1)S(1)}, u32[]{:S(2)}, u32[]{:S(2)}) collective-permute-start(bf16[256,128]{1,0:T(8,128)(2,1)} %get-tuple-element.86), channel_id=1, source_target_pairs={{3,4},{7,8},{11,12},{15,16},{19,20},{23,24},{27,28},{4,3},{8,7},{1... | collective-permute-start | bytes 196616 | tf_op jit(solution)/shard_map/ppermute | solution.py:56
  82.0 11.6 %collective-permute-start.20 = (bf16[4,128,128]{2,1,0:T(8,128)(2,1)S(1)}, bf16[4,128,128]{2,1,0:T(8,128)(2,1)S(1)}, u32[]{:S(2)}, u32[]{:S(2)}) collective-permute-start(bf16[4,128,128]{2,1,0:T(8,128)(2,1)S(1)} %pad_maximum_fusion.2), channel_id=1, source_target_pairs={{0,8},{1,9},{2,10},{3,11},{4,12},{5,13},{6,14},{7,15},{8,0},{9,1},... | collective-permute-start | bytes 393224 | tf_op jit(solution)/shard_map/ppermute | solution.py:65
  87.0 6.6 %collective-permute-start.21 = (bf16[4,128,128]{2,1,0:T(8,128)(2,1)S(1)}, bf16[4,128,128]{2,1,0:T(8,128)(2,1)S(1)}, u32[]{:S(2)}, u32[]{:S(2)}) collective-permute-start(bf16[4,128,128]{2,1,0:T(8,128)(2,1)S(1)} %pad_maximum_fusion.2), channel_id=1, source_target_pairs={{0,16},{1,17},{2,18},{3,19},{4,20},{5,21},{6,22},{7,23},{8,24},{9,... | collective-permute-start | bytes 393224 | tf_op jit(solution)/shard_map/ppermute | solution.py:65
  88.2 6.4 %collective-permute-start.22 = (bf16[4,128,128]{2,1,0:T(8,128)(2,1)S(1)}, bf16[4,128,128]{2,1,0:T(8,128)(2,1)S(1)}, u32[]{:S(2)}, u32[]{:S(2)}) collective-permute-start(bf16[4,128,128]{2,1,0:T(8,128)(2,1)S(1)} %pad_maximum_fusion.2), channel_id=1, source_target_pairs={{0,24},{1,25},{2,26},{3,27},{4,28},{5,29},{6,30},{7,31},{8,16},{9,... | collective-permute-start | bytes 393224 | tf_op jit(solution)/shard_map/ppermute | solution.py:65
  94.6 2.0 %collective-permute-start.23 = (bf16[16,128,128]{2,1,0:T(8,128)(2,1)S(1)}, bf16[16,128,128]{2,1,0:T(8,128)(2,1)S(1)}, u32[]{:S(2)}, u32[]{:S(2)}) collective-permute-start(bf16[16,128,128]{2,1,0:T(8,128)(2,1)S(1)} %constant_dynamic-update-slice_fusion.14.rest_0_), channel_id=1, source_target_pairs={{0,4},{1,5},{2,6},{3,7},{4,0},{5,1},{6,2},{7,3},{8,12},{9,13},{10,... | collective-permute-start | bytes 1572872 | tf_op jit(solution)/shard_map/ppermute | solution.py:65
  (22 other events, 139.4 us)

commit v22 on v19

--- a/solution.py
+++ b/solution.py
@@ -31,7 +31,7 @@
     bottom = current[:width]
     p1 = jnp.concatenate([owned, jnp.where(z % 2 == 0, top, bottom)], 0)
     p3 = jnp.concatenate([owned, jnp.where(z == 1, top, bottom)], 0)
-    pc = jnp.where(z == 3, top, bottom)
+    pc = jnp.where((z == 3) | (z == 1), top, bottom)
     return p1, p3, pc
 
 
@@ -46,17 +46,18 @@
         return middle((low, high)), [hub_all.reshape(-1, block_rows, owned.shape[1])], prep
     me = lax.axis_index(AXES)
     pairs = lambda m: [(i, i ^ m) for i in range(count)]
-    r3 = lax.ppermute(p3, AXES, pairs(3))
+    r3 = lax.ppermute(owned, AXES, pairs(3))
     r2 = lax.ppermute(owned, AXES, pairs(2))
     r1 = lax.ppermute(p1, AXES, pairs(1))
     groups = count // 4
     cross = [(4 * g + 3, 4 * g + 4) for g in range(groups - 1)]
     cross += [(4 * g + 4, 4 * g + 3) for g in range(groups - 1)]
+    cross += [(4 * g + 1, 4 * g + 2) for g in range(groups)] + [(4 * g + 2, 4 * g + 1) for g in range(groups)]
     rc = lax.ppermute(pc, AXES, cross)
     if prep is not None:
         (r1, r2, r3, rc), prep = lax.optimization_barrier(((r1, r2, r3, rc), prep))
     rows = block_rows
-    buf = jnp.concatenate([owned[None], r1[None, :rows], r2[None], r3[None, :rows]], 0)
+    buf = jnp.concatenate([owned[None], r1[None, :rows], r2[None], r3[None]], 0)
     offs = [0, 1, 2, 3]
     rounds = ROUNDS_32
     pieces = [buf]
@@ -94,10 +95,8 @@
     if fast:
         z = z_ref[0]
         low_r1 = pltpu.make_async_copy(r1_hbm.at[pl.ds(n_own, width)], low_dst, sem.at[0])
-        low_r3 = pltpu.make_async_copy(r3_hbm.at[pl.ds(n_own, width)], low_dst, sem.at[0])
         low_rc = pltpu.make_async_copy(rc_hbm, low_dst, sem.at[0])
         high_r1 = pltpu.make_async_copy(r1_hbm.at[pl.ds(n_own, width)], high_dst, sem.at[2])
-        high_r3 = pltpu.make_async_copy(r3_hbm.at[pl.ds(n_own, width)], high_dst, sem.at[2])
         high_rc = pltpu.make_async_copy(rc_hbm, high_dst, sem.at[2])
 
         @pl.when(z == 0)
@@ -108,11 +107,11 @@
         @pl.when(z == 1)
         def _():
             low_r1.start()
-            high_r3.start()
+            high_rc.start()
 
         @pl.when(z == 2)
         def _():
-            low_r3.start()
+            low_rc.start()
             high_r1.start()
 
         @pl.when(z == 3)
@@ -231,7 +230,7 @@
     bottom = cur_ref[pl.ds(0, width), :]
     p1_ref[pl.ds(n_own, width), :] = jnp.where(z % 2 == 0, top, bottom)
     p3_ref[pl.ds(n_own, width), :] = jnp.where(z == 1, top, bottom)
-    pc_ref[...] = jnp.where(z == 3, top, bottom)
+    pc_ref[...] = jnp.where((z == 3) | (z == 1), top, bottom)
 
 
 def hub_call(z, hub_index, pick, hub_pieces, hub_tiles, band, degree, seeds, width, final):

time: 96.5 us -> 96.2 us (level)
  waiting for transfers between devices: 8.91 us -> 6.89 us
  starting transfers between devices: 37.1 us -> 38.3 us
    ppermute x3, starting transfers between devices: 0.53 us -> 5.11 us  [exchange(): r3 = lax.ppermute(owned, AXES, pairs(3))]
    ppermute x3, waiting for transfers between devices: 3.44 us -> 0.01 us  [exchange(): r1 = lax.ppermute(p1, AXES, pairs(1))]
    ppermute x3, starting transfers between devices: 2.89 us -> 0.08 us  [exchange(): r2 = lax.ppermute(owned, AXES, pairs(2))]
    ppermute x12, starting transfers between devices: 13.3 us -> 15.7 us  [exchange(): lax.ppermute(buf, AXES, pairs(m))]
    ppermute x3, starting transfers between devices: 7.54 us -> 5.66 us  [exchange(): r1 = lax.ppermute(p1, AXES, pairs(1))]
    ppermute x3, waiting for transfers between devices: 0.01 us -> 1.15 us  [exchange(): rc = lax.ppermute(pc, AXES, cross)]
    ppermute x3, starting transfers between devices: 12.9 us -> 11.7 us  [exchange(): rc = lax.ppermute(pc, AXES, cross)]
    unnamed x58 -> x56, local copies, waits for them, and re-layouts: 7.68 us -> 7.7 us
  transfers between devices with their start and end apart: 24 -> 24, of which waited for: 6 -> 5; matrix products, arithmetic and copies ran while one was open for 13% -> 13% of each run, Pallas kernels for 15% -> 15%
where the time goes in v22:
time: 96.2 us; the launch traced here: 95.2 us
  starting transfers between devices  38.3 us (40%)
  Pallas kernels  29.5 us (31%)
  local copies, waits for them, and re-layouts  11.1 us (12%)
  other arithmetic  8.83 us (9%)
  waiting for transfers between devices  6.89 us (7%)
    ppermute x12, starting transfers between devices, exchange(): lax.ppermute(buf, AXES, pairs(m))  15.7 us
    pallas_call x3, Pallas kernels, hub_call(): pl.pallas_call(functools.partial(hub_kernel, n_hub, width, final), cost_e...  15.5 us
    pallas_call x3, Pallas kernels, band_call(): pl.pallas_call(functools.partial(band_kernel, fast, n_own), cost_estimate...  14 us
    ppermute x3, starting transfers between devices, exchange(): rc = lax.ppermute(pc, AXES, cross)  11.7 us
    unnamed x56, local copies, waits for them, and re-layouts  7.7 us
    ppermute x12, waiting for transfers between devices, exchange(): lax.ppermute(buf, AXES, pairs(m))  5.72 us
    ppermute x3, starting transfers between devices, exchange(): r1 = lax.ppermute(p1, AXES, pairs(1))  5.66 us
    ppermute x3, starting transfers between devices, exchange(): r3 = lax.ppermute(owned, AXES, pairs(3))  5.11 us
  transfers between devices with their start and end apart: 24, of which 5 were waited for; matrix products, arithmetic and copies ran while one was open for 13% of the time, Pallas kernels for 15%

profile of v22, /device:TPU:5, one launch (start us, length us, event | category | flops | bytes accessed | tf_op | source)
XLA Modules:
  0.0 95.2 jit_solution(4894282135725573053)
XLA Ops:
  3.4 3.4 %collective-permute-start.2 = (bf16[128,128]{1,0:T(8,128)(2,1)S(1)}, bf16[128,128]{1,0:T(8,128)(2,1)S(1)}, u32[]{:S(2)}, u32[]{:S(2)}) collective-permute-start(bf16[128,128]{1,0:T(8,128)(2,1)S(1)} %gather_fusion), channel_id=1, source_target_pairs={{0,3},{1,2},{2,1},{3,0},{4,7},{5,6},{6,5},{7,4},{8,11},{9,10},{10,... | collective-permute-start | bytes 98312 | tf_op jit(solution)/shard_map/ppermute | solution.py:49
  6.8 4.4 %collective-permute-start.3 = (bf16[256,128]{1,0:T(8,128)(2,1)S(1)}, bf16[256,128]{1,0:T(8,128)(2,1)S(1)}, u32[]{:S(2)}, u32[]{:S(2)}) collective-permute-start(bf16[256,128]{1,0:T(8,128)(2,1)S(1)} %get-tuple-element.71), channel_id=1, source_target_pairs={{3,4},{7,8},{11,12},{15,16},{19,20},{23,24},{27,28},{4,3},{8,7},{1... | collective-permute-start | bytes 196616 | tf_op jit(solution)/shard_map/ppermute | solution.py:56
  11.4 1.5 %fusion.rest_6_ = bf16[128,1024]{1,0:T(8,128)(2,1)} fusion(s32[128]{0:T(128)} %param.16), kind=kLoop, calls=%fused_computation.6 | loop fusion | flops 262144 | bytes 262656 | tf_op jit(solution)/shard_map/convert_element_type | solution.py:299
  13.7 2.2 %convert_reduce_fusion = f32[8,128]{1,0:T(8,128)S(1)} fusion(bf16[8,10,128,128]{3,2,1,0:T(8,128)(2,1)} %rest_3_.5), kind=kLoop, calls=%fused_computation.2 | loop fusion | flops 2620416 | bytes 2625536 | tf_op jit(solution)/shard_map/reduce_sum | solution.py:287
  16.7 1.3 %gather_fusion.1 = s32[48]{0:T(128)} fusion(s32[32]{0:T(128)S(1)} %copy-done, s32[1024]{0:T(1024)S(1)} %pad_clamp_fusion), kind=kCustom, calls=%fused_computation.1 | custom fusion | bytes 576 | tf_op jit(solution)/shard_map/gather | solution.py:281
  20.0 1.2 %collective-permute-start.5 = (bf16[4,128,128]{2,1,0:T(8,128)(2,1)S(1)}, bf16[4,128,128]{2,1,0:T(8,128)(2,1)S(1)}, u32[]{:S(2)}, u32[]{:S(2)}) collective-permute-start(bf16[4,128,128]{2,1,0:T(8,128)(2,1)S(1)} %pad_maximum_fusion), channel_id=1, source_target_pairs={{0,16},{1,17},{2,18},{3,19},{4,20},{5,21},{6,22},{7,23},{8,24},{9,... | collective-permute-start | bytes 393224 | tf_op jit(solution)/shard_map/ppermute | solution.py:66
  21.6 4.7 %shard_map.82.rest_3_ = f32[1024,128]{1,0:T(8,128)} custom-call(s32[1]{0:T(128)} %bitcast.z_ref, s32[80]{0:T(128)} %reshape.41.off_ref, bf16[1024,128]{1,0:T(8,128)(2,1)} %copy-done.2, bf16[384,128]{1,0:T(8,128)(2,1)} %copy-done.12, bf16[128,128]{1,0:T(8,128)(2,1)} %copy-done.9, bf16[256,128]{1,0:T(8,128)(2,1)} %copy-done.15, bf16[8,10,128,128]{3,2,1,0:T(8,128)(2,1)} %rest_3_.5), custom_call_target="tpu_custom_call" | custom-call | flops 335544320 | bytes 3670016 | tf_op jit(solution)/shard_map/pallas_call | solution.py:155
  27.1 2.7 %collective-permute-start.7 = (bf16[16,128,128]{2,1,0:T(8,128)(2,1)S(1)}, bf16[16,128,128]{2,1,0:T(8,128)(2,1)S(1)}, u32[]{:S(2)}, u32[]{:S(2)}) collective-permute-start(bf16[16,128,128]{2,1,0:T(8,128)(2,1)S(1)} %constant_dynamic-update-slice_fusion.rest_0_), channel_id=1, source_target_pairs={{0,4},{1,5},{2,6},{3,7},{4,0},{5,1},{6,2},{7,3},{8,12},{9,13},{10,... | collective-permute-start | bytes 1572872 | tf_op jit(solution)/shard_map/ppermute | solution.py:66
  29.8 1.5 %collective-permute-done.7.rest_1_ = bf16[16,128,128]{2,1,0:T(8,128)(2,1)S(1)} collective-permute-done((bf16[16,128,128]{2,1,0:T(8,128)(2,1)S(1)}, bf16[16,128,128]{2,1,0:T(8,128)(2,1)S(1)}, u32[]{:S(2)}, u32[]{:S(2)}) %collective-permute-start.7) | collective-permute-done | bytes 524320 | tf_op jit(solution)/shard_map/ppermute | solution.py:66
  32.2 5.2 %shard_map.83 = (bf16[1024,128]{1,0:T(8,128)(2,1)}, bf16[128,128]{1,0:T(8,128)(2,1)}, bf16[384,128]{1,0:T(8,128)(2,1)}, bf16[384,128]{1,0:T(8,128)(2,1)}, bf16[256,128]{1,0:T(8,128)(2,1)}) custom-call(s32[1]{0:T(128)} %bitcast.z_ref, s32[48]{0:T(128)} %gather_fusion.1, bf16[16,128,128]{2,1,0:T(8,128)(2,1)} %copy-done.4, bf16[16,128,128]{2,1,0:T(8,128)(2,1)} %copy-done.8, ...), custom_call_target="tpu_custom_call" | custom-call | flops 201326592 | bytes 4718592 | tf_op jit(solution)/shard_map/pallas_call | solution.py:255
  37.4 1.3 %collective-permute-start.10 = (bf16[128,128]{1,0:T(8,128)(2,1)}, bf16[128,128]{1,0:T(8,128)(2,1)S(1)}, u32[]{:S(2)}, u32[]{:S(2)}) collective-permute-start(bf16[128,128]{1,0:T(8,128)(2,1)} %get-tuple-element.55), channel_id=1, source_target_pairs={{0,3},{1,2},{2,1},{3,0},{4,7},{5,6},{6,5},{7,4},{8,11},{9,10},{10,... | collective-permute-start | bytes 98312 | tf_op jit(solution)/shard_map/ppermute | solution.py:49
  38.8 2.3 %collective-permute-start.8 = (bf16[384,128]{1,0:T(8,128)(2,1)}, bf16[384,128]{1,0:T(8,128)(2,1)S(1)}, u32[]{:S(2)}, u32[]{:S(2)}) collective-permute-start(bf16[384,128]{1,0:T(8,128)(2,1)} %get-tuple-element.56), channel_id=1, source_target_pairs={{0,1},{1,0},{2,3},{3,2},{4,5},{5,4},{6,7},{7,6},{8,9},{9,8},{10,11... | collective-permute-start | bytes 294920 | tf_op jit(solution)/shard_map/ppermute | solution.py:51
  41.8 4.2 %collective-permute-start.11 = (bf16[256,128]{1,0:T(8,128)(2,1)}, bf16[256,128]{1,0:T(8,128)(2,1)S(1)}, u32[]{:S(2)}, u32[]{:S(2)}) collective-permute-start(bf16[256,128]{1,0:T(8,128)(2,1)} %get-tuple-element.58), channel_id=1, source_target_pairs={{3,4},{7,8},{11,12},{15,16},{19,20},{23,24},{27,28},{4,3},{8,7},{1... | collective-permute-start | bytes 196616 | tf_op jit(solution)/shard_map/ppermute | solution.py:56
  50.3 4.7 %shard_map.84.rest_3_ = f32[1024,128]{1,0:T(8,128)} custom-call(s32[1]{0:T(128)} %bitcast.z_ref, s32[80]{0:T(128)} %reshape.41.off_ref, bf16[1024,128]{1,0:T(8,128)(2,1)} %get-tuple-element.57.cur_hbm, bf16[384,128]{1,0:T(8,128)(2,1)} %copy-done.14, bf16[128,128]{1,0:T(8,128)(2,1)} %copy-done.11, bf16[256,128]{1,0:T(8,128)(2,1)} %copy-done.17, ...), custom_call_target="tpu_custom_call" | custom-call | flops 335544320 | bytes 3670016 | tf_op jit(solution)/shard_map/pallas_call | solution.py:155
  56.9 2.0 %collective-permute-start.15 = (bf16[16,128,128]{2,1,0:T(8,128)(2,1)S(1)}, bf16[16,128,128]{2,1,0:T(8,128)(2,1)S(1)}, u32[]{:S(2)}, u32[]{:S(2)}) collective-permute-start(bf16[16,128,128]{2,1,0:T(8,128)(2,1)S(1)} %constant_dynamic-update-slice_fusion.7.rest_0_), channel_id=1, source_target_pairs={{0,4},{1,5},{2,6},{3,7},{4,0},{5,1},{6,2},{7,3},{8,12},{9,13},{10,... | collective-permute-start | bytes 1572872 | tf_op jit(solution)/shard_map/ppermute | solution.py:66
  58.9 1.5 %collective-permute-done.15.rest_1_ = bf16[16,128,128]{2,1,0:T(8,128)(2,1)S(1)} collective-permute-done((bf16[16,128,128]{2,1,0:T(8,128)(2,1)S(1)}, bf16[16,128,128]{2,1,0:T(8,128)(2,1)S(1)}, u32[]{:S(2)}, u32[]{:S(2)}) %collective-permute-start.15) | collective-permute-done | bytes 524320 | tf_op jit(solution)/shard_map/ppermute | solution.py:66
  61.2 5.2 %shard_map.85 = (bf16[1024,128]{1,0:T(8,128)(2,1)}, bf16[128,128]{1,0:T(8,128)(2,1)}, bf16[384,128]{1,0:T(8,128)(2,1)}, bf16[384,128]{1,0:T(8,128)(2,1)}, bf16[256,128]{1,0:T(8,128)(2,1)}) custom-call(s32[1]{0:T(128)} %bitcast.z_ref, s32[48]{0:T(128)} %gather_fusion.1, bf16[16,128,128]{2,1,0:T(8,128)(2,1)} %copy-done.5, bf16[16,128,128]{2,1,0:T(8,128)(2,1)} %copy-done.7, ...), custom_call_target="tpu_custom_call" | custom-call | flops 201326592 | bytes 4718592 | tf_op jit(solution)/shard_map/pallas_call | solution.py:255
  66.9 3.2 %collective-permute-start.16 = (bf16[384,128]{1,0:T(8,128)(2,1)}, bf16[384,128]{1,0:T(8,128)(2,1)S(1)}, u32[]{:S(2)}, u32[]{:S(2)}) collective-permute-start(bf16[384,128]{1,0:T(8,128)(2,1)} %get-tuple-element.64), channel_id=1, source_target_pairs={{0,1},{1,0},{2,3},{3,2},{4,5},{5,4},{6,7},{7,6},{8,9},{9,8},{10,11... | collective-permute-start | bytes 294920 | tf_op jit(solution)/shard_map/ppermute | solution.py:51
  70.8 3.2 %collective-permute-start.19 = (bf16[256,128]{1,0:T(8,128)(2,1)}, bf16[256,128]{1,0:T(8,128)(2,1)S(1)}, u32[]{:S(2)}, u32[]{:S(2)}) collective-permute-start(bf16[256,128]{1,0:T(8,128)(2,1)} %get-tuple-element.66), channel_id=1, source_target_pairs={{3,4},{7,8},{11,12},{15,16},{19,20},{23,24},{27,28},{4,3},{8,7},{1... | collective-permute-start | bytes 196616 | tf_op jit(solution)/shard_map/ppermute | solution.py:56
  74.9 1.5 %collective-permute-start.22 = (bf16[4,128,128]{2,1,0:T(8,128)(2,1)S(1)}, bf16[4,128,128]{2,1,0:T(8,128)(2,1)S(1)}, u32[]{:S(2)}, u32[]{:S(2)}) collective-permute-start(bf16[4,128,128]{2,1,0:T(8,128)(2,1)S(1)} %pad_maximum_fusion.2), channel_id=1, source_target_pairs={{0,24},{1,25},{2,26},{3,27},{4,28},{5,29},{6,30},{7,31},{8,16},{9,... | collective-permute-start | bytes 393224 | tf_op jit(solution)/shard_map/ppermute | solution.py:66
  79.4 4.7 %shard_map.86.rest_3_ = f32[1024,128]{1,0:T(8,128)} custom-call(s32[1]{0:T(128)} %bitcast.z_ref, s32[80]{0:T(128)} %reshape.41.off_ref, bf16[1024,128]{1,0:T(8,128)(2,1)} %get-tuple-element.65.cur_hbm, bf16[384,128]{1,0:T(8,128)(2,1)} %copy-done.13, bf16[128,128]{1,0:T(8,128)(2,1)} %copy-done.10, bf16[256,128]{1,0:T(8,128)(2,1)} %copy-done.16, ...), custom_call_target="tpu_custom_call" | custom-call | flops 335544320 | bytes 3670016 | tf_op jit(solution)/shard_map/pallas_call | solution.py:155
  84.9 2.9 %collective-permute-start.23 = (bf16[16,128,128]{2,1,0:T(8,128)(2,1)S(1)}, bf16[16,128,128]{2,1,0:T(8,128)(2,1)S(1)}, u32[]{:S(2)}, u32[]{:S(2)}) collective-permute-start(bf16[16,128,128]{2,1,0:T(8,128)(2,1)S(1)} %constant_dynamic-update-slice_fusion.14.rest_0_), channel_id=1, source_target_pairs={{0,4},{1,5},{2,6},{3,7},{4,0},{5,1},{6,2},{7,3},{8,12},{9,13},{10,... | collective-permute-start | bytes 1572872 | tf_op jit(solution)/shard_map/ppermute | solution.py:66
  87.9 1.5 %collective-permute-done.23.rest_1_ = bf16[16,128,128]{2,1,0:T(8,128)(2,1)S(1)} collective-permute-done((bf16[16,128,128]{2,1,0:T(8,128)(2,1)S(1)}, bf16[16,128,128]{2,1,0:T(8,128)(2,1)S(1)}, u32[]{:S(2)}, u32[]{:S(2)}) %collective-permute-start.23) | collective-permute-done | bytes 524320 | tf_op jit(solution)/shard_map/ppermute | solution.py:66
  90.2 5.0 %shard_map.87 = f32[1024,128]{1,0:T(8,128)} custom-call(s32[1]{0:T(128)} %bitcast.z_ref, s32[48]{0:T(128)} %gather_fusion.1, bf16[16,128,128]{2,1,0:T(8,128)(2,1)} %copy-done.3, bf16[16,128,128]{2,1,0:T(8,128)(2,1)} %copy-done.6, bf16[8,6,128,128]{3,2,1,0:T(8,128)(2,1)} %rest_2_.5, f32[1024,128]{1,0:T(8,128)} %shard_map.86.rest_3_, ...), custom_call_target="tpu_custom_call" | custom-call | flops 201326592 | bytes 4718592 | tf_op jit(solution)/shard_map/pallas_call | solution.py:255
  (112 shorter events, 23.5 us)
Async XLA Ops:
  3.4 15.3 %collective-permute-start.2 = (bf16[128,128]{1,0:T(8,128)(2,1)S(1)}, bf16[128,128]{1,0:T(8,128)(2,1)S(1)}, u32[]{:S(2)}, u32[]{:S(2)}) collective-permute-start(bf16[128,128]{1,0:T(8,128)(2,1)S(1)} %gather_fusion), channel_id=1, source_target_pairs={{0,3},{1,2},{2,1},{3,0},{4,7},{5,6},{6,5},{7,4},{8,11},{9,10},{10,... | collective-permute-start | bytes 98312 | tf_op jit(solution)/shard_map/ppermute | solution.py:49
  6.8 12.0 %collective-permute-start.1 = (bf16[128,128]{1,0:T(8,128)(2,1)S(1)}, bf16[128,128]{1,0:T(8,128)(2,1)S(1)}, u32[]{:S(2)}, u32[]{:S(2)}) collective-permute-start(bf16[128,128]{1,0:T(8,128)(2,1)S(1)} %gather_fusion), channel_id=1, source_target_pairs={{0,2},{1,3},{2,0},{3,1},{4,6},{5,7},{6,4},{7,5},{8,10},{9,11},{10,... | collective-permute-start | bytes 98312 | tf_op jit(solution)/shard_map/ppermute | solution.py:50
  6.8 11.9 %collective-permute-start.3 = (bf16[256,128]{1,0:T(8,128)(2,1)S(1)}, bf16[256,128]{1,0:T(8,128)(2,1)S(1)}, u32[]{:S(2)}, u32[]{:S(2)}) collective-permute-start(bf16[256,128]{1,0:T(8,128)(2,1)S(1)} %get-tuple-element.71), channel_id=1, source_target_pairs={{3,4},{7,8},{11,12},{15,16},{19,20},{23,24},{27,28},{4,3},{8,7},{1... | collective-permute-start | bytes 196616 | tf_op jit(solution)/shard_map/ppermute | solution.py:56
  11.2 7.6 %collective-permute-start = (bf16[384,128]{1,0:T(8,128)(2,1)S(1)}, bf16[384,128]{1,0:T(8,128)(2,1)S(1)}, u32[]{:S(2)}, u32[]{:S(2)}) collective-permute-start(bf16[384,128]{1,0:T(8,128)(2,1)S(1)} %pad_maximum_fusion.3), channel_id=1, source_target_pairs={{0,1},{1,0},{2,3},{3,2},{4,5},{5,4},{6,7},{7,6},{8,9},{9,8},{10,11... | collective-permute-start | bytes 294920 | tf_op jit(solution)/shard_map/ppermute | solution.py:51
  18.8 8.2 %collective-permute-start.6 = (bf16[4,128,128]{2,1,0:T(8,128)(2,1)S(1)}, bf16[4,128,128]{2,1,0:T(8,128)(2,1)S(1)}, u32[]{:S(2)}, u32[]{:S(2)}) collective-permute-start(bf16[4,128,128]{2,1,0:T(8,128)(2,1)S(1)} %pad_maximum_fusion), channel_id=1, source_target_pairs={{0,24},{1,25},{2,26},{3,27},{4,28},{5,29},{6,30},{7,31},{8,16},{9,... | collective-permute-start | bytes 393224 | tf_op jit(solution)/shard_map/ppermute | solution.py:66
  20.0 7.0 %collective-permute-start.5 = (bf16[4,128,128]{2,1,0:T(8,128)(2,1)S(1)}, bf16[4,128,128]{2,1,0:T(8,128)(2,1)S(1)}, u32[]{:S(2)}, u32[]{:S(2)}) collective-permute-start(bf16[4,128,128]{2,1,0:T(8,128)(2,1)S(1)} %pad_maximum_fusion), channel_id=1, source_target_pairs={{0,16},{1,17},{2,18},{3,19},{4,20},{5,21},{6,22},{7,23},{8,24},{9,... | collective-permute-start | bytes 393224 | tf_op jit(solution)/shard_map/ppermute | solution.py:66
  21.3 5.8 %collective-permute-start.4 = (bf16[4,128,128]{2,1,0:T(8,128)(2,1)S(1)}, bf16[4,128,128]{2,1,0:T(8,128)(2,1)S(1)}, u32[]{:S(2)}, u32[]{:S(2)}) collective-permute-start(bf16[4,128,128]{2,1,0:T(8,128)(2,1)S(1)} %pad_maximum_fusion), channel_id=1, source_target_pairs={{0,8},{1,9},{2,10},{3,11},{4,12},{5,13},{6,14},{7,15},{8,0},{9,1},... | collective-permute-start | bytes 393224 | tf_op jit(solution)/shard_map/ppermute | solution.py:66
  27.1 4.2 %collective-permute-start.7 = (bf16[16,128,128]{2,1,0:T(8,128)(2,1)S(1)}, bf16[16,128,128]{2,1,0:T(8,128)(2,1)S(1)}, u32[]{:S(2)}, u32[]{:S(2)}) collective-permute-start(bf16[16,128,128]{2,1,0:T(8,128)(2,1)S(1)} %constant_dynamic-update-slice_fusion.rest_0_), channel_id=1, source_target_pairs={{0,4},{1,5},{2,6},{3,7},{4,0},{5,1},{6,2},{7,3},{8,12},{9,13},{10,... | collective-permute-start | bytes 1572872 | tf_op jit(solution)/shard_map/ppermute | solution.py:66
  37.4 8.6 %collective-permute-start.10 = (bf16[128,128]{1,0:T(8,128)(2,1)}, bf16[128,128]{1,0:T(8,128)(2,1)S(1)}, u32[]{:S(2)}, u32[]{:S(2)}) collective-permute-start(bf16[128,128]{1,0:T(8,128)(2,1)} %get-tuple-element.55), channel_id=1, source_target_pairs={{0,3},{1,2},{2,1},{3,0},{4,7},{5,6},{6,5},{7,4},{8,11},{9,10},{10,... | collective-permute-start | bytes 98312 | tf_op jit(solution)/shard_map/ppermute | solution.py:49
  38.7 7.4 %collective-permute-start.9 = (bf16[128,128]{1,0:T(8,128)(2,1)}, bf16[128,128]{1,0:T(8,128)(2,1)S(1)}, u32[]{:S(2)}, u32[]{:S(2)}) collective-permute-start(bf16[128,128]{1,0:T(8,128)(2,1)} %get-tuple-element.55), channel_id=1, source_target_pairs={{0,2},{1,3},{2,0},{3,1},{4,6},{5,7},{6,4},{7,5},{8,10},{9,11},{10,... | collective-permute-start | bytes 98312 | tf_op jit(solution)/shard_map/ppermute | solution.py:50
  38.8 7.2 %collective-permute-start.8 = (bf16[384,128]{1,0:T(8,128)(2,1)}, bf16[384,128]{1,0:T(8,128)(2,1)S(1)}, u32[]{:S(2)}, u32[]{:S(2)}) collective-permute-start(bf16[384,128]{1,0:T(8,128)(2,1)} %get-tuple-element.56), channel_id=1, source_target_pairs={{0,1},{1,0},{2,3},{3,2},{4,5},{5,4},{6,7},{7,6},{8,9},{9,8},{10,11... | collective-permute-start | bytes 294920 | tf_op jit(solution)/shard_map/ppermute | solution.py:51
  41.8 7.8 %collective-permute-start.11 = (bf16[256,128]{1,0:T(8,128)(2,1)}, bf16[256,128]{1,0:T(8,128)(2,1)S(1)}, u32[]{:S(2)}, u32[]{:S(2)}) collective-permute-start(bf16[256,128]{1,0:T(8,128)(2,1)} %get-tuple-element.58), channel_id=1, source_target_pairs={{3,4},{7,8},{11,12},{15,16},{19,20},{23,24},{27,28},{4,3},{8,7},{1... | collective-permute-start | bytes 196616 | tf_op jit(solution)/shard_map/ppermute | solution.py:56
  46.9 8.8 %collective-permute-start.14 = (bf16[4,128,128]{2,1,0:T(8,128)(2,1)S(1)}, bf16[4,128,128]{2,1,0:T(8,128)(2,1)S(1)}, u32[]{:S(2)}, u32[]{:S(2)}) collective-permute-start(bf16[4,128,128]{2,1,0:T(8,128)(2,1)S(1)} %pad_maximum_fusion.1), channel_id=1, source_target_pairs={{0,24},{1,25},{2,26},{3,27},{4,28},{5,29},{6,30},{7,31},{8,16},{9,... | collective-permute-start | bytes 393224 | tf_op jit(solution)/shard_map/ppermute | solution.py:66
  48.1 8.7 %collective-permute-start.13 = (bf16[4,128,128]{2,1,0:T(8,128)(2,1)S(1)}, bf16[4,128,128]{2,1,0:T(8,128)(2,1)S(1)}, u32[]{:S(2)}, u32[]{:S(2)}) collective-permute-start(bf16[4,128,128]{2,1,0:T(8,128)(2,1)S(1)} %pad_maximum_fusion.1), channel_id=1, source_target_pairs={{0,16},{1,17},{2,18},{3,19},{4,20},{5,21},{6,22},{7,23},{8,24},{9,... | collective-permute-start | bytes 393224 | tf_op jit(solution)/shard_map/ppermute | solution.py:66
  48.8 8.0 %collective-permute-start.12 = (bf16[4,128,128]{2,1,0:T(8,128)(2,1)S(1)}, bf16[4,128,128]{2,1,0:T(8,128)(2,1)S(1)}, u32[]{:S(2)}, u32[]{:S(2)}) collective-permute-start(bf16[4,128,128]{2,1,0:T(8,128)(2,1)S(1)} %pad_maximum_fusion.1), channel_id=1, source_target_pairs={{0,8},{1,9},{2,10},{3,11},{4,12},{5,13},{6,14},{7,15},{8,0},{9,1},... | collective-permute-start | bytes 393224 | tf_op jit(solution)/shard_map/ppermute | solution.py:66
  56.9 3.5 %collective-permute-start.15 = (bf16[16,128,128]{2,1,0:T(8,128)(2,1)S(1)}, bf16[16,128,128]{2,1,0:T(8,128)(2,1)S(1)}, u32[]{:S(2)}, u32[]{:S(2)}) collective-permute-start(bf16[16,128,128]{2,1,0:T(8,128)(2,1)S(1)} %constant_dynamic-update-slice_fusion.7.rest_0_), channel_id=1, source_target_pairs={{0,4},{1,5},{2,6},{3,7},{4,0},{5,1},{6,2},{7,3},{8,12},{9,13},{10,... | collective-permute-start | bytes 1572872 | tf_op jit(solution)/shard_map/ppermute | solution.py:66
  66.5 7.6 %collective-permute-start.18 = (bf16[128,128]{1,0:T(8,128)(2,1)}, bf16[128,128]{1,0:T(8,128)(2,1)S(1)}, u32[]{:S(2)}, u32[]{:S(2)}) collective-permute-start(bf16[128,128]{1,0:T(8,128)(2,1)} %get-tuple-element.63), channel_id=1, source_target_pairs={{0,3},{1,2},{2,1},{3,0},{4,7},{5,6},{6,5},{7,4},{8,11},{9,10},{10,... | collective-permute-start | bytes 98312 | tf_op jit(solution)/shard_map/ppermute | solution.py:49
  66.9 7.1 %collective-permute-start.17 = (bf16[128,128]{1,0:T(8,128)(2,1)}, bf16[128,128]{1,0:T(8,128)(2,1)S(1)}, u32[]{:S(2)}, u32[]{:S(2)}) collective-permute-start(bf16[128,128]{1,0:T(8,128)(2,1)} %get-tuple-element.63), channel_id=1, source_target_pairs={{0,2},{1,3},{2,0},{3,1},{4,6},{5,7},{6,4},{7,5},{8,10},{9,11},{10,... | collective-permute-start | bytes 98312 | tf_op jit(solution)/shard_map/ppermute | solution.py:50
  66.9 7.1 %collective-permute-start.16 = (bf16[384,128]{1,0:T(8,128)(2,1)}, bf16[384,128]{1,0:T(8,128)(2,1)S(1)}, u32[]{:S(2)}, u32[]{:S(2)}) collective-permute-start(bf16[384,128]{1,0:T(8,128)(2,1)} %get-tuple-element.64), channel_id=1, source_target_pairs={{0,1},{1,0},{2,3},{3,2},{4,5},{5,4},{6,7},{7,6},{8,9},{9,8},{10,11... | collective-permute-start | bytes 294920 | tf_op jit(solution)/shard_map/ppermute | solution.py:51
  70.8 7.9 %collective-permute-start.19 = (bf16[256,128]{1,0:T(8,128)(2,1)}, bf16[256,128]{1,0:T(8,128)(2,1)S(1)}, u32[]{:S(2)}, u32[]{:S(2)}) collective-permute-start(bf16[256,128]{1,0:T(8,128)(2,1)} %get-tuple-element.66), channel_id=1, source_target_pairs={{3,4},{7,8},{11,12},{15,16},{19,20},{23,24},{27,28},{4,3},{8,7},{1... | collective-permute-start | bytes 196616 | tf_op jit(solution)/shard_map/ppermute | solution.py:56
  74.9 10.0 %collective-permute-start.22 = (bf16[4,128,128]{2,1,0:T(8,128)(2,1)S(1)}, bf16[4,128,128]{2,1,0:T(8,128)(2,1)S(1)}, u32[]{:S(2)}, u32[]{:S(2)}) collective-permute-start(bf16[4,128,128]{2,1,0:T(8,128)(2,1)S(1)} %pad_maximum_fusion.2), channel_id=1, source_target_pairs={{0,24},{1,25},{2,26},{3,27},{4,28},{5,29},{6,30},{7,31},{8,16},{9,... | collective-permute-start | bytes 393224 | tf_op jit(solution)/shard_map/ppermute | solution.py:66
  76.4 8.5 %collective-permute-start.21 = (bf16[4,128,128]{2,1,0:T(8,128)(2,1)S(1)}, bf16[4,128,128]{2,1,0:T(8,128)(2,1)S(1)}, u32[]{:S(2)}, u32[]{:S(2)}) collective-permute-start(bf16[4,128,128]{2,1,0:T(8,128)(2,1)S(1)} %pad_maximum_fusion.2), channel_id=1, source_target_pairs={{0,16},{1,17},{2,18},{3,19},{4,20},{5,21},{6,22},{7,23},{8,24},{9,... | collective-permute-start | bytes 393224 | tf_op jit(solution)/shard_map/ppermute | solution.py:66
  76.5 8.4 %collective-permute-start.20 = (bf16[4,128,128]{2,1,0:T(8,128)(2,1)S(1)}, bf16[4,128,128]{2,1,0:T(8,128)(2,1)S(1)}, u32[]{:S(2)}, u32[]{:S(2)}) collective-permute-start(bf16[4,128,128]{2,1,0:T(8,128)(2,1)S(1)} %pad_maximum_fusion.2), channel_id=1, source_target_pairs={{0,8},{1,9},{2,10},{3,11},{4,12},{5,13},{6,14},{7,15},{8,0},{9,1},... | collective-permute-start | bytes 393224 | tf_op jit(solution)/shard_map/ppermute | solution.py:66
  84.9 4.5 %collective-permute-start.23 = (bf16[16,128,128]{2,1,0:T(8,128)(2,1)S(1)}, bf16[16,128,128]{2,1,0:T(8,128)(2,1)S(1)}, u32[]{:S(2)}, u32[]{:S(2)}) collective-permute-start(bf16[16,128,128]{2,1,0:T(8,128)(2,1)S(1)} %constant_dynamic-update-slice_fusion.14.rest_0_), channel_id=1, source_target_pairs={{0,4},{1,5},{2,6},{3,7},{4,0},{5,1},{6,2},{7,3},{8,12},{9,13},{10,... | collective-permute-start | bytes 1572872 | tf_op jit(solution)/shard_map/ppermute | solution.py:66
  (19 other events, 97.8 us)

commit v23 on v22

--- a/solution.py
+++ b/solution.py
@@ -30,12 +30,11 @@
     top = current[current.shape[0] - width:]
     bottom = current[:width]
     p1 = jnp.concatenate([owned, jnp.where(z % 2 == 0, top, bottom)], 0)
-    p3 = jnp.concatenate([owned, jnp.where(z == 1, top, bottom)], 0)
     pc = jnp.where((z == 3) | (z == 1), top, bottom)
-    return p1, p3, pc
-
-
-def exchange(current, owned, p1, p3, pc, hub_blocks, width, block_rows, middle, prep):
+    return p1, pc
+
+
+def exchange(current, owned, p1, pc, hub_blocks, width, block_rows, middle, prep):
     count = lax.axis_size(AXES)
     if not fast_path(owned, block_rows):
         forward = [(i, i + 1) for i in range(count - 1)]
@@ -172,7 +171,7 @@
         (ht_hbm, band_hbm, deg_ref, seeds_hbm, out_ref, hub, ht, band, seeds, sem) = rest[n_hub:]
     else:
         (ht_hbm, band_hbm, deg_ref, seeds_hbm, pick_ref,
-         cur_ref, owned_ref, p1_ref, p3_ref, pc_ref,
+         cur_ref, owned_ref, p1_ref, pc_ref,
          hub, ht, band, seeds, sem) = rest[n_hub:]
     blocks, k_hub, rows = ht.shape[0], ht.shape[1], ht.shape[2]
     per_block = []
@@ -224,12 +223,10 @@
     owned = jnp.dot(pick_ref[...], cur_ref[...], preferred_element_type=jnp.float32).astype(owned_ref.dtype)
     owned_ref[...] = owned
     p1_ref[pl.ds(0, n_own), :] = owned
-    p3_ref[pl.ds(0, n_own), :] = owned
     z = z_ref[0]
     top = cur_ref[pl.ds(own - width, width), :]
     bottom = cur_ref[pl.ds(0, width), :]
     p1_ref[pl.ds(n_own, width), :] = jnp.where(z % 2 == 0, top, bottom)
-    p3_ref[pl.ds(n_own, width), :] = jnp.where(z == 1, top, bottom)
     pc_ref[...] = jnp.where((z == 3) | (z == 1), top, bottom)
 
 
@@ -248,7 +245,6 @@
         outs = [
             jax.ShapeDtypeStruct(seeds.shape, bf),
             jax.ShapeDtypeStruct((n_own, classes), bf),
-            jax.ShapeDtypeStruct((n_own + width, classes), bf),
             jax.ShapeDtypeStruct((n_own + width, classes), bf),
             jax.ShapeDtypeStruct((width, classes), bf),
         ]
@@ -294,7 +290,7 @@
     current = seeds.astype(jnp.bfloat16)
     seeds16 = current
     owned = current[hub_rows]
-    p1, p3, pc = payloads(current, owned, z[0], width)
+    p1, pc = payloads(current, owned, z[0], width)
     fast = fast_path(owned, block_rows)
     pick = (hub_rows[:, None] == jnp.arange(current.shape[0], dtype=hub_rows.dtype)[None, :]).astype(jnp.bfloat16)
     prep = (pick, degree, positions_of(hub_blocks, owned, block_rows).reshape(-1))
@@ -303,7 +299,7 @@
             band_call, z, band_offsets, current, band_tiles=band_tiles, fast=fast, n_own=owned.shape[0], width=width
         )
         band, hub_pieces, prep_out = exchange(
-            current, owned, p1, p3, pc, hub_blocks, width, block_rows, lambda rims: middle(rims), prep
+            current, owned, p1, pc, hub_blocks, width, block_rows, lambda rims: middle(rims), prep
         )
         if prep is not None:
             pick, degree, hub_index = prep_out
@@ -313,7 +309,7 @@
         if final:
             labels = outs[0]
         else:
-            current, owned, p1, p3, pc = outs
+            current, owned, p1, pc = outs
     return labels
 
 

time: 96.2 us -> 95.2 us (0.990)
    ppermute x3, starting transfers between devices: 5.66 us -> 0.62 us  [exchange(): r1 = lax.ppermute(p1, AXES, pairs(1))]
    ppermute x3, starting transfers between devices: 0.08 us -> 4.2 us  [exchange(): r2 = lax.ppermute(owned, AXES, pairs(2))]
    ppermute x3, starting transfers between devices: 11.7 us -> 13.1 us  [exchange(): rc = lax.ppermute(pc, AXES, cross)]
    ppermute x12, starting transfers between devices: 15.7 us -> 14.5 us  [exchange(): lax.ppermute(buf, AXES, pairs(m))]
    ppermute x3, starting transfers between devices: 5.11 us -> 6.13 us  [exchange(): r3 = lax.ppermute(owned, AXES, pairs(3))]
    unnamed x56 -> x58, local copies, waits for them, and re-layouts: 7.7 us -> 7.72 us
where the time goes in v23:
time: 95.2 us; the launch traced here: 94.2 us
  starting transfers between devices  38.5 us (40%)
  Pallas kernels  29.4 us (31%)
  local copies, waits for them, and re-layouts  11.1 us (12%)
  other arithmetic  8.17 us (9%)
  waiting for transfers between devices  6.54 us (7%)
    pallas_call x3, Pallas kernels, hub_call(): pl.pallas_call(functools.partial(hub_kernel, n_hub, width, final), cost_e...  15.4 us
    ppermute x12, starting transfers between devices, exchange(): lax.ppermute(buf, AXES, pairs(m))  14.5 us
    pallas_call x3, Pallas kernels, band_call(): pl.pallas_call(functools.partial(band_kernel, fast, n_own), cost_estimate...  14 us
    ppermute x3, starting transfers between devices, exchange(): rc = lax.ppermute(pc, AXES, cross)  13.1 us
    unnamed x58, local copies, waits for them, and re-layouts  7.72 us
    ppermute x3, starting transfers between devices, exchange(): r3 = lax.ppermute(owned, AXES, pairs(3))  6.13 us
    ppermute x12, waiting for transfers between devices, exchange(): lax.ppermute(buf, AXES, pairs(m))  5.44 us
    ppermute x3, starting transfers between devices, exchange(): r2 = lax.ppermute(owned, AXES, pairs(2))  4.2 us
  transfers between devices with their start and end apart: 24, of which 5 were waited for; matrix products, arithmetic and copies ran while one was open for 13% of the time, Pallas kernels for 15%

profile of v23, /device:TPU:5, one launch (start us, length us, event | category | flops | bytes accessed | tf_op | source)
XLA Modules:
  0.0 94.2 jit_solution(17271500676146000734)
XLA Ops:
  3.4 2.4 %collective-permute-start.1 = (bf16[128,128]{1,0:T(8,128)(2,1)S(1)}, bf16[128,128]{1,0:T(8,128)(2,1)S(1)}, u32[]{:S(2)}, u32[]{:S(2)}) collective-permute-start(bf16[128,128]{1,0:T(8,128)(2,1)S(1)} %gather_fusion), channel_id=1, source_target_pairs={{0,2},{1,3},{2,0},{3,1},{4,6},{5,7},{6,4},{7,5},{8,10},{9,11},{10,... | collective-permute-start | bytes 98312 | tf_op jit(solution)/shard_map/ppermute | solution.py:49
  7.2 5.7 %collective-permute-start.3 = (bf16[256,128]{1,0:T(8,128)(2,1)S(1)}, bf16[256,128]{1,0:T(8,128)(2,1)S(1)}, u32[]{:S(2)}, u32[]{:S(2)}) collective-permute-start(bf16[256,128]{1,0:T(8,128)(2,1)S(1)} %get-tuple-element.71), channel_id=1, source_target_pairs={{3,4},{7,8},{11,12},{15,16},{19,20},{23,24},{27,28},{4,3},{8,7},{1... | collective-permute-start | bytes 196616 | tf_op jit(solution)/shard_map/ppermute | solution.py:55
  12.8 1.5 %fusion.rest_6_ = bf16[128,1024]{1,0:T(8,128)(2,1)} fusion(s32[128]{0:T(128)} %param.16), kind=kLoop, calls=%fused_computation.6 | loop fusion | flops 262144 | bytes 262656 | tf_op jit(solution)/shard_map/convert_element_type | solution.py:295
  14.3 2.2 %convert_reduce_fusion = f32[8,128]{1,0:T(8,128)S(1)} fusion(bf16[8,10,128,128]{3,2,1,0:T(8,128)(2,1)} %rest_3_.5), kind=kLoop, calls=%fused_computation.2 | loop fusion | flops 2620416 | bytes 2625536 | tf_op jit(solution)/shard_map/reduce_sum | solution.py:283
  18.1 1.3 %gather_fusion.1 = s32[48]{0:T(128)} fusion(s32[32]{0:T(128)S(1)} %copy-done, s32[1024]{0:T(1024)S(1)} %pad_clamp_fusion), kind=kCustom, calls=%fused_computation.1 | custom fusion | bytes 576 | tf_op jit(solution)/shard_map/gather | solution.py:277
  19.5 1.3 %collective-permute-start.4 = (bf16[4,128,128]{2,1,0:T(8,128)(2,1)S(1)}, bf16[4,128,128]{2,1,0:T(8,128)(2,1)S(1)}, u32[]{:S(2)}, u32[]{:S(2)}) collective-permute-start(bf16[4,128,128]{2,1,0:T(8,128)(2,1)S(1)} %pad_maximum_fusion), channel_id=1, source_target_pairs={{0,8},{1,9},{2,10},{3,11},{4,12},{5,13},{6,14},{7,15},{8,0},{9,1},... | collective-permute-start | bytes 393224 | tf_op jit(solution)/shard_map/ppermute | solution.py:65
  21.0 1.2 %collective-permute-start.6 = (bf16[4,128,128]{2,1,0:T(8,128)(2,1)S(1)}, bf16[4,128,128]{2,1,0:T(8,128)(2,1)S(1)}, u32[]{:S(2)}, u32[]{:S(2)}) collective-permute-start(bf16[4,128,128]{2,1,0:T(8,128)(2,1)S(1)} %pad_maximum_fusion), channel_id=1, source_target_pairs={{0,24},{1,25},{2,26},{3,27},{4,28},{5,29},{6,30},{7,31},{8,16},{9,... | collective-permute-start | bytes 393224 | tf_op jit(solution)/shard_map/ppermute | solution.py:65
  22.3 4.7 %shard_map.82.rest_3_ = f32[1024,128]{1,0:T(8,128)} custom-call(s32[1]{0:T(128)} %bitcast.z_ref, s32[80]{0:T(128)} %reshape.41.off_ref, bf16[1024,128]{1,0:T(8,128)(2,1)} %copy-done.2, bf16[384,128]{1,0:T(8,128)(2,1)} %copy-done.12, bf16[128,128]{1,0:T(8,128)(2,1)} %copy-done.9, bf16[256,128]{1,0:T(8,128)(2,1)} %copy-done.15, bf16[8,10,128,128]{3,2,1,0:T(8,128)(2,1)} %rest_3_.5), custom_call_target="tpu_custom_call" | custom-call | flops 335544320 | bytes 3670016 | tf_op jit(solution)/shard_map/pallas_call | solution.py:154
  29.1 1.5 %collective-permute-done.7.rest_1_ = bf16[16,128,128]{2,1,0:T(8,128)(2,1)S(1)} collective-permute-done((bf16[16,128,128]{2,1,0:T(8,128)(2,1)S(1)}, bf16[16,128,128]{2,1,0:T(8,128)(2,1)S(1)}, u32[]{:S(2)}, u32[]{:S(2)}) %collective-permute-start.7) | collective-permute-done | bytes 524320 | tf_op jit(solution)/shard_map/ppermute | solution.py:65
  31.4 5.2 %shard_map.83 = (bf16[1024,128]{1,0:T(8,128)(2,1)}, bf16[128,128]{1,0:T(8,128)(2,1)}, bf16[384,128]{1,0:T(8,128)(2,1)}, bf16[256,128]{1,0:T(8,128)(2,1)}) custom-call(s32[1]{0:T(128)} %bitcast.z_ref, s32[48]{0:T(128)} %gather_fusion.1, bf16[16,128,128]{2,1,0:T(8,128)(2,1)} %copy-done.4, bf16[16,128,128]{2,1,0:T(8,128)(2,1)} %copy-done.8, ...), custom_call_target="tpu_custom_call" | custom-call | flops 201326592 | bytes 4718592 | tf_op jit(solution)/shard_map/pallas_call | solution.py:251
  38.8 2.3 %collective-permute-start.10 = (bf16[128,128]{1,0:T(8,128)(2,1)}, bf16[128,128]{1,0:T(8,128)(2,1)S(1)}, u32[]{:S(2)}, u32[]{:S(2)}) collective-permute-start(bf16[128,128]{1,0:T(8,128)(2,1)} %get-tuple-element.55), channel_id=1, source_target_pairs={{0,3},{1,2},{2,1},{3,0},{4,7},{5,6},{6,5},{7,4},{8,11},{9,10},{10,... | collective-permute-start | bytes 98312 | tf_op jit(solution)/shard_map/ppermute | solution.py:48
  41.0 4.0 %collective-permute-start.11 = (bf16[256,128]{1,0:T(8,128)(2,1)}, bf16[256,128]{1,0:T(8,128)(2,1)S(1)}, u32[]{:S(2)}, u32[]{:S(2)}) collective-permute-start(bf16[256,128]{1,0:T(8,128)(2,1)} %get-tuple-element.58), channel_id=1, source_target_pairs={{3,4},{7,8},{11,12},{15,16},{19,20},{23,24},{27,28},{4,3},{8,7},{1... | collective-permute-start | bytes 196616 | tf_op jit(solution)/shard_map/ppermute | solution.py:55
  47.1 1.5 %collective-permute-start.14 = (bf16[4,128,128]{2,1,0:T(8,128)(2,1)S(1)}, bf16[4,128,128]{2,1,0:T(8,128)(2,1)S(1)}, u32[]{:S(2)}, u32[]{:S(2)}) collective-permute-start(bf16[4,128,128]{2,1,0:T(8,128)(2,1)S(1)} %pad_maximum_fusion.1), channel_id=1, source_target_pairs={{0,24},{1,25},{2,26},{3,27},{4,28},{5,29},{6,30},{7,31},{8,16},{9,... | collective-permute-start | bytes 393224 | tf_op jit(solution)/shard_map/ppermute | solution.py:65
  49.3 4.7 %shard_map.84.rest_3_ = f32[1024,128]{1,0:T(8,128)} custom-call(s32[1]{0:T(128)} %bitcast.z_ref, s32[80]{0:T(128)} %reshape.41.off_ref, bf16[1024,128]{1,0:T(8,128)(2,1)} %get-tuple-element.57.cur_hbm, bf16[384,128]{1,0:T(8,128)(2,1)} %copy-done.14, bf16[128,128]{1,0:T(8,128)(2,1)} %copy-done.11, bf16[256,128]{1,0:T(8,128)(2,1)} %copy-done.17, ...), custom_call_target="tpu_custom_call" | custom-call | flops 335544320 | bytes 3670016 | tf_op jit(solution)/shard_map/pallas_call | solution.py:154
  54.8 3.2 %collective-permute-start.15 = (bf16[16,128,128]{2,1,0:T(8,128)(2,1)S(1)}, bf16[16,128,128]{2,1,0:T(8,128)(2,1)S(1)}, u32[]{:S(2)}, u32[]{:S(2)}) collective-permute-start(bf16[16,128,128]{2,1,0:T(8,128)(2,1)S(1)} %constant_dynamic-update-slice_fusion.7.rest_0_), channel_id=1, source_target_pairs={{0,4},{1,5},{2,6},{3,7},{4,0},{5,1},{6,2},{7,3},{8,12},{9,13},{10,... | collective-permute-start | bytes 1572872 | tf_op jit(solution)/shard_map/ppermute | solution.py:65
  58.0 1.5 %collective-permute-done.15.rest_1_ = bf16[16,128,128]{2,1,0:T(8,128)(2,1)S(1)} collective-permute-done((bf16[16,128,128]{2,1,0:T(8,128)(2,1)S(1)}, bf16[16,128,128]{2,1,0:T(8,128)(2,1)S(1)}, u32[]{:S(2)}, u32[]{:S(2)}) %collective-permute-start.15) | collective-permute-done | bytes 524320 | tf_op jit(solution)/shard_map/ppermute | solution.py:65
  60.4 5.2 %shard_map.85 = (bf16[1024,128]{1,0:T(8,128)(2,1)}, bf16[128,128]{1,0:T(8,128)(2,1)}, bf16[384,128]{1,0:T(8,128)(2,1)}, bf16[256,128]{1,0:T(8,128)(2,1)}) custom-call(s32[1]{0:T(128)} %bitcast.z_ref, s32[48]{0:T(128)} %gather_fusion.1, bf16[16,128,128]{2,1,0:T(8,128)(2,1)} %copy-done.5, bf16[16,128,128]{2,1,0:T(8,128)(2,1)} %copy-done.7, ...), custom_call_target="tpu_custom_call" | custom-call | flops 201326592 | bytes 4718592 | tf_op jit(solution)/shard_map/pallas_call | solution.py:251
  67.1 2.8 %collective-permute-start.18 = (bf16[128,128]{1,0:T(8,128)(2,1)}, bf16[128,128]{1,0:T(8,128)(2,1)S(1)}, u32[]{:S(2)}, u32[]{:S(2)}) collective-permute-start(bf16[128,128]{1,0:T(8,128)(2,1)} %get-tuple-element.63), channel_id=1, source_target_pairs={{0,3},{1,2},{2,1},{3,0},{4,7},{5,6},{6,5},{7,4},{8,11},{9,10},{10,... | collective-permute-start | bytes 98312 | tf_op jit(solution)/shard_map/ppermute | solution.py:48
  69.9 3.5 %collective-permute-start.19 = (bf16[256,128]{1,0:T(8,128)(2,1)}, bf16[256,128]{1,0:T(8,128)(2,1)S(1)}, u32[]{:S(2)}, u32[]{:S(2)}) collective-permute-start(bf16[256,128]{1,0:T(8,128)(2,1)} %get-tuple-element.66), channel_id=1, source_target_pairs={{3,4},{7,8},{11,12},{15,16},{19,20},{23,24},{27,28},{4,3},{8,7},{1... | collective-permute-start | bytes 196616 | tf_op jit(solution)/shard_map/ppermute | solution.py:55
  75.6 1.4 %collective-permute-start.22 = (bf16[4,128,128]{2,1,0:T(8,128)(2,1)S(1)}, bf16[4,128,128]{2,1,0:T(8,128)(2,1)S(1)}, u32[]{:S(2)}, u32[]{:S(2)}) collective-permute-start(bf16[4,128,128]{2,1,0:T(8,128)(2,1)S(1)} %pad_maximum_fusion.2), channel_id=1, source_target_pairs={{0,24},{1,25},{2,26},{3,27},{4,28},{5,29},{6,30},{7,31},{8,16},{9,... | collective-permute-start | bytes 393224 | tf_op jit(solution)/shard_map/ppermute | solution.py:65
  78.7 4.7 %shard_map.86.rest_3_ = f32[1024,128]{1,0:T(8,128)} custom-call(s32[1]{0:T(128)} %bitcast.z_ref, s32[80]{0:T(128)} %reshape.41.off_ref, bf16[1024,128]{1,0:T(8,128)(2,1)} %get-tuple-element.65.cur_hbm, bf16[384,128]{1,0:T(8,128)(2,1)} %copy-done.13, bf16[128,128]{1,0:T(8,128)(2,1)} %copy-done.10, bf16[256,128]{1,0:T(8,128)(2,1)} %copy-done.16, ...), custom_call_target="tpu_custom_call" | custom-call | flops 335544320 | bytes 3670016 | tf_op jit(solution)/shard_map/pallas_call | solution.py:154
  84.3 2.7 %collective-permute-start.23 = (bf16[16,128,128]{2,1,0:T(8,128)(2,1)S(1)}, bf16[16,128,128]{2,1,0:T(8,128)(2,1)S(1)}, u32[]{:S(2)}, u32[]{:S(2)}) collective-permute-start(bf16[16,128,128]{2,1,0:T(8,128)(2,1)S(1)} %constant_dynamic-update-slice_fusion.14.rest_0_), channel_id=1, source_target_pairs={{0,4},{1,5},{2,6},{3,7},{4,0},{5,1},{6,2},{7,3},{8,12},{9,13},{10,... | collective-permute-start | bytes 1572872 | tf_op jit(solution)/shard_map/ppermute | solution.py:65
  86.9 1.5 %collective-permute-done.23.rest_1_ = bf16[16,128,128]{2,1,0:T(8,128)(2,1)S(1)} collective-permute-done((bf16[16,128,128]{2,1,0:T(8,128)(2,1)S(1)}, bf16[16,128,128]{2,1,0:T(8,128)(2,1)S(1)}, u32[]{:S(2)}, u32[]{:S(2)}) %collective-permute-start.23) | collective-permute-done | bytes 524320 | tf_op jit(solution)/shard_map/ppermute | solution.py:65
  89.2 5.0 %shard_map.87 = f32[1024,128]{1,0:T(8,128)} custom-call(s32[1]{0:T(128)} %bitcast.z_ref, s32[48]{0:T(128)} %gather_fusion.1, bf16[16,128,128]{2,1,0:T(8,128)(2,1)} %copy-done.3, bf16[16,128,128]{2,1,0:T(8,128)(2,1)} %copy-done.6, bf16[8,6,128,128]{3,2,1,0:T(8,128)(2,1)} %rest_2_.5, f32[1024,128]{1,0:T(8,128)} %shard_map.86.rest_3_, ...), custom_call_target="tpu_custom_call" | custom-call | flops 201326592 | bytes 4718592 | tf_op jit(solution)/shard_map/pallas_call | solution.py:251
  (114 shorter events, 23.0 us)
Async XLA Ops:
  3.4 16.0 %collective-permute-start.1 = (bf16[128,128]{1,0:T(8,128)(2,1)S(1)}, bf16[128,128]{1,0:T(8,128)(2,1)S(1)}, u32[]{:S(2)}, u32[]{:S(2)}) collective-permute-start(bf16[128,128]{1,0:T(8,128)(2,1)S(1)} %gather_fusion), channel_id=1, source_target_pairs={{0,2},{1,3},{2,0},{3,1},{4,6},{5,7},{6,4},{7,5},{8,10},{9,11},{10,... | collective-permute-start | bytes 98312 | tf_op jit(solution)/shard_map/ppermute | solution.py:49
  5.8 13.7 %collective-permute-start.2 = (bf16[128,128]{1,0:T(8,128)(2,1)S(1)}, bf16[128,128]{1,0:T(8,128)(2,1)S(1)}, u32[]{:S(2)}, u32[]{:S(2)}) collective-permute-start(bf16[128,128]{1,0:T(8,128)(2,1)S(1)} %gather_fusion), channel_id=1, source_target_pairs={{0,3},{1,2},{2,1},{3,0},{4,7},{5,6},{6,5},{7,4},{8,11},{9,10},{10,... | collective-permute-start | bytes 98312 | tf_op jit(solution)/shard_map/ppermute | solution.py:48
  6.9 12.6 %collective-permute-start = (bf16[384,128]{1,0:T(8,128)(2,1)S(1)}, bf16[384,128]{1,0:T(8,128)(2,1)S(1)}, u32[]{:S(2)}, u32[]{:S(2)}) collective-permute-start(bf16[384,128]{1,0:T(8,128)(2,1)S(1)} %pad_maximum_fusion.3), channel_id=1, source_target_pairs={{0,1},{1,0},{2,3},{3,2},{4,5},{5,4},{6,7},{7,6},{8,9},{9,8},{10,11... | collective-permute-start | bytes 294920 | tf_op jit(solution)/shard_map/ppermute | solution.py:50
  7.2 12.3 %collective-permute-start.3 = (bf16[256,128]{1,0:T(8,128)(2,1)S(1)}, bf16[256,128]{1,0:T(8,128)(2,1)S(1)}, u32[]{:S(2)}, u32[]{:S(2)}) collective-permute-start(bf16[256,128]{1,0:T(8,128)(2,1)S(1)} %get-tuple-element.71), channel_id=1, source_target_pairs={{3,4},{7,8},{11,12},{15,16},{19,20},{23,24},{27,28},{4,3},{8,7},{1... | collective-permute-start | bytes 196616 | tf_op jit(solution)/shard_map/ppermute | solution.py:55
  19.5 8.2 %collective-permute-start.4 = (bf16[4,128,128]{2,1,0:T(8,128)(2,1)S(1)}, bf16[4,128,128]{2,1,0:T(8,128)(2,1)S(1)}, u32[]{:S(2)}, u32[]{:S(2)}) collective-permute-start(bf16[4,128,128]{2,1,0:T(8,128)(2,1)S(1)} %pad_maximum_fusion), channel_id=1, source_target_pairs={{0,8},{1,9},{2,10},{3,11},{4,12},{5,13},{6,14},{7,15},{8,0},{9,1},... | collective-permute-start | bytes 393224 | tf_op jit(solution)/shard_map/ppermute | solution.py:65
  20.8 7.7 %collective-permute-start.5 = (bf16[4,128,128]{2,1,0:T(8,128)(2,1)S(1)}, bf16[4,128,128]{2,1,0:T(8,128)(2,1)S(1)}, u32[]{:S(2)}, u32[]{:S(2)}) collective-permute-start(bf16[4,128,128]{2,1,0:T(8,128)(2,1)S(1)} %pad_maximum_fusion), channel_id=1, source_target_pairs={{0,16},{1,17},{2,18},{3,19},{4,20},{5,21},{6,22},{7,23},{8,24},{9,... | collective-permute-start | bytes 393224 | tf_op jit(solution)/shard_map/ppermute | solution.py:65
  21.0 7.5 %collective-permute-start.6 = (bf16[4,128,128]{2,1,0:T(8,128)(2,1)S(1)}, bf16[4,128,128]{2,1,0:T(8,128)(2,1)S(1)}, u32[]{:S(2)}, u32[]{:S(2)}) collective-permute-start(bf16[4,128,128]{2,1,0:T(8,128)(2,1)S(1)} %pad_maximum_fusion), channel_id=1, source_target_pairs={{0,24},{1,25},{2,26},{3,27},{4,28},{5,29},{6,30},{7,31},{8,16},{9,... | collective-permute-start | bytes 393224 | tf_op jit(solution)/shard_map/ppermute | solution.py:65
  28.6 2.0 %collective-permute-start.7 = (bf16[16,128,128]{2,1,0:T(8,128)(2,1)S(1)}, bf16[16,128,128]{2,1,0:T(8,128)(2,1)S(1)}, u32[]{:S(2)}, u32[]{:S(2)}) collective-permute-start(bf16[16,128,128]{2,1,0:T(8,128)(2,1)S(1)} %constant_dynamic-update-slice_fusion.rest_0_), channel_id=1, source_target_pairs={{0,4},{1,5},{2,6},{3,7},{4,0},{5,1},{6,2},{7,3},{8,12},{9,13},{10,... | collective-permute-start | bytes 1572872 | tf_op jit(solution)/shard_map/ppermute | solution.py:65
  36.6 8.4 %collective-permute-start.8 = (bf16[384,128]{1,0:T(8,128)(2,1)}, bf16[384,128]{1,0:T(8,128)(2,1)S(1)}, u32[]{:S(2)}, u32[]{:S(2)}) collective-permute-start(bf16[384,128]{1,0:T(8,128)(2,1)} %get-tuple-element.56), channel_id=1, source_target_pairs={{0,1},{1,0},{2,3},{3,2},{4,5},{5,4},{6,7},{7,6},{8,9},{9,8},{10,11... | collective-permute-start | bytes 294920 | tf_op jit(solution)/shard_map/ppermute | solution.py:50
  37.7 7.4 %collective-permute-start.9 = (bf16[128,128]{1,0:T(8,128)(2,1)}, bf16[128,128]{1,0:T(8,128)(2,1)S(1)}, u32[]{:S(2)}, u32[]{:S(2)}) collective-permute-start(bf16[128,128]{1,0:T(8,128)(2,1)} %get-tuple-element.55), channel_id=1, source_target_pairs={{0,2},{1,3},{2,0},{3,1},{4,6},{5,7},{6,4},{7,5},{8,10},{9,11},{10,... | collective-permute-start | bytes 98312 | tf_op jit(solution)/shard_map/ppermute | solution.py:49
  38.8 6.3 %collective-permute-start.10 = (bf16[128,128]{1,0:T(8,128)(2,1)}, bf16[128,128]{1,0:T(8,128)(2,1)S(1)}, u32[]{:S(2)}, u32[]{:S(2)}) collective-permute-start(bf16[128,128]{1,0:T(8,128)(2,1)} %get-tuple-element.55), channel_id=1, source_target_pairs={{0,3},{1,2},{2,1},{3,0},{4,7},{5,6},{6,5},{7,4},{8,11},{9,10},{10,... | collective-permute-start | bytes 98312 | tf_op jit(solution)/shard_map/ppermute | solution.py:48
  41.0 7.6 %collective-permute-start.11 = (bf16[256,128]{1,0:T(8,128)(2,1)}, bf16[256,128]{1,0:T(8,128)(2,1)S(1)}, u32[]{:S(2)}, u32[]{:S(2)}) collective-permute-start(bf16[256,128]{1,0:T(8,128)(2,1)} %get-tuple-element.58), channel_id=1, source_target_pairs={{3,4},{7,8},{11,12},{15,16},{19,20},{23,24},{27,28},{4,3},{8,7},{1... | collective-permute-start | bytes 196616 | tf_op jit(solution)/shard_map/ppermute | solution.py:55
  45.9 8.8 %collective-permute-start.12 = (bf16[4,128,128]{2,1,0:T(8,128)(2,1)S(1)}, bf16[4,128,128]{2,1,0:T(8,128)(2,1)S(1)}, u32[]{:S(2)}, u32[]{:S(2)}) collective-permute-start(bf16[4,128,128]{2,1,0:T(8,128)(2,1)S(1)} %pad_maximum_fusion.1), channel_id=1, source_target_pairs={{0,8},{1,9},{2,10},{3,11},{4,12},{5,13},{6,14},{7,15},{8,0},{9,1},... | collective-permute-start | bytes 393224 | tf_op jit(solution)/shard_map/ppermute | solution.py:65
  46.1 8.6 %collective-permute-start.13 = (bf16[4,128,128]{2,1,0:T(8,128)(2,1)S(1)}, bf16[4,128,128]{2,1,0:T(8,128)(2,1)S(1)}, u32[]{:S(2)}, u32[]{:S(2)}) collective-permute-start(bf16[4,128,128]{2,1,0:T(8,128)(2,1)S(1)} %pad_maximum_fusion.1), channel_id=1, source_target_pairs={{0,16},{1,17},{2,18},{3,19},{4,20},{5,21},{6,22},{7,23},{8,24},{9,... | collective-permute-start | bytes 393224 | tf_op jit(solution)/shard_map/ppermute | solution.py:65
  47.1 7.6 %collective-permute-start.14 = (bf16[4,128,128]{2,1,0:T(8,128)(2,1)S(1)}, bf16[4,128,128]{2,1,0:T(8,128)(2,1)S(1)}, u32[]{:S(2)}, u32[]{:S(2)}) collective-permute-start(bf16[4,128,128]{2,1,0:T(8,128)(2,1)S(1)} %pad_maximum_fusion.1), channel_id=1, source_target_pairs={{0,24},{1,25},{2,26},{3,27},{4,28},{5,29},{6,30},{7,31},{8,16},{9,... | collective-permute-start | bytes 393224 | tf_op jit(solution)/shard_map/ppermute | solution.py:65
  54.8 4.7 %collective-permute-start.15 = (bf16[16,128,128]{2,1,0:T(8,128)(2,1)S(1)}, bf16[16,128,128]{2,1,0:T(8,128)(2,1)S(1)}, u32[]{:S(2)}, u32[]{:S(2)}) collective-permute-start(bf16[16,128,128]{2,1,0:T(8,128)(2,1)S(1)} %constant_dynamic-update-slice_fusion.7.rest_0_), channel_id=1, source_target_pairs={{0,4},{1,5},{2,6},{3,7},{4,0},{5,1},{6,2},{7,3},{8,12},{9,13},{10,... | collective-permute-start | bytes 1572872 | tf_op jit(solution)/shard_map/ppermute | solution.py:65
  65.6 7.9 %collective-permute-start.16 = (bf16[384,128]{1,0:T(8,128)(2,1)}, bf16[384,128]{1,0:T(8,128)(2,1)S(1)}, u32[]{:S(2)}, u32[]{:S(2)}) collective-permute-start(bf16[384,128]{1,0:T(8,128)(2,1)} %get-tuple-element.64), channel_id=1, source_target_pairs={{0,1},{1,0},{2,3},{3,2},{4,5},{5,4},{6,7},{7,6},{8,9},{9,8},{10,11... | collective-permute-start | bytes 294920 | tf_op jit(solution)/shard_map/ppermute | solution.py:50
  66.4 7.1 %collective-permute-start.17 = (bf16[128,128]{1,0:T(8,128)(2,1)}, bf16[128,128]{1,0:T(8,128)(2,1)S(1)}, u32[]{:S(2)}, u32[]{:S(2)}) collective-permute-start(bf16[128,128]{1,0:T(8,128)(2,1)} %get-tuple-element.63), channel_id=1, source_target_pairs={{0,2},{1,3},{2,0},{3,1},{4,6},{5,7},{6,4},{7,5},{8,10},{9,11},{10,... | collective-permute-start | bytes 98312 | tf_op jit(solution)/shard_map/ppermute | solution.py:49
  67.1 6.3 %collective-permute-start.18 = (bf16[128,128]{1,0:T(8,128)(2,1)}, bf16[128,128]{1,0:T(8,128)(2,1)S(1)}, u32[]{:S(2)}, u32[]{:S(2)}) collective-permute-start(bf16[128,128]{1,0:T(8,128)(2,1)} %get-tuple-element.63), channel_id=1, source_target_pairs={{0,3},{1,2},{2,1},{3,0},{4,7},{5,6},{6,5},{7,4},{8,11},{9,10},{10,... | collective-permute-start | bytes 98312 | tf_op jit(solution)/shard_map/ppermute | solution.py:48
  69.9 8.1 %collective-permute-start.19 = (bf16[256,128]{1,0:T(8,128)(2,1)}, bf16[256,128]{1,0:T(8,128)(2,1)S(1)}, u32[]{:S(2)}, u32[]{:S(2)}) collective-permute-start(bf16[256,128]{1,0:T(8,128)(2,1)} %get-tuple-element.66), channel_id=1, source_target_pairs={{3,4},{7,8},{11,12},{15,16},{19,20},{23,24},{27,28},{4,3},{8,7},{1... | collective-permute-start | bytes 196616 | tf_op jit(solution)/shard_map/ppermute | solution.py:55
  74.3 9.9 %collective-permute-start.20 = (bf16[4,128,128]{2,1,0:T(8,128)(2,1)S(1)}, bf16[4,128,128]{2,1,0:T(8,128)(2,1)S(1)}, u32[]{:S(2)}, u32[]{:S(2)}) collective-permute-start(bf16[4,128,128]{2,1,0:T(8,128)(2,1)S(1)} %pad_maximum_fusion.2), channel_id=1, source_target_pairs={{0,8},{1,9},{2,10},{3,11},{4,12},{5,13},{6,14},{7,15},{8,0},{9,1},... | collective-permute-start | bytes 393224 | tf_op jit(solution)/shard_map/ppermute | solution.py:65
  75.2 9.0 %collective-permute-start.21 = (bf16[4,128,128]{2,1,0:T(8,128)(2,1)S(1)}, bf16[4,128,128]{2,1,0:T(8,128)(2,1)S(1)}, u32[]{:S(2)}, u32[]{:S(2)}) collective-permute-start(bf16[4,128,128]{2,1,0:T(8,128)(2,1)S(1)} %pad_maximum_fusion.2), channel_id=1, source_target_pairs={{0,16},{1,17},{2,18},{3,19},{4,20},{5,21},{6,22},{7,23},{8,24},{9,... | collective-permute-start | bytes 393224 | tf_op jit(solution)/shard_map/ppermute | solution.py:65
  75.6 8.6 %collective-permute-start.22 = (bf16[4,128,128]{2,1,0:T(8,128)(2,1)S(1)}, bf16[4,128,128]{2,1,0:T(8,128)(2,1)S(1)}, u32[]{:S(2)}, u32[]{:S(2)}) collective-permute-start(bf16[4,128,128]{2,1,0:T(8,128)(2,1)S(1)} %pad_maximum_fusion.2), channel_id=1, source_target_pairs={{0,24},{1,25},{2,26},{3,27},{4,28},{5,29},{6,30},{7,31},{8,16},{9,... | collective-permute-start | bytes 393224 | tf_op jit(solution)/shard_map/ppermute | solution.py:65
  84.3 4.2 %collective-permute-start.23 = (bf16[16,128,128]{2,1,0:T(8,128)(2,1)S(1)}, bf16[16,128,128]{2,1,0:T(8,128)(2,1)S(1)}, u32[]{:S(2)}, u32[]{:S(2)}) collective-permute-start(bf16[16,128,128]{2,1,0:T(8,128)(2,1)S(1)} %constant_dynamic-update-slice_fusion.14.rest_0_), channel_id=1, source_target_pairs={{0,4},{1,5},{2,6},{3,7},{4,0},{5,1},{6,2},{7,3},{8,12},{9,13},{10,... | collective-permute-start | bytes 1572872 | tf_op jit(solution)/shard_map/ppermute | solution.py:65
  (20 other events, 113.2 us)

commit v24 on v23

--- a/solution.py
+++ b/solution.py
@@ -65,7 +65,7 @@
         sent = {m: lax.ppermute(buf, AXES, pairs(m)) for m in sorted(group, key=lambda m: -m)}
         recvs = [sent[m] for m in group]
         if done is None:
-            done, recvs = lax.optimization_barrier((middle((r1, r3, rc)), recvs))
+            done, recvs = lax.optimization_barrier((middle((r1, rc)), recvs))
         offs = offs + [o ^ m for m in group for o in offs]
         pieces = [buf] + recvs
         if r + 2 < len(rounds):
@@ -79,7 +79,7 @@
 
 def band_kernel(fast, n_own, z_ref, off_ref, cur_hbm, *rest):
     if fast:
-        r1_hbm, r3_hbm, rc_hbm, bt_hbm, out_ref, ext, bt, sem = rest
+        r1_hbm, rc_hbm, bt_hbm, out_ref, ext, bt, sem = rest
     else:
         low_hbm, high_hbm, bt_hbm, out_ref, ext, bt, sem = rest
     blocks, k_band, rows = bt.shape[0], bt.shape[1], bt.shape[2]

time: 95.2 us -> 93.9 us (0.986)
  local copies, waits for them, and re-layouts: 11.1 us -> 8.85 us
  waiting for transfers between devices: 6.54 us -> 7.58 us
    unnamed x58 -> x52, local copies, waits for them, and re-layouts: 7.72 us -> 5.4 us
    ppermute x12, waiting for transfers between devices: 5.44 us -> 6.7 us  [exchange(): lax.ppermute(buf, AXES, pairs(m))]
  transfers between devices with their start and end apart: 24 -> 24, of which waited for: 5 -> 7; matrix products, arithmetic and copies ran while one was open for 13% -> 11% of each run, Pallas kernels for 15% -> 15%
where the time goes in v24:
time: 93.9 us; the launch traced here: 92.8 us
  starting transfers between devices  38.3 us (41%)
  Pallas kernels  29.4 us (31%)
  local copies, waits for them, and re-layouts  8.85 us (9%)
  other arithmetic  8.15 us (9%)
  waiting for transfers between devices  7.58 us (8%)
    pallas_call x3, Pallas kernels, hub_call(): pl.pallas_call(functools.partial(hub_kernel, n_hub, width, final), cost_e...  15.4 us
    pallas_call x3, Pallas kernels, band_call(): pl.pallas_call(functools.partial(band_kernel, fast, n_own), cost_estimate...  14 us
    ppermute x12, starting transfers between devices, exchange(): lax.ppermute(buf, AXES, pairs(m))  14 us
    ppermute x3, starting transfers between devices, exchange(): rc = lax.ppermute(pc, AXES, cross)  13.4 us
    ppermute x12, waiting for transfers between devices, exchange(): lax.ppermute(buf, AXES, pairs(m))  6.7 us
    ppermute x3, starting transfers between devices, exchange(): r3 = lax.ppermute(owned, AXES, pairs(3))  5.9 us
    unnamed x52, local copies, waits for them, and re-layouts  5.4 us
    ppermute x3, starting transfers between devices, exchange(): r2 = lax.ppermute(owned, AXES, pairs(2))  4.63 us
  transfers between devices with their start and end apart: 24, of which 7 were waited for; matrix products, arithmetic and copies ran while one was open for 11% of the time, Pallas kernels for 15%

profile of v24, /device:TPU:5, one launch (start us, length us, event | category | flops | bytes accessed | tf_op | source)
XLA Modules:
  0.0 92.8 jit_solution(5601714224548160613)
XLA Ops:
  3.4 2.4 %collective-permute-start.1 = (bf16[128,128]{1,0:T(8,128)(2,1)S(1)}, bf16[128,128]{1,0:T(8,128)(2,1)S(1)}, u32[]{:S(2)}, u32[]{:S(2)}) collective-permute-start(bf16[128,128]{1,0:T(8,128)(2,1)S(1)} %gather_fusion), channel_id=1, source_target_pairs={{0,2},{1,3},{2,0},{3,1},{4,6},{5,7},{6,4},{7,5},{8,10},{9,11},{10,... | collective-permute-start | bytes 98312 | tf_op jit(solution)/shard_map/ppermute | solution.py:49
  7.2 5.7 %collective-permute-start.3 = (bf16[256,128]{1,0:T(8,128)(2,1)S(1)}, bf16[256,128]{1,0:T(8,128)(2,1)S(1)}, u32[]{:S(2)}, u32[]{:S(2)}) collective-permute-start(bf16[256,128]{1,0:T(8,128)(2,1)S(1)} %get-tuple-element.71), channel_id=1, source_target_pairs={{3,4},{7,8},{11,12},{15,16},{19,20},{23,24},{27,28},{4,3},{8,7},{1... | collective-permute-start | bytes 196616 | tf_op jit(solution)/shard_map/ppermute | solution.py:55
  12.8 1.5 %fusion.rest_6_ = bf16[128,1024]{1,0:T(8,128)(2,1)} fusion(s32[128]{0:T(128)} %param.16), kind=kLoop, calls=%fused_computation.6 | loop fusion | flops 262144 | bytes 262656 | tf_op jit(solution)/shard_map/convert_element_type | solution.py:295
  14.3 2.2 %convert_reduce_fusion = f32[8,128]{1,0:T(8,128)S(1)} fusion(bf16[8,10,128,128]{3,2,1,0:T(8,128)(2,1)} %rest_2_.10), kind=kLoop, calls=%fused_computation.2 | loop fusion | flops 2620416 | bytes 2625536 | tf_op jit(solution)/shard_map/reduce_sum | solution.py:283
  18.1 1.3 %gather_fusion.1 = s32[48]{0:T(128)} fusion(s32[32]{0:T(128)S(1)} %copy-done, s32[1024]{0:T(1024)S(1)} %pad_clamp_fusion), kind=kCustom, calls=%fused_computation.1 | custom fusion | bytes 576 | tf_op jit(solution)/shard_map/gather | solution.py:277
  19.5 1.3 %collective-permute-start.4 = (bf16[4,128,128]{2,1,0:T(8,128)(2,1)S(1)}, bf16[4,128,128]{2,1,0:T(8,128)(2,1)S(1)}, u32[]{:S(2)}, u32[]{:S(2)}) collective-permute-start(bf16[4,128,128]{2,1,0:T(8,128)(2,1)S(1)} %pad_maximum_fusion), channel_id=1, source_target_pairs={{0,8},{1,9},{2,10},{3,11},{4,12},{5,13},{6,14},{7,15},{8,0},{9,1},... | collective-permute-start | bytes 393224 | tf_op jit(solution)/shard_map/ppermute | solution.py:65
  22.3 4.7 %shard_map.82.rest_3_ = f32[1024,128]{1,0:T(8,128)} custom-call(s32[1]{0:T(128)} %bitcast.z_ref, s32[80]{0:T(128)} %reshape.41.off_ref, bf16[1024,128]{1,0:T(8,128)(2,1)} %copy-done.2, bf16[384,128]{1,0:T(8,128)(2,1)} %copy-done.9, bf16[256,128]{1,0:T(8,128)(2,1)} %copy-done.12, bf16[8,10,128,128]{3,2,1,0:T(8,128)(2,1)} %rest_2_.10), custom_call_target="tpu_custom_call" | custom-call | flops 335544320 | bytes 3670016 | tf_op jit(solution)/shard_map/pallas_call | solution.py:154
  27.0 1.6 %collective-permute-done.5 = bf16[4,128,128]{2,1,0:T(8,128)(2,1)S(1)} collective-permute-done((bf16[4,128,128]{2,1,0:T(8,128)(2,1)S(1)}, bf16[4,128,128]{2,1,0:T(8,128)(2,1)S(1)}, u32[]{:S(2)}, u32[]{:S(2)}) %collective-permute-start.5) | collective-permute-done | bytes 131104 | tf_op jit(solution)/shard_map/ppermute | solution.py:65
  29.1 1.5 %collective-permute-done.7.rest_1_ = bf16[16,128,128]{2,1,0:T(8,128)(2,1)S(1)} collective-permute-done((bf16[16,128,128]{2,1,0:T(8,128)(2,1)S(1)}, bf16[16,128,128]{2,1,0:T(8,128)(2,1)S(1)}, u32[]{:S(2)}, u32[]{:S(2)}) %collective-permute-start.7) | collective-permute-done | bytes 524320 | tf_op jit(solution)/shard_map/ppermute | solution.py:65
  31.4 5.2 %shard_map.83 = (bf16[1024,128]{1,0:T(8,128)(2,1)}, bf16[128,128]{1,0:T(8,128)(2,1)}, bf16[384,128]{1,0:T(8,128)(2,1)}, bf16[256,128]{1,0:T(8,128)(2,1)}) custom-call(s32[1]{0:T(128)} %bitcast.z_ref, s32[48]{0:T(128)} %gather_fusion.1, bf16[16,128,128]{2,1,0:T(8,128)(2,1)} %copy-done.4, bf16[16,128,128]{2,1,0:T(8,128)(2,1)} %copy-done.8, ...), custom_call_target="tpu_custom_call" | custom-call | flops 201326592 | bytes 4718592 | tf_op jit(solution)/shard_map/pallas_call | solution.py:251
  37.5 1.3 %collective-permute-start.9 = (bf16[128,128]{1,0:T(8,128)(2,1)}, bf16[128,128]{1,0:T(8,128)(2,1)S(1)}, u32[]{:S(2)}, u32[]{:S(2)}) collective-permute-start(bf16[128,128]{1,0:T(8,128)(2,1)} %get-tuple-element.55), channel_id=1, source_target_pairs={{0,2},{1,3},{2,0},{3,1},{4,6},{5,7},{6,4},{7,5},{8,10},{9,11},{10,... | collective-permute-start | bytes 98312 | tf_op jit(solution)/shard_map/ppermute | solution.py:49
  38.8 2.3 %collective-permute-start.10 = (bf16[128,128]{1,0:T(8,128)(2,1)}, bf16[128,128]{1,0:T(8,128)(2,1)S(1)}, u32[]{:S(2)}, u32[]{:S(2)}) collective-permute-start(bf16[128,128]{1,0:T(8,128)(2,1)} %get-tuple-element.55), channel_id=1, source_target_pairs={{0,3},{1,2},{2,1},{3,0},{4,7},{5,6},{6,5},{7,4},{8,11},{9,10},{10,... | collective-permute-start | bytes 98312 | tf_op jit(solution)/shard_map/ppermute | solution.py:48
  41.0 4.0 %collective-permute-start.11 = (bf16[256,128]{1,0:T(8,128)(2,1)}, bf16[256,128]{1,0:T(8,128)(2,1)S(1)}, u32[]{:S(2)}, u32[]{:S(2)}) collective-permute-start(bf16[256,128]{1,0:T(8,128)(2,1)} %get-tuple-element.58), channel_id=1, source_target_pairs={{3,4},{7,8},{11,12},{15,16},{19,20},{23,24},{27,28},{4,3},{8,7},{1... | collective-permute-start | bytes 196616 | tf_op jit(solution)/shard_map/ppermute | solution.py:55
  47.1 1.5 %collective-permute-start.14 = (bf16[4,128,128]{2,1,0:T(8,128)(2,1)S(1)}, bf16[4,128,128]{2,1,0:T(8,128)(2,1)S(1)}, u32[]{:S(2)}, u32[]{:S(2)}) collective-permute-start(bf16[4,128,128]{2,1,0:T(8,128)(2,1)S(1)} %pad_maximum_fusion.1), channel_id=1, source_target_pairs={{0,24},{1,25},{2,26},{3,27},{4,28},{5,29},{6,30},{7,31},{8,16},{9,... | collective-permute-start | bytes 393224 | tf_op jit(solution)/shard_map/ppermute | solution.py:65
  49.3 4.7 %shard_map.84.rest_3_ = f32[1024,128]{1,0:T(8,128)} custom-call(s32[1]{0:T(128)} %bitcast.z_ref, s32[80]{0:T(128)} %reshape.41.off_ref, bf16[1024,128]{1,0:T(8,128)(2,1)} %get-tuple-element.57.cur_hbm, bf16[384,128]{1,0:T(8,128)(2,1)} %copy-done.11, bf16[256,128]{1,0:T(8,128)(2,1)} %copy-done.14, bf16[8,10,128,128]{3,2,1,0:T(8,128)(2,1)} %rest_2_.10), custom_call_target="tpu_custom_call" | custom-call | flops 335544320 | bytes 3670016 | tf_op jit(solution)/shard_map/pallas_call | solution.py:154
  54.2 3.1 %collective-permute-start.15 = (bf16[16,128,128]{2,1,0:T(8,128)(2,1)S(1)}, bf16[16,128,128]{2,1,0:T(8,128)(2,1)S(1)}, u32[]{:S(2)}, u32[]{:S(2)}) collective-permute-start(bf16[16,128,128]{2,1,0:T(8,128)(2,1)S(1)} %constant_dynamic-update-slice_fusion.7.rest_0_), channel_id=1, source_target_pairs={{0,4},{1,5},{2,6},{3,7},{4,0},{5,1},{6,2},{7,3},{8,12},{9,13},{10,... | collective-permute-start | bytes 1572872 | tf_op jit(solution)/shard_map/ppermute | solution.py:65
  57.3 1.5 %collective-permute-done.15.rest_1_ = bf16[16,128,128]{2,1,0:T(8,128)(2,1)S(1)} collective-permute-done((bf16[16,128,128]{2,1,0:T(8,128)(2,1)S(1)}, bf16[16,128,128]{2,1,0:T(8,128)(2,1)S(1)}, u32[]{:S(2)}, u32[]{:S(2)}) %collective-permute-start.15) | collective-permute-done | bytes 524320 | tf_op jit(solution)/shard_map/ppermute | solution.py:65
  59.6 5.2 %shard_map.85 = (bf16[1024,128]{1,0:T(8,128)(2,1)}, bf16[128,128]{1,0:T(8,128)(2,1)}, bf16[384,128]{1,0:T(8,128)(2,1)}, bf16[256,128]{1,0:T(8,128)(2,1)}) custom-call(s32[1]{0:T(128)} %bitcast.z_ref, s32[48]{0:T(128)} %gather_fusion.1, bf16[16,128,128]{2,1,0:T(8,128)(2,1)} %copy-done.5, bf16[16,128,128]{2,1,0:T(8,128)(2,1)} %copy-done.7, ...), custom_call_target="tpu_custom_call" | custom-call | flops 201326592 | bytes 4718592 | tf_op jit(solution)/shard_map/pallas_call | solution.py:251
  66.7 2.6 %collective-permute-start.18 = (bf16[128,128]{1,0:T(8,128)(2,1)}, bf16[128,128]{1,0:T(8,128)(2,1)S(1)}, u32[]{:S(2)}, u32[]{:S(2)}) collective-permute-start(bf16[128,128]{1,0:T(8,128)(2,1)} %get-tuple-element.63), channel_id=1, source_target_pairs={{0,3},{1,2},{2,1},{3,0},{4,7},{5,6},{6,5},{7,4},{8,11},{9,10},{10,... | collective-permute-start | bytes 98312 | tf_op jit(solution)/shard_map/ppermute | solution.py:48
  69.2 3.7 %collective-permute-start.19 = (bf16[256,128]{1,0:T(8,128)(2,1)}, bf16[256,128]{1,0:T(8,128)(2,1)S(1)}, u32[]{:S(2)}, u32[]{:S(2)}) collective-permute-start(bf16[256,128]{1,0:T(8,128)(2,1)} %get-tuple-element.66), channel_id=1, source_target_pairs={{3,4},{7,8},{11,12},{15,16},{19,20},{23,24},{27,28},{4,3},{8,7},{1... | collective-permute-start | bytes 196616 | tf_op jit(solution)/shard_map/ppermute | solution.py:55
  78.0 4.7 %shard_map.86.rest_3_ = f32[1024,128]{1,0:T(8,128)} custom-call(s32[1]{0:T(128)} %bitcast.z_ref, s32[80]{0:T(128)} %reshape.41.off_ref, bf16[1024,128]{1,0:T(8,128)(2,1)} %get-tuple-element.65.cur_hbm, bf16[384,128]{1,0:T(8,128)(2,1)} %copy-done.10, bf16[256,128]{1,0:T(8,128)(2,1)} %copy-done.13, bf16[8,10,128,128]{3,2,1,0:T(8,128)(2,1)} %rest_2_.10), custom_call_target="tpu_custom_call" | custom-call | flops 335544320 | bytes 3670016 | tf_op jit(solution)/shard_map/pallas_call | solution.py:154
  83.1 2.3 %collective-permute-start.23 = (bf16[16,128,128]{2,1,0:T(8,128)(2,1)S(1)}, bf16[16,128,128]{2,1,0:T(8,128)(2,1)S(1)}, u32[]{:S(2)}, u32[]{:S(2)}) collective-permute-start(bf16[16,128,128]{2,1,0:T(8,128)(2,1)S(1)} %constant_dynamic-update-slice_fusion.14.rest_0_), channel_id=1, source_target_pairs={{0,4},{1,5},{2,6},{3,7},{4,0},{5,1},{6,2},{7,3},{8,12},{9,13},{10,... | collective-permute-start | bytes 1572872 | tf_op jit(solution)/shard_map/ppermute | solution.py:65
  85.5 1.5 %collective-permute-done.23.rest_1_ = bf16[16,128,128]{2,1,0:T(8,128)(2,1)S(1)} collective-permute-done((bf16[16,128,128]{2,1,0:T(8,128)(2,1)S(1)}, bf16[16,128,128]{2,1,0:T(8,128)(2,1)S(1)}, u32[]{:S(2)}, u32[]{:S(2)}) %collective-permute-start.23) | collective-permute-done | bytes 524320 | tf_op jit(solution)/shard_map/ppermute | solution.py:65
  87.8 5.0 %shard_map.87 = f32[1024,128]{1,0:T(8,128)} custom-call(s32[1]{0:T(128)} %bitcast.z_ref, s32[48]{0:T(128)} %gather_fusion.1, bf16[16,128,128]{2,1,0:T(8,128)(2,1)} %copy-done.3, bf16[16,128,128]{2,1,0:T(8,128)(2,1)} %copy-done.6, bf16[8,6,128,128]{3,2,1,0:T(8,128)(2,1)} %rest_2_.11, f32[1024,128]{1,0:T(8,128)} %shard_map.86.rest_3_, ...), custom_call_target="tpu_custom_call" | custom-call | flops 201326592 | bytes 4718592 | tf_op jit(solution)/shard_map/pallas_call | solution.py:251
  (108 shorter events, 21.7 us)
Async XLA Ops:
  3.4 16.1 %collective-permute-start.1 = (bf16[128,128]{1,0:T(8,128)(2,1)S(1)}, bf16[128,128]{1,0:T(8,128)(2,1)S(1)}, u32[]{:S(2)}, u32[]{:S(2)}) collective-permute-start(bf16[128,128]{1,0:T(8,128)(2,1)S(1)} %gather_fusion), channel_id=1, source_target_pairs={{0,2},{1,3},{2,0},{3,1},{4,6},{5,7},{6,4},{7,5},{8,10},{9,11},{10,... | collective-permute-start | bytes 98312 | tf_op jit(solution)/shard_map/ppermute | solution.py:49
  5.8 13.7 %collective-permute-start.2 = (bf16[128,128]{1,0:T(8,128)(2,1)S(1)}, bf16[128,128]{1,0:T(8,128)(2,1)S(1)}, u32[]{:S(2)}, u32[]{:S(2)}) collective-permute-start(bf16[128,128]{1,0:T(8,128)(2,1)S(1)} %gather_fusion), channel_id=1, source_target_pairs={{0,3},{1,2},{2,1},{3,0},{4,7},{5,6},{6,5},{7,4},{8,11},{9,10},{10,... | collective-permute-start | bytes 98312 | tf_op jit(solution)/shard_map/ppermute | solution.py:48
  6.9 12.6 %collective-permute-start = (bf16[384,128]{1,0:T(8,128)(2,1)S(1)}, bf16[384,128]{1,0:T(8,128)(2,1)S(1)}, u32[]{:S(2)}, u32[]{:S(2)}) collective-permute-start(bf16[384,128]{1,0:T(8,128)(2,1)S(1)} %pad_maximum_fusion.3), channel_id=1, source_target_pairs={{0,1},{1,0},{2,3},{3,2},{4,5},{5,4},{6,7},{7,6},{8,9},{9,8},{10,11... | collective-permute-start | bytes 294920 | tf_op jit(solution)/shard_map/ppermute | solution.py:50
  7.2 12.3 %collective-permute-start.3 = (bf16[256,128]{1,0:T(8,128)(2,1)S(1)}, bf16[256,128]{1,0:T(8,128)(2,1)S(1)}, u32[]{:S(2)}, u32[]{:S(2)}) collective-permute-start(bf16[256,128]{1,0:T(8,128)(2,1)S(1)} %get-tuple-element.71), channel_id=1, source_target_pairs={{3,4},{7,8},{11,12},{15,16},{19,20},{23,24},{27,28},{4,3},{8,7},{1... | collective-permute-start | bytes 196616 | tf_op jit(solution)/shard_map/ppermute | solution.py:55
  19.5 7.5 %collective-permute-start.4 = (bf16[4,128,128]{2,1,0:T(8,128)(2,1)S(1)}, bf16[4,128,128]{2,1,0:T(8,128)(2,1)S(1)}, u32[]{:S(2)}, u32[]{:S(2)}) collective-permute-start(bf16[4,128,128]{2,1,0:T(8,128)(2,1)S(1)} %pad_maximum_fusion), channel_id=1, source_target_pairs={{0,8},{1,9},{2,10},{3,11},{4,12},{5,13},{6,14},{7,15},{8,0},{9,1},... | collective-permute-start | bytes 393224 | tf_op jit(solution)/shard_map/ppermute | solution.py:65
  20.8 7.7 %collective-permute-start.5 = (bf16[4,128,128]{2,1,0:T(8,128)(2,1)S(1)}, bf16[4,128,128]{2,1,0:T(8,128)(2,1)S(1)}, u32[]{:S(2)}, u32[]{:S(2)}) collective-permute-start(bf16[4,128,128]{2,1,0:T(8,128)(2,1)S(1)} %pad_maximum_fusion), channel_id=1, source_target_pairs={{0,16},{1,17},{2,18},{3,19},{4,20},{5,21},{6,22},{7,23},{8,24},{9,... | collective-permute-start | bytes 393224 | tf_op jit(solution)/shard_map/ppermute | solution.py:65
  21.0 7.5 %collective-permute-start.6 = (bf16[4,128,128]{2,1,0:T(8,128)(2,1)S(1)}, bf16[4,128,128]{2,1,0:T(8,128)(2,1)S(1)}, u32[]{:S(2)}, u32[]{:S(2)}) collective-permute-start(bf16[4,128,128]{2,1,0:T(8,128)(2,1)S(1)} %pad_maximum_fusion), channel_id=1, source_target_pairs={{0,24},{1,25},{2,26},{3,27},{4,28},{5,29},{6,30},{7,31},{8,16},{9,... | collective-permute-start | bytes 393224 | tf_op jit(solution)/shard_map/ppermute | solution.py:65
  28.6 2.0 %collective-permute-start.7 = (bf16[16,128,128]{2,1,0:T(8,128)(2,1)S(1)}, bf16[16,128,128]{2,1,0:T(8,128)(2,1)S(1)}, u32[]{:S(2)}, u32[]{:S(2)}) collective-permute-start(bf16[16,128,128]{2,1,0:T(8,128)(2,1)S(1)} %constant_dynamic-update-slice_fusion.rest_0_), channel_id=1, source_target_pairs={{0,4},{1,5},{2,6},{3,7},{4,0},{5,1},{6,2},{7,3},{8,12},{9,13},{10,... | collective-permute-start | bytes 1572872 | tf_op jit(solution)/shard_map/ppermute | solution.py:65
  36.7 8.4 %collective-permute-start.8 = (bf16[384,128]{1,0:T(8,128)(2,1)}, bf16[384,128]{1,0:T(8,128)(2,1)S(1)}, u32[]{:S(2)}, u32[]{:S(2)}) collective-permute-start(bf16[384,128]{1,0:T(8,128)(2,1)} %get-tuple-element.56), channel_id=1, source_target_pairs={{0,1},{1,0},{2,3},{3,2},{4,5},{5,4},{6,7},{7,6},{8,9},{9,8},{10,11... | collective-permute-start | bytes 294920 | tf_op jit(solution)/shard_map/ppermute | solution.py:50
  37.5 7.6 %collective-permute-start.9 = (bf16[128,128]{1,0:T(8,128)(2,1)}, bf16[128,128]{1,0:T(8,128)(2,1)S(1)}, u32[]{:S(2)}, u32[]{:S(2)}) collective-permute-start(bf16[128,128]{1,0:T(8,128)(2,1)} %get-tuple-element.55), channel_id=1, source_target_pairs={{0,2},{1,3},{2,0},{3,1},{4,6},{5,7},{6,4},{7,5},{8,10},{9,11},{10,... | collective-permute-start | bytes 98312 | tf_op jit(solution)/shard_map/ppermute | solution.py:49
  38.8 6.3 %collective-permute-start.10 = (bf16[128,128]{1,0:T(8,128)(2,1)}, bf16[128,128]{1,0:T(8,128)(2,1)S(1)}, u32[]{:S(2)}, u32[]{:S(2)}) collective-permute-start(bf16[128,128]{1,0:T(8,128)(2,1)} %get-tuple-element.55), channel_id=1, source_target_pairs={{0,3},{1,2},{2,1},{3,0},{4,7},{5,6},{6,5},{7,4},{8,11},{9,10},{10,... | collective-permute-start | bytes 98312 | tf_op jit(solution)/shard_map/ppermute | solution.py:48
  41.0 7.6 %collective-permute-start.11 = (bf16[256,128]{1,0:T(8,128)(2,1)}, bf16[256,128]{1,0:T(8,128)(2,1)S(1)}, u32[]{:S(2)}, u32[]{:S(2)}) collective-permute-start(bf16[256,128]{1,0:T(8,128)(2,1)} %get-tuple-element.58), channel_id=1, source_target_pairs={{3,4},{7,8},{11,12},{15,16},{19,20},{23,24},{27,28},{4,3},{8,7},{1... | collective-permute-start | bytes 196616 | tf_op jit(solution)/shard_map/ppermute | solution.py:55
  45.9 8.1 %collective-permute-start.12 = (bf16[4,128,128]{2,1,0:T(8,128)(2,1)S(1)}, bf16[4,128,128]{2,1,0:T(8,128)(2,1)S(1)}, u32[]{:S(2)}, u32[]{:S(2)}) collective-permute-start(bf16[4,128,128]{2,1,0:T(8,128)(2,1)S(1)} %pad_maximum_fusion.1), channel_id=1, source_target_pairs={{0,8},{1,9},{2,10},{3,11},{4,12},{5,13},{6,14},{7,15},{8,0},{9,1},... | collective-permute-start | bytes 393224 | tf_op jit(solution)/shard_map/ppermute | solution.py:65
  46.1 7.8 %collective-permute-start.13 = (bf16[4,128,128]{2,1,0:T(8,128)(2,1)S(1)}, bf16[4,128,128]{2,1,0:T(8,128)(2,1)S(1)}, u32[]{:S(2)}, u32[]{:S(2)}) collective-permute-start(bf16[4,128,128]{2,1,0:T(8,128)(2,1)S(1)} %pad_maximum_fusion.1), channel_id=1, source_target_pairs={{0,16},{1,17},{2,18},{3,19},{4,20},{5,21},{6,22},{7,23},{8,24},{9,... | collective-permute-start | bytes 393224 | tf_op jit(solution)/shard_map/ppermute | solution.py:65
  47.1 7.1 %collective-permute-start.14 = (bf16[4,128,128]{2,1,0:T(8,128)(2,1)S(1)}, bf16[4,128,128]{2,1,0:T(8,128)(2,1)S(1)}, u32[]{:S(2)}, u32[]{:S(2)}) collective-permute-start(bf16[4,128,128]{2,1,0:T(8,128)(2,1)S(1)} %pad_maximum_fusion.1), channel_id=1, source_target_pairs={{0,24},{1,25},{2,26},{3,27},{4,28},{5,29},{6,30},{7,31},{8,16},{9,... | collective-permute-start | bytes 393224 | tf_op jit(solution)/shard_map/ppermute | solution.py:65
  54.2 4.6 %collective-permute-start.15 = (bf16[16,128,128]{2,1,0:T(8,128)(2,1)S(1)}, bf16[16,128,128]{2,1,0:T(8,128)(2,1)S(1)}, u32[]{:S(2)}, u32[]{:S(2)}) collective-permute-start(bf16[16,128,128]{2,1,0:T(8,128)(2,1)S(1)} %constant_dynamic-update-slice_fusion.7.rest_0_), channel_id=1, source_target_pairs={{0,4},{1,5},{2,6},{3,7},{4,0},{5,1},{6,2},{7,3},{8,12},{9,13},{10,... | collective-permute-start | bytes 1572872 | tf_op jit(solution)/shard_map/ppermute | solution.py:65
  64.8 8.1 %collective-permute-start.16 = (bf16[384,128]{1,0:T(8,128)(2,1)}, bf16[384,128]{1,0:T(8,128)(2,1)S(1)}, u32[]{:S(2)}, u32[]{:S(2)}) collective-permute-start(bf16[384,128]{1,0:T(8,128)(2,1)} %get-tuple-element.64), channel_id=1, source_target_pairs={{0,1},{1,0},{2,3},{3,2},{4,5},{5,4},{6,7},{7,6},{8,9},{9,8},{10,11... | collective-permute-start | bytes 294920 | tf_op jit(solution)/shard_map/ppermute | solution.py:50
  65.7 7.3 %collective-permute-start.17 = (bf16[128,128]{1,0:T(8,128)(2,1)}, bf16[128,128]{1,0:T(8,128)(2,1)S(1)}, u32[]{:S(2)}, u32[]{:S(2)}) collective-permute-start(bf16[128,128]{1,0:T(8,128)(2,1)} %get-tuple-element.63), channel_id=1, source_target_pairs={{0,2},{1,3},{2,0},{3,1},{4,6},{5,7},{6,4},{7,5},{8,10},{9,11},{10,... | collective-permute-start | bytes 98312 | tf_op jit(solution)/shard_map/ppermute | solution.py:49
  66.7 6.3 %collective-permute-start.18 = (bf16[128,128]{1,0:T(8,128)(2,1)}, bf16[128,128]{1,0:T(8,128)(2,1)S(1)}, u32[]{:S(2)}, u32[]{:S(2)}) collective-permute-start(bf16[128,128]{1,0:T(8,128)(2,1)} %get-tuple-element.63), channel_id=1, source_target_pairs={{0,3},{1,2},{2,1},{3,0},{4,7},{5,6},{6,5},{7,4},{8,11},{9,10},{10,... | collective-permute-start | bytes 98312 | tf_op jit(solution)/shard_map/ppermute | solution.py:48
  69.2 8.1 %collective-permute-start.19 = (bf16[256,128]{1,0:T(8,128)(2,1)}, bf16[256,128]{1,0:T(8,128)(2,1)S(1)}, u32[]{:S(2)}, u32[]{:S(2)}) collective-permute-start(bf16[256,128]{1,0:T(8,128)(2,1)} %get-tuple-element.66), channel_id=1, source_target_pairs={{3,4},{7,8},{11,12},{15,16},{19,20},{23,24},{27,28},{4,3},{8,7},{1... | collective-permute-start | bytes 196616 | tf_op jit(solution)/shard_map/ppermute | solution.py:55
  73.8 8.9 %collective-permute-start.20 = (bf16[4,128,128]{2,1,0:T(8,128)(2,1)S(1)}, bf16[4,128,128]{2,1,0:T(8,128)(2,1)S(1)}, u32[]{:S(2)}, u32[]{:S(2)}) collective-permute-start(bf16[4,128,128]{2,1,0:T(8,128)(2,1)S(1)} %pad_maximum_fusion.2), channel_id=1, source_target_pairs={{0,8},{1,9},{2,10},{3,11},{4,12},{5,13},{6,14},{7,15},{8,0},{9,1},... | collective-permute-start | bytes 393224 | tf_op jit(solution)/shard_map/ppermute | solution.py:65
  75.0 7.7 %collective-permute-start.21 = (bf16[4,128,128]{2,1,0:T(8,128)(2,1)S(1)}, bf16[4,128,128]{2,1,0:T(8,128)(2,1)S(1)}, u32[]{:S(2)}, u32[]{:S(2)}) collective-permute-start(bf16[4,128,128]{2,1,0:T(8,128)(2,1)S(1)} %pad_maximum_fusion.2), channel_id=1, source_target_pairs={{0,16},{1,17},{2,18},{3,19},{4,20},{5,21},{6,22},{7,23},{8,24},{9,... | collective-permute-start | bytes 393224 | tf_op jit(solution)/shard_map/ppermute | solution.py:65
  75.5 7.6 %collective-permute-start.22 = (bf16[4,128,128]{2,1,0:T(8,128)(2,1)S(1)}, bf16[4,128,128]{2,1,0:T(8,128)(2,1)S(1)}, u32[]{:S(2)}, u32[]{:S(2)}) collective-permute-start(bf16[4,128,128]{2,1,0:T(8,128)(2,1)S(1)} %pad_maximum_fusion.2), channel_id=1, source_target_pairs={{0,24},{1,25},{2,26},{3,27},{4,28},{5,29},{6,30},{7,31},{8,16},{9,... | collective-permute-start | bytes 393224 | tf_op jit(solution)/shard_map/ppermute | solution.py:65
  83.1 3.9 %collective-permute-start.23 = (bf16[16,128,128]{2,1,0:T(8,128)(2,1)S(1)}, bf16[16,128,128]{2,1,0:T(8,128)(2,1)S(1)}, u32[]{:S(2)}, u32[]{:S(2)}) collective-permute-start(bf16[16,128,128]{2,1,0:T(8,128)(2,1)S(1)} %constant_dynamic-update-slice_fusion.14.rest_0_), channel_id=1, source_target_pairs={{0,4},{1,5},{2,6},{3,7},{4,0},{5,1},{6,2},{7,3},{8,12},{9,13},{10,... | collective-permute-start | bytes 1572872 | tf_op jit(solution)/shard_map/ppermute | solution.py:65
  (17 other events, 101.4 us)
